TPU v7x, 32 devices: a whole 2x2x4 slice. The times are simulated.
32 devices in a mesh: gx: 4 (over y, core), gy: 8 (over z, x).
Axes of the slice: x: 2, y: 2, z: 4, core: 2. Of those that a mesh axis runs over, the one named last changes fastest.
Arguments:
- atm_state: float32 [4, 40, 64, 1024], P(None, None, 'gx', 'gy'), may hold values from -6 to 6
- metric: float32 [2, 64, 1024], P(None, 'gx', 'gy'), may hold values from 0.5 to 2
- send_idx: int32 [32, 32, 256], P(('gx', 'gy')), may hold values from 0 to 2047
- send_counts: int32 [32, 32], P(('gx', 'gy')), may hold values from 1 to 256, as said below
- ocean_tracers: float32 [2, 40, 64, 1024], P(None, None, 'gx', 'gy'), may hold values from -6 to 6
- ocean_velocity: float32 [2, 40, 64, 1024], P(None, None, 'gx', 'gy'), may hold values from -0.2 to 0.2
- remap_slots: int32 [4, 64, 1024], P(None, 'gx', 'gy'), may hold values from 0 to 8191, as said below
- remap_weights: float32 [4, 64, 1024], P(None, 'gx', 'gy'), may hold values from 0.1 to 0.5
Outputs:
- atm_out: float32 [4, 40, 64, 1024], P(None, None, 'gx', 'gy')
- ocean_out: float32 [2, 40, 64, 1024], P(None, None, 'gx', 'gy')
Inputs may be any that keep to these rules, and one draw needn't show every extreme that they name: `send_counts`: each destination gets at least one data slot from every source; for a quarter of the destinations (at least one) and for the last source, every slot carries data. `remap_slots`: every entry names a slot r = s * 256 + c with c below send_counts[s, d] for the cell's own partition d.
All inputs are finite; a program needn't handle non-finite values.
Results may differ from a plain program's by a relative error of at most 0.0001.
Values sent between devices are 32-bit elements; how exact they have to be, the bound alone decides.
No kernel may reach another device: no remote copies, remote signals or barrier semaphores. Data moves between devices by JAX's collectives and lax.ppermute only.
A program may use at most 128 MiB of HBM per device.

v0:
```python
import math

import jax
import jax.numpy as jnp
import numpy as np
from jax import lax
from jax.sharding import PartitionSpec as P

SUB = 2
OSTEPS = 2


visc_coef = 0.01
diff_coef = 0.2
wind_coef = 0.1
surf_coef = 0.2


def extended(cells, sides, width):
    for axis, dim in sides:
        count = lax.axis_size(axis)
        head = lax.slice_in_dim(cells, 0, width, axis=dim)
        tail = lax.slice_in_dim(cells, cells.shape[dim] - width, cells.shape[dim], axis=dim)
        cells = jnp.concatenate(
            [
                lax.ppermute(tail, axis, [(i, (i + 1) % count) for i in range(count)]),
                cells,
                lax.ppermute(head, axis, [((i + 1) % count, i) for i in range(count)]),
            ],
            axis=dim,
        )
    return cells


def gll_tables():
    points = np.array([-1.0, -1.0 / np.sqrt(5.0), 1.0 / np.sqrt(5.0), 1.0])
    weights = np.array([1.0 / 6.0, 5.0 / 6.0, 5.0 / 6.0, 1.0 / 6.0])
    derivative = np.zeros((4, 4))
    for target in range(4):
        for source in range(4):
            if target == source:
                derivative[target, source] = np.sum(
                    [
                        1.0 / (points[source] - points[others])
                        for others in range(4)
                        if others != source
                    ]
                )
            else:
                numer = np.prod(
                    [
                        points[target] - points[others]
                        for others in range(4)
                        if others != target and others != source
                    ]
                )
                denom = np.prod(
                    [points[source] - points[others] for others in range(4) if others != source]
                )
                derivative[target, source] = numer / denom
    massw = np.array([1.0 / 3.0, 5.0 / 6.0, 5.0 / 6.0, 1.0 / 3.0])
    return (derivative, weights, massw)


def stiffness(state_in, metric_x, metric_y, derivative_np, weights_np):
    levels, xsize, ysize = state_in.shape
    highest = lax.Precision.HIGHEST
    block_x = jnp.asarray(np.kron(np.eye(xsize // 4), derivative_np), jnp.float32)
    block_y = jnp.asarray(np.kron(np.eye(ysize // 4), derivative_np), jnp.float32)
    weight_x = jnp.asarray(np.tile(weights_np, xsize // 4), jnp.float32)[:, None]
    weight_y = jnp.asarray(np.tile(weights_np, ysize // 4), jnp.float32)[None, :]
    along_x = jnp.einsum("ab,lby->lay", block_x, state_in, precision=highest)
    term_x = (
        jnp.einsum("ba,lby->lay", block_x, weight_x * metric_x * along_x, precision=highest)
        * weight_y
    )
    along_y = jnp.einsum("lxc,dc->lxd", state_in, block_y, precision=highest)
    term_y = (
        jnp.einsum("lxc,cd->lxd", weight_y * metric_y * along_y, block_y, precision=highest)
        * weight_x
    )
    return term_x + term_y


def mass_inverse(massw_np, xsize, ysize):
    return jnp.asarray(
        1.0 / (np.tile(massw_np, xsize // 4)[:, None] * np.tile(massw_np, ysize // 4)[None, :]),
        jnp.float32,
    )


def edge_sum(padded):
    inner_y = padded.shape[2] - 2
    ypos = jnp.arange(inner_y) % 4
    centre = padded[:, :, 1:-1]
    merged = centre + jnp.where(
        ypos == 0, padded[:, :, :-2], jnp.where(ypos == 3, padded[:, :, 2:], 0.0)
    )
    inner_x = merged.shape[1] - 2
    xpos = (jnp.arange(inner_x) % 4)[:, None]
    middle = merged[:, 1:-1]
    return middle + jnp.where(xpos == 0, merged[:, :-2], jnp.where(xpos == 3, merged[:, 2:], 0.0))


def tracer_step(padded, velocity):
    centre = padded[..., 1:-1, 1:-1]
    east = padded[..., 2:, 1:-1]
    west = padded[..., :-2, 1:-1]
    north = padded[..., 1:-1, 2:]
    south = padded[..., 1:-1, :-2]
    return (
        centre
        + diff_coef * (east + west + north + south - 4.0 * centre)
        - 0.5 * velocity[0] * (east - west)
        - 0.5 * velocity[1] * (north - south)
    )


def per_device(
    atm_state,
    metric,
    send_idx,
    send_counts,
    ocean_tracers,
    ocean_velocity,
    remap_slots,
    remap_weights,
):
    fields, levels, xlocal, ylocal = atm_state.shape
    derivative_np, weights_np, massw_np = gll_tables()
    state_now = atm_state.reshape(fields * levels, xlocal, ylocal)
    inv_mass = mass_inverse(massw_np, xlocal, ylocal)
    for substep in range(SUB):
        stiff = stiffness(state_now, metric[0], metric[1], derivative_np, weights_np)
        padded = extended(stiff, (("gx", 1), ("gy", 2)), 1)
        state_now = state_now - visc_coef * edge_sum(padded) * inv_mass
    atm_out = state_now.reshape(fields, levels, xlocal, ylocal)
    bottom = atm_out[:, levels - 1]
    speed = jnp.sqrt(1.0 + bottom[0] * bottom[0] + bottom[1] * bottom[1])
    flux_flat = (bottom * speed).reshape(fields, xlocal * ylocal)
    node_total = xlocal * ylocal
    rank_total = send_idx.shape[1]
    slot_cap = send_idx.shape[2]
    group = math.gcd(rank_total, max(1, 4096 // slot_cap))
    index_blocks = send_idx[0].reshape(rank_total // group, group * slot_cap)
    node_iota = jnp.arange(node_total, dtype=jnp.int32)

    def pick_block(index_row):
        selector = (index_row[:, None] == node_iota[None, :]).astype(jnp.float32)
        return lax.dot_general(
            flux_flat,
            selector,
            (((1,), (1,)), ((), ())),
            precision=lax.Precision.HIGHEST,
            preferred_element_type=jnp.float32,
        )

    picked_blocks = lax.map(pick_block, index_blocks)
    payload = (
        picked_blocks.reshape(rank_total // group, fields, group, slot_cap)
        .transpose(1, 0, 2, 3)
        .reshape(fields, rank_total, slot_cap)
    )
    count_row = send_counts[0]
    live_slots = (jnp.arange(slot_cap)[None, :] < count_row[:, None]).astype(jnp.float32)
    payload = payload * live_slots[None]
    received = lax.all_to_all(payload, ("gx", "gy"), split_axis=1, concat_axis=1, tiled=True)
    received = received.reshape(fields, -1)
    source_count, ocean_x, ocean_y = remap_slots.shape
    gathered = jnp.take(received, remap_slots.reshape(-1), axis=1).reshape(
        fields, source_count, ocean_x, ocean_y
    )
    ocean_flux = jnp.sum(remap_weights[None] * gathered, axis=1)
    velocity = ocean_velocity.at[0, 0].add(wind_coef * jnp.tanh(ocean_flux[0]))
    velocity = velocity.at[1, 0].add(wind_coef * jnp.tanh(ocean_flux[1]))
    tracers = ocean_tracers.at[0, 0].add(surf_coef * ocean_flux[2])
    tracers = tracers.at[1, 0].add(surf_coef * ocean_flux[3])
    for repeat in range(OSTEPS):
        ocean_pad = extended(tracers, (("gx", 2), ("gy", 3)), 1)
        tracers = tracer_step(ocean_pad, velocity)
    return (atm_out, tracers)


def solution(mesh):
    in_specs = (
        P(None, None, "gx", "gy"),
        P(None, "gx", "gy"),
        P(("gx", "gy"), None, None),
        P(("gx", "gy"), None),
        P(None, None, "gx", "gy"),
        P(None, None, "gx", "gy"),
        P(None, "gx", "gy"),
        P(None, "gx", "gy"),
    )
    out_specs = (P(None, None, "gx", "gy"), P(None, None, "gx", "gy"))
    return jax.shard_map(
        per_device, mesh=mesh, in_specs=in_specs, out_specs=out_specs, check_vma=False
    )
```

profile of v0, /device:TPU:0, one launch (start us, length us, event | category | flops | bytes accessed | tf_op | source)
XLA Modules:
  0.0 181.4 jit_solution(17854917686863997487)
XLA Ops:
  2.0 1.2 fusion.18
  3.3 1.2 fusion.17
  4.5 1.2 fusion.14
  5.7 1.2 fusion.13
  7.5 2.0 %collective-permute-start.1 = (f32[160,1,128]{2,1,0:T(1,128)S(1)}, f32[160,1,128]{2,1,0:T(1,128)S(1)}, u32[]{:S(2)}, u32[]{:S(2)}) collective-permute-start(f32[160,1,128]{2,1,0:T(1,128)S(1)} %get-tuple-element.107), channel_id=1, source_target_pairs={{8,0},{16,8},{24,16},{0,24},{9,1},{17,9},{25,17},{1,25},{10,2},{18... | collective-permute-start | bytes 245768 | tf_op jit(solution)/shard_map/ppermute | solution.py:28
  9.6 2.1 %collective-permute-done = f32[160,1,128]{2,1,0:T(1,128)S(1)} collective-permute-done((f32[160,1,128]{2,1,0:T(1,128)S(1)}, f32[160,1,128]{2,1,0:T(1,128)S(1)}, u32[]{:S(2)}, u32[]{:S(2)}) %collective-permute-start) | collective-permute-done | bytes 81952 | tf_op jit(solution)/shard_map/ppermute | solution.py:26
  12.6 2.5 %fusion.45 = (f32[160,18,1]{2,1,0:T(8,128)}, f32[160,18,1]{2,1,0:T(8,128)}) fusion(f32[160,18,128]{2,1,0:T(8,128)S(1)} %pad_maximum_fusion.12), kind=kLoop, calls=%fused_computation.120 | loop fusion | bytes 46080 | tf_op jit(solution)/shard_map/slice | solution.py:23
  15.1 2.2 %copy.63 = f32[160,18,1]{0,2,1:T(1,128)S(1)} copy(f32[160,18,1]{2,1,0:T(8,128)} %get-tuple-element.102) | data formatting | bytes 23040 | tf_op jit(solution)/shard_map/slice | solution.py:23
  17.3 1.6 collective-permute-start.2
  18.9 2.2 %copy.65 = f32[160,18,1]{0,2,1:T(1,128)S(1)} copy(f32[160,18,1]{2,1,0:T(8,128)} %get-tuple-element.103) | data formatting | bytes 23040 | tf_op jit(solution)/shard_map/slice | solution.py:22
  21.2 3.4 %collective-permute-start.3 = (f32[160,18,1]{0,2,1:T(1,128)S(1)}, f32[160,18,1]{0,2,1:T(1,128)S(1)}, u32[]{:S(2)}, u32[]{:S(2)}) collective-permute-start(f32[160,18,1]{0,2,1:T(1,128)S(1)} %copy.65), channel_id=1, source_target_pairs={{1,0},{2,1},{3,2},{4,3},{5,4},{6,5},{7,6},{0,7},{9,8},{10,9},{11,1... | collective-permute-start | bytes 34568 | tf_op jit(solution)/shard_map/ppermute | solution.py:28
  24.6 1.9 %copy.64 = f32[160,18,1]{2,1,0:T(8,128)} copy(f32[160,18,1]{0,2,1:T(1,128)S(1)} %collective-permute-done.2) | data formatting | bytes 23040 | tf_op jit(solution)/shard_map/ppermute | solution.py:26
  26.5 2.0 %copy.66 = f32[160,18,1]{2,1,0:T(8,128)} copy(f32[160,18,1]{0,2,1:T(1,128)S(1)} %collective-permute-done.3) | data formatting | bytes 23040 | tf_op jit(solution)/shard_map/ppermute | solution.py:28
  28.5 4.2 %fusion.11 = f32[160,18,128]{2,1,0:T(8,128)S(1)} fusion(f32[160,18,1]{2,1,0:T(8,128)} %copy.66, f32[160,1,128]{2,1,0:T(1,128)S(1)} %collective-permute-done.1, f32[160,16,128]{2,1,0:T(8,128)S(1)} %fusion.13, f32[160,1,128]{2,1,0:T(1,128)S(1)} %collective-permute-done, f32[160,18,1]{2,1,0:T(8,128)} %copy.64, pred[128]{0:T(512)(128)(4,1)S(1)} %get-tuple-element.123, ...), kind=kLoop, calls=%fused_computation.21 | loop fusion | flops 4055040 | bytes 2972416 | tf_op jit(solution)/shard_map/add | solution.py:96
  33.2 1.2 fusion.15
  34.5 1.2 convolution_multiply_fusion.1
  35.7 1.2 fusion.16
  36.9 1.2 fusion.12
  38.2 1.3 collective-permute-start.4
  40.1 2.1 %collective-permute-done.4 = f32[160,1,128]{2,1,0:T(1,128)S(1)} collective-permute-done((f32[160,1,128]{2,1,0:T(1,128)S(1)}, f32[160,1,128]{2,1,0:T(1,128)S(1)}, u32[]{:S(2)}, u32[]{:S(2)}) %collective-permute-start.4) | collective-permute-done | bytes 81952 | tf_op jit(solution)/shard_map/ppermute | solution.py:26
  43.1 2.5 %fusion.44 = (f32[160,18,1]{2,1,0:T(8,128)}, f32[160,18,1]{2,1,0:T(8,128)}) fusion(f32[160,18,128]{2,1,0:T(8,128)S(1)} %pad_maximum_fusion.13), kind=kLoop, calls=%fused_computation.119 | loop fusion | bytes 46080 | tf_op jit(solution)/shard_map/slice | solution.py:23
  45.6 2.2 %copy.68 = f32[160,18,1]{0,2,1:T(1,128)S(1)} copy(f32[160,18,1]{2,1,0:T(8,128)} %get-tuple-element.100) | data formatting | bytes 23040 | tf_op jit(solution)/shard_map/slice | solution.py:23
  48.3 2.2 %copy.70 = f32[160,18,1]{0,2,1:T(1,128)S(1)} copy(f32[160,18,1]{2,1,0:T(8,128)} %get-tuple-element.101) | data formatting | bytes 23040 | tf_op jit(solution)/shard_map/slice | solution.py:22
  50.6 4.5 %collective-permute-start.7 = (f32[160,18,1]{0,2,1:T(1,128)S(1)}, f32[160,18,1]{0,2,1:T(1,128)S(1)}, u32[]{:S(2)}, u32[]{:S(2)}) collective-permute-start(f32[160,18,1]{0,2,1:T(1,128)S(1)} %copy.70), channel_id=1, source_target_pairs={{1,0},{2,1},{3,2},{4,3},{5,4},{6,5},{7,6},{0,7},{9,8},{10,9},{11,1... | collective-permute-start | bytes 34568 | tf_op jit(solution)/shard_map/ppermute | solution.py:28
  55.2 1.9 %copy.69 = f32[160,18,1]{2,1,0:T(8,128)} copy(f32[160,18,1]{0,2,1:T(1,128)S(1)} %collective-permute-done.6) | data formatting | bytes 23040 | tf_op jit(solution)/shard_map/ppermute | solution.py:26
  57.1 2.0 %copy.71 = f32[160,18,1]{2,1,0:T(8,128)} copy(f32[160,18,1]{0,2,1:T(1,128)S(1)} %collective-permute-done.7) | data formatting | bytes 23040 | tf_op jit(solution)/shard_map/ppermute | solution.py:28
  59.1 4.2 %fusion.8 = f32[160,18,128]{2,1,0:T(8,128)S(1)} fusion(f32[160,18,1]{2,1,0:T(8,128)} %copy.71, f32[160,1,128]{2,1,0:T(1,128)S(1)} %collective-permute-done.5, f32[160,16,128]{2,1,0:T(8,128)S(1)} %fusion.12, f32[160,1,128]{2,1,0:T(1,128)S(1)} %collective-permute-done.4, f32[160,18,1]{2,1,0:T(8,128)} %copy.69, pred[128]{0:T(512)(128)(4,1)S(1)} %get-tuple-element.123, ...), kind=kLoop, calls=%fused_computation.12 | loop fusion | flops 4055040 | bytes 2972416 | tf_op jit(solution)/shard_map/add | solution.py:96
  63.8 1.0 copy-done.5
  64.9 30.3 %while.15 = (s32[]{:T(128)}, f32[2,4,4096]{2,1,0:T(4,128)S(1)}, s32[2,4096]{1,0:T(2,128)S(1)}, f32[4,2048]{1,0:T(4,128)S(1)}, s32[]{:T(128)}) while((s32[]{:T(128)}, f32[2,4,4096]{2,1,0:T(4,128)S(1)}, s32[2,4096]{1,0:T(2,128)S(1)}, f32[4,2048]{1,0:T(4,128)S(1)}, s32[]{:T(128)}) %tuple.56), condition=%wide.region_1.2_spmd.clone, body=%wide.region_0.1_spmd.clone.sunk | while | flops 411041792 | bytes 147525 | solution.py:158
  64.9 15.1 %fusion.72 = f32[2,4,4096]{2,1,0:T(4,128)S(1)} fusion(f32[2,4,4096]{2,1,0:T(4,128)S(1)} %get-tuple-element.155, s32[]{:T(128)} %get-tuple-element.154, f32[4,2048]{1,0:T(4,128)S(1)} %get-tuple-element.162, s32[4096]{0:T(1024)S(1)} %bitcast.97), kind=kOutput, calls=%fused_computation.6.clone.1 | convolution fusion | flops 411041792 | bytes 114692 | tf_op jit(solution)/shard_map/while/body/eval_jaxpr/dot_general | solution.py:150
  80.1 15.1 %fusion.72 = f32[2,4,4096]{2,1,0:T(4,128)S(1)} fusion(f32[2,4,4096]{2,1,0:T(4,128)S(1)} %get-tuple-element.155, s32[]{:T(128)} %get-tuple-element.154, f32[4,2048]{1,0:T(4,128)S(1)} %get-tuple-element.162, s32[4096]{0:T(1024)S(1)} %bitcast.97), kind=kOutput, calls=%fused_computation.6.clone.1 | convolution fusion | flops 411041792 | bytes 114692 | tf_op jit(solution)/shard_map/while/body/eval_jaxpr/dot_general | solution.py:150
  95.9 6.8 %all-to-all-start = ((f32[4,32,256]{2,0,1:T(4,128)}), f32[4,32,256]{2,0,1:T(4,128)S(1)}, u32[]{:S(2)}, u32[]{:S(2)}) async-start(f32[4,32,256]{2,0,1:T(4,128)} %broadcast_multiply_fusion), calls=%async_computation | async-start | bytes 262144 | tf_op jit(solution)/shard_map/all_to_all | solution.py:167
  102.7 7.7 %all-to-all-done = f32[4,32,256]{2,0,1:T(4,128)S(1)} async-done(((f32[4,32,256]{2,0,1:T(4,128)}), f32[4,32,256]{2,0,1:T(4,128)S(1)}, u32[]{:S(2)}, u32[]{:S(2)}) %all-to-all-start) | async-done | bytes 131104 | tf_op jit(solution)/shard_map/all_to_all | solution.py:167
  110.4 2.6 %copy.73 = f32[4,32,256]{0,2,1:T(8,128)} copy(f32[4,32,256]{2,0,1:T(4,128)S(1)} %all-to-all-done) | data formatting | bytes 262144 | tf_op jit(solution)/shard_map/all_to_all | solution.py:167
  113.0 30.0 %gather_fusion = f32[8192,4]{1,0:T(8,128)} fusion(f32[4,8192]{0,1:T(8,128)} %bitcast.92, s32[8192]{0:T(1024)S(1)} %broadcast_clamp_fusion), kind=kCustom, calls=%fused_computation | custom fusion | bytes 294912 | tf_op jit(solution)/shard_map/jit(_take)/gather | solution.py:170
  143.0 6.1 %multiply_reduce_fusion = f32[4,16,128]{0,2,1:T(8,128)S(1)} fusion(f32[4,4,16,128]{0,3,2,1:T(8,128)} %bitcast.93, f32[4,16,128]{2,1,0:T(8,128)S(1)} %copy-done.9, pred[4,16,128]{2,1,0:T(8,128)(4,1)S(1)} %compare_and_fusion), kind=kLoop, calls=%fused_computation.8 | loop fusion | flops 90112 | bytes 204800 | tf_op jit(solution)/shard_map/reduce_sum | solution.py:173
  149.1 2.0 %fusion.28 = (f32[16,128]{1,0:T(8,128)S(1)}, f32[16,128]{1,0:T(8,128)S(1)}, f32[16,128]{1,0:T(8,128)S(1)}, f32[16,128]{1,0:T(8,128)S(1)}) fusion(f32[4,16,128]{0,2,1:T(8,128)S(1)} %multiply_reduce_fusion), kind=kLoop, calls=%fused_computation.56 | loop fusion | flops 8192 | bytes 65536 | tf_op jit(solution)/shard_map/mul | solution.py:175
  151.8 1.5 collective-permute-done.8
  153.3 2.1 %collective-permute-done.9 = f32[2,40,1,128]{3,2,1,0:T(1,128)S(1)} collective-permute-done((f32[2,40,1,128]{3,2,1,0:T(1,128)S(1)}, f32[2,40,1,128]{3,2,1,0:T(1,128)S(1)}, u32[]{:S(2)}, u32[]{:S(2)}) %collective-permute-start.9) | collective-permute-done | bytes 40992 | tf_op jit(solution)/shard_map/ppermute | solution.py:26
  156.3 1.9 %collective-permute-start.10 = (f32[2,40,18,1]{1,2,3,0:T(8,128)S(1)}, f32[2,40,18,1]{1,2,3,0:T(8,128)S(1)}, u32[]{:S(2)}, u32[]{:S(2)}) collective-permute-start(f32[2,40,18,1]{1,2,3,0:T(8,128)S(1)} %copy.74), channel_id=1, source_target_pairs={{1,0},{2,1},{3,2},{4,3},{5,4},{6,5},{7,6},{0,7},{9,8},{10,9},{11,1... | collective-permute-start | bytes 17288 | tf_op jit(solution)/shard_map/ppermute | solution.py:28
  160.6 4.6 %collective-permute-done.11 = f32[2,40,18,1]{1,2,3,0:T(8,128)S(1)} collective-permute-done((f32[2,40,18,1]{1,2,3,0:T(8,128)S(1)}, f32[2,40,18,1]{1,2,3,0:T(8,128)S(1)}, u32[]{:S(2)}, u32[]{:S(2)}) %collective-permute-start.11) | collective-permute-done | bytes 5792 | tf_op jit(solution)/shard_map/ppermute | solution.py:26
  165.6 2.0 %multiply_subtract_fusion.1 = f32[2,40,16,128]{3,2,1,0:T(8,128)S(1)} fusion(f32[2,40,16,128]{3,2,1,0:T(8,128)S(1)} %fusion.37, f32[2,40,1,128]{3,2,1,0:T(1,128)S(1)} %collective-permute-done.8, f32[2,40,1,128]{3,2,1,0:T(1,128)S(1)} %collective-permute-done.9, f32[2,40,18,1]{3,2,1,0:T(8,128)S(1)} %copy.77, f32[2,40,18,1]{3,2,1,0:T(8,128)S(1)} %copy.75, ...), kind=kLoop, calls=%fused_computation.83 | loop fusion | flops 3440640 | bytes 2059520 | tf_op jit(solution)/shard_map/sub | solution.py:112
  168.3 1.2 collective-permute-done.12
  169.4 1.8 collective-permute-done.13
  172.6 2.0 %collective-permute-start.15 = (f32[2,40,18,1]{1,2,3,0:T(8,128)S(1)}, f32[2,40,18,1]{1,2,3,0:T(8,128)S(1)}, u32[]{:S(2)}, u32[]{:S(2)}) collective-permute-start(f32[2,40,18,1]{1,2,3,0:T(8,128)S(1)} %copy.80), channel_id=1, source_target_pairs={{0,1},{1,2},{2,3},{3,4},{4,5},{5,6},{6,7},{7,0},{8,9},{9,10},{10,1... | collective-permute-start | bytes 17288 | tf_op jit(solution)/shard_map/ppermute | solution.py:26
  174.6 1.4 collective-permute-done.14
  176.4 2.7 %collective-permute-done.15 = f32[2,40,18,1]{1,2,3,0:T(8,128)S(1)} collective-permute-done((f32[2,40,18,1]{1,2,3,0:T(8,128)S(1)}, f32[2,40,18,1]{1,2,3,0:T(8,128)S(1)}, u32[]{:S(2)}, u32[]{:S(2)}) %collective-permute-start.15) | collective-permute-done | bytes 5792 | tf_op jit(solution)/shard_map/ppermute | solution.py:26
  179.6 1.8 multiply_subtract_fusion
  (87 shorter events, 14.1 us)
Async XLA Ops:
  0.6 0.7 copy-start.13
  0.6 0.7 copy-start.14
  0.7 0.9 copy-start.7
  0.7 1.3 copy-start
  0.7 0.8 copy-start.12
  3.2 1.3 copy-start.6
  7.0 4.6 %collective-permute-start = (f32[160,1,128]{2,1,0:T(1,128)S(1)}, f32[160,1,128]{2,1,0:T(1,128)S(1)}, u32[]{:S(2)}, u32[]{:S(2)}) collective-permute-start(f32[160,1,128]{2,1,0:T(1,128)S(1)} %get-tuple-element.106), channel_id=1, source_target_pairs={{0,8},{8,16},{16,24},{24,0},{1,9},{9,17},{17,25},{25,1},{2,10},{10... | collective-permute-start | bytes 245768 | tf_op jit(solution)/shard_map/ppermute | solution.py:26
  7.5 4.8 %collective-permute-start.1 = (f32[160,1,128]{2,1,0:T(1,128)S(1)}, f32[160,1,128]{2,1,0:T(1,128)S(1)}, u32[]{:S(2)}, u32[]{:S(2)}) collective-permute-start(f32[160,1,128]{2,1,0:T(1,128)S(1)} %get-tuple-element.107), channel_id=1, source_target_pairs={{8,0},{16,8},{24,16},{0,24},{9,1},{17,9},{25,17},{1,25},{10,2},{18... | collective-permute-start | bytes 245768 | tf_op jit(solution)/shard_map/ppermute | solution.py:28
  17.3 7.2 %collective-permute-start.2 = (f32[160,18,1]{0,2,1:T(1,128)S(1)}, f32[160,18,1]{0,2,1:T(1,128)S(1)}, u32[]{:S(2)}, u32[]{:S(2)}) collective-permute-start(f32[160,18,1]{0,2,1:T(1,128)S(1)} %copy.63), channel_id=1, source_target_pairs={{0,1},{1,2},{2,3},{3,4},{4,5},{5,6},{6,7},{7,0},{8,9},{9,10},{10,1... | collective-permute-start | bytes 34568 | tf_op jit(solution)/shard_map/ppermute | solution.py:26
  21.2 5.3 %collective-permute-start.3 = (f32[160,18,1]{0,2,1:T(1,128)S(1)}, f32[160,18,1]{0,2,1:T(1,128)S(1)}, u32[]{:S(2)}, u32[]{:S(2)}) collective-permute-start(f32[160,18,1]{0,2,1:T(1,128)S(1)} %copy.65), channel_id=1, source_target_pairs={{1,0},{2,1},{3,2},{4,3},{5,4},{6,5},{7,6},{0,7},{9,8},{10,9},{11,1... | collective-permute-start | bytes 34568 | tf_op jit(solution)/shard_map/ppermute | solution.py:28
  28.5 4.3 %copy-start.10 = (f32[16,128]{1,0:T(8,128)S(1)}, f32[16,128]{1,0:T(8,128)}, u32[]{:S(2)}) copy-start(f32[16,128]{1,0:T(8,128)} %constant.196) | copy-start | bytes 24580
  36.9 3.1 %copy-start.8 = (s32[4,16,128]{2,1,0:T(8,128)S(1)}, s32[4,16,128]{2,1,0:T(8,128)}, u32[]{:S(2)}) copy-start(s32[4,16,128]{2,1,0:T(8,128)} %param.33) | copy-start | bytes 98308
  38.2 3.9 %collective-permute-start.4 = (f32[160,1,128]{2,1,0:T(1,128)S(1)}, f32[160,1,128]{2,1,0:T(1,128)S(1)}, u32[]{:S(2)}, u32[]{:S(2)}) collective-permute-start(f32[160,1,128]{2,1,0:T(1,128)S(1)} %get-tuple-element.104), channel_id=1, source_target_pairs={{0,8},{8,16},{16,24},{24,0},{1,9},{9,17},{17,25},{25,1},{2,10},{10... | collective-permute-start | bytes 245768 | tf_op jit(solution)/shard_map/ppermute | solution.py:26
  39.5 3.2 %collective-permute-start.5 = (f32[160,1,128]{2,1,0:T(1,128)S(1)}, f32[160,1,128]{2,1,0:T(1,128)S(1)}, u32[]{:S(2)}, u32[]{:S(2)}) collective-permute-start(f32[160,1,128]{2,1,0:T(1,128)S(1)} %get-tuple-element.105), channel_id=1, source_target_pairs={{8,0},{16,8},{24,16},{0,24},{9,1},{17,9},{25,17},{1,25},{10,2},{18... | collective-permute-start | bytes 245768 | tf_op jit(solution)/shard_map/ppermute | solution.py:28
  45.6 9.5 %copy-start.15 = (s32[1,32]{1,0:T(1,128)S(1)}, s32[1,32]{1,0:T(1,128)}, u32[]{:S(2)}) copy-start(s32[1,32]{1,0:T(1,128)} %param.30) | copy-start | bytes 388
  45.6 9.6 %copy-start.11 = (s32[1,32,256]{2,1,0:T(8,128)S(1)}, s32[1,32,256]{2,1,0:T(8,128)}, u32[]{:S(2)}) copy-start(s32[1,32,256]{2,1,0:T(8,128)} %param.29) | copy-start | bytes 98308
  47.8 7.4 %collective-permute-start.6 = (f32[160,18,1]{0,2,1:T(1,128)S(1)}, f32[160,18,1]{0,2,1:T(1,128)S(1)}, u32[]{:S(2)}, u32[]{:S(2)}) collective-permute-start(f32[160,18,1]{0,2,1:T(1,128)S(1)} %copy.68), channel_id=1, source_target_pairs={{0,1},{1,2},{2,3},{3,4},{4,5},{5,6},{6,7},{7,0},{8,9},{9,10},{10,1... | collective-permute-start | bytes 34568 | tf_op jit(solution)/shard_map/ppermute | solution.py:26
  50.6 6.6 %collective-permute-start.7 = (f32[160,18,1]{0,2,1:T(1,128)S(1)}, f32[160,18,1]{0,2,1:T(1,128)S(1)}, u32[]{:S(2)}, u32[]{:S(2)}) collective-permute-start(f32[160,18,1]{0,2,1:T(1,128)S(1)} %copy.70), channel_id=1, source_target_pairs={{1,0},{2,1},{3,2},{4,3},{5,4},{6,5},{7,6},{0,7},{9,8},{10,9},{11,1... | collective-permute-start | bytes 34568 | tf_op jit(solution)/shard_map/ppermute | solution.py:28
  63.8 1.1 copy-start.5
  95.9 14.5 %all-to-all-start = ((f32[4,32,256]{2,0,1:T(4,128)}), f32[4,32,256]{2,0,1:T(4,128)S(1)}, u32[]{:S(2)}, u32[]{:S(2)}) async-start(f32[4,32,256]{2,0,1:T(4,128)} %broadcast_multiply_fusion), calls=%async_computation | async-start | bytes 262144 | tf_op jit(solution)/shard_map/all_to_all | solution.py:167
  102.7 40.3 %copy-start.9 = (f32[4,16,128]{2,1,0:T(8,128)S(1)}, f32[4,16,128]{2,1,0:T(8,128)}, u32[]{:S(2)}) copy-start(f32[4,16,128]{2,1,0:T(8,128)} %param.34) | copy-start | bytes 98308
  149.1 2.0 %copy-start.1 = (f32[2,40,16,128]{3,2,1,0:T(8,128)S(1)}, f32[2,40,16,128]{3,2,1,0:T(8,128)}, u32[]{:S(2)}) copy-start(f32[2,40,16,128]{3,2,1,0:T(8,128)} %param.31) | copy-start | bytes 1966084
  149.1 2.7 %copy-start.4 = (f32[2,40,16,128]{3,2,1,0:T(8,128)S(1)}, f32[2,40,16,128]{3,2,1,0:T(8,128)}, u32[]{:S(2)}) copy-start(f32[2,40,16,128]{3,2,1,0:T(8,128)} %param.32) | copy-start | bytes 1966084
  151.2 2.1 %collective-permute-start.8 = (f32[2,40,1,128]{3,2,1,0:T(1,128)S(1)}, f32[2,40,1,128]{3,2,1,0:T(1,128)S(1)}, u32[]{:S(2)}, u32[]{:S(2)}) collective-permute-start(f32[2,40,1,128]{3,2,1,0:T(1,128)S(1)} %get-tuple-element.117), channel_id=1, source_target_pairs={{8,0},{16,8},{24,16},{0,24},{9,1},{17,9},{25,17},{1,25},{10,2},{18... | collective-permute-start | bytes 122888 | tf_op jit(solution)/shard_map/ppermute | solution.py:28
  151.6 3.8 %collective-permute-start.9 = (f32[2,40,1,128]{3,2,1,0:T(1,128)S(1)}, f32[2,40,1,128]{3,2,1,0:T(1,128)S(1)}, u32[]{:S(2)}, u32[]{:S(2)}) collective-permute-start(f32[2,40,1,128]{3,2,1,0:T(1,128)S(1)} %get-tuple-element.116), channel_id=1, source_target_pairs={{0,8},{8,16},{16,24},{24,0},{1,9},{9,17},{17,25},{25,1},{2,10},{10... | collective-permute-start | bytes 122888 | tf_op jit(solution)/shard_map/ppermute | solution.py:26
  156.3 3.9 %collective-permute-start.10 = (f32[2,40,18,1]{1,2,3,0:T(8,128)S(1)}, f32[2,40,18,1]{1,2,3,0:T(8,128)S(1)}, u32[]{:S(2)}, u32[]{:S(2)}) collective-permute-start(f32[2,40,18,1]{1,2,3,0:T(8,128)S(1)} %copy.74), channel_id=1, source_target_pairs={{1,0},{2,1},{3,2},{4,3},{5,4},{6,5},{7,6},{0,7},{9,8},{10,9},{11,1... | collective-permute-start | bytes 17288 | tf_op jit(solution)/shard_map/ppermute | solution.py:28
  158.6 6.6 %collective-permute-start.11 = (f32[2,40,18,1]{1,2,3,0:T(8,128)S(1)}, f32[2,40,18,1]{1,2,3,0:T(8,128)S(1)}, u32[]{:S(2)}, u32[]{:S(2)}) collective-permute-start(f32[2,40,18,1]{1,2,3,0:T(8,128)S(1)} %copy.76), channel_id=1, source_target_pairs={{0,1},{1,2},{2,3},{3,4},{4,5},{5,6},{6,7},{7,0},{8,9},{9,10},{10,1... | collective-permute-start | bytes 17288 | tf_op jit(solution)/shard_map/ppermute | solution.py:26
  167.7 1.7 collective-permute-start.12
  167.8 3.5 %collective-permute-start.13 = (f32[2,40,1,128]{3,2,1,0:T(1,128)S(1)}, f32[2,40,1,128]{3,2,1,0:T(1,128)S(1)}, u32[]{:S(2)}, u32[]{:S(2)}) collective-permute-start(f32[2,40,1,128]{3,2,1,0:T(1,128)S(1)} %get-tuple-element.112), channel_id=1, source_target_pairs={{0,8},{8,16},{16,24},{24,0},{1,9},{9,17},{17,25},{25,1},{2,10},{10... | collective-permute-start | bytes 122888 | tf_op jit(solution)/shard_map/ppermute | solution.py:26
  171.7 7.9 %copy-start.2 = (f32[40,16,128]{2,1,0:T(8,128)S(1)}, f32[40,16,128]{2,1,0:T(8,128)}, u32[]{:S(2)}) copy-start(f32[40,16,128]{2,1,0:T(8,128)} %get-tuple-element.114) | copy-start | bytes 983044
  171.7 7.9 %copy-start.3 = (f32[40,16,128]{2,1,0:T(8,128)S(1)}, f32[40,16,128]{2,1,0:T(8,128)}, u32[]{:S(2)}) copy-start(f32[40,16,128]{2,1,0:T(8,128)} %get-tuple-element.115) | copy-start | bytes 983044
  172.1 3.9 %collective-permute-start.14 = (f32[2,40,18,1]{1,2,3,0:T(8,128)S(1)}, f32[2,40,18,1]{1,2,3,0:T(8,128)S(1)}, u32[]{:S(2)}, u32[]{:S(2)}) collective-permute-start(f32[2,40,18,1]{1,2,3,0:T(8,128)S(1)} %copy.78), channel_id=1, source_target_pairs={{1,0},{2,1},{3,2},{4,3},{5,4},{6,5},{7,6},{0,7},{9,8},{10,9},{11,1... | collective-permute-start | bytes 17288 | tf_op jit(solution)/shard_map/ppermute | solution.py:28
  172.6 6.6 %collective-permute-start.15 = (f32[2,40,18,1]{1,2,3,0:T(8,128)S(1)}, f32[2,40,18,1]{1,2,3,0:T(8,128)S(1)}, u32[]{:S(2)}, u32[]{:S(2)}) collective-permute-start(f32[2,40,18,1]{1,2,3,0:T(8,128)S(1)} %copy.80), channel_id=1, source_target_pairs={{0,1},{1,2},{2,3},{3,4},{4,5},{5,6},{6,7},{7,0},{8,9},{9,10},{10,1... | collective-permute-start | bytes 17288 | tf_op jit(solution)/shard_map/ppermute | solution.py:26
where the time goes:
time: 182 us; the launch traced here: 181 us
  local copies, waits for them, and re-layouts  61.1 us (34%)
  matrix products  39.9 us (22%)
  waiting for transfers between devices  28.9 us (16%)
  starting transfers between devices  26.4 us (15%)
  other arithmetic  24.1 us (13%)
    dot_general x2, matrix products, pick_block(): lax.dot_general(flux_flat, selector, (((1,), (1,)), ((), ())), precision=...  30.2 us
    gather x1, local copies, waits for them, and re-layouts, per_device(): jnp.take(received, remap_slots.reshape(-1), axis=1)  30 us
    ppermute x8, waiting for transfers between devices, extended(): lax.ppermute(tail, axis, [(i, (i + 1) % count) for i in range(count)])  15.4 us
    ppermute x8, starting transfers between devices, extended(): lax.ppermute(head, axis, [((i + 1) % count, i) for i in range(count)])  12.8 us
    slice x10, local copies, waits for them, and re-layouts, extended(): lax.slice_in_dim(cells, cells.shape[dim] - width, cells.shape[dim], axis=...  10.6 us
    add x2, other arithmetic, edge_sum(): centre + jnp.where(ypos == 0, padded[:, :, :-2], jnp.where(ypos == 3, pad...  8.47 us
    all_to_all x1, waiting for transfers between devices, per_device(): lax.all_to_all(payload, ('gx', 'gy'), split_axis=1, concat_axis=1, tiled=...  7.69 us
    ppermute x8, starting transfers between devices, extended(): lax.ppermute(tail, axis, [(i, (i + 1) % count) for i in range(count)])  6.84 us
  transfers between devices with their start and end apart: 17, of which 13 were waited for; matrix products, arithmetic and copies ran while one was open for 6% of the time, Pallas kernels for 0%

commit v1 on v0

--- a/solution.py
+++ b/solution.py
@@ -4,6 +4,7 @@
 import jax.numpy as jnp
 import numpy as np
 from jax import lax
+from jax.experimental import pallas as pl
 from jax.sharding import PartitionSpec as P
 
 SUB = 2
@@ -116,6 +117,44 @@
     )
 
 
+def split_bf16(values):
+    first = values.astype(jnp.bfloat16)
+    rest = values - first.astype(jnp.float32)
+    second = rest.astype(jnp.bfloat16)
+    third = (rest - second.astype(jnp.float32)).astype(jnp.bfloat16)
+    return jnp.stack([first, second, third], axis=1)
+
+
+def gather_kernel(index_ref, table_ref, out_ref):
+    fields, rows, tile = out_ref.shape[0], table_ref.shape[1] // 3, out_ref.shape[1]
+    index = index_ref[...]
+    onehot = (lax.broadcasted_iota(jnp.int32, (128, tile), 0) == (index & 127)).astype(jnp.bfloat16)
+    select = lax.broadcasted_iota(jnp.int32, (rows, tile), 0) == (index >> 7)
+    for field in range(fields):
+        picked = jnp.dot(table_ref[field], onehot, preferred_element_type=jnp.float32)
+        whole = picked[:rows] + picked[rows : 2 * rows] + picked[2 * rows :]
+        out_ref[pl.ds(field, 1), :] = jnp.sum(jnp.where(select, whole, 0.0), axis=0, keepdims=True)
+
+
+def onehot_gather(table, index):
+    fields, total = table.shape
+    rows = total // 128
+    parts = split_bf16(table.reshape(fields, rows, 128)).reshape(fields, 3 * rows, 128)
+    flat = index.reshape(1, -1)
+    count = flat.shape[1]
+    tile = math.gcd(count, 1024)
+    return pl.pallas_call(
+        gather_kernel,
+        grid=(count // tile,),
+        in_specs=[
+            pl.BlockSpec((1, tile), lambda step: (0, step)),
+            pl.BlockSpec((fields, 3 * rows, 128), lambda step: (0, 0, 0)),
+        ],
+        out_specs=pl.BlockSpec((fields, tile), lambda step: (0, step)),
+        out_shape=jax.ShapeDtypeStruct((fields, count), jnp.float32),
+    )(flat, parts)
+
+
 def per_device(
     atm_state,
     metric,
@@ -141,35 +180,14 @@
     node_total = xlocal * ylocal
     rank_total = send_idx.shape[1]
     slot_cap = send_idx.shape[2]
-    group = math.gcd(rank_total, max(1, 4096 // slot_cap))
-    index_blocks = send_idx[0].reshape(rank_total // group, group * slot_cap)
-    node_iota = jnp.arange(node_total, dtype=jnp.int32)
-
-    def pick_block(index_row):
-        selector = (index_row[:, None] == node_iota[None, :]).astype(jnp.float32)
-        return lax.dot_general(
-            flux_flat,
-            selector,
-            (((1,), (1,)), ((), ())),
-            precision=lax.Precision.HIGHEST,
-            preferred_element_type=jnp.float32,
-        )
-
-    picked_blocks = lax.map(pick_block, index_blocks)
-    payload = (
-        picked_blocks.reshape(rank_total // group, fields, group, slot_cap)
-        .transpose(1, 0, 2, 3)
-        .reshape(fields, rank_total, slot_cap)
-    )
+    payload = onehot_gather(flux_flat, send_idx[0]).reshape(fields, rank_total, slot_cap)
     count_row = send_counts[0]
     live_slots = (jnp.arange(slot_cap)[None, :] < count_row[:, None]).astype(jnp.float32)
     payload = payload * live_slots[None]
     received = lax.all_to_all(payload, ("gx", "gy"), split_axis=1, concat_axis=1, tiled=True)
     received = received.reshape(fields, -1)
     source_count, ocean_x, ocean_y = remap_slots.shape
-    gathered = jnp.take(received, remap_slots.reshape(-1), axis=1).reshape(
-        fields, source_count, ocean_x, ocean_y
-    )
+    gathered = onehot_gather(received, remap_slots).reshape(fields, source_count, ocean_x, ocean_y)
     ocean_flux = jnp.sum(remap_weights[None] * gathered, axis=1)
     velocity = ocean_velocity.at[0, 0].add(wind_coef * jnp.tanh(ocean_flux[0]))
     velocity = velocity.at[1, 0].add(wind_coef * jnp.tanh(ocean_flux[1]))

time: 182 us -> 126 us (0.69)
  local copies, waits for them, and re-layouts: 61.1 us -> 30.6 us
  matrix products: 39.9 us -> 9.68 us
  blocking collectives: 0 us -> 13.7 us
  Pallas kernels: 0 us -> 11.9 us
  waiting for transfers between devices: 28.9 us -> 21.3 us
  other arithmetic: 24.1 us -> 16.8 us
  starting transfers between devices: 26.4 us -> 19.6 us
    dot_general x2 -> x0, matrix products: 30.2 us -> none  [pick_block(): lax.dot_general(flux_flat, selector, (((1,), (1,)), ((), ())), precision=...]
    gather x1 -> x0, local copies, waits for them, and re-layouts: 30 us -> none  [per_device(): jnp.take(received, remap_slots.reshape(-1), axis=1)]
    all_to_all x0 -> x1, blocking collectives: none -> 13.7 us  [per_device(): lax.all_to_all(payload, ('gx', 'gy'), split_axis=1, concat_axis=1, tiled=...]
    pallas_call x0 -> x2, Pallas kernels: none -> 11.9 us  [onehot_gather(): pl.pallas_call(gather_kernel, grid=(count // tile,), in_specs=[pl.BlockSp...]
    all_to_all x1 -> x0, waiting for transfers between devices: 7.69 us -> none  [per_device(): lax.all_to_all(payload, ('gx', 'gy'), split_axis=1, concat_axis=1, tiled=...]
    all_to_all x1 -> x0, starting transfers between devices: 6.76 us -> none  [per_device(): lax.all_to_all(payload, ('gx', 'gy'), split_axis=1, concat_axis=1, tiled=...]
    reduce_sum x1, other arithmetic: 6.11 us -> 0.01 us  [per_device(): ocean_flux = jnp.sum(remap_weights[None] * gathered, axis=1)]
    all_to_all x1, local copies, waits for them, and re-layouts: 2.62 us -> 0.03 us  [per_device(): lax.all_to_all(payload, ('gx', 'gy'), split_axis=1, concat_axis=1, tiled=...]
  transfers between devices with their start and end apart: 17 -> 16, of which waited for: 13 -> 12; matrix products, arithmetic and copies ran while one was open for 6% -> 9% of each run, Pallas kernels for 0% -> 0%
where the time goes in v1:
time: 126 us; the launch traced here: 125 us
  local copies, waits for them, and re-layouts  30.6 us (24%)
  waiting for transfers between devices  21.3 us (17%)
  starting transfers between devices  19.6 us (16%)
  other arithmetic  16.8 us (13%)
  blocking collectives  13.7 us (11%)
  Pallas kernels  11.9 us (9%)
  matrix products  9.68 us (8%)
    ppermute x8, waiting for transfers between devices, extended(): lax.ppermute(tail, axis, [(i, (i + 1) % count) for i in range(count)])  15.4 us
    all_to_all x1, blocking collectives, per_device(): lax.all_to_all(payload, ('gx', 'gy'), split_axis=1, concat_axis=1, tiled=...  13.7 us
    ppermute x8, starting transfers between devices, extended(): lax.ppermute(head, axis, [((i + 1) % count, i) for i in range(count)])  12.7 us
    pallas_call x2, Pallas kernels, onehot_gather(): pl.pallas_call(gather_kernel, grid=(count // tile,), in_specs=[pl.BlockSp...  11.9 us
    slice x10, local copies, waits for them, and re-layouts, extended(): lax.slice_in_dim(cells, cells.shape[dim] - width, cells.shape[dim], axis=...  10.6 us
    add x2, other arithmetic, edge_sum(): centre + jnp.where(ypos == 0, padded[:, :, :-2], jnp.where(ypos == 3, pad...  8.47 us
    ppermute x8, starting transfers between devices, extended(): lax.ppermute(tail, axis, [(i, (i + 1) % count) for i in range(count)])  6.88 us
    slice x6, local copies, waits for them, and re-layouts, extended(): head = lax.slice_in_dim(cells, 0, width, axis=dim)  5.91 us
  transfers between devices with their start and end apart: 16, of which 12 were waited for; matrix products, arithmetic and copies ran while one was open for 9% of the time, Pallas kernels for 0%

profile of v1, /device:TPU:0, one launch (start us, length us, event | category | flops | bytes accessed | tf_op | source)
XLA Modules:
  0.0 124.6 jit_solution(16176338103967961793)
XLA Ops:
  2.0 1.2 fusion.12
  3.3 1.2 fusion.11
  4.5 1.2 fusion.8
  5.7 1.2 fusion.7
  7.5 2.0 %collective-permute-start.1 = (f32[160,1,128]{2,1,0:T(1,128)S(1)}, f32[160,1,128]{2,1,0:T(1,128)S(1)}, u32[]{:S(2)}, u32[]{:S(2)}) collective-permute-start(f32[160,1,128]{2,1,0:T(1,128)S(1)} %get-tuple-element.62), channel_id=1, source_target_pairs={{8,0},{16,8},{24,16},{0,24},{9,1},{17,9},{25,17},{1,25},{10,2},{18... | collective-permute-start | bytes 245768 | tf_op jit(solution)/shard_map/ppermute | solution.py:29
  9.6 2.1 %collective-permute-done = f32[160,1,128]{2,1,0:T(1,128)S(1)} collective-permute-done((f32[160,1,128]{2,1,0:T(1,128)S(1)}, f32[160,1,128]{2,1,0:T(1,128)S(1)}, u32[]{:S(2)}, u32[]{:S(2)}) %collective-permute-start) | collective-permute-done | bytes 81952 | tf_op jit(solution)/shard_map/ppermute | solution.py:27
  11.6 0.7 collective-permute-done.1
  12.6 2.5 %fusion.48 = (f32[160,18,1]{2,1,0:T(8,128)}, f32[160,18,1]{2,1,0:T(8,128)}) fusion(f32[160,18,128]{2,1,0:T(8,128)S(1)} %pad_maximum_fusion.12), kind=kLoop, calls=%fused_computation.116 | loop fusion | bytes 46080 | tf_op jit(solution)/shard_map/slice | solution.py:24
  15.1 2.2 %copy.37 = f32[160,18,1]{0,2,1:T(1,128)S(1)} copy(f32[160,18,1]{2,1,0:T(8,128)} %get-tuple-element.57) | data formatting | bytes 23040 | tf_op jit(solution)/shard_map/slice | solution.py:24
  17.3 1.6 %collective-permute-start.2 = (f32[160,18,1]{0,2,1:T(1,128)S(1)}, f32[160,18,1]{0,2,1:T(1,128)S(1)}, u32[]{:S(2)}, u32[]{:S(2)}) collective-permute-start(f32[160,18,1]{0,2,1:T(1,128)S(1)} %copy.37), channel_id=1, source_target_pairs={{0,1},{1,2},{2,3},{3,4},{4,5},{5,6},{6,7},{7,0},{8,9},{9,10},{10,1... | collective-permute-start | bytes 34568 | tf_op jit(solution)/shard_map/ppermute | solution.py:27
  18.9 2.2 %copy.39 = f32[160,18,1]{0,2,1:T(1,128)S(1)} copy(f32[160,18,1]{2,1,0:T(8,128)} %get-tuple-element.58) | data formatting | bytes 23040 | tf_op jit(solution)/shard_map/slice | solution.py:23
  21.2 3.4 %collective-permute-start.3 = (f32[160,18,1]{0,2,1:T(1,128)S(1)}, f32[160,18,1]{0,2,1:T(1,128)S(1)}, u32[]{:S(2)}, u32[]{:S(2)}) collective-permute-start(f32[160,18,1]{0,2,1:T(1,128)S(1)} %copy.39), channel_id=1, source_target_pairs={{1,0},{2,1},{3,2},{4,3},{5,4},{6,5},{7,6},{0,7},{9,8},{10,9},{11,1... | collective-permute-start | bytes 34568 | tf_op jit(solution)/shard_map/ppermute | solution.py:29
  24.5 1.9 %copy.38 = f32[160,18,1]{2,1,0:T(8,128)} copy(f32[160,18,1]{0,2,1:T(1,128)S(1)} %collective-permute-done.2) | data formatting | bytes 23040 | tf_op jit(solution)/shard_map/ppermute | solution.py:27
  26.5 2.0 %copy.40 = f32[160,18,1]{2,1,0:T(8,128)} copy(f32[160,18,1]{0,2,1:T(1,128)S(1)} %collective-permute-done.3) | data formatting | bytes 23040 | tf_op jit(solution)/shard_map/ppermute | solution.py:29
  28.4 4.2 %fusion.5 = f32[160,18,128]{2,1,0:T(8,128)S(1)} fusion(f32[160,18,1]{2,1,0:T(8,128)} %copy.40, f32[160,1,128]{2,1,0:T(1,128)S(1)} %collective-permute-done.1, f32[160,16,128]{2,1,0:T(8,128)S(1)} %fusion.7, f32[160,1,128]{2,1,0:T(1,128)S(1)} %collective-permute-done, f32[160,18,1]{2,1,0:T(8,128)} %copy.38, pred[128]{0:T(512)(128)(4,1)S(1)} %get-tuple-element.85, ...), kind=kLoop, calls=%fused_computation.12 | loop fusion | flops 4055040 | bytes 2972416 | tf_op jit(solution)/shard_map/add | solution.py:97
  33.2 1.2 fusion.9
  34.4 1.2 convolution_multiply_fusion.1
  35.6 1.2 fusion.10
  36.9 1.2 fusion.6
  38.2 1.3 %collective-permute-start.4 = (f32[160,1,128]{2,1,0:T(1,128)S(1)}, f32[160,1,128]{2,1,0:T(1,128)S(1)}, u32[]{:S(2)}, u32[]{:S(2)}) collective-permute-start(f32[160,1,128]{2,1,0:T(1,128)S(1)} %get-tuple-element.59), channel_id=1, source_target_pairs={{0,8},{8,16},{16,24},{24,0},{1,9},{9,17},{17,25},{25,1},{2,10},{10... | collective-permute-start | bytes 245768 | tf_op jit(solution)/shard_map/ppermute | solution.py:27
  40.0 2.1 %collective-permute-done.4 = f32[160,1,128]{2,1,0:T(1,128)S(1)} collective-permute-done((f32[160,1,128]{2,1,0:T(1,128)S(1)}, f32[160,1,128]{2,1,0:T(1,128)S(1)}, u32[]{:S(2)}, u32[]{:S(2)}) %collective-permute-start.4) | collective-permute-done | bytes 81952 | tf_op jit(solution)/shard_map/ppermute | solution.py:27
  43.0 2.5 %fusion.47 = (f32[160,18,1]{2,1,0:T(8,128)}, f32[160,18,1]{2,1,0:T(8,128)}) fusion(f32[160,18,128]{2,1,0:T(8,128)S(1)} %pad_maximum_fusion.13), kind=kLoop, calls=%fused_computation.115 | loop fusion | bytes 46080 | tf_op jit(solution)/shard_map/slice | solution.py:24
  45.5 2.2 %copy.42 = f32[160,18,1]{0,2,1:T(1,128)S(1)} copy(f32[160,18,1]{2,1,0:T(8,128)} %get-tuple-element.55) | data formatting | bytes 23040 | tf_op jit(solution)/shard_map/slice | solution.py:24
  48.3 2.2 %copy.44 = f32[160,18,1]{0,2,1:T(1,128)S(1)} copy(f32[160,18,1]{2,1,0:T(8,128)} %get-tuple-element.56) | data formatting | bytes 23040 | tf_op jit(solution)/shard_map/slice | solution.py:23
  50.5 4.5 %collective-permute-start.7 = (f32[160,18,1]{0,2,1:T(1,128)S(1)}, f32[160,18,1]{0,2,1:T(1,128)S(1)}, u32[]{:S(2)}, u32[]{:S(2)}) collective-permute-start(f32[160,18,1]{0,2,1:T(1,128)S(1)} %copy.44), channel_id=1, source_target_pairs={{1,0},{2,1},{3,2},{4,3},{5,4},{6,5},{7,6},{0,7},{9,8},{10,9},{11,1... | collective-permute-start | bytes 34568 | tf_op jit(solution)/shard_map/ppermute | solution.py:29
  55.1 0.7 copy.61
  55.7 1.9 %copy.43 = f32[160,18,1]{2,1,0:T(8,128)} copy(f32[160,18,1]{0,2,1:T(1,128)S(1)} %collective-permute-done.6) | data formatting | bytes 23040 | tf_op jit(solution)/shard_map/ppermute | solution.py:27
  57.7 2.0 %copy.45 = f32[160,18,1]{2,1,0:T(8,128)} copy(f32[160,18,1]{0,2,1:T(1,128)S(1)} %collective-permute-done.7) | data formatting | bytes 23040 | tf_op jit(solution)/shard_map/ppermute | solution.py:29
  59.6 4.2 %fusion.2 = f32[160,18,128]{2,1,0:T(8,128)S(1)} fusion(f32[160,18,1]{2,1,0:T(8,128)} %copy.45, f32[160,1,128]{2,1,0:T(1,128)S(1)} %collective-permute-done.5, f32[160,16,128]{2,1,0:T(8,128)S(1)} %fusion.6, f32[160,1,128]{2,1,0:T(1,128)S(1)} %collective-permute-done.4, f32[160,18,1]{2,1,0:T(8,128)} %copy.43, pred[128]{0:T(512)(128)(4,1)S(1)} %get-tuple-element.85, ...), kind=kLoop, calls=%fused_computation.3 | loop fusion | flops 4055040 | bytes 2972416 | tf_op jit(solution)/shard_map/add | solution.py:97
  64.4 1.0 copy-done.5
  66.0 5.3 %shard_map.176 = f32[4,8192]{1,0:T(4,128)} custom-call(s32[1,8192]{1,0:T(1,128)} %bitcast.91, bf16[4,48,128]{2,1,0:T(8,128)(2,1)} %bitcast.90), custom_call_target="tpu_custom_call" | custom-call | tf_op jit(solution)/shard_map/pallas_call | solution.py:146
  71.3 0.9 broadcast_multiply_fusion
  72.3 13.7 %all_to_all.5 = f32[4,32,256]{2,0,1:T(4,128)S(1)} all-to-all(f32[4,32,256]{2,0,1:T(4,128)S(1)} %broadcast_multiply_fusion), channel_id=1, replica_groups=mesh['gx'=4,'gy'=8] {'gx','gy'}, dimensions={1} | all-to-all | bytes 262144 | tf_op jit(solution)/shard_map/all_to_all | solution.py:187
  86.1 0.7 copy.48
  86.8 6.6 %shard_map.177 = f32[4,8192]{1,0:T(4,128)} custom-call(s32[1,8192]{1,0:T(1,128)} %bitcast.93, bf16[4,192,128]{2,1,0:T(8,128)(2,1)} %bitcast.86), custom_call_target="tpu_custom_call" | custom-call | tf_op jit(solution)/shard_map/pallas_call | solution.py:146
  93.4 0.9 copy.62
  95.0 1.5 %collective-permute-done.8 = f32[2,40,1,128]{3,2,1,0:T(1,128)S(1)} collective-permute-done((f32[2,40,1,128]{3,2,1,0:T(1,128)S(1)}, f32[2,40,1,128]{3,2,1,0:T(1,128)S(1)}, u32[]{:S(2)}, u32[]{:S(2)}) %collective-permute-start.8) | collective-permute-done | bytes 40992 | tf_op jit(solution)/shard_map/ppermute | solution.py:29
  96.5 2.1 %collective-permute-done.9 = f32[2,40,1,128]{3,2,1,0:T(1,128)S(1)} collective-permute-done((f32[2,40,1,128]{3,2,1,0:T(1,128)S(1)}, f32[2,40,1,128]{3,2,1,0:T(1,128)S(1)}, u32[]{:S(2)}, u32[]{:S(2)}) %collective-permute-start.9) | collective-permute-done | bytes 40992 | tf_op jit(solution)/shard_map/ppermute | solution.py:27
  99.5 1.9 %collective-permute-start.10 = (f32[2,40,18,1]{1,2,3,0:T(8,128)S(1)}, f32[2,40,18,1]{1,2,3,0:T(8,128)S(1)}, u32[]{:S(2)}, u32[]{:S(2)}) collective-permute-start(f32[2,40,18,1]{1,2,3,0:T(8,128)S(1)} %copy.49), channel_id=1, source_target_pairs={{1,0},{2,1},{3,2},{4,3},{5,4},{6,5},{7,6},{0,7},{9,8},{10,9},{11,1... | collective-permute-start | bytes 17288 | tf_op jit(solution)/shard_map/ppermute | solution.py:29
  102.0 0.9 fusion.22
  103.8 4.6 %collective-permute-done.11 = f32[2,40,18,1]{1,2,3,0:T(8,128)S(1)} collective-permute-done((f32[2,40,18,1]{1,2,3,0:T(8,128)S(1)}, f32[2,40,18,1]{1,2,3,0:T(8,128)S(1)}, u32[]{:S(2)}, u32[]{:S(2)}) %collective-permute-start.11) | collective-permute-done | bytes 5792 | tf_op jit(solution)/shard_map/ppermute | solution.py:27
  108.9 2.0 %multiply_subtract_fusion.1 = f32[2,40,16,128]{3,2,1,0:T(8,128)S(1)} fusion(f32[2,40,16,128]{3,2,1,0:T(8,128)S(1)} %get-tuple-element.77, f32[2,40,1,128]{3,2,1,0:T(1,128)S(1)} %collective-permute-done.8, f32[2,40,1,128]{3,2,1,0:T(1,128)S(1)} %collective-permute-done.9, f32[2,40,18,1]{3,2,1,0:T(8,128)S(1)} %copy.52, f32[2,40,18,1]{3,2,1,0:T(8,128)S(1)} %copy.50, ...), kind=kLoop, calls=%fused_computation.64 | loop fusion | flops 3440640 | bytes 2059520 | tf_op jit(solution)/shard_map/sub | solution.py:113
  111.5 1.2 collective-permute-done.12
  112.7 1.8 %collective-permute-done.13 = f32[2,40,1,128]{3,2,1,0:T(1,128)S(1)} collective-permute-done((f32[2,40,1,128]{3,2,1,0:T(1,128)S(1)}, f32[2,40,1,128]{3,2,1,0:T(1,128)S(1)}, u32[]{:S(2)}, u32[]{:S(2)}) %collective-permute-start.13) | collective-permute-done | bytes 40992 | tf_op jit(solution)/shard_map/ppermute | solution.py:27
  115.8 2.0 %collective-permute-start.15 = (f32[2,40,18,1]{1,2,3,0:T(8,128)S(1)}, f32[2,40,18,1]{1,2,3,0:T(8,128)S(1)}, u32[]{:S(2)}, u32[]{:S(2)}) collective-permute-start(f32[2,40,18,1]{1,2,3,0:T(8,128)S(1)} %copy.55), channel_id=1, source_target_pairs={{0,1},{1,2},{2,3},{3,4},{4,5},{5,6},{6,7},{7,0},{8,9},{9,10},{10,1... | collective-permute-start | bytes 17288 | tf_op jit(solution)/shard_map/ppermute | solution.py:27
  117.9 1.4 %collective-permute-done.14 = f32[2,40,18,1]{1,2,3,0:T(8,128)S(1)} collective-permute-done((f32[2,40,18,1]{1,2,3,0:T(8,128)S(1)}, f32[2,40,18,1]{1,2,3,0:T(8,128)S(1)}, u32[]{:S(2)}, u32[]{:S(2)}) %collective-permute-start.14) | collective-permute-done | bytes 5792 | tf_op jit(solution)/shard_map/ppermute | solution.py:29
  119.7 2.7 %collective-permute-done.15 = f32[2,40,18,1]{1,2,3,0:T(8,128)S(1)} collective-permute-done((f32[2,40,18,1]{1,2,3,0:T(8,128)S(1)}, f32[2,40,18,1]{1,2,3,0:T(8,128)S(1)}, u32[]{:S(2)}, u32[]{:S(2)}) %collective-permute-start.15) | collective-permute-done | bytes 5792 | tf_op jit(solution)/shard_map/ppermute | solution.py:27
  122.9 1.8 %multiply_subtract_fusion = f32[2,40,16,128]{3,2,1,0:T(8,128)} fusion(f32[2,40,16,128]{3,2,1,0:T(8,128)S(1)} %multiply_subtract_fusion.1, f32[2,40,1,128]{3,2,1,0:T(1,128)S(1)} %collective-permute-done.12, f32[2,40,1,128]{3,2,1,0:T(1,128)S(1)} %collective-permute-done.13, f32[2,40,18,1]{3,2,1,0:T(8,128)S(1)} %copy.56, f32[2,40,18,1]{3,2,1,0:T(8,128)S(1)} %copy.54, ...), kind=kLoop, calls=%fused_computation.63 | loop fusion | flops 3440640 | bytes 2059520 | tf_op jit(solution)/shard_map/sub | solution.py:113
  (78 shorter events, 12.5 us)
Async XLA Ops:
  0.6 0.7 copy-start.12
  0.6 0.7 copy-start.13
  0.7 0.9 copy-start.7
  0.7 1.3 %copy-start = (f32[4,40,16,128]{3,2,1,0:T(8,128)S(1)}, f32[4,40,16,128]{3,2,1,0:T(8,128)}, u32[]{:S(2)}) copy-start(f32[4,40,16,128]{3,2,1,0:T(8,128)} %param.25) | copy-start | bytes 3932164
  0.7 0.8 copy-start.11
  3.2 1.3 %copy-start.6 = (f32[128,128,1]{1,0,2:T(8,128)S(1)}, f32[128,128,1]{1,0,2:T(8,128)}, u32[]{:S(2)}) copy-start(f32[128,128,1]{1,0,2:T(8,128)} %constant.172) | copy-start | bytes 196612
  7.0 4.6 %collective-permute-start = (f32[160,1,128]{2,1,0:T(1,128)S(1)}, f32[160,1,128]{2,1,0:T(1,128)S(1)}, u32[]{:S(2)}, u32[]{:S(2)}) collective-permute-start(f32[160,1,128]{2,1,0:T(1,128)S(1)} %get-tuple-element.61), channel_id=1, source_target_pairs={{0,8},{8,16},{16,24},{24,0},{1,9},{9,17},{17,25},{25,1},{2,10},{10... | collective-permute-start | bytes 245768 | tf_op jit(solution)/shard_map/ppermute | solution.py:27
  7.5 4.8 %collective-permute-start.1 = (f32[160,1,128]{2,1,0:T(1,128)S(1)}, f32[160,1,128]{2,1,0:T(1,128)S(1)}, u32[]{:S(2)}, u32[]{:S(2)}) collective-permute-start(f32[160,1,128]{2,1,0:T(1,128)S(1)} %get-tuple-element.62), channel_id=1, source_target_pairs={{8,0},{16,8},{24,16},{0,24},{9,1},{17,9},{25,17},{1,25},{10,2},{18... | collective-permute-start | bytes 245768 | tf_op jit(solution)/shard_map/ppermute | solution.py:29
  17.3 7.2 %collective-permute-start.2 = (f32[160,18,1]{0,2,1:T(1,128)S(1)}, f32[160,18,1]{0,2,1:T(1,128)S(1)}, u32[]{:S(2)}, u32[]{:S(2)}) collective-permute-start(f32[160,18,1]{0,2,1:T(1,128)S(1)} %copy.37), channel_id=1, source_target_pairs={{0,1},{1,2},{2,3},{3,4},{4,5},{5,6},{6,7},{7,0},{8,9},{9,10},{10,1... | collective-permute-start | bytes 34568 | tf_op jit(solution)/shard_map/ppermute | solution.py:27
  21.2 5.3 %collective-permute-start.3 = (f32[160,18,1]{0,2,1:T(1,128)S(1)}, f32[160,18,1]{0,2,1:T(1,128)S(1)}, u32[]{:S(2)}, u32[]{:S(2)}) collective-permute-start(f32[160,18,1]{0,2,1:T(1,128)S(1)} %copy.39), channel_id=1, source_target_pairs={{1,0},{2,1},{3,2},{4,3},{5,4},{6,5},{7,6},{0,7},{9,8},{10,9},{11,1... | collective-permute-start | bytes 34568 | tf_op jit(solution)/shard_map/ppermute | solution.py:29
  28.4 4.3 %copy-start.8 = (f32[16,128]{1,0:T(8,128)S(1)}, f32[16,128]{1,0:T(8,128)}, u32[]{:S(2)}) copy-start(f32[16,128]{1,0:T(8,128)} %constant.170) | copy-start | bytes 24580
  38.2 3.9 %collective-permute-start.4 = (f32[160,1,128]{2,1,0:T(1,128)S(1)}, f32[160,1,128]{2,1,0:T(1,128)S(1)}, u32[]{:S(2)}, u32[]{:S(2)}) collective-permute-start(f32[160,1,128]{2,1,0:T(1,128)S(1)} %get-tuple-element.59), channel_id=1, source_target_pairs={{0,8},{8,16},{16,24},{24,0},{1,9},{9,17},{17,25},{25,1},{2,10},{10... | collective-permute-start | bytes 245768 | tf_op jit(solution)/shard_map/ppermute | solution.py:27
  39.5 3.2 %collective-permute-start.5 = (f32[160,1,128]{2,1,0:T(1,128)S(1)}, f32[160,1,128]{2,1,0:T(1,128)S(1)}, u32[]{:S(2)}, u32[]{:S(2)}) collective-permute-start(f32[160,1,128]{2,1,0:T(1,128)S(1)} %get-tuple-element.60), channel_id=1, source_target_pairs={{8,0},{16,8},{24,16},{0,24},{9,1},{17,9},{25,17},{1,25},{10,2},{18... | collective-permute-start | bytes 245768 | tf_op jit(solution)/shard_map/ppermute | solution.py:29
  47.7 7.3 %copy-start.14 = (s32[1,32]{1,0:T(1,128)S(1)}, s32[1,32]{1,0:T(1,128)}, u32[]{:S(2)}) copy-start(s32[1,32]{1,0:T(1,128)} %param.28) | copy-start | bytes 388
  47.7 7.4 %copy-start.9 = (s32[1,32,256]{2,1,0:T(8,128)S(1)}, s32[1,32,256]{2,1,0:T(8,128)}, u32[]{:S(2)}) copy-start(s32[1,32,256]{2,1,0:T(8,128)} %param.27) | copy-start | bytes 98308
  47.7 8.0 %collective-permute-start.6 = (f32[160,18,1]{0,2,1:T(1,128)S(1)}, f32[160,18,1]{0,2,1:T(1,128)S(1)}, u32[]{:S(2)}, u32[]{:S(2)}) collective-permute-start(f32[160,18,1]{0,2,1:T(1,128)S(1)} %copy.42), channel_id=1, source_target_pairs={{0,1},{1,2},{2,3},{3,4},{4,5},{5,6},{6,7},{7,0},{8,9},{9,10},{10,1... | collective-permute-start | bytes 34568 | tf_op jit(solution)/shard_map/ppermute | solution.py:27
  50.5 7.1 %collective-permute-start.7 = (f32[160,18,1]{0,2,1:T(1,128)S(1)}, f32[160,18,1]{0,2,1:T(1,128)S(1)}, u32[]{:S(2)}, u32[]{:S(2)}) collective-permute-start(f32[160,18,1]{0,2,1:T(1,128)S(1)} %copy.44), channel_id=1, source_target_pairs={{1,0},{2,1},{3,2},{4,3},{5,4},{6,5},{7,6},{0,7},{9,8},{10,9},{11,1... | collective-permute-start | bytes 34568 | tf_op jit(solution)/shard_map/ppermute | solution.py:29
  64.3 1.1 copy-start.5
  72.3 22.0 %copy-start.10 = (f32[4,16,128]{2,1,0:T(8,128)S(1)}, f32[4,16,128]{2,1,0:T(8,128)}, u32[]{:S(2)}) copy-start(f32[4,16,128]{2,1,0:T(8,128)} %param.32) | copy-start | bytes 98308
  72.3 22.1 %copy-start.1 = (f32[2,40,16,128]{3,2,1,0:T(8,128)S(1)}, f32[2,40,16,128]{3,2,1,0:T(8,128)}, u32[]{:S(2)}) copy-start(f32[2,40,16,128]{3,2,1,0:T(8,128)} %param.29) | copy-start | bytes 1966084
  72.3 22.1 %copy-start.4 = (f32[2,40,16,128]{3,2,1,0:T(8,128)S(1)}, f32[2,40,16,128]{3,2,1,0:T(8,128)}, u32[]{:S(2)}) copy-start(f32[2,40,16,128]{3,2,1,0:T(8,128)} %param.30) | copy-start | bytes 1966084
  94.5 2.1 %collective-permute-start.8 = (f32[2,40,1,128]{3,2,1,0:T(1,128)S(1)}, f32[2,40,1,128]{3,2,1,0:T(1,128)S(1)}, u32[]{:S(2)}, u32[]{:S(2)}) collective-permute-start(f32[2,40,1,128]{3,2,1,0:T(1,128)S(1)} %get-tuple-element.72), channel_id=1, source_target_pairs={{8,0},{16,8},{24,16},{0,24},{9,1},{17,9},{25,17},{1,25},{10,2},{18... | collective-permute-start | bytes 122888 | tf_op jit(solution)/shard_map/ppermute | solution.py:29
  94.9 3.8 %collective-permute-start.9 = (f32[2,40,1,128]{3,2,1,0:T(1,128)S(1)}, f32[2,40,1,128]{3,2,1,0:T(1,128)S(1)}, u32[]{:S(2)}, u32[]{:S(2)}) collective-permute-start(f32[2,40,1,128]{3,2,1,0:T(1,128)S(1)} %get-tuple-element.71), channel_id=1, source_target_pairs={{0,8},{8,16},{16,24},{24,0},{1,9},{9,17},{17,25},{25,1},{2,10},{10... | collective-permute-start | bytes 122888 | tf_op jit(solution)/shard_map/ppermute | solution.py:27
  99.5 3.9 %collective-permute-start.10 = (f32[2,40,18,1]{1,2,3,0:T(8,128)S(1)}, f32[2,40,18,1]{1,2,3,0:T(8,128)S(1)}, u32[]{:S(2)}, u32[]{:S(2)}) collective-permute-start(f32[2,40,18,1]{1,2,3,0:T(8,128)S(1)} %copy.49), channel_id=1, source_target_pairs={{1,0},{2,1},{3,2},{4,3},{5,4},{6,5},{7,6},{0,7},{9,8},{10,9},{11,1... | collective-permute-start | bytes 17288 | tf_op jit(solution)/shard_map/ppermute | solution.py:29
  101.9 6.6 %collective-permute-start.11 = (f32[2,40,18,1]{1,2,3,0:T(8,128)S(1)}, f32[2,40,18,1]{1,2,3,0:T(8,128)S(1)}, u32[]{:S(2)}, u32[]{:S(2)}) collective-permute-start(f32[2,40,18,1]{1,2,3,0:T(8,128)S(1)} %copy.51), channel_id=1, source_target_pairs={{0,1},{1,2},{2,3},{3,4},{4,5},{5,6},{6,7},{7,0},{8,9},{9,10},{10,1... | collective-permute-start | bytes 17288 | tf_op jit(solution)/shard_map/ppermute | solution.py:27
  110.9 1.7 %collective-permute-start.12 = (f32[2,40,1,128]{3,2,1,0:T(1,128)S(1)}, f32[2,40,1,128]{3,2,1,0:T(1,128)S(1)}, u32[]{:S(2)}, u32[]{:S(2)}) collective-permute-start(f32[2,40,1,128]{3,2,1,0:T(1,128)S(1)} %get-tuple-element.68), channel_id=1, source_target_pairs={{8,0},{16,8},{24,16},{0,24},{9,1},{17,9},{25,17},{1,25},{10,2},{18... | collective-permute-start | bytes 122888 | tf_op jit(solution)/shard_map/ppermute | solution.py:29
  111.0 3.5 %collective-permute-start.13 = (f32[2,40,1,128]{3,2,1,0:T(1,128)S(1)}, f32[2,40,1,128]{3,2,1,0:T(1,128)S(1)}, u32[]{:S(2)}, u32[]{:S(2)}) collective-permute-start(f32[2,40,1,128]{3,2,1,0:T(1,128)S(1)} %get-tuple-element.67), channel_id=1, source_target_pairs={{0,8},{8,16},{16,24},{24,0},{1,9},{9,17},{17,25},{25,1},{2,10},{10... | collective-permute-start | bytes 122888 | tf_op jit(solution)/shard_map/ppermute | solution.py:27
  115.4 3.9 %collective-permute-start.14 = (f32[2,40,18,1]{1,2,3,0:T(8,128)S(1)}, f32[2,40,18,1]{1,2,3,0:T(8,128)S(1)}, u32[]{:S(2)}, u32[]{:S(2)}) collective-permute-start(f32[2,40,18,1]{1,2,3,0:T(8,128)S(1)} %copy.53), channel_id=1, source_target_pairs={{1,0},{2,1},{3,2},{4,3},{5,4},{6,5},{7,6},{0,7},{9,8},{10,9},{11,1... | collective-permute-start | bytes 17288 | tf_op jit(solution)/shard_map/ppermute | solution.py:29
  115.4 7.4 %copy-start.2 = (f32[40,16,128]{2,1,0:T(8,128)S(1)}, f32[40,16,128]{2,1,0:T(8,128)}, u32[]{:S(2)}) copy-start(f32[40,16,128]{2,1,0:T(8,128)} %get-tuple-element.69) | copy-start | bytes 983044
  115.4 7.4 %copy-start.3 = (f32[40,16,128]{2,1,0:T(8,128)S(1)}, f32[40,16,128]{2,1,0:T(8,128)}, u32[]{:S(2)}) copy-start(f32[40,16,128]{2,1,0:T(8,128)} %get-tuple-element.70) | copy-start | bytes 983044
  115.8 6.6 %collective-permute-start.15 = (f32[2,40,18,1]{1,2,3,0:T(8,128)S(1)}, f32[2,40,18,1]{1,2,3,0:T(8,128)S(1)}, u32[]{:S(2)}, u32[]{:S(2)}) collective-permute-start(f32[2,40,18,1]{1,2,3,0:T(8,128)S(1)} %copy.55), channel_id=1, source_target_pairs={{0,1},{1,2},{2,3},{3,4},{4,5},{5,6},{6,7},{7,0},{8,9},{9,10},{10,1... | collective-permute-start | bytes 17288 | tf_op jit(solution)/shard_map/ppermute | solution.py:27

commit v2 on v1

--- a/solution.py
+++ b/solution.py
@@ -117,29 +117,24 @@
     )
 
 
-def split_bf16(values):
-    first = values.astype(jnp.bfloat16)
-    rest = values - first.astype(jnp.float32)
-    second = rest.astype(jnp.bfloat16)
-    third = (rest - second.astype(jnp.float32)).astype(jnp.bfloat16)
-    return jnp.stack([first, second, third], axis=1)
-
-
 def gather_kernel(index_ref, table_ref, out_ref):
-    fields, rows, tile = out_ref.shape[0], table_ref.shape[1] // 3, out_ref.shape[1]
+    fields, rows, tile = table_ref.shape[0], table_ref.shape[1], out_ref.shape[1]
     index = index_ref[...]
     onehot = (lax.broadcasted_iota(jnp.int32, (128, tile), 0) == (index & 127)).astype(jnp.bfloat16)
     select = lax.broadcasted_iota(jnp.int32, (rows, tile), 0) == (index >> 7)
     for field in range(fields):
-        picked = jnp.dot(table_ref[field], onehot, preferred_element_type=jnp.float32)
-        whole = picked[:rows] + picked[rows : 2 * rows] + picked[2 * rows :]
+        rest = table_ref[field]
+        whole = jnp.zeros((rows, tile), jnp.float32)
+        for part in range(3):
+            piece = rest.astype(jnp.bfloat16)
+            rest = rest - piece.astype(jnp.float32)
+            whole = whole + jnp.dot(piece, onehot, preferred_element_type=jnp.float32)
         out_ref[pl.ds(field, 1), :] = jnp.sum(jnp.where(select, whole, 0.0), axis=0, keepdims=True)
 
 
 def onehot_gather(table, index):
     fields, total = table.shape
     rows = total // 128
-    parts = split_bf16(table.reshape(fields, rows, 128)).reshape(fields, 3 * rows, 128)
     flat = index.reshape(1, -1)
     count = flat.shape[1]
     tile = math.gcd(count, 1024)
@@ -148,11 +143,11 @@
         grid=(count // tile,),
         in_specs=[
             pl.BlockSpec((1, tile), lambda step: (0, step)),
-            pl.BlockSpec((fields, 3 * rows, 128), lambda step: (0, 0, 0)),
+            pl.BlockSpec((fields, rows, 128), lambda step: (0, 0, 0)),
         ],
         out_specs=pl.BlockSpec((fields, tile), lambda step: (0, step)),
         out_shape=jax.ShapeDtypeStruct((fields, count), jnp.float32),
-    )(flat, parts)
+    )(flat, table.reshape(fields, rows, 128))
 
 
 def per_device(

time: 126 us -> 127 us (level)
  no operation moved by 1% of the time
where the time goes in v2:
time: 127 us; the launch traced here: 126 us
  local copies, waits for them, and re-layouts  30.5 us (24%)
  waiting for transfers between devices  21.3 us (17%)
  starting transfers between devices  19.6 us (15%)
  other arithmetic  16.8 us (13%)
  blocking collectives  13.7 us (11%)
  Pallas kernels  13.1 us (10%)
  matrix products  9.68 us (8%)
    ppermute x8, waiting for transfers between devices, extended(): lax.ppermute(tail, axis, [(i, (i + 1) % count) for i in range(count)])  15.4 us
    all_to_all x1, blocking collectives, per_device(): lax.all_to_all(payload, ('gx', 'gy'), split_axis=1, concat_axis=1, tiled=...  13.7 us
    pallas_call x2, Pallas kernels, onehot_gather(): pl.pallas_call(gather_kernel, grid=(count // tile,), in_specs=[pl.BlockSp...  13.1 us
    ppermute x8, starting transfers between devices, extended(): lax.ppermute(head, axis, [((i + 1) % count, i) for i in range(count)])  12.8 us
    slice x10, local copies, waits for them, and re-layouts, extended(): lax.slice_in_dim(cells, cells.shape[dim] - width, cells.shape[dim], axis=...  10.6 us
    add x2, other arithmetic, edge_sum(): centre + jnp.where(ypos == 0, padded[:, :, :-2], jnp.where(ypos == 3, pad...  8.47 us
    ppermute x8, starting transfers between devices, extended(): lax.ppermute(tail, axis, [(i, (i + 1) % count) for i in range(count)])  6.87 us
    slice x6, local copies, waits for them, and re-layouts, extended(): head = lax.slice_in_dim(cells, 0, width, axis=dim)  5.91 us
  transfers between devices with their start and end apart: 16, of which 12 were waited for; matrix products, arithmetic and copies ran while one was open for 9% of the time, Pallas kernels for 0%

profile of v2, /device:TPU:0, one launch (start us, length us, event | category | flops | bytes accessed | tf_op | source)
XLA Modules:
  0.0 125.7 jit_solution(4655848697680170038)
XLA Ops:
  2.0 1.2 fusion.12
  3.3 1.2 fusion.11
  4.5 1.2 fusion.8
  5.7 1.2 fusion.7
  7.5 2.0 %collective-permute-start.1 = (f32[160,1,128]{2,1,0:T(1,128)S(1)}, f32[160,1,128]{2,1,0:T(1,128)S(1)}, u32[]{:S(2)}, u32[]{:S(2)}) collective-permute-start(f32[160,1,128]{2,1,0:T(1,128)S(1)} %get-tuple-element.61), channel_id=1, source_target_pairs={{8,0},{16,8},{24,16},{0,24},{9,1},{17,9},{25,17},{1,25},{10,2},{18... | collective-permute-start | bytes 245768 | tf_op jit(solution)/shard_map/ppermute | solution.py:29
  9.6 2.1 %collective-permute-done = f32[160,1,128]{2,1,0:T(1,128)S(1)} collective-permute-done((f32[160,1,128]{2,1,0:T(1,128)S(1)}, f32[160,1,128]{2,1,0:T(1,128)S(1)}, u32[]{:S(2)}, u32[]{:S(2)}) %collective-permute-start) | collective-permute-done | bytes 81952 | tf_op jit(solution)/shard_map/ppermute | solution.py:27
  11.6 0.7 collective-permute-done.1
  12.6 2.5 %fusion.44 = (f32[160,18,1]{2,1,0:T(8,128)}, f32[160,18,1]{2,1,0:T(8,128)}) fusion(f32[160,18,128]{2,1,0:T(8,128)S(1)} %pad_maximum_fusion.12), kind=kLoop, calls=%fused_computation.108 | loop fusion | bytes 46080 | tf_op jit(solution)/shard_map/slice | solution.py:24
  15.1 2.2 %copy.43 = f32[160,18,1]{0,2,1:T(1,128)S(1)} copy(f32[160,18,1]{2,1,0:T(8,128)} %get-tuple-element.56) | data formatting | bytes 23040 | tf_op jit(solution)/shard_map/slice | solution.py:24
  17.3 1.6 %collective-permute-start.2 = (f32[160,18,1]{0,2,1:T(1,128)S(1)}, f32[160,18,1]{0,2,1:T(1,128)S(1)}, u32[]{:S(2)}, u32[]{:S(2)}) collective-permute-start(f32[160,18,1]{0,2,1:T(1,128)S(1)} %copy.43), channel_id=1, source_target_pairs={{0,1},{1,2},{2,3},{3,4},{4,5},{5,6},{6,7},{7,0},{8,9},{9,10},{10,1... | collective-permute-start | bytes 34568 | tf_op jit(solution)/shard_map/ppermute | solution.py:27
  18.9 2.2 %copy.45 = f32[160,18,1]{0,2,1:T(1,128)S(1)} copy(f32[160,18,1]{2,1,0:T(8,128)} %get-tuple-element.57) | data formatting | bytes 23040 | tf_op jit(solution)/shard_map/slice | solution.py:23
  21.2 3.4 %collective-permute-start.3 = (f32[160,18,1]{0,2,1:T(1,128)S(1)}, f32[160,18,1]{0,2,1:T(1,128)S(1)}, u32[]{:S(2)}, u32[]{:S(2)}) collective-permute-start(f32[160,18,1]{0,2,1:T(1,128)S(1)} %copy.45), channel_id=1, source_target_pairs={{1,0},{2,1},{3,2},{4,3},{5,4},{6,5},{7,6},{0,7},{9,8},{10,9},{11,1... | collective-permute-start | bytes 34568 | tf_op jit(solution)/shard_map/ppermute | solution.py:29
  24.5 1.9 %copy.44 = f32[160,18,1]{2,1,0:T(8,128)} copy(f32[160,18,1]{0,2,1:T(1,128)S(1)} %collective-permute-done.2) | data formatting | bytes 23040 | tf_op jit(solution)/shard_map/ppermute | solution.py:27
  26.5 2.0 %copy.46 = f32[160,18,1]{2,1,0:T(8,128)} copy(f32[160,18,1]{0,2,1:T(1,128)S(1)} %collective-permute-done.3) | data formatting | bytes 23040 | tf_op jit(solution)/shard_map/ppermute | solution.py:29
  28.4 4.2 %fusion.5 = f32[160,18,128]{2,1,0:T(8,128)S(1)} fusion(f32[160,18,1]{2,1,0:T(8,128)} %copy.46, f32[160,1,128]{2,1,0:T(1,128)S(1)} %collective-permute-done.1, f32[160,16,128]{2,1,0:T(8,128)S(1)} %fusion.7, f32[160,1,128]{2,1,0:T(1,128)S(1)} %collective-permute-done, f32[160,18,1]{2,1,0:T(8,128)} %copy.44, pred[128]{0:T(512)(128)(4,1)S(1)} %get-tuple-element.81, ...), kind=kLoop, calls=%fused_computation.12 | loop fusion | flops 4055040 | bytes 2972416 | tf_op jit(solution)/shard_map/add | solution.py:97
  33.2 1.2 fusion.9
  34.4 1.2 convolution_multiply_fusion.1
  35.6 1.2 fusion.10
  36.9 1.2 fusion.6
  38.2 1.3 %collective-permute-start.4 = (f32[160,1,128]{2,1,0:T(1,128)S(1)}, f32[160,1,128]{2,1,0:T(1,128)S(1)}, u32[]{:S(2)}, u32[]{:S(2)}) collective-permute-start(f32[160,1,128]{2,1,0:T(1,128)S(1)} %get-tuple-element.58), channel_id=1, source_target_pairs={{0,8},{8,16},{16,24},{24,0},{1,9},{9,17},{17,25},{25,1},{2,10},{10... | collective-permute-start | bytes 245768 | tf_op jit(solution)/shard_map/ppermute | solution.py:27
  40.0 2.1 %collective-permute-done.4 = f32[160,1,128]{2,1,0:T(1,128)S(1)} collective-permute-done((f32[160,1,128]{2,1,0:T(1,128)S(1)}, f32[160,1,128]{2,1,0:T(1,128)S(1)}, u32[]{:S(2)}, u32[]{:S(2)}) %collective-permute-start.4) | collective-permute-done | bytes 81952 | tf_op jit(solution)/shard_map/ppermute | solution.py:27
  43.0 2.5 %fusion.43 = (f32[160,18,1]{2,1,0:T(8,128)}, f32[160,18,1]{2,1,0:T(8,128)}) fusion(f32[160,18,128]{2,1,0:T(8,128)S(1)} %pad_maximum_fusion.13), kind=kLoop, calls=%fused_computation.107 | loop fusion | bytes 46080 | tf_op jit(solution)/shard_map/slice | solution.py:24
  45.5 2.2 %copy.48 = f32[160,18,1]{0,2,1:T(1,128)S(1)} copy(f32[160,18,1]{2,1,0:T(8,128)} %get-tuple-element.54) | data formatting | bytes 23040 | tf_op jit(solution)/shard_map/slice | solution.py:24
  48.3 2.2 %copy.50 = f32[160,18,1]{0,2,1:T(1,128)S(1)} copy(f32[160,18,1]{2,1,0:T(8,128)} %get-tuple-element.55) | data formatting | bytes 23040 | tf_op jit(solution)/shard_map/slice | solution.py:23
  50.6 4.5 %collective-permute-start.7 = (f32[160,18,1]{0,2,1:T(1,128)S(1)}, f32[160,18,1]{0,2,1:T(1,128)S(1)}, u32[]{:S(2)}, u32[]{:S(2)}) collective-permute-start(f32[160,18,1]{0,2,1:T(1,128)S(1)} %copy.50), channel_id=1, source_target_pairs={{1,0},{2,1},{3,2},{4,3},{5,4},{6,5},{7,6},{0,7},{9,8},{10,9},{11,1... | collective-permute-start | bytes 34568 | tf_op jit(solution)/shard_map/ppermute | solution.py:29
  55.1 0.7 copy.68
  55.7 1.9 %copy.49 = f32[160,18,1]{2,1,0:T(8,128)} copy(f32[160,18,1]{0,2,1:T(1,128)S(1)} %collective-permute-done.6) | data formatting | bytes 23040 | tf_op jit(solution)/shard_map/ppermute | solution.py:27
  57.7 2.0 %copy.51 = f32[160,18,1]{2,1,0:T(8,128)} copy(f32[160,18,1]{0,2,1:T(1,128)S(1)} %collective-permute-done.7) | data formatting | bytes 23040 | tf_op jit(solution)/shard_map/ppermute | solution.py:29
  59.6 4.2 %fusion.2 = f32[160,18,128]{2,1,0:T(8,128)S(1)} fusion(f32[160,18,1]{2,1,0:T(8,128)} %copy.51, f32[160,1,128]{2,1,0:T(1,128)S(1)} %collective-permute-done.5, f32[160,16,128]{2,1,0:T(8,128)S(1)} %fusion.6, f32[160,1,128]{2,1,0:T(1,128)S(1)} %collective-permute-done.4, f32[160,18,1]{2,1,0:T(8,128)} %copy.49, pred[128]{0:T(512)(128)(4,1)S(1)} %get-tuple-element.81, ...), kind=kLoop, calls=%fused_computation.3 | loop fusion | flops 4055040 | bytes 2972416 | tf_op jit(solution)/shard_map/add | solution.py:97
  64.4 1.0 copy-done.5
  66.0 6.2 %shard_map.176 = f32[4,8192]{1,0:T(4,128)} custom-call(s32[1,8192]{1,0:T(1,128)} %bitcast.93, f32[4,16,128]{2,1,0:T(8,128)} %fusion.23.table_ref), custom_call_target="tpu_custom_call" | custom-call | tf_op jit(solution)/shard_map/pallas_call | solution.py:141
  72.2 0.9 broadcast_multiply_fusion
  73.2 13.7 %all_to_all.5 = f32[4,32,256]{2,0,1:T(4,128)S(1)} all-to-all(f32[4,32,256]{2,0,1:T(4,128)S(1)} %broadcast_multiply_fusion), channel_id=1, replica_groups=mesh['gx'=4,'gy'=8] {'gx','gy'}, dimensions={1} | all-to-all | bytes 262144 | tf_op jit(solution)/shard_map/all_to_all | solution.py:182
  86.9 0.7 reshape_reshape.3.table_ref
  87.6 6.9 %shard_map.177 = f32[4,8192]{1,0:T(4,128)} custom-call(s32[1,8192]{1,0:T(1,128)} %bitcast.94, f32[4,64,128]{2,1,0:T(8,128)} %reshape_reshape.3.table_ref), custom_call_target="tpu_custom_call" | custom-call | tf_op jit(solution)/shard_map/pallas_call | solution.py:141
  94.4 0.9 copy.69
  96.1 1.5 %collective-permute-done.8 = f32[2,40,1,128]{3,2,1,0:T(1,128)S(1)} collective-permute-done((f32[2,40,1,128]{3,2,1,0:T(1,128)S(1)}, f32[2,40,1,128]{3,2,1,0:T(1,128)S(1)}, u32[]{:S(2)}, u32[]{:S(2)}) %collective-permute-start.8) | collective-permute-done | bytes 40992 | tf_op jit(solution)/shard_map/ppermute | solution.py:29
  97.6 2.1 %collective-permute-done.9 = f32[2,40,1,128]{3,2,1,0:T(1,128)S(1)} collective-permute-done((f32[2,40,1,128]{3,2,1,0:T(1,128)S(1)}, f32[2,40,1,128]{3,2,1,0:T(1,128)S(1)}, u32[]{:S(2)}, u32[]{:S(2)}) %collective-permute-start.9) | collective-permute-done | bytes 40992 | tf_op jit(solution)/shard_map/ppermute | solution.py:27
  100.6 1.9 %collective-permute-start.10 = (f32[2,40,18,1]{1,2,3,0:T(8,128)S(1)}, f32[2,40,18,1]{1,2,3,0:T(8,128)S(1)}, u32[]{:S(2)}, u32[]{:S(2)}) collective-permute-start(f32[2,40,18,1]{1,2,3,0:T(8,128)S(1)} %copy.55), channel_id=1, source_target_pairs={{1,0},{2,1},{3,2},{4,3},{5,4},{6,5},{7,6},{0,7},{9,8},{10,9},{11,1... | collective-permute-start | bytes 17288 | tf_op jit(solution)/shard_map/ppermute | solution.py:29
  103.1 0.9 fusion.22
  104.9 4.6 %collective-permute-done.11 = f32[2,40,18,1]{1,2,3,0:T(8,128)S(1)} collective-permute-done((f32[2,40,18,1]{1,2,3,0:T(8,128)S(1)}, f32[2,40,18,1]{1,2,3,0:T(8,128)S(1)}, u32[]{:S(2)}, u32[]{:S(2)}) %collective-permute-start.11) | collective-permute-done | bytes 5792 | tf_op jit(solution)/shard_map/ppermute | solution.py:27
  109.9 2.0 %multiply_subtract_fusion.1 = f32[2,40,16,128]{3,2,1,0:T(8,128)S(1)} fusion(f32[2,40,16,128]{3,2,1,0:T(8,128)S(1)} %get-tuple-element.73, f32[2,40,1,128]{3,2,1,0:T(1,128)S(1)} %collective-permute-done.8, f32[2,40,1,128]{3,2,1,0:T(1,128)S(1)} %collective-permute-done.9, f32[2,40,18,1]{3,2,1,0:T(8,128)S(1)} %copy.58, f32[2,40,18,1]{3,2,1,0:T(8,128)S(1)} %copy.56, ...), kind=kLoop, calls=%fused_computation.64 | loop fusion | flops 3440640 | bytes 2059520 | tf_op jit(solution)/shard_map/sub | solution.py:113
  112.5 1.2 collective-permute-done.12
  113.7 1.8 %collective-permute-done.13 = f32[2,40,1,128]{3,2,1,0:T(1,128)S(1)} collective-permute-done((f32[2,40,1,128]{3,2,1,0:T(1,128)S(1)}, f32[2,40,1,128]{3,2,1,0:T(1,128)S(1)}, u32[]{:S(2)}, u32[]{:S(2)}) %collective-permute-start.13) | collective-permute-done | bytes 40992 | tf_op jit(solution)/shard_map/ppermute | solution.py:27
  116.9 2.0 %collective-permute-start.15 = (f32[2,40,18,1]{1,2,3,0:T(8,128)S(1)}, f32[2,40,18,1]{1,2,3,0:T(8,128)S(1)}, u32[]{:S(2)}, u32[]{:S(2)}) collective-permute-start(f32[2,40,18,1]{1,2,3,0:T(8,128)S(1)} %copy.61), channel_id=1, source_target_pairs={{0,1},{1,2},{2,3},{3,4},{4,5},{5,6},{6,7},{7,0},{8,9},{9,10},{10,1... | collective-permute-start | bytes 17288 | tf_op jit(solution)/shard_map/ppermute | solution.py:27
  118.9 1.4 %collective-permute-done.14 = f32[2,40,18,1]{1,2,3,0:T(8,128)S(1)} collective-permute-done((f32[2,40,18,1]{1,2,3,0:T(8,128)S(1)}, f32[2,40,18,1]{1,2,3,0:T(8,128)S(1)}, u32[]{:S(2)}, u32[]{:S(2)}) %collective-permute-start.14) | collective-permute-done | bytes 5792 | tf_op jit(solution)/shard_map/ppermute | solution.py:29
  120.7 2.7 %collective-permute-done.15 = f32[2,40,18,1]{1,2,3,0:T(8,128)S(1)} collective-permute-done((f32[2,40,18,1]{1,2,3,0:T(8,128)S(1)}, f32[2,40,18,1]{1,2,3,0:T(8,128)S(1)}, u32[]{:S(2)}, u32[]{:S(2)}) %collective-permute-start.15) | collective-permute-done | bytes 5792 | tf_op jit(solution)/shard_map/ppermute | solution.py:27
  123.9 1.8 %multiply_subtract_fusion = f32[2,40,16,128]{3,2,1,0:T(8,128)} fusion(f32[2,40,16,128]{3,2,1,0:T(8,128)S(1)} %multiply_subtract_fusion.1, f32[2,40,1,128]{3,2,1,0:T(1,128)S(1)} %collective-permute-done.12, f32[2,40,1,128]{3,2,1,0:T(1,128)S(1)} %collective-permute-done.13, f32[2,40,18,1]{3,2,1,0:T(8,128)S(1)} %copy.62, f32[2,40,18,1]{3,2,1,0:T(8,128)S(1)} %copy.60, ...), kind=kLoop, calls=%fused_computation.63 | loop fusion | flops 3440640 | bytes 2059520 | tf_op jit(solution)/shard_map/sub | solution.py:113
  (74 shorter events, 12.4 us)
Async XLA Ops:
  0.6 0.7 copy-start.12
  0.6 0.7 copy-start.13
  0.7 0.9 copy-start.7
  0.7 1.3 %copy-start = (f32[4,40,16,128]{3,2,1,0:T(8,128)S(1)}, f32[4,40,16,128]{3,2,1,0:T(8,128)}, u32[]{:S(2)}) copy-start(f32[4,40,16,128]{3,2,1,0:T(8,128)} %param.25) | copy-start | bytes 3932164
  0.7 0.8 copy-start.11
  3.2 1.3 %copy-start.6 = (f32[128,128,1]{1,0,2:T(8,128)S(1)}, f32[128,128,1]{1,0,2:T(8,128)}, u32[]{:S(2)}) copy-start(f32[128,128,1]{1,0,2:T(8,128)} %constant.172) | copy-start | bytes 196612
  7.0 4.6 %collective-permute-start = (f32[160,1,128]{2,1,0:T(1,128)S(1)}, f32[160,1,128]{2,1,0:T(1,128)S(1)}, u32[]{:S(2)}, u32[]{:S(2)}) collective-permute-start(f32[160,1,128]{2,1,0:T(1,128)S(1)} %get-tuple-element.60), channel_id=1, source_target_pairs={{0,8},{8,16},{16,24},{24,0},{1,9},{9,17},{17,25},{25,1},{2,10},{10... | collective-permute-start | bytes 245768 | tf_op jit(solution)/shard_map/ppermute | solution.py:27
  7.5 4.8 %collective-permute-start.1 = (f32[160,1,128]{2,1,0:T(1,128)S(1)}, f32[160,1,128]{2,1,0:T(1,128)S(1)}, u32[]{:S(2)}, u32[]{:S(2)}) collective-permute-start(f32[160,1,128]{2,1,0:T(1,128)S(1)} %get-tuple-element.61), channel_id=1, source_target_pairs={{8,0},{16,8},{24,16},{0,24},{9,1},{17,9},{25,17},{1,25},{10,2},{18... | collective-permute-start | bytes 245768 | tf_op jit(solution)/shard_map/ppermute | solution.py:29
  17.3 7.2 %collective-permute-start.2 = (f32[160,18,1]{0,2,1:T(1,128)S(1)}, f32[160,18,1]{0,2,1:T(1,128)S(1)}, u32[]{:S(2)}, u32[]{:S(2)}) collective-permute-start(f32[160,18,1]{0,2,1:T(1,128)S(1)} %copy.43), channel_id=1, source_target_pairs={{0,1},{1,2},{2,3},{3,4},{4,5},{5,6},{6,7},{7,0},{8,9},{9,10},{10,1... | collective-permute-start | bytes 34568 | tf_op jit(solution)/shard_map/ppermute | solution.py:27
  21.2 5.3 %collective-permute-start.3 = (f32[160,18,1]{0,2,1:T(1,128)S(1)}, f32[160,18,1]{0,2,1:T(1,128)S(1)}, u32[]{:S(2)}, u32[]{:S(2)}) collective-permute-start(f32[160,18,1]{0,2,1:T(1,128)S(1)} %copy.45), channel_id=1, source_target_pairs={{1,0},{2,1},{3,2},{4,3},{5,4},{6,5},{7,6},{0,7},{9,8},{10,9},{11,1... | collective-permute-start | bytes 34568 | tf_op jit(solution)/shard_map/ppermute | solution.py:29
  28.4 4.3 %copy-start.8 = (f32[16,128]{1,0:T(8,128)S(1)}, f32[16,128]{1,0:T(8,128)}, u32[]{:S(2)}) copy-start(f32[16,128]{1,0:T(8,128)} %constant.170) | copy-start | bytes 24580
  38.2 3.9 %collective-permute-start.4 = (f32[160,1,128]{2,1,0:T(1,128)S(1)}, f32[160,1,128]{2,1,0:T(1,128)S(1)}, u32[]{:S(2)}, u32[]{:S(2)}) collective-permute-start(f32[160,1,128]{2,1,0:T(1,128)S(1)} %get-tuple-element.58), channel_id=1, source_target_pairs={{0,8},{8,16},{16,24},{24,0},{1,9},{9,17},{17,25},{25,1},{2,10},{10... | collective-permute-start | bytes 245768 | tf_op jit(solution)/shard_map/ppermute | solution.py:27
  39.5 3.2 %collective-permute-start.5 = (f32[160,1,128]{2,1,0:T(1,128)S(1)}, f32[160,1,128]{2,1,0:T(1,128)S(1)}, u32[]{:S(2)}, u32[]{:S(2)}) collective-permute-start(f32[160,1,128]{2,1,0:T(1,128)S(1)} %get-tuple-element.59), channel_id=1, source_target_pairs={{8,0},{16,8},{24,16},{0,24},{9,1},{17,9},{25,17},{1,25},{10,2},{18... | collective-permute-start | bytes 245768 | tf_op jit(solution)/shard_map/ppermute | solution.py:29
  47.7 7.3 %copy-start.14 = (s32[1,32]{1,0:T(1,128)S(1)}, s32[1,32]{1,0:T(1,128)}, u32[]{:S(2)}) copy-start(s32[1,32]{1,0:T(1,128)} %param.28) | copy-start | bytes 388
  47.7 7.4 %copy-start.9 = (s32[1,32,256]{2,1,0:T(8,128)S(1)}, s32[1,32,256]{2,1,0:T(8,128)}, u32[]{:S(2)}) copy-start(s32[1,32,256]{2,1,0:T(8,128)} %param.27) | copy-start | bytes 98308
  47.7 8.0 %collective-permute-start.6 = (f32[160,18,1]{0,2,1:T(1,128)S(1)}, f32[160,18,1]{0,2,1:T(1,128)S(1)}, u32[]{:S(2)}, u32[]{:S(2)}) collective-permute-start(f32[160,18,1]{0,2,1:T(1,128)S(1)} %copy.48), channel_id=1, source_target_pairs={{0,1},{1,2},{2,3},{3,4},{4,5},{5,6},{6,7},{7,0},{8,9},{9,10},{10,1... | collective-permute-start | bytes 34568 | tf_op jit(solution)/shard_map/ppermute | solution.py:27
  50.6 7.1 %collective-permute-start.7 = (f32[160,18,1]{0,2,1:T(1,128)S(1)}, f32[160,18,1]{0,2,1:T(1,128)S(1)}, u32[]{:S(2)}, u32[]{:S(2)}) collective-permute-start(f32[160,18,1]{0,2,1:T(1,128)S(1)} %copy.50), channel_id=1, source_target_pairs={{1,0},{2,1},{3,2},{4,3},{5,4},{6,5},{7,6},{0,7},{9,8},{10,9},{11,1... | collective-permute-start | bytes 34568 | tf_op jit(solution)/shard_map/ppermute | solution.py:29
  64.3 1.1 copy-start.5
  64.3 31.0 %copy-start.10 = (f32[4,16,128]{2,1,0:T(8,128)S(1)}, f32[4,16,128]{2,1,0:T(8,128)}, u32[]{:S(2)}) copy-start(f32[4,16,128]{2,1,0:T(8,128)} %param.32) | copy-start | bytes 98308
  64.4 31.0 %copy-start.1 = (f32[2,40,16,128]{3,2,1,0:T(8,128)S(1)}, f32[2,40,16,128]{3,2,1,0:T(8,128)}, u32[]{:S(2)}) copy-start(f32[2,40,16,128]{3,2,1,0:T(8,128)} %param.29) | copy-start | bytes 1966084
  64.4 31.0 %copy-start.4 = (f32[2,40,16,128]{3,2,1,0:T(8,128)S(1)}, f32[2,40,16,128]{3,2,1,0:T(8,128)}, u32[]{:S(2)}) copy-start(f32[2,40,16,128]{3,2,1,0:T(8,128)} %param.30) | copy-start | bytes 1966084
  95.5 2.1 %collective-permute-start.8 = (f32[2,40,1,128]{3,2,1,0:T(1,128)S(1)}, f32[2,40,1,128]{3,2,1,0:T(1,128)S(1)}, u32[]{:S(2)}, u32[]{:S(2)}) collective-permute-start(f32[2,40,1,128]{3,2,1,0:T(1,128)S(1)} %get-tuple-element.71), channel_id=1, source_target_pairs={{8,0},{16,8},{24,16},{0,24},{9,1},{17,9},{25,17},{1,25},{10,2},{18... | collective-permute-start | bytes 122888 | tf_op jit(solution)/shard_map/ppermute | solution.py:29
  95.9 3.8 %collective-permute-start.9 = (f32[2,40,1,128]{3,2,1,0:T(1,128)S(1)}, f32[2,40,1,128]{3,2,1,0:T(1,128)S(1)}, u32[]{:S(2)}, u32[]{:S(2)}) collective-permute-start(f32[2,40,1,128]{3,2,1,0:T(1,128)S(1)} %get-tuple-element.70), channel_id=1, source_target_pairs={{0,8},{8,16},{16,24},{24,0},{1,9},{9,17},{17,25},{25,1},{2,10},{10... | collective-permute-start | bytes 122888 | tf_op jit(solution)/shard_map/ppermute | solution.py:27
  100.6 3.9 %collective-permute-start.10 = (f32[2,40,18,1]{1,2,3,0:T(8,128)S(1)}, f32[2,40,18,1]{1,2,3,0:T(8,128)S(1)}, u32[]{:S(2)}, u32[]{:S(2)}) collective-permute-start(f32[2,40,18,1]{1,2,3,0:T(8,128)S(1)} %copy.55), channel_id=1, source_target_pairs={{1,0},{2,1},{3,2},{4,3},{5,4},{6,5},{7,6},{0,7},{9,8},{10,9},{11,1... | collective-permute-start | bytes 17288 | tf_op jit(solution)/shard_map/ppermute | solution.py:29
  102.9 6.6 %collective-permute-start.11 = (f32[2,40,18,1]{1,2,3,0:T(8,128)S(1)}, f32[2,40,18,1]{1,2,3,0:T(8,128)S(1)}, u32[]{:S(2)}, u32[]{:S(2)}) collective-permute-start(f32[2,40,18,1]{1,2,3,0:T(8,128)S(1)} %copy.57), channel_id=1, source_target_pairs={{0,1},{1,2},{2,3},{3,4},{4,5},{5,6},{6,7},{7,0},{8,9},{9,10},{10,1... | collective-permute-start | bytes 17288 | tf_op jit(solution)/shard_map/ppermute | solution.py:27
  112.0 1.7 %collective-permute-start.12 = (f32[2,40,1,128]{3,2,1,0:T(1,128)S(1)}, f32[2,40,1,128]{3,2,1,0:T(1,128)S(1)}, u32[]{:S(2)}, u32[]{:S(2)}) collective-permute-start(f32[2,40,1,128]{3,2,1,0:T(1,128)S(1)} %get-tuple-element.67), channel_id=1, source_target_pairs={{8,0},{16,8},{24,16},{0,24},{9,1},{17,9},{25,17},{1,25},{10,2},{18... | collective-permute-start | bytes 122888 | tf_op jit(solution)/shard_map/ppermute | solution.py:29
  112.0 3.5 %collective-permute-start.13 = (f32[2,40,1,128]{3,2,1,0:T(1,128)S(1)}, f32[2,40,1,128]{3,2,1,0:T(1,128)S(1)}, u32[]{:S(2)}, u32[]{:S(2)}) collective-permute-start(f32[2,40,1,128]{3,2,1,0:T(1,128)S(1)} %get-tuple-element.66), channel_id=1, source_target_pairs={{0,8},{8,16},{16,24},{24,0},{1,9},{9,17},{17,25},{25,1},{2,10},{10... | collective-permute-start | bytes 122888 | tf_op jit(solution)/shard_map/ppermute | solution.py:27
  116.4 3.9 %collective-permute-start.14 = (f32[2,40,18,1]{1,2,3,0:T(8,128)S(1)}, f32[2,40,18,1]{1,2,3,0:T(8,128)S(1)}, u32[]{:S(2)}, u32[]{:S(2)}) collective-permute-start(f32[2,40,18,1]{1,2,3,0:T(8,128)S(1)} %copy.59), channel_id=1, source_target_pairs={{1,0},{2,1},{3,2},{4,3},{5,4},{6,5},{7,6},{0,7},{9,8},{10,9},{11,1... | collective-permute-start | bytes 17288 | tf_op jit(solution)/shard_map/ppermute | solution.py:29
  116.5 7.4 %copy-start.2 = (f32[40,16,128]{2,1,0:T(8,128)S(1)}, f32[40,16,128]{2,1,0:T(8,128)}, u32[]{:S(2)}) copy-start(f32[40,16,128]{2,1,0:T(8,128)} %get-tuple-element.68) | copy-start | bytes 983044
  116.5 7.4 %copy-start.3 = (f32[40,16,128]{2,1,0:T(8,128)S(1)}, f32[40,16,128]{2,1,0:T(8,128)}, u32[]{:S(2)}) copy-start(f32[40,16,128]{2,1,0:T(8,128)} %get-tuple-element.69) | copy-start | bytes 983044
  116.9 6.6 %collective-permute-start.15 = (f32[2,40,18,1]{1,2,3,0:T(8,128)S(1)}, f32[2,40,18,1]{1,2,3,0:T(8,128)S(1)}, u32[]{:S(2)}, u32[]{:S(2)}) collective-permute-start(f32[2,40,18,1]{1,2,3,0:T(8,128)S(1)} %copy.61), channel_id=1, source_target_pairs={{0,1},{1,2},{2,3},{3,4},{4,5},{5,6},{6,7},{7,0},{8,9},{9,10},{10,1... | collective-permute-start | bytes 17288 | tf_op jit(solution)/shard_map/ppermute | solution.py:27

commit v3 on v2

--- a/solution.py
+++ b/solution.py
@@ -17,20 +17,114 @@
 surf_coef = 0.2
 
 
-def extended(cells, sides, width):
-    for axis, dim in sides:
-        count = lax.axis_size(axis)
-        head = lax.slice_in_dim(cells, 0, width, axis=dim)
-        tail = lax.slice_in_dim(cells, cells.shape[dim] - width, cells.shape[dim], axis=dim)
-        cells = jnp.concatenate(
-            [
-                lax.ppermute(tail, axis, [(i, (i + 1) % count) for i in range(count)]),
-                cells,
-                lax.ppermute(head, axis, [((i + 1) % count, i) for i in range(count)]),
-            ],
-            axis=dim,
+def neighbour(values, step_x, step_y):
+    count_x, count_y = lax.axis_size("gx"), lax.axis_size("gy")
+    if step_y == 0:
+        return lax.ppermute(values, "gx", [(i, (i + step_x) % count_x) for i in range(count_x)])
+    if step_x == 0:
+        return lax.ppermute(values, "gy", [(j, (j + step_y) % count_y) for j in range(count_y)])
+    pairs = [
+        (i * count_y + j, ((i + step_x) % count_x) * count_y + (j + step_y) % count_y)
+        for i in range(count_x)
+        for j in range(count_y)
+    ]
+    return lax.ppermute(values, ("gx", "gy"), pairs)
+
+
+def shifted(values, before, after, axis):
+    size = values.shape[axis]
+    prev = jnp.concatenate([before, lax.slice_in_dim(values, 0, size - 1, axis=axis)], axis=axis)
+    nxt = jnp.concatenate([lax.slice_in_dim(values, 1, size, axis=axis), after], axis=axis)
+    return prev, nxt
+
+
+def pair_merge(values, before, after, axis):
+    size = values.shape[axis]
+    layout = [1] * values.ndim
+    layout[axis] = size
+    position = (jnp.arange(size) % 4).reshape(layout)
+    prev, nxt = shifted(values, before, after, axis)
+    return values + jnp.where(position == 0, prev, jnp.where(position == 3, nxt, 0.0))
+
+
+def assemble(stiff):
+    last_x, last_y = stiff.shape[1] - 1, stiff.shape[2] - 1
+    from_left = neighbour(stiff[:, :, last_y:], 0, 1)
+    from_right = neighbour(stiff[:, :, :1], 0, -1)
+    from_up = neighbour(stiff[:, last_x:, :], 1, 0)
+    from_down = neighbour(stiff[:, :1, :], -1, 0)
+    up_left = neighbour(stiff[:, last_x:, last_y:], 1, 1)
+    up_right = neighbour(stiff[:, last_x:, :1], 1, -1)
+    down_left = neighbour(stiff[:, :1, last_y:], -1, 1)
+    down_right = neighbour(stiff[:, :1, :1], -1, -1)
+    merged = pair_merge(stiff, from_left, from_right, 2)
+    merged_up = pair_merge(from_up, up_left, up_right, 2)
+    merged_down = pair_merge(from_down, down_left, down_right, 2)
+    return pair_merge(merged, merged_up, merged_down, 1)
+
+
+def stiff_kernel(state_ref, wmx_ref, wmy_ref, wx_ref, wy_ref, kx_ref, ay_ref, by_ref, out_ref):
+    highest = lax.Precision.HIGHEST
+    chunk = kx_ref.shape[0]
+    kx = kx_ref[...]
+    for part in range(state_ref.shape[0] // chunk):
+        rows = pl.ds(part * chunk, chunk)
+        block = state_ref[rows, :]
+        along_x = jnp.dot(kx, block, precision=highest, preferred_element_type=jnp.float32)
+        term_x = lax.dot_general(
+            kx,
+            wmx_ref[...] * along_x,
+            (((0,), (0,)), ((), ())),
+            precision=highest,
+            preferred_element_type=jnp.float32,
         )
-    return cells
+        along_y = jnp.dot(block, ay_ref[...], precision=highest, preferred_element_type=jnp.float32)
+        term_y = jnp.dot(wmy_ref[...] * along_y, by_ref[...], precision=highest, preferred_element_type=jnp.float32)
+        out_ref[rows, :] = term_x * wy_ref[...] + term_y * wx_ref[...]
+
+
+def stiffness(state_in, metric, derivative_np, weights_np):
+    levels, xsize, ysize = state_in.shape
+    chunk = 128 if 128 % xsize == 0 else xsize
+    total = levels * xsize
+    tile = chunk * math.gcd(total // chunk, 5)
+    weight_x = np.tile(weights_np, xsize // 4)[:, None]
+    weight_y = np.tile(weights_np, ysize // 4)[None, :]
+    reps = chunk // xsize
+    wmx = jnp.tile(jnp.asarray(weight_x, jnp.float32) * metric[0], (reps, 1))
+    wmy = jnp.tile(jnp.asarray(weight_y, jnp.float32) * metric[1], (reps, 1))
+    wx = jnp.asarray(np.tile(np.broadcast_to(weight_x, (xsize, ysize)), (reps, 1)), jnp.float32)
+    wy = jnp.asarray(np.tile(np.broadcast_to(weight_y, (xsize, ysize)), (reps, 1)), jnp.float32)
+    kx = jnp.asarray(np.kron(np.eye(chunk // 4), derivative_np), jnp.float32)
+    ay = jnp.asarray(np.kron(np.eye(ysize // 4), derivative_np.T), jnp.float32)
+    by = jnp.asarray(np.kron(np.eye(ysize // 4), derivative_np), jnp.float32)
+    fixed = lambda step: (0, 0)
+    out = pl.pallas_call(
+        stiff_kernel,
+        grid=(total // tile,),
+        in_specs=[pl.BlockSpec((tile, ysize), lambda step: (step, 0))]
+        + [pl.BlockSpec((chunk, ysize), fixed)] * 4
+        + [pl.BlockSpec((chunk, chunk), fixed), pl.BlockSpec((ysize, ysize), fixed), pl.BlockSpec((ysize, ysize), fixed)],
+        out_specs=pl.BlockSpec((tile, ysize), lambda step: (step, 0)),
+        out_shape=jax.ShapeDtypeStruct((total, ysize), jnp.float32),
+    )(state_in.reshape(total, ysize), wmx, wmy, wx, wy, kx, ay, by)
+    return out.reshape(levels, xsize, ysize)
+
+
+def tracer_step(tracers, velocity):
+    last_x, last_y = tracers.shape[-2] - 1, tracers.shape[-1] - 1
+    from_up = neighbour(tracers[..., last_x:, :], 1, 0)
+    from_down = neighbour(tracers[..., :1, :], -1, 0)
+    from_left = neighbour(tracers[..., last_y:], 0, 1)
+    from_right = neighbour(tracers[..., :1], 0, -1)
+    west, east = shifted(tracers, from_up, from_down, tracers.ndim - 2)
+    south, north = shifted(tracers, from_left, from_right, tracers.ndim - 1)
+    return (
+        tracers
+        + diff_coef * (east + west + north + south - 4.0 * tracers)
+        - 0.5 * velocity[0] * (east - west)
+        - 0.5 * velocity[1] * (north - south)
+    )
 
 
 def gll_tables():
@@ -63,57 +157,10 @@
     return (derivative, weights, massw)
 
 
-def stiffness(state_in, metric_x, metric_y, derivative_np, weights_np):
-    levels, xsize, ysize = state_in.shape
-    highest = lax.Precision.HIGHEST
-    block_x = jnp.asarray(np.kron(np.eye(xsize // 4), derivative_np), jnp.float32)
-    block_y = jnp.asarray(np.kron(np.eye(ysize // 4), derivative_np), jnp.float32)
-    weight_x = jnp.asarray(np.tile(weights_np, xsize // 4), jnp.float32)[:, None]
-    weight_y = jnp.asarray(np.tile(weights_np, ysize // 4), jnp.float32)[None, :]
-    along_x = jnp.einsum("ab,lby->lay", block_x, state_in, precision=highest)
-    term_x = (
-        jnp.einsum("ba,lby->lay", block_x, weight_x * metric_x * along_x, precision=highest)
-        * weight_y
-    )
-    along_y = jnp.einsum("lxc,dc->lxd", state_in, block_y, precision=highest)
-    term_y = (
-        jnp.einsum("lxc,cd->lxd", weight_y * metric_y * along_y, block_y, precision=highest)
-        * weight_x
-    )
-    return term_x + term_y
-
-
 def mass_inverse(massw_np, xsize, ysize):
     return jnp.asarray(
         1.0 / (np.tile(massw_np, xsize // 4)[:, None] * np.tile(massw_np, ysize // 4)[None, :]),
         jnp.float32,
-    )
-
-
-def edge_sum(padded):
-    inner_y = padded.shape[2] - 2
-    ypos = jnp.arange(inner_y) % 4
-    centre = padded[:, :, 1:-1]
-    merged = centre + jnp.where(
-        ypos == 0, padded[:, :, :-2], jnp.where(ypos == 3, padded[:, :, 2:], 0.0)
-    )
-    inner_x = merged.shape[1] - 2
-    xpos = (jnp.arange(inner_x) % 4)[:, None]
-    middle = merged[:, 1:-1]
-    return middle + jnp.where(xpos == 0, merged[:, :-2], jnp.where(xpos == 3, merged[:, 2:], 0.0))
-
-
-def tracer_step(padded, velocity):
-    centre = padded[..., 1:-1, 1:-1]
-    east = padded[..., 2:, 1:-1]
-    west = padded[..., :-2, 1:-1]
-    north = padded[..., 1:-1, 2:]
-    south = padded[..., 1:-1, :-2]
-    return (
-        centre
-        + diff_coef * (east + west + north + south - 4.0 * centre)
-        - 0.5 * velocity[0] * (east - west)
-        - 0.5 * velocity[1] * (north - south)
     )
 
 
@@ -165,9 +212,8 @@
     state_now = atm_state.reshape(fields * levels, xlocal, ylocal)
     inv_mass = mass_inverse(massw_np, xlocal, ylocal)
     for substep in range(SUB):
-        stiff = stiffness(state_now, metric[0], metric[1], derivative_np, weights_np)
-        padded = extended(stiff, (("gx", 1), ("gy", 2)), 1)
-        state_now = state_now - visc_coef * edge_sum(padded) * inv_mass
+        stiff = stiffness(state_now, metric, derivative_np, weights_np)
+        state_now = state_now - visc_coef * assemble(stiff) * inv_mass
     atm_out = state_now.reshape(fields, levels, xlocal, ylocal)
     bottom = atm_out[:, levels - 1]
     speed = jnp.sqrt(1.0 + bottom[0] * bottom[0] + bottom[1] * bottom[1])
@@ -189,8 +235,7 @@
     tracers = ocean_tracers.at[0, 0].add(surf_coef * ocean_flux[2])
     tracers = tracers.at[1, 0].add(surf_coef * ocean_flux[3])
     for repeat in range(OSTEPS):
-        ocean_pad = extended(tracers, (("gx", 2), ("gy", 3)), 1)
-        tracers = tracer_step(ocean_pad, velocity)
+        tracers = tracer_step(tracers, velocity)
     return (atm_out, tracers)
 
 

time: 127 us -> 191 us (1.50)
  local copies, waits for them, and re-layouts: 30.5 us -> 73.9 us
  starting transfers between devices: 19.6 us -> 41.5 us
  Pallas kernels: 13.1 us -> 28.1 us
  blocking collectives: 13.7 us -> 0 us
  other arithmetic: 16.8 us -> 28.6 us
  matrix products: 9.68 us -> 0 us
  waiting for transfers between devices: 21.3 us -> 16.5 us
    slice x16 -> x30, local copies, waits for them, and re-layouts: 16.5 us -> 36.2 us  [the longest x12 10.1 us: shifted(): lax.slice_in_dim(values, 1, size, axis=axis)]
    ppermute x16 -> x24, starting transfers between devices: 19.6 us -> 35.5 us  [the longest x8 17.2 us: neighbour(): return lax.ppermute(values, ('gx', 'gy'), pairs)]
    pallas_call x0 -> x2, Pallas kernels: none -> 15 us  [stiffness(): pl.pallas_call(stiff_kernel, grid=(total // tile,), in_specs=[pl.BlockSpe...]
    all_to_all x1 -> x0, blocking collectives: 13.7 us -> none  [per_device(): lax.all_to_all(payload, ('gx', 'gy'), split_axis=1, concat_axis=1, tiled=...]
    concatenate x0 -> x14, local copies, waits for them, and re-layouts: none -> 12.6 us  [the longest x7 6.34 us: shifted(): jnp.concatenate([lax.slice_in_dim(values, 1, size, axis=axis), after], ax...]
    sub x4, other arithmetic: 4.74 us -> 17 us  [the longest x2 11.7 us: per_device(): state_now = state_now - visc_coef * assemble(stiff) * inv_mass]
    ppermute x16 -> x24, waiting for transfers between devices: 21.3 us -> 11.3 us  [the longest x8 7.18 us: neighbour(): lax.ppermute(values, 'gy', [(j, (j + step_y) % count_y) for j in range(co...]
    dot_general x8 -> x0, matrix products: 9.68 us -> none  [the longest x2 2.49 us: stiffness(): jnp.einsum('ba,lby->lay', block_x, weight_x * metric_x * along_x, precisi...]
  transfers between devices with their start and end apart: 16 -> 25, of which waited for: 12 -> 6; matrix products, arithmetic and copies ran while one was open for 9% -> 29% of each run, Pallas kernels for 0% -> 0%
where the time goes in v3:
time: 191 us; the launch traced here: 190 us
  local copies, waits for them, and re-layouts  73.9 us (39%)
  starting transfers between devices  41.5 us (22%)
  other arithmetic  28.6 us (15%)
  Pallas kernels  28.1 us (15%)
  waiting for transfers between devices  16.5 us (9%)
    ppermute x8, starting transfers between devices, neighbour(): return lax.ppermute(values, ('gx', 'gy'), pairs)  17.2 us
    pallas_call x2, Pallas kernels, stiffness(): pl.pallas_call(stiff_kernel, grid=(total // tile,), in_specs=[pl.BlockSpe...  15 us
    ppermute x8, starting transfers between devices, neighbour(): lax.ppermute(values, 'gy', [(j, (j + step_y) % count_y) for j in range(co...  14.1 us
    pallas_call x2, Pallas kernels, onehot_gather(): pl.pallas_call(gather_kernel, grid=(count // tile,), in_specs=[pl.BlockSp...  13.1 us
    ppermute x10, local copies, waits for them, and re-layouts, neighbour(): lax.ppermute(values, 'gy', [(j, (j + step_y) % count_y) for j in range(co...  12.2 us
    sub x2, other arithmetic, per_device(): state_now = state_now - visc_coef * assemble(stiff) * inv_mass  11.7 us
    slice x12, local copies, waits for them, and re-layouts, shifted(): lax.slice_in_dim(values, 1, size, axis=axis)  10.1 us
    slice x4, local copies, waits for them, and re-layouts, assemble(): from_right = neighbour(stiff[:, :, :1], 0, -1)  9.76 us
  transfers between devices with their start and end apart: 25, of which 6 were waited for; matrix products, arithmetic and copies ran while one was open for 29% of the time, Pallas kernels for 0%

profile of v3, /device:TPU:0, one launch (start us, length us, event | category | flops | bytes accessed | tf_op | source)
XLA Modules:
  0.0 189.8 jit_solution(3844672021878313311)
XLA Ops:
  2.7 7.5 %shard_map.230 = f32[2560,128]{1,0:T(8,128)} custom-call(f32[2560,128]{1,0:T(8,128)} %bitcast.110, f32[128,128]{1,0:T(8,128)} %bitcast.115, f32[128,128]{1,0:T(8,128)} %bitcast.117, f32[128,128]{1,0:T(8,128)} %constant.182.clone.wx_ref, f32[128,128]{1,0:T(8,128)} %constant.183.clone.wy_ref, f32[128,128]{1,0:T(8,128)} %constant.184.clone.kx_ref.by_ref, ...), custom_call_target="tpu_custom_call" | custom-call | tf_op jit(solution)/shard_map/pallas_call | solution.py:102
  10.2 2.0 %fusion.48 = (f32[160,1,128]{2,1,0:T(1,128)}, f32[160,1,128]{2,1,0:T(1,128)S(1)}) fusion(f32[160,16,128]{2,1,0:T(8,128)} %bitcast.90), kind=kLoop, calls=%fused_computation.103 | loop fusion | bytes 327680 | tf_op jit(solution)/shard_map/slice | solution.py:55
  12.2 2.4 %collective-permute-start.5 = (f32[160,1,128]{2,1,0:T(1,128)}, f32[160,1,128]{2,1,0:T(1,128)S(1)}, u32[]{:S(2)}, u32[]{:S(2)}) collective-permute-start(f32[160,1,128]{2,1,0:T(1,128)} %get-tuple-element.76), channel_id=1, source_target_pairs={{0,24},{8,0},{16,8},{24,16},{1,25},{9,1},{17,9},{25,17},{2,26},{10... | collective-permute-start | bytes 245768 | tf_op jit(solution)/shard_map/ppermute | solution.py:23
  14.6 2.8 %fusion.47 = (f32[160,1,1]{2,1,0:T(1,128)S(1)}, f32[160,1,1]{2,1,0:T(1,128)S(1)}, f32[160,1,1]{2,1,0:T(1,128)S(1)}, f32[160,1,1]{2,1,0:T(1,128)}) fusion(f32[160,16,128]{2,1,0:T(8,128)} %bitcast.91), kind=kLoop, calls=%fused_computation.102 | loop fusion | bytes 5120 | tf_op jit(solution)/shard_map/slice | solution.py:59
  17.4 1.8 collective-permute-start.3
  19.2 3.2 %fusion.50 = (f32[160,16,1]{2,1,0:T(8,128)S(1)}, f32[160,16,1]{2,1,0:T(8,128)}) fusion(f32[160,16,128]{2,1,0:T(8,128)} %bitcast.92), kind=kLoop, calls=%fused_computation.105 | loop fusion | bytes 40960 | tf_op jit(solution)/shard_map/slice | solution.py:53
  22.4 2.1 %copy.99 = f32[160,16,1]{0,1,2:T(8,128)S(1)} copy(f32[160,16,1]{2,1,0:T(8,128)} %get-tuple-element.81) | data formatting | bytes 20480 | tf_op jit(solution)/shard_map/slice | solution.py:52
  24.4 1.6 collective-permute-start
  26.7 3.2 %collective-permute-start.1 = (f32[160,16,1]{0,1,2:T(8,128)S(1)}, f32[160,16,1]{0,1,2:T(8,128)S(1)}, u32[]{:S(2)}, u32[]{:S(2)}) collective-permute-start(f32[160,16,1]{0,1,2:T(8,128)S(1)} %copy.102), channel_id=1, source_target_pairs={{0,7},{1,0},{2,1},{3,2},{4,3},{5,4},{6,5},{7,6},{8,15},{9,8},{10,9... | collective-permute-start | bytes 30728 | tf_op jit(solution)/shard_map/ppermute | solution.py:25
  33.8 1.7 copy.106
  35.4 2.6 %collective-permute-start.6 = (f32[160,1,1]{2,1,0:T(1,128)S(1)}, f32[160,1,1]{2,1,0:T(1,128)S(1)}, u32[]{:S(2)}, u32[]{:S(2)}) collective-permute-start(f32[160,1,1]{2,1,0:T(1,128)S(1)} %get-tuple-element.73), channel_id=1, source_target_pairs={{0,25},{1,26},{2,27},{3,28},{4,29},{5,30},{6,31},{7,24},{8,1},{9,2... | collective-permute-start | bytes 1928 | tf_op jit(solution)/shard_map/ppermute | solution.py:31
  38.1 1.6 copy.107
  39.7 2.9 %fusion.5 = f32[160,16,128]{2,1,0:T(8,128)S(1)} fusion(f32[160,16,128]{2,1,0:T(8,128)S(1)} %bitcast.94, f32[160,16,127]{2,1,0:T(8,128)} %get-tuple-element.79, f32[160,16,1]{2,1,0:T(8,128)} %copy.106, f32[160,16,1]{2,1,0:T(8,128)} %copy.107, f32[160,16,127]{2,1,0:T(8,128)S(1)} %get-tuple-element.78, pred[128]{0:T(512)(128)(4,1)S(1)} %get-tuple-element.121, ...), kind=kLoop, calls=%fused_computation.8 | loop fusion | flops 1638400 | bytes 5243136 | tf_op jit(solution)/shard_map/add | solution.py:47
  42.6 1.7 fusion.46
  44.3 1.7 concatenate.269
  46.2 1.8 concatenate.270
  48.1 2.1 %copy.100 = f32[4,40,16,1]{3,2,0,1:T(8,128)} copy(f32[4,40,16,1]{1,0,2,3:T(4,128)S(1)} %concatenate.215) | data formatting | bytes 20480 | tf_op jit(solution)/shard_map/concatenate | solution.py:36
  50.2 2.1 %copy.104 = f32[4,40,16,1]{3,2,0,1:T(8,128)} copy(f32[4,40,16,1]{1,0,2,3:T(4,128)S(1)} %concatenate.219) | data formatting | bytes 20480 | tf_op jit(solution)/shard_map/concatenate | solution.py:37
  52.3 2.7 %collective-permute-start.7 = (f32[160,1,1]{2,1,0:T(1,128)S(1)}, f32[160,1,1]{2,1,0:T(1,128)S(1)}, u32[]{:S(2)}, u32[]{:S(2)}) collective-permute-start(f32[160,1,1]{2,1,0:T(1,128)S(1)} %get-tuple-element.72), channel_id=1, source_target_pairs={{0,31},{1,24},{2,25},{3,26},{4,27},{5,28},{6,29},{7,30},{8,7},{9,0... | collective-permute-start | bytes 1928 | tf_op jit(solution)/shard_map/ppermute | solution.py:31
  55.5 2.3 %collective-permute-done.7 = f32[160,1,1]{2,1,0:T(1,128)S(1)} collective-permute-done((f32[160,1,1]{2,1,0:T(1,128)S(1)}, f32[160,1,1]{2,1,0:T(1,128)S(1)}, u32[]{:S(2)}, u32[]{:S(2)}) %collective-permute-start.7) | collective-permute-done | bytes 672 | tf_op jit(solution)/shard_map/ppermute | solution.py:31
  62.4 5.1 %fusion.9.state_ref = f32[2560,128]{1,0:T(8,128)} fusion(f32[2560,128]{1,0:T(8,128)S(1)} %copy-done, f32[2560,127]{1,0:T(8,128)S(1)} %bitcast.105, f32[2560,1]{1,0:T(8,128)S(1)} %copy-done.10, f32[2560,1]{1,0:T(8,128)} %concatenate.270, f32[2560,127]{1,0:T(8,128)S(1)} %bitcast.102, f32[160,16,128]{2,1,0:T(8,128)S(1)} %pad_maximum_fusion.1, ...), kind=kLoop, calls=%fused_computation.16 | loop fusion | flops 3276800 | bytes 9188608 | tf_op jit(solution)/shard_map/sub | solution.py:216
  67.4 7.6 %shard_map.231 = f32[2560,128]{1,0:T(8,128)} custom-call(f32[2560,128]{1,0:T(8,128)} %fusion.9.state_ref, f32[128,128]{1,0:T(8,128)} %bitcast.116, f32[128,128]{1,0:T(8,128)} %bitcast.118, f32[128,128]{1,0:T(8,128)} %constant.182.clone.wx_ref, f32[128,128]{1,0:T(8,128)} %constant.183.clone.wy_ref, f32[128,128]{1,0:T(8,128)} %constant.184.clone.kx_ref.by_ref, ...), custom_call_target="tpu_custom_call" | custom-call | tf_op jit(solution)/shard_map/pallas_call | solution.py:102
  75.0 4.0 %fusion.45 = (f32[160,16,1]{2,1,0:T(8,128)}, f32[160,16,1]{2,1,0:T(8,128)}) fusion(f32[160,16,128]{2,1,0:T(8,128)} %bitcast.96), kind=kLoop, calls=%fused_computation.100 | loop fusion | bytes 40960 | tf_op jit(solution)/shard_map/slice | solution.py:53
  78.9 2.0 %fusion.44 = (f32[160,16,127]{2,1,0:T(8,128)}, f32[160,16,127]{2,1,0:T(8,128)}) fusion(f32[160,16,128]{2,1,0:T(8,128)S(1)} %bitcast.97), kind=kLoop, calls=%fused_computation.99 | loop fusion | bytes 5201920 | tf_op jit(solution)/shard_map/slice | solution.py:37
  82.0 1.9 %copy.119 = f32[160,16,1]{0,1,2:T(8,128)S(1)} copy(f32[160,16,1]{2,1,0:T(8,128)} %get-tuple-element.69) | data formatting | bytes 20480 | tf_op jit(solution)/shard_map/slice | solution.py:52
  83.9 1.9 %copy.122 = f32[160,16,1]{0,1,2:T(8,128)S(1)} copy(f32[160,16,1]{2,1,0:T(8,128)} %get-tuple-element.68) | data formatting | bytes 20480 | tf_op jit(solution)/shard_map/slice | solution.py:53
  85.9 5.1 %collective-permute-start.9 = (f32[160,16,1]{0,1,2:T(8,128)S(1)}, f32[160,16,1]{0,1,2:T(8,128)S(1)}, u32[]{:S(2)}, u32[]{:S(2)}) collective-permute-start(f32[160,16,1]{0,1,2:T(8,128)S(1)} %copy.122), channel_id=1, source_target_pairs={{0,7},{1,0},{2,1},{3,2},{4,3},{5,4},{6,5},{7,6},{8,15},{9,8},{10,9... | collective-permute-start | bytes 30728 | tf_op jit(solution)/shard_map/ppermute | solution.py:25
  92.7 4.5 %collective-permute-start.12 = (f32[160,1,1]{2,1,0:T(1,128)S(1)}, f32[160,1,1]{2,1,0:T(1,128)S(1)}, u32[]{:S(2)}, u32[]{:S(2)}) collective-permute-start(f32[160,1,1]{2,1,0:T(1,128)S(1)} %get-tuple-element.62), channel_id=1, source_target_pairs={{0,15},{1,8},{2,9},{3,10},{4,11},{5,12},{6,13},{7,14},{8,23},{9,16... | collective-permute-start | bytes 1928 | tf_op jit(solution)/shard_map/ppermute | solution.py:31
  97.1 1.7 copy.126
  99.4 2.4 %copy.127 = f32[160,16,1]{2,1,0:T(8,128)} copy(f32[160,16,1]{0,1,2:T(8,128)} %copy-done.14) | data formatting | bytes 20480 | tf_op jit(solution)/shard_map/ppermute | solution.py:25
  101.8 3.2 %fusion.13 = f32[160,16,128]{2,1,0:T(8,128)S(1)} fusion(f32[160,16,128]{2,1,0:T(8,128)S(1)} %bitcast.100, f32[160,16,127]{2,1,0:T(8,128)} %get-tuple-element.67, f32[160,16,1]{2,1,0:T(8,128)} %copy.126, f32[160,16,1]{2,1,0:T(8,128)} %copy.127, f32[160,16,127]{2,1,0:T(8,128)} %get-tuple-element.66, pred[128]{0:T(512)(128)(4,1)S(1)} %copy-done.26, ...), kind=kLoop, calls=%fused_computation.26 | loop fusion | flops 1638400 | bytes 5243136 | tf_op jit(solution)/shard_map/add | solution.py:47
  105.1 1.7 fusion.41
  106.9 2.1 %copy.120 = f32[4,40,16,1]{3,2,0,1:T(8,128)} copy(f32[4,40,16,1]{1,0,2,3:T(4,128)S(1)} %concatenate.243) | data formatting | bytes 20480 | tf_op jit(solution)/shard_map/concatenate | solution.py:36
  109.0 2.1 %copy.124 = f32[4,40,16,1]{3,2,0,1:T(8,128)} copy(f32[4,40,16,1]{1,0,2,3:T(4,128)S(1)} %concatenate.247) | data formatting | bytes 20480 | tf_op jit(solution)/shard_map/concatenate | solution.py:37
  111.2 5.6 %collective-permute-start.15 = (f32[160,1,1]{2,1,0:T(1,128)S(1)}, f32[160,1,1]{2,1,0:T(1,128)S(1)}, u32[]{:S(2)}, u32[]{:S(2)}) collective-permute-start(f32[160,1,1]{2,1,0:T(1,128)S(1)} %get-tuple-element.60), channel_id=1, source_target_pairs={{0,31},{1,24},{2,25},{3,26},{4,27},{5,28},{6,29},{7,30},{8,7},{9,0... | collective-permute-start | bytes 1928 | tf_op jit(solution)/shard_map/ppermute | solution.py:31
  117.3 1.8 collective-permute-done.15
  120.7 6.7 %fusion.4 = f32[4,40,16,128]{3,2,0,1:T(8,128)S(1)} fusion(f32[4,40,16,1]{3,2,0,1:T(8,128)} %copy.100, f32[4,40,16,1]{3,2,0,1:T(8,128)} %copy.104, f32[4,40,1,128]{3,2,0,1:T(1,128)S(1)} %copy.109, f32[4,40,1,128]{3,2,0,1:T(1,128)S(1)} %copy.113, f32[4,40,16,1]{3,2,0,1:T(8,128)} %copy.120, f32[4,40,16,1]{3,2,0,1:T(8,128)} %copy.124, ...), kind=kLoop, calls=%fused_computation.5 | loop fusion | flops 7864320 | bytes 15737120 | tf_op jit(solution)/shard_map/sub | solution.py:216
  129.1 6.2 %shard_map.232 = f32[4,8192]{1,0:T(4,128)} custom-call(s32[1,8192]{1,0:T(1,128)} %bitcast.124, f32[4,16,128]{2,1,0:T(8,128)} %fusion.21.table_ref), custom_call_target="tpu_custom_call" | custom-call | tf_op jit(solution)/shard_map/pallas_call | solution.py:188
  135.3 1.6 broadcast_multiply_fusion
  136.9 6.1 %all-to-all-start = ((f32[4,32,256]{2,0,1:T(4,128)}), f32[4,32,256]{2,0,1:T(4,128)S(1)}, u32[]{:S(2)}, u32[]{:S(2)}) async-start(f32[4,32,256]{2,0,1:T(4,128)} %broadcast_multiply_fusion), calls=%async_computation | async-start | bytes 262144 | tf_op jit(solution)/shard_map/all_to_all | solution.py:228
  143.0 2.6 %copy.144 = f32[4,40,16,128]{3,2,1,0:T(8,128)} copy(f32[4,40,16,128]{3,2,0,1:T(8,128)} %copy-done.9) | data formatting | bytes 2621440
  145.6 5.1 %all-to-all-done = f32[4,32,256]{2,0,1:T(4,128)S(1)} async-done(((f32[4,32,256]{2,0,1:T(4,128)}), f32[4,32,256]{2,0,1:T(4,128)S(1)}, u32[]{:S(2)}, u32[]{:S(2)}) %all-to-all-start) | async-done | bytes 131104 | tf_op jit(solution)/shard_map/all_to_all | solution.py:228
  151.4 6.9 %shard_map.233 = f32[4,8192]{1,0:T(4,128)} custom-call(s32[1,8192]{1,0:T(1,128)} %bitcast.125, f32[4,64,128]{2,1,0:T(8,128)} %reshape_reshape.7.table_ref), custom_call_target="tpu_custom_call" | custom-call | tf_op jit(solution)/shard_map/pallas_call | solution.py:188
  163.1 2.1 %collective-permute-start.18 = (f32[2,40,16,1]{1,2,3,0:T(8,128)S(1)}, f32[2,40,16,1]{1,2,3,0:T(8,128)S(1)}, u32[]{:S(2)}, u32[]{:S(2)}) collective-permute-start(f32[2,40,16,1]{1,2,3,0:T(8,128)S(1)} %copy.136), channel_id=1, source_target_pairs={{0,7},{1,0},{2,1},{3,2},{4,3},{5,4},{6,5},{7,6},{8,15},{9,8},{10,9... | collective-permute-start | bytes 15368 | tf_op jit(solution)/shard_map/ppermute | solution.py:25
  168.0 3.9 %collective-permute-done.19 = f32[2,40,16,1]{1,2,3,0:T(8,128)S(1)} collective-permute-done((f32[2,40,16,1]{1,2,3,0:T(8,128)S(1)}, f32[2,40,16,1]{1,2,3,0:T(8,128)S(1)}, u32[]{:S(2)}, u32[]{:S(2)}) %collective-permute-start.19) | collective-permute-done | bytes 5152 | tf_op jit(solution)/shard_map/ppermute | solution.py:25
  173.1 2.3 %multiply_subtract_fusion.1 = f32[2,40,16,128]{3,2,1,0:T(8,128)S(1)} fusion(f32[2,40,16,128]{3,2,1,0:T(8,128)S(1)} %get-tuple-element.109, f32[2,40,16,127]{3,2,1,0:T(8,128)} %get-tuple-element.97, f32[2,40,16,1]{3,2,1,0:T(8,128)} %copy.139, f32[2,40,16,1]{3,2,1,0:T(8,128)} %copy.137, f32[2,40,16,127]{3,2,1,0:T(8,128)} %get-tuple-element.96, ...), kind=kLoop, calls=%fused_computation.41 | loop fusion | flops 2785280 | bytes 4587520 | tf_op jit(solution)/shard_map/sub | solution.py:123
  183.2 2.5 %collective-permute-done.23 = f32[2,40,16,1]{1,2,3,0:T(8,128)S(1)} collective-permute-done((f32[2,40,16,1]{1,2,3,0:T(8,128)S(1)}, f32[2,40,16,1]{1,2,3,0:T(8,128)S(1)}, u32[]{:S(2)}, u32[]{:S(2)}) %collective-permute-start.23) | collective-permute-done | bytes 5152 | tf_op jit(solution)/shard_map/ppermute | solution.py:25
  186.9 3.0 %multiply_subtract_fusion = f32[2,40,16,128]{3,2,1,0:T(8,128)} fusion(f32[2,40,16,128]{3,2,1,0:T(8,128)S(1)} %multiply_subtract_fusion.1, f32[2,40,16,127]{3,2,1,0:T(8,128)} %get-tuple-element.87, f32[2,40,16,1]{3,2,1,0:T(8,128)} %copy.143, f32[2,40,16,1]{3,2,1,0:T(8,128)} %copy.141, f32[2,40,16,127]{3,2,1,0:T(8,128)S(1)} %get-tuple-element.86, ...), kind=kLoop, calls=%fused_computation.40 | loop fusion | flops 2785280 | bytes 4587520 | tf_op jit(solution)/shard_map/sub | solution.py:123
  (168 shorter events, 37.4 us)
Async XLA Ops:
  12.2 40.1 %collective-permute-start.5 = (f32[160,1,128]{2,1,0:T(1,128)}, f32[160,1,128]{2,1,0:T(1,128)S(1)}, u32[]{:S(2)}, u32[]{:S(2)}) collective-permute-start(f32[160,1,128]{2,1,0:T(1,128)} %get-tuple-element.76), channel_id=1, source_target_pairs={{0,24},{8,0},{16,8},{24,16},{1,25},{9,1},{17,9},{25,17},{2,26},{10... | collective-permute-start | bytes 245768 | tf_op jit(solution)/shard_map/ppermute | solution.py:23
  14.6 40.6 %collective-permute-start.2 = (f32[160,1,128]{2,1,0:T(1,128)S(1)}, f32[160,1,128]{2,1,0:T(1,128)S(1)}, u32[]{:S(2)}, u32[]{:S(2)}) collective-permute-start(f32[160,1,128]{2,1,0:T(1,128)S(1)} %get-tuple-element.77), channel_id=1, source_target_pairs={{0,8},{8,16},{16,24},{24,0},{1,9},{9,17},{17,25},{25,1},{2,10},{10... | collective-permute-start | bytes 245768 | tf_op jit(solution)/shard_map/ppermute | solution.py:23
  17.4 38.1 %collective-permute-start.3 = (f32[160,1,1]{2,1,0:T(1,128)}, f32[160,1,1]{2,1,0:T(1,128)S(1)}, u32[]{:S(2)}, u32[]{:S(2)}) collective-permute-start(f32[160,1,1]{2,1,0:T(1,128)} %get-tuple-element.75), channel_id=1, source_target_pairs={{0,9},{1,10},{2,11},{3,12},{4,13},{5,14},{6,15},{7,8},{8,17},{9,18... | collective-permute-start | bytes 1928 | tf_op jit(solution)/shard_map/ppermute | solution.py:31
  22.4 7.5 %copy-start = (f32[2560,128]{1,0:T(8,128)S(1)}, f32[2560,128]{1,0:T(8,128)}, u32[]{:S(2)}) copy-start(f32[2560,128]{1,0:T(8,128)} %shard_map.230) | copy-start | bytes 3932164
  24.4 9.3 %collective-permute-start = (f32[160,16,1]{0,1,2:T(8,128)S(1)}, f32[160,16,1]{0,1,2:T(8,128)S(1)}, u32[]{:S(2)}, u32[]{:S(2)}) collective-permute-start(f32[160,16,1]{0,1,2:T(8,128)S(1)} %copy.99), channel_id=1, source_target_pairs={{0,1},{1,2},{2,3},{3,4},{4,5},{5,6},{6,7},{7,0},{8,9},{9,10},{10,1... | collective-permute-start | bytes 30728 | tf_op jit(solution)/shard_map/ppermute | solution.py:25
  26.7 8.8 %collective-permute-start.1 = (f32[160,16,1]{0,1,2:T(8,128)S(1)}, f32[160,16,1]{0,1,2:T(8,128)S(1)}, u32[]{:S(2)}, u32[]{:S(2)}) collective-permute-start(f32[160,16,1]{0,1,2:T(8,128)S(1)} %copy.102), channel_id=1, source_target_pairs={{0,7},{1,0},{2,1},{3,2},{4,3},{5,4},{6,5},{7,6},{8,15},{9,8},{10,9... | collective-permute-start | bytes 30728 | tf_op jit(solution)/shard_map/ppermute | solution.py:25
  29.9 9.8 %copy-start.20 = (pred[128]{0:T(512)(128)(4,1)}, pred[128]{0:T(512)(128)(4,1)S(1)}, u32[]{:S(2)}) copy-start(pred[128]{0:T(512)(128)(4,1)S(1)} %get-tuple-element.120) | copy-start | bytes 388
  29.9 9.8 %copy-start.24 = (pred[128]{0:T(512)(128)(4,1)}, pred[128]{0:T(512)(128)(4,1)S(1)}, u32[]{:S(2)}) copy-start(pred[128]{0:T(512)(128)(4,1)S(1)} %get-tuple-element.121) | copy-start | bytes 388
  29.9 3.2 %copy-start.18 = (s32[1,32,256]{2,1,0:T(8,128)S(1)}, s32[1,32,256]{2,1,0:T(8,128)}, u32[]{:S(2)}) copy-start(s32[1,32,256]{2,1,0:T(8,128)} %param.33) | copy-start | bytes 98308
  31.4 29.4 %copy-start.3 = (f32[160,16,127]{2,1,0:T(8,128)}, f32[160,16,127]{2,1,0:T(8,128)S(1)}, u32[]{:S(2)}) copy-start(f32[160,16,127]{2,1,0:T(8,128)S(1)} %get-tuple-element.78) | copy-start | bytes 3901444
  31.5 8.2 %copy-start.31 = (pred[16]{0:T(512)(128)(4,1)}, pred[16]{0:T(512)(128)(4,1)S(1)}, u32[]{:S(2)}) copy-start(pred[16]{0:T(512)(128)(4,1)S(1)} %get-tuple-element.118) | copy-start | bytes 52
  31.5 8.2 %copy-start.33 = (pred[16]{0:T(512)(128)(4,1)}, pred[16]{0:T(512)(128)(4,1)S(1)}, u32[]{:S(2)}) copy-start(pred[16]{0:T(512)(128)(4,1)S(1)} %get-tuple-element.119) | copy-start | bytes 52
  33.8 21.8 %collective-permute-start.4 = (f32[160,1,1]{2,1,0:T(1,128)S(1)}, f32[160,1,1]{2,1,0:T(1,128)S(1)}, u32[]{:S(2)}, u32[]{:S(2)}) collective-permute-start(f32[160,1,1]{2,1,0:T(1,128)S(1)} %get-tuple-element.74), channel_id=1, source_target_pairs={{0,15},{1,8},{2,9},{3,10},{4,11},{5,12},{6,13},{7,14},{8,23},{9,16... | collective-permute-start | bytes 1928 | tf_op jit(solution)/shard_map/ppermute | solution.py:31
  35.4 20.1 %collective-permute-start.6 = (f32[160,1,1]{2,1,0:T(1,128)S(1)}, f32[160,1,1]{2,1,0:T(1,128)S(1)}, u32[]{:S(2)}, u32[]{:S(2)}) collective-permute-start(f32[160,1,1]{2,1,0:T(1,128)S(1)} %get-tuple-element.73), channel_id=1, source_target_pairs={{0,25},{1,26},{2,27},{3,28},{4,29},{5,30},{6,31},{7,24},{8,1},{9,2... | collective-permute-start | bytes 1928 | tf_op jit(solution)/shard_map/ppermute | solution.py:31
  52.3 6.9 %copy-start.7 = (f32[160,15,128]{2,1,0:T(8,128)S(1)}, f32[160,15,128]{2,1,0:T(8,128)}, u32[]{:S(2)}) copy-start(f32[160,15,128]{2,1,0:T(8,128)} %get-tuple-element.71) | copy-start | bytes 3686404
  52.3 5.5 %collective-permute-start.7 = (f32[160,1,1]{2,1,0:T(1,128)S(1)}, f32[160,1,1]{2,1,0:T(1,128)S(1)}, u32[]{:S(2)}, u32[]{:S(2)}) collective-permute-start(f32[160,1,1]{2,1,0:T(1,128)S(1)} %get-tuple-element.72), channel_id=1, source_target_pairs={{0,31},{1,24},{2,25},{3,26},{4,27},{5,28},{6,29},{7,30},{8,7},{9,0... | collective-permute-start | bytes 1928 | tf_op jit(solution)/shard_map/ppermute | solution.py:31
  60.6 1.8 copy-start.21
  75.0 4.0 %copy-start.1 = (f32[2560,128]{1,0:T(8,128)S(1)}, f32[2560,128]{1,0:T(8,128)}, u32[]{:S(2)}) copy-start(f32[2560,128]{1,0:T(8,128)} %shard_map.231) | copy-start | bytes 3932164
  83.9 8.7 %collective-permute-start.8 = (f32[160,16,1]{0,1,2:T(8,128)S(1)}, f32[160,16,1]{0,1,2:T(8,128)S(1)}, u32[]{:S(2)}, u32[]{:S(2)}) collective-permute-start(f32[160,16,1]{0,1,2:T(8,128)S(1)} %copy.119), channel_id=1, source_target_pairs={{0,1},{1,2},{2,3},{3,4},{4,5},{5,6},{6,7},{7,0},{8,9},{9,10},{10,1... | collective-permute-start | bytes 30728 | tf_op jit(solution)/shard_map/ppermute | solution.py:25
  85.9 12.9 %collective-permute-start.9 = (f32[160,16,1]{0,1,2:T(8,128)S(1)}, f32[160,16,1]{0,1,2:T(8,128)S(1)}, u32[]{:S(2)}, u32[]{:S(2)}) collective-permute-start(f32[160,16,1]{0,1,2:T(8,128)S(1)} %copy.122), channel_id=1, source_target_pairs={{0,7},{1,0},{2,1},{3,2},{4,3},{5,4},{6,5},{7,6},{8,15},{9,8},{10,9... | collective-permute-start | bytes 30728 | tf_op jit(solution)/shard_map/ppermute | solution.py:25
  91.8 19.3 %collective-permute-start.13 = (f32[160,1,128]{2,1,0:T(1,128)}, f32[160,1,128]{2,1,0:T(1,128)S(1)}, u32[]{:S(2)}, u32[]{:S(2)}) collective-permute-start(f32[160,1,128]{2,1,0:T(1,128)} %get-tuple-element.64), channel_id=1, source_target_pairs={{0,24},{8,0},{16,8},{24,16},{1,25},{9,1},{17,9},{25,17},{2,26},{10... | collective-permute-start | bytes 245768 | tf_op jit(solution)/shard_map/ppermute | solution.py:23
  92.4 24.6 %collective-permute-start.10 = (f32[160,1,128]{2,1,0:T(1,128)}, f32[160,1,128]{2,1,0:T(1,128)S(1)}, u32[]{:S(2)}, u32[]{:S(2)}) collective-permute-start(f32[160,1,128]{2,1,0:T(1,128)} %get-tuple-element.65), channel_id=1, source_target_pairs={{0,8},{8,16},{16,24},{24,0},{1,9},{9,17},{17,25},{25,1},{2,10},{10... | collective-permute-start | bytes 245768 | tf_op jit(solution)/shard_map/ppermute | solution.py:23
  92.5 24.8 %collective-permute-start.11 = (f32[160,1,1]{2,1,0:T(1,128)}, f32[160,1,1]{2,1,0:T(1,128)S(1)}, u32[]{:S(2)}, u32[]{:S(2)}) collective-permute-start(f32[160,1,1]{2,1,0:T(1,128)} %get-tuple-element.63), channel_id=1, source_target_pairs={{0,9},{1,10},{2,11},{3,12},{4,13},{5,14},{6,15},{7,8},{8,17},{9,18... | collective-permute-start | bytes 1928 | tf_op jit(solution)/shard_map/ppermute | solution.py:31
  92.6 6.2 %copy-start.12 = (f32[160,16,1]{0,1,2:T(8,128)}, f32[160,16,1]{0,1,2:T(8,128)S(1)}, u32[]{:S(2)}) copy-start(f32[160,16,1]{0,1,2:T(8,128)S(1)} %collective-permute-done.8) | copy-start | bytes 30724
  92.7 9.2 %copy-start.22 = (pred[128]{0:T(512)(128)(4,1)S(1)}, pred[128]{0:T(512)(128)(4,1)}, u32[]{:S(2)}) copy-start(pred[128]{0:T(512)(128)(4,1)} %copy-done.20) | copy-start | bytes 388
  92.7 9.2 %copy-start.26 = (pred[128]{0:T(512)(128)(4,1)S(1)}, pred[128]{0:T(512)(128)(4,1)}, u32[]{:S(2)}) copy-start(pred[128]{0:T(512)(128)(4,1)} %copy-done.24) | copy-start | bytes 388
  92.7 24.6 %collective-permute-start.12 = (f32[160,1,1]{2,1,0:T(1,128)S(1)}, f32[160,1,1]{2,1,0:T(1,128)S(1)}, u32[]{:S(2)}, u32[]{:S(2)}) collective-permute-start(f32[160,1,1]{2,1,0:T(1,128)S(1)} %get-tuple-element.62), channel_id=1, source_target_pairs={{0,15},{1,8},{2,9},{3,10},{4,11},{5,12},{6,13},{7,14},{8,23},{9,16... | collective-permute-start | bytes 1928 | tf_op jit(solution)/shard_map/ppermute | solution.py:31
  99.4 17.9 %collective-permute-start.14 = (f32[160,1,1]{2,1,0:T(1,128)S(1)}, f32[160,1,1]{2,1,0:T(1,128)S(1)}, u32[]{:S(2)}, u32[]{:S(2)}) collective-permute-start(f32[160,1,1]{2,1,0:T(1,128)S(1)} %get-tuple-element.61), channel_id=1, source_target_pairs={{0,25},{1,26},{2,27},{3,28},{4,29},{5,30},{6,31},{7,24},{8,1},{9,2... | collective-permute-start | bytes 1928 | tf_op jit(solution)/shard_map/ppermute | solution.py:31
  106.8 2.2 %copy-start.15 = (f32[160,16,1]{0,1,2:T(8,128)S(1)}, f32[160,16,1]{0,1,2:T(8,128)}, u32[]{:S(2)}) copy-start(f32[160,16,1]{0,1,2:T(8,128)} %copy-done.14) | copy-start | bytes 30724
  111.1 9.6 %copy-start.4 = (f32[160,16,127]{2,1,0:T(8,128)S(1)}, f32[160,16,127]{2,1,0:T(8,128)}, u32[]{:S(2)}) copy-start(f32[160,16,127]{2,1,0:T(8,128)} %copy-done.3) | copy-start | bytes 3901444
  111.1 9.6 %copy-start.17 = (f32[16,128]{1,0:T(8,128)S(1)}, f32[16,128]{1,0:T(8,128)}, u32[]{:S(2)}) copy-start(f32[16,128]{1,0:T(8,128)} %constant.190) | copy-start | bytes 24580
  111.1 9.6 %copy-start.23 = (pred[128]{0:T(512)(128)(4,1)S(1)}, pred[128]{0:T(512)(128)(4,1)}, u32[]{:S(2)}) copy-start(pred[128]{0:T(512)(128)(4,1)} %copy-done.20) | copy-start | bytes 388
  111.1 9.6 %copy-start.27 = (pred[128]{0:T(512)(128)(4,1)S(1)}, pred[128]{0:T(512)(128)(4,1)}, u32[]{:S(2)}) copy-start(pred[128]{0:T(512)(128)(4,1)} %copy-done.24) | copy-start | bytes 388
  111.1 9.6 %copy-start.32 = (pred[16]{0:T(512)(128)(4,1)S(1)}, pred[16]{0:T(512)(128)(4,1)}, u32[]{:S(2)}) copy-start(pred[16]{0:T(512)(128)(4,1)} %copy-done.31) | copy-start | bytes 52
  111.1 9.6 %copy-start.34 = (pred[16]{0:T(512)(128)(4,1)S(1)}, pred[16]{0:T(512)(128)(4,1)}, u32[]{:S(2)}) copy-start(pred[16]{0:T(512)(128)(4,1)} %copy-done.33) | copy-start | bytes 52
  111.2 8.0 %collective-permute-start.15 = (f32[160,1,1]{2,1,0:T(1,128)S(1)}, f32[160,1,1]{2,1,0:T(1,128)S(1)}, u32[]{:S(2)}, u32[]{:S(2)}) collective-permute-start(f32[160,1,1]{2,1,0:T(1,128)S(1)} %get-tuple-element.60), channel_id=1, source_target_pairs={{0,31},{1,24},{2,25},{3,26},{4,27},{5,28},{6,29},{7,30},{8,7},{9,0... | collective-permute-start | bytes 1928 | tf_op jit(solution)/shard_map/ppermute | solution.py:31
  136.9 13.8 %all-to-all-start = ((f32[4,32,256]{2,0,1:T(4,128)}), f32[4,32,256]{2,0,1:T(4,128)S(1)}, u32[]{:S(2)}, u32[]{:S(2)}) async-start(f32[4,32,256]{2,0,1:T(4,128)} %broadcast_multiply_fusion), calls=%async_computation | async-start | bytes 262144 | tf_op jit(solution)/shard_map/all_to_all | solution.py:228
  143.0 16.2 %copy-start.19 = (f32[4,16,128]{2,1,0:T(8,128)S(1)}, f32[4,16,128]{2,1,0:T(8,128)}, u32[]{:S(2)}) copy-start(f32[4,16,128]{2,1,0:T(8,128)} %param.38) | copy-start | bytes 98308
  143.0 16.2 %copy-start.2 = (f32[2,40,16,128]{3,2,1,0:T(8,128)S(1)}, f32[2,40,16,128]{3,2,1,0:T(8,128)}, u32[]{:S(2)}) copy-start(f32[2,40,16,128]{3,2,1,0:T(8,128)} %param.35) | copy-start | bytes 1966084
  143.0 16.2 %copy-start.11 = (f32[2,40,16,128]{3,2,1,0:T(8,128)S(1)}, f32[2,40,16,128]{3,2,1,0:T(8,128)}, u32[]{:S(2)}) copy-start(f32[2,40,16,128]{3,2,1,0:T(8,128)} %param.36) | copy-start | bytes 1966084
  163.1 3.8 %collective-permute-start.18 = (f32[2,40,16,1]{1,2,3,0:T(8,128)S(1)}, f32[2,40,16,1]{1,2,3,0:T(8,128)S(1)}, u32[]{:S(2)}, u32[]{:S(2)}) collective-permute-start(f32[2,40,16,1]{1,2,3,0:T(8,128)S(1)} %copy.136), channel_id=1, source_target_pairs={{0,7},{1,0},{2,1},{3,2},{4,3},{5,4},{6,5},{7,6},{8,15},{9,8},{10,9... | collective-permute-start | bytes 15368 | tf_op jit(solution)/shard_map/ppermute | solution.py:25
  165.5 6.5 %collective-permute-start.19 = (f32[2,40,16,1]{1,2,3,0:T(8,128)S(1)}, f32[2,40,16,1]{1,2,3,0:T(8,128)S(1)}, u32[]{:S(2)}, u32[]{:S(2)}) collective-permute-start(f32[2,40,16,1]{1,2,3,0:T(8,128)S(1)} %copy.138), channel_id=1, source_target_pairs={{0,1},{1,2},{2,3},{3,4},{4,5},{5,6},{6,7},{7,0},{8,9},{9,10},{10,1... | collective-permute-start | bytes 15368 | tf_op jit(solution)/shard_map/ppermute | solution.py:25
  165.5 7.6 %collective-permute-start.16 = (f32[2,40,1,128]{3,2,1,0:T(1,128)S(1)}, f32[2,40,1,128]{3,2,1,0:T(1,128)S(1)}, u32[]{:S(2)}, u32[]{:S(2)}) collective-permute-start(f32[2,40,1,128]{3,2,1,0:T(1,128)S(1)} %get-tuple-element.94), channel_id=1, source_target_pairs={{0,24},{8,0},{16,8},{24,16},{1,25},{9,1},{17,9},{25,17},{2,26},{10... | collective-permute-start | bytes 122888 | tf_op jit(solution)/shard_map/ppermute | solution.py:23
  165.6 7.5 %collective-permute-start.17 = (f32[2,40,1,128]{3,2,1,0:T(1,128)S(1)}, f32[2,40,1,128]{3,2,1,0:T(1,128)S(1)}, u32[]{:S(2)}, u32[]{:S(2)}) collective-permute-start(f32[2,40,1,128]{3,2,1,0:T(1,128)S(1)} %get-tuple-element.95), channel_id=1, source_target_pairs={{0,8},{8,16},{16,24},{24,0},{1,9},{9,17},{17,25},{25,1},{2,10},{10... | collective-permute-start | bytes 122888 | tf_op jit(solution)/shard_map/ppermute | solution.py:23
  178.1 4.0 %collective-permute-start.22 = (f32[2,40,16,1]{1,2,3,0:T(8,128)S(1)}, f32[2,40,16,1]{1,2,3,0:T(8,128)S(1)}, u32[]{:S(2)}, u32[]{:S(2)}) collective-permute-start(f32[2,40,16,1]{1,2,3,0:T(8,128)S(1)} %copy.140), channel_id=1, source_target_pairs={{0,7},{1,0},{2,1},{3,2},{4,3},{5,4},{6,5},{7,6},{8,15},{9,8},{10,9... | collective-permute-start | bytes 15368 | tf_op jit(solution)/shard_map/ppermute | solution.py:25
  179.2 6.5 %collective-permute-start.23 = (f32[2,40,16,1]{1,2,3,0:T(8,128)S(1)}, f32[2,40,16,1]{1,2,3,0:T(8,128)S(1)}, u32[]{:S(2)}, u32[]{:S(2)}) collective-permute-start(f32[2,40,16,1]{1,2,3,0:T(8,128)S(1)} %copy.142), channel_id=1, source_target_pairs={{0,1},{1,2},{2,3},{3,4},{4,5},{5,6},{6,7},{7,0},{8,9},{9,10},{10,1... | collective-permute-start | bytes 15368 | tf_op jit(solution)/shard_map/ppermute | solution.py:25
  180.5 6.4 %collective-permute-start.20 = (f32[2,40,1,128]{3,2,1,0:T(1,128)S(1)}, f32[2,40,1,128]{3,2,1,0:T(1,128)S(1)}, u32[]{:S(2)}, u32[]{:S(2)}) collective-permute-start(f32[2,40,1,128]{3,2,1,0:T(1,128)S(1)} %get-tuple-element.84), channel_id=1, source_target_pairs={{0,24},{8,0},{16,8},{24,16},{1,25},{9,1},{17,9},{25,17},{2,26},{10... | collective-permute-start | bytes 122888 | tf_op jit(solution)/shard_map/ppermute | solution.py:23
  180.5 6.4 %collective-permute-start.21 = (f32[2,40,1,128]{3,2,1,0:T(1,128)S(1)}, f32[2,40,1,128]{3,2,1,0:T(1,128)S(1)}, u32[]{:S(2)}, u32[]{:S(2)}) collective-permute-start(f32[2,40,1,128]{3,2,1,0:T(1,128)S(1)} %get-tuple-element.85), channel_id=1, source_target_pairs={{0,8},{8,16},{16,24},{24,0},{1,9},{9,17},{17,25},{25,1},{2,10},{10... | collective-permute-start | bytes 122888 | tf_op jit(solution)/shard_map/ppermute | solution.py:23
  (15 other events, 20.3 us)

commit v4 on v3

--- a/solution.py
+++ b/solution.py
@@ -47,76 +47,52 @@
     return values + jnp.where(position == 0, prev, jnp.where(position == 3, nxt, 0.0))
 
 
+def packed(values):
+    if values.size % 128:
+        return values
+    return values.reshape(-1, 128)
+
+
+def exchange(values, step_x, step_y):
+    return neighbour(packed(values), step_x, step_y).reshape(values.shape)
+
+
 def assemble(stiff):
     last_x, last_y = stiff.shape[1] - 1, stiff.shape[2] - 1
-    from_left = neighbour(stiff[:, :, last_y:], 0, 1)
-    from_right = neighbour(stiff[:, :, :1], 0, -1)
-    from_up = neighbour(stiff[:, last_x:, :], 1, 0)
-    from_down = neighbour(stiff[:, :1, :], -1, 0)
-    up_left = neighbour(stiff[:, last_x:, last_y:], 1, 1)
-    up_right = neighbour(stiff[:, last_x:, :1], 1, -1)
-    down_left = neighbour(stiff[:, :1, last_y:], -1, 1)
-    down_right = neighbour(stiff[:, :1, :1], -1, -1)
+    from_left = exchange(stiff[:, :, last_y], 0, 1)[..., None]
+    from_right = exchange(stiff[:, :, 0], 0, -1)[..., None]
     merged = pair_merge(stiff, from_left, from_right, 2)
-    merged_up = pair_merge(from_up, up_left, up_right, 2)
-    merged_down = pair_merge(from_down, down_left, down_right, 2)
-    return pair_merge(merged, merged_up, merged_down, 1)
-
-
-def stiff_kernel(state_ref, wmx_ref, wmy_ref, wx_ref, wy_ref, kx_ref, ay_ref, by_ref, out_ref):
-    highest = lax.Precision.HIGHEST
-    chunk = kx_ref.shape[0]
-    kx = kx_ref[...]
-    for part in range(state_ref.shape[0] // chunk):
-        rows = pl.ds(part * chunk, chunk)
-        block = state_ref[rows, :]
-        along_x = jnp.dot(kx, block, precision=highest, preferred_element_type=jnp.float32)
-        term_x = lax.dot_general(
-            kx,
-            wmx_ref[...] * along_x,
-            (((0,), (0,)), ((), ())),
-            precision=highest,
-            preferred_element_type=jnp.float32,
-        )
-        along_y = jnp.dot(block, ay_ref[...], precision=highest, preferred_element_type=jnp.float32)
-        term_y = jnp.dot(wmy_ref[...] * along_y, by_ref[...], precision=highest, preferred_element_type=jnp.float32)
-        out_ref[rows, :] = term_x * wy_ref[...] + term_y * wx_ref[...]
+    from_up = exchange(merged[:, last_x, :], 1, 0)[:, None, :]
+    from_down = exchange(merged[:, 0, :], -1, 0)[:, None, :]
+    return pair_merge(merged, from_up, from_down, 1)
 
 
 def stiffness(state_in, metric, derivative_np, weights_np):
     levels, xsize, ysize = state_in.shape
-    chunk = 128 if 128 % xsize == 0 else xsize
-    total = levels * xsize
-    tile = chunk * math.gcd(total // chunk, 5)
-    weight_x = np.tile(weights_np, xsize // 4)[:, None]
-    weight_y = np.tile(weights_np, ysize // 4)[None, :]
-    reps = chunk // xsize
-    wmx = jnp.tile(jnp.asarray(weight_x, jnp.float32) * metric[0], (reps, 1))
-    wmy = jnp.tile(jnp.asarray(weight_y, jnp.float32) * metric[1], (reps, 1))
-    wx = jnp.asarray(np.tile(np.broadcast_to(weight_x, (xsize, ysize)), (reps, 1)), jnp.float32)
-    wy = jnp.asarray(np.tile(np.broadcast_to(weight_y, (xsize, ysize)), (reps, 1)), jnp.float32)
-    kx = jnp.asarray(np.kron(np.eye(chunk // 4), derivative_np), jnp.float32)
-    ay = jnp.asarray(np.kron(np.eye(ysize // 4), derivative_np.T), jnp.float32)
-    by = jnp.asarray(np.kron(np.eye(ysize // 4), derivative_np), jnp.float32)
-    fixed = lambda step: (0, 0)
-    out = pl.pallas_call(
-        stiff_kernel,
-        grid=(total // tile,),
-        in_specs=[pl.BlockSpec((tile, ysize), lambda step: (step, 0))]
-        + [pl.BlockSpec((chunk, ysize), fixed)] * 4
-        + [pl.BlockSpec((chunk, chunk), fixed), pl.BlockSpec((ysize, ysize), fixed), pl.BlockSpec((ysize, ysize), fixed)],
-        out_specs=pl.BlockSpec((tile, ysize), lambda step: (step, 0)),
-        out_shape=jax.ShapeDtypeStruct((total, ysize), jnp.float32),
-    )(state_in.reshape(total, ysize), wmx, wmy, wx, wy, kx, ay, by)
-    return out.reshape(levels, xsize, ysize)
+    highest = lax.Precision.HIGHEST
+    block_x = jnp.asarray(np.kron(np.eye(xsize // 4), derivative_np), jnp.float32)
+    block_y = jnp.asarray(np.kron(np.eye(ysize // 4), derivative_np), jnp.float32)
+    weight_x = jnp.asarray(np.tile(weights_np, xsize // 4), jnp.float32)[:, None]
+    weight_y = jnp.asarray(np.tile(weights_np, ysize // 4), jnp.float32)[None, :]
+    along_x = jnp.einsum("ab,lby->lay", block_x, state_in, precision=highest)
+    term_x = (
+        jnp.einsum("ba,lby->lay", block_x, weight_x * metric[0] * along_x, precision=highest)
+        * weight_y
+    )
+    along_y = jnp.einsum("lxc,dc->lxd", state_in, block_y, precision=highest)
+    term_y = (
+        jnp.einsum("lxc,cd->lxd", weight_y * metric[1] * along_y, block_y, precision=highest)
+        * weight_x
+    )
+    return term_x + term_y
 
 
 def tracer_step(tracers, velocity):
     last_x, last_y = tracers.shape[-2] - 1, tracers.shape[-1] - 1
-    from_up = neighbour(tracers[..., last_x:, :], 1, 0)
-    from_down = neighbour(tracers[..., :1, :], -1, 0)
-    from_left = neighbour(tracers[..., last_y:], 0, 1)
-    from_right = neighbour(tracers[..., :1], 0, -1)
+    from_up = exchange(tracers[..., last_x, :], 1, 0)[..., None, :]
+    from_down = exchange(tracers[..., 0, :], -1, 0)[..., None, :]
+    from_left = exchange(tracers[..., last_y], 0, 1)[..., None]
+    from_right = exchange(tracers[..., 0], 0, -1)[..., None]
     west, east = shifted(tracers, from_up, from_down, tracers.ndim - 2)
     south, north = shifted(tracers, from_left, from_right, tracers.ndim - 1)
     return (

time: 191 us -> 111 us (0.58)
  local copies, waits for them, and re-layouts: 73.9 us -> 29.4 us
  starting transfers between devices: 41.5 us -> 19.7 us
  Pallas kernels: 28.1 us -> 13.1 us
  other arithmetic: 28.6 us -> 14.3 us
  blocking collectives: 0 us -> 11.8 us
  matrix products: 0 us -> 9.68 us
  waiting for transfers between devices: 16.5 us -> 11.3 us
    slice x18 -> x8, local copies, waits for them, and re-layouts: 26 us -> 3.75 us  [the longest x2 2.21 us: assemble(): from_right = exchange(stiff[:, :, 0], 0, -1)[..., None]]
    ppermute x8 -> x0, starting transfers between devices: 17.2 us -> none  [neighbour(): return lax.ppermute(values, ('gx', 'gy'), pairs)]
    pallas_call x2 -> x0, Pallas kernels: 15 us -> none  [stiffness(): pl.pallas_call(stiff_kernel, grid=(total // tile,), in_specs=[pl.BlockSpe...]
    another operation x2 -> x16, local copies, waits for them, and re-layouts: 1.26 us -> 14.8 us  [the longest x2 4.42 us: assemble(): from_right = exchange(stiff[:, :, 0], 0, -1)[..., None]]
    concatenate x14 -> x0, local copies, waits for them, and re-layouts: 12.6 us -> none  [the longest x7 6.34 us: shifted(): jnp.concatenate([lax.slice_in_dim(values, 1, size, axis=axis), after], ax...]
    ppermute x10 -> x0, local copies, waits for them, and re-layouts: 12.2 us -> none  [neighbour(): lax.ppermute(values, 'gy', [(j, (j + step_y) % count_y) for j in range(co...]
    all_to_all x0 -> x1, blocking collectives: none -> 11.8 us  [per_device(): lax.all_to_all(payload, ('gx', 'gy'), split_axis=1, concat_axis=1, tiled=...]
    sub x2, other arithmetic: 11.7 us -> 1.09 us  [per_device(): state_now = state_now - visc_coef * assemble(stiff) * inv_mass]
  transfers between devices with their start and end apart: 25 -> 16, of which waited for: 6 -> 7; matrix products, arithmetic and copies ran while one was open for 29% -> 14% of each run, Pallas kernels for 0% -> 0%
where the time goes in v4:
time: 111 us; the launch traced here: 110 us
  local copies, waits for them, and re-layouts  29.4 us (26%)
  starting transfers between devices  19.7 us (18%)
  other arithmetic  14.3 us (13%)
  Pallas kernels  13.1 us (12%)
  blocking collectives  11.8 us (11%)
  waiting for transfers between devices  11.3 us (10%)
  matrix products  9.68 us (9%)
    ppermute x8, starting transfers between devices, neighbour(): lax.ppermute(values, 'gy', [(j, (j + step_y) % count_y) for j in range(co...  15.1 us
    pallas_call x2, Pallas kernels, onehot_gather(): pl.pallas_call(gather_kernel, grid=(count // tile,), in_specs=[pl.BlockSp...  13.1 us
    all_to_all x1, blocking collectives, per_device(): lax.all_to_all(payload, ('gx', 'gy'), split_axis=1, concat_axis=1, tiled=...  11.8 us
    ppermute x8, waiting for transfers between devices, neighbour(): lax.ppermute(values, 'gy', [(j, (j + step_y) % count_y) for j in range(co...  7.06 us
    slice x8, local copies, waits for them, and re-layouts, shifted(): lax.slice_in_dim(values, 1, size, axis=axis)  6.24 us
    add x2, other arithmetic, pair_merge(): values + jnp.where(position == 0, prev, jnp.where(position == 3, nxt, 0.0))  6.09 us
    sub x2, other arithmetic, tracer_step(): tracers + diff_coef * (east + west + north + south - 4.0 * tracers)  5.3 us
    ppermute x8, starting transfers between devices, neighbour(): lax.ppermute(values, 'gx', [(i, (i + step_x) % count_x) for i in range(co...  4.63 us
  transfers between devices with their start and end apart: 16, of which 7 were waited for; matrix products, arithmetic and copies ran while one was open for 14% of the time, Pallas kernels for 0%

profile of v4, /device:TPU:0, one launch (start us, length us, event | category | flops | bytes accessed | tf_op | source)
XLA Modules:
  0.0 110.3 jit_solution(15848681492187787385)
XLA Ops:
  2.0 1.2 %fusion.6 = f32[160,16,128]{2,1,0:T(8,128)S(1)} fusion(f32[16,16,1]{1,0,2:T(8,128)S(1)} %copy-done.6, f32[160,16,128]{2,1,0:T(8,128)S(1)} %bitcast.109, f32[16,128]{1,0:T(8,128)S(1)} %get-tuple-element.91), kind=kOutput, calls=%fused_computation.14 | convolution fusion | flops 63242240 | bytes 2630656 | tf_op jit(solution)/shard_map/ab,lby->lay/dot_general | solution.py:77
  3.3 1.2 %fusion.5 = f32[160,16,128]{2,1,0:T(8,128)S(1)} fusion(f32[160,16,128]{2,1,0:T(8,128)S(1)} %fusion.6, f32[16,16,1]{1,0,2:T(8,128)S(1)} %copy-done.6, f32[128]{0:T(128)S(1)} %copy-done.12), kind=kOutput, calls=%fused_computation.12 | convolution fusion | flops 63242240 | bytes 2622976 | tf_op jit(solution)/shard_map/ba,lby->lay/dot_general | solution.py:79
  4.5 1.2 %fusion.2 = f32[160,16,128]{2,1,0:T(8,128)S(1)} fusion(f32[128,128,1]{1,0,2:T(8,128)S(1)} %copy-done.5, f32[160,16,128]{2,1,0:T(8,128)S(1)} %bitcast.110, f32[16,128]{1,0:T(8,128)S(1)} %get-tuple-element.90), kind=kOutput, calls=%fused_computation.6 | convolution fusion | flops 503644160 | bytes 2695168 | tf_op jit(solution)/shard_map/lxc,dc->lxd/dot_general | solution.py:82
  5.7 1.2 %fusion.1 = f32[160,16,128]{2,1,0:T(8,128)S(1)} fusion(f32[160,16,128]{2,1,0:T(8,128)S(1)} %fusion.5, f32[160,16,128]{2,1,0:T(8,128)S(1)} %fusion.2, f32[128,128,1]{1,0,2:T(8,128)S(1)} %copy-done.5, f32[16]{0:T(128)S(1)} %copy-done.11), kind=kOutput, calls=%fused_computation.4 | convolution fusion | flops 503971840 | bytes 3997760 | tf_op jit(solution)/shard_map/lxc,cd->lxd/dot_general | solution.py:84
  6.9 1.1 %slice_reduce_fusion.2 = (f32[160,16]{1,0:T(8,128)S(1)}, f32[160,16]{1,0:T(8,128)S(1)}) fusion(f32[160,16,128]{2,1,0:T(8,128)S(1)} %fusion.1), kind=kLoop, calls=%fused_computation.17 | loop fusion | bytes 40960 | tf_op jit(solution)/shard_map/slice | solution.py:63
  8.1 3.0 %collective-permute-start = (f32[20,128]{1,0:T(8,128)S(1)}, f32[20,128]{1,0:T(8,128)S(1)}, u32[]{:S(2)}, u32[]{:S(2)}) collective-permute-start(f32[20,128]{1,0:T(8,128)S(1)} %reshape_squeeze.39), channel_id=1, source_target_pairs={{0,1},{1,2},{2,3},{3,4},{4,5},{5,6},{6,7},{7,0},{8,9},{9,10},{10,1... | collective-permute-start | bytes 30728 | tf_op jit(solution)/shard_map/ppermute | solution.py:25
  11.2 3.1 %collective-permute-start.1 = (f32[20,128]{1,0:T(8,128)S(1)}, f32[20,128]{1,0:T(8,128)S(1)}, u32[]{:S(2)}, u32[]{:S(2)}) collective-permute-start(f32[20,128]{1,0:T(8,128)S(1)} %reshape_squeeze.40), channel_id=1, source_target_pairs={{0,7},{1,0},{2,1},{3,2},{4,3},{5,4},{6,5},{7,6},{8,15},{9,8},{10,9... | collective-permute-start | bytes 30728 | tf_op jit(solution)/shard_map/ppermute | solution.py:25
  14.3 1.5 %fusion.42 = (f32[160,16,127]{2,1,0:T(8,128)S(1)}, f32[160,16,127]{2,1,0:T(8,128)}) fusion(f32[160,16,128]{2,1,0:T(8,128)S(1)} %fusion.1), kind=kLoop, calls=%fused_computation.96 | loop fusion | bytes 5201920 | tf_op jit(solution)/shard_map/slice | solution.py:37
  15.9 0.6 copy.62
  16.5 2.2 %broadcast_in_dim_reshape.48 = f32[160,16,1]{2,1,0:T(8,128)} reshape(f32[20,128]{1,0:T(8,128)S(1)} %collective-permute-done) | data formatting | bytes 20480 | tf_op jit(solution)/shard_map/broadcast_in_dim;reshape | solution.py:62
  18.7 2.2 %broadcast_in_dim_reshape.49 = f32[160,16,1]{2,1,0:T(8,128)} reshape(f32[20,128]{1,0:T(8,128)S(1)} %collective-permute-done.1) | data formatting | bytes 20480 | tf_op jit(solution)/shard_map/broadcast_in_dim;reshape | solution.py:63
  20.9 2.8 %fusion.7 = f32[160,16,128]{2,1,0:T(8,128)S(1)} fusion(f32[160,16,128]{2,1,0:T(8,128)S(1)} %fusion.1, f32[160,16,127]{2,1,0:T(8,128)} %get-tuple-element.71, f32[160,16,1]{2,1,0:T(8,128)} %broadcast_in_dim_reshape.48, f32[160,16,1]{2,1,0:T(8,128)} %broadcast_in_dim_reshape.49, f32[160,16,127]{2,1,0:T(8,128)S(1)} %get-tuple-element.70, ...), kind=kLoop, calls=%fused_computation.20 | loop fusion | flops 1638400 | bytes 5243136 | tf_op jit(solution)/shard_map/add | solution.py:47
  24.0 1.7 %collective-permute-start.3 = (f32[160,128]{1,0:T(8,128)S(1)}, f32[160,128]{1,0:T(8,128)S(1)}, u32[]{:S(2)}, u32[]{:S(2)}) collective-permute-start(f32[160,128]{1,0:T(8,128)S(1)} %bitcast.118), channel_id=1, source_target_pairs={{0,24},{8,0},{16,8},{24,16},{1,25},{9,1},{17,9},{25,17},{2,26},{10... | collective-permute-start | bytes 245768 | tf_op jit(solution)/shard_map/ppermute | solution.py:23
  25.9 1.9 %collective-permute-done.2 = f32[160,128]{1,0:T(8,128)S(1)} collective-permute-done((f32[160,128]{1,0:T(8,128)S(1)}, f32[160,128]{1,0:T(8,128)S(1)}, u32[]{:S(2)}, u32[]{:S(2)}) %collective-permute-start.2) | collective-permute-done | bytes 81952 | tf_op jit(solution)/shard_map/ppermute | solution.py:23
  28.5 1.2 %fusion.3 = f32[160,16,128]{2,1,0:T(8,128)S(1)} fusion(f32[160,16,128]{2,1,0:T(8,128)S(1)} %fusion.10, f32[16,16,1]{1,0,2:T(8,128)S(1)} %copy-done.6, f32[16,128]{1,0:T(8,128)S(1)} %get-tuple-element.91), kind=kOutput, calls=%fused_computation.8 | convolution fusion | flops 63242240 | bytes 2630656 | tf_op jit(solution)/shard_map/ab,lby->lay/dot_general | solution.py:77
  29.7 1.2 %convolution_multiply_fusion.1 = f32[160,16,128]{2,1,0:T(8,128)S(1)} fusion(f32[160,16,128]{2,1,0:T(8,128)S(1)} %fusion.10, f32[128,128,1]{1,0,2:T(8,128)S(1)} %copy-done.5, f32[16,128]{1,0:T(8,128)S(1)} %get-tuple-element.90), kind=kOutput, calls=%fused_computation.2 | convolution fusion | flops 503644160 | bytes 2695168 | tf_op jit(solution)/shard_map/lxc,dc->lxd/dot_general | solution.py:82
  30.9 1.2 %fusion.4 = f32[160,16,128]{2,1,0:T(8,128)S(1)} fusion(f32[160,16,128]{2,1,0:T(8,128)S(1)} %fusion.3, f32[16,16,1]{1,0,2:T(8,128)S(1)} %copy-done.6, f32[128]{0:T(128)S(1)} %copy-done.12), kind=kOutput, calls=%fused_computation.10 | convolution fusion | flops 63242240 | bytes 2622976 | tf_op jit(solution)/shard_map/ba,lby->lay/dot_general | solution.py:79
  32.2 1.2 %fusion = f32[160,16,128]{2,1,0:T(8,128)S(1)} fusion(f32[160,16,128]{2,1,0:T(8,128)S(1)} %fusion.4, f32[160,16,128]{2,1,0:T(8,128)S(1)} %convolution_multiply_fusion.1, f32[128,128,1]{1,0,2:T(8,128)S(1)} %copy-done.5, f32[16]{0:T(128)S(1)} %copy-done.11), kind=kOutput, calls=%fused_computation.1 | convolution fusion | flops 503971840 | bytes 3997760 | tf_op jit(solution)/shard_map/lxc,cd->lxd/dot_general | solution.py:84
  33.4 1.1 %slice_reduce_fusion = (f32[160,16]{1,0:T(8,128)S(1)}, f32[160,16]{1,0:T(8,128)S(1)}) fusion(f32[160,16,128]{2,1,0:T(8,128)S(1)} %fusion), kind=kLoop, calls=%fused_computation.15 | loop fusion | bytes 40960 | tf_op jit(solution)/shard_map/slice | solution.py:63
  34.7 4.8 %collective-permute-start.5 = (f32[20,128]{1,0:T(8,128)S(1)}, f32[20,128]{1,0:T(8,128)S(1)}, u32[]{:S(2)}, u32[]{:S(2)}) collective-permute-start(f32[20,128]{1,0:T(8,128)S(1)} %reshape_squeeze.42), channel_id=1, source_target_pairs={{0,7},{1,0},{2,1},{3,2},{4,3},{5,4},{6,5},{7,6},{8,15},{9,8},{10,9... | collective-permute-start | bytes 30728 | tf_op jit(solution)/shard_map/ppermute | solution.py:25
  39.5 1.9 %fusion.39 = (f32[160,16,127]{2,1,0:T(8,128)}, f32[160,16,127]{2,1,0:T(8,128)}) fusion(f32[160,16,128]{2,1,0:T(8,128)S(1)} %fusion), kind=kLoop, calls=%fused_computation.93 | loop fusion | bytes 5201920 | tf_op jit(solution)/shard_map/slice | solution.py:37
  41.4 2.2 %broadcast_in_dim_reshape.50 = f32[160,16,1]{2,1,0:T(8,128)} reshape(f32[20,128]{1,0:T(8,128)S(1)} %collective-permute-done.4) | data formatting | bytes 20480 | tf_op jit(solution)/shard_map/broadcast_in_dim;reshape | solution.py:62
  43.6 2.2 %broadcast_in_dim_reshape.51 = f32[160,16,1]{2,1,0:T(8,128)} reshape(f32[20,128]{1,0:T(8,128)S(1)} %collective-permute-done.5) | data formatting | bytes 20480 | tf_op jit(solution)/shard_map/broadcast_in_dim;reshape | solution.py:63
  45.8 3.2 %fusion.11 = f32[160,16,128]{2,1,0:T(8,128)S(1)} fusion(f32[160,16,128]{2,1,0:T(8,128)S(1)} %fusion, f32[160,16,127]{2,1,0:T(8,128)} %get-tuple-element.65, f32[160,16,1]{2,1,0:T(8,128)} %broadcast_in_dim_reshape.50, f32[160,16,1]{2,1,0:T(8,128)} %broadcast_in_dim_reshape.51, f32[160,16,127]{2,1,0:T(8,128)} %get-tuple-element.64, ...), kind=kLoop, calls=%fused_computation.28 | loop fusion | flops 1638400 | bytes 5243136 | tf_op jit(solution)/shard_map/add | solution.py:47
  49.2 1.2 %collective-permute-start.6 = (f32[160,128]{1,0:T(8,128)S(1)}, f32[160,128]{1,0:T(8,128)S(1)}, u32[]{:S(2)}, u32[]{:S(2)}) collective-permute-start(f32[160,128]{1,0:T(8,128)S(1)} %bitcast.121), channel_id=1, source_target_pairs={{0,8},{8,16},{16,24},{24,0},{1,9},{9,17},{17,25},{25,1},{2,10},{10... | collective-permute-start | bytes 245768 | tf_op jit(solution)/shard_map/ppermute | solution.py:23
  51.2 1.9 %collective-permute-done.6 = f32[160,128]{1,0:T(8,128)S(1)} collective-permute-done((f32[160,128]{1,0:T(8,128)S(1)}, f32[160,128]{1,0:T(8,128)S(1)}, u32[]{:S(2)}, u32[]{:S(2)}) %collective-permute-start.6) | collective-permute-done | bytes 81952 | tf_op jit(solution)/shard_map/ppermute | solution.py:23
  54.1 1.0 copy-done.4
  55.0 0.6 fusion.17.table_ref
  55.7 6.2 %shard_map.176 = f32[4,8192]{1,0:T(4,128)} custom-call(s32[1,8192]{1,0:T(1,128)} %bitcast.117, f32[4,16,128]{2,1,0:T(8,128)} %fusion.17.table_ref), custom_call_target="tpu_custom_call" | custom-call | tf_op jit(solution)/shard_map/pallas_call | solution.py:164
  61.9 0.9 broadcast_multiply_fusion
  62.8 11.8 %all_to_all.5 = f32[4,32,256]{2,0,1:T(4,128)S(1)} all-to-all(f32[4,32,256]{2,0,1:T(4,128)S(1)} %broadcast_multiply_fusion), channel_id=1, replica_groups=mesh['gx'=4,'gy'=8] {'gx','gy'}, dimensions={1} | all-to-all | bytes 262144 | tf_op jit(solution)/shard_map/all_to_all | solution.py:204
  74.7 0.7 reshape_reshape.3.table_ref
  75.3 6.9 %shard_map.177 = f32[4,8192]{1,0:T(4,128)} custom-call(s32[1,8192]{1,0:T(1,128)} %bitcast.134, f32[4,64,128]{2,1,0:T(8,128)} %reshape_reshape.3.table_ref), custom_call_target="tpu_custom_call" | custom-call | tf_op jit(solution)/shard_map/pallas_call | solution.py:164
  82.2 0.9 copy.63
  83.3 1.2 %fusion.48 = (f32[2,40,16,127]{3,2,1,0:T(8,128)}, f32[2,40,16,127]{3,2,1,0:T(8,128)}) fusion(f32[2,40,16,128]{3,2,1,0:T(8,128)S(1)} %get-tuple-element.87), kind=kLoop, calls=%fused_computation.102 | loop fusion | bytes 2600960 | tf_op jit(solution)/shard_map/slice | solution.py:37
  85.3 2.1 %collective-permute-start.10 = (f32[10,128]{1,0:T(8,128)S(1)}, f32[10,128]{1,0:T(8,128)S(1)}, u32[]{:S(2)}, u32[]{:S(2)}) collective-permute-start(f32[10,128]{1,0:T(8,128)S(1)} %reshape_squeeze.46), channel_id=1, source_target_pairs={{0,7},{1,0},{2,1},{3,2},{4,3},{5,4},{6,5},{7,6},{8,15},{9,8},{10,9... | collective-permute-start | bytes 15368 | tf_op jit(solution)/shard_map/ppermute | solution.py:25
  88.1 0.9 collective-permute-done.10
  88.9 1.3 %broadcast_in_dim_reshape.52 = f32[2,40,16,1]{3,2,1,0:T(8,128)} reshape(f32[10,128]{1,0:T(8,128)S(1)} %collective-permute-done.10) | data formatting | bytes 10240 | tf_op jit(solution)/shard_map/broadcast_in_dim;reshape | solution.py:95
  90.3 3.5 %collective-permute-done.11 = f32[10,128]{1,0:T(8,128)S(1)} collective-permute-done((f32[10,128]{1,0:T(8,128)S(1)}, f32[10,128]{1,0:T(8,128)S(1)}, u32[]{:S(2)}, u32[]{:S(2)}) %collective-permute-start.11) | collective-permute-done | bytes 5152 | tf_op jit(solution)/shard_map/ppermute | solution.py:25
  93.8 1.3 %broadcast_in_dim_reshape.53 = f32[2,40,16,1]{3,2,1,0:T(8,128)} reshape(f32[10,128]{1,0:T(8,128)S(1)} %collective-permute-done.11) | data formatting | bytes 10240 | tf_op jit(solution)/shard_map/broadcast_in_dim;reshape | solution.py:94
  95.1 2.3 %multiply_subtract_fusion.1 = f32[2,40,16,128]{3,2,1,0:T(8,128)S(1)} fusion(f32[2,40,16,128]{3,2,1,0:T(8,128)S(1)} %get-tuple-element.87, f32[2,40,16,127]{3,2,1,0:T(8,128)} %get-tuple-element.85, f32[2,40,16,1]{3,2,1,0:T(8,128)} %broadcast_in_dim_reshape.53, f32[2,40,16,1]{3,2,1,0:T(8,128)} %broadcast_in_dim_reshape.52, ...), kind=kLoop, calls=%fused_computation.48 | loop fusion | flops 2785280 | bytes 4587520 | tf_op jit(solution)/shard_map/sub | solution.py:99
  98.3 1.3 %collective-permute-start.14 = (f32[10,128]{1,0:T(8,128)S(1)}, f32[10,128]{1,0:T(8,128)S(1)}, u32[]{:S(2)}, u32[]{:S(2)}) collective-permute-start(f32[10,128]{1,0:T(8,128)S(1)} %reshape_squeeze.50), channel_id=1, source_target_pairs={{0,7},{1,0},{2,1},{3,2},{4,3},{5,4},{6,5},{7,6},{8,15},{9,8},{10,9... | collective-permute-start | bytes 15368 | tf_op jit(solution)/shard_map/ppermute | solution.py:25
  99.6 0.8 collective-permute-start.15
  101.0 1.1 fusion.45
  102.0 1.3 %broadcast_in_dim_reshape.54 = f32[2,40,16,1]{3,2,1,0:T(8,128)} reshape(f32[10,128]{1,0:T(8,128)S(1)} %collective-permute-done.14) | data formatting | bytes 10240 | tf_op jit(solution)/shard_map/broadcast_in_dim;reshape | solution.py:95
  103.3 2.7 %collective-permute-done.15 = f32[10,128]{1,0:T(8,128)S(1)} collective-permute-done((f32[10,128]{1,0:T(8,128)S(1)}, f32[10,128]{1,0:T(8,128)S(1)}, u32[]{:S(2)}, u32[]{:S(2)}) %collective-permute-start.15) | collective-permute-done | bytes 5152 | tf_op jit(solution)/shard_map/ppermute | solution.py:25
  106.0 1.3 %broadcast_in_dim_reshape.55 = f32[2,40,16,1]{3,2,1,0:T(8,128)} reshape(f32[10,128]{1,0:T(8,128)S(1)} %collective-permute-done.15) | data formatting | bytes 10240 | tf_op jit(solution)/shard_map/broadcast_in_dim;reshape | solution.py:94
  107.3 3.0 %multiply_subtract_fusion = f32[2,40,16,128]{3,2,1,0:T(8,128)} fusion(f32[2,40,16,128]{3,2,1,0:T(8,128)S(1)} %multiply_subtract_fusion.1, f32[2,40,16,127]{3,2,1,0:T(8,128)} %get-tuple-element.77, f32[2,40,16,1]{3,2,1,0:T(8,128)} %broadcast_in_dim_reshape.55, f32[2,40,16,1]{3,2,1,0:T(8,128)} %broadcast_in_dim_reshape.54, ...), kind=kLoop, calls=%fused_computation.47 | loop fusion | flops 2785280 | bytes 4587520 | tf_op jit(solution)/shard_map/sub | solution.py:99
  (76 shorter events, 7.7 us)
Async XLA Ops:
  0.6 0.7 copy-start.11
  0.6 0.7 copy-start.12
  0.7 0.9 copy-start.6
  0.7 1.3 %copy-start.1 = (f32[4,40,16,128]{3,2,1,0:T(8,128)S(1)}, f32[4,40,16,128]{3,2,1,0:T(8,128)}, u32[]{:S(2)}) copy-start(f32[4,40,16,128]{3,2,1,0:T(8,128)} %param.25) | copy-start | bytes 3932164
  0.7 0.8 copy-start.10
  3.2 1.3 %copy-start.5 = (f32[128,128,1]{1,0,2:T(8,128)S(1)}, f32[128,128,1]{1,0,2:T(8,128)}, u32[]{:S(2)}) copy-start(f32[128,128,1]{1,0,2:T(8,128)} %constant.172) | copy-start | bytes 196612
  8.1 8.4 %collective-permute-start = (f32[20,128]{1,0:T(8,128)S(1)}, f32[20,128]{1,0:T(8,128)S(1)}, u32[]{:S(2)}, u32[]{:S(2)}) collective-permute-start(f32[20,128]{1,0:T(8,128)S(1)} %reshape_squeeze.39), channel_id=1, source_target_pairs={{0,1},{1,2},{2,3},{3,4},{4,5},{5,6},{6,7},{7,0},{8,9},{9,10},{10,1... | collective-permute-start | bytes 30728 | tf_op jit(solution)/shard_map/ppermute | solution.py:25
  11.2 4.6 %copy-start.13 = (s32[1,32]{1,0:T(1,128)S(1)}, s32[1,32]{1,0:T(1,128)}, u32[]{:S(2)}) copy-start(s32[1,32]{1,0:T(1,128)} %param.28) | copy-start | bytes 388
  11.2 4.7 %copy-start.8 = (s32[1,32,256]{2,1,0:T(8,128)S(1)}, s32[1,32,256]{2,1,0:T(8,128)}, u32[]{:S(2)}) copy-start(s32[1,32,256]{2,1,0:T(8,128)} %param.27) | copy-start | bytes 98308
  11.2 7.5 %collective-permute-start.1 = (f32[20,128]{1,0:T(8,128)S(1)}, f32[20,128]{1,0:T(8,128)S(1)}, u32[]{:S(2)}, u32[]{:S(2)}) collective-permute-start(f32[20,128]{1,0:T(8,128)S(1)} %reshape_squeeze.40), channel_id=1, source_target_pairs={{0,7},{1,0},{2,1},{3,2},{4,3},{5,4},{6,5},{7,6},{8,15},{9,8},{10,9... | collective-permute-start | bytes 30728 | tf_op jit(solution)/shard_map/ppermute | solution.py:25
  23.9 3.9 %collective-permute-start.2 = (f32[160,128]{1,0:T(8,128)S(1)}, f32[160,128]{1,0:T(8,128)S(1)}, u32[]{:S(2)}, u32[]{:S(2)}) collective-permute-start(f32[160,128]{1,0:T(8,128)S(1)} %bitcast.120), channel_id=1, source_target_pairs={{0,8},{8,16},{16,24},{24,0},{1,9},{9,17},{17,25},{25,1},{2,10},{10... | collective-permute-start | bytes 245768 | tf_op jit(solution)/shard_map/ppermute | solution.py:23
  24.0 4.0 %copy-start.2 = (f32[4,40,16,128]{3,2,1,0:T(8,128)S(1)}, f32[4,40,16,128]{3,2,1,0:T(8,128)}, u32[]{:S(2)}) copy-start(f32[4,40,16,128]{3,2,1,0:T(8,128)} %param.25) | copy-start | bytes 3932164
  24.0 3.9 %copy-start.7 = (f32[16,128]{1,0:T(8,128)S(1)}, f32[16,128]{1,0:T(8,128)}, u32[]{:S(2)}) copy-start(f32[16,128]{1,0:T(8,128)} %constant.170) | copy-start | bytes 24580
  24.0 3.9 %collective-permute-start.3 = (f32[160,128]{1,0:T(8,128)S(1)}, f32[160,128]{1,0:T(8,128)S(1)}, u32[]{:S(2)}, u32[]{:S(2)}) collective-permute-start(f32[160,128]{1,0:T(8,128)S(1)} %bitcast.118), channel_id=1, source_target_pairs={{0,24},{8,0},{16,8},{24,16},{1,25},{9,1},{17,9},{25,17},{2,26},{10... | collective-permute-start | bytes 245768 | tf_op jit(solution)/shard_map/ppermute | solution.py:23
  34.6 6.8 %collective-permute-start.4 = (f32[20,128]{1,0:T(8,128)S(1)}, f32[20,128]{1,0:T(8,128)S(1)}, u32[]{:S(2)}, u32[]{:S(2)}) collective-permute-start(f32[20,128]{1,0:T(8,128)S(1)} %reshape_squeeze.41), channel_id=1, source_target_pairs={{0,1},{1,2},{2,3},{3,4},{4,5},{5,6},{6,7},{7,0},{8,9},{9,10},{10,1... | collective-permute-start | bytes 30728 | tf_op jit(solution)/shard_map/ppermute | solution.py:25
  34.7 8.9 %collective-permute-start.5 = (f32[20,128]{1,0:T(8,128)S(1)}, f32[20,128]{1,0:T(8,128)S(1)}, u32[]{:S(2)}, u32[]{:S(2)}) collective-permute-start(f32[20,128]{1,0:T(8,128)S(1)} %reshape_squeeze.42), channel_id=1, source_target_pairs={{0,7},{1,0},{2,1},{3,2},{4,3},{5,4},{6,5},{7,6},{8,15},{9,8},{10,9... | collective-permute-start | bytes 30728 | tf_op jit(solution)/shard_map/ppermute | solution.py:25
  49.2 3.9 %collective-permute-start.6 = (f32[160,128]{1,0:T(8,128)S(1)}, f32[160,128]{1,0:T(8,128)S(1)}, u32[]{:S(2)}, u32[]{:S(2)}) collective-permute-start(f32[160,128]{1,0:T(8,128)S(1)} %bitcast.121), channel_id=1, source_target_pairs={{0,8},{8,16},{16,24},{24,0},{1,9},{9,17},{17,25},{25,1},{2,10},{10... | collective-permute-start | bytes 245768 | tf_op jit(solution)/shard_map/ppermute | solution.py:23
  50.4 3.0 %collective-permute-start.7 = (f32[160,128]{1,0:T(8,128)S(1)}, f32[160,128]{1,0:T(8,128)S(1)}, u32[]{:S(2)}, u32[]{:S(2)}) collective-permute-start(f32[160,128]{1,0:T(8,128)S(1)} %bitcast.119), channel_id=1, source_target_pairs={{0,24},{8,0},{16,8},{24,16},{1,25},{9,1},{17,9},{25,17},{2,26},{10... | collective-permute-start | bytes 245768 | tf_op jit(solution)/shard_map/ppermute | solution.py:23
  54.0 1.1 copy-start.4
  54.0 29.1 %copy-start.9 = (f32[4,16,128]{2,1,0:T(8,128)S(1)}, f32[4,16,128]{2,1,0:T(8,128)}, u32[]{:S(2)}) copy-start(f32[4,16,128]{2,1,0:T(8,128)} %param.32) | copy-start | bytes 98308
  54.0 29.1 %copy-start = (f32[2,40,16,128]{3,2,1,0:T(8,128)S(1)}, f32[2,40,16,128]{3,2,1,0:T(8,128)}, u32[]{:S(2)}) copy-start(f32[2,40,16,128]{3,2,1,0:T(8,128)} %param.29) | copy-start | bytes 1966084
  54.0 29.1 %copy-start.3 = (f32[2,40,16,128]{3,2,1,0:T(8,128)S(1)}, f32[2,40,16,128]{3,2,1,0:T(8,128)}, u32[]{:S(2)}) copy-start(f32[2,40,16,128]{3,2,1,0:T(8,128)} %param.30) | copy-start | bytes 1966084
  85.3 3.7 %collective-permute-start.10 = (f32[10,128]{1,0:T(8,128)S(1)}, f32[10,128]{1,0:T(8,128)S(1)}, u32[]{:S(2)}, u32[]{:S(2)}) collective-permute-start(f32[10,128]{1,0:T(8,128)S(1)} %reshape_squeeze.46), channel_id=1, source_target_pairs={{0,7},{1,0},{2,1},{3,2},{4,3},{5,4},{6,5},{7,6},{8,15},{9,8},{10,9... | collective-permute-start | bytes 15368 | tf_op jit(solution)/shard_map/ppermute | solution.py:25
  87.4 6.4 %collective-permute-start.11 = (f32[10,128]{1,0:T(8,128)S(1)}, f32[10,128]{1,0:T(8,128)S(1)}, u32[]{:S(2)}, u32[]{:S(2)}) collective-permute-start(f32[10,128]{1,0:T(8,128)S(1)} %reshape_squeeze.47), channel_id=1, source_target_pairs={{0,1},{1,2},{2,3},{3,4},{4,5},{5,6},{6,7},{7,0},{8,9},{9,10},{10,1... | collective-permute-start | bytes 15368 | tf_op jit(solution)/shard_map/ppermute | solution.py:25
  87.4 7.7 %collective-permute-start.8 = (f32[80,128]{1,0:T(8,128)S(1)}, f32[80,128]{1,0:T(8,128)S(1)}, u32[]{:S(2)}, u32[]{:S(2)}) collective-permute-start(f32[80,128]{1,0:T(8,128)S(1)} %bitcast.132), channel_id=1, source_target_pairs={{0,24},{8,0},{16,8},{24,16},{1,25},{9,1},{17,9},{25,17},{2,26},{10... | collective-permute-start | bytes 122888 | tf_op jit(solution)/shard_map/ppermute | solution.py:23
  87.5 7.6 %collective-permute-start.9 = (f32[80,128]{1,0:T(8,128)S(1)}, f32[80,128]{1,0:T(8,128)S(1)}, u32[]{:S(2)}, u32[]{:S(2)}) collective-permute-start(f32[80,128]{1,0:T(8,128)S(1)} %bitcast.130), channel_id=1, source_target_pairs={{0,8},{8,16},{16,24},{24,0},{1,9},{9,17},{17,25},{25,1},{2,10},{10... | collective-permute-start | bytes 122888 | tf_op jit(solution)/shard_map/ppermute | solution.py:23
  98.3 3.7 %collective-permute-start.14 = (f32[10,128]{1,0:T(8,128)S(1)}, f32[10,128]{1,0:T(8,128)S(1)}, u32[]{:S(2)}, u32[]{:S(2)}) collective-permute-start(f32[10,128]{1,0:T(8,128)S(1)} %reshape_squeeze.50), channel_id=1, source_target_pairs={{0,7},{1,0},{2,1},{3,2},{4,3},{5,4},{6,5},{7,6},{8,15},{9,8},{10,9... | collective-permute-start | bytes 15368 | tf_op jit(solution)/shard_map/ppermute | solution.py:25
  99.6 6.4 %collective-permute-start.15 = (f32[10,128]{1,0:T(8,128)S(1)}, f32[10,128]{1,0:T(8,128)S(1)}, u32[]{:S(2)}, u32[]{:S(2)}) collective-permute-start(f32[10,128]{1,0:T(8,128)S(1)} %reshape_squeeze.51), channel_id=1, source_target_pairs={{0,1},{1,2},{2,3},{3,4},{4,5},{5,6},{6,7},{7,0},{8,9},{9,10},{10,1... | collective-permute-start | bytes 15368 | tf_op jit(solution)/shard_map/ppermute | solution.py:25
  100.5 6.9 %collective-permute-start.12 = (f32[80,128]{1,0:T(8,128)S(1)}, f32[80,128]{1,0:T(8,128)S(1)}, u32[]{:S(2)}, u32[]{:S(2)}) collective-permute-start(f32[80,128]{1,0:T(8,128)S(1)} %bitcast.133), channel_id=1, source_target_pairs={{0,24},{8,0},{16,8},{24,16},{1,25},{9,1},{17,9},{25,17},{2,26},{10... | collective-permute-start | bytes 122888 | tf_op jit(solution)/shard_map/ppermute | solution.py:23
  100.5 6.9 %collective-permute-start.13 = (f32[80,128]{1,0:T(8,128)S(1)}, f32[80,128]{1,0:T(8,128)S(1)}, u32[]{:S(2)}, u32[]{:S(2)}) collective-permute-start(f32[80,128]{1,0:T(8,128)S(1)} %bitcast.131), channel_id=1, source_target_pairs={{0,8},{8,16},{16,24},{24,0},{1,9},{9,17},{17,25},{25,1},{2,10},{10... | collective-permute-start | bytes 122888 | tf_op jit(solution)/shard_map/ppermute | solution.py:23

commit v5 on v4

--- a/solution.py
+++ b/solution.py
@@ -186,12 +186,14 @@
     fields, levels, xlocal, ylocal = atm_state.shape
     derivative_np, weights_np, massw_np = gll_tables()
     state_now = atm_state.reshape(fields * levels, xlocal, ylocal)
+    bottom = atm_state[:, levels - 1]
     inv_mass = mass_inverse(massw_np, xlocal, ylocal)
     for substep in range(SUB):
+        stiff = stiffness(bottom, metric, derivative_np, weights_np)
+        bottom = bottom - visc_coef * assemble(stiff) * inv_mass
         stiff = stiffness(state_now, metric, derivative_np, weights_np)
         state_now = state_now - visc_coef * assemble(stiff) * inv_mass
     atm_out = state_now.reshape(fields, levels, xlocal, ylocal)
-    bottom = atm_out[:, levels - 1]
     speed = jnp.sqrt(1.0 + bottom[0] * bottom[0] + bottom[1] * bottom[1])
     flux_flat = (bottom * speed).reshape(fields, xlocal * ylocal)
     node_total = xlocal * ylocal
@@ -206,12 +208,17 @@
     source_count, ocean_x, ocean_y = remap_slots.shape
     gathered = onehot_gather(received, remap_slots).reshape(fields, source_count, ocean_x, ocean_y)
     ocean_flux = jnp.sum(remap_weights[None] * gathered, axis=1)
-    velocity = ocean_velocity.at[0, 0].add(wind_coef * jnp.tanh(ocean_flux[0]))
+    velocity = ocean_velocity[:, :1]
+    velocity = velocity.at[0, 0].add(wind_coef * jnp.tanh(ocean_flux[0]))
     velocity = velocity.at[1, 0].add(wind_coef * jnp.tanh(ocean_flux[1]))
-    tracers = ocean_tracers.at[0, 0].add(surf_coef * ocean_flux[2])
-    tracers = tracers.at[1, 0].add(surf_coef * ocean_flux[3])
+    surface = ocean_tracers[:, :1]
+    surface = surface.at[0, 0].add(surf_coef * ocean_flux[2])
+    surface = surface.at[1, 0].add(surf_coef * ocean_flux[3])
+    tracers = ocean_tracers
     for repeat in range(OSTEPS):
-        tracers = tracer_step(tracers, velocity)
+        tracers = tracer_step(tracers, ocean_velocity)
+        surface = tracer_step(surface, velocity)
+    tracers = lax.dynamic_update_slice_in_dim(tracers, surface, 0, axis=1)
     return (atm_out, tracers)
 
 

time: 111 us -> 157 us (1.41)
  starting transfers between devices: 19.7 us -> 54.9 us
  local copies, waits for them, and re-layouts: 29.4 us -> 42.6 us
  blocking collectives: 11.8 us -> 0 us
  other arithmetic: 14.3 us -> 21.8 us
  matrix products: 9.68 us -> 13.3 us
  waiting for transfers between devices: 11.3 us -> 9.12 us
    ppermute x8 -> x16, starting transfers between devices: 15.1 us -> 39.4 us  [neighbour(): lax.ppermute(values, 'gy', [(j, (j + step_y) % count_y) for j in range(co...]
    all_to_all x1 -> x0, blocking collectives: 11.8 us -> none  [per_device(): lax.all_to_all(payload, ('gx', 'gy'), split_axis=1, concat_axis=1, tiled=...]
    ppermute x8 -> x16, starting transfers between devices: 4.63 us -> 12.9 us  [neighbour(): lax.ppermute(values, 'gx', [(i, (i + step_x) % count_x) for i in range(co...]
    slice x8 -> x16, local copies, waits for them, and re-layouts: 6.24 us -> 11.1 us  [shifted(): lax.slice_in_dim(values, 1, size, axis=axis)]
    another operation x8, local copies, waits for them, and re-layouts: 0.65 us -> 4.62 us  [packed(): return values.reshape(-1, 128)]
    all_to_all x0 -> x1, starting transfers between devices: none -> 2.57 us  [per_device(): lax.all_to_all(payload, ('gx', 'gy'), split_axis=1, concat_axis=1, tiled=...]
    ppermute x8 -> x16, waiting for transfers between devices: 7.06 us -> 4.61 us  [neighbour(): lax.ppermute(values, 'gy', [(j, (j + step_y) % count_y) for j in range(co...]
    sub x2, other arithmetic: 1.09 us -> 3.14 us  [per_device(): state_now = state_now - visc_coef * assemble(stiff) * inv_mass]
  transfers between devices with their start and end apart: 16 -> 33, of which waited for: 7 -> 7; matrix products, arithmetic and copies ran while one was open for 14% -> 42% of each run, Pallas kernels for 0% -> 4%
where the time goes in v5:
time: 157 us; the launch traced here: 156 us
  starting transfers between devices  54.9 us (35%)
  local copies, waits for them, and re-layouts  42.6 us (27%)
  other arithmetic  21.8 us (14%)
  matrix products  13.3 us (8%)
  Pallas kernels  13.1 us (8%)
  waiting for transfers between devices  9.12 us (6%)
    ppermute x16, starting transfers between devices, neighbour(): lax.ppermute(values, 'gy', [(j, (j + step_y) % count_y) for j in range(co...  39.4 us
    pallas_call x2, Pallas kernels, onehot_gather(): pl.pallas_call(gather_kernel, grid=(count // tile,), in_specs=[pl.BlockSp...  13.1 us
    ppermute x16, starting transfers between devices, neighbour(): lax.ppermute(values, 'gx', [(i, (i + step_x) % count_x) for i in range(co...  12.9 us
    slice x16, local copies, waits for them, and re-layouts, shifted(): lax.slice_in_dim(values, 1, size, axis=axis)  11.1 us
    add x4, other arithmetic, pair_merge(): values + jnp.where(position == 0, prev, jnp.where(position == 3, nxt, 0.0))  7.71 us
    sub x3, other arithmetic, tracer_step(): tracers + diff_coef * (east + west + north + south - 4.0 * tracers)  5.27 us
    another operation x2, local copies, waits for them, and re-layouts, assemble(): from_right = exchange(stiff[:, :, 0], 0, -1)[..., None]  5.15 us
    another operation x2, local copies, waits for them, and re-layouts, assemble(): from_left = exchange(stiff[:, :, last_y], 0, 1)[..., None]  5.12 us
  transfers between devices with their start and end apart: 33, of which 7 were waited for; matrix products, arithmetic and copies ran while one was open for 42% of the time, Pallas kernels for 4%

profile of v5, /device:TPU:0, one launch (start us, length us, event | category | flops | bytes accessed | tf_op | source)
XLA Modules:
  0.0 156.1 jit_solution(7278352953746868378)
XLA Ops:
  1.4 2.6 %fusion.6 = f32[160,16,128]{2,1,0:T(8,128)S(1)} fusion(f32[16,16,1]{1,0,2:T(8,128)} %constant.186, f32[160,16,128]{2,1,0:T(8,128)} %bitcast.193, f32[16,128]{1,0:T(8,128)S(1)} %get-tuple-element.120), kind=kOutput, calls=%fused_computation.14 | convolution fusion | flops 63242240 | bytes 2630656 | tf_op jit(solution)/shard_map/ab,lby->lay/dot_general | solution.py:77
  4.0 1.2 fusion.5
  9.6 2.9 %collective-permute-start = (f32[20,128]{1,0:T(8,128)}, f32[20,128]{1,0:T(8,128)}, u32[]{:S(2)}, u32[]{:S(2)}) collective-permute-start(f32[20,128]{1,0:T(8,128)} %reshape_squeeze.51), channel_id=1, source_target_pairs={{0,1},{1,2},{2,3},{3,4},{4,5},{5,6},{6,7},{7,0},{8,9},{9,10},{10,1... | collective-permute-start | bytes 30728 | tf_op jit(solution)/shard_map/ppermute | solution.py:25
  13.2 3.0 %collective-permute-start.1 = (f32[20,128]{1,0:T(8,128)}, f32[20,128]{1,0:T(8,128)}, u32[]{:S(2)}, u32[]{:S(2)}) collective-permute-start(f32[20,128]{1,0:T(8,128)} %reshape_squeeze.52), channel_id=1, source_target_pairs={{0,7},{1,0},{2,1},{3,2},{4,3},{5,4},{6,5},{7,6},{8,15},{9,8},{10,9... | collective-permute-start | bytes 30728 | tf_op jit(solution)/shard_map/ppermute | solution.py:25
  19.1 1.5 collective-permute-start.16
  20.6 3.4 %collective-permute-start.17 = (f32[4,16]{1,0:T(4,128)S(1)}, f32[4,16]{1,0:T(4,128)S(1)}, u32[]{:S(2)}, u32[]{:S(2)}) collective-permute-start(f32[4,16]{1,0:T(4,128)S(1)} %get-tuple-element.60), channel_id=1, source_target_pairs={{0,7},{1,0},{2,1},{3,2},{4,3},{5,4},{6,5},{7,6},{8,15},{9,8},{10,9... | collective-permute-start | bytes 776 | tf_op jit(solution)/shard_map/ppermute | solution.py:25
  24.0 1.9 %fusion.60 = (f32[160,16,127]{2,1,0:T(8,128)}, f32[160,16,127]{2,1,0:T(8,128)}) fusion(f32[160,16,128]{2,1,0:T(8,128)S(1)} %fusion.1), kind=kLoop, calls=%fused_computation.148 | loop fusion | bytes 5201920 | tf_op jit(solution)/shard_map/slice | solution.py:37
  26.0 1.2 fusion.66
  33.4 1.7 %collective-permute-start.19 = (f32[4,128]{1,0:T(4,128)S(1)}, f32[4,128]{1,0:T(4,128)S(1)}, u32[]{:S(2)}, u32[]{:S(2)}) collective-permute-start(f32[4,128]{1,0:T(4,128)S(1)} %bitcast.219), channel_id=1, source_target_pairs={{0,24},{8,0},{16,8},{24,16},{1,25},{9,1},{17,9},{25,17},{2,26},{10... | collective-permute-start | bytes 6152 | tf_op jit(solution)/shard_map/ppermute | solution.py:23
  35.1 1.2 collective-permute-done.18
  37.6 4.7 %collective-permute-start.21 = (f32[4,16]{1,0:T(4,128)S(1)}, f32[4,16]{1,0:T(4,128)S(1)}, u32[]{:S(2)}, u32[]{:S(2)}) collective-permute-start(f32[4,16]{1,0:T(4,128)S(1)} %get-tuple-element.58), channel_id=1, source_target_pairs={{0,7},{1,0},{2,1},{3,2},{4,3},{5,4},{6,5},{7,6},{8,15},{9,8},{10,9... | collective-permute-start | bytes 776 | tf_op jit(solution)/shard_map/ppermute | solution.py:25
  42.4 1.5 collective-permute-done.20
  47.9 4.6 %collective-permute-start.10 = (f32[10,128]{1,0:T(8,128)}, f32[10,128]{1,0:T(8,128)S(1)}, u32[]{:S(2)}, u32[]{:S(2)}) collective-permute-start(f32[10,128]{1,0:T(8,128)} %reshape_squeeze.57), channel_id=1, source_target_pairs={{0,7},{1,0},{2,1},{3,2},{4,3},{5,4},{6,5},{7,6},{8,15},{9,8},{10,9... | collective-permute-start | bytes 15368 | tf_op jit(solution)/shard_map/ppermute | solution.py:25
  53.2 6.2 %shard_map.248 = f32[4,8192]{1,0:T(4,128)} custom-call(s32[1,8192]{1,0:T(1,128)} %bitcast.199, f32[4,16,128]{2,1,0:T(8,128)} %broadcast_multiply_fusion.1.table_ref), custom_call_target="tpu_custom_call" | custom-call | tf_op jit(solution)/shard_map/pallas_call | solution.py:164
  59.5 1.6 %broadcast_multiply_fusion = f32[4,32,256]{2,0,1:T(4,128)} fusion(f32[4,32,256]{2,0,1:T(4,128)} %bitcast.196, f32[32,256]{1,0:T(8,128)S(1)} %fusion.32), kind=kLoop, calls=%fused_computation.67 | loop fusion | flops 32768 | bytes 294912 | tf_op jit(solution)/shard_map/mul | solution.py:205
  61.1 2.6 %all-to-all-start = ((f32[4,32,256]{2,0,1:T(4,128)}), f32[4,32,256]{2,0,1:T(4,128)S(1)}, u32[]{:S(2)}, u32[]{:S(2)}) async-start(f32[4,32,256]{2,0,1:T(4,128)} %broadcast_multiply_fusion), calls=%async_computation | async-start | bytes 262144 | tf_op jit(solution)/shard_map/all_to_all | solution.py:206
  63.6 1.7 %collective-permute-start.8 = (f32[80,128]{1,0:T(8,128)}, f32[80,128]{1,0:T(8,128)}, u32[]{:S(2)}, u32[]{:S(2)}) collective-permute-start(f32[80,128]{1,0:T(8,128)} %bitcast.204), channel_id=1, source_target_pairs={{0,24},{8,0},{16,8},{24,16},{1,25},{9,1},{17,9},{25,17},{2,26},{10... | collective-permute-start | bytes 122888 | tf_op jit(solution)/shard_map/ppermute | solution.py:23
  65.3 2.0 %broadcast_in_dim_reshape.57 = f32[2,40,16,1]{3,2,1,0:T(8,128)} reshape(f32[10,128]{1,0:T(8,128)} %collective-permute-done.11) | data formatting | bytes 10240 | tf_op jit(solution)/shard_map/broadcast_in_dim;reshape | solution.py:94
  67.4 1.3 broadcast_in_dim_reshape.56
  68.7 2.9 %broadcast_in_dim_reshape.52 = f32[160,16,1]{2,1,0:T(8,128)} reshape(f32[20,128]{1,0:T(8,128)} %collective-permute-done) | data formatting | bytes 20480 | tf_op jit(solution)/shard_map/broadcast_in_dim;reshape | solution.py:62
  71.6 2.9 %broadcast_in_dim_reshape.53 = f32[160,16,1]{2,1,0:T(8,128)} reshape(f32[20,128]{1,0:T(8,128)} %collective-permute-done.1) | data formatting | bytes 20480 | tf_op jit(solution)/shard_map/broadcast_in_dim;reshape | solution.py:63
  74.5 3.2 %fusion.7 = f32[160,16,128]{2,1,0:T(8,128)S(1)} fusion(f32[160,16,128]{2,1,0:T(8,128)S(1)} %fusion.1, f32[160,16,127]{2,1,0:T(8,128)} %get-tuple-element.77, f32[160,16,1]{2,1,0:T(8,128)} %broadcast_in_dim_reshape.52, f32[160,16,1]{2,1,0:T(8,128)} %broadcast_in_dim_reshape.53, f32[160,16,127]{2,1,0:T(8,128)} %get-tuple-element.76, ...), kind=kLoop, calls=%fused_computation.20 | loop fusion | flops 1638400 | bytes 5243136 | tf_op jit(solution)/shard_map/add | solution.py:47
  77.9 1.7 %fusion.58 = (f32[160,15,128]{2,1,0:T(8,128)}, f32[160,15,128]{2,1,0:T(8,128)}) fusion(f32[160,16,128]{2,1,0:T(8,128)S(1)} %fusion.7), kind=kLoop, calls=%fused_computation.146 | loop fusion | bytes 4915200 | tf_op jit(solution)/shard_map/slice | solution.py:37
  81.1 1.5 multiply_subtract_fusion.1
  82.6 1.2 fusion.63
  86.6 1.5 collective-permute-start.15
  88.9 3.4 %collective-permute-start.14 = (f32[10,128]{1,0:T(8,128)S(1)}, f32[10,128]{1,0:T(8,128)S(1)}, u32[]{:S(2)}, u32[]{:S(2)}) collective-permute-start(f32[10,128]{1,0:T(8,128)S(1)} %reshape_squeeze.61), channel_id=1, source_target_pairs={{0,7},{1,0},{2,1},{3,2},{4,3},{5,4},{6,5},{7,6},{8,15},{9,8},{10,9... | collective-permute-start | bytes 15368 | tf_op jit(solution)/shard_map/ppermute | solution.py:25
  95.3 1.3 broadcast_in_dim_reshape.59
  96.6 1.3 broadcast_in_dim_reshape.58
  98.0 3.7 %multiply_subtract_fusion = f32[2,40,16,128]{3,2,1,0:T(8,128)} fusion(f32[2,40,16,128]{3,2,1,0:T(8,128)S(1)} %multiply_subtract_fusion.1, f32[2,40,16,127]{3,2,1,0:T(8,128)} %get-tuple-element.85, f32[2,40,16,1]{3,2,1,0:T(8,128)} %broadcast_in_dim_reshape.59, f32[2,40,16,1]{3,2,1,0:T(8,128)} %broadcast_in_dim_reshape.58, ...), kind=kLoop, calls=%fused_computation.60 | loop fusion | flops 2785280 | bytes 4587520 | tf_op jit(solution)/shard_map/sub | solution.py:99
  101.8 1.5 fusion.10
  103.3 1.2 fusion.3
  105.7 1.2 fusion.4
  109.5 4.8 %collective-permute-start.5 = (f32[20,128]{1,0:T(8,128)S(1)}, f32[20,128]{1,0:T(8,128)S(1)}, u32[]{:S(2)}, u32[]{:S(2)}) collective-permute-start(f32[20,128]{1,0:T(8,128)S(1)} %reshape_squeeze.54), channel_id=1, source_target_pairs={{0,7},{1,0},{2,1},{3,2},{4,3},{5,4},{6,5},{7,6},{8,15},{9,8},{10,9... | collective-permute-start | bytes 30728 | tf_op jit(solution)/shard_map/ppermute | solution.py:25
  114.3 1.5 fusion.57
  115.8 2.2 %broadcast_in_dim_reshape.54 = f32[160,16,1]{2,1,0:T(8,128)} reshape(f32[20,128]{1,0:T(8,128)S(1)} %collective-permute-done.4) | data formatting | bytes 20480 | tf_op jit(solution)/shard_map/broadcast_in_dim;reshape | solution.py:62
  118.0 2.2 %broadcast_in_dim_reshape.55 = f32[160,16,1]{2,1,0:T(8,128)} reshape(f32[20,128]{1,0:T(8,128)S(1)} %collective-permute-done.5) | data formatting | bytes 20480 | tf_op jit(solution)/shard_map/broadcast_in_dim;reshape | solution.py:63
  120.3 2.8 %fusion.11 = f32[160,16,128]{2,1,0:T(8,128)S(1)} fusion(f32[160,16,128]{2,1,0:T(8,128)S(1)} %fusion, f32[160,16,127]{2,1,0:T(8,128)} %get-tuple-element.71, f32[160,16,1]{2,1,0:T(8,128)} %broadcast_in_dim_reshape.54, f32[160,16,1]{2,1,0:T(8,128)} %broadcast_in_dim_reshape.55, f32[160,16,127]{2,1,0:T(8,128)S(1)} %get-tuple-element.70, ...), kind=kLoop, calls=%fused_computation.28 | loop fusion | flops 1638400 | bytes 5243136 | tf_op jit(solution)/shard_map/add | solution.py:47
  123.3 1.7 %collective-permute-start.7 = (f32[160,128]{1,0:T(8,128)S(1)}, f32[160,128]{1,0:T(8,128)S(1)}, u32[]{:S(2)}, u32[]{:S(2)}) collective-permute-start(f32[160,128]{1,0:T(8,128)S(1)} %bitcast.200), channel_id=1, source_target_pairs={{0,24},{8,0},{16,8},{24,16},{1,25},{9,1},{17,9},{25,17},{2,26},{10... | collective-permute-start | bytes 245768 | tf_op jit(solution)/shard_map/ppermute | solution.py:23
  125.2 1.9 %collective-permute-done.6 = f32[160,128]{1,0:T(8,128)S(1)} collective-permute-done((f32[160,128]{1,0:T(8,128)S(1)}, f32[160,128]{1,0:T(8,128)S(1)}, u32[]{:S(2)}, u32[]{:S(2)}) %collective-permute-start.6) | collective-permute-done | bytes 81952 | tf_op jit(solution)/shard_map/ppermute | solution.py:23
  127.2 1.6 %fusion.14 = f32[160,16,128]{2,1,0:T(8,128)} fusion(f32[160,16,128]{2,1,0:T(8,128)S(1)} %copy-done.2, f32[160,16,128]{2,1,0:T(8,128)S(1)} %fusion.11, f32[160,15,128]{2,1,0:T(8,128)S(1)} %get-tuple-element.67, f32[160,1,128]{2,1,0:T(1,128)S(1)} %bitcast.202, f32[160,1,128]{2,1,0:T(1,128)S(1)} %bitcast.203, f32[160,15,128]{2,1,0:T(8,128)S(1)} %get-tuple-element.66, ...), kind=kLoop, calls=%fused_computation.33 | loop fusion | flops 2293760 | bytes 6561824 | tf_op jit(solution)/shard_map/sub | solution.py:195
  129.5 6.8 %shard_map.249 = f32[4,8192]{1,0:T(4,128)} custom-call(s32[1,8192]{1,0:T(1,128)} %bitcast.208, f32[4,64,128]{2,1,0:T(8,128)} %reshape_reshape.3.table_ref), custom_call_target="tpu_custom_call" | custom-call | tf_op jit(solution)/shard_map/pallas_call | solution.py:164
  138.2 1.8 %collective-permute-start.25 = (f32[2,128]{1,0:T(2,128)S(1)}, f32[2,128]{1,0:T(2,128)S(1)}, u32[]{:S(2)}, u32[]{:S(2)}) collective-permute-start(f32[2,128]{1,0:T(2,128)S(1)} %bitcast.236), channel_id=1, source_target_pairs={{0,8},{8,16},{16,24},{24,0},{1,9},{9,17},{17,25},{25,1},{2,10},{10... | collective-permute-start | bytes 3080 | tf_op jit(solution)/shard_map/ppermute | solution.py:23
  140.4 4.7 %collective-permute-start.26 = (f32[2,1,16]{2,0,1:T(2,128)S(1)}, f32[2,1,16]{2,0,1:T(2,128)S(1)}, u32[]{:S(2)}, u32[]{:S(2)}) collective-permute-start(f32[2,1,16]{2,0,1:T(2,128)S(1)} %bitcast.226), channel_id=1, source_target_pairs={{0,7},{1,0},{2,1},{3,2},{4,3},{5,4},{6,5},{7,6},{8,15},{9,8},{10,9... | collective-permute-start | bytes 392 | tf_op jit(solution)/shard_map/ppermute | solution.py:25
  145.1 1.5 collective-permute-done.27
  147.1 1.7 %collective-permute-start.28 = (f32[2,128]{1,0:T(2,128)S(1)}, f32[2,128]{1,0:T(2,128)S(1)}, u32[]{:S(2)}, u32[]{:S(2)}) collective-permute-start(f32[2,128]{1,0:T(2,128)S(1)} %bitcast.235), channel_id=1, source_target_pairs={{0,24},{8,0},{16,8},{24,16},{1,25},{9,1},{17,9},{25,17},{2,26},{10... | collective-permute-start | bytes 3080 | tf_op jit(solution)/shard_map/ppermute | solution.py:23
  149.0 4.7 %collective-permute-start.30 = (f32[2,1,16]{2,0,1:T(2,128)S(1)}, f32[2,1,16]{2,0,1:T(2,128)S(1)}, u32[]{:S(2)}, u32[]{:S(2)}) collective-permute-start(f32[2,1,16]{2,0,1:T(2,128)S(1)} %bitcast.227), channel_id=1, source_target_pairs={{0,7},{1,0},{2,1},{3,2},{4,3},{5,4},{6,5},{7,6},{8,15},{9,8},{10,9... | collective-permute-start | bytes 392 | tf_op jit(solution)/shard_map/ppermute | solution.py:25
  153.7 1.5 collective-permute-done.31
  (193 shorter events, 37.4 us)
Async XLA Ops:
  1.4 16.1 %copy-start.18 = (f32[16,128]{1,0:T(8,128)}, f32[16,128]{1,0:T(8,128)S(1)}, u32[]{:S(2)}) copy-start(f32[16,128]{1,0:T(8,128)S(1)} %get-tuple-element.120) | copy-start | bytes 24580
  7.7 8.5 %copy-start = (f32[2,40,16,128]{3,2,1,0:T(8,128)S(1)}, f32[2,40,16,128]{3,2,1,0:T(8,128)}, u32[]{:S(2)}) copy-start(f32[2,40,16,128]{3,2,1,0:T(8,128)} %param.37) | copy-start | bytes 1966084
  9.6 59.1 %collective-permute-start = (f32[20,128]{1,0:T(8,128)}, f32[20,128]{1,0:T(8,128)}, u32[]{:S(2)}, u32[]{:S(2)}) collective-permute-start(f32[20,128]{1,0:T(8,128)} %reshape_squeeze.51), channel_id=1, source_target_pairs={{0,1},{1,2},{2,3},{3,4},{4,5},{5,6},{6,7},{7,0},{8,9},{9,10},{10,1... | collective-permute-start | bytes 30728 | tf_op jit(solution)/shard_map/ppermute | solution.py:25
  13.2 58.4 %collective-permute-start.1 = (f32[20,128]{1,0:T(8,128)}, f32[20,128]{1,0:T(8,128)}, u32[]{:S(2)}, u32[]{:S(2)}) collective-permute-start(f32[20,128]{1,0:T(8,128)} %reshape_squeeze.52), channel_id=1, source_target_pairs={{0,7},{1,0},{2,1},{3,2},{4,3},{5,4},{6,5},{7,6},{8,15},{9,8},{10,9... | collective-permute-start | bytes 30728 | tf_op jit(solution)/shard_map/ppermute | solution.py:25
  17.5 46.1 %collective-permute-start.11 = (f32[10,128]{1,0:T(8,128)}, f32[10,128]{1,0:T(8,128)}, u32[]{:S(2)}, u32[]{:S(2)}) collective-permute-start(f32[10,128]{1,0:T(8,128)} %reshape_squeeze.58), channel_id=1, source_target_pairs={{0,1},{1,2},{2,3},{3,4},{4,5},{5,6},{6,7},{7,0},{8,9},{9,10},{10,1... | collective-permute-start | bytes 15368 | tf_op jit(solution)/shard_map/ppermute | solution.py:25
  19.1 13.0 %collective-permute-start.16 = (f32[4,16]{1,0:T(4,128)S(1)}, f32[4,16]{1,0:T(4,128)S(1)}, u32[]{:S(2)}, u32[]{:S(2)}) collective-permute-start(f32[4,16]{1,0:T(4,128)S(1)} %get-tuple-element.61), channel_id=1, source_target_pairs={{0,1},{1,2},{2,3},{3,4},{4,5},{5,6},{6,7},{7,0},{8,9},{9,10},{10,1... | collective-permute-start | bytes 776 | tf_op jit(solution)/shard_map/ppermute | solution.py:25
  20.6 11.7 %collective-permute-start.17 = (f32[4,16]{1,0:T(4,128)S(1)}, f32[4,16]{1,0:T(4,128)S(1)}, u32[]{:S(2)}, u32[]{:S(2)}) collective-permute-start(f32[4,16]{1,0:T(4,128)S(1)} %get-tuple-element.60), channel_id=1, source_target_pairs={{0,7},{1,0},{2,1},{3,2},{4,3},{5,4},{6,5},{7,6},{8,15},{9,8},{10,9... | collective-permute-start | bytes 776 | tf_op jit(solution)/shard_map/ppermute | solution.py:25
  25.9 6.5 %copy-start.31 = (pred[128]{0:T(512)(128)(4,1)}, pred[128]{0:T(512)(128)(4,1)S(1)}, u32[]{:S(2)}) copy-start(pred[128]{0:T(512)(128)(4,1)S(1)} %get-tuple-element.123) | copy-start | bytes 388
  25.9 6.5 %copy-start.33 = (pred[128]{0:T(512)(128)(4,1)}, pred[128]{0:T(512)(128)(4,1)S(1)}, u32[]{:S(2)}) copy-start(pred[128]{0:T(512)(128)(4,1)S(1)} %get-tuple-element.124) | copy-start | bytes 388
  25.9 26.6 %copy-start.27 = (pred[16]{0:T(512)(128)(4,1)}, pred[16]{0:T(512)(128)(4,1)S(1)}, u32[]{:S(2)}) copy-start(pred[16]{0:T(512)(128)(4,1)S(1)} %get-tuple-element.121) | copy-start | bytes 52
  25.9 26.6 %copy-start.29 = (pred[16]{0:T(512)(128)(4,1)}, pred[16]{0:T(512)(128)(4,1)S(1)}, u32[]{:S(2)}) copy-start(pred[16]{0:T(512)(128)(4,1)S(1)} %get-tuple-element.122) | copy-start | bytes 52
  28.4 8.0 %copy-start.20 = (f32[16,128]{1,0:T(8,128)S(1)}, f32[16,128]{1,0:T(8,128)}, u32[]{:S(2)}) copy-start(f32[16,128]{1,0:T(8,128)} %constant.185) | copy-start | bytes 24580
  28.4 8.1 %copy-start.19 = (f32[16,128]{1,0:T(8,128)S(1)}, f32[16,128]{1,0:T(8,128)}, u32[]{:S(2)}) copy-start(f32[16,128]{1,0:T(8,128)} %copy-done.18) | copy-start | bytes 24580
  28.4 8.5 %copy-start.26 = (f32[128]{0:T(128)S(1)}, f32[128]{0:T(128)}, u32[]{:S(2)}) copy-start(f32[128]{0:T(128)} %constant.182.clone) | copy-start | bytes 1540
  28.4 8.7 %copy-start.24 = (f32[16]{0:T(128)S(1)}, f32[16]{0:T(128)}, u32[]{:S(2)}) copy-start(f32[16]{0:T(128)} %constant.181.clone) | copy-start | bytes 196
  33.3 3.1 %collective-permute-start.18 = (f32[4,128]{1,0:T(4,128)S(1)}, f32[4,128]{1,0:T(4,128)S(1)}, u32[]{:S(2)}, u32[]{:S(2)}) collective-permute-start(f32[4,128]{1,0:T(4,128)S(1)} %bitcast.220), channel_id=1, source_target_pairs={{0,8},{8,16},{16,24},{24,0},{1,9},{9,17},{17,25},{25,1},{2,10},{10... | collective-permute-start | bytes 6152 | tf_op jit(solution)/shard_map/ppermute | solution.py:23
  33.4 3.1 %collective-permute-start.19 = (f32[4,128]{1,0:T(4,128)S(1)}, f32[4,128]{1,0:T(4,128)S(1)}, u32[]{:S(2)}, u32[]{:S(2)}) collective-permute-start(f32[4,128]{1,0:T(4,128)S(1)} %bitcast.219), channel_id=1, source_target_pairs={{0,24},{8,0},{16,8},{24,16},{1,25},{9,1},{17,9},{25,17},{2,26},{10... | collective-permute-start | bytes 6152 | tf_op jit(solution)/shard_map/ppermute | solution.py:23
  37.5 6.3 %collective-permute-start.20 = (f32[4,16]{1,0:T(4,128)S(1)}, f32[4,16]{1,0:T(4,128)S(1)}, u32[]{:S(2)}, u32[]{:S(2)}) collective-permute-start(f32[4,16]{1,0:T(4,128)S(1)} %get-tuple-element.59), channel_id=1, source_target_pairs={{0,1},{1,2},{2,3},{3,4},{4,5},{5,6},{6,7},{7,0},{8,9},{9,10},{10,1... | collective-permute-start | bytes 776 | tf_op jit(solution)/shard_map/ppermute | solution.py:25
  37.6 6.4 %collective-permute-start.21 = (f32[4,16]{1,0:T(4,128)S(1)}, f32[4,16]{1,0:T(4,128)S(1)}, u32[]{:S(2)}, u32[]{:S(2)}) collective-permute-start(f32[4,16]{1,0:T(4,128)S(1)} %get-tuple-element.58), channel_id=1, source_target_pairs={{0,7},{1,0},{2,1},{3,2},{4,3},{5,4},{6,5},{7,6},{8,15},{9,8},{10,9... | collective-permute-start | bytes 776 | tf_op jit(solution)/shard_map/ppermute | solution.py:25
  44.8 3.1 %collective-permute-start.22 = (f32[4,128]{1,0:T(4,128)S(1)}, f32[4,128]{1,0:T(4,128)S(1)}, u32[]{:S(2)}, u32[]{:S(2)}) collective-permute-start(f32[4,128]{1,0:T(4,128)S(1)} %bitcast.221), channel_id=1, source_target_pairs={{0,8},{8,16},{16,24},{24,0},{1,9},{9,17},{17,25},{25,1},{2,10},{10... | collective-permute-start | bytes 6152 | tf_op jit(solution)/shard_map/ppermute | solution.py:23
  45.5 7.0 %collective-permute-start.23 = (f32[4,128]{1,0:T(4,128)S(1)}, f32[4,128]{1,0:T(4,128)S(1)}, u32[]{:S(2)}, u32[]{:S(2)}) collective-permute-start(f32[4,128]{1,0:T(4,128)S(1)} %bitcast.218), channel_id=1, source_target_pairs={{0,24},{8,0},{16,8},{24,16},{1,25},{9,1},{17,9},{25,17},{2,26},{10... | collective-permute-start | bytes 6152 | tf_op jit(solution)/shard_map/ppermute | solution.py:23
  47.9 19.5 %collective-permute-start.10 = (f32[10,128]{1,0:T(8,128)}, f32[10,128]{1,0:T(8,128)S(1)}, u32[]{:S(2)}, u32[]{:S(2)}) collective-permute-start(f32[10,128]{1,0:T(8,128)} %reshape_squeeze.57), channel_id=1, source_target_pairs={{0,7},{1,0},{2,1},{3,2},{4,3},{5,4},{6,5},{7,6},{8,15},{9,8},{10,9... | collective-permute-start | bytes 15368 | tf_op jit(solution)/shard_map/ppermute | solution.py:25
  52.5 28.0 %collective-permute-start.9 = (f32[80,128]{1,0:T(8,128)}, f32[80,128]{1,0:T(8,128)}, u32[]{:S(2)}, u32[]{:S(2)}) collective-permute-start(f32[80,128]{1,0:T(8,128)} %bitcast.205), channel_id=1, source_target_pairs={{0,8},{8,16},{16,24},{24,0},{1,9},{9,17},{17,25},{25,1},{2,10},{10... | collective-permute-start | bytes 122888 | tf_op jit(solution)/shard_map/ppermute | solution.py:23
  61.1 67.8 %all-to-all-start = ((f32[4,32,256]{2,0,1:T(4,128)}), f32[4,32,256]{2,0,1:T(4,128)S(1)}, u32[]{:S(2)}, u32[]{:S(2)}) async-start(f32[4,32,256]{2,0,1:T(4,128)} %broadcast_multiply_fusion), calls=%async_computation | async-start | bytes 262144 | tf_op jit(solution)/shard_map/all_to_all | solution.py:206
  63.6 16.8 %collective-permute-start.8 = (f32[80,128]{1,0:T(8,128)}, f32[80,128]{1,0:T(8,128)}, u32[]{:S(2)}, u32[]{:S(2)}) collective-permute-start(f32[80,128]{1,0:T(8,128)} %bitcast.204), channel_id=1, source_target_pairs={{0,24},{8,0},{16,8},{24,16},{1,25},{9,1},{17,9},{25,17},{2,26},{10... | collective-permute-start | bytes 122888 | tf_op jit(solution)/shard_map/ppermute | solution.py:23
  68.7 5.9 %copy-start.32 = (pred[128]{0:T(512)(128)(4,1)S(1)}, pred[128]{0:T(512)(128)(4,1)}, u32[]{:S(2)}) copy-start(pred[128]{0:T(512)(128)(4,1)} %copy-done.31) | copy-start | bytes 388
  68.7 5.9 %copy-start.34 = (pred[128]{0:T(512)(128)(4,1)S(1)}, pred[128]{0:T(512)(128)(4,1)}, u32[]{:S(2)}) copy-start(pred[128]{0:T(512)(128)(4,1)} %copy-done.33) | copy-start | bytes 388
  80.3 21.4 %collective-permute-start.2 = (f32[160,128]{1,0:T(8,128)}, f32[160,128]{1,0:T(8,128)}, u32[]{:S(2)}, u32[]{:S(2)}) collective-permute-start(f32[160,128]{1,0:T(8,128)} %bitcast.9), channel_id=1, source_target_pairs={{0,8},{8,16},{16,24},{24,0},{1,9},{9,17},{17,25},{25,1},{2,10},{10... | collective-permute-start | bytes 245768 | tf_op jit(solution)/shard_map/ppermute | solution.py:23
  86.6 8.6 %collective-permute-start.15 = (f32[10,128]{1,0:T(8,128)S(1)}, f32[10,128]{1,0:T(8,128)S(1)}, u32[]{:S(2)}, u32[]{:S(2)}) collective-permute-start(f32[10,128]{1,0:T(8,128)S(1)} %reshape_squeeze.62), channel_id=1, source_target_pairs={{0,1},{1,2},{2,3},{3,4},{4,5},{5,6},{6,7},{7,0},{8,9},{9,10},{10,1... | collective-permute-start | bytes 15368 | tf_op jit(solution)/shard_map/ppermute | solution.py:25
  88.9 7.7 %collective-permute-start.14 = (f32[10,128]{1,0:T(8,128)S(1)}, f32[10,128]{1,0:T(8,128)S(1)}, u32[]{:S(2)}, u32[]{:S(2)}) collective-permute-start(f32[10,128]{1,0:T(8,128)S(1)} %reshape_squeeze.61), channel_id=1, source_target_pairs={{0,7},{1,0},{2,1},{3,2},{4,3},{5,4},{6,5},{7,6},{8,15},{9,8},{10,9... | collective-permute-start | bytes 15368 | tf_op jit(solution)/shard_map/ppermute | solution.py:25
  92.3 5.7 %collective-permute-start.13 = (f32[80,128]{1,0:T(8,128)}, f32[80,128]{1,0:T(8,128)}, u32[]{:S(2)}, u32[]{:S(2)}) collective-permute-start(f32[80,128]{1,0:T(8,128)} %bitcast.207), channel_id=1, source_target_pairs={{0,8},{8,16},{16,24},{24,0},{1,9},{9,17},{17,25},{25,1},{2,10},{10... | collective-permute-start | bytes 122888 | tf_op jit(solution)/shard_map/ppermute | solution.py:23
  92.9 5.0 %collective-permute-start.12 = (f32[80,128]{1,0:T(8,128)}, f32[80,128]{1,0:T(8,128)}, u32[]{:S(2)}, u32[]{:S(2)}) collective-permute-start(f32[80,128]{1,0:T(8,128)} %bitcast.206), channel_id=1, source_target_pairs={{0,24},{8,0},{16,8},{24,16},{1,25},{9,1},{17,9},{25,17},{2,26},{10... | collective-permute-start | bytes 122888 | tf_op jit(solution)/shard_map/ppermute | solution.py:23
  95.2 6.5 %collective-permute-start.3 = (f32[160,128]{1,0:T(8,128)}, f32[160,128]{1,0:T(8,128)}, u32[]{:S(2)}, u32[]{:S(2)}) collective-permute-start(f32[160,128]{1,0:T(8,128)} %bitcast.11), channel_id=1, source_target_pairs={{0,24},{8,0},{16,8},{24,16},{1,25},{9,1},{17,9},{25,17},{2,26},{10... | collective-permute-start | bytes 245768 | tf_op jit(solution)/shard_map/ppermute | solution.py:23
  109.4 6.4 %collective-permute-start.4 = (f32[20,128]{1,0:T(8,128)S(1)}, f32[20,128]{1,0:T(8,128)S(1)}, u32[]{:S(2)}, u32[]{:S(2)}) collective-permute-start(f32[20,128]{1,0:T(8,128)S(1)} %reshape_squeeze.53), channel_id=1, source_target_pairs={{0,1},{1,2},{2,3},{3,4},{4,5},{5,6},{6,7},{7,0},{8,9},{9,10},{10,1... | collective-permute-start | bytes 30728 | tf_op jit(solution)/shard_map/ppermute | solution.py:25
  109.5 8.5 %collective-permute-start.5 = (f32[20,128]{1,0:T(8,128)S(1)}, f32[20,128]{1,0:T(8,128)S(1)}, u32[]{:S(2)}, u32[]{:S(2)}) collective-permute-start(f32[20,128]{1,0:T(8,128)S(1)} %reshape_squeeze.54), channel_id=1, source_target_pairs={{0,7},{1,0},{2,1},{3,2},{4,3},{5,4},{6,5},{7,6},{8,15},{9,8},{10,9... | collective-permute-start | bytes 30728 | tf_op jit(solution)/shard_map/ppermute | solution.py:25
  123.2 3.9 %collective-permute-start.6 = (f32[160,128]{1,0:T(8,128)S(1)}, f32[160,128]{1,0:T(8,128)S(1)}, u32[]{:S(2)}, u32[]{:S(2)}) collective-permute-start(f32[160,128]{1,0:T(8,128)S(1)} %bitcast.201), channel_id=1, source_target_pairs={{0,8},{8,16},{16,24},{24,0},{1,9},{9,17},{17,25},{25,1},{2,10},{10... | collective-permute-start | bytes 245768 | tf_op jit(solution)/shard_map/ppermute | solution.py:23
  123.3 3.9 %copy-start.2 = (f32[160,16,128]{2,1,0:T(8,128)S(1)}, f32[160,16,128]{2,1,0:T(8,128)}, u32[]{:S(2)}) copy-start(f32[160,16,128]{2,1,0:T(8,128)} %copy-done.1) | copy-start | bytes 3932164
  123.3 3.9 %collective-permute-start.7 = (f32[160,128]{1,0:T(8,128)S(1)}, f32[160,128]{1,0:T(8,128)S(1)}, u32[]{:S(2)}, u32[]{:S(2)}) collective-permute-start(f32[160,128]{1,0:T(8,128)S(1)} %bitcast.200), channel_id=1, source_target_pairs={{0,24},{8,0},{16,8},{24,16},{1,25},{9,1},{17,9},{25,17},{2,26},{10... | collective-permute-start | bytes 245768 | tf_op jit(solution)/shard_map/ppermute | solution.py:23
  127.2 10.1 %copy-start.22 = (f32[4,16,128]{2,1,0:T(8,128)S(1)}, f32[4,16,128]{2,1,0:T(8,128)}, u32[]{:S(2)}) copy-start(f32[4,16,128]{2,1,0:T(8,128)} %param.40) | copy-start | bytes 98308
  127.2 10.1 %slice-start = ((f32[2,40,16,128]{3,2,1,0:T(8,128)}), f32[2,1,16,128]{3,2,1,0:T(8,128)S(1)}, s32[]{:S(2)}) async-start(f32[2,40,16,128]{3,2,1,0:T(8,128)} %param.37), calls=%async_computation.1 | async-start | bytes 32768 | tf_op jit(solution)/shard_map/slice | solution.py:214
  138.2 8.6 %collective-permute-start.25 = (f32[2,128]{1,0:T(2,128)S(1)}, f32[2,128]{1,0:T(2,128)S(1)}, u32[]{:S(2)}, u32[]{:S(2)}) collective-permute-start(f32[2,128]{1,0:T(2,128)S(1)} %bitcast.236), channel_id=1, source_target_pairs={{0,8},{8,16},{16,24},{24,0},{1,9},{9,17},{17,25},{25,1},{2,10},{10... | collective-permute-start | bytes 3080 | tf_op jit(solution)/shard_map/ppermute | solution.py:23
  139.9 6.9 %collective-permute-start.24 = (f32[2,128]{1,0:T(2,128)S(1)}, f32[2,128]{1,0:T(2,128)S(1)}, u32[]{:S(2)}, u32[]{:S(2)}) collective-permute-start(f32[2,128]{1,0:T(2,128)S(1)} %bitcast.234), channel_id=1, source_target_pairs={{0,24},{8,0},{16,8},{24,16},{1,25},{9,1},{17,9},{25,17},{2,26},{10... | collective-permute-start | bytes 3080 | tf_op jit(solution)/shard_map/ppermute | solution.py:23
  140.3 6.3 %collective-permute-start.27 = (f32[2,1,16]{2,0,1:T(2,128)S(1)}, f32[2,1,16]{2,0,1:T(2,128)S(1)}, u32[]{:S(2)}, u32[]{:S(2)}) collective-permute-start(f32[2,1,16]{2,0,1:T(2,128)S(1)} %bitcast.230), channel_id=1, source_target_pairs={{0,1},{1,2},{2,3},{3,4},{4,5},{5,6},{6,7},{7,0},{8,9},{9,10},{10,1... | collective-permute-start | bytes 392 | tf_op jit(solution)/shard_map/ppermute | solution.py:25
  140.4 6.3 %collective-permute-start.26 = (f32[2,1,16]{2,0,1:T(2,128)S(1)}, f32[2,1,16]{2,0,1:T(2,128)S(1)}, u32[]{:S(2)}, u32[]{:S(2)}) collective-permute-start(f32[2,1,16]{2,0,1:T(2,128)S(1)} %bitcast.226), channel_id=1, source_target_pairs={{0,7},{1,0},{2,1},{3,2},{4,3},{5,4},{6,5},{7,6},{8,15},{9,8},{10,9... | collective-permute-start | bytes 392 | tf_op jit(solution)/shard_map/ppermute | solution.py:25
  147.0 8.4 %collective-permute-start.29 = (f32[2,128]{1,0:T(2,128)S(1)}, f32[2,128]{1,0:T(2,128)S(1)}, u32[]{:S(2)}, u32[]{:S(2)}) collective-permute-start(f32[2,128]{1,0:T(2,128)S(1)} %bitcast.237), channel_id=1, source_target_pairs={{0,8},{8,16},{16,24},{24,0},{1,9},{9,17},{17,25},{25,1},{2,10},{10... | collective-permute-start | bytes 3080 | tf_op jit(solution)/shard_map/ppermute | solution.py:23
  147.1 8.4 %collective-permute-start.28 = (f32[2,128]{1,0:T(2,128)S(1)}, f32[2,128]{1,0:T(2,128)S(1)}, u32[]{:S(2)}, u32[]{:S(2)}) collective-permute-start(f32[2,128]{1,0:T(2,128)S(1)} %bitcast.235), channel_id=1, source_target_pairs={{0,24},{8,0},{16,8},{24,16},{1,25},{9,1},{17,9},{25,17},{2,26},{10... | collective-permute-start | bytes 3080 | tf_op jit(solution)/shard_map/ppermute | solution.py:23
  148.9 6.3 %collective-permute-start.31 = (f32[2,1,16]{2,0,1:T(2,128)S(1)}, f32[2,1,16]{2,0,1:T(2,128)S(1)}, u32[]{:S(2)}, u32[]{:S(2)}) collective-permute-start(f32[2,1,16]{2,0,1:T(2,128)S(1)} %bitcast.232), channel_id=1, source_target_pairs={{0,1},{1,2},{2,3},{3,4},{4,5},{5,6},{6,7},{7,0},{8,9},{9,10},{10,1... | collective-permute-start | bytes 392 | tf_op jit(solution)/shard_map/ppermute | solution.py:25
  149.0 6.3 %collective-permute-start.30 = (f32[2,1,16]{2,0,1:T(2,128)S(1)}, f32[2,1,16]{2,0,1:T(2,128)S(1)}, u32[]{:S(2)}, u32[]{:S(2)}) collective-permute-start(f32[2,1,16]{2,0,1:T(2,128)S(1)} %bitcast.227), channel_id=1, source_target_pairs={{0,7},{1,0},{2,1},{3,2},{4,3},{5,4},{6,5},{7,6},{8,15},{9,8},{10,9... | collective-permute-start | bytes 392 | tf_op jit(solution)/shard_map/ppermute | solution.py:25
  (22 other events, 59.8 us)

commit v6 on v4

--- a/solution.py
+++ b/solution.py
@@ -33,8 +33,13 @@
 
 def shifted(values, before, after, axis):
     size = values.shape[axis]
-    prev = jnp.concatenate([before, lax.slice_in_dim(values, 0, size - 1, axis=axis)], axis=axis)
-    nxt = jnp.concatenate([lax.slice_in_dim(values, 1, size, axis=axis), after], axis=axis)
+    layout = [1] * values.ndim
+    layout[axis] = size
+    position = jnp.arange(size).reshape(layout)
+    prev = jnp.concatenate([lax.slice_in_dim(values, 0, 1, axis=axis), lax.slice_in_dim(values, 0, size - 1, axis=axis)], axis=axis)
+    nxt = jnp.concatenate([lax.slice_in_dim(values, 1, size, axis=axis), lax.slice_in_dim(values, size - 1, size, axis=axis)], axis=axis)
+    prev = jnp.where(position == 0, jnp.broadcast_to(before, values.shape), prev)
+    nxt = jnp.where(position == size - 1, jnp.broadcast_to(after, values.shape), nxt)
     return prev, nxt
 
 
@@ -59,8 +64,8 @@
 
 def assemble(stiff):
     last_x, last_y = stiff.shape[1] - 1, stiff.shape[2] - 1
-    from_left = exchange(stiff[:, :, last_y], 0, 1)[..., None]
-    from_right = exchange(stiff[:, :, 0], 0, -1)[..., None]
+    from_left = exchange(stiff[:, :, last_y], 0, 1)[:, :, None]
+    from_right = exchange(stiff[:, :, 0], 0, -1)[:, :, None]
     merged = pair_merge(stiff, from_left, from_right, 2)
     from_up = exchange(merged[:, last_x, :], 1, 0)[:, None, :]
     from_down = exchange(merged[:, 0, :], -1, 0)[:, None, :]

time: 111 us -> 106 us (0.955)
  local copies, waits for them, and re-layouts: 29.4 us -> 19.2 us
  waiting for transfers between devices: 11.3 us -> 14.1 us
  blocking collectives: 11.8 us -> 13.9 us
    another operation x8 -> x0, local copies, waits for them, and re-layouts: 14.2 us -> none  [the longest x2 4.42 us: assemble(): from_right = exchange(stiff[:, :, 0], 0, -1)[..., None]]
    ppermute x8, waiting for transfers between devices: 7.06 us -> 9.79 us  [neighbour(): lax.ppermute(values, 'gy', [(j, (j + step_y) % count_y) for j in range(co...]
    all_to_all x1, blocking collectives: 11.8 us -> 13.9 us  [per_device(): lax.all_to_all(payload, ('gx', 'gy'), split_axis=1, concat_axis=1, tiled=...]
    slice x6, local copies, waits for them, and re-layouts: 2.56 us -> 4.43 us  [the longest x2 4.08 us: assemble(): from_left = exchange(stiff[:, :, last_y], 0, 1)[:, :, None]]
    slice x2, local copies, waits for them, and re-layouts: 1.19 us -> 2.67 us  [tracer_step(): from_right = exchange(tracers[..., 0], 0, -1)[..., None]]
  transfers between devices with their start and end apart: 16 -> 16, of which waited for: 7 -> 7; matrix products, arithmetic and copies ran while one was open for 14% -> 6% of each run, Pallas kernels for 0% -> 0%
where the time goes in v6:
time: 106 us
  starting transfers between devices  19.9 us (19%)
  local copies, waits for them, and re-layouts  19.2 us (18%)
  other arithmetic  14.6 us (14%)
  waiting for transfers between devices  14.1 us (13%)
  blocking collectives  13.9 us (13%)
  Pallas kernels  13.1 us (12%)
  matrix products  9.68 us (9%)
  between operations  1.16 us (1%)
    ppermute x8, starting transfers between devices, neighbour(): lax.ppermute(values, 'gy', [(j, (j + step_y) % count_y) for j in range(co...  15.1 us
    all_to_all x1, blocking collectives, per_device(): lax.all_to_all(payload, ('gx', 'gy'), split_axis=1, concat_axis=1, tiled=...  13.9 us
    pallas_call x2, Pallas kernels, onehot_gather(): pl.pallas_call(gather_kernel, grid=(count // tile,), in_specs=[pl.BlockSp...  13.1 us
    ppermute x8, waiting for transfers between devices, neighbour(): lax.ppermute(values, 'gy', [(j, (j + step_y) % count_y) for j in range(co...  9.79 us
    add x2, other arithmetic, pair_merge(): values + jnp.where(position == 0, prev, jnp.where(position == 3, nxt, 0.0))  6.3 us
    slice x8, local copies, waits for them, and re-layouts, shifted(): lax.slice_in_dim(values, 1, size, axis=axis)  6.23 us
    sub x2, other arithmetic, tracer_step(): tracers + diff_coef * (east + west + north + south - 4.0 * tracers)  5.22 us
    ppermute x8, starting transfers between devices, neighbour(): lax.ppermute(values, 'gx', [(i, (i + step_x) % count_x) for i in range(co...  4.85 us
  transfers between devices with their start and end apart: 16, of which 7 were waited for; matrix products, arithmetic and copies ran while one was open for 6% of the time, Pallas kernels for 0%

profile of v6, /device:TPU:0, one launch (start us, length us, event | category | flops | bytes accessed | tf_op | source)
XLA Modules:
  0.0 105.6 jit_solution(17719686269487345893)
XLA Ops:
  0.7 0.6 copy-done.11
  2.0 1.2 %fusion.6 = f32[160,16,128]{2,1,0:T(8,128)S(1)} fusion(f32[16,16,1]{1,0,2:T(8,128)S(1)} %copy-done.6, f32[160,16,128]{2,1,0:T(8,128)S(1)} %bitcast.97, f32[16,128]{1,0:T(8,128)S(1)} %get-tuple-element.99), kind=kOutput, calls=%fused_computation.14 | convolution fusion | flops 63242240 | bytes 2630656 | tf_op jit(solution)/shard_map/ab,lby->lay/dot_general | solution.py:82
  3.3 1.2 %fusion.5 = f32[160,16,128]{2,1,0:T(8,128)S(1)} fusion(f32[160,16,128]{2,1,0:T(8,128)S(1)} %fusion.6, f32[16,16,1]{1,0,2:T(8,128)S(1)} %copy-done.6, f32[128]{0:T(128)S(1)} %copy-done.12), kind=kOutput, calls=%fused_computation.12 | convolution fusion | flops 63242240 | bytes 2622976 | tf_op jit(solution)/shard_map/ba,lby->lay/dot_general | solution.py:84
  4.5 1.2 %fusion.2 = f32[160,16,128]{2,1,0:T(8,128)S(1)} fusion(f32[128,128,1]{1,0,2:T(8,128)S(1)} %copy-done.5, f32[160,16,128]{2,1,0:T(8,128)S(1)} %bitcast.98, f32[16,128]{1,0:T(8,128)S(1)} %get-tuple-element.98), kind=kOutput, calls=%fused_computation.6 | convolution fusion | flops 503644160 | bytes 2695168 | tf_op jit(solution)/shard_map/lxc,dc->lxd/dot_general | solution.py:87
  5.7 1.2 %fusion.1 = f32[160,16,128]{2,1,0:T(8,128)S(1)} fusion(f32[160,16,128]{2,1,0:T(8,128)S(1)} %fusion.5, f32[160,16,128]{2,1,0:T(8,128)S(1)} %fusion.2, f32[128,128,1]{1,0,2:T(8,128)S(1)} %copy-done.5, f32[16]{0:T(128)S(1)} %copy-done.11), kind=kOutput, calls=%fused_computation.4 | convolution fusion | flops 503971840 | bytes 3997760 | tf_op jit(solution)/shard_map/lxc,cd->lxd/dot_general | solution.py:89
  6.9 2.0 %slice_reduce_fusion.7 = (f32[160,16]{1,0:T(8,128)S(1)}, f32[160,16]{1,0:T(8,128)S(1)}, f32[160,16,1]{2,1,0:T(8,128)}, f32[160,16,1]{2,1,0:T(8,128)}) fusion(f32[160,16,128]{2,1,0:T(8,128)S(1)} %fusion.1), kind=kLoop, calls=%fused_computation.102 | loop fusion | bytes 61440 | tf_op jit(solution)/shard_map/slice | solution.py:67
  9.0 3.0 %collective-permute-start = (f32[20,128]{1,0:T(8,128)S(1)}, f32[20,128]{1,0:T(8,128)S(1)}, u32[]{:S(2)}, u32[]{:S(2)}) collective-permute-start(f32[20,128]{1,0:T(8,128)S(1)} %reshape_squeeze.39), channel_id=1, source_target_pairs={{0,1},{1,2},{2,3},{3,4},{4,5},{5,6},{6,7},{7,0},{8,9},{9,10},{10,1... | collective-permute-start | bytes 30728 | tf_op jit(solution)/shard_map/ppermute | solution.py:25
  12.1 3.1 %collective-permute-start.1 = (f32[20,128]{1,0:T(8,128)S(1)}, f32[20,128]{1,0:T(8,128)S(1)}, u32[]{:S(2)}, u32[]{:S(2)}) collective-permute-start(f32[20,128]{1,0:T(8,128)S(1)} %reshape_squeeze.40), channel_id=1, source_target_pairs={{0,7},{1,0},{2,1},{3,2},{4,3},{5,4},{6,5},{7,6},{8,15},{9,8},{10,9... | collective-permute-start | bytes 30728 | tf_op jit(solution)/shard_map/ppermute | solution.py:25
  15.2 1.5 %fusion.50 = (f32[160,16,127]{2,1,0:T(8,128)S(1)}, f32[160,16,127]{2,1,0:T(8,128)}) fusion(f32[160,16,128]{2,1,0:T(8,128)S(1)} %fusion.1), kind=kLoop, calls=%fused_computation.108 | loop fusion | bytes 5201920 | tf_op jit(solution)/shard_map/slice | solution.py:40
  16.8 0.6 copy.31
  17.7 3.0 %fusion.8 = f32[160,16,128]{2,1,0:T(8,128)S(1)} fusion(f32[160,16,128]{2,1,0:T(8,128)S(1)} %fusion.1, f32[160,16,127]{2,1,0:T(8,128)} %get-tuple-element.75, f32[160,16,1]{2,1,0:T(8,128)} %get-tuple-element.72, f32[160,16,1]{2,1,0:T(8,128)} %get-tuple-element.73, f32[160,16,127]{2,1,0:T(8,128)S(1)} %get-tuple-element.74, ...), kind=kLoop, calls=%fused_computation.17 | loop fusion | flops 2293760 | bytes 5263872 | tf_op jit(solution)/shard_map/add | solution.py:52
  20.9 1.7 %collective-permute-start.3 = (f32[160,128]{1,0:T(8,128)S(1)}, f32[160,128]{1,0:T(8,128)S(1)}, u32[]{:S(2)}, u32[]{:S(2)}) collective-permute-start(f32[160,128]{1,0:T(8,128)S(1)} %bitcast.108), channel_id=1, source_target_pairs={{0,24},{8,0},{16,8},{24,16},{1,25},{9,1},{17,9},{25,17},{2,26},{10... | collective-permute-start | bytes 245768 | tf_op jit(solution)/shard_map/ppermute | solution.py:23
  22.8 1.9 %collective-permute-done.2 = f32[160,128]{1,0:T(8,128)S(1)} collective-permute-done((f32[160,128]{1,0:T(8,128)S(1)}, f32[160,128]{1,0:T(8,128)S(1)}, u32[]{:S(2)}, u32[]{:S(2)}) %collective-permute-start.2) | collective-permute-done | bytes 81952 | tf_op jit(solution)/shard_map/ppermute | solution.py:23
  24.9 0.6 fusion.13
  25.5 1.2 %fusion.3 = f32[160,16,128]{2,1,0:T(8,128)S(1)} fusion(f32[160,16,128]{2,1,0:T(8,128)S(1)} %fusion.13, f32[16,16,1]{1,0,2:T(8,128)S(1)} %copy-done.6, f32[16,128]{1,0:T(8,128)S(1)} %get-tuple-element.99), kind=kOutput, calls=%fused_computation.8 | convolution fusion | flops 63242240 | bytes 2630656 | tf_op jit(solution)/shard_map/ab,lby->lay/dot_general | solution.py:82
  26.7 1.2 %convolution_multiply_fusion.1 = f32[160,16,128]{2,1,0:T(8,128)S(1)} fusion(f32[160,16,128]{2,1,0:T(8,128)S(1)} %fusion.13, f32[128,128,1]{1,0,2:T(8,128)S(1)} %copy-done.5, f32[16,128]{1,0:T(8,128)S(1)} %get-tuple-element.98), kind=kOutput, calls=%fused_computation.2 | convolution fusion | flops 503644160 | bytes 2695168 | tf_op jit(solution)/shard_map/lxc,dc->lxd/dot_general | solution.py:87
  27.9 1.2 %fusion.4 = f32[160,16,128]{2,1,0:T(8,128)S(1)} fusion(f32[160,16,128]{2,1,0:T(8,128)S(1)} %fusion.3, f32[16,16,1]{1,0,2:T(8,128)S(1)} %copy-done.6, f32[128]{0:T(128)S(1)} %copy-done.12), kind=kOutput, calls=%fused_computation.10 | convolution fusion | flops 63242240 | bytes 2622976 | tf_op jit(solution)/shard_map/ba,lby->lay/dot_general | solution.py:84
  29.2 1.2 %fusion = f32[160,16,128]{2,1,0:T(8,128)S(1)} fusion(f32[160,16,128]{2,1,0:T(8,128)S(1)} %fusion.4, f32[160,16,128]{2,1,0:T(8,128)S(1)} %convolution_multiply_fusion.1, f32[128,128,1]{1,0,2:T(8,128)S(1)} %copy-done.5, f32[16]{0:T(128)S(1)} %copy-done.11), kind=kOutput, calls=%fused_computation.1 | convolution fusion | flops 503971840 | bytes 3997760 | tf_op jit(solution)/shard_map/lxc,cd->lxd/dot_general | solution.py:89
  30.4 2.0 %slice_reduce_fusion.5 = (f32[160,16]{1,0:T(8,128)S(1)}, f32[160,16]{1,0:T(8,128)S(1)}, f32[160,16,1]{2,1,0:T(8,128)}, f32[160,16,1]{2,1,0:T(8,128)}) fusion(f32[160,16,128]{2,1,0:T(8,128)S(1)} %fusion), kind=kLoop, calls=%fused_computation.100 | loop fusion | bytes 61440 | tf_op jit(solution)/shard_map/slice | solution.py:67
  32.5 0.7 collective-permute-start.4
  33.3 4.1 %collective-permute-start.5 = (f32[20,128]{1,0:T(8,128)S(1)}, f32[20,128]{1,0:T(8,128)S(1)}, u32[]{:S(2)}, u32[]{:S(2)}) collective-permute-start(f32[20,128]{1,0:T(8,128)S(1)} %reshape_squeeze.42), channel_id=1, source_target_pairs={{0,7},{1,0},{2,1},{3,2},{4,3},{5,4},{6,5},{7,6},{8,15},{9,8},{10,9... | collective-permute-start | bytes 30728 | tf_op jit(solution)/shard_map/ppermute | solution.py:25
  37.4 1.9 %fusion.47 = (f32[160,16,127]{2,1,0:T(8,128)}, f32[160,16,127]{2,1,0:T(8,128)}) fusion(f32[160,16,128]{2,1,0:T(8,128)S(1)} %fusion), kind=kLoop, calls=%fused_computation.105 | loop fusion | bytes 5201920 | tf_op jit(solution)/shard_map/slice | solution.py:40
  39.5 3.3 %fusion.16 = f32[160,16,128]{2,1,0:T(8,128)S(1)} fusion(f32[160,16,128]{2,1,0:T(8,128)S(1)} %fusion, f32[160,16,127]{2,1,0:T(8,128)} %get-tuple-element.67, f32[160,16,1]{2,1,0:T(8,128)} %get-tuple-element.64, f32[160,16,1]{2,1,0:T(8,128)} %get-tuple-element.65, f32[160,16,127]{2,1,0:T(8,128)} %get-tuple-element.66, f32[160,16]{1,0:T(8,128)S(1)} %broadcast_in_dim.289, ...), kind=kLoop, calls=%fused_computation.29 | loop fusion | flops 2293760 | bytes 5263872 | tf_op jit(solution)/shard_map/add | solution.py:52
  42.9 1.2 %collective-permute-start.6 = (f32[160,128]{1,0:T(8,128)S(1)}, f32[160,128]{1,0:T(8,128)S(1)}, u32[]{:S(2)}, u32[]{:S(2)}) collective-permute-start(f32[160,128]{1,0:T(8,128)S(1)} %bitcast.105), channel_id=1, source_target_pairs={{0,8},{8,16},{16,24},{24,0},{1,9},{9,17},{17,25},{25,1},{2,10},{10... | collective-permute-start | bytes 245768 | tf_op jit(solution)/shard_map/ppermute | solution.py:23
  44.1 0.6 collective-permute-start.7
  44.9 1.9 %collective-permute-done.6 = f32[160,128]{1,0:T(8,128)S(1)} collective-permute-done((f32[160,128]{1,0:T(8,128)S(1)}, f32[160,128]{1,0:T(8,128)S(1)}, u32[]{:S(2)}, u32[]{:S(2)}) %collective-permute-start.6) | collective-permute-done | bytes 81952 | tf_op jit(solution)/shard_map/ppermute | solution.py:23
  47.2 0.6 fusion.21
  47.9 1.0 copy-done.4
  48.9 0.6 fusion.25.table_ref
  49.5 6.2 %shard_map.176 = f32[4,8192]{1,0:T(4,128)} custom-call(s32[1,8192]{1,0:T(1,128)} %bitcast.113, f32[4,16,128]{2,1,0:T(8,128)} %fusion.25.table_ref), custom_call_target="tpu_custom_call" | custom-call | tf_op jit(solution)/shard_map/pallas_call | solution.py:169
  55.7 0.9 broadcast_multiply_fusion
  56.6 13.9 %all_to_all.5 = f32[4,32,256]{2,0,1:T(4,128)S(1)} all-to-all(f32[4,32,256]{2,0,1:T(4,128)S(1)} %broadcast_multiply_fusion), channel_id=1, replica_groups=mesh['gx'=4,'gy'=8] {'gx','gy'}, dimensions={1} | all-to-all | bytes 262144 | tf_op jit(solution)/shard_map/all_to_all | solution.py:209
  70.6 0.7 reshape_reshape.3.table_ref
  71.2 6.9 %shard_map.177 = f32[4,8192]{1,0:T(4,128)} custom-call(s32[1,8192]{1,0:T(1,128)} %bitcast.118, f32[4,64,128]{2,1,0:T(8,128)} %reshape_reshape.3.table_ref), custom_call_target="tpu_custom_call" | custom-call | tf_op jit(solution)/shard_map/pallas_call | solution.py:169
  78.1 0.9 copy.32
  79.1 1.3 %slice_reduce_fusion.3 = (f32[2,40,16]{2,1,0:T(8,128)S(1)}, f32[2,40,16]{2,1,0:T(8,128)S(1)}, f32[2,40,16,1]{3,2,1,0:T(8,128)}, f32[2,40,16,1]{3,2,1,0:T(8,128)}) fusion(f32[2,40,16,128]{3,2,1,0:T(8,128)S(1)} %get-tuple-element.95), kind=kLoop, calls=%fused_computation.98 | loop fusion | bytes 30720 | tf_op jit(solution)/shard_map/slice | solution.py:100
  80.5 1.2 %fusion.56 = (f32[2,40,16,127]{3,2,1,0:T(8,128)}, f32[2,40,16,127]{3,2,1,0:T(8,128)}) fusion(f32[2,40,16,128]{3,2,1,0:T(8,128)S(1)} %get-tuple-element.95), kind=kLoop, calls=%fused_computation.114 | loop fusion | bytes 2600960 | tf_op jit(solution)/shard_map/slice | solution.py:40
  81.9 2.1 %collective-permute-start.10 = (f32[10,128]{1,0:T(8,128)S(1)}, f32[10,128]{1,0:T(8,128)S(1)}, u32[]{:S(2)}, u32[]{:S(2)}) collective-permute-start(f32[10,128]{1,0:T(8,128)S(1)} %reshape_squeeze.46), channel_id=1, source_target_pairs={{0,7},{1,0},{2,1},{3,2},{4,3},{5,4},{6,5},{7,6},{8,15},{9,8},{10,9... | collective-permute-start | bytes 15368 | tf_op jit(solution)/shard_map/ppermute | solution.py:25
  84.4 0.5 collective-permute-start.9
  84.9 0.7 collective-permute-done.10
  85.7 4.8 %collective-permute-done.11 = f32[10,128]{1,0:T(8,128)S(1)} collective-permute-done((f32[10,128]{1,0:T(8,128)S(1)}, f32[10,128]{1,0:T(8,128)S(1)}, u32[]{:S(2)}, u32[]{:S(2)}) %collective-permute-start.11) | collective-permute-done | bytes 5152 | tf_op jit(solution)/shard_map/ppermute | solution.py:25
  90.5 2.3 %multiply_subtract_fusion.1 = f32[2,40,16,128]{3,2,1,0:T(8,128)S(1)} fusion(f32[2,40,16,128]{3,2,1,0:T(8,128)S(1)} %get-tuple-element.95, f32[2,40,16,127]{3,2,1,0:T(8,128)} %get-tuple-element.93, f32[2,40,16,1]{3,2,1,0:T(8,128)} %get-tuple-element.85, f32[2,40,16,1]{3,2,1,0:T(8,128)} %get-tuple-element.84, f32[2,40,16,127]{3,2,1,0:T(8,128)} %get-tuple-element.92, ...), kind=kLoop, calls=%fused_computation.48 | loop fusion | flops 3440640 | bytes 4679968 | tf_op jit(solution)/shard_map/sub | solution.py:104
  92.9 1.3 %slice_reduce_fusion.1 = (f32[2,40,16]{2,1,0:T(8,128)S(1)}, f32[2,40,16]{2,1,0:T(8,128)S(1)}, f32[2,40,16,1]{3,2,1,0:T(8,128)}, f32[2,40,16,1]{3,2,1,0:T(8,128)}) fusion(f32[2,40,16,128]{3,2,1,0:T(8,128)S(1)} %multiply_subtract_fusion.1), kind=kLoop, calls=%fused_computation.96 | loop fusion | bytes 30720 | tf_op jit(solution)/shard_map/slice | solution.py:100
  94.4 1.7 %collective-permute-start.14 = (f32[10,128]{1,0:T(8,128)S(1)}, f32[10,128]{1,0:T(8,128)S(1)}, u32[]{:S(2)}, u32[]{:S(2)}) collective-permute-start(f32[10,128]{1,0:T(8,128)S(1)} %reshape_squeeze.50), channel_id=1, source_target_pairs={{0,7},{1,0},{2,1},{3,2},{4,3},{5,4},{6,5},{7,6},{8,15},{9,8},{10,9... | collective-permute-start | bytes 15368 | tf_op jit(solution)/shard_map/ppermute | solution.py:25
  96.6 0.5 collective-permute-start.13
  97.1 1.0 fusion.53
  98.2 4.4 %collective-permute-done.15 = f32[10,128]{1,0:T(8,128)S(1)} collective-permute-done((f32[10,128]{1,0:T(8,128)S(1)}, f32[10,128]{1,0:T(8,128)S(1)}, u32[]{:S(2)}, u32[]{:S(2)}) %collective-permute-start.15) | collective-permute-done | bytes 5152 | tf_op jit(solution)/shard_map/ppermute | solution.py:25
  102.7 2.9 %multiply_subtract_fusion = f32[2,40,16,128]{3,2,1,0:T(8,128)} fusion(f32[2,40,16,128]{3,2,1,0:T(8,128)S(1)} %multiply_subtract_fusion.1, f32[2,40,16,127]{3,2,1,0:T(8,128)} %get-tuple-element.83, f32[2,40,16,1]{3,2,1,0:T(8,128)} %get-tuple-element.77, f32[2,40,16,1]{3,2,1,0:T(8,128)} %get-tuple-element.76, f32[2,40,16,127]{3,2,1,0:T(8,128)S(1)} %get-tuple-element.82, ...), kind=kLoop, calls=%fused_computation.47 | loop fusion | flops 3440640 | bytes 4679968 | tf_op jit(solution)/shard_map/sub | solution.py:104
  (78 shorter events, 4.4 us)
Async XLA Ops:
  0.6 0.7 copy-start.11
  0.6 0.7 copy-start.12
  0.7 0.9 copy-start.6
  0.7 1.3 %copy-start.1 = (f32[4,40,16,128]{3,2,1,0:T(8,128)S(1)}, f32[4,40,16,128]{3,2,1,0:T(8,128)}, u32[]{:S(2)}) copy-start(f32[4,40,16,128]{3,2,1,0:T(8,128)} %param.25) | copy-start | bytes 3932164
  0.7 0.8 copy-start.10
  3.2 1.3 %copy-start.5 = (f32[128,128,1]{1,0,2:T(8,128)S(1)}, f32[128,128,1]{1,0,2:T(8,128)}, u32[]{:S(2)}) copy-start(f32[128,128,1]{1,0,2:T(8,128)} %constant.180) | copy-start | bytes 196612
  9.0 8.4 %collective-permute-start = (f32[20,128]{1,0:T(8,128)S(1)}, f32[20,128]{1,0:T(8,128)S(1)}, u32[]{:S(2)}, u32[]{:S(2)}) collective-permute-start(f32[20,128]{1,0:T(8,128)S(1)} %reshape_squeeze.39), channel_id=1, source_target_pairs={{0,1},{1,2},{2,3},{3,4},{4,5},{5,6},{6,7},{7,0},{8,9},{9,10},{10,1... | collective-permute-start | bytes 30728 | tf_op jit(solution)/shard_map/ppermute | solution.py:25
  12.1 4.6 %copy-start.13 = (s32[1,32]{1,0:T(1,128)S(1)}, s32[1,32]{1,0:T(1,128)}, u32[]{:S(2)}) copy-start(s32[1,32]{1,0:T(1,128)} %param.28) | copy-start | bytes 388
  12.1 4.7 %copy-start.8 = (s32[1,32,256]{2,1,0:T(8,128)S(1)}, s32[1,32,256]{2,1,0:T(8,128)}, u32[]{:S(2)}) copy-start(s32[1,32,256]{2,1,0:T(8,128)} %param.27) | copy-start | bytes 98308
  12.1 5.4 %collective-permute-start.1 = (f32[20,128]{1,0:T(8,128)S(1)}, f32[20,128]{1,0:T(8,128)S(1)}, u32[]{:S(2)}, u32[]{:S(2)}) collective-permute-start(f32[20,128]{1,0:T(8,128)S(1)} %reshape_squeeze.40), channel_id=1, source_target_pairs={{0,7},{1,0},{2,1},{3,2},{4,3},{5,4},{6,5},{7,6},{8,15},{9,8},{10,9... | collective-permute-start | bytes 30728 | tf_op jit(solution)/shard_map/ppermute | solution.py:25
  20.8 3.9 %collective-permute-start.2 = (f32[160,128]{1,0:T(8,128)S(1)}, f32[160,128]{1,0:T(8,128)S(1)}, u32[]{:S(2)}, u32[]{:S(2)}) collective-permute-start(f32[160,128]{1,0:T(8,128)S(1)} %bitcast.107), channel_id=1, source_target_pairs={{0,8},{8,16},{16,24},{24,0},{1,9},{9,17},{17,25},{25,1},{2,10},{10... | collective-permute-start | bytes 245768 | tf_op jit(solution)/shard_map/ppermute | solution.py:23
  20.9 4.0 %copy-start.2 = (f32[4,40,16,128]{3,2,1,0:T(8,128)S(1)}, f32[4,40,16,128]{3,2,1,0:T(8,128)}, u32[]{:S(2)}) copy-start(f32[4,40,16,128]{3,2,1,0:T(8,128)} %param.25) | copy-start | bytes 3932164
  20.9 3.9 %copy-start.7 = (f32[16,128]{1,0:T(8,128)S(1)}, f32[16,128]{1,0:T(8,128)}, u32[]{:S(2)}) copy-start(f32[16,128]{1,0:T(8,128)} %constant.178) | copy-start | bytes 24580
  20.9 3.9 %collective-permute-start.3 = (f32[160,128]{1,0:T(8,128)S(1)}, f32[160,128]{1,0:T(8,128)S(1)}, u32[]{:S(2)}, u32[]{:S(2)}) collective-permute-start(f32[160,128]{1,0:T(8,128)S(1)} %bitcast.108), channel_id=1, source_target_pairs={{0,24},{8,0},{16,8},{24,16},{1,25},{9,1},{17,9},{25,17},{2,26},{10... | collective-permute-start | bytes 245768 | tf_op jit(solution)/shard_map/ppermute | solution.py:23
  32.5 6.8 %collective-permute-start.4 = (f32[20,128]{1,0:T(8,128)S(1)}, f32[20,128]{1,0:T(8,128)S(1)}, u32[]{:S(2)}, u32[]{:S(2)}) collective-permute-start(f32[20,128]{1,0:T(8,128)S(1)} %reshape_squeeze.41), channel_id=1, source_target_pairs={{0,1},{1,2},{2,3},{3,4},{4,5},{5,6},{6,7},{7,0},{8,9},{9,10},{10,1... | collective-permute-start | bytes 30728 | tf_op jit(solution)/shard_map/ppermute | solution.py:25
  33.3 6.1 %collective-permute-start.5 = (f32[20,128]{1,0:T(8,128)S(1)}, f32[20,128]{1,0:T(8,128)S(1)}, u32[]{:S(2)}, u32[]{:S(2)}) collective-permute-start(f32[20,128]{1,0:T(8,128)S(1)} %reshape_squeeze.42), channel_id=1, source_target_pairs={{0,7},{1,0},{2,1},{3,2},{4,3},{5,4},{6,5},{7,6},{8,15},{9,8},{10,9... | collective-permute-start | bytes 30728 | tf_op jit(solution)/shard_map/ppermute | solution.py:25
  42.9 3.9 %collective-permute-start.6 = (f32[160,128]{1,0:T(8,128)S(1)}, f32[160,128]{1,0:T(8,128)S(1)}, u32[]{:S(2)}, u32[]{:S(2)}) collective-permute-start(f32[160,128]{1,0:T(8,128)S(1)} %bitcast.105), channel_id=1, source_target_pairs={{0,8},{8,16},{16,24},{24,0},{1,9},{9,17},{17,25},{25,1},{2,10},{10... | collective-permute-start | bytes 245768 | tf_op jit(solution)/shard_map/ppermute | solution.py:23
  44.1 3.0 %collective-permute-start.7 = (f32[160,128]{1,0:T(8,128)S(1)}, f32[160,128]{1,0:T(8,128)S(1)}, u32[]{:S(2)}, u32[]{:S(2)}) collective-permute-start(f32[160,128]{1,0:T(8,128)S(1)} %bitcast.106), channel_id=1, source_target_pairs={{0,24},{8,0},{16,8},{24,16},{1,25},{9,1},{17,9},{25,17},{2,26},{10... | collective-permute-start | bytes 245768 | tf_op jit(solution)/shard_map/ppermute | solution.py:23
  47.8 1.1 %copy-start.4 = (f32[160,16,128]{2,1,0:T(8,128)}, f32[160,16,128]{2,1,0:T(8,128)S(1)}, u32[]{:S(2)}) copy-start(f32[160,16,128]{2,1,0:T(8,128)S(1)} %fusion.21) | copy-start | bytes 3932164
  47.8 31.2 %copy-start.9 = (f32[4,16,128]{2,1,0:T(8,128)S(1)}, f32[4,16,128]{2,1,0:T(8,128)}, u32[]{:S(2)}) copy-start(f32[4,16,128]{2,1,0:T(8,128)} %param.32) | copy-start | bytes 98308
  47.8 31.2 %copy-start = (f32[2,40,16,128]{3,2,1,0:T(8,128)S(1)}, f32[2,40,16,128]{3,2,1,0:T(8,128)}, u32[]{:S(2)}) copy-start(f32[2,40,16,128]{3,2,1,0:T(8,128)} %param.29) | copy-start | bytes 1966084
  47.8 31.2 %copy-start.3 = (f32[2,40,16,128]{3,2,1,0:T(8,128)S(1)}, f32[2,40,16,128]{3,2,1,0:T(8,128)}, u32[]{:S(2)}) copy-start(f32[2,40,16,128]{3,2,1,0:T(8,128)} %param.30) | copy-start | bytes 1966084
  81.9 3.7 %collective-permute-start.10 = (f32[10,128]{1,0:T(8,128)S(1)}, f32[10,128]{1,0:T(8,128)S(1)}, u32[]{:S(2)}, u32[]{:S(2)}) collective-permute-start(f32[10,128]{1,0:T(8,128)S(1)} %reshape_squeeze.46), channel_id=1, source_target_pairs={{0,7},{1,0},{2,1},{3,2},{4,3},{5,4},{6,5},{7,6},{8,15},{9,8},{10,9... | collective-permute-start | bytes 15368 | tf_op jit(solution)/shard_map/ppermute | solution.py:25
  84.1 6.4 %collective-permute-start.11 = (f32[10,128]{1,0:T(8,128)S(1)}, f32[10,128]{1,0:T(8,128)S(1)}, u32[]{:S(2)}, u32[]{:S(2)}) collective-permute-start(f32[10,128]{1,0:T(8,128)S(1)} %reshape_squeeze.47), channel_id=1, source_target_pairs={{0,1},{1,2},{2,3},{3,4},{4,5},{5,6},{6,7},{7,0},{8,9},{9,10},{10,1... | collective-permute-start | bytes 15368 | tf_op jit(solution)/shard_map/ppermute | solution.py:25
  84.1 6.4 %collective-permute-start.8 = (f32[80,128]{1,0:T(8,128)S(1)}, f32[80,128]{1,0:T(8,128)S(1)}, u32[]{:S(2)}, u32[]{:S(2)}) collective-permute-start(f32[80,128]{1,0:T(8,128)S(1)} %bitcast.112), channel_id=1, source_target_pairs={{0,24},{8,0},{16,8},{24,16},{1,25},{9,1},{17,9},{25,17},{2,26},{10... | collective-permute-start | bytes 122888 | tf_op jit(solution)/shard_map/ppermute | solution.py:23
  84.4 6.1 %collective-permute-start.9 = (f32[80,128]{1,0:T(8,128)S(1)}, f32[80,128]{1,0:T(8,128)S(1)}, u32[]{:S(2)}, u32[]{:S(2)}) collective-permute-start(f32[80,128]{1,0:T(8,128)S(1)} %bitcast.111), channel_id=1, source_target_pairs={{0,8},{8,16},{16,24},{24,0},{1,9},{9,17},{17,25},{25,1},{2,10},{10... | collective-permute-start | bytes 122888 | tf_op jit(solution)/shard_map/ppermute | solution.py:23
  94.4 3.7 %collective-permute-start.14 = (f32[10,128]{1,0:T(8,128)S(1)}, f32[10,128]{1,0:T(8,128)S(1)}, u32[]{:S(2)}, u32[]{:S(2)}) collective-permute-start(f32[10,128]{1,0:T(8,128)S(1)} %reshape_squeeze.50), channel_id=1, source_target_pairs={{0,7},{1,0},{2,1},{3,2},{4,3},{5,4},{6,5},{7,6},{8,15},{9,8},{10,9... | collective-permute-start | bytes 15368 | tf_op jit(solution)/shard_map/ppermute | solution.py:25
  96.2 6.4 %collective-permute-start.15 = (f32[10,128]{1,0:T(8,128)S(1)}, f32[10,128]{1,0:T(8,128)S(1)}, u32[]{:S(2)}, u32[]{:S(2)}) collective-permute-start(f32[10,128]{1,0:T(8,128)S(1)} %reshape_squeeze.51), channel_id=1, source_target_pairs={{0,1},{1,2},{2,3},{3,4},{4,5},{5,6},{6,7},{7,0},{8,9},{9,10},{10,1... | collective-permute-start | bytes 15368 | tf_op jit(solution)/shard_map/ppermute | solution.py:25
  96.6 6.1 %collective-permute-start.12 = (f32[80,128]{1,0:T(8,128)S(1)}, f32[80,128]{1,0:T(8,128)S(1)}, u32[]{:S(2)}, u32[]{:S(2)}) collective-permute-start(f32[80,128]{1,0:T(8,128)S(1)} %bitcast.110), channel_id=1, source_target_pairs={{0,24},{8,0},{16,8},{24,16},{1,25},{9,1},{17,9},{25,17},{2,26},{10... | collective-permute-start | bytes 122888 | tf_op jit(solution)/shard_map/ppermute | solution.py:23
  96.6 6.1 %collective-permute-start.13 = (f32[80,128]{1,0:T(8,128)S(1)}, f32[80,128]{1,0:T(8,128)S(1)}, u32[]{:S(2)}, u32[]{:S(2)}) collective-permute-start(f32[80,128]{1,0:T(8,128)S(1)} %bitcast.109), channel_id=1, source_target_pairs={{0,8},{8,16},{16,24},{24,0},{1,9},{9,17},{17,25},{25,1},{2,10},{10... | collective-permute-start | bytes 122888 | tf_op jit(solution)/shard_map/ppermute | solution.py:23

commit v7 on v6

--- a/solution.py
+++ b/solution.py
@@ -74,19 +74,19 @@
 
 def stiffness(state_in, metric, derivative_np, weights_np):
     levels, xsize, ysize = state_in.shape
-    highest = lax.Precision.HIGHEST
+    precision = lax.Precision.HIGH
     block_x = jnp.asarray(np.kron(np.eye(xsize // 4), derivative_np), jnp.float32)
     block_y = jnp.asarray(np.kron(np.eye(ysize // 4), derivative_np), jnp.float32)
     weight_x = jnp.asarray(np.tile(weights_np, xsize // 4), jnp.float32)[:, None]
     weight_y = jnp.asarray(np.tile(weights_np, ysize // 4), jnp.float32)[None, :]
-    along_x = jnp.einsum("ab,lby->lay", block_x, state_in, precision=highest)
+    along_x = jnp.einsum("ab,lby->lay", block_x, state_in, precision=precision)
     term_x = (
-        jnp.einsum("ba,lby->lay", block_x, weight_x * metric[0] * along_x, precision=highest)
+        jnp.einsum("ba,lby->lay", block_x, weight_x * metric[0] * along_x, precision=precision)
         * weight_y
     )
-    along_y = jnp.einsum("lxc,dc->lxd", state_in, block_y, precision=highest)
+    along_y = jnp.einsum("lxc,dc->lxd", state_in, block_y, precision=precision)
     term_y = (
-        jnp.einsum("lxc,cd->lxd", weight_y * metric[1] * along_y, block_y, precision=highest)
+        jnp.einsum("lxc,cd->lxd", weight_y * metric[1] * along_y, block_y, precision=precision)
         * weight_x
     )
     return term_x + term_y

time: 106 us -> 102 us (0.962)
  matrix products: 9.68 us -> 5.49 us
    dot_general x4, matrix products: 4.85 us -> 2.69 us  [the longest x2 1.38 us: stiffness(): along_y = jnp.einsum('lxc,dc->lxd', state_in, block_y, precision=precision)]
where the time goes in v7:
time: 102 us; the launch traced here: 101 us
  starting transfers between devices  19.7 us (19%)
  local copies, waits for them, and re-layouts  19.3 us (19%)
  other arithmetic  14.6 us (14%)
  waiting for transfers between devices  14.3 us (14%)
  blocking collectives  13.9 us (14%)
  Pallas kernels  13.1 us (13%)
  matrix products  5.49 us (5%)
  between operations  1.16 us (1%)
    ppermute x8, starting transfers between devices, neighbour(): lax.ppermute(values, 'gy', [(j, (j + step_y) % count_y) for j in range(co...  15.1 us
    all_to_all x1, blocking collectives, per_device(): lax.all_to_all(payload, ('gx', 'gy'), split_axis=1, concat_axis=1, tiled=...  13.9 us
    pallas_call x2, Pallas kernels, onehot_gather(): pl.pallas_call(gather_kernel, grid=(count // tile,), in_specs=[pl.BlockSp...  13.1 us
    ppermute x8, waiting for transfers between devices, neighbour(): lax.ppermute(values, 'gy', [(j, (j + step_y) % count_y) for j in range(co...  10 us
    add x2, other arithmetic, pair_merge(): values + jnp.where(position == 0, prev, jnp.where(position == 3, nxt, 0.0))  6.3 us
    slice x8, local copies, waits for them, and re-layouts, shifted(): lax.slice_in_dim(values, 1, size, axis=axis)  6.23 us
    sub x2, other arithmetic, tracer_step(): tracers + diff_coef * (east + west + north + south - 4.0 * tracers)  5.22 us
    ppermute x8, starting transfers between devices, neighbour(): lax.ppermute(values, 'gx', [(i, (i + step_x) % count_x) for i in range(co...  4.63 us
  transfers between devices with their start and end apart: 16, of which 7 were waited for; matrix products, arithmetic and copies ran while one was open for 6% of the time, Pallas kernels for 0%

profile of v7, /device:TPU:0, one launch (start us, length us, event | category | flops | bytes accessed | tf_op | source)
XLA Modules:
  0.0 101.5 jit_solution(5119805773975958354)
XLA Ops:
  0.7 0.6 copy-done.11
  2.0 0.7 fusion.6
  2.7 0.7 fusion.5
  3.5 0.7 fusion.2
  4.2 0.7 fusion.1
  4.9 2.0 %slice_reduce_fusion.7 = (f32[160,16]{1,0:T(8,128)S(1)}, f32[160,16]{1,0:T(8,128)S(1)}, f32[160,16,1]{2,1,0:T(8,128)}, f32[160,16,1]{2,1,0:T(8,128)}) fusion(f32[160,16,128]{2,1,0:T(8,128)S(1)} %fusion.1), kind=kLoop, calls=%fused_computation.102 | loop fusion | bytes 61440 | tf_op jit(solution)/shard_map/slice | solution.py:67
  7.0 3.0 %collective-permute-start = (f32[20,128]{1,0:T(8,128)S(1)}, f32[20,128]{1,0:T(8,128)S(1)}, u32[]{:S(2)}, u32[]{:S(2)}) collective-permute-start(f32[20,128]{1,0:T(8,128)S(1)} %reshape_squeeze.39), channel_id=1, source_target_pairs={{0,1},{1,2},{2,3},{3,4},{4,5},{5,6},{6,7},{7,0},{8,9},{9,10},{10,1... | collective-permute-start | bytes 30728 | tf_op jit(solution)/shard_map/ppermute | solution.py:25
  10.1 3.1 %collective-permute-start.1 = (f32[20,128]{1,0:T(8,128)S(1)}, f32[20,128]{1,0:T(8,128)S(1)}, u32[]{:S(2)}, u32[]{:S(2)}) collective-permute-start(f32[20,128]{1,0:T(8,128)S(1)} %reshape_squeeze.40), channel_id=1, source_target_pairs={{0,7},{1,0},{2,1},{3,2},{4,3},{5,4},{6,5},{7,6},{8,15},{9,8},{10,9... | collective-permute-start | bytes 30728 | tf_op jit(solution)/shard_map/ppermute | solution.py:25
  13.2 1.5 %fusion.50 = (f32[160,16,127]{2,1,0:T(8,128)S(1)}, f32[160,16,127]{2,1,0:T(8,128)}) fusion(f32[160,16,128]{2,1,0:T(8,128)S(1)} %fusion.1), kind=kLoop, calls=%fused_computation.108 | loop fusion | bytes 5201920 | tf_op jit(solution)/shard_map/slice | solution.py:40
  14.8 0.6 copy.31
  15.7 3.0 %fusion.8 = f32[160,16,128]{2,1,0:T(8,128)S(1)} fusion(f32[160,16,128]{2,1,0:T(8,128)S(1)} %fusion.1, f32[160,16,127]{2,1,0:T(8,128)} %get-tuple-element.75, f32[160,16,1]{2,1,0:T(8,128)} %get-tuple-element.72, f32[160,16,1]{2,1,0:T(8,128)} %get-tuple-element.73, f32[160,16,127]{2,1,0:T(8,128)S(1)} %get-tuple-element.74, ...), kind=kLoop, calls=%fused_computation.17 | loop fusion | flops 2293760 | bytes 5263872 | tf_op jit(solution)/shard_map/add | solution.py:52
  18.9 1.7 %collective-permute-start.3 = (f32[160,128]{1,0:T(8,128)S(1)}, f32[160,128]{1,0:T(8,128)S(1)}, u32[]{:S(2)}, u32[]{:S(2)}) collective-permute-start(f32[160,128]{1,0:T(8,128)S(1)} %bitcast.108), channel_id=1, source_target_pairs={{0,24},{8,0},{16,8},{24,16},{1,25},{9,1},{17,9},{25,17},{2,26},{10... | collective-permute-start | bytes 245768 | tf_op jit(solution)/shard_map/ppermute | solution.py:23
  20.8 1.9 %collective-permute-done.2 = f32[160,128]{1,0:T(8,128)S(1)} collective-permute-done((f32[160,128]{1,0:T(8,128)S(1)}, f32[160,128]{1,0:T(8,128)S(1)}, u32[]{:S(2)}, u32[]{:S(2)}) %collective-permute-start.2) | collective-permute-done | bytes 81952 | tf_op jit(solution)/shard_map/ppermute | solution.py:23
  22.9 0.6 fusion.13
  23.5 0.7 fusion.3
  24.2 0.7 convolution_multiply_fusion.1
  24.9 0.7 fusion.4
  25.6 0.7 fusion
  26.3 2.0 %slice_reduce_fusion.5 = (f32[160,16]{1,0:T(8,128)S(1)}, f32[160,16]{1,0:T(8,128)S(1)}, f32[160,16,1]{2,1,0:T(8,128)}, f32[160,16,1]{2,1,0:T(8,128)}) fusion(f32[160,16,128]{2,1,0:T(8,128)S(1)} %fusion), kind=kLoop, calls=%fused_computation.100 | loop fusion | bytes 61440 | tf_op jit(solution)/shard_map/slice | solution.py:67
  28.4 0.7 collective-permute-start.4
  29.2 4.1 %collective-permute-start.5 = (f32[20,128]{1,0:T(8,128)S(1)}, f32[20,128]{1,0:T(8,128)S(1)}, u32[]{:S(2)}, u32[]{:S(2)}) collective-permute-start(f32[20,128]{1,0:T(8,128)S(1)} %reshape_squeeze.42), channel_id=1, source_target_pairs={{0,7},{1,0},{2,1},{3,2},{4,3},{5,4},{6,5},{7,6},{8,15},{9,8},{10,9... | collective-permute-start | bytes 30728 | tf_op jit(solution)/shard_map/ppermute | solution.py:25
  33.3 1.9 %fusion.47 = (f32[160,16,127]{2,1,0:T(8,128)}, f32[160,16,127]{2,1,0:T(8,128)}) fusion(f32[160,16,128]{2,1,0:T(8,128)S(1)} %fusion), kind=kLoop, calls=%fused_computation.105 | loop fusion | bytes 5201920 | tf_op jit(solution)/shard_map/slice | solution.py:40
  35.4 3.3 %fusion.16 = f32[160,16,128]{2,1,0:T(8,128)S(1)} fusion(f32[160,16,128]{2,1,0:T(8,128)S(1)} %fusion, f32[160,16,127]{2,1,0:T(8,128)} %get-tuple-element.67, f32[160,16,1]{2,1,0:T(8,128)} %get-tuple-element.64, f32[160,16,1]{2,1,0:T(8,128)} %get-tuple-element.65, f32[160,16,127]{2,1,0:T(8,128)} %get-tuple-element.66, f32[160,16]{1,0:T(8,128)S(1)} %broadcast_in_dim.289, ...), kind=kLoop, calls=%fused_computation.29 | loop fusion | flops 2293760 | bytes 5263872 | tf_op jit(solution)/shard_map/add | solution.py:52
  38.8 1.2 %collective-permute-start.6 = (f32[160,128]{1,0:T(8,128)S(1)}, f32[160,128]{1,0:T(8,128)S(1)}, u32[]{:S(2)}, u32[]{:S(2)}) collective-permute-start(f32[160,128]{1,0:T(8,128)S(1)} %bitcast.105), channel_id=1, source_target_pairs={{0,8},{8,16},{16,24},{24,0},{1,9},{9,17},{17,25},{25,1},{2,10},{10... | collective-permute-start | bytes 245768 | tf_op jit(solution)/shard_map/ppermute | solution.py:23
  40.0 0.6 collective-permute-start.7
  40.8 1.9 %collective-permute-done.6 = f32[160,128]{1,0:T(8,128)S(1)} collective-permute-done((f32[160,128]{1,0:T(8,128)S(1)}, f32[160,128]{1,0:T(8,128)S(1)}, u32[]{:S(2)}, u32[]{:S(2)}) %collective-permute-start.6) | collective-permute-done | bytes 81952 | tf_op jit(solution)/shard_map/ppermute | solution.py:23
  43.1 0.6 fusion.21
  43.8 1.0 copy-done.4
  44.7 0.6 fusion.25.table_ref
  45.4 6.2 %shard_map.176 = f32[4,8192]{1,0:T(4,128)} custom-call(s32[1,8192]{1,0:T(1,128)} %bitcast.113, f32[4,16,128]{2,1,0:T(8,128)} %fusion.25.table_ref), custom_call_target="tpu_custom_call" | custom-call | tf_op jit(solution)/shard_map/pallas_call | solution.py:169
  51.6 0.9 broadcast_multiply_fusion
  52.5 13.9 %all_to_all.5 = f32[4,32,256]{2,0,1:T(4,128)S(1)} all-to-all(f32[4,32,256]{2,0,1:T(4,128)S(1)} %broadcast_multiply_fusion), channel_id=1, replica_groups=mesh['gx'=4,'gy'=8] {'gx','gy'}, dimensions={1} | all-to-all | bytes 262144 | tf_op jit(solution)/shard_map/all_to_all | solution.py:209
  66.5 0.7 reshape_reshape.3.table_ref
  67.1 6.9 %shard_map.177 = f32[4,8192]{1,0:T(4,128)} custom-call(s32[1,8192]{1,0:T(1,128)} %bitcast.118, f32[4,64,128]{2,1,0:T(8,128)} %reshape_reshape.3.table_ref), custom_call_target="tpu_custom_call" | custom-call | tf_op jit(solution)/shard_map/pallas_call | solution.py:169
  74.0 0.9 copy.32
  75.0 1.3 %slice_reduce_fusion.3 = (f32[2,40,16]{2,1,0:T(8,128)S(1)}, f32[2,40,16]{2,1,0:T(8,128)S(1)}, f32[2,40,16,1]{3,2,1,0:T(8,128)}, f32[2,40,16,1]{3,2,1,0:T(8,128)}) fusion(f32[2,40,16,128]{3,2,1,0:T(8,128)S(1)} %get-tuple-element.95), kind=kLoop, calls=%fused_computation.98 | loop fusion | bytes 30720 | tf_op jit(solution)/shard_map/slice | solution.py:100
  76.4 1.2 %fusion.56 = (f32[2,40,16,127]{3,2,1,0:T(8,128)}, f32[2,40,16,127]{3,2,1,0:T(8,128)}) fusion(f32[2,40,16,128]{3,2,1,0:T(8,128)S(1)} %get-tuple-element.95), kind=kLoop, calls=%fused_computation.114 | loop fusion | bytes 2600960 | tf_op jit(solution)/shard_map/slice | solution.py:40
  77.8 2.1 %collective-permute-start.10 = (f32[10,128]{1,0:T(8,128)S(1)}, f32[10,128]{1,0:T(8,128)S(1)}, u32[]{:S(2)}, u32[]{:S(2)}) collective-permute-start(f32[10,128]{1,0:T(8,128)S(1)} %reshape_squeeze.46), channel_id=1, source_target_pairs={{0,7},{1,0},{2,1},{3,2},{4,3},{5,4},{6,5},{7,6},{8,15},{9,8},{10,9... | collective-permute-start | bytes 15368 | tf_op jit(solution)/shard_map/ppermute | solution.py:25
  80.1 0.5 collective-permute-start.9
  80.6 0.9 collective-permute-done.10
  81.6 4.8 %collective-permute-done.11 = f32[10,128]{1,0:T(8,128)S(1)} collective-permute-done((f32[10,128]{1,0:T(8,128)S(1)}, f32[10,128]{1,0:T(8,128)S(1)}, u32[]{:S(2)}, u32[]{:S(2)}) %collective-permute-start.11) | collective-permute-done | bytes 5152 | tf_op jit(solution)/shard_map/ppermute | solution.py:25
  86.4 2.3 %multiply_subtract_fusion.1 = f32[2,40,16,128]{3,2,1,0:T(8,128)S(1)} fusion(f32[2,40,16,128]{3,2,1,0:T(8,128)S(1)} %get-tuple-element.95, f32[2,40,16,127]{3,2,1,0:T(8,128)} %get-tuple-element.93, f32[2,40,16,1]{3,2,1,0:T(8,128)} %get-tuple-element.85, f32[2,40,16,1]{3,2,1,0:T(8,128)} %get-tuple-element.84, f32[2,40,16,127]{3,2,1,0:T(8,128)} %get-tuple-element.92, ...), kind=kLoop, calls=%fused_computation.48 | loop fusion | flops 3440640 | bytes 4679968 | tf_op jit(solution)/shard_map/sub | solution.py:104
  88.8 1.3 %slice_reduce_fusion.1 = (f32[2,40,16]{2,1,0:T(8,128)S(1)}, f32[2,40,16]{2,1,0:T(8,128)S(1)}, f32[2,40,16,1]{3,2,1,0:T(8,128)}, f32[2,40,16,1]{3,2,1,0:T(8,128)}) fusion(f32[2,40,16,128]{3,2,1,0:T(8,128)S(1)} %multiply_subtract_fusion.1), kind=kLoop, calls=%fused_computation.96 | loop fusion | bytes 30720 | tf_op jit(solution)/shard_map/slice | solution.py:100
  90.3 1.7 %collective-permute-start.14 = (f32[10,128]{1,0:T(8,128)S(1)}, f32[10,128]{1,0:T(8,128)S(1)}, u32[]{:S(2)}, u32[]{:S(2)}) collective-permute-start(f32[10,128]{1,0:T(8,128)S(1)} %reshape_squeeze.50), channel_id=1, source_target_pairs={{0,7},{1,0},{2,1},{3,2},{4,3},{5,4},{6,5},{7,6},{8,15},{9,8},{10,9... | collective-permute-start | bytes 15368 | tf_op jit(solution)/shard_map/ppermute | solution.py:25
  92.5 0.5 collective-permute-start.13
  93.0 1.0 %fusion.53 = (f32[2,40,16,127]{3,2,1,0:T(8,128)S(1)}, f32[2,40,16,127]{3,2,1,0:T(8,128)}) fusion(f32[2,40,16,128]{3,2,1,0:T(8,128)S(1)} %multiply_subtract_fusion.1), kind=kLoop, calls=%fused_computation.111 | loop fusion | bytes 2600960 | tf_op jit(solution)/shard_map/slice | solution.py:40
  94.1 4.4 %collective-permute-done.15 = f32[10,128]{1,0:T(8,128)S(1)} collective-permute-done((f32[10,128]{1,0:T(8,128)S(1)}, f32[10,128]{1,0:T(8,128)S(1)}, u32[]{:S(2)}, u32[]{:S(2)}) %collective-permute-start.15) | collective-permute-done | bytes 5152 | tf_op jit(solution)/shard_map/ppermute | solution.py:25
  98.6 2.9 %multiply_subtract_fusion = f32[2,40,16,128]{3,2,1,0:T(8,128)} fusion(f32[2,40,16,128]{3,2,1,0:T(8,128)S(1)} %multiply_subtract_fusion.1, f32[2,40,16,127]{3,2,1,0:T(8,128)} %get-tuple-element.83, f32[2,40,16,1]{3,2,1,0:T(8,128)} %get-tuple-element.77, f32[2,40,16,1]{3,2,1,0:T(8,128)} %get-tuple-element.76, f32[2,40,16,127]{3,2,1,0:T(8,128)S(1)} %get-tuple-element.82, ...), kind=kLoop, calls=%fused_computation.47 | loop fusion | flops 3440640 | bytes 4679968 | tf_op jit(solution)/shard_map/sub | solution.py:104
  (78 shorter events, 4.3 us)
Async XLA Ops:
  0.6 0.7 copy-start.11
  0.6 0.7 copy-start.12
  0.7 0.9 copy-start.6
  0.7 1.3 %copy-start.1 = (f32[4,40,16,128]{3,2,1,0:T(8,128)S(1)}, f32[4,40,16,128]{3,2,1,0:T(8,128)}, u32[]{:S(2)}) copy-start(f32[4,40,16,128]{3,2,1,0:T(8,128)} %param.25) | copy-start | bytes 3932164
  0.7 0.8 copy-start.10
  2.7 0.8 copy-start.5
  7.0 8.4 %collective-permute-start = (f32[20,128]{1,0:T(8,128)S(1)}, f32[20,128]{1,0:T(8,128)S(1)}, u32[]{:S(2)}, u32[]{:S(2)}) collective-permute-start(f32[20,128]{1,0:T(8,128)S(1)} %reshape_squeeze.39), channel_id=1, source_target_pairs={{0,1},{1,2},{2,3},{3,4},{4,5},{5,6},{6,7},{7,0},{8,9},{9,10},{10,1... | collective-permute-start | bytes 30728 | tf_op jit(solution)/shard_map/ppermute | solution.py:25
  10.1 4.6 %copy-start.13 = (s32[1,32]{1,0:T(1,128)S(1)}, s32[1,32]{1,0:T(1,128)}, u32[]{:S(2)}) copy-start(s32[1,32]{1,0:T(1,128)} %param.28) | copy-start | bytes 388
  10.1 4.7 %copy-start.8 = (s32[1,32,256]{2,1,0:T(8,128)S(1)}, s32[1,32,256]{2,1,0:T(8,128)}, u32[]{:S(2)}) copy-start(s32[1,32,256]{2,1,0:T(8,128)} %param.27) | copy-start | bytes 98308
  10.1 5.4 %collective-permute-start.1 = (f32[20,128]{1,0:T(8,128)S(1)}, f32[20,128]{1,0:T(8,128)S(1)}, u32[]{:S(2)}, u32[]{:S(2)}) collective-permute-start(f32[20,128]{1,0:T(8,128)S(1)} %reshape_squeeze.40), channel_id=1, source_target_pairs={{0,7},{1,0},{2,1},{3,2},{4,3},{5,4},{6,5},{7,6},{8,15},{9,8},{10,9... | collective-permute-start | bytes 30728 | tf_op jit(solution)/shard_map/ppermute | solution.py:25
  18.8 3.9 %collective-permute-start.2 = (f32[160,128]{1,0:T(8,128)S(1)}, f32[160,128]{1,0:T(8,128)S(1)}, u32[]{:S(2)}, u32[]{:S(2)}) collective-permute-start(f32[160,128]{1,0:T(8,128)S(1)} %bitcast.107), channel_id=1, source_target_pairs={{0,8},{8,16},{16,24},{24,0},{1,9},{9,17},{17,25},{25,1},{2,10},{10... | collective-permute-start | bytes 245768 | tf_op jit(solution)/shard_map/ppermute | solution.py:23
  18.9 4.0 %copy-start.2 = (f32[4,40,16,128]{3,2,1,0:T(8,128)S(1)}, f32[4,40,16,128]{3,2,1,0:T(8,128)}, u32[]{:S(2)}) copy-start(f32[4,40,16,128]{3,2,1,0:T(8,128)} %param.25) | copy-start | bytes 3932164
  18.9 3.9 %copy-start.7 = (f32[16,128]{1,0:T(8,128)S(1)}, f32[16,128]{1,0:T(8,128)}, u32[]{:S(2)}) copy-start(f32[16,128]{1,0:T(8,128)} %constant.178) | copy-start | bytes 24580
  18.9 3.9 %collective-permute-start.3 = (f32[160,128]{1,0:T(8,128)S(1)}, f32[160,128]{1,0:T(8,128)S(1)}, u32[]{:S(2)}, u32[]{:S(2)}) collective-permute-start(f32[160,128]{1,0:T(8,128)S(1)} %bitcast.108), channel_id=1, source_target_pairs={{0,24},{8,0},{16,8},{24,16},{1,25},{9,1},{17,9},{25,17},{2,26},{10... | collective-permute-start | bytes 245768 | tf_op jit(solution)/shard_map/ppermute | solution.py:23
  28.4 6.8 %collective-permute-start.4 = (f32[20,128]{1,0:T(8,128)S(1)}, f32[20,128]{1,0:T(8,128)S(1)}, u32[]{:S(2)}, u32[]{:S(2)}) collective-permute-start(f32[20,128]{1,0:T(8,128)S(1)} %reshape_squeeze.41), channel_id=1, source_target_pairs={{0,1},{1,2},{2,3},{3,4},{4,5},{5,6},{6,7},{7,0},{8,9},{9,10},{10,1... | collective-permute-start | bytes 30728 | tf_op jit(solution)/shard_map/ppermute | solution.py:25
  29.2 6.1 %collective-permute-start.5 = (f32[20,128]{1,0:T(8,128)S(1)}, f32[20,128]{1,0:T(8,128)S(1)}, u32[]{:S(2)}, u32[]{:S(2)}) collective-permute-start(f32[20,128]{1,0:T(8,128)S(1)} %reshape_squeeze.42), channel_id=1, source_target_pairs={{0,7},{1,0},{2,1},{3,2},{4,3},{5,4},{6,5},{7,6},{8,15},{9,8},{10,9... | collective-permute-start | bytes 30728 | tf_op jit(solution)/shard_map/ppermute | solution.py:25
  38.8 3.9 %collective-permute-start.6 = (f32[160,128]{1,0:T(8,128)S(1)}, f32[160,128]{1,0:T(8,128)S(1)}, u32[]{:S(2)}, u32[]{:S(2)}) collective-permute-start(f32[160,128]{1,0:T(8,128)S(1)} %bitcast.105), channel_id=1, source_target_pairs={{0,8},{8,16},{16,24},{24,0},{1,9},{9,17},{17,25},{25,1},{2,10},{10... | collective-permute-start | bytes 245768 | tf_op jit(solution)/shard_map/ppermute | solution.py:23
  40.0 3.0 %collective-permute-start.7 = (f32[160,128]{1,0:T(8,128)S(1)}, f32[160,128]{1,0:T(8,128)S(1)}, u32[]{:S(2)}, u32[]{:S(2)}) collective-permute-start(f32[160,128]{1,0:T(8,128)S(1)} %bitcast.106), channel_id=1, source_target_pairs={{0,24},{8,0},{16,8},{24,16},{1,25},{9,1},{17,9},{25,17},{2,26},{10... | collective-permute-start | bytes 245768 | tf_op jit(solution)/shard_map/ppermute | solution.py:23
  43.7 1.1 %copy-start.4 = (f32[160,16,128]{2,1,0:T(8,128)}, f32[160,16,128]{2,1,0:T(8,128)S(1)}, u32[]{:S(2)}) copy-start(f32[160,16,128]{2,1,0:T(8,128)S(1)} %fusion.21) | copy-start | bytes 3932164
  43.7 31.2 %copy-start.9 = (f32[4,16,128]{2,1,0:T(8,128)S(1)}, f32[4,16,128]{2,1,0:T(8,128)}, u32[]{:S(2)}) copy-start(f32[4,16,128]{2,1,0:T(8,128)} %param.32) | copy-start | bytes 98308
  43.7 31.2 %copy-start = (f32[2,40,16,128]{3,2,1,0:T(8,128)S(1)}, f32[2,40,16,128]{3,2,1,0:T(8,128)}, u32[]{:S(2)}) copy-start(f32[2,40,16,128]{3,2,1,0:T(8,128)} %param.29) | copy-start | bytes 1966084
  43.7 31.2 %copy-start.3 = (f32[2,40,16,128]{3,2,1,0:T(8,128)S(1)}, f32[2,40,16,128]{3,2,1,0:T(8,128)}, u32[]{:S(2)}) copy-start(f32[2,40,16,128]{3,2,1,0:T(8,128)} %param.30) | copy-start | bytes 1966084
  77.8 3.7 %collective-permute-start.10 = (f32[10,128]{1,0:T(8,128)S(1)}, f32[10,128]{1,0:T(8,128)S(1)}, u32[]{:S(2)}, u32[]{:S(2)}) collective-permute-start(f32[10,128]{1,0:T(8,128)S(1)} %reshape_squeeze.46), channel_id=1, source_target_pairs={{0,7},{1,0},{2,1},{3,2},{4,3},{5,4},{6,5},{7,6},{8,15},{9,8},{10,9... | collective-permute-start | bytes 15368 | tf_op jit(solution)/shard_map/ppermute | solution.py:25
  80.0 6.4 %collective-permute-start.11 = (f32[10,128]{1,0:T(8,128)S(1)}, f32[10,128]{1,0:T(8,128)S(1)}, u32[]{:S(2)}, u32[]{:S(2)}) collective-permute-start(f32[10,128]{1,0:T(8,128)S(1)} %reshape_squeeze.47), channel_id=1, source_target_pairs={{0,1},{1,2},{2,3},{3,4},{4,5},{5,6},{6,7},{7,0},{8,9},{9,10},{10,1... | collective-permute-start | bytes 15368 | tf_op jit(solution)/shard_map/ppermute | solution.py:25
  80.0 6.4 %collective-permute-start.8 = (f32[80,128]{1,0:T(8,128)S(1)}, f32[80,128]{1,0:T(8,128)S(1)}, u32[]{:S(2)}, u32[]{:S(2)}) collective-permute-start(f32[80,128]{1,0:T(8,128)S(1)} %bitcast.112), channel_id=1, source_target_pairs={{0,24},{8,0},{16,8},{24,16},{1,25},{9,1},{17,9},{25,17},{2,26},{10... | collective-permute-start | bytes 122888 | tf_op jit(solution)/shard_map/ppermute | solution.py:23
  80.1 6.4 %collective-permute-start.9 = (f32[80,128]{1,0:T(8,128)S(1)}, f32[80,128]{1,0:T(8,128)S(1)}, u32[]{:S(2)}, u32[]{:S(2)}) collective-permute-start(f32[80,128]{1,0:T(8,128)S(1)} %bitcast.111), channel_id=1, source_target_pairs={{0,8},{8,16},{16,24},{24,0},{1,9},{9,17},{17,25},{25,1},{2,10},{10... | collective-permute-start | bytes 122888 | tf_op jit(solution)/shard_map/ppermute | solution.py:23
  90.3 3.7 %collective-permute-start.14 = (f32[10,128]{1,0:T(8,128)S(1)}, f32[10,128]{1,0:T(8,128)S(1)}, u32[]{:S(2)}, u32[]{:S(2)}) collective-permute-start(f32[10,128]{1,0:T(8,128)S(1)} %reshape_squeeze.50), channel_id=1, source_target_pairs={{0,7},{1,0},{2,1},{3,2},{4,3},{5,4},{6,5},{7,6},{8,15},{9,8},{10,9... | collective-permute-start | bytes 15368 | tf_op jit(solution)/shard_map/ppermute | solution.py:25
  92.1 6.4 %collective-permute-start.15 = (f32[10,128]{1,0:T(8,128)S(1)}, f32[10,128]{1,0:T(8,128)S(1)}, u32[]{:S(2)}, u32[]{:S(2)}) collective-permute-start(f32[10,128]{1,0:T(8,128)S(1)} %reshape_squeeze.51), channel_id=1, source_target_pairs={{0,1},{1,2},{2,3},{3,4},{4,5},{5,6},{6,7},{7,0},{8,9},{9,10},{10,1... | collective-permute-start | bytes 15368 | tf_op jit(solution)/shard_map/ppermute | solution.py:25
  92.5 6.1 %collective-permute-start.12 = (f32[80,128]{1,0:T(8,128)S(1)}, f32[80,128]{1,0:T(8,128)S(1)}, u32[]{:S(2)}, u32[]{:S(2)}) collective-permute-start(f32[80,128]{1,0:T(8,128)S(1)} %bitcast.110), channel_id=1, source_target_pairs={{0,24},{8,0},{16,8},{24,16},{1,25},{9,1},{17,9},{25,17},{2,26},{10... | collective-permute-start | bytes 122888 | tf_op jit(solution)/shard_map/ppermute | solution.py:23
  92.5 6.1 %collective-permute-start.13 = (f32[80,128]{1,0:T(8,128)S(1)}, f32[80,128]{1,0:T(8,128)S(1)}, u32[]{:S(2)}, u32[]{:S(2)}) collective-permute-start(f32[80,128]{1,0:T(8,128)S(1)} %bitcast.109), channel_id=1, source_target_pairs={{0,8},{8,16},{16,24},{24,0},{1,9},{9,17},{17,25},{25,1},{2,10},{10... | collective-permute-start | bytes 122888 | tf_op jit(solution)/shard_map/ppermute | solution.py:23

commit v8 on v7

--- a/solution.py
+++ b/solution.py
@@ -43,15 +43,6 @@
     return prev, nxt
 
 
-def pair_merge(values, before, after, axis):
-    size = values.shape[axis]
-    layout = [1] * values.ndim
-    layout[axis] = size
-    position = (jnp.arange(size) % 4).reshape(layout)
-    prev, nxt = shifted(values, before, after, axis)
-    return values + jnp.where(position == 0, prev, jnp.where(position == 3, nxt, 0.0))
-
-
 def packed(values):
     if values.size % 128:
         return values
@@ -62,34 +53,48 @@
     return neighbour(packed(values), step_x, step_y).reshape(values.shape)
 
 
-def assemble(stiff):
-    last_x, last_y = stiff.shape[1] - 1, stiff.shape[2] - 1
-    from_left = exchange(stiff[:, :, last_y], 0, 1)[:, :, None]
-    from_right = exchange(stiff[:, :, 0], 0, -1)[:, :, None]
-    merged = pair_merge(stiff, from_left, from_right, 2)
+def pair_matrix(size):
+    position = np.arange(size)
+    starts = position[position % 4 == 0][1:]
+    ends = position[position % 4 == 3][:-1]
+    pair = np.eye(size)
+    pair[starts - 1, starts] = 1.0
+    pair[ends + 1, ends] = 1.0
+    return pair
+
+
+def substep(state_in, metric, derivative_np, weights_np, inv_mass):
+    levels, xsize, ysize = state_in.shape
+    precision = lax.Precision.HIGH
+    block_x = np.kron(np.eye(xsize // 4), derivative_np)
+    block_y = np.kron(np.eye(ysize // 4), derivative_np)
+    weight_x = np.tile(weights_np, xsize // 4)
+    weight_y = np.tile(weights_np, ysize // 4)
+    pair_y = pair_matrix(ysize)
+    term_x_right = jnp.asarray(weight_y[:, None] * pair_y, jnp.float32)
+    term_y_right = jnp.asarray(block_y @ pair_y, jnp.float32)
+    pair_x = jnp.asarray(pair_matrix(xsize).T, jnp.float32)
+    block_x = jnp.asarray(block_x, jnp.float32)
+    along_x = jnp.einsum("ab,lby->lay", block_x, state_in, precision=precision)
+    scaled_x = jnp.asarray(weight_x[:, None], jnp.float32) * metric[0] * along_x
+    term_x = jnp.einsum("ba,lby->lay", block_x, scaled_x, precision=precision)
+    along_y = jnp.einsum("lxc,dc->lxd", state_in, jnp.asarray(block_y, jnp.float32), precision=precision)
+    scaled_y = jnp.asarray(weight_y[None, :], jnp.float32) * metric[1] * along_y
+    merged = jnp.einsum("lxc,cd->lxd", term_x, term_x_right, precision=precision) + jnp.einsum(
+        "lxc,cd->lxd", scaled_y, term_y_right, precision=precision
+    ) * jnp.asarray(weight_x[:, None], jnp.float32)
+    last_x, last_y = xsize - 1, ysize - 1
+    from_left = exchange(merged[:, :, last_y], 0, 1)[:, :, None]
+    from_right = exchange(merged[:, :, 0], 0, -1)[:, :, None]
+    column = jnp.arange(ysize)
+    merged = merged + jnp.where(column == 0, from_left, jnp.where(column == last_y, from_right, 0.0))
     from_up = exchange(merged[:, last_x, :], 1, 0)[:, None, :]
     from_down = exchange(merged[:, 0, :], -1, 0)[:, None, :]
-    return pair_merge(merged, from_up, from_down, 1)
-
-
-def stiffness(state_in, metric, derivative_np, weights_np):
-    levels, xsize, ysize = state_in.shape
-    precision = lax.Precision.HIGH
-    block_x = jnp.asarray(np.kron(np.eye(xsize // 4), derivative_np), jnp.float32)
-    block_y = jnp.asarray(np.kron(np.eye(ysize // 4), derivative_np), jnp.float32)
-    weight_x = jnp.asarray(np.tile(weights_np, xsize // 4), jnp.float32)[:, None]
-    weight_y = jnp.asarray(np.tile(weights_np, ysize // 4), jnp.float32)[None, :]
-    along_x = jnp.einsum("ab,lby->lay", block_x, state_in, precision=precision)
-    term_x = (
-        jnp.einsum("ba,lby->lay", block_x, weight_x * metric[0] * along_x, precision=precision)
-        * weight_y
-    )
-    along_y = jnp.einsum("lxc,dc->lxd", state_in, block_y, precision=precision)
-    term_y = (
-        jnp.einsum("lxc,cd->lxd", weight_y * metric[1] * along_y, block_y, precision=precision)
-        * weight_x
-    )
-    return term_x + term_y
+    row = jnp.arange(xsize)[:, None]
+    total = jnp.einsum("ab,lby->lay", pair_x, merged, precision=precision) + jnp.where(
+        row == 0, from_up, jnp.where(row == last_x, from_down, 0.0)
+    )
+    return state_in - visc_coef * total * inv_mass
 
 
 def tracer_step(tracers, velocity):
@@ -192,9 +197,8 @@
     derivative_np, weights_np, massw_np = gll_tables()
     state_now = atm_state.reshape(fields * levels, xlocal, ylocal)
     inv_mass = mass_inverse(massw_np, xlocal, ylocal)
-    for substep in range(SUB):
-        stiff = stiffness(state_now, metric, derivative_np, weights_np)
-        state_now = state_now - visc_coef * assemble(stiff) * inv_mass
+    for repeat in range(SUB):
+        state_now = substep(state_now, metric, derivative_np, weights_np, inv_mass)
     atm_out = state_now.reshape(fields, levels, xlocal, ylocal)
     bottom = atm_out[:, levels - 1]
     speed = jnp.sqrt(1.0 + bottom[0] * bottom[0] + bottom[1] * bottom[1])

time: 102 us -> 99.5 us (0.975)
  other arithmetic: 14.6 us -> 8.69 us
  local copies, waits for them, and re-layouts: 19.3 us -> 13.9 us
  starting transfers between devices: 19.7 us -> 22.7 us
  matrix products: 5.49 us -> 8.48 us
  waiting for transfers between devices: 14.3 us -> 17 us
    ppermute x8, starting transfers between devices: 15.1 us -> 20.6 us  [neighbour(): lax.ppermute(values, 'gy', [(j, (j + step_y) % count_y) for j in range(co...]
    add x2, other arithmetic: 6.3 us -> 1.69 us  [substep(): merged + jnp.where(column == 0, from_left, jnp.where(column == last_y, fr...]
    slice x8 -> x4, local copies, waits for them, and re-layouts: 6.23 us -> 2.48 us  [shifted(): lax.slice_in_dim(values, 1, size, axis=axis)]
    dot_general x8 -> x12, matrix products: 5.49 us -> 8.48 us  [the longest x2 1.66 us: substep(): jnp.einsum('ab,lby->lay', pair_x, merged, precision=precision)]
    ppermute x8, waiting for transfers between devices: 4.28 us -> 7.18 us  [neighbour(): lax.ppermute(values, 'gx', [(i, (i + step_x) % count_x) for i in range(co...]
    ppermute x8, starting transfers between devices: 4.63 us -> 2.13 us  [neighbour(): lax.ppermute(values, 'gx', [(i, (i + step_x) % count_x) for i in range(co...]
    slice x4, local copies, waits for them, and re-layouts: 4.31 us -> 2.43 us  [the longest x2 2.2 us: substep(): from_left = exchange(merged[:, :, last_y], 0, 1)[:, :, None]]
    sub x2 -> x0, other arithmetic: 1.25 us -> none  [per_device(): state_now = state_now - visc_coef * assemble(stiff) * inv_mass]
  transfers between devices with their start and end apart: 16 -> 16, of which waited for: 7 -> 10; matrix products, arithmetic and copies ran while one was open for 6% -> 3% of each run, Pallas kernels for 0% -> 0%
where the time goes in v8:
time: 99.5 us; the launch traced here: 98.4 us
  starting transfers between devices  22.7 us (23%)
  waiting for transfers between devices  17 us (17%)
  local copies, waits for them, and re-layouts  13.9 us (14%)
  blocking collectives  13.3 us (13%)
  Pallas kernels  13.1 us (13%)
  other arithmetic  8.69 us (9%)
  matrix products  8.48 us (9%)
  between operations  1.17 us (1%)
    ppermute x8, starting transfers between devices, neighbour(): lax.ppermute(values, 'gy', [(j, (j + step_y) % count_y) for j in range(co...  20.6 us
    all_to_all x1, blocking collectives, per_device(): lax.all_to_all(payload, ('gx', 'gy'), split_axis=1, concat_axis=1, tiled=...  13.3 us
    pallas_call x2, Pallas kernels, onehot_gather(): pl.pallas_call(gather_kernel, grid=(count // tile,), in_specs=[pl.BlockSp...  13.1 us
    ppermute x8, waiting for transfers between devices, neighbour(): lax.ppermute(values, 'gy', [(j, (j + step_y) % count_y) for j in range(co...  9.82 us
    ppermute x8, waiting for transfers between devices, neighbour(): lax.ppermute(values, 'gx', [(i, (i + step_x) % count_x) for i in range(co...  7.18 us
    sub x2, other arithmetic, tracer_step(): tracers + diff_coef * (east + west + north + south - 4.0 * tracers)  5.22 us
    unnamed x34, local copies, waits for them, and re-layouts  4.27 us
    slice x2, local copies, waits for them, and re-layouts, tracer_step(): from_right = exchange(tracers[..., 0], 0, -1)[..., None]  2.67 us
  transfers between devices with their start and end apart: 16, of which 10 were waited for; matrix products, arithmetic and copies ran while one was open for 3% of the time, Pallas kernels for 0%

profile of v8, /device:TPU:0, one launch (start us, length us, event | category | flops | bytes accessed | tf_op | source)
XLA Modules:
  0.0 98.4 jit_solution(7822386873538552273)
XLA Ops:
  0.7 0.6 copy-done.13
  2.0 0.7 fusion.10
  2.7 0.7 convolution_bitcast_fusion.5
  3.5 0.7 fusion.2
  4.4 0.7 fusion.41
  5.2 0.7 fusion.1
  5.9 1.1 %slice_reduce_fusion.3 = (f32[160,16]{1,0:T(8,128)S(1)}, f32[160,16]{1,0:T(8,128)S(1)}) fusion(f32[160,16,128]{2,1,0:T(8,128)S(1)} %fusion.1), kind=kLoop, calls=%fused_computation.24 | loop fusion | bytes 40960 | tf_op jit(solution)/shard_map/slice | solution.py:87
  7.1 6.0 %collective-permute-start.1 = (f32[20,128]{1,0:T(8,128)S(1)}, f32[20,128]{1,0:T(8,128)S(1)}, u32[]{:S(2)}, u32[]{:S(2)}) collective-permute-start(f32[20,128]{1,0:T(8,128)S(1)} %reshape_squeeze.40), channel_id=1, source_target_pairs={{0,7},{1,0},{2,1},{3,2},{4,3},{5,4},{6,5},{7,6},{8,15},{9,8},{10,9... | collective-permute-start | bytes 30728 | tf_op jit(solution)/shard_map/ppermute | solution.py:25
  13.3 6.4 %collective-permute-done = f32[20,128]{1,0:T(8,128)S(1)} collective-permute-done((f32[20,128]{1,0:T(8,128)S(1)}, f32[20,128]{1,0:T(8,128)S(1)}, u32[]{:S(2)}, u32[]{:S(2)}) %collective-permute-start) | collective-permute-done | bytes 10272 | tf_op jit(solution)/shard_map/ppermute | solution.py:25
  19.9 0.8 select_add_fusion.1
  20.9 0.5 collective-permute-start.2
  21.4 1.5 %collective-permute-done.3 = f32[160,128]{1,0:T(8,128)S(1)} collective-permute-done((f32[160,128]{1,0:T(8,128)S(1)}, f32[160,128]{1,0:T(8,128)S(1)}, u32[]{:S(2)}, u32[]{:S(2)}) %collective-permute-start.3) | collective-permute-done | bytes 81952 | tf_op jit(solution)/shard_map/ppermute | solution.py:23
  23.0 2.7 %collective-permute-done.2 = f32[160,128]{1,0:T(8,128)S(1)} collective-permute-done((f32[160,128]{1,0:T(8,128)S(1)}, f32[160,128]{1,0:T(8,128)S(1)}, u32[]{:S(2)}, u32[]{:S(2)}) %collective-permute-start.2) | collective-permute-done | bytes 81952 | tf_op jit(solution)/shard_map/ppermute | solution.py:23
  25.7 0.8 fusion.5
  26.5 0.7 convolution_multiply_fusion.1
  27.2 0.7 fusion.6
  27.9 0.7 convolution_bitcast_fusion.2
  28.6 0.7 fusion.42
  29.3 0.7 fusion
  30.0 1.1 %slice_reduce_fusion.1 = (f32[160,16]{1,0:T(8,128)S(1)}, f32[160,16]{1,0:T(8,128)S(1)}) fusion(f32[160,16,128]{2,1,0:T(8,128)S(1)} %fusion), kind=kLoop, calls=%fused_computation.22 | loop fusion | bytes 40960 | tf_op jit(solution)/shard_map/slice | solution.py:87
  31.3 4.8 %collective-permute-start.5 = (f32[20,128]{1,0:T(8,128)S(1)}, f32[20,128]{1,0:T(8,128)S(1)}, u32[]{:S(2)}, u32[]{:S(2)}) collective-permute-start(f32[20,128]{1,0:T(8,128)S(1)} %reshape_squeeze.42), channel_id=1, source_target_pairs={{0,7},{1,0},{2,1},{3,2},{4,3},{5,4},{6,5},{7,6},{8,15},{9,8},{10,9... | collective-permute-start | bytes 30728 | tf_op jit(solution)/shard_map/ppermute | solution.py:25
  36.1 1.5 %collective-permute-done.4 = f32[20,128]{1,0:T(8,128)S(1)} collective-permute-done((f32[20,128]{1,0:T(8,128)S(1)}, f32[20,128]{1,0:T(8,128)S(1)}, u32[]{:S(2)}, u32[]{:S(2)}) %collective-permute-start.4) | collective-permute-done | bytes 10272 | tf_op jit(solution)/shard_map/ppermute | solution.py:25
  37.8 0.8 select_add_fusion
  38.9 0.5 collective-permute-start.6
  39.4 0.6 copy.39
  40.1 1.3 %collective-permute-done.7 = f32[160,128]{1,0:T(8,128)S(1)} collective-permute-done((f32[160,128]{1,0:T(8,128)S(1)}, f32[160,128]{1,0:T(8,128)S(1)}, u32[]{:S(2)}, u32[]{:S(2)}) %collective-permute-start.7) | collective-permute-done | bytes 81952 | tf_op jit(solution)/shard_map/ppermute | solution.py:23
  41.4 1.6 %collective-permute-done.6 = f32[160,128]{1,0:T(8,128)S(1)} collective-permute-done((f32[160,128]{1,0:T(8,128)S(1)}, f32[160,128]{1,0:T(8,128)S(1)}, u32[]{:S(2)}, u32[]{:S(2)}) %collective-permute-start.6) | collective-permute-done | bytes 81952 | tf_op jit(solution)/shard_map/ppermute | solution.py:23
  43.0 0.8 fusion.9
  43.9 1.0 %copy-done.3 = f32[160,16,128]{2,1,0:T(8,128)} copy-done((f32[160,16,128]{2,1,0:T(8,128)}, f32[160,16,128]{2,1,0:T(8,128)S(1)}, u32[]{:S(2)}) %copy-start.3) | copy-done | bytes 1310744
  44.9 0.6 fusion.13.table_ref
  45.5 6.2 %shard_map.248 = f32[4,8192]{1,0:T(4,128)} custom-call(s32[1,8192]{1,0:T(1,128)} %bitcast.136, f32[4,16,128]{2,1,0:T(8,128)} %fusion.13.table_ref), custom_call_target="tpu_custom_call" | custom-call | tf_op jit(solution)/shard_map/pallas_call | solution.py:174
  51.7 0.9 broadcast_multiply_fusion
  52.6 13.3 %all_to_all.5 = f32[4,32,256]{2,0,1:T(4,128)S(1)} all-to-all(f32[4,32,256]{2,0,1:T(4,128)S(1)} %broadcast_multiply_fusion), channel_id=1, replica_groups=mesh['gx'=4,'gy'=8] {'gx','gy'}, dimensions={1} | all-to-all | bytes 262144 | tf_op jit(solution)/shard_map/all_to_all | solution.py:213
  66.0 0.7 reshape_reshape.3.table_ref
  66.7 6.9 %shard_map.249 = f32[4,8192]{1,0:T(4,128)} custom-call(s32[1,8192]{1,0:T(1,128)} %bitcast.145, f32[4,64,128]{2,1,0:T(8,128)} %reshape_reshape.3.table_ref), custom_call_target="tpu_custom_call" | custom-call | tf_op jit(solution)/shard_map/pallas_call | solution.py:174
  73.5 0.9 copy.40
  74.7 1.2 %fusion.40 = (f32[2,40,16,127]{3,2,1,0:T(8,128)}, f32[2,40,16,127]{3,2,1,0:T(8,128)}) fusion(f32[2,40,16,128]{3,2,1,0:T(8,128)S(1)} %get-tuple-element.83), kind=kLoop, calls=%fused_computation.88 | loop fusion | bytes 2600960 | tf_op jit(solution)/shard_map/slice | solution.py:40
  75.9 1.3 %slice_reduce_fusion.7 = (f32[2,40,16]{2,1,0:T(8,128)S(1)}, f32[2,40,16]{2,1,0:T(8,128)S(1)}, f32[2,40,16,1]{3,2,1,0:T(8,128)}, f32[2,40,16,1]{3,2,1,0:T(8,128)}) fusion(f32[2,40,16,128]{3,2,1,0:T(8,128)S(1)} %get-tuple-element.83), kind=kLoop, calls=%fused_computation.80 | loop fusion | bytes 30720 | tf_op jit(solution)/shard_map/slice | solution.py:105
  77.9 1.3 %collective-permute-start.11 = (f32[10,128]{1,0:T(8,128)S(1)}, f32[10,128]{1,0:T(8,128)S(1)}, u32[]{:S(2)}, u32[]{:S(2)}) collective-permute-start(f32[10,128]{1,0:T(8,128)S(1)} %reshape_squeeze.47), channel_id=1, source_target_pairs={{0,1},{1,2},{2,3},{3,4},{4,5},{5,6},{6,7},{7,0},{8,9},{9,10},{10,1... | collective-permute-start | bytes 15368 | tf_op jit(solution)/shard_map/ppermute | solution.py:25
  79.2 3.5 %collective-permute-start.10 = (f32[10,128]{1,0:T(8,128)S(1)}, f32[10,128]{1,0:T(8,128)S(1)}, u32[]{:S(2)}, u32[]{:S(2)}) collective-permute-start(f32[10,128]{1,0:T(8,128)S(1)} %reshape_squeeze.46), channel_id=1, source_target_pairs={{0,7},{1,0},{2,1},{3,2},{4,3},{5,4},{6,5},{7,6},{8,15},{9,8},{10,9... | collective-permute-start | bytes 15368 | tf_op jit(solution)/shard_map/ppermute | solution.py:25
  82.7 1.3 %collective-permute-done.10 = f32[10,128]{1,0:T(8,128)S(1)} collective-permute-done((f32[10,128]{1,0:T(8,128)S(1)}, f32[10,128]{1,0:T(8,128)S(1)}, u32[]{:S(2)}, u32[]{:S(2)}) %collective-permute-start.10) | collective-permute-done | bytes 5152 | tf_op jit(solution)/shard_map/ppermute | solution.py:25
  84.4 2.3 %multiply_subtract_fusion.1 = f32[2,40,16,128]{3,2,1,0:T(8,128)S(1)} fusion(f32[2,40,16,128]{3,2,1,0:T(8,128)S(1)} %get-tuple-element.83, f32[2,40,16,127]{3,2,1,0:T(8,128)} %get-tuple-element.81, f32[2,40,16,1]{3,2,1,0:T(8,128)} %get-tuple-element.73, f32[2,40,16,1]{3,2,1,0:T(8,128)} %get-tuple-element.72, f32[2,40,16,127]{3,2,1,0:T(8,128)} %get-tuple-element.80, ...), kind=kLoop, calls=%fused_computation.36 | loop fusion | flops 3440640 | bytes 4679968 | tf_op jit(solution)/shard_map/sub | solution.py:109
  86.9 1.3 %slice_reduce_fusion.5 = (f32[2,40,16]{2,1,0:T(8,128)S(1)}, f32[2,40,16]{2,1,0:T(8,128)S(1)}, f32[2,40,16,1]{3,2,1,0:T(8,128)}, f32[2,40,16,1]{3,2,1,0:T(8,128)}) fusion(f32[2,40,16,128]{3,2,1,0:T(8,128)S(1)} %multiply_subtract_fusion.1), kind=kLoop, calls=%fused_computation.78 | loop fusion | bytes 30720 | tf_op jit(solution)/shard_map/slice | solution.py:105
  88.2 0.4 collective-permute-start.12
  88.9 0.8 collective-permute-start.15
  89.7 4.1 %collective-permute-start.14 = (f32[10,128]{1,0:T(8,128)S(1)}, f32[10,128]{1,0:T(8,128)S(1)}, u32[]{:S(2)}, u32[]{:S(2)}) collective-permute-start(f32[10,128]{1,0:T(8,128)S(1)} %reshape_squeeze.50), channel_id=1, source_target_pairs={{0,7},{1,0},{2,1},{3,2},{4,3},{5,4},{6,5},{7,6},{8,15},{9,8},{10,9... | collective-permute-start | bytes 15368 | tf_op jit(solution)/shard_map/ppermute | solution.py:25
  93.8 1.1 %fusion.37 = (f32[2,40,16,127]{3,2,1,0:T(8,128)S(1)}, f32[2,40,16,127]{3,2,1,0:T(8,128)}) fusion(f32[2,40,16,128]{3,2,1,0:T(8,128)S(1)} %multiply_subtract_fusion.1), kind=kLoop, calls=%fused_computation.85 | loop fusion | bytes 2600960 | tf_op jit(solution)/shard_map/slice | solution.py:40
  95.5 2.9 %multiply_subtract_fusion = f32[2,40,16,128]{3,2,1,0:T(8,128)} fusion(f32[2,40,16,128]{3,2,1,0:T(8,128)S(1)} %multiply_subtract_fusion.1, f32[2,40,16,127]{3,2,1,0:T(8,128)} %get-tuple-element.71, f32[2,40,16,1]{3,2,1,0:T(8,128)} %get-tuple-element.65, f32[2,40,16,1]{3,2,1,0:T(8,128)} %get-tuple-element.64, f32[2,40,16,127]{3,2,1,0:T(8,128)S(1)} %get-tuple-element.70, ...), kind=kLoop, calls=%fused_computation.35 | loop fusion | flops 3440640 | bytes 4679968 | tf_op jit(solution)/shard_map/sub | solution.py:109
  (78 shorter events, 4.6 us)
Async XLA Ops:
  0.6 0.7 copy-start.13
  0.6 0.7 copy-start.15
  0.7 0.9 copy-start.7
  0.7 1.3 %copy-start.1 = (f32[4,40,16,128]{3,2,1,0:T(8,128)S(1)}, f32[4,40,16,128]{3,2,1,0:T(8,128)}, u32[]{:S(2)}) copy-start(f32[4,40,16,128]{3,2,1,0:T(8,128)} %param.33) | copy-start | bytes 3932164
  0.7 0.8 copy-start.12
  2.7 0.8 copy-start.5
  3.5 0.8 copy-start.6
  4.4 0.8 copy-start.4
  7.1 12.7 %collective-permute-start.1 = (f32[20,128]{1,0:T(8,128)S(1)}, f32[20,128]{1,0:T(8,128)S(1)}, u32[]{:S(2)}, u32[]{:S(2)}) collective-permute-start(f32[20,128]{1,0:T(8,128)S(1)} %reshape_squeeze.40), channel_id=1, source_target_pairs={{0,7},{1,0},{2,1},{3,2},{4,3},{5,4},{6,5},{7,6},{8,15},{9,8},{10,9... | collective-permute-start | bytes 30728 | tf_op jit(solution)/shard_map/ppermute | solution.py:25
  13.2 6.4 %collective-permute-start = (f32[20,128]{1,0:T(8,128)S(1)}, f32[20,128]{1,0:T(8,128)S(1)}, u32[]{:S(2)}, u32[]{:S(2)}) collective-permute-start(f32[20,128]{1,0:T(8,128)S(1)} %reshape_squeeze.39), channel_id=1, source_target_pairs={{0,1},{1,2},{2,3},{3,4},{4,5},{5,6},{6,7},{7,0},{8,9},{9,10},{10,1... | collective-permute-start | bytes 30728 | tf_op jit(solution)/shard_map/ppermute | solution.py:25
  19.8 5.9 %copy-start.8 = (f32[16,16,1]{1,0,2:T(8,128)S(1)}, f32[16,16,1]{1,0,2:T(8,128)}, u32[]{:S(2)}) copy-start(f32[16,16,1]{1,0,2:T(8,128)} %constant.162) | copy-start | bytes 3076
  19.8 5.8 %copy-start.9 = (f32[16,128]{1,0:T(8,128)S(1)}, f32[16,128]{1,0:T(8,128)}, u32[]{:S(2)}) copy-start(f32[16,128]{1,0:T(8,128)} %constant.157) | copy-start | bytes 24580
  20.8 2.1 %collective-permute-start.3 = (f32[160,128]{1,0:T(8,128)S(1)}, f32[160,128]{1,0:T(8,128)S(1)}, u32[]{:S(2)}, u32[]{:S(2)}) collective-permute-start(f32[160,128]{1,0:T(8,128)S(1)} %bitcast.139), channel_id=1, source_target_pairs={{0,24},{8,0},{16,8},{24,16},{1,25},{9,1},{17,9},{25,17},{2,26},{10... | collective-permute-start | bytes 245768 | tf_op jit(solution)/shard_map/ppermute | solution.py:23
  20.9 4.8 %collective-permute-start.2 = (f32[160,128]{1,0:T(8,128)S(1)}, f32[160,128]{1,0:T(8,128)S(1)}, u32[]{:S(2)}, u32[]{:S(2)}) collective-permute-start(f32[160,128]{1,0:T(8,128)S(1)} %bitcast.137), channel_id=1, source_target_pairs={{0,8},{8,16},{16,24},{24,0},{1,9},{9,17},{17,25},{25,1},{2,10},{10... | collective-permute-start | bytes 245768 | tf_op jit(solution)/shard_map/ppermute | solution.py:23
  31.2 6.4 %collective-permute-start.4 = (f32[20,128]{1,0:T(8,128)S(1)}, f32[20,128]{1,0:T(8,128)S(1)}, u32[]{:S(2)}, u32[]{:S(2)}) collective-permute-start(f32[20,128]{1,0:T(8,128)S(1)} %reshape_squeeze.41), channel_id=1, source_target_pairs={{0,1},{1,2},{2,3},{3,4},{4,5},{5,6},{6,7},{7,0},{8,9},{9,10},{10,1... | collective-permute-start | bytes 30728 | tf_op jit(solution)/shard_map/ppermute | solution.py:25
  31.3 6.4 %collective-permute-start.5 = (f32[20,128]{1,0:T(8,128)S(1)}, f32[20,128]{1,0:T(8,128)S(1)}, u32[]{:S(2)}, u32[]{:S(2)}) collective-permute-start(f32[20,128]{1,0:T(8,128)S(1)} %reshape_squeeze.42), channel_id=1, source_target_pairs={{0,7},{1,0},{2,1},{3,2},{4,3},{5,4},{6,5},{7,6},{8,15},{9,8},{10,9... | collective-permute-start | bytes 30728 | tf_op jit(solution)/shard_map/ppermute | solution.py:25
  37.8 1.6 %copy-start.14 = (s32[1,32]{1,0:T(1,128)S(1)}, s32[1,32]{1,0:T(1,128)}, u32[]{:S(2)}) copy-start(s32[1,32]{1,0:T(1,128)} %param.36) | copy-start | bytes 388
  37.8 1.6 %copy-start.10 = (s32[1,32,256]{2,1,0:T(8,128)S(1)}, s32[1,32,256]{2,1,0:T(8,128)}, u32[]{:S(2)}) copy-start(s32[1,32,256]{2,1,0:T(8,128)} %param.35) | copy-start | bytes 98308
  38.8 2.6 %collective-permute-start.7 = (f32[160,128]{1,0:T(8,128)S(1)}, f32[160,128]{1,0:T(8,128)S(1)}, u32[]{:S(2)}, u32[]{:S(2)}) collective-permute-start(f32[160,128]{1,0:T(8,128)S(1)} %bitcast.140), channel_id=1, source_target_pairs={{0,24},{8,0},{16,8},{24,16},{1,25},{9,1},{17,9},{25,17},{2,26},{10... | collective-permute-start | bytes 245768 | tf_op jit(solution)/shard_map/ppermute | solution.py:23
  38.9 4.1 %collective-permute-start.6 = (f32[160,128]{1,0:T(8,128)S(1)}, f32[160,128]{1,0:T(8,128)S(1)}, u32[]{:S(2)}, u32[]{:S(2)}) collective-permute-start(f32[160,128]{1,0:T(8,128)S(1)} %bitcast.138), channel_id=1, source_target_pairs={{0,8},{8,16},{16,24},{24,0},{1,9},{9,17},{17,25},{25,1},{2,10},{10... | collective-permute-start | bytes 245768 | tf_op jit(solution)/shard_map/ppermute | solution.py:23
  43.8 1.1 %copy-start.3 = (f32[160,16,128]{2,1,0:T(8,128)}, f32[160,16,128]{2,1,0:T(8,128)S(1)}, u32[]{:S(2)}) copy-start(f32[160,16,128]{2,1,0:T(8,128)S(1)} %fusion.9) | copy-start | bytes 3932164
  43.8 30.6 %copy-start.11 = (f32[4,16,128]{2,1,0:T(8,128)S(1)}, f32[4,16,128]{2,1,0:T(8,128)}, u32[]{:S(2)}) copy-start(f32[4,16,128]{2,1,0:T(8,128)} %param.40) | copy-start | bytes 98308
  43.8 30.6 %copy-start = (f32[2,40,16,128]{3,2,1,0:T(8,128)S(1)}, f32[2,40,16,128]{3,2,1,0:T(8,128)}, u32[]{:S(2)}) copy-start(f32[2,40,16,128]{3,2,1,0:T(8,128)} %param.37) | copy-start | bytes 1966084
  43.8 30.6 %copy-start.2 = (f32[2,40,16,128]{3,2,1,0:T(8,128)S(1)}, f32[2,40,16,128]{3,2,1,0:T(8,128)}, u32[]{:S(2)}) copy-start(f32[2,40,16,128]{3,2,1,0:T(8,128)} %param.38) | copy-start | bytes 1966084
  77.3 7.1 %collective-permute-start.8 = (f32[80,128]{1,0:T(8,128)S(1)}, f32[80,128]{1,0:T(8,128)S(1)}, u32[]{:S(2)}, u32[]{:S(2)}) collective-permute-start(f32[80,128]{1,0:T(8,128)S(1)} %bitcast.133), channel_id=1, source_target_pairs={{0,24},{8,0},{16,8},{24,16},{1,25},{9,1},{17,9},{25,17},{2,26},{10... | collective-permute-start | bytes 122888 | tf_op jit(solution)/shard_map/ppermute | solution.py:23
  77.6 6.8 %collective-permute-start.9 = (f32[80,128]{1,0:T(8,128)S(1)}, f32[80,128]{1,0:T(8,128)S(1)}, u32[]{:S(2)}, u32[]{:S(2)}) collective-permute-start(f32[80,128]{1,0:T(8,128)S(1)} %bitcast.132), channel_id=1, source_target_pairs={{0,8},{8,16},{16,24},{24,0},{1,9},{9,17},{17,25},{25,1},{2,10},{10... | collective-permute-start | bytes 122888 | tf_op jit(solution)/shard_map/ppermute | solution.py:23
  77.9 6.4 %collective-permute-start.11 = (f32[10,128]{1,0:T(8,128)S(1)}, f32[10,128]{1,0:T(8,128)S(1)}, u32[]{:S(2)}, u32[]{:S(2)}) collective-permute-start(f32[10,128]{1,0:T(8,128)S(1)} %reshape_squeeze.47), channel_id=1, source_target_pairs={{0,1},{1,2},{2,3},{3,4},{4,5},{5,6},{6,7},{7,0},{8,9},{9,10},{10,1... | collective-permute-start | bytes 15368 | tf_op jit(solution)/shard_map/ppermute | solution.py:25
  79.2 4.9 %collective-permute-start.10 = (f32[10,128]{1,0:T(8,128)S(1)}, f32[10,128]{1,0:T(8,128)S(1)}, u32[]{:S(2)}, u32[]{:S(2)}) collective-permute-start(f32[10,128]{1,0:T(8,128)S(1)} %reshape_squeeze.46), channel_id=1, source_target_pairs={{0,7},{1,0},{2,1},{3,2},{4,3},{5,4},{6,5},{7,6},{8,15},{9,8},{10,9... | collective-permute-start | bytes 15368 | tf_op jit(solution)/shard_map/ppermute | solution.py:25
  88.2 7.2 %collective-permute-start.12 = (f32[80,128]{1,0:T(8,128)S(1)}, f32[80,128]{1,0:T(8,128)S(1)}, u32[]{:S(2)}, u32[]{:S(2)}) collective-permute-start(f32[80,128]{1,0:T(8,128)S(1)} %bitcast.135), channel_id=1, source_target_pairs={{0,24},{8,0},{16,8},{24,16},{1,25},{9,1},{17,9},{25,17},{2,26},{10... | collective-permute-start | bytes 122888 | tf_op jit(solution)/shard_map/ppermute | solution.py:23
  88.7 6.8 %collective-permute-start.13 = (f32[80,128]{1,0:T(8,128)S(1)}, f32[80,128]{1,0:T(8,128)S(1)}, u32[]{:S(2)}, u32[]{:S(2)}) collective-permute-start(f32[80,128]{1,0:T(8,128)S(1)} %bitcast.134), channel_id=1, source_target_pairs={{0,8},{8,16},{16,24},{24,0},{1,9},{9,17},{17,25},{25,1},{2,10},{10... | collective-permute-start | bytes 122888 | tf_op jit(solution)/shard_map/ppermute | solution.py:23
  88.9 6.5 %collective-permute-start.15 = (f32[10,128]{1,0:T(8,128)S(1)}, f32[10,128]{1,0:T(8,128)S(1)}, u32[]{:S(2)}, u32[]{:S(2)}) collective-permute-start(f32[10,128]{1,0:T(8,128)S(1)} %reshape_squeeze.51), channel_id=1, source_target_pairs={{0,1},{1,2},{2,3},{3,4},{4,5},{5,6},{6,7},{7,0},{8,9},{9,10},{10,1... | collective-permute-start | bytes 15368 | tf_op jit(solution)/shard_map/ppermute | solution.py:25
  89.7 5.4 %collective-permute-start.14 = (f32[10,128]{1,0:T(8,128)S(1)}, f32[10,128]{1,0:T(8,128)S(1)}, u32[]{:S(2)}, u32[]{:S(2)}) collective-permute-start(f32[10,128]{1,0:T(8,128)S(1)} %reshape_squeeze.50), channel_id=1, source_target_pairs={{0,7},{1,0},{2,1},{3,2},{4,3},{5,4},{6,5},{7,6},{8,15},{9,8},{10,9... | collective-permute-start | bytes 15368 | tf_op jit(solution)/shard_map/ppermute | solution.py:25

commit v9 on v8

--- a/solution.py
+++ b/solution.py
@@ -210,8 +210,10 @@
     count_row = send_counts[0]
     live_slots = (jnp.arange(slot_cap)[None, :] < count_row[:, None]).astype(jnp.float32)
     payload = payload * live_slots[None]
-    received = lax.all_to_all(payload, ("gx", "gy"), split_axis=1, concat_axis=1, tiled=True)
-    received = received.reshape(fields, -1)
+    staged = payload.reshape(fields, lax.axis_size("gx"), lax.axis_size("gy"), slot_cap)
+    staged = lax.all_to_all(staged, "gy", split_axis=2, concat_axis=2, tiled=True)
+    staged = lax.all_to_all(staged, "gx", split_axis=1, concat_axis=1, tiled=True)
+    received = staged.reshape(fields, -1)
     source_count, ocean_x, ocean_y = remap_slots.shape
     gathered = onehot_gather(received, remap_slots).reshape(fields, source_count, ocean_x, ocean_y)
     ocean_flux = jnp.sum(remap_weights[None] * gathered, axis=1)

time: 99.5 us -> 106 us (1.065)
  blocking collectives: 13.3 us -> 20 us
  local copies, waits for them, and re-layouts: 13.9 us -> 15.7 us
  waiting for transfers between devices: 17 us -> 15.9 us
    all_to_all x1 -> x2, blocking collectives: 13.3 us -> 20 us  [the longest x1 13 us: per_device(): lax.all_to_all(staged, 'gy', split_axis=2, concat_axis=2, tiled=True)]
    unnamed x34 -> x36, local copies, waits for them, and re-layouts: 4.27 us -> 5.85 us
    ppermute x8, waiting for transfers between devices: 9.82 us -> 8.49 us  [neighbour(): lax.ppermute(values, 'gy', [(j, (j + step_y) % count_y) for j in range(co...]
  transfers between devices with their start and end apart: 16 -> 16, of which waited for: 10 -> 10; matrix products, arithmetic and copies ran while one was open for 3% -> 4% of each run, Pallas kernels for 0% -> 0%
where the time goes in v9:
time: 106 us; the launch traced here: 105 us
  starting transfers between devices  22.7 us (21%)
  blocking collectives  20 us (19%)
  waiting for transfers between devices  15.9 us (15%)
  local copies, waits for them, and re-layouts  15.7 us (15%)
  Pallas kernels  13.1 us (12%)
  other arithmetic  8.48 us (8%)
  matrix products  8.47 us (8%)
  between operations  1.17 us (1%)
    ppermute x8, starting transfers between devices, neighbour(): lax.ppermute(values, 'gy', [(j, (j + step_y) % count_y) for j in range(co...  20.6 us
    pallas_call x2, Pallas kernels, onehot_gather(): pl.pallas_call(gather_kernel, grid=(count // tile,), in_specs=[pl.BlockSp...  13.1 us
    all_to_all x1, blocking collectives, per_device(): lax.all_to_all(staged, 'gy', split_axis=2, concat_axis=2, tiled=True)  13 us
    ppermute x8, waiting for transfers between devices, neighbour(): lax.ppermute(values, 'gy', [(j, (j + step_y) % count_y) for j in range(co...  8.49 us
    ppermute x8, waiting for transfers between devices, neighbour(): lax.ppermute(values, 'gx', [(i, (i + step_x) % count_x) for i in range(co...  7.36 us
    all_to_all x1, blocking collectives, per_device(): lax.all_to_all(staged, 'gx', split_axis=1, concat_axis=1, tiled=True)  7.02 us
    unnamed x36, local copies, waits for them, and re-layouts  5.85 us
    sub x2, other arithmetic, tracer_step(): tracers + diff_coef * (east + west + north + south - 4.0 * tracers)  5.22 us
  transfers between devices with their start and end apart: 16, of which 10 were waited for; matrix products, arithmetic and copies ran while one was open for 4% of the time, Pallas kernels for 0%

profile of v9, /device:TPU:0, one launch (start us, length us, event | category | flops | bytes accessed | tf_op | source)
XLA Modules:
  0.0 105.5 jit_solution(8722558426409855563)
XLA Ops:
  0.7 0.6 copy-done.13
  2.0 0.7 fusion.10
  2.7 0.7 convolution_bitcast_fusion.5
  3.5 0.7 fusion.2
  4.4 0.7 fusion.41
  5.2 0.7 fusion.1
  5.9 1.1 %slice_reduce_fusion.3 = (f32[160,16]{1,0:T(8,128)S(1)}, f32[160,16]{1,0:T(8,128)S(1)}) fusion(f32[160,16,128]{2,1,0:T(8,128)S(1)} %fusion.1), kind=kLoop, calls=%fused_computation.24 | loop fusion | bytes 40960 | tf_op jit(solution)/shard_map/slice | solution.py:87
  7.1 6.0 %collective-permute-start.1 = (f32[20,128]{1,0:T(8,128)S(1)}, f32[20,128]{1,0:T(8,128)S(1)}, u32[]{:S(2)}, u32[]{:S(2)}) collective-permute-start(f32[20,128]{1,0:T(8,128)S(1)} %reshape_squeeze.40), channel_id=1, source_target_pairs={{0,7},{1,0},{2,1},{3,2},{4,3},{5,4},{6,5},{7,6},{8,15},{9,8},{10,9... | collective-permute-start | bytes 30728 | tf_op jit(solution)/shard_map/ppermute | solution.py:25
  13.3 6.4 %collective-permute-done = f32[20,128]{1,0:T(8,128)S(1)} collective-permute-done((f32[20,128]{1,0:T(8,128)S(1)}, f32[20,128]{1,0:T(8,128)S(1)}, u32[]{:S(2)}, u32[]{:S(2)}) %collective-permute-start) | collective-permute-done | bytes 10272 | tf_op jit(solution)/shard_map/ppermute | solution.py:25
  19.9 0.8 select_add_fusion.1
  20.9 0.5 collective-permute-start.2
  21.4 1.5 %collective-permute-done.3 = f32[160,128]{1,0:T(8,128)S(1)} collective-permute-done((f32[160,128]{1,0:T(8,128)S(1)}, f32[160,128]{1,0:T(8,128)S(1)}, u32[]{:S(2)}, u32[]{:S(2)}) %collective-permute-start.3) | collective-permute-done | bytes 81952 | tf_op jit(solution)/shard_map/ppermute | solution.py:23
  23.0 2.7 %collective-permute-done.2 = f32[160,128]{1,0:T(8,128)S(1)} collective-permute-done((f32[160,128]{1,0:T(8,128)S(1)}, f32[160,128]{1,0:T(8,128)S(1)}, u32[]{:S(2)}, u32[]{:S(2)}) %collective-permute-start.2) | collective-permute-done | bytes 81952 | tf_op jit(solution)/shard_map/ppermute | solution.py:23
  25.7 0.8 fusion.5
  26.5 0.7 convolution_multiply_fusion.1
  27.2 0.7 fusion.6
  27.9 0.7 convolution_bitcast_fusion.2
  28.6 0.7 fusion.42
  29.3 0.7 fusion
  30.0 1.1 %slice_reduce_fusion.1 = (f32[160,16]{1,0:T(8,128)S(1)}, f32[160,16]{1,0:T(8,128)S(1)}) fusion(f32[160,16,128]{2,1,0:T(8,128)S(1)} %fusion), kind=kLoop, calls=%fused_computation.22 | loop fusion | bytes 40960 | tf_op jit(solution)/shard_map/slice | solution.py:87
  31.3 4.8 %collective-permute-start.5 = (f32[20,128]{1,0:T(8,128)S(1)}, f32[20,128]{1,0:T(8,128)S(1)}, u32[]{:S(2)}, u32[]{:S(2)}) collective-permute-start(f32[20,128]{1,0:T(8,128)S(1)} %reshape_squeeze.42), channel_id=1, source_target_pairs={{0,7},{1,0},{2,1},{3,2},{4,3},{5,4},{6,5},{7,6},{8,15},{9,8},{10,9... | collective-permute-start | bytes 30728 | tf_op jit(solution)/shard_map/ppermute | solution.py:25
  36.1 0.5 broadcast.227
  36.6 0.7 reduce.27
  37.8 0.8 select_add_fusion
  38.9 0.5 collective-permute-start.6
  39.5 0.6 copy.41
  40.1 1.2 %collective-permute-done.7 = f32[160,128]{1,0:T(8,128)S(1)} collective-permute-done((f32[160,128]{1,0:T(8,128)S(1)}, f32[160,128]{1,0:T(8,128)S(1)}, u32[]{:S(2)}, u32[]{:S(2)}) %collective-permute-start.7) | collective-permute-done | bytes 81952 | tf_op jit(solution)/shard_map/ppermute | solution.py:23
  41.3 1.8 %collective-permute-done.6 = f32[160,128]{1,0:T(8,128)S(1)} collective-permute-done((f32[160,128]{1,0:T(8,128)S(1)}, f32[160,128]{1,0:T(8,128)S(1)}, u32[]{:S(2)}, u32[]{:S(2)}) %collective-permute-start.6) | collective-permute-done | bytes 81952 | tf_op jit(solution)/shard_map/ppermute | solution.py:23
  43.2 0.8 fusion.9
  44.0 1.0 copy-done.3
  45.1 0.6 fusion.13.table_ref
  45.7 6.2 %shard_map.248 = f32[4,8192]{1,0:T(4,128)} custom-call(s32[1,8192]{1,0:T(1,128)} %bitcast.142, f32[4,16,128]{2,1,0:T(8,128)} %fusion.13.table_ref), custom_call_target="tpu_custom_call" | custom-call | tf_op jit(solution)/shard_map/pallas_call | solution.py:174
  51.9 1.0 copy.46
  53.0 13.0 %all_to_all.10 = f32[4,4,8,256]{3,1,0,2:T(4,128)S(1)} all-to-all(f32[4,4,8,256]{3,1,0,2:T(4,128)S(1)} %copy_multiply_fusion), channel_id=1, replica_groups=mesh['gx'=4,'gy'=8] {'gy'}, dimensions={2} | all-to-all | bytes 262144 | tf_op jit(solution)/shard_map/all_to_all | solution.py:214
  66.1 7.0 %all_to_all.11 = f32[4,4,8,256]{3,2,0,1:T(8,128)S(1)} all-to-all(f32[4,4,8,256]{3,2,0,1:T(8,128)S(1)} %copy.34), channel_id=1, replica_groups=mesh['gx'=4,'gy'=8] {'gx'}, dimensions={1} | all-to-all | bytes 262144 | tf_op jit(solution)/shard_map/all_to_all | solution.py:215
  73.1 0.7 reshape_reshape.3.table_ref
  73.8 6.9 %shard_map.249 = f32[4,8192]{1,0:T(4,128)} custom-call(s32[1,8192]{1,0:T(1,128)} %bitcast.151, f32[4,64,128]{2,1,0:T(8,128)} %reshape_reshape.3.table_ref), custom_call_target="tpu_custom_call" | custom-call | tf_op jit(solution)/shard_map/pallas_call | solution.py:174
  80.6 0.9 copy.43
  81.8 1.2 %fusion.40 = (f32[2,40,16,127]{3,2,1,0:T(8,128)}, f32[2,40,16,127]{3,2,1,0:T(8,128)}) fusion(f32[2,40,16,128]{3,2,1,0:T(8,128)S(1)} %get-tuple-element.83), kind=kLoop, calls=%fused_computation.89 | loop fusion | bytes 2600960 | tf_op jit(solution)/shard_map/slice | solution.py:40
  83.0 1.3 %slice_reduce_fusion.7 = (f32[2,40,16]{2,1,0:T(8,128)S(1)}, f32[2,40,16]{2,1,0:T(8,128)S(1)}, f32[2,40,16,1]{3,2,1,0:T(8,128)}, f32[2,40,16,1]{3,2,1,0:T(8,128)}) fusion(f32[2,40,16,128]{3,2,1,0:T(8,128)S(1)} %get-tuple-element.83), kind=kLoop, calls=%fused_computation.81 | loop fusion | bytes 30720 | tf_op jit(solution)/shard_map/slice | solution.py:105
  84.4 0.5 collective-permute-start.9
  85.3 4.5 %collective-permute-start.10 = (f32[10,128]{1,0:T(8,128)S(1)}, f32[10,128]{1,0:T(8,128)S(1)}, u32[]{:S(2)}, u32[]{:S(2)}) collective-permute-start(f32[10,128]{1,0:T(8,128)S(1)} %reshape_squeeze.46), channel_id=1, source_target_pairs={{0,7},{1,0},{2,1},{3,2},{4,3},{5,4},{6,5},{7,6},{8,15},{9,8},{10,9... | collective-permute-start | bytes 15368 | tf_op jit(solution)/shard_map/ppermute | solution.py:25
  89.8 1.3 %collective-permute-done.10 = f32[10,128]{1,0:T(8,128)S(1)} collective-permute-done((f32[10,128]{1,0:T(8,128)S(1)}, f32[10,128]{1,0:T(8,128)S(1)}, u32[]{:S(2)}, u32[]{:S(2)}) %collective-permute-start.10) | collective-permute-done | bytes 5152 | tf_op jit(solution)/shard_map/ppermute | solution.py:25
  91.5 2.3 %multiply_subtract_fusion.1 = f32[2,40,16,128]{3,2,1,0:T(8,128)S(1)} fusion(f32[2,40,16,128]{3,2,1,0:T(8,128)S(1)} %get-tuple-element.83, f32[2,40,16,127]{3,2,1,0:T(8,128)} %get-tuple-element.81, f32[2,40,16,1]{3,2,1,0:T(8,128)} %get-tuple-element.73, f32[2,40,16,1]{3,2,1,0:T(8,128)} %get-tuple-element.72, f32[2,40,16,127]{3,2,1,0:T(8,128)} %get-tuple-element.80, ...), kind=kLoop, calls=%fused_computation.36 | loop fusion | flops 3440640 | bytes 4679968 | tf_op jit(solution)/shard_map/sub | solution.py:109
  94.0 1.3 %slice_reduce_fusion.5 = (f32[2,40,16]{2,1,0:T(8,128)S(1)}, f32[2,40,16]{2,1,0:T(8,128)S(1)}, f32[2,40,16,1]{3,2,1,0:T(8,128)}, f32[2,40,16,1]{3,2,1,0:T(8,128)}) fusion(f32[2,40,16,128]{3,2,1,0:T(8,128)S(1)} %multiply_subtract_fusion.1), kind=kLoop, calls=%fused_computation.79 | loop fusion | bytes 30720 | tf_op jit(solution)/shard_map/slice | solution.py:105
  96.0 4.9 %collective-permute-start.14 = (f32[10,128]{1,0:T(8,128)S(1)}, f32[10,128]{1,0:T(8,128)S(1)}, u32[]{:S(2)}, u32[]{:S(2)}) collective-permute-start(f32[10,128]{1,0:T(8,128)S(1)} %reshape_squeeze.50), channel_id=1, source_target_pairs={{0,7},{1,0},{2,1},{3,2},{4,3},{5,4},{6,5},{7,6},{8,15},{9,8},{10,9... | collective-permute-start | bytes 15368 | tf_op jit(solution)/shard_map/ppermute | solution.py:25
  100.9 1.0 fusion.37
  102.6 2.9 %multiply_subtract_fusion = f32[2,40,16,128]{3,2,1,0:T(8,128)} fusion(f32[2,40,16,128]{3,2,1,0:T(8,128)S(1)} %multiply_subtract_fusion.1, f32[2,40,16,127]{3,2,1,0:T(8,128)} %get-tuple-element.71, f32[2,40,16,1]{3,2,1,0:T(8,128)} %get-tuple-element.65, f32[2,40,16,1]{3,2,1,0:T(8,128)} %get-tuple-element.64, f32[2,40,16,127]{3,2,1,0:T(8,128)S(1)} %get-tuple-element.70, ...), kind=kLoop, calls=%fused_computation.35 | loop fusion | flops 3440640 | bytes 4679968 | tf_op jit(solution)/shard_map/sub | solution.py:109
  (85 shorter events, 5.3 us)
Async XLA Ops:
  0.6 0.7 copy-start.13
  0.6 0.7 copy-start.14
  0.7 0.9 copy-start.7
  0.7 1.3 %copy-start.1 = (f32[4,40,16,128]{3,2,1,0:T(8,128)S(1)}, f32[4,40,16,128]{3,2,1,0:T(8,128)}, u32[]{:S(2)}) copy-start(f32[4,40,16,128]{3,2,1,0:T(8,128)} %param.33) | copy-start | bytes 3932164
  0.7 0.8 copy-start.12
  2.7 0.8 copy-start.5
  3.5 0.8 copy-start.6
  4.4 0.8 copy-start.4
  7.1 12.7 %collective-permute-start.1 = (f32[20,128]{1,0:T(8,128)S(1)}, f32[20,128]{1,0:T(8,128)S(1)}, u32[]{:S(2)}, u32[]{:S(2)}) collective-permute-start(f32[20,128]{1,0:T(8,128)S(1)} %reshape_squeeze.40), channel_id=1, source_target_pairs={{0,7},{1,0},{2,1},{3,2},{4,3},{5,4},{6,5},{7,6},{8,15},{9,8},{10,9... | collective-permute-start | bytes 30728 | tf_op jit(solution)/shard_map/ppermute | solution.py:25
  13.2 6.4 %collective-permute-start = (f32[20,128]{1,0:T(8,128)S(1)}, f32[20,128]{1,0:T(8,128)S(1)}, u32[]{:S(2)}, u32[]{:S(2)}) collective-permute-start(f32[20,128]{1,0:T(8,128)S(1)} %reshape_squeeze.39), channel_id=1, source_target_pairs={{0,1},{1,2},{2,3},{3,4},{4,5},{5,6},{6,7},{7,0},{8,9},{9,10},{10,1... | collective-permute-start | bytes 30728 | tf_op jit(solution)/shard_map/ppermute | solution.py:25
  19.8 5.9 %copy-start.8 = (f32[16,16,1]{1,0,2:T(8,128)S(1)}, f32[16,16,1]{1,0,2:T(8,128)}, u32[]{:S(2)}) copy-start(f32[16,16,1]{1,0,2:T(8,128)} %constant.162) | copy-start | bytes 3076
  19.8 5.8 %copy-start.9 = (f32[16,128]{1,0:T(8,128)S(1)}, f32[16,128]{1,0:T(8,128)}, u32[]{:S(2)}) copy-start(f32[16,128]{1,0:T(8,128)} %constant.157) | copy-start | bytes 24580
  20.8 2.1 %collective-permute-start.3 = (f32[160,128]{1,0:T(8,128)S(1)}, f32[160,128]{1,0:T(8,128)S(1)}, u32[]{:S(2)}, u32[]{:S(2)}) collective-permute-start(f32[160,128]{1,0:T(8,128)S(1)} %bitcast.145), channel_id=1, source_target_pairs={{0,24},{8,0},{16,8},{24,16},{1,25},{9,1},{17,9},{25,17},{2,26},{10... | collective-permute-start | bytes 245768 | tf_op jit(solution)/shard_map/ppermute | solution.py:23
  20.9 4.8 %collective-permute-start.2 = (f32[160,128]{1,0:T(8,128)S(1)}, f32[160,128]{1,0:T(8,128)S(1)}, u32[]{:S(2)}, u32[]{:S(2)}) collective-permute-start(f32[160,128]{1,0:T(8,128)S(1)} %bitcast.143), channel_id=1, source_target_pairs={{0,8},{8,16},{16,24},{24,0},{1,9},{9,17},{17,25},{25,1},{2,10},{10... | collective-permute-start | bytes 245768 | tf_op jit(solution)/shard_map/ppermute | solution.py:23
  30.0 6.6 %copy-start.15 = (s32[1,32]{1,0:T(1,128)S(1)}, s32[1,32]{1,0:T(1,128)}, u32[]{:S(2)}) copy-start(s32[1,32]{1,0:T(1,128)} %param.36) | copy-start | bytes 388
  31.2 6.4 %collective-permute-start.4 = (f32[20,128]{1,0:T(8,128)S(1)}, f32[20,128]{1,0:T(8,128)S(1)}, u32[]{:S(2)}, u32[]{:S(2)}) collective-permute-start(f32[20,128]{1,0:T(8,128)S(1)} %reshape_squeeze.41), channel_id=1, source_target_pairs={{0,1},{1,2},{2,3},{3,4},{4,5},{5,6},{6,7},{7,0},{8,9},{9,10},{10,1... | collective-permute-start | bytes 30728 | tf_op jit(solution)/shard_map/ppermute | solution.py:25
  31.3 6.4 %collective-permute-start.5 = (f32[20,128]{1,0:T(8,128)S(1)}, f32[20,128]{1,0:T(8,128)S(1)}, u32[]{:S(2)}, u32[]{:S(2)}) collective-permute-start(f32[20,128]{1,0:T(8,128)S(1)} %reshape_squeeze.42), channel_id=1, source_target_pairs={{0,7},{1,0},{2,1},{3,2},{4,3},{5,4},{6,5},{7,6},{8,15},{9,8},{10,9... | collective-permute-start | bytes 30728 | tf_op jit(solution)/shard_map/ppermute | solution.py:25
  37.8 1.6 %copy-start.10 = (s32[1,32,256]{2,1,0:T(8,128)S(1)}, s32[1,32,256]{2,1,0:T(8,128)}, u32[]{:S(2)}) copy-start(s32[1,32,256]{2,1,0:T(8,128)} %param.35) | copy-start | bytes 98308
  38.8 2.5 %collective-permute-start.7 = (f32[160,128]{1,0:T(8,128)S(1)}, f32[160,128]{1,0:T(8,128)S(1)}, u32[]{:S(2)}, u32[]{:S(2)}) collective-permute-start(f32[160,128]{1,0:T(8,128)S(1)} %bitcast.146), channel_id=1, source_target_pairs={{0,24},{8,0},{16,8},{24,16},{1,25},{9,1},{17,9},{25,17},{2,26},{10... | collective-permute-start | bytes 245768 | tf_op jit(solution)/shard_map/ppermute | solution.py:23
  38.9 4.3 %collective-permute-start.6 = (f32[160,128]{1,0:T(8,128)S(1)}, f32[160,128]{1,0:T(8,128)S(1)}, u32[]{:S(2)}, u32[]{:S(2)}) collective-permute-start(f32[160,128]{1,0:T(8,128)S(1)} %bitcast.144), channel_id=1, source_target_pairs={{0,8},{8,16},{16,24},{24,0},{1,9},{9,17},{17,25},{25,1},{2,10},{10... | collective-permute-start | bytes 245768 | tf_op jit(solution)/shard_map/ppermute | solution.py:23
  44.0 1.1 %copy-start.3 = (f32[160,16,128]{2,1,0:T(8,128)}, f32[160,16,128]{2,1,0:T(8,128)S(1)}, u32[]{:S(2)}) copy-start(f32[160,16,128]{2,1,0:T(8,128)S(1)} %fusion.9) | copy-start | bytes 3932164
  45.7 35.9 %copy-start.11 = (f32[4,16,128]{2,1,0:T(8,128)S(1)}, f32[4,16,128]{2,1,0:T(8,128)}, u32[]{:S(2)}) copy-start(f32[4,16,128]{2,1,0:T(8,128)} %param.40) | copy-start | bytes 98308
  51.9 29.7 %copy-start = (f32[2,40,16,128]{3,2,1,0:T(8,128)S(1)}, f32[2,40,16,128]{3,2,1,0:T(8,128)}, u32[]{:S(2)}) copy-start(f32[2,40,16,128]{3,2,1,0:T(8,128)} %param.37) | copy-start | bytes 1966084
  51.9 29.7 %copy-start.2 = (f32[2,40,16,128]{3,2,1,0:T(8,128)S(1)}, f32[2,40,16,128]{3,2,1,0:T(8,128)}, u32[]{:S(2)}) copy-start(f32[2,40,16,128]{3,2,1,0:T(8,128)} %param.38) | copy-start | bytes 1966084
  84.4 7.1 %collective-permute-start.8 = (f32[80,128]{1,0:T(8,128)S(1)}, f32[80,128]{1,0:T(8,128)S(1)}, u32[]{:S(2)}, u32[]{:S(2)}) collective-permute-start(f32[80,128]{1,0:T(8,128)S(1)} %bitcast.139), channel_id=1, source_target_pairs={{0,24},{8,0},{16,8},{24,16},{1,25},{9,1},{17,9},{25,17},{2,26},{10... | collective-permute-start | bytes 122888 | tf_op jit(solution)/shard_map/ppermute | solution.py:23
  84.4 7.1 %collective-permute-start.9 = (f32[80,128]{1,0:T(8,128)S(1)}, f32[80,128]{1,0:T(8,128)S(1)}, u32[]{:S(2)}, u32[]{:S(2)}) collective-permute-start(f32[80,128]{1,0:T(8,128)S(1)} %bitcast.138), channel_id=1, source_target_pairs={{0,8},{8,16},{16,24},{24,0},{1,9},{9,17},{17,25},{25,1},{2,10},{10... | collective-permute-start | bytes 122888 | tf_op jit(solution)/shard_map/ppermute | solution.py:23
  85.0 6.4 %collective-permute-start.11 = (f32[10,128]{1,0:T(8,128)S(1)}, f32[10,128]{1,0:T(8,128)S(1)}, u32[]{:S(2)}, u32[]{:S(2)}) collective-permute-start(f32[10,128]{1,0:T(8,128)S(1)} %reshape_squeeze.47), channel_id=1, source_target_pairs={{0,1},{1,2},{2,3},{3,4},{4,5},{5,6},{6,7},{7,0},{8,9},{9,10},{10,1... | collective-permute-start | bytes 15368 | tf_op jit(solution)/shard_map/ppermute | solution.py:25
  85.3 5.9 %collective-permute-start.10 = (f32[10,128]{1,0:T(8,128)S(1)}, f32[10,128]{1,0:T(8,128)S(1)}, u32[]{:S(2)}, u32[]{:S(2)}) collective-permute-start(f32[10,128]{1,0:T(8,128)S(1)} %reshape_squeeze.46), channel_id=1, source_target_pairs={{0,7},{1,0},{2,1},{3,2},{4,3},{5,4},{6,5},{7,6},{8,15},{9,8},{10,9... | collective-permute-start | bytes 15368 | tf_op jit(solution)/shard_map/ppermute | solution.py:25
  95.3 7.2 %collective-permute-start.12 = (f32[80,128]{1,0:T(8,128)S(1)}, f32[80,128]{1,0:T(8,128)S(1)}, u32[]{:S(2)}, u32[]{:S(2)}) collective-permute-start(f32[80,128]{1,0:T(8,128)S(1)} %bitcast.141), channel_id=1, source_target_pairs={{0,24},{8,0},{16,8},{24,16},{1,25},{9,1},{17,9},{25,17},{2,26},{10... | collective-permute-start | bytes 122888 | tf_op jit(solution)/shard_map/ppermute | solution.py:23
  95.7 6.9 %collective-permute-start.13 = (f32[80,128]{1,0:T(8,128)S(1)}, f32[80,128]{1,0:T(8,128)S(1)}, u32[]{:S(2)}, u32[]{:S(2)}) collective-permute-start(f32[80,128]{1,0:T(8,128)S(1)} %bitcast.140), channel_id=1, source_target_pairs={{0,8},{8,16},{16,24},{24,0},{1,9},{9,17},{17,25},{25,1},{2,10},{10... | collective-permute-start | bytes 122888 | tf_op jit(solution)/shard_map/ppermute | solution.py:23
  96.0 6.5 %collective-permute-start.15 = (f32[10,128]{1,0:T(8,128)S(1)}, f32[10,128]{1,0:T(8,128)S(1)}, u32[]{:S(2)}, u32[]{:S(2)}) collective-permute-start(f32[10,128]{1,0:T(8,128)S(1)} %reshape_squeeze.51), channel_id=1, source_target_pairs={{0,1},{1,2},{2,3},{3,4},{4,5},{5,6},{6,7},{7,0},{8,9},{9,10},{10,1... | collective-permute-start | bytes 15368 | tf_op jit(solution)/shard_map/ppermute | solution.py:25
  96.0 6.2 %collective-permute-start.14 = (f32[10,128]{1,0:T(8,128)S(1)}, f32[10,128]{1,0:T(8,128)S(1)}, u32[]{:S(2)}, u32[]{:S(2)}) collective-permute-start(f32[10,128]{1,0:T(8,128)S(1)} %reshape_squeeze.50), channel_id=1, source_target_pairs={{0,7},{1,0},{2,1},{3,2},{4,3},{5,4},{6,5},{7,6},{8,15},{9,8},{10,9... | collective-permute-start | bytes 15368 | tf_op jit(solution)/shard_map/ppermute | solution.py:25

commit v10 on v8

--- a/solution.py
+++ b/solution.py
@@ -98,18 +98,34 @@
 
 
 def tracer_step(tracers, velocity):
-    last_x, last_y = tracers.shape[-2] - 1, tracers.shape[-1] - 1
+    xsize, ysize = tracers.shape[-2], tracers.shape[-1]
+    last_x, last_y = xsize - 1, ysize - 1
+    precision = lax.Precision.HIGH
     from_up = exchange(tracers[..., last_x, :], 1, 0)[..., None, :]
     from_down = exchange(tracers[..., 0, :], -1, 0)[..., None, :]
     from_left = exchange(tracers[..., last_y], 0, 1)[..., None]
     from_right = exchange(tracers[..., 0], 0, -1)[..., None]
-    west, east = shifted(tracers, from_up, from_down, tracers.ndim - 2)
-    south, north = shifted(tracers, from_left, from_right, tracers.ndim - 1)
+    above_x = np.eye(xsize, k=1)
+    above_y = np.eye(ysize, k=1)
+    sum_x = jnp.asarray(above_x + above_x.T, jnp.float32)
+    diff_x = jnp.asarray(above_x - above_x.T, jnp.float32)
+    sum_y = jnp.asarray(above_y + above_y.T, jnp.float32)
+    diff_y = jnp.asarray(above_y.T - above_y, jnp.float32)
+    row = jnp.arange(xsize)[:, None]
+    column = jnp.arange(ysize)
+    east = jnp.where(row == last_x, from_down, 0.0)
+    west = jnp.where(row == 0, from_up, 0.0)
+    north = jnp.where(column == last_y, from_right, 0.0)
+    south = jnp.where(column == 0, from_left, 0.0)
+    across_x = jnp.einsum("ab,...by->...ay", sum_x, tracers, precision=precision) + (east + west)
+    slope_x = jnp.einsum("ab,...by->...ay", diff_x, tracers, precision=precision) + (east - west)
+    across_y = jnp.einsum("...xc,cd->...xd", tracers, sum_y, precision=precision) + (north + south)
+    slope_y = jnp.einsum("...xc,cd->...xd", tracers, diff_y, precision=precision) + (north - south)
     return (
         tracers
-        + diff_coef * (east + west + north + south - 4.0 * tracers)
-        - 0.5 * velocity[0] * (east - west)
-        - 0.5 * velocity[1] * (north - south)
+        + diff_coef * (across_x + across_y - 4.0 * tracers)
+        - 0.5 * velocity[0] * slope_x
+        - 0.5 * velocity[1] * slope_y
     )
 
 

time: 99.5 us -> 96.1 us (0.966)
  matrix products: 8.48 us -> 15.2 us
  other arithmetic: 8.69 us -> 4.31 us
  local copies, waits for them, and re-layouts: 13.9 us -> 9.69 us
  starting transfers between devices: 22.7 us -> 19.8 us
  blocking collectives: 13.3 us -> 14.3 us
    dot_general x0 -> x8, matrix products: none -> 6.71 us  [the longest x2 4.25 us: tracer_step(): jnp.einsum('ab,...by->...ay', sum_x, tracers, precision=precision)]
    ppermute x8, starting transfers between devices: 20.6 us -> 15.1 us  [neighbour(): lax.ppermute(values, 'gy', [(j, (j + step_y) % count_y) for j in range(co...]
    sub x2 -> x0, other arithmetic: 5.22 us -> none  [tracer_step(): tracers + diff_coef * (east + west + north + south - 4.0 * tracers)]
    ppermute x8, waiting for transfers between devices: 9.82 us -> 13.1 us  [neighbour(): lax.ppermute(values, 'gy', [(j, (j + step_y) % count_y) for j in range(co...]
    ppermute x8, waiting for transfers between devices: 7.18 us -> 3.93 us  [neighbour(): lax.ppermute(values, 'gx', [(i, (i + step_x) % count_x) for i in range(co...]
    ppermute x8, starting transfers between devices: 2.13 us -> 4.7 us  [neighbour(): lax.ppermute(values, 'gx', [(i, (i + step_x) % count_x) for i in range(co...]
    slice x6 -> x2, local copies, waits for them, and re-layouts: 2.6 us -> 0.74 us  [tracer_step(): from_down = exchange(tracers[..., 0, :], -1, 0)[..., None, :]]
    slice x2, local copies, waits for them, and re-layouts: 2.67 us -> 1.19 us  [tracer_step(): from_right = exchange(tracers[..., 0], 0, -1)[..., None]]
where the time goes in v10:
time: 96.1 us; the launch traced here: 95.1 us
  starting transfers between devices  19.8 us (21%)
  waiting for transfers between devices  17.1 us (18%)
  matrix products  15.2 us (16%)
  blocking collectives  14.3 us (15%)
  Pallas kernels  13.3 us (14%)
  local copies, waits for them, and re-layouts  9.69 us (10%)
  other arithmetic  4.31 us (4%)
  between operations  1.35 us (1%)
    ppermute x8, starting transfers between devices, neighbour(): lax.ppermute(values, 'gy', [(j, (j + step_y) % count_y) for j in range(co...  15.1 us
    all_to_all x1, blocking collectives, per_device(): lax.all_to_all(payload, ('gx', 'gy'), split_axis=1, concat_axis=1, tiled=...  14.3 us
    pallas_call x2, Pallas kernels, onehot_gather(): pl.pallas_call(gather_kernel, grid=(count // tile,), in_specs=[pl.BlockSp...  13.3 us
    ppermute x8, waiting for transfers between devices, neighbour(): lax.ppermute(values, 'gy', [(j, (j + step_y) % count_y) for j in range(co...  13.1 us
    ppermute x8, starting transfers between devices, neighbour(): lax.ppermute(values, 'gx', [(i, (i + step_x) % count_x) for i in range(co...  4.7 us
    dot_general x2, matrix products, tracer_step(): jnp.einsum('ab,...by->...ay', sum_x, tracers, precision=precision)  4.25 us
    ppermute x8, waiting for transfers between devices, neighbour(): lax.ppermute(values, 'gx', [(i, (i + step_x) % count_x) for i in range(co...  3.93 us
    unnamed x62, local copies, waits for them, and re-layouts  3.35 us
  transfers between devices with their start and end apart: 16, of which 10 were waited for; matrix products, arithmetic and copies ran while one was open for 3% of the time, Pallas kernels for 0%

profile of v10, /device:TPU:0, one launch (start us, length us, event | category | flops | bytes accessed | tf_op | source)
XLA Modules:
  0.0 95.1 jit_solution(875256616454595642)
XLA Ops:
  0.7 0.6 copy-done.18
  2.0 0.7 fusion.10
  2.7 0.7 convolution_bitcast_fusion.5
  3.5 0.7 fusion.61
  4.4 0.7 fusion.2
  5.2 0.7 fusion.1
  5.9 1.1 %slice_reduce_fusion.3 = (f32[160,16]{1,0:T(8,128)S(1)}, f32[160,16]{1,0:T(8,128)S(1)}) fusion(f32[160,16,128]{2,1,0:T(8,128)S(1)} %fusion.1), kind=kLoop, calls=%fused_computation.24 | loop fusion | bytes 40960 | tf_op jit(solution)/shard_map/slice | solution.py:87
  7.1 3.0 %collective-permute-start = (f32[20,128]{1,0:T(8,128)S(1)}, f32[20,128]{1,0:T(8,128)S(1)}, u32[]{:S(2)}, u32[]{:S(2)}) collective-permute-start(f32[20,128]{1,0:T(8,128)S(1)} %reshape_squeeze.39), channel_id=1, source_target_pairs={{0,1},{1,2},{2,3},{3,4},{4,5},{5,6},{6,7},{7,0},{8,9},{9,10},{10,1... | collective-permute-start | bytes 30728 | tf_op jit(solution)/shard_map/ppermute | solution.py:25
  10.1 3.1 %collective-permute-start.1 = (f32[20,128]{1,0:T(8,128)S(1)}, f32[20,128]{1,0:T(8,128)S(1)}, u32[]{:S(2)}, u32[]{:S(2)}) collective-permute-start(f32[20,128]{1,0:T(8,128)S(1)} %reshape_squeeze.40), channel_id=1, source_target_pairs={{0,7},{1,0},{2,1},{3,2},{4,3},{5,4},{6,5},{7,6},{8,15},{9,8},{10,9... | collective-permute-start | bytes 30728 | tf_op jit(solution)/shard_map/ppermute | solution.py:25
  13.3 1.5 %collective-permute-done = f32[20,128]{1,0:T(8,128)S(1)} collective-permute-done((f32[20,128]{1,0:T(8,128)S(1)}, f32[20,128]{1,0:T(8,128)S(1)}, u32[]{:S(2)}, u32[]{:S(2)}) %collective-permute-start) | collective-permute-done | bytes 10272 | tf_op jit(solution)/shard_map/ppermute | solution.py:25
  15.0 0.8 select_add_fusion.1
  16.0 1.7 %collective-permute-start.3 = (f32[160,128]{1,0:T(8,128)S(1)}, f32[160,128]{1,0:T(8,128)S(1)}, u32[]{:S(2)}, u32[]{:S(2)}) collective-permute-start(f32[160,128]{1,0:T(8,128)S(1)} %bitcast.169), channel_id=1, source_target_pairs={{0,24},{8,0},{16,8},{24,16},{1,25},{9,1},{17,9},{25,17},{2,26},{10... | collective-permute-start | bytes 245768 | tf_op jit(solution)/shard_map/ppermute | solution.py:23
  17.8 2.1 %collective-permute-done.2 = f32[160,128]{1,0:T(8,128)S(1)} collective-permute-done((f32[160,128]{1,0:T(8,128)S(1)}, f32[160,128]{1,0:T(8,128)S(1)}, u32[]{:S(2)}, u32[]{:S(2)}) %collective-permute-start.2) | collective-permute-done | bytes 81952 | tf_op jit(solution)/shard_map/ppermute | solution.py:23
  20.0 0.8 fusion.5
  20.8 0.7 fusion.6
  21.5 0.7 convolution_multiply_fusion.1
  22.2 0.7 convolution_bitcast_fusion.2
  22.9 0.7 fusion.62
  23.6 0.7 fusion
  24.3 1.1 %slice_reduce_fusion.1 = (f32[160,16]{1,0:T(8,128)S(1)}, f32[160,16]{1,0:T(8,128)S(1)}) fusion(f32[160,16,128]{2,1,0:T(8,128)S(1)} %fusion), kind=kLoop, calls=%fused_computation.22 | loop fusion | bytes 40960 | tf_op jit(solution)/shard_map/slice | solution.py:87
  25.5 1.4 %collective-permute-start.4 = (f32[20,128]{1,0:T(8,128)S(1)}, f32[20,128]{1,0:T(8,128)S(1)}, u32[]{:S(2)}, u32[]{:S(2)}) collective-permute-start(f32[20,128]{1,0:T(8,128)S(1)} %reshape_squeeze.41), channel_id=1, source_target_pairs={{0,1},{1,2},{2,3},{3,4},{4,5},{5,6},{6,7},{7,0},{8,9},{9,10},{10,1... | collective-permute-start | bytes 30728 | tf_op jit(solution)/shard_map/ppermute | solution.py:25
  27.0 3.4 %collective-permute-start.5 = (f32[20,128]{1,0:T(8,128)S(1)}, f32[20,128]{1,0:T(8,128)S(1)}, u32[]{:S(2)}, u32[]{:S(2)}) collective-permute-start(f32[20,128]{1,0:T(8,128)S(1)} %reshape_squeeze.42), channel_id=1, source_target_pairs={{0,7},{1,0},{2,1},{3,2},{4,3},{5,4},{6,5},{7,6},{8,15},{9,8},{10,9... | collective-permute-start | bytes 30728 | tf_op jit(solution)/shard_map/ppermute | solution.py:25
  30.4 1.5 %collective-permute-done.4 = f32[20,128]{1,0:T(8,128)S(1)} collective-permute-done((f32[20,128]{1,0:T(8,128)S(1)}, f32[20,128]{1,0:T(8,128)S(1)}, u32[]{:S(2)}, u32[]{:S(2)}) %collective-permute-start.4) | collective-permute-done | bytes 10272 | tf_op jit(solution)/shard_map/ppermute | solution.py:25
  32.2 0.8 select_add_fusion
  33.2 0.9 collective-permute-start.6
  34.1 0.9 collective-permute-start.7
  35.1 0.6 copy.51
  35.7 1.4 %collective-permute-done.6 = f32[160,128]{1,0:T(8,128)S(1)} collective-permute-done((f32[160,128]{1,0:T(8,128)S(1)}, f32[160,128]{1,0:T(8,128)S(1)}, u32[]{:S(2)}, u32[]{:S(2)}) %collective-permute-start.6) | collective-permute-done | bytes 81952 | tf_op jit(solution)/shard_map/ppermute | solution.py:23
  37.4 0.8 fusion.9
  38.3 0.6 fusion.37.table_ref
  38.9 6.5 %shard_map.320 = f32[4,8192]{1,0:T(4,128)} custom-call(s32[1,8192]{1,0:T(1,128)} %bitcast.168, f32[4,16,128]{2,1,0:T(8,128)} %fusion.37.table_ref), custom_call_target="tpu_custom_call" | custom-call | tf_op jit(solution)/shard_map/pallas_call | solution.py:190
  45.4 0.9 broadcast_multiply_fusion
  46.3 14.3 %all_to_all.5 = f32[4,32,256]{2,0,1:T(4,128)S(1)} all-to-all(f32[4,32,256]{2,0,1:T(4,128)S(1)} %broadcast_multiply_fusion), channel_id=1, replica_groups=mesh['gx'=4,'gy'=8] {'gx','gy'}, dimensions={1} | all-to-all | bytes 262144 | tf_op jit(solution)/shard_map/all_to_all | solution.py:229
  60.7 0.7 reshape_reshape.3.table_ref
  61.4 6.9 %shard_map.321 = f32[4,8192]{1,0:T(4,128)} custom-call(s32[1,8192]{1,0:T(1,128)} %bitcast.177, f32[4,64,128]{2,1,0:T(8,128)} %reshape_reshape.3.table_ref), custom_call_target="tpu_custom_call" | custom-call | tf_op jit(solution)/shard_map/pallas_call | solution.py:190
  68.3 0.9 copy.52
  69.3 0.6 slice_reduce_fusion.7
  69.9 0.7 fusion.60
  71.9 2.1 %collective-permute-start.10 = (f32[10,128]{1,0:T(8,128)S(1)}, f32[10,128]{1,0:T(8,128)S(1)}, u32[]{:S(2)}, u32[]{:S(2)}) collective-permute-start(f32[10,128]{1,0:T(8,128)S(1)} %reshape_squeeze.46), channel_id=1, source_target_pairs={{0,7},{1,0},{2,1},{3,2},{4,3},{5,4},{6,5},{7,6},{8,15},{9,8},{10,9... | collective-permute-start | bytes 15368 | tf_op jit(solution)/shard_map/ppermute | solution.py:25
  74.2 0.5 collective-permute-start.9
  74.7 0.9 fusion.36
  75.7 4.8 %collective-permute-done.11 = f32[10,128]{1,0:T(8,128)S(1)} collective-permute-done((f32[10,128]{1,0:T(8,128)S(1)}, f32[10,128]{1,0:T(8,128)S(1)}, u32[]{:S(2)}, u32[]{:S(2)}) %collective-permute-start.11) | collective-permute-done | bytes 5152 | tf_op jit(solution)/shard_map/ppermute | solution.py:25
  80.5 1.9 %fusion.17 = f32[2,40,16,128]{3,2,1,0:T(8,128)S(1)} fusion(f32[2,40,16,128]{3,2,1,0:T(8,128)S(1)} %get-tuple-element.71, f32[2,40,16,128]{3,2,1,0:T(8,128)S(1)} %convolution_bitcast_fusion.8, f32[2,40,16,128]{3,2,1,0:T(8,128)S(1)} %fusion.63, f32[2,40,16,128]{3,2,1,0:T(8,128)S(1)} %fusion.64, f32[40,16,128]{2,1,0:T(8,128)} %get-tuple-element.69, ...), kind=kOutput, calls=%fused_computation.45 | convolution fusion | flops 19169280 | bytes 4025632 | tf_op jit(solution)/shard_map/ab,...by->...ay/dot_general | solution.py:120
  83.3 0.6 slice_reduce_fusion.5
  84.1 2.0 %collective-permute-start.14 = (f32[10,128]{1,0:T(8,128)S(1)}, f32[10,128]{1,0:T(8,128)S(1)}, u32[]{:S(2)}, u32[]{:S(2)}) collective-permute-start(f32[10,128]{1,0:T(8,128)S(1)} %reshape_squeeze.50), channel_id=1, source_target_pairs={{0,7},{1,0},{2,1},{3,2},{4,3},{5,4},{6,5},{7,6},{8,15},{9,8},{10,9... | collective-permute-start | bytes 15368 | tf_op jit(solution)/shard_map/ppermute | solution.py:25
  87.2 0.6 collective-permute-done.14
  87.9 4.7 %collective-permute-done.15 = f32[10,128]{1,0:T(8,128)S(1)} collective-permute-done((f32[10,128]{1,0:T(8,128)S(1)}, f32[10,128]{1,0:T(8,128)S(1)}, u32[]{:S(2)}, u32[]{:S(2)}) %collective-permute-start.15) | collective-permute-done | bytes 5152 | tf_op jit(solution)/shard_map/ppermute | solution.py:25
  92.7 2.4 %fusion.29 = f32[2,40,16,128]{3,2,1,0:T(8,128)} fusion(f32[2,40,16,128]{3,2,1,0:T(8,128)S(1)} %fusion.17, f32[2,40,16,128]{3,2,1,0:T(8,128)S(1)} %convolution_bitcast_fusion.6, f32[2,40,16,128]{3,2,1,0:T(8,128)S(1)} %fusion.65, f32[2,40,16,128]{3,2,1,0:T(8,128)S(1)} %fusion.66, f32[2,40,16]{2,1,0:T(8,128)S(1)} %broadcast_in_dim.278, ...), kind=kOutput, calls=%fused_computation.57 | convolution fusion | flops 19169280 | bytes 4025632 | tf_op jit(solution)/shard_map/ab,...by->...ay/dot_general | solution.py:120
  (108 shorter events, 6.7 us)
Async XLA Ops:
  0.6 0.7 copy-start.18
  0.6 0.7 copy-start.28
  0.7 0.9 copy-start.11
  0.7 1.3 %copy-start.1 = (f32[4,40,16,128]{3,2,1,0:T(8,128)S(1)}, f32[4,40,16,128]{3,2,1,0:T(8,128)}, u32[]{:S(2)}) copy-start(f32[4,40,16,128]{3,2,1,0:T(8,128)} %param.41) | copy-start | bytes 3932164
  0.7 0.8 copy-start.17
  2.7 0.8 copy-start.10
  3.5 0.8 copy-start.7
  4.4 0.8 copy-start.6
  7.1 7.7 %collective-permute-start = (f32[20,128]{1,0:T(8,128)S(1)}, f32[20,128]{1,0:T(8,128)S(1)}, u32[]{:S(2)}, u32[]{:S(2)}) collective-permute-start(f32[20,128]{1,0:T(8,128)S(1)} %reshape_squeeze.39), channel_id=1, source_target_pairs={{0,1},{1,2},{2,3},{3,4},{4,5},{5,6},{6,7},{7,0},{8,9},{9,10},{10,1... | collective-permute-start | bytes 30728 | tf_op jit(solution)/shard_map/ppermute | solution.py:25
  10.1 4.7 %collective-permute-start.1 = (f32[20,128]{1,0:T(8,128)S(1)}, f32[20,128]{1,0:T(8,128)S(1)}, u32[]{:S(2)}, u32[]{:S(2)}) collective-permute-start(f32[20,128]{1,0:T(8,128)S(1)} %reshape_squeeze.40), channel_id=1, source_target_pairs={{0,7},{1,0},{2,1},{3,2},{4,3},{5,4},{6,5},{7,6},{8,15},{9,8},{10,9... | collective-permute-start | bytes 30728 | tf_op jit(solution)/shard_map/ppermute | solution.py:25
  13.3 18.9 %copy-start.19 = (pred[128]{0:T(512)(128)(4,1)}, pred[128]{0:T(512)(128)(4,1)S(1)}, u32[]{:S(2)}) copy-start(pred[128]{0:T(512)(128)(4,1)S(1)} %get-tuple-element.76) | copy-start | bytes 388
  13.3 18.9 %copy-start.21 = (pred[128]{0:T(512)(128)(4,1)}, pred[128]{0:T(512)(128)(4,1)S(1)}, u32[]{:S(2)}) copy-start(pred[128]{0:T(512)(128)(4,1)S(1)} %get-tuple-element.77) | copy-start | bytes 388
  15.0 5.0 %copy-start.13 = (f32[16,128]{1,0:T(8,128)S(1)}, f32[16,128]{1,0:T(8,128)}, u32[]{:S(2)}) copy-start(f32[16,128]{1,0:T(8,128)} %constant.165) | copy-start | bytes 24580
  15.0 5.0 %copy-start.14 = (f32[16,16,1]{1,0,2:T(8,128)S(1)}, f32[16,16,1]{1,0,2:T(8,128)}, u32[]{:S(2)}) copy-start(f32[16,16,1]{1,0,2:T(8,128)} %constant.170) | copy-start | bytes 3076
  16.0 3.9 %collective-permute-start.2 = (f32[160,128]{1,0:T(8,128)S(1)}, f32[160,128]{1,0:T(8,128)S(1)}, u32[]{:S(2)}, u32[]{:S(2)}) collective-permute-start(f32[160,128]{1,0:T(8,128)S(1)} %bitcast.171), channel_id=1, source_target_pairs={{0,8},{8,16},{16,24},{24,0},{1,9},{9,17},{17,25},{25,1},{2,10},{10... | collective-permute-start | bytes 245768 | tf_op jit(solution)/shard_map/ppermute | solution.py:23
  16.0 4.0 %collective-permute-start.3 = (f32[160,128]{1,0:T(8,128)S(1)}, f32[160,128]{1,0:T(8,128)S(1)}, u32[]{:S(2)}, u32[]{:S(2)}) collective-permute-start(f32[160,128]{1,0:T(8,128)S(1)} %bitcast.169), channel_id=1, source_target_pairs={{0,24},{8,0},{16,8},{24,16},{1,25},{9,1},{17,9},{25,17},{2,26},{10... | collective-permute-start | bytes 245768 | tf_op jit(solution)/shard_map/ppermute | solution.py:23
  17.8 19.6 %copy-start.23 = (pred[16]{0:T(512)(128)(4,1)}, pred[16]{0:T(512)(128)(4,1)S(1)}, u32[]{:S(2)}) copy-start(pred[16]{0:T(512)(128)(4,1)S(1)} %get-tuple-element.78) | copy-start | bytes 52
  17.8 19.6 %copy-start.25 = (pred[16]{0:T(512)(128)(4,1)}, pred[16]{0:T(512)(128)(4,1)S(1)}, u32[]{:S(2)}) copy-start(pred[16]{0:T(512)(128)(4,1)S(1)} %get-tuple-element.79) | copy-start | bytes 52
  25.5 6.5 %collective-permute-start.4 = (f32[20,128]{1,0:T(8,128)S(1)}, f32[20,128]{1,0:T(8,128)S(1)}, u32[]{:S(2)}, u32[]{:S(2)}) collective-permute-start(f32[20,128]{1,0:T(8,128)S(1)} %reshape_squeeze.41), channel_id=1, source_target_pairs={{0,1},{1,2},{2,3},{3,4},{4,5},{5,6},{6,7},{7,0},{8,9},{9,10},{10,1... | collective-permute-start | bytes 30728 | tf_op jit(solution)/shard_map/ppermute | solution.py:25
  27.0 5.1 %collective-permute-start.5 = (f32[20,128]{1,0:T(8,128)S(1)}, f32[20,128]{1,0:T(8,128)S(1)}, u32[]{:S(2)}, u32[]{:S(2)}) collective-permute-start(f32[20,128]{1,0:T(8,128)S(1)} %reshape_squeeze.42), channel_id=1, source_target_pairs={{0,7},{1,0},{2,1},{3,2},{4,3},{5,4},{6,5},{7,6},{8,15},{9,8},{10,9... | collective-permute-start | bytes 30728 | tf_op jit(solution)/shard_map/ppermute | solution.py:25
  32.2 2.8 %copy-start.27 = (s32[1,32]{1,0:T(1,128)S(1)}, s32[1,32]{1,0:T(1,128)}, u32[]{:S(2)}) copy-start(s32[1,32]{1,0:T(1,128)} %param.44) | copy-start | bytes 388
  32.2 2.9 %copy-start.15 = (s32[1,32,256]{2,1,0:T(8,128)S(1)}, s32[1,32,256]{2,1,0:T(8,128)}, u32[]{:S(2)}) copy-start(s32[1,32,256]{2,1,0:T(8,128)} %param.43) | copy-start | bytes 98308
  33.2 3.9 %collective-permute-start.6 = (f32[160,128]{1,0:T(8,128)S(1)}, f32[160,128]{1,0:T(8,128)S(1)}, u32[]{:S(2)}, u32[]{:S(2)}) collective-permute-start(f32[160,128]{1,0:T(8,128)S(1)} %bitcast.172), channel_id=1, source_target_pairs={{0,8},{8,16},{16,24},{24,0},{1,9},{9,17},{17,25},{25,1},{2,10},{10... | collective-permute-start | bytes 245768 | tf_op jit(solution)/shard_map/ppermute | solution.py:23
  34.1 3.3 %collective-permute-start.7 = (f32[160,128]{1,0:T(8,128)S(1)}, f32[160,128]{1,0:T(8,128)S(1)}, u32[]{:S(2)}, u32[]{:S(2)}) collective-permute-start(f32[160,128]{1,0:T(8,128)S(1)} %bitcast.170), channel_id=1, source_target_pairs={{0,24},{8,0},{16,8},{24,16},{1,25},{9,1},{17,9},{25,17},{2,26},{10... | collective-permute-start | bytes 245768 | tf_op jit(solution)/shard_map/ppermute | solution.py:23
  38.3 31.6 %copy-start.3 = (f32[160,16,128]{2,1,0:T(8,128)}, f32[160,16,128]{2,1,0:T(8,128)S(1)}, u32[]{:S(2)}) copy-start(f32[160,16,128]{2,1,0:T(8,128)S(1)} %fusion.9) | copy-start | bytes 3932164
  38.3 30.9 %copy-start.16 = (f32[4,16,128]{2,1,0:T(8,128)S(1)}, f32[4,16,128]{2,1,0:T(8,128)}, u32[]{:S(2)}) copy-start(f32[4,16,128]{2,1,0:T(8,128)} %param.48) | copy-start | bytes 98308
  38.3 30.9 %copy-start = (f32[2,40,16,128]{3,2,1,0:T(8,128)S(1)}, f32[2,40,16,128]{3,2,1,0:T(8,128)}, u32[]{:S(2)}) copy-start(f32[2,40,16,128]{3,2,1,0:T(8,128)} %param.45) | copy-start | bytes 1966084
  38.3 30.9 %copy-start.2 = (f32[2,40,16,128]{3,2,1,0:T(8,128)S(1)}, f32[2,40,16,128]{3,2,1,0:T(8,128)}, u32[]{:S(2)}) copy-start(f32[2,40,16,128]{3,2,1,0:T(8,128)} %param.46) | copy-start | bytes 1966084
  60.7 9.8 %copy-start.12 = (f32[16,16,1,1]{1,0,3,2:T(8,128)S(1)}, f32[16,16,1,1]{1,0,3,2:T(8,128)}, u32[]{:S(2)}) copy-start(f32[16,16,1,1]{1,0,3,2:T(8,128)} %constant.173) | copy-start | bytes 3076
  69.3 1.7 %copy-start.9 = (f32[128,128,1,1]{1,0,3,2:T(8,128)S(1)}, f32[128,128,1,1]{1,0,3,2:T(8,128)}, u32[]{:S(2)}) copy-start(f32[128,128,1,1]{1,0,3,2:T(8,128)} %constant.172) | copy-start | bytes 196612
  70.6 0.8 copy-start.8
  71.9 3.7 %collective-permute-start.10 = (f32[10,128]{1,0:T(8,128)S(1)}, f32[10,128]{1,0:T(8,128)S(1)}, u32[]{:S(2)}, u32[]{:S(2)}) collective-permute-start(f32[10,128]{1,0:T(8,128)S(1)} %reshape_squeeze.46), channel_id=1, source_target_pairs={{0,7},{1,0},{2,1},{3,2},{4,3},{5,4},{6,5},{7,6},{8,15},{9,8},{10,9... | collective-permute-start | bytes 15368 | tf_op jit(solution)/shard_map/ppermute | solution.py:25
  74.1 6.4 %collective-permute-start.11 = (f32[10,128]{1,0:T(8,128)S(1)}, f32[10,128]{1,0:T(8,128)S(1)}, u32[]{:S(2)}, u32[]{:S(2)}) collective-permute-start(f32[10,128]{1,0:T(8,128)S(1)} %reshape_squeeze.47), channel_id=1, source_target_pairs={{0,1},{1,2},{2,3},{3,4},{4,5},{5,6},{6,7},{7,0},{8,9},{9,10},{10,1... | collective-permute-start | bytes 15368 | tf_op jit(solution)/shard_map/ppermute | solution.py:25
  74.1 6.4 %collective-permute-start.8 = (f32[80,128]{1,0:T(8,128)}, f32[80,128]{1,0:T(8,128)}, u32[]{:S(2)}, u32[]{:S(2)}) collective-permute-start(f32[80,128]{1,0:T(8,128)} %bitcast.174), channel_id=1, source_target_pairs={{0,24},{8,0},{16,8},{24,16},{1,25},{9,1},{17,9},{25,17},{2,26},{10... | collective-permute-start | bytes 122888 | tf_op jit(solution)/shard_map/ppermute | solution.py:23
  74.2 6.4 %collective-permute-start.9 = (f32[80,128]{1,0:T(8,128)S(1)}, f32[80,128]{1,0:T(8,128)}, u32[]{:S(2)}, u32[]{:S(2)}) collective-permute-start(f32[80,128]{1,0:T(8,128)S(1)} %bitcast.173), channel_id=1, source_target_pairs={{0,8},{8,16},{16,24},{24,0},{1,9},{9,17},{17,25},{25,1},{2,10},{10... | collective-permute-start | bytes 122888 | tf_op jit(solution)/shard_map/ppermute | solution.py:23
  83.3 9.4 %copy-start.4 = (f32[40,16,128]{2,1,0:T(8,128)S(1)}, f32[40,16,128]{2,1,0:T(8,128)}, u32[]{:S(2)}) copy-start(f32[40,16,128]{2,1,0:T(8,128)} %get-tuple-element.68) | copy-start | bytes 983044
  83.3 9.4 %copy-start.5 = (f32[40,16,128]{2,1,0:T(8,128)S(1)}, f32[40,16,128]{2,1,0:T(8,128)}, u32[]{:S(2)}) copy-start(f32[40,16,128]{2,1,0:T(8,128)} %get-tuple-element.69) | copy-start | bytes 983044
  83.3 9.4 %copy-start.20 = (pred[128]{0:T(512)(128)(4,1)S(1)}, pred[128]{0:T(512)(128)(4,1)}, u32[]{:S(2)}) copy-start(pred[128]{0:T(512)(128)(4,1)} %copy-done.19) | copy-start | bytes 388
  83.3 9.4 %copy-start.22 = (pred[128]{0:T(512)(128)(4,1)S(1)}, pred[128]{0:T(512)(128)(4,1)}, u32[]{:S(2)}) copy-start(pred[128]{0:T(512)(128)(4,1)} %copy-done.21) | copy-start | bytes 388
  83.3 9.4 %copy-start.24 = (pred[16]{0:T(512)(128)(4,1)S(1)}, pred[16]{0:T(512)(128)(4,1)}, u32[]{:S(2)}) copy-start(pred[16]{0:T(512)(128)(4,1)} %copy-done.23) | copy-start | bytes 52
  83.3 9.4 %copy-start.26 = (pred[16]{0:T(512)(128)(4,1)S(1)}, pred[16]{0:T(512)(128)(4,1)}, u32[]{:S(2)}) copy-start(pred[16]{0:T(512)(128)(4,1)} %copy-done.25) | copy-start | bytes 52
  83.3 9.4 %copy-start.29 = (f32[16,16,1,1]{1,0,3,2:T(8,128)S(1)}, f32[16,16,1,1]{1,0,3,2:T(8,128)}, u32[]{:S(2)}) copy-start(f32[16,16,1,1]{1,0,3,2:T(8,128)} %constant.171) | copy-start | bytes 3076
  84.1 3.7 %collective-permute-start.14 = (f32[10,128]{1,0:T(8,128)S(1)}, f32[10,128]{1,0:T(8,128)S(1)}, u32[]{:S(2)}, u32[]{:S(2)}) collective-permute-start(f32[10,128]{1,0:T(8,128)S(1)} %reshape_squeeze.50), channel_id=1, source_target_pairs={{0,7},{1,0},{2,1},{3,2},{4,3},{5,4},{6,5},{7,6},{8,15},{9,8},{10,9... | collective-permute-start | bytes 15368 | tf_op jit(solution)/shard_map/ppermute | solution.py:25
  86.2 6.4 %collective-permute-start.15 = (f32[10,128]{1,0:T(8,128)S(1)}, f32[10,128]{1,0:T(8,128)S(1)}, u32[]{:S(2)}, u32[]{:S(2)}) collective-permute-start(f32[10,128]{1,0:T(8,128)S(1)} %reshape_squeeze.51), channel_id=1, source_target_pairs={{0,1},{1,2},{2,3},{3,4},{4,5},{5,6},{6,7},{7,0},{8,9},{9,10},{10,1... | collective-permute-start | bytes 15368 | tf_op jit(solution)/shard_map/ppermute | solution.py:25
  86.2 6.4 %collective-permute-start.12 = (f32[80,128]{1,0:T(8,128)S(1)}, f32[80,128]{1,0:T(8,128)S(1)}, u32[]{:S(2)}, u32[]{:S(2)}) collective-permute-start(f32[80,128]{1,0:T(8,128)S(1)} %bitcast.176), channel_id=1, source_target_pairs={{0,24},{8,0},{16,8},{24,16},{1,25},{9,1},{17,9},{25,17},{2,26},{10... | collective-permute-start | bytes 122888 | tf_op jit(solution)/shard_map/ppermute | solution.py:23
  86.5 6.1 %collective-permute-start.13 = (f32[80,128]{1,0:T(8,128)S(1)}, f32[80,128]{1,0:T(8,128)}, u32[]{:S(2)}, u32[]{:S(2)}) collective-permute-start(f32[80,128]{1,0:T(8,128)S(1)} %bitcast.175), channel_id=1, source_target_pairs={{0,8},{8,16},{16,24},{24,0},{1,9},{9,17},{17,25},{25,1},{2,10},{10... | collective-permute-start | bytes 122888 | tf_op jit(solution)/shard_map/ppermute | solution.py:23

commit v11 on v10

--- a/solution.py
+++ b/solution.py
@@ -171,13 +171,17 @@
     index = index_ref[...]
     onehot = (lax.broadcasted_iota(jnp.int32, (128, tile), 0) == (index & 127)).astype(jnp.bfloat16)
     select = lax.broadcasted_iota(jnp.int32, (rows, tile), 0) == (index >> 7)
+    rest = table_ref[...]
+    parts = []
+    for part in range(3):
+        piece = rest.astype(jnp.bfloat16)
+        rest = rest - piece.astype(jnp.float32)
+        parts.append(piece)
+    stacked = jnp.concatenate(parts, axis=1).reshape(fields * 3 * rows, 128)
+    picked = jnp.dot(stacked, onehot, preferred_element_type=jnp.float32)
     for field in range(fields):
-        rest = table_ref[field]
-        whole = jnp.zeros((rows, tile), jnp.float32)
-        for part in range(3):
-            piece = rest.astype(jnp.bfloat16)
-            rest = rest - piece.astype(jnp.float32)
-            whole = whole + jnp.dot(piece, onehot, preferred_element_type=jnp.float32)
+        base = field * 3 * rows
+        whole = picked[base : base + rows] + picked[base + rows : base + 2 * rows] + picked[base + 2 * rows : base + 3 * rows]
         out_ref[pl.ds(field, 1), :] = jnp.sum(jnp.where(select, whole, 0.0), axis=0, keepdims=True)
 
 
@@ -186,7 +190,9 @@
     rows = total // 128
     flat = index.reshape(1, -1)
     count = flat.shape[1]
-    tile = math.gcd(count, 1024)
+    tile = 128
+    while tile < 2048 and count % (2 * tile) == 0 and fields * 3 * rows * tile * 8 <= 4 * 2**20:
+        tile *= 2
     return pl.pallas_call(
         gather_kernel,
         grid=(count // tile,),

time: 96.1 us -> 93 us (0.968)
  Pallas kernels: 13.3 us -> 10.3 us
    pallas_call x2, Pallas kernels: 13.3 us -> 10.3 us  [onehot_gather(): pl.pallas_call(gather_kernel, grid=(count // tile,), in_specs=[pl.BlockSp...]
where the time goes in v11:
time: 93 us; the launch traced here: 92.1 us
  starting transfers between devices  19.8 us (21%)
  waiting for transfers between devices  17.1 us (18%)
  matrix products  15.2 us (16%)
  blocking collectives  14.3 us (15%)
  Pallas kernels  10.3 us (11%)
  local copies, waits for them, and re-layouts  9.69 us (10%)
  other arithmetic  4.31 us (5%)
  between operations  1.35 us (1%)
    ppermute x8, starting transfers between devices, neighbour(): lax.ppermute(values, 'gy', [(j, (j + step_y) % count_y) for j in range(co...  15.1 us
    all_to_all x1, blocking collectives, per_device(): lax.all_to_all(payload, ('gx', 'gy'), split_axis=1, concat_axis=1, tiled=...  14.3 us
    ppermute x8, waiting for transfers between devices, neighbour(): lax.ppermute(values, 'gy', [(j, (j + step_y) % count_y) for j in range(co...  13.1 us
    pallas_call x2, Pallas kernels, onehot_gather(): pl.pallas_call(gather_kernel, grid=(count // tile,), in_specs=[pl.BlockSp...  10.3 us
    ppermute x8, starting transfers between devices, neighbour(): lax.ppermute(values, 'gx', [(i, (i + step_x) % count_x) for i in range(co...  4.71 us
    dot_general x2, matrix products, tracer_step(): jnp.einsum('ab,...by->...ay', sum_x, tracers, precision=precision)  4.25 us
    ppermute x8, waiting for transfers between devices, neighbour(): lax.ppermute(values, 'gx', [(i, (i + step_x) % count_x) for i in range(co...  3.93 us
    unnamed x62, local copies, waits for them, and re-layouts  3.35 us
  transfers between devices with their start and end apart: 16, of which 10 were waited for; matrix products, arithmetic and copies ran while one was open for 3% of the time, Pallas kernels for 0%

profile of v11, /device:TPU:0, one launch (start us, length us, event | category | flops | bytes accessed | tf_op | source)
XLA Modules:
  0.0 92.1 jit_solution(7827254262490167354)
XLA Ops:
  0.7 0.6 copy-done.18
  2.0 0.7 fusion.10
  2.7 0.7 convolution_bitcast_fusion.5
  3.5 0.7 fusion.61
  4.4 0.7 fusion.2
  5.2 0.7 fusion.1
  5.9 1.1 %slice_reduce_fusion.3 = (f32[160,16]{1,0:T(8,128)S(1)}, f32[160,16]{1,0:T(8,128)S(1)}) fusion(f32[160,16,128]{2,1,0:T(8,128)S(1)} %fusion.1), kind=kLoop, calls=%fused_computation.24 | loop fusion | bytes 40960 | tf_op jit(solution)/shard_map/slice | solution.py:87
  7.1 3.0 %collective-permute-start = (f32[20,128]{1,0:T(8,128)S(1)}, f32[20,128]{1,0:T(8,128)S(1)}, u32[]{:S(2)}, u32[]{:S(2)}) collective-permute-start(f32[20,128]{1,0:T(8,128)S(1)} %reshape_squeeze.39), channel_id=1, source_target_pairs={{0,1},{1,2},{2,3},{3,4},{4,5},{5,6},{6,7},{7,0},{8,9},{9,10},{10,1... | collective-permute-start | bytes 30728 | tf_op jit(solution)/shard_map/ppermute | solution.py:25
  10.1 3.1 %collective-permute-start.1 = (f32[20,128]{1,0:T(8,128)S(1)}, f32[20,128]{1,0:T(8,128)S(1)}, u32[]{:S(2)}, u32[]{:S(2)}) collective-permute-start(f32[20,128]{1,0:T(8,128)S(1)} %reshape_squeeze.40), channel_id=1, source_target_pairs={{0,7},{1,0},{2,1},{3,2},{4,3},{5,4},{6,5},{7,6},{8,15},{9,8},{10,9... | collective-permute-start | bytes 30728 | tf_op jit(solution)/shard_map/ppermute | solution.py:25
  13.3 1.5 %collective-permute-done = f32[20,128]{1,0:T(8,128)S(1)} collective-permute-done((f32[20,128]{1,0:T(8,128)S(1)}, f32[20,128]{1,0:T(8,128)S(1)}, u32[]{:S(2)}, u32[]{:S(2)}) %collective-permute-start) | collective-permute-done | bytes 10272 | tf_op jit(solution)/shard_map/ppermute | solution.py:25
  15.0 0.8 select_add_fusion.1
  16.0 1.7 %collective-permute-start.3 = (f32[160,128]{1,0:T(8,128)S(1)}, f32[160,128]{1,0:T(8,128)S(1)}, u32[]{:S(2)}, u32[]{:S(2)}) collective-permute-start(f32[160,128]{1,0:T(8,128)S(1)} %bitcast.169), channel_id=1, source_target_pairs={{0,24},{8,0},{16,8},{24,16},{1,25},{9,1},{17,9},{25,17},{2,26},{10... | collective-permute-start | bytes 245768 | tf_op jit(solution)/shard_map/ppermute | solution.py:23
  17.8 2.1 %collective-permute-done.2 = f32[160,128]{1,0:T(8,128)S(1)} collective-permute-done((f32[160,128]{1,0:T(8,128)S(1)}, f32[160,128]{1,0:T(8,128)S(1)}, u32[]{:S(2)}, u32[]{:S(2)}) %collective-permute-start.2) | collective-permute-done | bytes 81952 | tf_op jit(solution)/shard_map/ppermute | solution.py:23
  20.0 0.8 fusion.5
  20.8 0.7 fusion.6
  21.5 0.7 convolution_multiply_fusion.1
  22.2 0.7 convolution_bitcast_fusion.2
  22.9 0.7 fusion.62
  23.6 0.7 fusion
  24.3 1.1 %slice_reduce_fusion.1 = (f32[160,16]{1,0:T(8,128)S(1)}, f32[160,16]{1,0:T(8,128)S(1)}) fusion(f32[160,16,128]{2,1,0:T(8,128)S(1)} %fusion), kind=kLoop, calls=%fused_computation.22 | loop fusion | bytes 40960 | tf_op jit(solution)/shard_map/slice | solution.py:87
  25.5 1.4 %collective-permute-start.4 = (f32[20,128]{1,0:T(8,128)S(1)}, f32[20,128]{1,0:T(8,128)S(1)}, u32[]{:S(2)}, u32[]{:S(2)}) collective-permute-start(f32[20,128]{1,0:T(8,128)S(1)} %reshape_squeeze.41), channel_id=1, source_target_pairs={{0,1},{1,2},{2,3},{3,4},{4,5},{5,6},{6,7},{7,0},{8,9},{9,10},{10,1... | collective-permute-start | bytes 30728 | tf_op jit(solution)/shard_map/ppermute | solution.py:25
  27.0 3.4 %collective-permute-start.5 = (f32[20,128]{1,0:T(8,128)S(1)}, f32[20,128]{1,0:T(8,128)S(1)}, u32[]{:S(2)}, u32[]{:S(2)}) collective-permute-start(f32[20,128]{1,0:T(8,128)S(1)} %reshape_squeeze.42), channel_id=1, source_target_pairs={{0,7},{1,0},{2,1},{3,2},{4,3},{5,4},{6,5},{7,6},{8,15},{9,8},{10,9... | collective-permute-start | bytes 30728 | tf_op jit(solution)/shard_map/ppermute | solution.py:25
  30.4 1.5 %collective-permute-done.4 = f32[20,128]{1,0:T(8,128)S(1)} collective-permute-done((f32[20,128]{1,0:T(8,128)S(1)}, f32[20,128]{1,0:T(8,128)S(1)}, u32[]{:S(2)}, u32[]{:S(2)}) %collective-permute-start.4) | collective-permute-done | bytes 10272 | tf_op jit(solution)/shard_map/ppermute | solution.py:25
  32.2 0.8 select_add_fusion
  33.2 0.9 collective-permute-start.6
  34.1 0.9 collective-permute-start.7
  35.1 0.6 copy.51
  35.7 1.4 %collective-permute-done.6 = f32[160,128]{1,0:T(8,128)S(1)} collective-permute-done((f32[160,128]{1,0:T(8,128)S(1)}, f32[160,128]{1,0:T(8,128)S(1)}, u32[]{:S(2)}, u32[]{:S(2)}) %collective-permute-start.6) | collective-permute-done | bytes 81952 | tf_op jit(solution)/shard_map/ppermute | solution.py:23
  37.4 0.8 fusion.9
  38.3 0.6 fusion.37.table_ref
  38.9 3.8 %shard_map.320 = f32[4,8192]{1,0:T(4,128)} custom-call(s32[1,8192]{1,0:T(1,128)} %bitcast.168, f32[4,16,128]{2,1,0:T(8,128)} %fusion.37.table_ref), custom_call_target="tpu_custom_call" | custom-call | tf_op jit(solution)/shard_map/pallas_call | solution.py:196
  42.8 0.9 %broadcast_multiply_fusion = f32[4,32,256]{2,0,1:T(4,128)S(1)} fusion(f32[4,32,256]{2,0,1:T(4,128)} %bitcast.165, f32[32,256]{1,0:T(8,128)S(1)} %fusion.38), kind=kLoop, calls=%fused_computation.72 | loop fusion | flops 32768 | bytes 294912 | tf_op jit(solution)/shard_map/mul | solution.py:234
  43.7 14.3 %all_to_all.5 = f32[4,32,256]{2,0,1:T(4,128)S(1)} all-to-all(f32[4,32,256]{2,0,1:T(4,128)S(1)} %broadcast_multiply_fusion), channel_id=1, replica_groups=mesh['gx'=4,'gy'=8] {'gx','gy'}, dimensions={1} | all-to-all | bytes 262144 | tf_op jit(solution)/shard_map/all_to_all | solution.py:235
  58.1 0.7 reshape_reshape.3.table_ref
  58.8 6.5 %shard_map.321 = f32[4,8192]{1,0:T(4,128)} custom-call(s32[1,8192]{1,0:T(1,128)} %bitcast.177, f32[4,64,128]{2,1,0:T(8,128)} %reshape_reshape.3.table_ref), custom_call_target="tpu_custom_call" | custom-call | tf_op jit(solution)/shard_map/pallas_call | solution.py:196
  65.3 0.9 copy.52
  66.3 0.6 slice_reduce_fusion.7
  66.9 0.7 fusion.60
  68.9 2.1 %collective-permute-start.10 = (f32[10,128]{1,0:T(8,128)S(1)}, f32[10,128]{1,0:T(8,128)S(1)}, u32[]{:S(2)}, u32[]{:S(2)}) collective-permute-start(f32[10,128]{1,0:T(8,128)S(1)} %reshape_squeeze.46), channel_id=1, source_target_pairs={{0,7},{1,0},{2,1},{3,2},{4,3},{5,4},{6,5},{7,6},{8,15},{9,8},{10,9... | collective-permute-start | bytes 15368 | tf_op jit(solution)/shard_map/ppermute | solution.py:25
  71.2 0.5 collective-permute-start.9
  71.7 0.9 fusion.36
  72.7 4.8 %collective-permute-done.11 = f32[10,128]{1,0:T(8,128)S(1)} collective-permute-done((f32[10,128]{1,0:T(8,128)S(1)}, f32[10,128]{1,0:T(8,128)S(1)}, u32[]{:S(2)}, u32[]{:S(2)}) %collective-permute-start.11) | collective-permute-done | bytes 5152 | tf_op jit(solution)/shard_map/ppermute | solution.py:25
  77.6 1.9 %fusion.17 = f32[2,40,16,128]{3,2,1,0:T(8,128)S(1)} fusion(f32[2,40,16,128]{3,2,1,0:T(8,128)S(1)} %get-tuple-element.71, f32[2,40,16,128]{3,2,1,0:T(8,128)S(1)} %convolution_bitcast_fusion.8, f32[2,40,16,128]{3,2,1,0:T(8,128)S(1)} %fusion.63, f32[2,40,16,128]{3,2,1,0:T(8,128)S(1)} %fusion.64, f32[40,16,128]{2,1,0:T(8,128)} %get-tuple-element.69, ...), kind=kOutput, calls=%fused_computation.45 | convolution fusion | flops 19169280 | bytes 4025632 | tf_op jit(solution)/shard_map/ab,...by->...ay/dot_general | solution.py:120
  80.4 0.6 slice_reduce_fusion.5
  81.1 2.0 %collective-permute-start.14 = (f32[10,128]{1,0:T(8,128)S(1)}, f32[10,128]{1,0:T(8,128)S(1)}, u32[]{:S(2)}, u32[]{:S(2)}) collective-permute-start(f32[10,128]{1,0:T(8,128)S(1)} %reshape_squeeze.50), channel_id=1, source_target_pairs={{0,7},{1,0},{2,1},{3,2},{4,3},{5,4},{6,5},{7,6},{8,15},{9,8},{10,9... | collective-permute-start | bytes 15368 | tf_op jit(solution)/shard_map/ppermute | solution.py:25
  84.2 0.6 collective-permute-done.14
  84.9 4.7 %collective-permute-done.15 = f32[10,128]{1,0:T(8,128)S(1)} collective-permute-done((f32[10,128]{1,0:T(8,128)S(1)}, f32[10,128]{1,0:T(8,128)S(1)}, u32[]{:S(2)}, u32[]{:S(2)}) %collective-permute-start.15) | collective-permute-done | bytes 5152 | tf_op jit(solution)/shard_map/ppermute | solution.py:25
  89.8 2.4 %fusion.29 = f32[2,40,16,128]{3,2,1,0:T(8,128)} fusion(f32[2,40,16,128]{3,2,1,0:T(8,128)S(1)} %fusion.17, f32[2,40,16,128]{3,2,1,0:T(8,128)S(1)} %convolution_bitcast_fusion.6, f32[2,40,16,128]{3,2,1,0:T(8,128)S(1)} %fusion.65, f32[2,40,16,128]{3,2,1,0:T(8,128)S(1)} %fusion.66, f32[2,40,16]{2,1,0:T(8,128)S(1)} %broadcast_in_dim.278, ...), kind=kOutput, calls=%fused_computation.57 | convolution fusion | flops 19169280 | bytes 4025632 | tf_op jit(solution)/shard_map/ab,...by->...ay/dot_general | solution.py:120
  (108 shorter events, 6.7 us)
Async XLA Ops:
  0.6 0.7 copy-start.18
  0.6 0.7 copy-start.28
  0.7 0.9 copy-start.11
  0.7 1.3 %copy-start.1 = (f32[4,40,16,128]{3,2,1,0:T(8,128)S(1)}, f32[4,40,16,128]{3,2,1,0:T(8,128)}, u32[]{:S(2)}) copy-start(f32[4,40,16,128]{3,2,1,0:T(8,128)} %param.41) | copy-start | bytes 3932164
  0.7 0.8 copy-start.17
  2.7 0.8 copy-start.10
  3.5 0.8 copy-start.7
  4.4 0.8 copy-start.6
  7.1 7.7 %collective-permute-start = (f32[20,128]{1,0:T(8,128)S(1)}, f32[20,128]{1,0:T(8,128)S(1)}, u32[]{:S(2)}, u32[]{:S(2)}) collective-permute-start(f32[20,128]{1,0:T(8,128)S(1)} %reshape_squeeze.39), channel_id=1, source_target_pairs={{0,1},{1,2},{2,3},{3,4},{4,5},{5,6},{6,7},{7,0},{8,9},{9,10},{10,1... | collective-permute-start | bytes 30728 | tf_op jit(solution)/shard_map/ppermute | solution.py:25
  10.1 4.7 %collective-permute-start.1 = (f32[20,128]{1,0:T(8,128)S(1)}, f32[20,128]{1,0:T(8,128)S(1)}, u32[]{:S(2)}, u32[]{:S(2)}) collective-permute-start(f32[20,128]{1,0:T(8,128)S(1)} %reshape_squeeze.40), channel_id=1, source_target_pairs={{0,7},{1,0},{2,1},{3,2},{4,3},{5,4},{6,5},{7,6},{8,15},{9,8},{10,9... | collective-permute-start | bytes 30728 | tf_op jit(solution)/shard_map/ppermute | solution.py:25
  13.3 18.9 %copy-start.19 = (pred[128]{0:T(512)(128)(4,1)}, pred[128]{0:T(512)(128)(4,1)S(1)}, u32[]{:S(2)}) copy-start(pred[128]{0:T(512)(128)(4,1)S(1)} %get-tuple-element.76) | copy-start | bytes 388
  13.3 18.9 %copy-start.21 = (pred[128]{0:T(512)(128)(4,1)}, pred[128]{0:T(512)(128)(4,1)S(1)}, u32[]{:S(2)}) copy-start(pred[128]{0:T(512)(128)(4,1)S(1)} %get-tuple-element.77) | copy-start | bytes 388
  15.0 5.0 %copy-start.13 = (f32[16,128]{1,0:T(8,128)S(1)}, f32[16,128]{1,0:T(8,128)}, u32[]{:S(2)}) copy-start(f32[16,128]{1,0:T(8,128)} %constant.165) | copy-start | bytes 24580
  15.0 5.0 %copy-start.14 = (f32[16,16,1]{1,0,2:T(8,128)S(1)}, f32[16,16,1]{1,0,2:T(8,128)}, u32[]{:S(2)}) copy-start(f32[16,16,1]{1,0,2:T(8,128)} %constant.170) | copy-start | bytes 3076
  16.0 3.9 %collective-permute-start.2 = (f32[160,128]{1,0:T(8,128)S(1)}, f32[160,128]{1,0:T(8,128)S(1)}, u32[]{:S(2)}, u32[]{:S(2)}) collective-permute-start(f32[160,128]{1,0:T(8,128)S(1)} %bitcast.171), channel_id=1, source_target_pairs={{0,8},{8,16},{16,24},{24,0},{1,9},{9,17},{17,25},{25,1},{2,10},{10... | collective-permute-start | bytes 245768 | tf_op jit(solution)/shard_map/ppermute | solution.py:23
  16.0 4.0 %collective-permute-start.3 = (f32[160,128]{1,0:T(8,128)S(1)}, f32[160,128]{1,0:T(8,128)S(1)}, u32[]{:S(2)}, u32[]{:S(2)}) collective-permute-start(f32[160,128]{1,0:T(8,128)S(1)} %bitcast.169), channel_id=1, source_target_pairs={{0,24},{8,0},{16,8},{24,16},{1,25},{9,1},{17,9},{25,17},{2,26},{10... | collective-permute-start | bytes 245768 | tf_op jit(solution)/shard_map/ppermute | solution.py:23
  17.8 19.6 %copy-start.23 = (pred[16]{0:T(512)(128)(4,1)}, pred[16]{0:T(512)(128)(4,1)S(1)}, u32[]{:S(2)}) copy-start(pred[16]{0:T(512)(128)(4,1)S(1)} %get-tuple-element.78) | copy-start | bytes 52
  17.8 19.6 %copy-start.25 = (pred[16]{0:T(512)(128)(4,1)}, pred[16]{0:T(512)(128)(4,1)S(1)}, u32[]{:S(2)}) copy-start(pred[16]{0:T(512)(128)(4,1)S(1)} %get-tuple-element.79) | copy-start | bytes 52
  25.5 6.5 %collective-permute-start.4 = (f32[20,128]{1,0:T(8,128)S(1)}, f32[20,128]{1,0:T(8,128)S(1)}, u32[]{:S(2)}, u32[]{:S(2)}) collective-permute-start(f32[20,128]{1,0:T(8,128)S(1)} %reshape_squeeze.41), channel_id=1, source_target_pairs={{0,1},{1,2},{2,3},{3,4},{4,5},{5,6},{6,7},{7,0},{8,9},{9,10},{10,1... | collective-permute-start | bytes 30728 | tf_op jit(solution)/shard_map/ppermute | solution.py:25
  27.0 5.1 %collective-permute-start.5 = (f32[20,128]{1,0:T(8,128)S(1)}, f32[20,128]{1,0:T(8,128)S(1)}, u32[]{:S(2)}, u32[]{:S(2)}) collective-permute-start(f32[20,128]{1,0:T(8,128)S(1)} %reshape_squeeze.42), channel_id=1, source_target_pairs={{0,7},{1,0},{2,1},{3,2},{4,3},{5,4},{6,5},{7,6},{8,15},{9,8},{10,9... | collective-permute-start | bytes 30728 | tf_op jit(solution)/shard_map/ppermute | solution.py:25
  32.2 2.8 %copy-start.27 = (s32[1,32]{1,0:T(1,128)S(1)}, s32[1,32]{1,0:T(1,128)}, u32[]{:S(2)}) copy-start(s32[1,32]{1,0:T(1,128)} %param.44) | copy-start | bytes 388
  32.2 2.9 %copy-start.15 = (s32[1,32,256]{2,1,0:T(8,128)S(1)}, s32[1,32,256]{2,1,0:T(8,128)}, u32[]{:S(2)}) copy-start(s32[1,32,256]{2,1,0:T(8,128)} %param.43) | copy-start | bytes 98308
  33.2 3.9 %collective-permute-start.6 = (f32[160,128]{1,0:T(8,128)S(1)}, f32[160,128]{1,0:T(8,128)S(1)}, u32[]{:S(2)}, u32[]{:S(2)}) collective-permute-start(f32[160,128]{1,0:T(8,128)S(1)} %bitcast.172), channel_id=1, source_target_pairs={{0,8},{8,16},{16,24},{24,0},{1,9},{9,17},{17,25},{25,1},{2,10},{10... | collective-permute-start | bytes 245768 | tf_op jit(solution)/shard_map/ppermute | solution.py:23
  34.1 3.3 %collective-permute-start.7 = (f32[160,128]{1,0:T(8,128)S(1)}, f32[160,128]{1,0:T(8,128)S(1)}, u32[]{:S(2)}, u32[]{:S(2)}) collective-permute-start(f32[160,128]{1,0:T(8,128)S(1)} %bitcast.170), channel_id=1, source_target_pairs={{0,24},{8,0},{16,8},{24,16},{1,25},{9,1},{17,9},{25,17},{2,26},{10... | collective-permute-start | bytes 245768 | tf_op jit(solution)/shard_map/ppermute | solution.py:23
  38.3 28.6 %copy-start.3 = (f32[160,16,128]{2,1,0:T(8,128)}, f32[160,16,128]{2,1,0:T(8,128)S(1)}, u32[]{:S(2)}) copy-start(f32[160,16,128]{2,1,0:T(8,128)S(1)} %fusion.9) | copy-start | bytes 3932164
  38.3 27.9 %copy-start.16 = (f32[4,16,128]{2,1,0:T(8,128)S(1)}, f32[4,16,128]{2,1,0:T(8,128)}, u32[]{:S(2)}) copy-start(f32[4,16,128]{2,1,0:T(8,128)} %param.48) | copy-start | bytes 98308
  38.3 27.9 %copy-start = (f32[2,40,16,128]{3,2,1,0:T(8,128)S(1)}, f32[2,40,16,128]{3,2,1,0:T(8,128)}, u32[]{:S(2)}) copy-start(f32[2,40,16,128]{3,2,1,0:T(8,128)} %param.45) | copy-start | bytes 1966084
  38.3 27.9 %copy-start.2 = (f32[2,40,16,128]{3,2,1,0:T(8,128)S(1)}, f32[2,40,16,128]{3,2,1,0:T(8,128)}, u32[]{:S(2)}) copy-start(f32[2,40,16,128]{3,2,1,0:T(8,128)} %param.46) | copy-start | bytes 1966084
  58.1 9.5 %copy-start.12 = (f32[16,16,1,1]{1,0,3,2:T(8,128)S(1)}, f32[16,16,1,1]{1,0,3,2:T(8,128)}, u32[]{:S(2)}) copy-start(f32[16,16,1,1]{1,0,3,2:T(8,128)} %constant.173) | copy-start | bytes 3076
  66.3 1.7 %copy-start.9 = (f32[128,128,1,1]{1,0,3,2:T(8,128)S(1)}, f32[128,128,1,1]{1,0,3,2:T(8,128)}, u32[]{:S(2)}) copy-start(f32[128,128,1,1]{1,0,3,2:T(8,128)} %constant.172) | copy-start | bytes 196612
  67.6 0.8 copy-start.8
  68.9 3.7 %collective-permute-start.10 = (f32[10,128]{1,0:T(8,128)S(1)}, f32[10,128]{1,0:T(8,128)S(1)}, u32[]{:S(2)}, u32[]{:S(2)}) collective-permute-start(f32[10,128]{1,0:T(8,128)S(1)} %reshape_squeeze.46), channel_id=1, source_target_pairs={{0,7},{1,0},{2,1},{3,2},{4,3},{5,4},{6,5},{7,6},{8,15},{9,8},{10,9... | collective-permute-start | bytes 15368 | tf_op jit(solution)/shard_map/ppermute | solution.py:25
  71.1 6.4 %collective-permute-start.11 = (f32[10,128]{1,0:T(8,128)S(1)}, f32[10,128]{1,0:T(8,128)S(1)}, u32[]{:S(2)}, u32[]{:S(2)}) collective-permute-start(f32[10,128]{1,0:T(8,128)S(1)} %reshape_squeeze.47), channel_id=1, source_target_pairs={{0,1},{1,2},{2,3},{3,4},{4,5},{5,6},{6,7},{7,0},{8,9},{9,10},{10,1... | collective-permute-start | bytes 15368 | tf_op jit(solution)/shard_map/ppermute | solution.py:25
  71.1 6.4 %collective-permute-start.8 = (f32[80,128]{1,0:T(8,128)}, f32[80,128]{1,0:T(8,128)}, u32[]{:S(2)}, u32[]{:S(2)}) collective-permute-start(f32[80,128]{1,0:T(8,128)} %bitcast.174), channel_id=1, source_target_pairs={{0,24},{8,0},{16,8},{24,16},{1,25},{9,1},{17,9},{25,17},{2,26},{10... | collective-permute-start | bytes 122888 | tf_op jit(solution)/shard_map/ppermute | solution.py:23
  71.2 6.4 %collective-permute-start.9 = (f32[80,128]{1,0:T(8,128)S(1)}, f32[80,128]{1,0:T(8,128)}, u32[]{:S(2)}, u32[]{:S(2)}) collective-permute-start(f32[80,128]{1,0:T(8,128)S(1)} %bitcast.173), channel_id=1, source_target_pairs={{0,8},{8,16},{16,24},{24,0},{1,9},{9,17},{17,25},{25,1},{2,10},{10... | collective-permute-start | bytes 122888 | tf_op jit(solution)/shard_map/ppermute | solution.py:23
  80.3 9.4 %copy-start.4 = (f32[40,16,128]{2,1,0:T(8,128)S(1)}, f32[40,16,128]{2,1,0:T(8,128)}, u32[]{:S(2)}) copy-start(f32[40,16,128]{2,1,0:T(8,128)} %get-tuple-element.68) | copy-start | bytes 983044
  80.3 9.4 %copy-start.5 = (f32[40,16,128]{2,1,0:T(8,128)S(1)}, f32[40,16,128]{2,1,0:T(8,128)}, u32[]{:S(2)}) copy-start(f32[40,16,128]{2,1,0:T(8,128)} %get-tuple-element.69) | copy-start | bytes 983044
  80.3 9.4 %copy-start.20 = (pred[128]{0:T(512)(128)(4,1)S(1)}, pred[128]{0:T(512)(128)(4,1)}, u32[]{:S(2)}) copy-start(pred[128]{0:T(512)(128)(4,1)} %copy-done.19) | copy-start | bytes 388
  80.3 9.4 %copy-start.22 = (pred[128]{0:T(512)(128)(4,1)S(1)}, pred[128]{0:T(512)(128)(4,1)}, u32[]{:S(2)}) copy-start(pred[128]{0:T(512)(128)(4,1)} %copy-done.21) | copy-start | bytes 388
  80.3 9.4 %copy-start.24 = (pred[16]{0:T(512)(128)(4,1)S(1)}, pred[16]{0:T(512)(128)(4,1)}, u32[]{:S(2)}) copy-start(pred[16]{0:T(512)(128)(4,1)} %copy-done.23) | copy-start | bytes 52
  80.3 9.4 %copy-start.26 = (pred[16]{0:T(512)(128)(4,1)S(1)}, pred[16]{0:T(512)(128)(4,1)}, u32[]{:S(2)}) copy-start(pred[16]{0:T(512)(128)(4,1)} %copy-done.25) | copy-start | bytes 52
  80.4 9.4 %copy-start.29 = (f32[16,16,1,1]{1,0,3,2:T(8,128)S(1)}, f32[16,16,1,1]{1,0,3,2:T(8,128)}, u32[]{:S(2)}) copy-start(f32[16,16,1,1]{1,0,3,2:T(8,128)} %constant.171) | copy-start | bytes 3076
  81.1 3.7 %collective-permute-start.14 = (f32[10,128]{1,0:T(8,128)S(1)}, f32[10,128]{1,0:T(8,128)S(1)}, u32[]{:S(2)}, u32[]{:S(2)}) collective-permute-start(f32[10,128]{1,0:T(8,128)S(1)} %reshape_squeeze.50), channel_id=1, source_target_pairs={{0,7},{1,0},{2,1},{3,2},{4,3},{5,4},{6,5},{7,6},{8,15},{9,8},{10,9... | collective-permute-start | bytes 15368 | tf_op jit(solution)/shard_map/ppermute | solution.py:25
  83.2 6.4 %collective-permute-start.15 = (f32[10,128]{1,0:T(8,128)S(1)}, f32[10,128]{1,0:T(8,128)S(1)}, u32[]{:S(2)}, u32[]{:S(2)}) collective-permute-start(f32[10,128]{1,0:T(8,128)S(1)} %reshape_squeeze.51), channel_id=1, source_target_pairs={{0,1},{1,2},{2,3},{3,4},{4,5},{5,6},{6,7},{7,0},{8,9},{9,10},{10,1... | collective-permute-start | bytes 15368 | tf_op jit(solution)/shard_map/ppermute | solution.py:25
  83.3 6.4 %collective-permute-start.12 = (f32[80,128]{1,0:T(8,128)S(1)}, f32[80,128]{1,0:T(8,128)S(1)}, u32[]{:S(2)}, u32[]{:S(2)}) collective-permute-start(f32[80,128]{1,0:T(8,128)S(1)} %bitcast.176), channel_id=1, source_target_pairs={{0,24},{8,0},{16,8},{24,16},{1,25},{9,1},{17,9},{25,17},{2,26},{10... | collective-permute-start | bytes 122888 | tf_op jit(solution)/shard_map/ppermute | solution.py:23
  83.5 6.1 %collective-permute-start.13 = (f32[80,128]{1,0:T(8,128)S(1)}, f32[80,128]{1,0:T(8,128)}, u32[]{:S(2)}, u32[]{:S(2)}) collective-permute-start(f32[80,128]{1,0:T(8,128)S(1)} %bitcast.175), channel_id=1, source_target_pairs={{0,8},{8,16},{16,24},{24,0},{1,9},{9,17},{17,25},{25,1},{2,10},{10... | collective-permute-start | bytes 122888 | tf_op jit(solution)/shard_map/ppermute | solution.py:23

commit v12 on v11

--- a/solution.py
+++ b/solution.py
@@ -177,11 +177,10 @@
         piece = rest.astype(jnp.bfloat16)
         rest = rest - piece.astype(jnp.float32)
         parts.append(piece)
-    stacked = jnp.concatenate(parts, axis=1).reshape(fields * 3 * rows, 128)
-    picked = jnp.dot(stacked, onehot, preferred_element_type=jnp.float32)
+    stacked = jnp.concatenate(parts, axis=2).reshape(fields * rows, 3 * 128)
+    picked = jnp.dot(stacked, jnp.concatenate([onehot] * 3, axis=0), preferred_element_type=jnp.float32)
     for field in range(fields):
-        base = field * 3 * rows
-        whole = picked[base : base + rows] + picked[base + rows : base + 2 * rows] + picked[base + 2 * rows : base + 3 * rows]
+        whole = picked[field * rows : (field + 1) * rows]
         out_ref[pl.ds(field, 1), :] = jnp.sum(jnp.where(select, whole, 0.0), axis=0, keepdims=True)
 
 

time: 93 us -> 92.4 us (level)
  no operation moved by 1% of the time
where the time goes in v12:
time: 92.4 us; the launch traced here: 91.6 us
  starting transfers between devices  19.8 us (21%)
  waiting for transfers between devices  17.1 us (19%)
  matrix products  15.2 us (16%)
  blocking collectives  14.3 us (15%)
  Pallas kernels  9.81 us (11%)
  local copies, waits for them, and re-layouts  9.69 us (10%)
  other arithmetic  4.31 us (5%)
  between operations  1.35 us (1%)
    ppermute x8, starting transfers between devices, neighbour(): lax.ppermute(values, 'gy', [(j, (j + step_y) % count_y) for j in range(co...  15.1 us
    all_to_all x1, blocking collectives, per_device(): lax.all_to_all(payload, ('gx', 'gy'), split_axis=1, concat_axis=1, tiled=...  14.3 us
    ppermute x8, waiting for transfers between devices, neighbour(): lax.ppermute(values, 'gy', [(j, (j + step_y) % count_y) for j in range(co...  13.1 us
    pallas_call x2, Pallas kernels, onehot_gather(): pl.pallas_call(gather_kernel, grid=(count // tile,), in_specs=[pl.BlockSp...  9.81 us
    ppermute x8, starting transfers between devices, neighbour(): lax.ppermute(values, 'gx', [(i, (i + step_x) % count_x) for i in range(co...  4.71 us
    dot_general x2, matrix products, tracer_step(): jnp.einsum('ab,...by->...ay', sum_x, tracers, precision=precision)  4.24 us
    ppermute x8, waiting for transfers between devices, neighbour(): lax.ppermute(values, 'gx', [(i, (i + step_x) % count_x) for i in range(co...  3.93 us
    unnamed x62, local copies, waits for them, and re-layouts  3.35 us
  transfers between devices with their start and end apart: 16, of which 10 were waited for; matrix products, arithmetic and copies ran while one was open for 3% of the time, Pallas kernels for 0%

profile of v12, /device:TPU:0, one launch (start us, length us, event | category | flops | bytes accessed | tf_op | source)
XLA Modules:
  0.0 91.6 jit_solution(10366054105604246032)
XLA Ops:
  0.7 0.6 copy-done.18
  2.0 0.7 fusion.10
  2.7 0.7 convolution_bitcast_fusion.5
  3.5 0.7 fusion.61
  4.4 0.7 fusion.2
  5.2 0.7 fusion.1
  5.9 1.1 %slice_reduce_fusion.3 = (f32[160,16]{1,0:T(8,128)S(1)}, f32[160,16]{1,0:T(8,128)S(1)}) fusion(f32[160,16,128]{2,1,0:T(8,128)S(1)} %fusion.1), kind=kLoop, calls=%fused_computation.24 | loop fusion | bytes 40960 | tf_op jit(solution)/shard_map/slice | solution.py:87
  7.1 3.0 %collective-permute-start = (f32[20,128]{1,0:T(8,128)S(1)}, f32[20,128]{1,0:T(8,128)S(1)}, u32[]{:S(2)}, u32[]{:S(2)}) collective-permute-start(f32[20,128]{1,0:T(8,128)S(1)} %reshape_squeeze.39), channel_id=1, source_target_pairs={{0,1},{1,2},{2,3},{3,4},{4,5},{5,6},{6,7},{7,0},{8,9},{9,10},{10,1... | collective-permute-start | bytes 30728 | tf_op jit(solution)/shard_map/ppermute | solution.py:25
  10.1 3.1 %collective-permute-start.1 = (f32[20,128]{1,0:T(8,128)S(1)}, f32[20,128]{1,0:T(8,128)S(1)}, u32[]{:S(2)}, u32[]{:S(2)}) collective-permute-start(f32[20,128]{1,0:T(8,128)S(1)} %reshape_squeeze.40), channel_id=1, source_target_pairs={{0,7},{1,0},{2,1},{3,2},{4,3},{5,4},{6,5},{7,6},{8,15},{9,8},{10,9... | collective-permute-start | bytes 30728 | tf_op jit(solution)/shard_map/ppermute | solution.py:25
  13.3 1.5 %collective-permute-done = f32[20,128]{1,0:T(8,128)S(1)} collective-permute-done((f32[20,128]{1,0:T(8,128)S(1)}, f32[20,128]{1,0:T(8,128)S(1)}, u32[]{:S(2)}, u32[]{:S(2)}) %collective-permute-start) | collective-permute-done | bytes 10272 | tf_op jit(solution)/shard_map/ppermute | solution.py:25
  15.0 0.8 select_add_fusion.1
  16.0 1.7 %collective-permute-start.3 = (f32[160,128]{1,0:T(8,128)S(1)}, f32[160,128]{1,0:T(8,128)S(1)}, u32[]{:S(2)}, u32[]{:S(2)}) collective-permute-start(f32[160,128]{1,0:T(8,128)S(1)} %bitcast.169), channel_id=1, source_target_pairs={{0,24},{8,0},{16,8},{24,16},{1,25},{9,1},{17,9},{25,17},{2,26},{10... | collective-permute-start | bytes 245768 | tf_op jit(solution)/shard_map/ppermute | solution.py:23
  17.8 2.1 %collective-permute-done.2 = f32[160,128]{1,0:T(8,128)S(1)} collective-permute-done((f32[160,128]{1,0:T(8,128)S(1)}, f32[160,128]{1,0:T(8,128)S(1)}, u32[]{:S(2)}, u32[]{:S(2)}) %collective-permute-start.2) | collective-permute-done | bytes 81952 | tf_op jit(solution)/shard_map/ppermute | solution.py:23
  20.0 0.8 fusion.5
  20.8 0.7 fusion.6
  21.5 0.7 convolution_multiply_fusion.1
  22.2 0.7 convolution_bitcast_fusion.2
  22.9 0.7 fusion.62
  23.6 0.7 fusion
  24.3 1.1 %slice_reduce_fusion.1 = (f32[160,16]{1,0:T(8,128)S(1)}, f32[160,16]{1,0:T(8,128)S(1)}) fusion(f32[160,16,128]{2,1,0:T(8,128)S(1)} %fusion), kind=kLoop, calls=%fused_computation.22 | loop fusion | bytes 40960 | tf_op jit(solution)/shard_map/slice | solution.py:87
  25.5 1.4 %collective-permute-start.4 = (f32[20,128]{1,0:T(8,128)S(1)}, f32[20,128]{1,0:T(8,128)S(1)}, u32[]{:S(2)}, u32[]{:S(2)}) collective-permute-start(f32[20,128]{1,0:T(8,128)S(1)} %reshape_squeeze.41), channel_id=1, source_target_pairs={{0,1},{1,2},{2,3},{3,4},{4,5},{5,6},{6,7},{7,0},{8,9},{9,10},{10,1... | collective-permute-start | bytes 30728 | tf_op jit(solution)/shard_map/ppermute | solution.py:25
  27.0 3.4 %collective-permute-start.5 = (f32[20,128]{1,0:T(8,128)S(1)}, f32[20,128]{1,0:T(8,128)S(1)}, u32[]{:S(2)}, u32[]{:S(2)}) collective-permute-start(f32[20,128]{1,0:T(8,128)S(1)} %reshape_squeeze.42), channel_id=1, source_target_pairs={{0,7},{1,0},{2,1},{3,2},{4,3},{5,4},{6,5},{7,6},{8,15},{9,8},{10,9... | collective-permute-start | bytes 30728 | tf_op jit(solution)/shard_map/ppermute | solution.py:25
  30.4 1.5 %collective-permute-done.4 = f32[20,128]{1,0:T(8,128)S(1)} collective-permute-done((f32[20,128]{1,0:T(8,128)S(1)}, f32[20,128]{1,0:T(8,128)S(1)}, u32[]{:S(2)}, u32[]{:S(2)}) %collective-permute-start.4) | collective-permute-done | bytes 10272 | tf_op jit(solution)/shard_map/ppermute | solution.py:25
  32.2 0.8 select_add_fusion
  33.2 0.9 collective-permute-start.6
  34.1 0.9 collective-permute-start.7
  35.1 0.6 copy.51
  35.7 1.4 %collective-permute-done.6 = f32[160,128]{1,0:T(8,128)S(1)} collective-permute-done((f32[160,128]{1,0:T(8,128)S(1)}, f32[160,128]{1,0:T(8,128)S(1)}, u32[]{:S(2)}, u32[]{:S(2)}) %collective-permute-start.6) | collective-permute-done | bytes 81952 | tf_op jit(solution)/shard_map/ppermute | solution.py:23
  37.4 0.8 fusion.9
  38.3 0.6 fusion.37.table_ref
  38.9 3.8 %shard_map.320 = f32[4,8192]{1,0:T(4,128)} custom-call(s32[1,8192]{1,0:T(1,128)} %bitcast.168, f32[4,16,128]{2,1,0:T(8,128)} %fusion.37.table_ref), custom_call_target="tpu_custom_call" | custom-call | tf_op jit(solution)/shard_map/pallas_call | solution.py:195
  42.7 0.9 %broadcast_multiply_fusion = f32[4,32,256]{2,0,1:T(4,128)S(1)} fusion(f32[4,32,256]{2,0,1:T(4,128)} %bitcast.165, f32[32,256]{1,0:T(8,128)S(1)} %fusion.38), kind=kLoop, calls=%fused_computation.72 | loop fusion | flops 32768 | bytes 294912 | tf_op jit(solution)/shard_map/mul | solution.py:233
  43.7 14.3 %all_to_all.5 = f32[4,32,256]{2,0,1:T(4,128)S(1)} all-to-all(f32[4,32,256]{2,0,1:T(4,128)S(1)} %broadcast_multiply_fusion), channel_id=1, replica_groups=mesh['gx'=4,'gy'=8] {'gx','gy'}, dimensions={1} | all-to-all | bytes 262144 | tf_op jit(solution)/shard_map/all_to_all | solution.py:234
  58.1 0.7 reshape_reshape.3.table_ref
  58.7 6.0 %shard_map.321 = f32[4,8192]{1,0:T(4,128)} custom-call(s32[1,8192]{1,0:T(1,128)} %bitcast.177, f32[4,64,128]{2,1,0:T(8,128)} %reshape_reshape.3.table_ref), custom_call_target="tpu_custom_call" | custom-call | tf_op jit(solution)/shard_map/pallas_call | solution.py:195
  64.7 0.9 copy.52
  65.8 0.6 slice_reduce_fusion.7
  66.4 0.7 fusion.60
  68.4 2.1 %collective-permute-start.10 = (f32[10,128]{1,0:T(8,128)S(1)}, f32[10,128]{1,0:T(8,128)S(1)}, u32[]{:S(2)}, u32[]{:S(2)}) collective-permute-start(f32[10,128]{1,0:T(8,128)S(1)} %reshape_squeeze.46), channel_id=1, source_target_pairs={{0,7},{1,0},{2,1},{3,2},{4,3},{5,4},{6,5},{7,6},{8,15},{9,8},{10,9... | collective-permute-start | bytes 15368 | tf_op jit(solution)/shard_map/ppermute | solution.py:25
  70.7 0.5 collective-permute-start.9
  71.2 0.9 fusion.36
  72.2 4.8 %collective-permute-done.11 = f32[10,128]{1,0:T(8,128)S(1)} collective-permute-done((f32[10,128]{1,0:T(8,128)S(1)}, f32[10,128]{1,0:T(8,128)S(1)}, u32[]{:S(2)}, u32[]{:S(2)}) %collective-permute-start.11) | collective-permute-done | bytes 5152 | tf_op jit(solution)/shard_map/ppermute | solution.py:25
  77.0 1.9 %fusion.17 = f32[2,40,16,128]{3,2,1,0:T(8,128)S(1)} fusion(f32[2,40,16,128]{3,2,1,0:T(8,128)S(1)} %get-tuple-element.71, f32[2,40,16,128]{3,2,1,0:T(8,128)S(1)} %convolution_bitcast_fusion.8, f32[2,40,16,128]{3,2,1,0:T(8,128)S(1)} %fusion.63, f32[2,40,16,128]{3,2,1,0:T(8,128)S(1)} %fusion.64, f32[40,16,128]{2,1,0:T(8,128)} %get-tuple-element.69, ...), kind=kOutput, calls=%fused_computation.45 | convolution fusion | flops 19169280 | bytes 4025632 | tf_op jit(solution)/shard_map/ab,...by->...ay/dot_general | solution.py:120
  79.8 0.6 slice_reduce_fusion.5
  80.6 2.0 %collective-permute-start.14 = (f32[10,128]{1,0:T(8,128)S(1)}, f32[10,128]{1,0:T(8,128)S(1)}, u32[]{:S(2)}, u32[]{:S(2)}) collective-permute-start(f32[10,128]{1,0:T(8,128)S(1)} %reshape_squeeze.50), channel_id=1, source_target_pairs={{0,7},{1,0},{2,1},{3,2},{4,3},{5,4},{6,5},{7,6},{8,15},{9,8},{10,9... | collective-permute-start | bytes 15368 | tf_op jit(solution)/shard_map/ppermute | solution.py:25
  83.7 0.6 collective-permute-done.14
  84.3 4.7 %collective-permute-done.15 = f32[10,128]{1,0:T(8,128)S(1)} collective-permute-done((f32[10,128]{1,0:T(8,128)S(1)}, f32[10,128]{1,0:T(8,128)S(1)}, u32[]{:S(2)}, u32[]{:S(2)}) %collective-permute-start.15) | collective-permute-done | bytes 5152 | tf_op jit(solution)/shard_map/ppermute | solution.py:25
  89.2 2.4 %fusion.29 = f32[2,40,16,128]{3,2,1,0:T(8,128)} fusion(f32[2,40,16,128]{3,2,1,0:T(8,128)S(1)} %fusion.17, f32[2,40,16,128]{3,2,1,0:T(8,128)S(1)} %convolution_bitcast_fusion.6, f32[2,40,16,128]{3,2,1,0:T(8,128)S(1)} %fusion.65, f32[2,40,16,128]{3,2,1,0:T(8,128)S(1)} %fusion.66, f32[2,40,16]{2,1,0:T(8,128)S(1)} %broadcast_in_dim.278, ...), kind=kOutput, calls=%fused_computation.57 | convolution fusion | flops 19169280 | bytes 4025632 | tf_op jit(solution)/shard_map/ab,...by->...ay/dot_general | solution.py:120
  (108 shorter events, 6.7 us)
Async XLA Ops:
  0.6 0.7 copy-start.18
  0.6 0.7 copy-start.28
  0.7 0.9 %copy-start.11 = (f32[16,16,1]{1,0,2:T(8,128)S(1)}, f32[16,16,1]{1,0,2:T(8,128)}, u32[]{:S(2)}) copy-start(f32[16,16,1]{1,0,2:T(8,128)} %constant.166) | copy-start | bytes 3076
  0.7 1.3 %copy-start.1 = (f32[4,40,16,128]{3,2,1,0:T(8,128)S(1)}, f32[4,40,16,128]{3,2,1,0:T(8,128)}, u32[]{:S(2)}) copy-start(f32[4,40,16,128]{3,2,1,0:T(8,128)} %param.41) | copy-start | bytes 3932164
  0.7 0.8 copy-start.17
  2.7 0.8 copy-start.10
  3.5 0.8 copy-start.7
  4.4 0.8 copy-start.6
  7.1 7.7 %collective-permute-start = (f32[20,128]{1,0:T(8,128)S(1)}, f32[20,128]{1,0:T(8,128)S(1)}, u32[]{:S(2)}, u32[]{:S(2)}) collective-permute-start(f32[20,128]{1,0:T(8,128)S(1)} %reshape_squeeze.39), channel_id=1, source_target_pairs={{0,1},{1,2},{2,3},{3,4},{4,5},{5,6},{6,7},{7,0},{8,9},{9,10},{10,1... | collective-permute-start | bytes 30728 | tf_op jit(solution)/shard_map/ppermute | solution.py:25
  10.1 4.7 %collective-permute-start.1 = (f32[20,128]{1,0:T(8,128)S(1)}, f32[20,128]{1,0:T(8,128)S(1)}, u32[]{:S(2)}, u32[]{:S(2)}) collective-permute-start(f32[20,128]{1,0:T(8,128)S(1)} %reshape_squeeze.40), channel_id=1, source_target_pairs={{0,7},{1,0},{2,1},{3,2},{4,3},{5,4},{6,5},{7,6},{8,15},{9,8},{10,9... | collective-permute-start | bytes 30728 | tf_op jit(solution)/shard_map/ppermute | solution.py:25
  13.3 18.9 %copy-start.19 = (pred[128]{0:T(512)(128)(4,1)}, pred[128]{0:T(512)(128)(4,1)S(1)}, u32[]{:S(2)}) copy-start(pred[128]{0:T(512)(128)(4,1)S(1)} %get-tuple-element.76) | copy-start | bytes 388
  13.3 18.9 %copy-start.21 = (pred[128]{0:T(512)(128)(4,1)}, pred[128]{0:T(512)(128)(4,1)S(1)}, u32[]{:S(2)}) copy-start(pred[128]{0:T(512)(128)(4,1)S(1)} %get-tuple-element.77) | copy-start | bytes 388
  15.0 5.0 %copy-start.13 = (f32[16,128]{1,0:T(8,128)S(1)}, f32[16,128]{1,0:T(8,128)}, u32[]{:S(2)}) copy-start(f32[16,128]{1,0:T(8,128)} %constant.165) | copy-start | bytes 24580
  15.0 5.0 %copy-start.14 = (f32[16,16,1]{1,0,2:T(8,128)S(1)}, f32[16,16,1]{1,0,2:T(8,128)}, u32[]{:S(2)}) copy-start(f32[16,16,1]{1,0,2:T(8,128)} %constant.170) | copy-start | bytes 3076
  16.0 3.9 %collective-permute-start.2 = (f32[160,128]{1,0:T(8,128)S(1)}, f32[160,128]{1,0:T(8,128)S(1)}, u32[]{:S(2)}, u32[]{:S(2)}) collective-permute-start(f32[160,128]{1,0:T(8,128)S(1)} %bitcast.171), channel_id=1, source_target_pairs={{0,8},{8,16},{16,24},{24,0},{1,9},{9,17},{17,25},{25,1},{2,10},{10... | collective-permute-start | bytes 245768 | tf_op jit(solution)/shard_map/ppermute | solution.py:23
  16.0 4.0 %collective-permute-start.3 = (f32[160,128]{1,0:T(8,128)S(1)}, f32[160,128]{1,0:T(8,128)S(1)}, u32[]{:S(2)}, u32[]{:S(2)}) collective-permute-start(f32[160,128]{1,0:T(8,128)S(1)} %bitcast.169), channel_id=1, source_target_pairs={{0,24},{8,0},{16,8},{24,16},{1,25},{9,1},{17,9},{25,17},{2,26},{10... | collective-permute-start | bytes 245768 | tf_op jit(solution)/shard_map/ppermute | solution.py:23
  17.8 19.6 %copy-start.23 = (pred[16]{0:T(512)(128)(4,1)}, pred[16]{0:T(512)(128)(4,1)S(1)}, u32[]{:S(2)}) copy-start(pred[16]{0:T(512)(128)(4,1)S(1)} %get-tuple-element.78) | copy-start | bytes 52
  17.8 19.6 %copy-start.25 = (pred[16]{0:T(512)(128)(4,1)}, pred[16]{0:T(512)(128)(4,1)S(1)}, u32[]{:S(2)}) copy-start(pred[16]{0:T(512)(128)(4,1)S(1)} %get-tuple-element.79) | copy-start | bytes 52
  25.5 6.5 %collective-permute-start.4 = (f32[20,128]{1,0:T(8,128)S(1)}, f32[20,128]{1,0:T(8,128)S(1)}, u32[]{:S(2)}, u32[]{:S(2)}) collective-permute-start(f32[20,128]{1,0:T(8,128)S(1)} %reshape_squeeze.41), channel_id=1, source_target_pairs={{0,1},{1,2},{2,3},{3,4},{4,5},{5,6},{6,7},{7,0},{8,9},{9,10},{10,1... | collective-permute-start | bytes 30728 | tf_op jit(solution)/shard_map/ppermute | solution.py:25
  27.0 5.1 %collective-permute-start.5 = (f32[20,128]{1,0:T(8,128)S(1)}, f32[20,128]{1,0:T(8,128)S(1)}, u32[]{:S(2)}, u32[]{:S(2)}) collective-permute-start(f32[20,128]{1,0:T(8,128)S(1)} %reshape_squeeze.42), channel_id=1, source_target_pairs={{0,7},{1,0},{2,1},{3,2},{4,3},{5,4},{6,5},{7,6},{8,15},{9,8},{10,9... | collective-permute-start | bytes 30728 | tf_op jit(solution)/shard_map/ppermute | solution.py:25
  32.2 2.8 %copy-start.27 = (s32[1,32]{1,0:T(1,128)S(1)}, s32[1,32]{1,0:T(1,128)}, u32[]{:S(2)}) copy-start(s32[1,32]{1,0:T(1,128)} %param.44) | copy-start | bytes 388
  32.2 2.9 %copy-start.15 = (s32[1,32,256]{2,1,0:T(8,128)S(1)}, s32[1,32,256]{2,1,0:T(8,128)}, u32[]{:S(2)}) copy-start(s32[1,32,256]{2,1,0:T(8,128)} %param.43) | copy-start | bytes 98308
  33.2 3.9 %collective-permute-start.6 = (f32[160,128]{1,0:T(8,128)S(1)}, f32[160,128]{1,0:T(8,128)S(1)}, u32[]{:S(2)}, u32[]{:S(2)}) collective-permute-start(f32[160,128]{1,0:T(8,128)S(1)} %bitcast.172), channel_id=1, source_target_pairs={{0,8},{8,16},{16,24},{24,0},{1,9},{9,17},{17,25},{25,1},{2,10},{10... | collective-permute-start | bytes 245768 | tf_op jit(solution)/shard_map/ppermute | solution.py:23
  34.1 3.3 %collective-permute-start.7 = (f32[160,128]{1,0:T(8,128)S(1)}, f32[160,128]{1,0:T(8,128)S(1)}, u32[]{:S(2)}, u32[]{:S(2)}) collective-permute-start(f32[160,128]{1,0:T(8,128)S(1)} %bitcast.170), channel_id=1, source_target_pairs={{0,24},{8,0},{16,8},{24,16},{1,25},{9,1},{17,9},{25,17},{2,26},{10... | collective-permute-start | bytes 245768 | tf_op jit(solution)/shard_map/ppermute | solution.py:23
  38.3 28.1 %copy-start.3 = (f32[160,16,128]{2,1,0:T(8,128)}, f32[160,16,128]{2,1,0:T(8,128)S(1)}, u32[]{:S(2)}) copy-start(f32[160,16,128]{2,1,0:T(8,128)S(1)} %fusion.9) | copy-start | bytes 3932164
  38.3 27.4 %copy-start.16 = (f32[4,16,128]{2,1,0:T(8,128)S(1)}, f32[4,16,128]{2,1,0:T(8,128)}, u32[]{:S(2)}) copy-start(f32[4,16,128]{2,1,0:T(8,128)} %param.48) | copy-start | bytes 98308
  38.3 27.4 %copy-start = (f32[2,40,16,128]{3,2,1,0:T(8,128)S(1)}, f32[2,40,16,128]{3,2,1,0:T(8,128)}, u32[]{:S(2)}) copy-start(f32[2,40,16,128]{3,2,1,0:T(8,128)} %param.45) | copy-start | bytes 1966084
  38.3 27.4 %copy-start.2 = (f32[2,40,16,128]{3,2,1,0:T(8,128)S(1)}, f32[2,40,16,128]{3,2,1,0:T(8,128)}, u32[]{:S(2)}) copy-start(f32[2,40,16,128]{3,2,1,0:T(8,128)} %param.46) | copy-start | bytes 1966084
  58.0 9.0 %copy-start.12 = (f32[16,16,1,1]{1,0,3,2:T(8,128)S(1)}, f32[16,16,1,1]{1,0,3,2:T(8,128)}, u32[]{:S(2)}) copy-start(f32[16,16,1,1]{1,0,3,2:T(8,128)} %constant.173) | copy-start | bytes 3076
  65.7 1.7 %copy-start.9 = (f32[128,128,1,1]{1,0,3,2:T(8,128)S(1)}, f32[128,128,1,1]{1,0,3,2:T(8,128)}, u32[]{:S(2)}) copy-start(f32[128,128,1,1]{1,0,3,2:T(8,128)} %constant.172) | copy-start | bytes 196612
  67.1 0.8 copy-start.8
  68.4 3.7 %collective-permute-start.10 = (f32[10,128]{1,0:T(8,128)S(1)}, f32[10,128]{1,0:T(8,128)S(1)}, u32[]{:S(2)}, u32[]{:S(2)}) collective-permute-start(f32[10,128]{1,0:T(8,128)S(1)} %reshape_squeeze.46), channel_id=1, source_target_pairs={{0,7},{1,0},{2,1},{3,2},{4,3},{5,4},{6,5},{7,6},{8,15},{9,8},{10,9... | collective-permute-start | bytes 15368 | tf_op jit(solution)/shard_map/ppermute | solution.py:25
  70.6 6.4 %collective-permute-start.11 = (f32[10,128]{1,0:T(8,128)S(1)}, f32[10,128]{1,0:T(8,128)S(1)}, u32[]{:S(2)}, u32[]{:S(2)}) collective-permute-start(f32[10,128]{1,0:T(8,128)S(1)} %reshape_squeeze.47), channel_id=1, source_target_pairs={{0,1},{1,2},{2,3},{3,4},{4,5},{5,6},{6,7},{7,0},{8,9},{9,10},{10,1... | collective-permute-start | bytes 15368 | tf_op jit(solution)/shard_map/ppermute | solution.py:25
  70.6 6.4 %collective-permute-start.8 = (f32[80,128]{1,0:T(8,128)}, f32[80,128]{1,0:T(8,128)}, u32[]{:S(2)}, u32[]{:S(2)}) collective-permute-start(f32[80,128]{1,0:T(8,128)} %bitcast.174), channel_id=1, source_target_pairs={{0,24},{8,0},{16,8},{24,16},{1,25},{9,1},{17,9},{25,17},{2,26},{10... | collective-permute-start | bytes 122888 | tf_op jit(solution)/shard_map/ppermute | solution.py:23
  70.7 6.4 %collective-permute-start.9 = (f32[80,128]{1,0:T(8,128)S(1)}, f32[80,128]{1,0:T(8,128)}, u32[]{:S(2)}, u32[]{:S(2)}) collective-permute-start(f32[80,128]{1,0:T(8,128)S(1)} %bitcast.173), channel_id=1, source_target_pairs={{0,8},{8,16},{16,24},{24,0},{1,9},{9,17},{17,25},{25,1},{2,10},{10... | collective-permute-start | bytes 122888 | tf_op jit(solution)/shard_map/ppermute | solution.py:23
  79.8 9.4 %copy-start.4 = (f32[40,16,128]{2,1,0:T(8,128)S(1)}, f32[40,16,128]{2,1,0:T(8,128)}, u32[]{:S(2)}) copy-start(f32[40,16,128]{2,1,0:T(8,128)} %get-tuple-element.68) | copy-start | bytes 983044
  79.8 9.4 %copy-start.5 = (f32[40,16,128]{2,1,0:T(8,128)S(1)}, f32[40,16,128]{2,1,0:T(8,128)}, u32[]{:S(2)}) copy-start(f32[40,16,128]{2,1,0:T(8,128)} %get-tuple-element.69) | copy-start | bytes 983044
  79.8 9.4 %copy-start.20 = (pred[128]{0:T(512)(128)(4,1)S(1)}, pred[128]{0:T(512)(128)(4,1)}, u32[]{:S(2)}) copy-start(pred[128]{0:T(512)(128)(4,1)} %copy-done.19) | copy-start | bytes 388
  79.8 9.4 %copy-start.22 = (pred[128]{0:T(512)(128)(4,1)S(1)}, pred[128]{0:T(512)(128)(4,1)}, u32[]{:S(2)}) copy-start(pred[128]{0:T(512)(128)(4,1)} %copy-done.21) | copy-start | bytes 388
  79.8 9.4 %copy-start.24 = (pred[16]{0:T(512)(128)(4,1)S(1)}, pred[16]{0:T(512)(128)(4,1)}, u32[]{:S(2)}) copy-start(pred[16]{0:T(512)(128)(4,1)} %copy-done.23) | copy-start | bytes 52
  79.8 9.4 %copy-start.26 = (pred[16]{0:T(512)(128)(4,1)S(1)}, pred[16]{0:T(512)(128)(4,1)}, u32[]{:S(2)}) copy-start(pred[16]{0:T(512)(128)(4,1)} %copy-done.25) | copy-start | bytes 52
  79.8 9.4 %copy-start.29 = (f32[16,16,1,1]{1,0,3,2:T(8,128)S(1)}, f32[16,16,1,1]{1,0,3,2:T(8,128)}, u32[]{:S(2)}) copy-start(f32[16,16,1,1]{1,0,3,2:T(8,128)} %constant.171) | copy-start | bytes 3076
  80.6 3.7 %collective-permute-start.14 = (f32[10,128]{1,0:T(8,128)S(1)}, f32[10,128]{1,0:T(8,128)S(1)}, u32[]{:S(2)}, u32[]{:S(2)}) collective-permute-start(f32[10,128]{1,0:T(8,128)S(1)} %reshape_squeeze.50), channel_id=1, source_target_pairs={{0,7},{1,0},{2,1},{3,2},{4,3},{5,4},{6,5},{7,6},{8,15},{9,8},{10,9... | collective-permute-start | bytes 15368 | tf_op jit(solution)/shard_map/ppermute | solution.py:25
  82.7 6.4 %collective-permute-start.15 = (f32[10,128]{1,0:T(8,128)S(1)}, f32[10,128]{1,0:T(8,128)S(1)}, u32[]{:S(2)}, u32[]{:S(2)}) collective-permute-start(f32[10,128]{1,0:T(8,128)S(1)} %reshape_squeeze.51), channel_id=1, source_target_pairs={{0,1},{1,2},{2,3},{3,4},{4,5},{5,6},{6,7},{7,0},{8,9},{9,10},{10,1... | collective-permute-start | bytes 15368 | tf_op jit(solution)/shard_map/ppermute | solution.py:25
  82.7 6.4 %collective-permute-start.12 = (f32[80,128]{1,0:T(8,128)S(1)}, f32[80,128]{1,0:T(8,128)S(1)}, u32[]{:S(2)}, u32[]{:S(2)}) collective-permute-start(f32[80,128]{1,0:T(8,128)S(1)} %bitcast.176), channel_id=1, source_target_pairs={{0,24},{8,0},{16,8},{24,16},{1,25},{9,1},{17,9},{25,17},{2,26},{10... | collective-permute-start | bytes 122888 | tf_op jit(solution)/shard_map/ppermute | solution.py:23
  83.0 6.1 %collective-permute-start.13 = (f32[80,128]{1,0:T(8,128)S(1)}, f32[80,128]{1,0:T(8,128)}, u32[]{:S(2)}, u32[]{:S(2)}) collective-permute-start(f32[80,128]{1,0:T(8,128)S(1)} %bitcast.175), channel_id=1, source_target_pairs={{0,8},{8,16},{16,24},{24,0},{1,9},{9,17},{17,25},{25,1},{2,10},{10... | collective-permute-start | bytes 122888 | tf_op jit(solution)/shard_map/ppermute | solution.py:23

commit v13 on v12

--- a/solution.py
+++ b/solution.py
@@ -53,6 +53,16 @@
     return neighbour(packed(values), step_x, step_y).reshape(values.shape)
 
 
+def exchange_many(pieces, step_x, step_y):
+    flat = [piece.reshape(-1, piece.shape[-1]) for piece in pieces]
+    got = neighbour(jnp.concatenate(flat, axis=0), step_x, step_y)
+    out, start = [], 0
+    for piece, part in zip(pieces, flat):
+        out.append(got[start : start + part.shape[0]].reshape(piece.shape))
+        start += part.shape[0]
+    return out
+
+
 def pair_matrix(size):
     position = np.arange(size)
     starts = position[position % 4 == 0][1:]
@@ -63,7 +73,7 @@
     return pair
 
 
-def substep(state_in, metric, derivative_np, weights_np, inv_mass):
+def substep(state_in, metric, derivative_np, weights_np, inv_mass, tracers, velocity):
     levels, xsize, ysize = state_in.shape
     precision = lax.Precision.HIGH
     block_x = np.kron(np.eye(xsize // 4), derivative_np)
@@ -84,27 +94,35 @@
         "lxc,cd->lxd", scaled_y, term_y_right, precision=precision
     ) * jnp.asarray(weight_x[:, None], jnp.float32)
     last_x, last_y = xsize - 1, ysize - 1
-    from_left = exchange(merged[:, :, last_y], 0, 1)[:, :, None]
-    from_right = exchange(merged[:, :, 0], 0, -1)[:, :, None]
+    ocean_x, ocean_y = tracers.shape[-2] - 1, tracers.shape[-1] - 1
+    from_left, sea_left = exchange_many([merged[:, :, last_y], tracers[..., ocean_y]], 0, 1)
+    from_right, sea_right = exchange_many([merged[:, :, 0], tracers[..., 0]], 0, -1)
     column = jnp.arange(ysize)
-    merged = merged + jnp.where(column == 0, from_left, jnp.where(column == last_y, from_right, 0.0))
-    from_up = exchange(merged[:, last_x, :], 1, 0)[:, None, :]
-    from_down = exchange(merged[:, 0, :], -1, 0)[:, None, :]
+    merged = merged + jnp.where(column == 0, from_left[:, :, None], jnp.where(column == last_y, from_right[:, :, None], 0.0))
+    from_up, sea_up = exchange_many([merged[:, last_x, :], tracers[..., ocean_x, :]], 1, 0)
+    from_down, sea_down = exchange_many([merged[:, 0, :], tracers[..., 0, :]], -1, 0)
+    from_up, from_down = from_up[:, None, :], from_down[:, None, :]
+    halos = (sea_up[..., None, :], sea_down[..., None, :], sea_left[..., None], sea_right[..., None])
+    tracers = tracer_step(tracers, velocity, halos)
     row = jnp.arange(xsize)[:, None]
     total = jnp.einsum("ab,lby->lay", pair_x, merged, precision=precision) + jnp.where(
         row == 0, from_up, jnp.where(row == last_x, from_down, 0.0)
     )
-    return state_in - visc_coef * total * inv_mass
-
-
-def tracer_step(tracers, velocity):
+    return state_in - visc_coef * total * inv_mass, tracers
+
+
+def tracer_step(tracers, velocity, halos=None):
     xsize, ysize = tracers.shape[-2], tracers.shape[-1]
     last_x, last_y = xsize - 1, ysize - 1
     precision = lax.Precision.HIGH
-    from_up = exchange(tracers[..., last_x, :], 1, 0)[..., None, :]
-    from_down = exchange(tracers[..., 0, :], -1, 0)[..., None, :]
-    from_left = exchange(tracers[..., last_y], 0, 1)[..., None]
-    from_right = exchange(tracers[..., 0], 0, -1)[..., None]
+    if halos is None:
+        halos = (
+            exchange(tracers[..., last_x, :], 1, 0)[..., None, :],
+            exchange(tracers[..., 0, :], -1, 0)[..., None, :],
+            exchange(tracers[..., last_y], 0, 1)[..., None],
+            exchange(tracers[..., 0], 0, -1)[..., None],
+        )
+    from_up, from_down, from_left, from_right = halos
     above_x = np.eye(xsize, k=1)
     above_y = np.eye(ysize, k=1)
     sum_x = jnp.asarray(above_x + above_x.T, jnp.float32)
@@ -218,8 +236,14 @@
     derivative_np, weights_np, massw_np = gll_tables()
     state_now = atm_state.reshape(fields * levels, xlocal, ylocal)
     inv_mass = mass_inverse(massw_np, xlocal, ylocal)
+    deep = ocean_tracers
     for repeat in range(SUB):
-        state_now = substep(state_now, metric, derivative_np, weights_np, inv_mass)
+        if repeat < OSTEPS:
+            state_now, deep = substep(state_now, metric, derivative_np, weights_np, inv_mass, deep, ocean_velocity)
+        else:
+            state_now, unused = substep(state_now, metric, derivative_np, weights_np, inv_mass, deep[:, :0], ocean_velocity[:, :0])
+    for repeat in range(SUB, OSTEPS):
+        deep = tracer_step(deep, ocean_velocity)
     atm_out = state_now.reshape(fields, levels, xlocal, ylocal)
     bottom = atm_out[:, levels - 1]
     speed = jnp.sqrt(1.0 + bottom[0] * bottom[0] + bottom[1] * bottom[1])
@@ -236,12 +260,15 @@
     source_count, ocean_x, ocean_y = remap_slots.shape
     gathered = onehot_gather(received, remap_slots).reshape(fields, source_count, ocean_x, ocean_y)
     ocean_flux = jnp.sum(remap_weights[None] * gathered, axis=1)
-    velocity = ocean_velocity.at[0, 0].add(wind_coef * jnp.tanh(ocean_flux[0]))
+    velocity = ocean_velocity[:, :1]
+    velocity = velocity.at[0, 0].add(wind_coef * jnp.tanh(ocean_flux[0]))
     velocity = velocity.at[1, 0].add(wind_coef * jnp.tanh(ocean_flux[1]))
-    tracers = ocean_tracers.at[0, 0].add(surf_coef * ocean_flux[2])
-    tracers = tracers.at[1, 0].add(surf_coef * ocean_flux[3])
+    surface = ocean_tracers[:, :1]
+    surface = surface.at[0, 0].add(surf_coef * ocean_flux[2])
+    surface = surface.at[1, 0].add(surf_coef * ocean_flux[3])
     for repeat in range(OSTEPS):
-        tracers = tracer_step(tracers, velocity)
+        surface = tracer_step(surface, velocity)
+    tracers = lax.dynamic_update_slice_in_dim(deep, surface, 0, axis=1)
     return (atm_out, tracers)
 
 

time: 92.4 us -> 124 us (1.34)
  local copies, waits for them, and re-layouts: 9.69 us -> 34.5 us
  blocking collectives: 14.3 us -> 0 us
  matrix products: 15.2 us -> 23.8 us
  starting transfers between devices: 19.8 us -> 26.4 us
  other arithmetic: 4.31 us -> 10.1 us
    slice x8 -> x36, local copies, waits for them, and re-layouts: 4.37 us -> 25.1 us  [the longest x4 7.37 us: substep(): merged[:, :, last_y]]
    all_to_all x1 -> x0, blocking collectives: 14.3 us -> none  [per_device(): lax.all_to_all(payload, ('gx', 'gy'), split_axis=1, concat_axis=1, tiled=...]
    all_to_all x0 -> x1, starting transfers between devices: none -> 6.7 us  [per_device(): lax.all_to_all(payload, ('gx', 'gy'), split_axis=1, concat_axis=1, tiled=...]
    unnamed x62 -> x121, local copies, waits for them, and re-layouts: 3.35 us -> 8.03 us
    all_to_all x0 -> x1, waiting for transfers between devices: none -> 3.71 us  [per_device(): lax.all_to_all(payload, ('gx', 'gy'), split_axis=1, concat_axis=1, tiled=...]
    concatenate x0 -> x8, other arithmetic: none -> 2.85 us  [exchange_many(): got = neighbour(jnp.concatenate(flat, axis=0), step_x, step_y)]
    dot_general x2 -> x4, matrix products: 0.83 us -> 3.57 us  [tracer_step(): jnp.einsum('...xc,cd->...xd', tracers, diff_y, precision=precision)]
    ppermute x8, waiting for transfers between devices: 3.93 us -> 1.44 us  [neighbour(): lax.ppermute(values, 'gx', [(i, (i + step_x) % count_x) for i in range(co...]
  transfers between devices with their start and end apart: 16 -> 17, of which waited for: 10 -> 8; matrix products, arithmetic and copies ran while one was open for 3% -> 18% of each run, Pallas kernels for 0% -> 0%
where the time goes in v13:
time: 124 us; the launch traced here: 122 us
  local copies, waits for them, and re-layouts  34.5 us (28%)
  starting transfers between devices  26.4 us (21%)
  matrix products  23.8 us (19%)
  waiting for transfers between devices  16.5 us (13%)
  other arithmetic  10.1 us (8%)
  Pallas kernels  9.54 us (8%)
  between operations  1.48 us (1%)
    ppermute x8, starting transfers between devices, neighbour(): lax.ppermute(values, 'gy', [(j, (j + step_y) % count_y) for j in range(co...  14.9 us
    ppermute x8, waiting for transfers between devices, neighbour(): lax.ppermute(values, 'gy', [(j, (j + step_y) % count_y) for j in range(co...  11.3 us
    pallas_call x2, Pallas kernels, onehot_gather(): pl.pallas_call(gather_kernel, grid=(count // tile,), in_specs=[pl.BlockSp...  9.54 us
    unnamed x121, local copies, waits for them, and re-layouts  8.03 us
    slice x4, local copies, waits for them, and re-layouts, substep(): merged[:, :, last_y]  7.37 us
    all_to_all x1, starting transfers between devices, per_device(): lax.all_to_all(payload, ('gx', 'gy'), split_axis=1, concat_axis=1, tiled=...  6.7 us
    slice x16, local copies, waits for them, and re-layouts, exchange_many(): out.append(got[start:start + part.shape[0]].reshape(piece.shape))  5.47 us
    slice x4, local copies, waits for them, and re-layouts, substep(): tracers[..., ocean_y]  5.39 us
  transfers between devices with their start and end apart: 17, of which 8 were waited for; matrix products, arithmetic and copies ran while one was open for 18% of the time, Pallas kernels for 0%

profile of v13, /device:TPU:0, one launch (start us, length us, event | category | flops | bytes accessed | tf_op | source)
XLA Modules:
  0.0 122.3 jit_solution(16923593003747991068)
XLA Ops:
  1.4 2.0 %fusion.4 = f32[160,16,128]{2,1,0:T(8,128)S(1)} fusion(f32[16,16,1]{1,0,2:T(8,128)} %constant.168, f32[160,16,128]{2,1,0:T(8,128)} %bitcast.290, f32[16,128]{1,0:T(8,128)S(1)} %get-tuple-element.81), kind=kOutput, calls=%fused_computation.14 | convolution fusion | flops 31784960 | bytes 2630656 | tf_op jit(solution)/shard_map/ab,lby->lay/dot_general | solution.py:88
  7.1 1.5 %fusion.95 = (f32[160,16,1]{2,1,0:T(8,128)}, f32[160,16,1]{2,1,0:T(8,128)S(1)}) fusion(f32[160,16,128]{2,1,0:T(8,128)S(1)} %fusion.1), kind=kLoop, calls=%fused_computation.168 | loop fusion | bytes 40960 | tf_op jit(solution)/shard_map/slice | solution.py:98
  8.6 2.0 %copy.76 = f32[160,16,1]{0,1,2:T(8,128)S(1)} copy(f32[160,16,1]{2,1,0:T(8,128)} %get-tuple-element.62) | data formatting | bytes 20480 | tf_op jit(solution)/shard_map/slice | solution.py:98
  10.6 1.3 %fusion.99 = (f32[2,40,16,1]{3,2,1,0:T(8,128)}, f32[2,40,16,1]{3,2,1,0:T(8,128)}) fusion(f32[2,40,16,128]{3,2,1,0:T(8,128)S(1)} %copy-done), kind=kLoop, calls=%fused_computation.172 | loop fusion | bytes 20480 | tf_op jit(solution)/shard_map/slice | solution.py:98
  11.9 1.4 %copy.77 = f32[2,40,16,1]{1,0,2,3:T(2,128)S(1)} copy(f32[2,40,16,1]{3,2,1,0:T(8,128)} %get-tuple-element.74) | data formatting | bytes 10240 | tf_op jit(solution)/shard_map/slice | solution.py:98
  14.1 2.9 %collective-permute-start = (f32[240,16]{0,1:T(8,128)}, f32[240,16]{0,1:T(8,128)S(1)}, u32[]{:S(2)}, u32[]{:S(2)}) collective-permute-start(f32[240,16]{0,1:T(8,128)} %pad_maximum_fusion.4), channel_id=1, source_target_pairs={{0,1},{1,2},{2,3},{3,4},{4,5},{5,6},{6,7},{7,0},{8,9},{9,10},{10,1... | collective-permute-start | bytes 46088 | tf_op jit(solution)/shard_map/ppermute | solution.py:25
  17.7 1.5 %copy.80 = f32[2,40,16,1]{1,0,2,3:T(2,128)S(1)} copy(f32[2,40,16,1]{3,2,1,0:T(8,128)} %get-tuple-element.75) | data formatting | bytes 10240 | tf_op jit(solution)/shard_map/slice | solution.py:99
  20.0 3.0 %collective-permute-start.1 = (f32[240,16]{0,1:T(8,128)}, f32[240,16]{0,1:T(8,128)S(1)}, u32[]{:S(2)}, u32[]{:S(2)}) collective-permute-start(f32[240,16]{0,1:T(8,128)} %pad_maximum_fusion.5), channel_id=1, source_target_pairs={{0,7},{1,0},{2,1},{3,2},{4,3},{5,4},{6,5},{7,6},{8,15},{9,8},{10,9... | collective-permute-start | bytes 46088 | tf_op jit(solution)/shard_map/ppermute | solution.py:25
  23.2 1.2 %convolution_bitcast_fusion.11 = f32[2,40,16,128]{3,2,1,0:T(8,128)} fusion(f32[16,16,1,1]{1,0,3,2:T(8,128)S(1)} %copy-done.30, f32[2,40,16,128]{3,2,1,0:T(8,128)S(1)} %copy-done), kind=kOutput, calls=%fused_computation.28 | convolution fusion | flops 15728640 | bytes 1311744 | tf_op jit(solution)/shard_map/ab,...by->...ay/dot_general | solution.py:138
  24.5 1.3 %convolution_bitcast_fusion.9 = f32[2,40,16,128]{3,2,1,0:T(8,128)} fusion(f32[16,16,1,1]{1,0,3,2:T(8,128)S(1)} %copy-done.32, f32[2,40,16,128]{3,2,1,0:T(8,128)S(1)} %copy-done), kind=kOutput, calls=%fused_computation.25 | convolution fusion | flops 15728640 | bytes 1311744 | tf_op jit(solution)/shard_map/ab,...by->...ay/dot_general | solution.py:139
  27.3 0.8 select_add_fusion.1
  28.1 1.0 copy-done.5
  29.4 2.0 %collective-permute-start.3 = (f32[240,128]{1,0:T(8,128)S(1)}, f32[240,128]{1,0:T(8,128)S(1)}, u32[]{:S(2)}, u32[]{:S(2)}) collective-permute-start(f32[240,128]{1,0:T(8,128)S(1)} %pad_maximum_fusion.1), channel_id=1, source_target_pairs={{0,24},{8,0},{16,8},{24,16},{1,25},{9,1},{17,9},{25,17},{2,26},{10... | collective-permute-start | bytes 368648 | tf_op jit(solution)/shard_map/ppermute | solution.py:23
  31.7 1.1 fusion.13
  32.8 0.9 collective-permute-done.2
  34.3 2.5 %multiply_subtract_fusion.1 = f32[160,16,128]{2,1,0:T(8,128)S(1)} fusion(f32[16,128]{1,0:T(8,128)S(1)} %copy-done.26, f32[160,128]{1,0:T(8,128)S(1)} %slice.355, f32[160,128]{1,0:T(8,128)S(1)} %slice.353, pred[16]{0:T(512)(128)(4,1)S(1)} %copy-done.45, pred[16]{0:T(512)(128)(4,1)S(1)} %copy-done.50, f32[4,40,16,128]{3,2,1,0:T(8,128)} %param.49, ...), kind=kOutput, calls=%fused_computation.17 | convolution fusion | flops 33095680 | bytes 4105248 | tf_op jit(solution)/shard_map/ab,lby->lay/dot_general | solution.py:108
  39.8 1.2 %fusion.97 = (f32[2,40,16,1]{3,2,1,0:T(8,128)}, f32[2,40,16,1]{3,2,1,0:T(8,128)}) fusion(f32[2,40,16,128]{3,2,1,0:T(8,128)S(1)} %fusion.12), kind=kLoop, calls=%fused_computation.170 | loop fusion | bytes 20480 | tf_op jit(solution)/shard_map/slice | solution.py:98
  41.0 1.3 %convolution_bitcast_fusion.6 = f32[2,40,16,128]{3,2,1,0:T(8,128)} fusion(f32[2,40,16,128]{3,2,1,0:T(8,128)S(1)} %fusion.12, f32[16,16,1,1]{1,0,3,2:T(8,128)S(1)} %copy-done.33), kind=kOutput, calls=%fused_computation.21 | convolution fusion | flops 15728640 | bytes 1311744 | tf_op jit(solution)/shard_map/ab,...by->...ay/dot_general | solution.py:139
  42.3 1.2 %convolution_bitcast_fusion.7 = f32[2,40,16,128]{3,2,1,0:T(8,128)} fusion(f32[2,40,16,128]{3,2,1,0:T(8,128)S(1)} %fusion.12, f32[16,16,1,1]{1,0,3,2:T(8,128)S(1)} %copy-done.31), kind=kOutput, calls=%fused_computation.22 | convolution fusion | flops 15728640 | bytes 1311744 | tf_op jit(solution)/shard_map/ab,...by->...ay/dot_general | solution.py:138
  45.8 1.9 %fusion.93 = (f32[160,16,1]{2,1,0:T(8,128)}, f32[160,16,1]{2,1,0:T(8,128)}) fusion(f32[160,16,128]{2,1,0:T(8,128)S(1)} %fusion), kind=kLoop, calls=%fused_computation.166 | loop fusion | bytes 40960 | tf_op jit(solution)/shard_map/slice | solution.py:98
  47.7 1.9 %copy.83 = f32[160,16,1]{0,1,2:T(8,128)S(1)} copy(f32[160,16,1]{2,1,0:T(8,128)} %get-tuple-element.58) | data formatting | bytes 20480 | tf_op jit(solution)/shard_map/slice | solution.py:98
  49.7 1.5 %copy.86 = f32[2,40,16,1]{1,0,2,3:T(2,128)S(1)} copy(f32[2,40,16,1]{3,2,1,0:T(8,128)} %get-tuple-element.68) | data formatting | bytes 10240 | tf_op jit(solution)/shard_map/slice | solution.py:98
  51.3 1.9 %copy.88 = f32[160,16,1]{0,1,2:T(8,128)S(1)} copy(f32[160,16,1]{2,1,0:T(8,128)} %get-tuple-element.59) | data formatting | bytes 20480 | tf_op jit(solution)/shard_map/slice | solution.py:99
  53.2 1.5 %copy.89 = f32[2,40,16,1]{1,0,2,3:T(2,128)S(1)} copy(f32[2,40,16,1]{3,2,1,0:T(8,128)} %get-tuple-element.69) | data formatting | bytes 10240 | tf_op jit(solution)/shard_map/slice | solution.py:99
  54.8 4.7 %collective-permute-start.5 = (f32[240,16]{0,1:T(8,128)S(1)}, f32[240,16]{0,1:T(8,128)S(1)}, u32[]{:S(2)}, u32[]{:S(2)}) collective-permute-start(f32[240,16]{0,1:T(8,128)S(1)} %pad_maximum_fusion.7), channel_id=1, source_target_pairs={{0,7},{1,0},{2,1},{3,2},{4,3},{5,4},{6,5},{7,6},{8,15},{9,8},{10,9... | collective-permute-start | bytes 46088 | tf_op jit(solution)/shard_map/ppermute | solution.py:25
  61.6 0.8 copy.90
  62.5 2.0 %select_add_fusion = f32[160,16,128]{2,1,0:T(8,128)S(1)} fusion(f32[160,16,128]{2,1,0:T(8,128)} %copy-done.1, f32[160,16]{1,0:T(8,128)S(1)} %copy.90, f32[160,16]{1,0:T(8,128)S(1)} %copy.87, pred[128]{0:T(512)(128)(4,1)} %copy-done.37, pred[128]{0:T(512)(128)(4,1)} %copy-done.41), kind=kLoop, calls=%fused_computation.16 | loop fusion | flops 983040 | bytes 2642176 | tf_op jit(solution)/shard_map/add | solution.py:101
  64.5 1.0 copy-done.3
  66.3 0.9 collective-permute-start.6
  67.8 0.9 collective-permute-start.7
  69.8 2.2 %fusion.20 = f32[2,40,16,128]{3,2,1,0:T(8,128)} fusion(f32[2,40,16,128]{3,2,1,0:T(8,128)S(1)} %fusion.12, f32[128,128,1,1]{1,0,3,2:T(8,128)} %constant.176, f32[2,40,16]{2,1,0:T(8,128)S(1)} %bitcast.298, f32[2,40,16]{2,1,0:T(8,128)S(1)} %bitcast.300, f32[40,16,128]{2,1,0:T(8,128)S(1)} %get-tuple-element.71, pred[128]{0:T(512)(128)(4,1)} %copy-done.41, ...), kind=kOutput, calls=%fused_computation.42 | convolution fusion | flops 126648320 | bytes 1714432 | tf_op jit(solution)/shard_map/...xc,cd->...xd/dot_general | solution.py:141
  72.0 0.9 slice.368
  72.9 0.9 slice.371
  74.7 1.0 copy-done.8
  76.4 3.5 %shard_map.392 = f32[4,8192]{1,0:T(4,128)} custom-call(s32[1,8192]{1,0:T(1,128)} %bitcast.318, f32[4,16,128]{2,1,0:T(8,128)} %fusion.27.table_ref), custom_call_target="tpu_custom_call" | custom-call | tf_op jit(solution)/shard_map/pallas_call | solution.py:213
  79.9 1.6 %broadcast_multiply_fusion = f32[4,32,256]{2,0,1:T(4,128)} fusion(f32[4,32,256]{2,0,1:T(4,128)} %bitcast.295, f32[32,256]{1,0:T(8,128)S(1)} %fusion.28), kind=kLoop, calls=%fused_computation.68 | loop fusion | flops 32768 | bytes 294912 | tf_op jit(solution)/shard_map/mul | solution.py:257
  81.5 6.7 %all-to-all-start = ((f32[4,32,256]{2,0,1:T(4,128)}), f32[4,32,256]{2,0,1:T(4,128)S(1)}, u32[]{:S(2)}, u32[]{:S(2)}) async-start(f32[4,32,256]{2,0,1:T(4,128)} %broadcast_multiply_fusion), calls=%async_computation | async-start | bytes 262144 | tf_op jit(solution)/shard_map/all_to_all | solution.py:258
  89.8 2.1 %fusion.19 = f32[2,40,16,128]{3,2,1,0:T(8,128)S(1)} fusion(f32[2,40,16,128]{3,2,1,0:T(8,128)} %fusion.20, f32[2,40,16,128]{3,2,1,0:T(8,128)S(1)} %fusion.12, f32[128,128,1,1]{1,0,3,2:T(8,128)S(1)} %copy-done.11, f32[2,40,16,128]{3,2,1,0:T(8,128)} %convolution_bitcast_fusion.7, f32[2,40,16,128]{3,2,1,0:T(8,128)} %convolution_bitcast_fusion.6, ...), kind=kOutput, calls=%fused_computation.41 | convolution fusion | flops 128778240 | bytes 3762464 | tf_op jit(solution)/shard_map/...xc,cd->...xd/dot_general | solution.py:140
  92.0 3.7 %all-to-all-done = f32[4,32,256]{2,0,1:T(4,128)S(1)} async-done(((f32[4,32,256]{2,0,1:T(4,128)}), f32[4,32,256]{2,0,1:T(4,128)S(1)}, u32[]{:S(2)}, u32[]{:S(2)}) %all-to-all-start) | async-done | bytes 131104 | tf_op jit(solution)/shard_map/all_to_all | solution.py:258
  96.4 6.0 %shard_map.393 = f32[4,8192]{1,0:T(4,128)} custom-call(s32[1,8192]{1,0:T(1,128)} %bitcast.327, f32[4,64,128]{2,1,0:T(8,128)} %reshape_reshape.3.table_ref), custom_call_target="tpu_custom_call" | custom-call | tf_op jit(solution)/shard_map/pallas_call | solution.py:213
  102.4 0.9 copy.114
  104.6 2.1 %collective-permute-start.10 = (f32[2,1,16]{2,0,1:T(2,128)S(1)}, f32[2,1,16]{2,0,1:T(2,128)S(1)}, u32[]{:S(2)}, u32[]{:S(2)}) collective-permute-start(f32[2,1,16]{2,0,1:T(2,128)S(1)} %bitcast.330), channel_id=1, source_target_pairs={{0,7},{1,0},{2,1},{3,2},{4,3},{5,4},{6,5},{7,6},{8,15},{9,8},{10,9... | collective-permute-start | bytes 392 | tf_op jit(solution)/shard_map/ppermute | solution.py:25
  107.3 0.9 collective-permute-done.10
  108.2 4.7 %collective-permute-done.11 = f32[2,1,16]{2,0,1:T(2,128)S(1)} collective-permute-done((f32[2,1,16]{2,0,1:T(2,128)S(1)}, f32[2,1,16]{2,0,1:T(2,128)S(1)}, u32[]{:S(2)}, u32[]{:S(2)}) %collective-permute-start.11) | collective-permute-done | bytes 160 | tf_op jit(solution)/shard_map/ppermute | solution.py:25
  113.6 1.5 %collective-permute-start.14 = (f32[2,1,16]{2,0,1:T(2,128)S(1)}, f32[2,1,16]{2,0,1:T(2,128)S(1)}, u32[]{:S(2)}, u32[]{:S(2)}) collective-permute-start(f32[2,1,16]{2,0,1:T(2,128)S(1)} %bitcast.332), channel_id=1, source_target_pairs={{0,7},{1,0},{2,1},{3,2},{4,3},{5,4},{6,5},{7,6},{8,15},{9,8},{10,9... | collective-permute-start | bytes 392 | tf_op jit(solution)/shard_map/ppermute | solution.py:25
  116.3 0.9 collective-permute-done.14
  117.2 4.1 %collective-permute-done.15 = f32[2,1,16]{2,0,1:T(2,128)S(1)} collective-permute-done((f32[2,1,16]{2,0,1:T(2,128)S(1)}, f32[2,1,16]{2,0,1:T(2,128)S(1)}, u32[]{:S(2)}, u32[]{:S(2)}) %collective-permute-start.15) | collective-permute-done | bytes 160 | tf_op jit(solution)/shard_map/ppermute | solution.py:25
  121.5 0.8 copy-done.10
  (205 shorter events, 26.8 us)
Async XLA Ops:
  14.1 13.0 %collective-permute-start = (f32[240,16]{0,1:T(8,128)}, f32[240,16]{0,1:T(8,128)S(1)}, u32[]{:S(2)}, u32[]{:S(2)}) collective-permute-start(f32[240,16]{0,1:T(8,128)} %pad_maximum_fusion.4), channel_id=1, source_target_pairs={{0,1},{1,2},{2,3},{3,4},{4,5},{5,6},{6,7},{7,0},{8,9},{9,10},{10,1... | collective-permute-start | bytes 46088 | tf_op jit(solution)/shard_map/ppermute | solution.py:25
  17.7 5.4 %copy-start.9 = (f32[2,40,16,128]{3,2,1,0:T(8,128)S(1)}, f32[2,40,16,128]{3,2,1,0:T(8,128)}, u32[]{:S(2)}) copy-start(f32[2,40,16,128]{3,2,1,0:T(8,128)} %param.54) | copy-start | bytes 1966084
  17.7 5.5 %copy-start.30 = (f32[16,16,1,1]{1,0,3,2:T(8,128)S(1)}, f32[16,16,1,1]{1,0,3,2:T(8,128)}, u32[]{:S(2)}) copy-start(f32[16,16,1,1]{1,0,3,2:T(8,128)} %constant.173) | copy-start | bytes 3076
  20.0 7.2 %collective-permute-start.1 = (f32[240,16]{0,1:T(8,128)}, f32[240,16]{0,1:T(8,128)S(1)}, u32[]{:S(2)}, u32[]{:S(2)}) collective-permute-start(f32[240,16]{0,1:T(8,128)} %pad_maximum_fusion.5), channel_id=1, source_target_pairs={{0,7},{1,0},{2,1},{3,2},{4,3},{5,4},{6,5},{7,6},{8,15},{9,8},{10,9... | collective-permute-start | bytes 46088 | tf_op jit(solution)/shard_map/ppermute | solution.py:25
  23.0 4.2 %copy-start.37 = (pred[128]{0:T(512)(128)(4,1)}, pred[128]{0:T(512)(128)(4,1)S(1)}, u32[]{:S(2)}) copy-start(pred[128]{0:T(512)(128)(4,1)S(1)} %get-tuple-element.82) | copy-start | bytes 388
  23.0 4.2 %copy-start.41 = (pred[128]{0:T(512)(128)(4,1)}, pred[128]{0:T(512)(128)(4,1)S(1)}, u32[]{:S(2)}) copy-start(pred[128]{0:T(512)(128)(4,1)S(1)} %get-tuple-element.83) | copy-start | bytes 388
  23.2 3.2 %copy-start.35 = (s32[1,32,256]{2,1,0:T(8,128)S(1)}, s32[1,32,256]{2,1,0:T(8,128)}, u32[]{:S(2)}) copy-start(s32[1,32,256]{2,1,0:T(8,128)} %param.51) | copy-start | bytes 98308
  27.3 4.5 %copy-start.13 = (f32[128,128,1,1]{1,0,3,2:T(8,128)S(1)}, f32[128,128,1,1]{1,0,3,2:T(8,128)}, u32[]{:S(2)}) copy-start(f32[128,128,1,1]{1,0,3,2:T(8,128)} %constant.176) | copy-start | bytes 196612
  29.3 5.0 %copy-start.26 = (f32[16,128]{1,0:T(8,128)S(1)}, f32[16,128]{1,0:T(8,128)}, u32[]{:S(2)}) copy-start(f32[16,128]{1,0:T(8,128)} %constant.167) | copy-start | bytes 24580
  29.3 4.9 %copy-start.28 = (f32[16,16,1]{1,0,2:T(8,128)S(1)}, f32[16,16,1]{1,0,2:T(8,128)}, u32[]{:S(2)}) copy-start(f32[16,16,1]{1,0,2:T(8,128)} %constant.172) | copy-start | bytes 3076
  29.3 4.9 %copy-start.45 = (pred[16]{0:T(512)(128)(4,1)S(1)}, pred[16]{0:T(512)(128)(4,1)}, u32[]{:S(2)}) copy-start(pred[16]{0:T(512)(128)(4,1)} %get-tuple-element.84) | copy-start | bytes 52
  29.3 4.9 %copy-start.50 = (pred[16]{0:T(512)(128)(4,1)S(1)}, pred[16]{0:T(512)(128)(4,1)}, u32[]{:S(2)}) copy-start(pred[16]{0:T(512)(128)(4,1)} %get-tuple-element.85) | copy-start | bytes 52
  29.4 4.4 %collective-permute-start.2 = (f32[240,128]{1,0:T(8,128)S(1)}, f32[240,128]{1,0:T(8,128)S(1)}, u32[]{:S(2)}, u32[]{:S(2)}) collective-permute-start(f32[240,128]{1,0:T(8,128)S(1)} %pad_maximum_fusion), channel_id=1, source_target_pairs={{0,8},{8,16},{16,24},{24,0},{1,9},{9,17},{17,25},{25,1},{2,10},{10... | collective-permute-start | bytes 368648 | tf_op jit(solution)/shard_map/ppermute | solution.py:23
  29.4 4.8 %collective-permute-start.3 = (f32[240,128]{1,0:T(8,128)S(1)}, f32[240,128]{1,0:T(8,128)S(1)}, u32[]{:S(2)}, u32[]{:S(2)}) collective-permute-start(f32[240,128]{1,0:T(8,128)S(1)} %pad_maximum_fusion.1), channel_id=1, source_target_pairs={{0,24},{8,0},{16,8},{24,16},{1,25},{9,1},{17,9},{25,17},{2,26},{10... | collective-permute-start | bytes 368648 | tf_op jit(solution)/shard_map/ppermute | solution.py:23
  51.3 9.0 %collective-permute-start.4 = (f32[240,16]{0,1:T(8,128)S(1)}, f32[240,16]{0,1:T(8,128)S(1)}, u32[]{:S(2)}, u32[]{:S(2)}) collective-permute-start(f32[240,16]{0,1:T(8,128)S(1)} %pad_maximum_fusion.6), channel_id=1, source_target_pairs={{0,1},{1,2},{2,3},{3,4},{4,5},{5,6},{6,7},{7,0},{8,9},{9,10},{10,1... | collective-permute-start | bytes 46088 | tf_op jit(solution)/shard_map/ppermute | solution.py:25
  54.8 6.2 %collective-permute-start.5 = (f32[240,16]{0,1:T(8,128)S(1)}, f32[240,16]{0,1:T(8,128)S(1)}, u32[]{:S(2)}, u32[]{:S(2)}) collective-permute-start(f32[240,16]{0,1:T(8,128)S(1)} %pad_maximum_fusion.7), channel_id=1, source_target_pairs={{0,7},{1,0},{2,1},{3,2},{4,3},{5,4},{6,5},{7,6},{8,15},{9,8},{10,9... | collective-permute-start | bytes 46088 | tf_op jit(solution)/shard_map/ppermute | solution.py:25
  62.4 3.2 %copy-start.21 = (f32[2,40,1,128]{3,2,1,0:T(1,128)S(1)}, f32[2,40,1,128]{3,2,1,0:T(1,128)}, u32[]{:S(2)}) copy-start(f32[2,40,1,128]{3,2,1,0:T(1,128)} %get-tuple-element.66) | copy-start | bytes 122884
  62.4 4.7 %copy-start.20 = (f32[2,40,1,128]{3,2,1,0:T(1,128)S(1)}, f32[2,40,1,128]{3,2,1,0:T(1,128)}, u32[]{:S(2)}) copy-start(f32[2,40,1,128]{3,2,1,0:T(1,128)} %get-tuple-element.67) | copy-start | bytes 122884
  62.4 6.3 %copy-start.24 = (f32[240,16]{0,1:T(8,128)S(1)}, f32[240,16]{0,1:T(8,128)}, u32[]{:S(2)}) copy-start(f32[240,16]{0,1:T(8,128)} %copy-done.23) | copy-start | bytes 46084
  66.3 7.5 %copy-start.27 = (f32[16,128]{1,0:T(8,128)S(1)}, f32[16,128]{1,0:T(8,128)}, u32[]{:S(2)}) copy-start(f32[16,128]{1,0:T(8,128)} %constant.167) | copy-start | bytes 24580
  66.3 7.5 %copy-start.29 = (f32[16,16,1]{1,0,2:T(8,128)S(1)}, f32[16,16,1]{1,0,2:T(8,128)}, u32[]{:S(2)}) copy-start(f32[16,16,1]{1,0,2:T(8,128)} %constant.172) | copy-start | bytes 3076
  66.3 7.5 %copy-start.47 = (pred[16]{0:T(512)(128)(4,1)S(1)}, pred[16]{0:T(512)(128)(4,1)}, u32[]{:S(2)}) copy-start(pred[16]{0:T(512)(128)(4,1)} %get-tuple-element.84) | copy-start | bytes 52
  66.3 7.6 %copy-start.52 = (pred[16]{0:T(512)(128)(4,1)S(1)}, pred[16]{0:T(512)(128)(4,1)}, u32[]{:S(2)}) copy-start(pred[16]{0:T(512)(128)(4,1)} %get-tuple-element.85) | copy-start | bytes 52
  66.3 5.7 %collective-permute-start.6 = (f32[240,128]{1,0:T(8,128)}, f32[240,128]{1,0:T(8,128)}, u32[]{:S(2)}, u32[]{:S(2)}) collective-permute-start(f32[240,128]{1,0:T(8,128)} %pad_maximum_fusion.2), channel_id=1, source_target_pairs={{0,8},{8,16},{16,24},{24,0},{1,9},{9,17},{17,25},{25,1},{2,10},{10... | collective-permute-start | bytes 368648 | tf_op jit(solution)/shard_map/ppermute | solution.py:23
  67.8 5.1 %collective-permute-start.7 = (f32[240,128]{1,0:T(8,128)}, f32[240,128]{1,0:T(8,128)}, u32[]{:S(2)}, u32[]{:S(2)}) collective-permute-start(f32[240,128]{1,0:T(8,128)} %pad_maximum_fusion.3), channel_id=1, source_target_pairs={{0,24},{8,0},{16,8},{24,16},{1,25},{9,1},{17,9},{25,17},{2,26},{10... | collective-permute-start | bytes 368648 | tf_op jit(solution)/shard_map/ppermute | solution.py:23
  69.8 4.1 %copy-start.4 = (f32[160,16,128]{2,1,0:T(8,128)S(1)}, f32[160,16,128]{2,1,0:T(8,128)}, u32[]{:S(2)}) copy-start(f32[160,16,128]{2,1,0:T(8,128)} %copy-done.3) | copy-start | bytes 3932164
  73.9 15.9 %copy-start.39 = (pred[128]{0:T(512)(128)(4,1)S(1)}, pred[128]{0:T(512)(128)(4,1)}, u32[]{:S(2)}) copy-start(pred[128]{0:T(512)(128)(4,1)} %copy-done.37) | copy-start | bytes 388
  73.9 15.9 %copy-start.43 = (pred[128]{0:T(512)(128)(4,1)S(1)}, pred[128]{0:T(512)(128)(4,1)}, u32[]{:S(2)}) copy-start(pred[128]{0:T(512)(128)(4,1)} %copy-done.41) | copy-start | bytes 388
  73.9 15.9 %copy-start.48 = (pred[16]{0:T(512)(128)(4,1)S(1)}, pred[16]{0:T(512)(128)(4,1)}, u32[]{:S(2)}) copy-start(pred[16]{0:T(512)(128)(4,1)} %get-tuple-element.84) | copy-start | bytes 52
  73.9 15.9 %copy-start.53 = (pred[16]{0:T(512)(128)(4,1)S(1)}, pred[16]{0:T(512)(128)(4,1)}, u32[]{:S(2)}) copy-start(pred[16]{0:T(512)(128)(4,1)} %get-tuple-element.85) | copy-start | bytes 52
  81.5 14.2 %all-to-all-start = ((f32[4,32,256]{2,0,1:T(4,128)}), f32[4,32,256]{2,0,1:T(4,128)S(1)}, u32[]{:S(2)}, u32[]{:S(2)}) async-start(f32[4,32,256]{2,0,1:T(4,128)} %broadcast_multiply_fusion), calls=%async_computation | async-start | bytes 262144 | tf_op jit(solution)/shard_map/all_to_all | solution.py:258
  89.8 13.6 %copy-start.36 = (f32[4,16,128]{2,1,0:T(8,128)S(1)}, f32[4,16,128]{2,1,0:T(8,128)}, u32[]{:S(2)}) copy-start(f32[4,16,128]{2,1,0:T(8,128)} %param.56) | copy-start | bytes 98308
  91.9 12.4 %copy-start.17 = (f32[128,128,1]{1,0,2:T(8,128)S(1)}, f32[128,128,1]{1,0,2:T(8,128)}, u32[]{:S(2)}) copy-start(f32[128,128,1]{1,0,2:T(8,128)} %constant.180) | copy-start | bytes 196612
  91.9 12.5 %copy-start.16 = (f32[128,128,1]{1,0,2:T(8,128)S(1)}, f32[128,128,1]{1,0,2:T(8,128)}, u32[]{:S(2)}) copy-start(f32[128,128,1]{1,0,2:T(8,128)} %constant.178) | copy-start | bytes 196612
  91.9 15.2 %copy-start.34 = (f32[16,16,1]{1,0,2:T(8,128)S(1)}, f32[16,16,1]{1,0,2:T(8,128)}, u32[]{:S(2)}) copy-start(f32[16,16,1]{1,0,2:T(8,128)} %constant.179) | copy-start | bytes 3076
  92.0 21.0 %copy-start.40 = (pred[128]{0:T(512)(128)(4,1)S(1)}, pred[128]{0:T(512)(128)(4,1)}, u32[]{:S(2)}) copy-start(pred[128]{0:T(512)(128)(4,1)} %copy-done.37) | copy-start | bytes 388
  92.0 21.0 %copy-start.44 = (pred[128]{0:T(512)(128)(4,1)S(1)}, pred[128]{0:T(512)(128)(4,1)}, u32[]{:S(2)}) copy-start(pred[128]{0:T(512)(128)(4,1)} %copy-done.41) | copy-start | bytes 388
  92.0 21.0 %copy-start.49 = (pred[16]{0:T(512)(128)(4,1)S(1)}, pred[16]{0:T(512)(128)(4,1)}, u32[]{:S(2)}) copy-start(pred[16]{0:T(512)(128)(4,1)} %get-tuple-element.84) | copy-start | bytes 52
  92.0 21.0 %copy-start.54 = (pred[16]{0:T(512)(128)(4,1)S(1)}, pred[16]{0:T(512)(128)(4,1)}, u32[]{:S(2)}) copy-start(pred[16]{0:T(512)(128)(4,1)} %get-tuple-element.85) | copy-start | bytes 52
  92.0 21.0 %copy-start.58 = (f32[16,16,1]{1,0,2:T(8,128)S(1)}, f32[16,16,1]{1,0,2:T(8,128)}, u32[]{:S(2)}) copy-start(f32[16,16,1]{1,0,2:T(8,128)} %constant.177) | copy-start | bytes 3076
  104.6 3.6 %collective-permute-start.10 = (f32[2,1,16]{2,0,1:T(2,128)S(1)}, f32[2,1,16]{2,0,1:T(2,128)S(1)}, u32[]{:S(2)}, u32[]{:S(2)}) collective-permute-start(f32[2,1,16]{2,0,1:T(2,128)S(1)} %bitcast.330), channel_id=1, source_target_pairs={{0,7},{1,0},{2,1},{3,2},{4,3},{5,4},{6,5},{7,6},{8,15},{9,8},{10,9... | collective-permute-start | bytes 392 | tf_op jit(solution)/shard_map/ppermute | solution.py:25
  106.7 6.3 %collective-permute-start.11 = (f32[2,1,16]{2,0,1:T(2,128)S(1)}, f32[2,1,16]{2,0,1:T(2,128)S(1)}, u32[]{:S(2)}, u32[]{:S(2)}) collective-permute-start(f32[2,1,16]{2,0,1:T(2,128)S(1)} %bitcast.329), channel_id=1, source_target_pairs={{0,1},{1,2},{2,3},{3,4},{4,5},{5,6},{6,7},{7,0},{8,9},{9,10},{10,1... | collective-permute-start | bytes 392 | tf_op jit(solution)/shard_map/ppermute | solution.py:25
  106.7 6.3 %collective-permute-start.8 = (f32[2,128]{1,0:T(2,128)S(1)}, f32[2,128]{1,0:T(2,128)S(1)}, u32[]{:S(2)}, u32[]{:S(2)}) collective-permute-start(f32[2,128]{1,0:T(2,128)S(1)} %bitcast.334), channel_id=1, source_target_pairs={{0,24},{8,0},{16,8},{24,16},{1,25},{9,1},{17,9},{25,17},{2,26},{10... | collective-permute-start | bytes 3080 | tf_op jit(solution)/shard_map/ppermute | solution.py:23
  106.7 6.3 %collective-permute-start.9 = (f32[2,128]{1,0:T(2,128)S(1)}, f32[2,128]{1,0:T(2,128)S(1)}, u32[]{:S(2)}, u32[]{:S(2)}) collective-permute-start(f32[2,128]{1,0:T(2,128)S(1)} %bitcast.333), channel_id=1, source_target_pairs={{0,8},{8,16},{16,24},{24,0},{1,9},{9,17},{17,25},{25,1},{2,10},{10... | collective-permute-start | bytes 3080 | tf_op jit(solution)/shard_map/ppermute | solution.py:23
  113.6 3.6 %collective-permute-start.14 = (f32[2,1,16]{2,0,1:T(2,128)S(1)}, f32[2,1,16]{2,0,1:T(2,128)S(1)}, u32[]{:S(2)}, u32[]{:S(2)}) collective-permute-start(f32[2,1,16]{2,0,1:T(2,128)S(1)} %bitcast.332), channel_id=1, source_target_pairs={{0,7},{1,0},{2,1},{3,2},{4,3},{5,4},{6,5},{7,6},{8,15},{9,8},{10,9... | collective-permute-start | bytes 392 | tf_op jit(solution)/shard_map/ppermute | solution.py:25
  115.1 6.3 %collective-permute-start.15 = (f32[2,1,16]{2,0,1:T(2,128)S(1)}, f32[2,1,16]{2,0,1:T(2,128)S(1)}, u32[]{:S(2)}, u32[]{:S(2)}) collective-permute-start(f32[2,1,16]{2,0,1:T(2,128)S(1)} %bitcast.331), channel_id=1, source_target_pairs={{0,1},{1,2},{2,3},{3,4},{4,5},{5,6},{6,7},{7,0},{8,9},{9,10},{10,1... | collective-permute-start | bytes 392 | tf_op jit(solution)/shard_map/ppermute | solution.py:25
  115.7 5.7 %collective-permute-start.12 = (f32[2,128]{1,0:T(2,128)S(1)}, f32[2,128]{1,0:T(2,128)S(1)}, u32[]{:S(2)}, u32[]{:S(2)}) collective-permute-start(f32[2,128]{1,0:T(2,128)S(1)} %bitcast.336), channel_id=1, source_target_pairs={{0,24},{8,0},{16,8},{24,16},{1,25},{9,1},{17,9},{25,17},{2,26},{10... | collective-permute-start | bytes 3080 | tf_op jit(solution)/shard_map/ppermute | solution.py:23
  115.7 5.7 %collective-permute-start.13 = (f32[2,128]{1,0:T(2,128)S(1)}, f32[2,128]{1,0:T(2,128)S(1)}, u32[]{:S(2)}, u32[]{:S(2)}) collective-permute-start(f32[2,128]{1,0:T(2,128)S(1)} %bitcast.335), channel_id=1, source_target_pairs={{0,8},{8,16},{16,24},{24,0},{1,9},{9,17},{17,25},{25,1},{2,10},{10... | collective-permute-start | bytes 3080 | tf_op jit(solution)/shard_map/ppermute | solution.py:23
  (28 other events, 34.0 us)

commit v14 on v12

--- a/solution.py
+++ b/solution.py
@@ -166,7 +166,7 @@
     )
 
 
-def gather_kernel(index_ref, table_ref, out_ref):
+def gather_kernel(index_ref, scale_ref, table_ref, out_ref):
     fields, rows, tile = table_ref.shape[0], table_ref.shape[1], out_ref.shape[1]
     index = index_ref[...]
     onehot = (lax.broadcasted_iota(jnp.int32, (128, tile), 0) == (index & 127)).astype(jnp.bfloat16)
@@ -179,29 +179,42 @@
         parts.append(piece)
     stacked = jnp.concatenate(parts, axis=2).reshape(fields * rows, 3 * 128)
     picked = jnp.dot(stacked, jnp.concatenate([onehot] * 3, axis=0), preferred_element_type=jnp.float32)
-    for field in range(fields):
-        whole = picked[field * rows : (field + 1) * rows]
-        out_ref[pl.ds(field, 1), :] = jnp.sum(jnp.where(select, whole, 0.0), axis=0, keepdims=True)
-
-
-def onehot_gather(table, index):
+    scale = scale_ref[...]
+    values = jnp.concatenate(
+        [jnp.sum(jnp.where(select, picked[f * rows : (f + 1) * rows], 0.0), axis=0, keepdims=True) for f in range(fields)],
+        axis=0,
+    ) * scale
+
+    @pl.when(pl.program_id(1) == 0)
+    def first():
+        out_ref[...] = values
+
+    @pl.when(pl.program_id(1) > 0)
+    def rest_steps():
+        out_ref[...] = out_ref[...] + values
+
+
+def onehot_gather(table, index, scale, groups):
     fields, total = table.shape
     rows = total // 128
     flat = index.reshape(1, -1)
     count = flat.shape[1]
+    width = count // groups
     tile = 128
-    while tile < 2048 and count % (2 * tile) == 0 and fields * 3 * rows * tile * 8 <= 4 * 2**20:
+    while tile < 2048 and width % (2 * tile) == 0 and fields * rows * tile * 8 <= 4 * 2**20:
         tile *= 2
+    blocks = width // tile
     return pl.pallas_call(
         gather_kernel,
-        grid=(count // tile,),
+        grid=(blocks, groups),
         in_specs=[
-            pl.BlockSpec((1, tile), lambda step: (0, step)),
-            pl.BlockSpec((fields, rows, 128), lambda step: (0, 0, 0)),
+            pl.BlockSpec((1, tile), lambda step, group: (0, group * blocks + step)),
+            pl.BlockSpec((1, tile), lambda step, group: (0, group * blocks + step)),
+            pl.BlockSpec((fields, rows, 128), lambda step, group: (0, 0, 0)),
         ],
-        out_specs=pl.BlockSpec((fields, tile), lambda step: (0, step)),
-        out_shape=jax.ShapeDtypeStruct((fields, count), jnp.float32),
-    )(flat, table.reshape(fields, rows, 128))
+        out_specs=pl.BlockSpec((fields, tile), lambda step, group: (0, step)),
+        out_shape=jax.ShapeDtypeStruct((fields, width), jnp.float32),
+    )(flat, scale.reshape(1, -1), table.reshape(fields, rows, 128))
 
 
 def per_device(
@@ -227,15 +240,13 @@
     node_total = xlocal * ylocal
     rank_total = send_idx.shape[1]
     slot_cap = send_idx.shape[2]
-    payload = onehot_gather(flux_flat, send_idx[0]).reshape(fields, rank_total, slot_cap)
     count_row = send_counts[0]
     live_slots = (jnp.arange(slot_cap)[None, :] < count_row[:, None]).astype(jnp.float32)
-    payload = payload * live_slots[None]
+    payload = onehot_gather(flux_flat, send_idx[0], live_slots, 1).reshape(fields, rank_total, slot_cap)
     received = lax.all_to_all(payload, ("gx", "gy"), split_axis=1, concat_axis=1, tiled=True)
     received = received.reshape(fields, -1)
     source_count, ocean_x, ocean_y = remap_slots.shape
-    gathered = onehot_gather(received, remap_slots).reshape(fields, source_count, ocean_x, ocean_y)
-    ocean_flux = jnp.sum(remap_weights[None] * gathered, axis=1)
+    ocean_flux = onehot_gather(received, remap_slots, remap_weights, source_count).reshape(fields, ocean_x, ocean_y)
     velocity = ocean_velocity.at[0, 0].add(wind_coef * jnp.tanh(ocean_flux[0]))
     velocity = velocity.at[1, 0].add(wind_coef * jnp.tanh(ocean_flux[1]))
     tracers = ocean_tracers.at[0, 0].add(surf_coef * ocean_flux[2])

time: 92.4 us -> 90.7 us (0.982)
  waiting for transfers between devices: 17.1 us -> 15.7 us
  Pallas kernels: 9.81 us -> 8.55 us
  local copies, waits for them, and re-layouts: 9.69 us -> 10.7 us
    pallas_call x2, Pallas kernels: 9.81 us -> 8.55 us  [onehot_gather(): pl.pallas_call(gather_kernel, grid=(blocks, groups), in_specs=[pl.BlockSp...]
    unnamed x62 -> x58, local copies, waits for them, and re-layouts: 3.35 us -> 3.05 us
  transfers between devices with their start and end apart: 16 -> 16, of which waited for: 10 -> 10; matrix products, arithmetic and copies ran while one was open for 3% -> 5% of each run, Pallas kernels for 0% -> 0%
where the time goes in v14:
time: 90.7 us; the launch traced here: 90 us
  starting transfers between devices  19.8 us (22%)
  waiting for transfers between devices  15.7 us (17%)
  matrix products  15.1 us (17%)
  blocking collectives  14.5 us (16%)
  local copies, waits for them, and re-layouts  10.7 us (12%)
  Pallas kernels  8.55 us (9%)
  other arithmetic  4.31 us (5%)
  between operations  1.29 us (1%)
    ppermute x8, starting transfers between devices, neighbour(): lax.ppermute(values, 'gy', [(j, (j + step_y) % count_y) for j in range(co...  15.1 us
    all_to_all x1, blocking collectives, per_device(): lax.all_to_all(payload, ('gx', 'gy'), split_axis=1, concat_axis=1, tiled=...  14.5 us
    ppermute x8, waiting for transfers between devices, neighbour(): lax.ppermute(values, 'gy', [(j, (j + step_y) % count_y) for j in range(co...  12.4 us
    pallas_call x2, Pallas kernels, onehot_gather(): pl.pallas_call(gather_kernel, grid=(blocks, groups), in_specs=[pl.BlockSp...  8.55 us
    ppermute x8, starting transfers between devices, neighbour(): lax.ppermute(values, 'gx', [(i, (i + step_x) % count_x) for i in range(co...  4.67 us
    dot_general x2, matrix products, tracer_step(): jnp.einsum('ab,...by->...ay', sum_x, tracers, precision=precision)  4.15 us
    ppermute x8, waiting for transfers between devices, neighbour(): lax.ppermute(values, 'gx', [(i, (i + step_x) % count_x) for i in range(co...  3.3 us
    unnamed x58, local copies, waits for them, and re-layouts  3.05 us
  transfers between devices with their start and end apart: 16, of which 10 were waited for; matrix products, arithmetic and copies ran while one was open for 5% of the time, Pallas kernels for 0%

profile of v14, /device:TPU:0, one launch (start us, length us, event | category | flops | bytes accessed | tf_op | source)
XLA Modules:
  0.0 90.0 jit_solution(3799775778310661900)
XLA Ops:
  0.7 0.6 copy-done.17
  2.0 0.7 fusion.10
  2.7 0.7 convolution_bitcast_fusion.5
  3.5 0.7 fusion.50
  4.4 0.7 fusion.2
  5.2 0.7 fusion.1
  5.9 1.1 %slice_reduce_fusion.3 = (f32[160,16]{1,0:T(8,128)S(1)}, f32[160,16]{1,0:T(8,128)S(1)}) fusion(f32[160,16,128]{2,1,0:T(8,128)S(1)} %fusion.1), kind=kLoop, calls=%fused_computation.24 | loop fusion | bytes 40960 | tf_op jit(solution)/shard_map/slice | solution.py:87
  7.1 3.0 %collective-permute-start = (f32[20,128]{1,0:T(8,128)S(1)}, f32[20,128]{1,0:T(8,128)S(1)}, u32[]{:S(2)}, u32[]{:S(2)}) collective-permute-start(f32[20,128]{1,0:T(8,128)S(1)} %reshape_squeeze.39), channel_id=1, source_target_pairs={{0,1},{1,2},{2,3},{3,4},{4,5},{5,6},{6,7},{7,0},{8,9},{9,10},{10,1... | collective-permute-start | bytes 30728 | tf_op jit(solution)/shard_map/ppermute | solution.py:25
  10.1 3.1 %collective-permute-start.1 = (f32[20,128]{1,0:T(8,128)S(1)}, f32[20,128]{1,0:T(8,128)S(1)}, u32[]{:S(2)}, u32[]{:S(2)}) collective-permute-start(f32[20,128]{1,0:T(8,128)S(1)} %reshape_squeeze.40), channel_id=1, source_target_pairs={{0,7},{1,0},{2,1},{3,2},{4,3},{5,4},{6,5},{7,6},{8,15},{9,8},{10,9... | collective-permute-start | bytes 30728 | tf_op jit(solution)/shard_map/ppermute | solution.py:25
  13.3 1.5 %collective-permute-done = f32[20,128]{1,0:T(8,128)S(1)} collective-permute-done((f32[20,128]{1,0:T(8,128)S(1)}, f32[20,128]{1,0:T(8,128)S(1)}, u32[]{:S(2)}, u32[]{:S(2)}) %collective-permute-start) | collective-permute-done | bytes 10272 | tf_op jit(solution)/shard_map/ppermute | solution.py:25
  15.0 0.8 select_add_fusion.1
  16.0 1.7 %collective-permute-start.3 = (f32[160,128]{1,0:T(8,128)S(1)}, f32[160,128]{1,0:T(8,128)S(1)}, u32[]{:S(2)}, u32[]{:S(2)}) collective-permute-start(f32[160,128]{1,0:T(8,128)S(1)} %bitcast.151), channel_id=1, source_target_pairs={{0,24},{8,0},{16,8},{24,16},{1,25},{9,1},{17,9},{25,17},{2,26},{10... | collective-permute-start | bytes 245768 | tf_op jit(solution)/shard_map/ppermute | solution.py:23
  17.8 2.1 %collective-permute-done.2 = f32[160,128]{1,0:T(8,128)S(1)} collective-permute-done((f32[160,128]{1,0:T(8,128)S(1)}, f32[160,128]{1,0:T(8,128)S(1)}, u32[]{:S(2)}, u32[]{:S(2)}) %collective-permute-start.2) | collective-permute-done | bytes 81952 | tf_op jit(solution)/shard_map/ppermute | solution.py:23
  20.0 0.8 fusion.5
  20.8 0.7 fusion.6
  21.5 0.7 convolution_multiply_fusion.1
  22.2 0.7 convolution_bitcast_fusion.2
  22.9 0.7 fusion.51
  23.6 0.7 fusion
  24.3 1.1 %slice_reduce_fusion.1 = (f32[160,16]{1,0:T(8,128)S(1)}, f32[160,16]{1,0:T(8,128)S(1)}) fusion(f32[160,16,128]{2,1,0:T(8,128)S(1)} %fusion), kind=kLoop, calls=%fused_computation.22 | loop fusion | bytes 40960 | tf_op jit(solution)/shard_map/slice | solution.py:87
  25.5 1.4 %collective-permute-start.4 = (f32[20,128]{1,0:T(8,128)S(1)}, f32[20,128]{1,0:T(8,128)S(1)}, u32[]{:S(2)}, u32[]{:S(2)}) collective-permute-start(f32[20,128]{1,0:T(8,128)S(1)} %reshape_squeeze.41), channel_id=1, source_target_pairs={{0,1},{1,2},{2,3},{3,4},{4,5},{5,6},{6,7},{7,0},{8,9},{9,10},{10,1... | collective-permute-start | bytes 30728 | tf_op jit(solution)/shard_map/ppermute | solution.py:25
  27.0 3.4 %collective-permute-start.5 = (f32[20,128]{1,0:T(8,128)S(1)}, f32[20,128]{1,0:T(8,128)S(1)}, u32[]{:S(2)}, u32[]{:S(2)}) collective-permute-start(f32[20,128]{1,0:T(8,128)S(1)} %reshape_squeeze.42), channel_id=1, source_target_pairs={{0,7},{1,0},{2,1},{3,2},{4,3},{5,4},{6,5},{7,6},{8,15},{9,8},{10,9... | collective-permute-start | bytes 30728 | tf_op jit(solution)/shard_map/ppermute | solution.py:25
  30.4 1.5 %collective-permute-done.4 = f32[20,128]{1,0:T(8,128)S(1)} collective-permute-done((f32[20,128]{1,0:T(8,128)S(1)}, f32[20,128]{1,0:T(8,128)S(1)}, u32[]{:S(2)}, u32[]{:S(2)}) %collective-permute-start.4) | collective-permute-done | bytes 10272 | tf_op jit(solution)/shard_map/ppermute | solution.py:25
  32.2 0.8 select_add_fusion
  33.2 0.9 %collective-permute-start.6 = (f32[160,128]{1,0:T(8,128)S(1)}, f32[160,128]{1,0:T(8,128)S(1)}, u32[]{:S(2)}, u32[]{:S(2)}) collective-permute-start(f32[160,128]{1,0:T(8,128)S(1)} %bitcast.152), channel_id=1, source_target_pairs={{0,8},{8,16},{16,24},{24,0},{1,9},{9,17},{17,25},{25,1},{2,10},{10... | collective-permute-start | bytes 245768 | tf_op jit(solution)/shard_map/ppermute | solution.py:23
  34.1 0.9 collective-permute-start.7
  35.1 0.6 copy.52
  35.7 0.6 copy.51
  36.3 0.8 collective-permute-done.6
  37.4 0.8 fusion.9
  38.3 0.6 fusion.37.table_ref
  38.9 3.6 %shard_map.320 = f32[4,8192]{1,0:T(4,128)} custom-call(s32[1,8192]{1,0:T(1,128)} %bitcast.149, f32[1,8192]{1,0:T(1,128)} %bitcast.148, f32[4,16,128]{2,1,0:T(8,128)} %fusion.37.table_ref), custom_call_target="tpu_custom_call" | custom-call | tf_op jit(solution)/shard_map/pallas_call | solution.py:207
  42.5 14.5 %all_to_all.5 = f32[4,32,256]{2,0,1:T(4,128)S(1)} all-to-all(f32[4,32,256]{2,0,1:T(4,128)} %bitcast.147), channel_id=1, replica_groups=mesh['gx'=4,'gy'=8] {'gx','gy'}, dimensions={1} | all-to-all | bytes 262144 | tf_op jit(solution)/shard_map/all_to_all | solution.py:246
  57.1 0.7 reshape_reshape.3.table_ref
  57.8 4.9 %shard_map.321 = f32[4,2048]{1,0:T(4,128)} custom-call(s32[1,8192]{1,0:T(1,128)} %bitcast.158, f32[1,8192]{1,0:T(1,128)} %bitcast.159, f32[4,64,128]{2,1,0:T(8,128)} %reshape_reshape.3.table_ref), custom_call_target="tpu_custom_call" | custom-call | tf_op jit(solution)/shard_map/pallas_call | solution.py:207
  62.7 1.0 %fusion.38 = (f32[1,2048]{1,0:T(1,128)S(1)}, f32[1,2048]{1,0:T(1,128)S(1)}, f32[1,2048]{1,0:T(1,128)S(1)}, f32[1,2048]{1,0:T(1,128)S(1)}) fusion(f32[4,2048]{1,0:T(4,128)} %shard_map.321), kind=kLoop, calls=%fused_computation.76 | loop fusion | flops 8192 | bytes 65536 | tf_op jit(solution)/shard_map/mul | solution.py:251
  64.3 0.7 fusion.49
  66.3 0.7 reshape_squeeze.46
  67.0 2.0 %collective-permute-start.10 = (f32[10,128]{1,0:T(8,128)}, f32[10,128]{1,0:T(8,128)S(1)}, u32[]{:S(2)}, u32[]{:S(2)}) collective-permute-start(f32[10,128]{1,0:T(8,128)} %reshape_squeeze.46), channel_id=1, source_target_pairs={{0,7},{1,0},{2,1},{3,2},{4,3},{5,4},{6,5},{7,6},{8,15},{9,8},{10,9... | collective-permute-start | bytes 15368 | tf_op jit(solution)/shard_map/ppermute | solution.py:25
  69.7 0.9 fusion.36
  70.9 4.7 %collective-permute-done.11 = f32[10,128]{1,0:T(8,128)} collective-permute-done((f32[10,128]{1,0:T(8,128)S(1)}, f32[10,128]{1,0:T(8,128)}, u32[]{:S(2)}, u32[]{:S(2)}) %collective-permute-start.11) | collective-permute-done | bytes 5152 | tf_op jit(solution)/shard_map/ppermute | solution.py:25
  75.6 0.8 broadcast_in_dim.268
  76.4 1.9 %fusion.17 = f32[2,40,16,128]{3,2,1,0:T(8,128)S(1)} fusion(f32[2,40,16,128]{3,2,1,0:T(8,128)S(1)} %fusion.41, f32[2,40,16,128]{3,2,1,0:T(8,128)S(1)} %convolution_bitcast_fusion.8, f32[2,40,16,128]{3,2,1,0:T(8,128)S(1)} %fusion.52, f32[2,40,16,128]{3,2,1,0:T(8,128)S(1)} %fusion.53, f32[40,16,128]{2,1,0:T(8,128)} %get-tuple-element.69, ...), kind=kOutput, calls=%fused_computation.45 | convolution fusion | flops 19169280 | bytes 4025632 | tf_op jit(solution)/shard_map/ab,...by->...ay/dot_general | solution.py:120
  79.9 1.2 %collective-permute-start.14 = (f32[10,128]{1,0:T(8,128)S(1)}, f32[10,128]{1,0:T(8,128)S(1)}, u32[]{:S(2)}, u32[]{:S(2)}) collective-permute-start(f32[10,128]{1,0:T(8,128)S(1)} %reshape_squeeze.50), channel_id=1, source_target_pairs={{0,7},{1,0},{2,1},{3,2},{4,3},{5,4},{6,5},{7,6},{8,15},{9,8},{10,9... | collective-permute-start | bytes 15368 | tf_op jit(solution)/shard_map/ppermute | solution.py:25
  81.2 0.8 collective-permute-start.15
  83.0 0.6 collective-permute-done.14
  83.6 3.9 %collective-permute-done.15 = f32[10,128]{1,0:T(8,128)S(1)} collective-permute-done((f32[10,128]{1,0:T(8,128)S(1)}, f32[10,128]{1,0:T(8,128)S(1)}, u32[]{:S(2)}, u32[]{:S(2)}) %collective-permute-start.15) | collective-permute-done | bytes 5152 | tf_op jit(solution)/shard_map/ppermute | solution.py:25
  87.7 2.3 %fusion.29 = f32[2,40,16,128]{3,2,1,0:T(8,128)} fusion(f32[2,40,16,128]{3,2,1,0:T(8,128)S(1)} %fusion.17, f32[2,40,16,128]{3,2,1,0:T(8,128)S(1)} %convolution_bitcast_fusion.6, f32[2,40,16,128]{3,2,1,0:T(8,128)S(1)} %fusion.54, f32[2,40,16,128]{3,2,1,0:T(8,128)S(1)} %fusion.55, f32[2,40,16]{2,1,0:T(8,128)S(1)} %broadcast_in_dim.276, ...), kind=kOutput, calls=%fused_computation.57 | convolution fusion | flops 19169280 | bytes 4025632 | tf_op jit(solution)/shard_map/ab,...by->...ay/dot_general | solution.py:120
  (105 shorter events, 8.3 us)
Async XLA Ops:
  0.6 0.7 copy-start.17
  0.6 0.7 copy-start.27
  0.7 0.9 %copy-start.11 = (f32[16,16,1]{1,0,2:T(8,128)S(1)}, f32[16,16,1]{1,0,2:T(8,128)}, u32[]{:S(2)}) copy-start(f32[16,16,1]{1,0,2:T(8,128)} %constant.166) | copy-start | bytes 3076
  0.7 1.3 %copy-start.1 = (f32[4,40,16,128]{3,2,1,0:T(8,128)S(1)}, f32[4,40,16,128]{3,2,1,0:T(8,128)}, u32[]{:S(2)}) copy-start(f32[4,40,16,128]{3,2,1,0:T(8,128)} %param.41) | copy-start | bytes 3932164
  0.7 0.8 copy-start.16
  2.7 0.8 copy-start.10
  3.5 0.8 copy-start.7
  4.4 0.8 copy-start.6
  7.1 7.7 %collective-permute-start = (f32[20,128]{1,0:T(8,128)S(1)}, f32[20,128]{1,0:T(8,128)S(1)}, u32[]{:S(2)}, u32[]{:S(2)}) collective-permute-start(f32[20,128]{1,0:T(8,128)S(1)} %reshape_squeeze.39), channel_id=1, source_target_pairs={{0,1},{1,2},{2,3},{3,4},{4,5},{5,6},{6,7},{7,0},{8,9},{9,10},{10,1... | collective-permute-start | bytes 30728 | tf_op jit(solution)/shard_map/ppermute | solution.py:25
  10.1 4.7 %collective-permute-start.1 = (f32[20,128]{1,0:T(8,128)S(1)}, f32[20,128]{1,0:T(8,128)S(1)}, u32[]{:S(2)}, u32[]{:S(2)}) collective-permute-start(f32[20,128]{1,0:T(8,128)S(1)} %reshape_squeeze.40), channel_id=1, source_target_pairs={{0,7},{1,0},{2,1},{3,2},{4,3},{5,4},{6,5},{7,6},{8,15},{9,8},{10,9... | collective-permute-start | bytes 30728 | tf_op jit(solution)/shard_map/ppermute | solution.py:25
  13.3 18.9 %copy-start.18 = (pred[128]{0:T(512)(128)(4,1)}, pred[128]{0:T(512)(128)(4,1)S(1)}, u32[]{:S(2)}) copy-start(pred[128]{0:T(512)(128)(4,1)S(1)} %get-tuple-element.76) | copy-start | bytes 388
  13.3 18.9 %copy-start.20 = (pred[128]{0:T(512)(128)(4,1)}, pred[128]{0:T(512)(128)(4,1)S(1)}, u32[]{:S(2)}) copy-start(pred[128]{0:T(512)(128)(4,1)S(1)} %get-tuple-element.77) | copy-start | bytes 388
  15.0 5.0 %copy-start.13 = (f32[16,128]{1,0:T(8,128)S(1)}, f32[16,128]{1,0:T(8,128)}, u32[]{:S(2)}) copy-start(f32[16,128]{1,0:T(8,128)} %constant.165) | copy-start | bytes 24580
  15.0 5.0 %copy-start.14 = (f32[16,16,1]{1,0,2:T(8,128)S(1)}, f32[16,16,1]{1,0,2:T(8,128)}, u32[]{:S(2)}) copy-start(f32[16,16,1]{1,0,2:T(8,128)} %constant.170) | copy-start | bytes 3076
  16.0 3.9 %collective-permute-start.2 = (f32[160,128]{1,0:T(8,128)S(1)}, f32[160,128]{1,0:T(8,128)S(1)}, u32[]{:S(2)}, u32[]{:S(2)}) collective-permute-start(f32[160,128]{1,0:T(8,128)S(1)} %bitcast.153), channel_id=1, source_target_pairs={{0,8},{8,16},{16,24},{24,0},{1,9},{9,17},{17,25},{25,1},{2,10},{10... | collective-permute-start | bytes 245768 | tf_op jit(solution)/shard_map/ppermute | solution.py:23
  16.0 4.0 %collective-permute-start.3 = (f32[160,128]{1,0:T(8,128)S(1)}, f32[160,128]{1,0:T(8,128)S(1)}, u32[]{:S(2)}, u32[]{:S(2)}) collective-permute-start(f32[160,128]{1,0:T(8,128)S(1)} %bitcast.151), channel_id=1, source_target_pairs={{0,24},{8,0},{16,8},{24,16},{1,25},{9,1},{17,9},{25,17},{2,26},{10... | collective-permute-start | bytes 245768 | tf_op jit(solution)/shard_map/ppermute | solution.py:23
  17.8 19.6 %copy-start.22 = (pred[16]{0:T(512)(128)(4,1)}, pred[16]{0:T(512)(128)(4,1)S(1)}, u32[]{:S(2)}) copy-start(pred[16]{0:T(512)(128)(4,1)S(1)} %get-tuple-element.78) | copy-start | bytes 52
  17.8 19.6 %copy-start.24 = (pred[16]{0:T(512)(128)(4,1)}, pred[16]{0:T(512)(128)(4,1)S(1)}, u32[]{:S(2)}) copy-start(pred[16]{0:T(512)(128)(4,1)S(1)} %get-tuple-element.79) | copy-start | bytes 52
  25.5 6.5 %collective-permute-start.4 = (f32[20,128]{1,0:T(8,128)S(1)}, f32[20,128]{1,0:T(8,128)S(1)}, u32[]{:S(2)}, u32[]{:S(2)}) collective-permute-start(f32[20,128]{1,0:T(8,128)S(1)} %reshape_squeeze.41), channel_id=1, source_target_pairs={{0,1},{1,2},{2,3},{3,4},{4,5},{5,6},{6,7},{7,0},{8,9},{9,10},{10,1... | collective-permute-start | bytes 30728 | tf_op jit(solution)/shard_map/ppermute | solution.py:25
  27.0 5.1 %collective-permute-start.5 = (f32[20,128]{1,0:T(8,128)S(1)}, f32[20,128]{1,0:T(8,128)S(1)}, u32[]{:S(2)}, u32[]{:S(2)}) collective-permute-start(f32[20,128]{1,0:T(8,128)S(1)} %reshape_squeeze.42), channel_id=1, source_target_pairs={{0,7},{1,0},{2,1},{3,2},{4,3},{5,4},{6,5},{7,6},{8,15},{9,8},{10,9... | collective-permute-start | bytes 30728 | tf_op jit(solution)/shard_map/ppermute | solution.py:25
  32.2 2.8 %copy-start.26 = (s32[1,32]{1,0:T(1,128)S(1)}, s32[1,32]{1,0:T(1,128)}, u32[]{:S(2)}) copy-start(s32[1,32]{1,0:T(1,128)} %param.44) | copy-start | bytes 388
  32.2 3.5 %copy-start.15 = (s32[1,32,256]{2,1,0:T(8,128)S(1)}, s32[1,32,256]{2,1,0:T(8,128)}, u32[]{:S(2)}) copy-start(s32[1,32,256]{2,1,0:T(8,128)} %param.43) | copy-start | bytes 98308
  33.2 3.9 %collective-permute-start.6 = (f32[160,128]{1,0:T(8,128)S(1)}, f32[160,128]{1,0:T(8,128)S(1)}, u32[]{:S(2)}, u32[]{:S(2)}) collective-permute-start(f32[160,128]{1,0:T(8,128)S(1)} %bitcast.152), channel_id=1, source_target_pairs={{0,8},{8,16},{16,24},{24,0},{1,9},{9,17},{17,25},{25,1},{2,10},{10... | collective-permute-start | bytes 245768 | tf_op jit(solution)/shard_map/ppermute | solution.py:23
  34.1 3.3 %collective-permute-start.7 = (f32[160,128]{1,0:T(8,128)S(1)}, f32[160,128]{1,0:T(8,128)S(1)}, u32[]{:S(2)}, u32[]{:S(2)}) collective-permute-start(f32[160,128]{1,0:T(8,128)S(1)} %bitcast.150), channel_id=1, source_target_pairs={{0,24},{8,0},{16,8},{24,16},{1,25},{9,1},{17,9},{25,17},{2,26},{10... | collective-permute-start | bytes 245768 | tf_op jit(solution)/shard_map/ppermute | solution.py:23
  38.3 26.1 %copy-start.3 = (f32[160,16,128]{2,1,0:T(8,128)}, f32[160,16,128]{2,1,0:T(8,128)S(1)}, u32[]{:S(2)}) copy-start(f32[160,16,128]{2,1,0:T(8,128)S(1)} %fusion.9) | copy-start | bytes 3932164
  38.3 25.4 %copy-start = (f32[2,40,16,128]{3,2,1,0:T(8,128)S(1)}, f32[2,40,16,128]{3,2,1,0:T(8,128)}, u32[]{:S(2)}) copy-start(f32[2,40,16,128]{3,2,1,0:T(8,128)} %param.45) | copy-start | bytes 1966084
  42.5 22.5 %copy-start.12 = (f32[16,16,1,1]{1,0,3,2:T(8,128)S(1)}, f32[16,16,1,1]{1,0,3,2:T(8,128)}, u32[]{:S(2)}) copy-start(f32[16,16,1,1]{1,0,3,2:T(8,128)} %constant.173) | copy-start | bytes 3076
  63.7 1.7 %copy-start.9 = (f32[128,128,1,1]{1,0,3,2:T(8,128)S(1)}, f32[128,128,1,1]{1,0,3,2:T(8,128)}, u32[]{:S(2)}) copy-start(f32[128,128,1,1]{1,0,3,2:T(8,128)} %constant.172) | copy-start | bytes 196612
  65.0 0.9 copy-start.8
  65.4 4.3 %copy-start.2 = (f32[2,40,16,128]{3,2,1,0:T(8,128)S(1)}, f32[2,40,16,128]{3,2,1,0:T(8,128)}, u32[]{:S(2)}) copy-start(f32[2,40,16,128]{3,2,1,0:T(8,128)} %param.46) | copy-start | bytes 1966084
  67.0 3.9 %collective-permute-start.10 = (f32[10,128]{1,0:T(8,128)}, f32[10,128]{1,0:T(8,128)S(1)}, u32[]{:S(2)}, u32[]{:S(2)}) collective-permute-start(f32[10,128]{1,0:T(8,128)} %reshape_squeeze.46), channel_id=1, source_target_pairs={{0,7},{1,0},{2,1},{3,2},{4,3},{5,4},{6,5},{7,6},{8,15},{9,8},{10,9... | collective-permute-start | bytes 15368 | tf_op jit(solution)/shard_map/ppermute | solution.py:25
  69.1 6.5 %collective-permute-start.11 = (f32[10,128]{1,0:T(8,128)S(1)}, f32[10,128]{1,0:T(8,128)}, u32[]{:S(2)}, u32[]{:S(2)}) collective-permute-start(f32[10,128]{1,0:T(8,128)S(1)} %reshape_squeeze.47), channel_id=1, source_target_pairs={{0,1},{1,2},{2,3},{3,4},{4,5},{5,6},{6,7},{7,0},{8,9},{9,10},{10,1... | collective-permute-start | bytes 15368 | tf_op jit(solution)/shard_map/ppermute | solution.py:25
  69.1 7.2 %collective-permute-start.8 = (f32[80,128]{1,0:T(8,128)}, f32[80,128]{1,0:T(8,128)}, u32[]{:S(2)}, u32[]{:S(2)}) collective-permute-start(f32[80,128]{1,0:T(8,128)} %bitcast.155), channel_id=1, source_target_pairs={{0,24},{8,0},{16,8},{24,16},{1,25},{9,1},{17,9},{25,17},{2,26},{10... | collective-permute-start | bytes 122888 | tf_op jit(solution)/shard_map/ppermute | solution.py:23
  69.2 7.2 %collective-permute-start.9 = (f32[80,128]{1,0:T(8,128)S(1)}, f32[80,128]{1,0:T(8,128)}, u32[]{:S(2)}, u32[]{:S(2)}) collective-permute-start(f32[80,128]{1,0:T(8,128)S(1)} %bitcast.154), channel_id=1, source_target_pairs={{0,8},{8,16},{16,24},{24,0},{1,9},{9,17},{17,25},{25,1},{2,10},{10... | collective-permute-start | bytes 122888 | tf_op jit(solution)/shard_map/ppermute | solution.py:23
  69.7 6.7 %copy-start.19 = (pred[128]{0:T(512)(128)(4,1)S(1)}, pred[128]{0:T(512)(128)(4,1)}, u32[]{:S(2)}) copy-start(pred[128]{0:T(512)(128)(4,1)} %copy-done.18) | copy-start | bytes 388
  69.7 6.7 %copy-start.21 = (pred[128]{0:T(512)(128)(4,1)S(1)}, pred[128]{0:T(512)(128)(4,1)}, u32[]{:S(2)}) copy-start(pred[128]{0:T(512)(128)(4,1)} %copy-done.20) | copy-start | bytes 388
  69.7 6.7 %copy-start.23 = (pred[16]{0:T(512)(128)(4,1)S(1)}, pred[16]{0:T(512)(128)(4,1)}, u32[]{:S(2)}) copy-start(pred[16]{0:T(512)(128)(4,1)} %copy-done.22) | copy-start | bytes 52
  69.7 6.7 %copy-start.25 = (pred[16]{0:T(512)(128)(4,1)S(1)}, pred[16]{0:T(512)(128)(4,1)}, u32[]{:S(2)}) copy-start(pred[16]{0:T(512)(128)(4,1)} %copy-done.24) | copy-start | bytes 52
  79.1 8.5 %copy-start.4 = (f32[40,16,128]{2,1,0:T(8,128)S(1)}, f32[40,16,128]{2,1,0:T(8,128)}, u32[]{:S(2)}) copy-start(f32[40,16,128]{2,1,0:T(8,128)} %get-tuple-element.68) | copy-start | bytes 983044
  79.1 8.5 %copy-start.5 = (f32[40,16,128]{2,1,0:T(8,128)S(1)}, f32[40,16,128]{2,1,0:T(8,128)}, u32[]{:S(2)}) copy-start(f32[40,16,128]{2,1,0:T(8,128)} %get-tuple-element.69) | copy-start | bytes 983044
  79.9 3.7 %collective-permute-start.14 = (f32[10,128]{1,0:T(8,128)S(1)}, f32[10,128]{1,0:T(8,128)S(1)}, u32[]{:S(2)}, u32[]{:S(2)}) collective-permute-start(f32[10,128]{1,0:T(8,128)S(1)} %reshape_squeeze.50), channel_id=1, source_target_pairs={{0,7},{1,0},{2,1},{3,2},{4,3},{5,4},{6,5},{7,6},{8,15},{9,8},{10,9... | collective-permute-start | bytes 15368 | tf_op jit(solution)/shard_map/ppermute | solution.py:25
  81.2 6.4 %collective-permute-start.15 = (f32[10,128]{1,0:T(8,128)S(1)}, f32[10,128]{1,0:T(8,128)S(1)}, u32[]{:S(2)}, u32[]{:S(2)}) collective-permute-start(f32[10,128]{1,0:T(8,128)S(1)} %reshape_squeeze.51), channel_id=1, source_target_pairs={{0,1},{1,2},{2,3},{3,4},{4,5},{5,6},{6,7},{7,0},{8,9},{9,10},{10,1... | collective-permute-start | bytes 15368 | tf_op jit(solution)/shard_map/ppermute | solution.py:25
  82.0 5.6 %collective-permute-start.12 = (f32[80,128]{1,0:T(8,128)S(1)}, f32[80,128]{1,0:T(8,128)S(1)}, u32[]{:S(2)}, u32[]{:S(2)}) collective-permute-start(f32[80,128]{1,0:T(8,128)S(1)} %bitcast.157), channel_id=1, source_target_pairs={{0,24},{8,0},{16,8},{24,16},{1,25},{9,1},{17,9},{25,17},{2,26},{10... | collective-permute-start | bytes 122888 | tf_op jit(solution)/shard_map/ppermute | solution.py:23
  82.0 5.6 %collective-permute-start.13 = (f32[80,128]{1,0:T(8,128)S(1)}, f32[80,128]{1,0:T(8,128)S(1)}, u32[]{:S(2)}, u32[]{:S(2)}) collective-permute-start(f32[80,128]{1,0:T(8,128)S(1)} %bitcast.156), channel_id=1, source_target_pairs={{0,8},{8,16},{16,24},{24,0},{1,9},{9,17},{17,25},{25,1},{2,10},{10... | collective-permute-start | bytes 122888 | tf_op jit(solution)/shard_map/ppermute | solution.py:23

commit v15 on v14

--- a/solution.py
+++ b/solution.py
@@ -167,17 +167,18 @@
 
 
 def gather_kernel(index_ref, scale_ref, table_ref, out_ref):
-    fields, rows, tile = table_ref.shape[0], table_ref.shape[1], out_ref.shape[1]
+    fields, rows, lanes = table_ref.shape
+    tile = out_ref.shape[1]
     index = index_ref[...]
-    onehot = (lax.broadcasted_iota(jnp.int32, (128, tile), 0) == (index & 127)).astype(jnp.bfloat16)
-    select = lax.broadcasted_iota(jnp.int32, (rows, tile), 0) == (index >> 7)
+    onehot = (lax.broadcasted_iota(jnp.int32, (lanes, tile), 0) == (index % lanes)).astype(jnp.bfloat16)
+    select = lax.broadcasted_iota(jnp.int32, (rows, tile), 0) == (index // lanes)
     rest = table_ref[...]
     parts = []
     for part in range(3):
         piece = rest.astype(jnp.bfloat16)
         rest = rest - piece.astype(jnp.float32)
         parts.append(piece)
-    stacked = jnp.concatenate(parts, axis=2).reshape(fields * rows, 3 * 128)
+    stacked = jnp.concatenate(parts, axis=2).reshape(fields * rows, 3 * lanes)
     picked = jnp.dot(stacked, jnp.concatenate([onehot] * 3, axis=0), preferred_element_type=jnp.float32)
     scale = scale_ref[...]
     values = jnp.concatenate(
@@ -195,8 +196,7 @@
 
 
 def onehot_gather(table, index, scale, groups):
-    fields, total = table.shape
-    rows = total // 128
+    fields, rows, lanes = table.shape
     flat = index.reshape(1, -1)
     count = flat.shape[1]
     width = count // groups
@@ -210,11 +210,11 @@
         in_specs=[
             pl.BlockSpec((1, tile), lambda step, group: (0, group * blocks + step)),
             pl.BlockSpec((1, tile), lambda step, group: (0, group * blocks + step)),
-            pl.BlockSpec((fields, rows, 128), lambda step, group: (0, 0, 0)),
+            pl.BlockSpec((fields, rows, lanes), lambda step, group: (0, 0, 0)),
         ],
         out_specs=pl.BlockSpec((fields, tile), lambda step, group: (0, step)),
         out_shape=jax.ShapeDtypeStruct((fields, width), jnp.float32),
-    )(flat, scale.reshape(1, -1), table.reshape(fields, rows, 128))
+    )(flat, scale.reshape(1, -1), table)
 
 
 def per_device(
@@ -242,9 +242,9 @@
     slot_cap = send_idx.shape[2]
     count_row = send_counts[0]
     live_slots = (jnp.arange(slot_cap)[None, :] < count_row[:, None]).astype(jnp.float32)
-    payload = onehot_gather(flux_flat, send_idx[0], live_slots, 1).reshape(fields, rank_total, slot_cap)
+    flux_table = flux_flat.reshape(fields, node_total // 128, 128)
+    payload = onehot_gather(flux_table, send_idx[0], live_slots, 1).reshape(fields, rank_total, slot_cap)
     received = lax.all_to_all(payload, ("gx", "gy"), split_axis=1, concat_axis=1, tiled=True)
-    received = received.reshape(fields, -1)
     source_count, ocean_x, ocean_y = remap_slots.shape
     ocean_flux = onehot_gather(received, remap_slots, remap_weights, source_count).reshape(fields, ocean_x, ocean_y)
     velocity = ocean_velocity.at[0, 0].add(wind_coef * jnp.tanh(ocean_flux[0]))

time: 90.7 us -> 90.5 us (level)
  no operation moved by 1% of the time
where the time goes in v15:
time: 90.5 us; the launch traced here: 89.7 us
  starting transfers between devices  19.8 us (22%)
  waiting for transfers between devices  15.7 us (17%)
  matrix products  15.1 us (17%)
  blocking collectives  14.6 us (16%)
  local copies, waits for them, and re-layouts  10.7 us (12%)
  Pallas kernels  8.27 us (9%)
  other arithmetic  4.39 us (5%)
  between operations  1.27 us (1%)
    ppermute x8, starting transfers between devices, neighbour(): lax.ppermute(values, 'gy', [(j, (j + step_y) % count_y) for j in range(co...  15.1 us
    all_to_all x1, blocking collectives, per_device(): lax.all_to_all(payload, ('gx', 'gy'), split_axis=1, concat_axis=1, tiled=...  14.6 us
    ppermute x8, waiting for transfers between devices, neighbour(): lax.ppermute(values, 'gy', [(j, (j + step_y) % count_y) for j in range(co...  12.4 us
    pallas_call x2, Pallas kernels, onehot_gather(): pl.pallas_call(gather_kernel, grid=(blocks, groups), in_specs=[pl.BlockSp...  8.27 us
    ppermute x8, starting transfers between devices, neighbour(): lax.ppermute(values, 'gx', [(i, (i + step_x) % count_x) for i in range(co...  4.67 us
    dot_general x2, matrix products, tracer_step(): jnp.einsum('ab,...by->...ay', sum_x, tracers, precision=precision)  4.15 us
    ppermute x8, waiting for transfers between devices, neighbour(): lax.ppermute(values, 'gx', [(i, (i + step_x) % count_x) for i in range(co...  3.3 us
    unnamed x58, local copies, waits for them, and re-layouts  3.05 us
  transfers between devices with their start and end apart: 16, of which 10 were waited for; matrix products, arithmetic and copies ran while one was open for 5% of the time, Pallas kernels for 0%

profile of v15, /device:TPU:0, one launch (start us, length us, event | category | flops | bytes accessed | tf_op | source)
XLA Modules:
  0.0 89.7 jit_solution(18395806628784506991)
XLA Ops:
  0.7 0.6 copy-done.17
  2.0 0.7 fusion.10
  2.7 0.7 convolution_bitcast_fusion.5
  3.5 0.7 fusion.50
  4.4 0.7 fusion.2
  5.2 0.7 fusion.1
  5.9 1.1 %slice_reduce_fusion.3 = (f32[160,16]{1,0:T(8,128)S(1)}, f32[160,16]{1,0:T(8,128)S(1)}) fusion(f32[160,16,128]{2,1,0:T(8,128)S(1)} %fusion.1), kind=kLoop, calls=%fused_computation.24 | loop fusion | bytes 40960 | tf_op jit(solution)/shard_map/slice | solution.py:87
  7.1 3.0 %collective-permute-start = (f32[20,128]{1,0:T(8,128)S(1)}, f32[20,128]{1,0:T(8,128)S(1)}, u32[]{:S(2)}, u32[]{:S(2)}) collective-permute-start(f32[20,128]{1,0:T(8,128)S(1)} %reshape_squeeze.39), channel_id=1, source_target_pairs={{0,1},{1,2},{2,3},{3,4},{4,5},{5,6},{6,7},{7,0},{8,9},{9,10},{10,1... | collective-permute-start | bytes 30728 | tf_op jit(solution)/shard_map/ppermute | solution.py:25
  10.1 3.1 %collective-permute-start.1 = (f32[20,128]{1,0:T(8,128)S(1)}, f32[20,128]{1,0:T(8,128)S(1)}, u32[]{:S(2)}, u32[]{:S(2)}) collective-permute-start(f32[20,128]{1,0:T(8,128)S(1)} %reshape_squeeze.40), channel_id=1, source_target_pairs={{0,7},{1,0},{2,1},{3,2},{4,3},{5,4},{6,5},{7,6},{8,15},{9,8},{10,9... | collective-permute-start | bytes 30728 | tf_op jit(solution)/shard_map/ppermute | solution.py:25
  13.3 1.5 %collective-permute-done = f32[20,128]{1,0:T(8,128)S(1)} collective-permute-done((f32[20,128]{1,0:T(8,128)S(1)}, f32[20,128]{1,0:T(8,128)S(1)}, u32[]{:S(2)}, u32[]{:S(2)}) %collective-permute-start) | collective-permute-done | bytes 10272 | tf_op jit(solution)/shard_map/ppermute | solution.py:25
  15.0 0.8 select_add_fusion.1
  16.0 1.7 %collective-permute-start.3 = (f32[160,128]{1,0:T(8,128)S(1)}, f32[160,128]{1,0:T(8,128)S(1)}, u32[]{:S(2)}, u32[]{:S(2)}) collective-permute-start(f32[160,128]{1,0:T(8,128)S(1)} %bitcast.151), channel_id=1, source_target_pairs={{0,24},{8,0},{16,8},{24,16},{1,25},{9,1},{17,9},{25,17},{2,26},{10... | collective-permute-start | bytes 245768 | tf_op jit(solution)/shard_map/ppermute | solution.py:23
  17.8 2.1 %collective-permute-done.2 = f32[160,128]{1,0:T(8,128)S(1)} collective-permute-done((f32[160,128]{1,0:T(8,128)S(1)}, f32[160,128]{1,0:T(8,128)S(1)}, u32[]{:S(2)}, u32[]{:S(2)}) %collective-permute-start.2) | collective-permute-done | bytes 81952 | tf_op jit(solution)/shard_map/ppermute | solution.py:23
  20.0 0.8 fusion.5
  20.8 0.7 fusion.6
  21.5 0.7 convolution_multiply_fusion.1
  22.2 0.7 convolution_bitcast_fusion.2
  22.9 0.7 fusion.51
  23.6 0.7 fusion
  24.3 1.1 %slice_reduce_fusion.1 = (f32[160,16]{1,0:T(8,128)S(1)}, f32[160,16]{1,0:T(8,128)S(1)}) fusion(f32[160,16,128]{2,1,0:T(8,128)S(1)} %fusion), kind=kLoop, calls=%fused_computation.22 | loop fusion | bytes 40960 | tf_op jit(solution)/shard_map/slice | solution.py:87
  25.5 1.4 %collective-permute-start.4 = (f32[20,128]{1,0:T(8,128)S(1)}, f32[20,128]{1,0:T(8,128)S(1)}, u32[]{:S(2)}, u32[]{:S(2)}) collective-permute-start(f32[20,128]{1,0:T(8,128)S(1)} %reshape_squeeze.41), channel_id=1, source_target_pairs={{0,1},{1,2},{2,3},{3,4},{4,5},{5,6},{6,7},{7,0},{8,9},{9,10},{10,1... | collective-permute-start | bytes 30728 | tf_op jit(solution)/shard_map/ppermute | solution.py:25
  27.0 3.4 %collective-permute-start.5 = (f32[20,128]{1,0:T(8,128)S(1)}, f32[20,128]{1,0:T(8,128)S(1)}, u32[]{:S(2)}, u32[]{:S(2)}) collective-permute-start(f32[20,128]{1,0:T(8,128)S(1)} %reshape_squeeze.42), channel_id=1, source_target_pairs={{0,7},{1,0},{2,1},{3,2},{4,3},{5,4},{6,5},{7,6},{8,15},{9,8},{10,9... | collective-permute-start | bytes 30728 | tf_op jit(solution)/shard_map/ppermute | solution.py:25
  30.4 1.5 %collective-permute-done.4 = f32[20,128]{1,0:T(8,128)S(1)} collective-permute-done((f32[20,128]{1,0:T(8,128)S(1)}, f32[20,128]{1,0:T(8,128)S(1)}, u32[]{:S(2)}, u32[]{:S(2)}) %collective-permute-start.4) | collective-permute-done | bytes 10272 | tf_op jit(solution)/shard_map/ppermute | solution.py:25
  32.2 0.8 select_add_fusion
  33.2 0.9 %collective-permute-start.6 = (f32[160,128]{1,0:T(8,128)S(1)}, f32[160,128]{1,0:T(8,128)S(1)}, u32[]{:S(2)}, u32[]{:S(2)}) collective-permute-start(f32[160,128]{1,0:T(8,128)S(1)} %bitcast.152), channel_id=1, source_target_pairs={{0,8},{8,16},{16,24},{24,0},{1,9},{9,17},{17,25},{25,1},{2,10},{10... | collective-permute-start | bytes 245768 | tf_op jit(solution)/shard_map/ppermute | solution.py:23
  34.1 0.9 collective-permute-start.7
  35.1 0.6 copy.52
  35.7 0.6 copy.51
  36.3 0.8 collective-permute-done.6
  37.4 0.8 fusion.9
  38.3 0.7 fusion.37.table_ref
  39.0 3.6 %shard_map.320 = f32[4,8192]{1,0:T(4,128)} custom-call(s32[1,8192]{1,0:T(1,128)} %bitcast.149, f32[1,8192]{1,0:T(1,128)} %bitcast.148, f32[4,16,128]{2,1,0:T(8,128)} %fusion.37.table_ref), custom_call_target="tpu_custom_call" | custom-call | tf_op jit(solution)/shard_map/pallas_call | solution.py:207
  42.6 14.6 %all_to_all.5 = f32[4,32,256]{2,0,1:T(4,128)S(1)} all-to-all(f32[4,32,256]{2,0,1:T(4,128)} %bitcast.147), channel_id=1, replica_groups=mesh['gx'=4,'gy'=8] {'gx','gy'}, dimensions={1} | all-to-all | bytes 262144 | tf_op jit(solution)/shard_map/all_to_all | solution.py:247
  57.1 0.7 copy.41.table_ref
  57.8 4.7 %shard_map.321 = f32[4,2048]{1,0:T(4,128)} custom-call(s32[1,8192]{1,0:T(1,128)} %bitcast.158, f32[1,8192]{1,0:T(1,128)} %bitcast.159, f32[4,32,256]{2,1,0:T(8,128)} %copy.41.table_ref), custom_call_target="tpu_custom_call" | custom-call | tf_op jit(solution)/shard_map/pallas_call | solution.py:207
  62.5 1.0 %fusion.38 = (f32[1,2048]{1,0:T(1,128)S(1)}, f32[1,2048]{1,0:T(1,128)S(1)}, f32[1,2048]{1,0:T(1,128)S(1)}, f32[1,2048]{1,0:T(1,128)S(1)}) fusion(f32[4,2048]{1,0:T(4,128)} %shard_map.321), kind=kLoop, calls=%fused_computation.76 | loop fusion | flops 8192 | bytes 65536 | tf_op jit(solution)/shard_map/mul | solution.py:251
  64.1 0.7 fusion.49
  66.1 0.7 reshape_squeeze.46
  66.7 2.0 %collective-permute-start.10 = (f32[10,128]{1,0:T(8,128)}, f32[10,128]{1,0:T(8,128)S(1)}, u32[]{:S(2)}, u32[]{:S(2)}) collective-permute-start(f32[10,128]{1,0:T(8,128)} %reshape_squeeze.46), channel_id=1, source_target_pairs={{0,7},{1,0},{2,1},{3,2},{4,3},{5,4},{6,5},{7,6},{8,15},{9,8},{10,9... | collective-permute-start | bytes 15368 | tf_op jit(solution)/shard_map/ppermute | solution.py:25
  69.5 0.9 fusion.36
  70.7 4.7 %collective-permute-done.11 = f32[10,128]{1,0:T(8,128)} collective-permute-done((f32[10,128]{1,0:T(8,128)S(1)}, f32[10,128]{1,0:T(8,128)}, u32[]{:S(2)}, u32[]{:S(2)}) %collective-permute-start.11) | collective-permute-done | bytes 5152 | tf_op jit(solution)/shard_map/ppermute | solution.py:25
  75.3 0.8 broadcast_in_dim.268
  76.2 1.9 %fusion.17 = f32[2,40,16,128]{3,2,1,0:T(8,128)S(1)} fusion(f32[2,40,16,128]{3,2,1,0:T(8,128)S(1)} %fusion.41, f32[2,40,16,128]{3,2,1,0:T(8,128)S(1)} %convolution_bitcast_fusion.8, f32[2,40,16,128]{3,2,1,0:T(8,128)S(1)} %fusion.52, f32[2,40,16,128]{3,2,1,0:T(8,128)S(1)} %fusion.53, f32[40,16,128]{2,1,0:T(8,128)} %get-tuple-element.69, ...), kind=kOutput, calls=%fused_computation.45 | convolution fusion | flops 19169280 | bytes 4025632 | tf_op jit(solution)/shard_map/ab,...by->...ay/dot_general | solution.py:120
  79.6 1.2 %collective-permute-start.14 = (f32[10,128]{1,0:T(8,128)S(1)}, f32[10,128]{1,0:T(8,128)S(1)}, u32[]{:S(2)}, u32[]{:S(2)}) collective-permute-start(f32[10,128]{1,0:T(8,128)S(1)} %reshape_squeeze.50), channel_id=1, source_target_pairs={{0,7},{1,0},{2,1},{3,2},{4,3},{5,4},{6,5},{7,6},{8,15},{9,8},{10,9... | collective-permute-start | bytes 15368 | tf_op jit(solution)/shard_map/ppermute | solution.py:25
  80.9 0.9 collective-permute-start.15
  82.7 0.6 collective-permute-done.14
  83.4 3.9 %collective-permute-done.15 = f32[10,128]{1,0:T(8,128)S(1)} collective-permute-done((f32[10,128]{1,0:T(8,128)S(1)}, f32[10,128]{1,0:T(8,128)S(1)}, u32[]{:S(2)}, u32[]{:S(2)}) %collective-permute-start.15) | collective-permute-done | bytes 5152 | tf_op jit(solution)/shard_map/ppermute | solution.py:25
  87.4 2.3 %fusion.29 = f32[2,40,16,128]{3,2,1,0:T(8,128)} fusion(f32[2,40,16,128]{3,2,1,0:T(8,128)S(1)} %fusion.17, f32[2,40,16,128]{3,2,1,0:T(8,128)S(1)} %convolution_bitcast_fusion.6, f32[2,40,16,128]{3,2,1,0:T(8,128)S(1)} %fusion.54, f32[2,40,16,128]{3,2,1,0:T(8,128)S(1)} %fusion.55, f32[2,40,16]{2,1,0:T(8,128)S(1)} %broadcast_in_dim.276, ...), kind=kOutput, calls=%fused_computation.57 | convolution fusion | flops 19169280 | bytes 4025632 | tf_op jit(solution)/shard_map/ab,...by->...ay/dot_general | solution.py:120
  (104 shorter events, 8.2 us)
Async XLA Ops:
  0.6 0.7 copy-start.17
  0.6 0.7 copy-start.27
  0.7 0.9 %copy-start.11 = (f32[16,16,1]{1,0,2:T(8,128)S(1)}, f32[16,16,1]{1,0,2:T(8,128)}, u32[]{:S(2)}) copy-start(f32[16,16,1]{1,0,2:T(8,128)} %constant.166) | copy-start | bytes 3076
  0.7 1.3 %copy-start.1 = (f32[4,40,16,128]{3,2,1,0:T(8,128)S(1)}, f32[4,40,16,128]{3,2,1,0:T(8,128)}, u32[]{:S(2)}) copy-start(f32[4,40,16,128]{3,2,1,0:T(8,128)} %param.41) | copy-start | bytes 3932164
  0.7 0.8 copy-start.16
  2.7 0.8 copy-start.10
  3.5 0.8 copy-start.7
  4.4 0.8 copy-start.6
  7.1 7.7 %collective-permute-start = (f32[20,128]{1,0:T(8,128)S(1)}, f32[20,128]{1,0:T(8,128)S(1)}, u32[]{:S(2)}, u32[]{:S(2)}) collective-permute-start(f32[20,128]{1,0:T(8,128)S(1)} %reshape_squeeze.39), channel_id=1, source_target_pairs={{0,1},{1,2},{2,3},{3,4},{4,5},{5,6},{6,7},{7,0},{8,9},{9,10},{10,1... | collective-permute-start | bytes 30728 | tf_op jit(solution)/shard_map/ppermute | solution.py:25
  10.1 4.7 %collective-permute-start.1 = (f32[20,128]{1,0:T(8,128)S(1)}, f32[20,128]{1,0:T(8,128)S(1)}, u32[]{:S(2)}, u32[]{:S(2)}) collective-permute-start(f32[20,128]{1,0:T(8,128)S(1)} %reshape_squeeze.40), channel_id=1, source_target_pairs={{0,7},{1,0},{2,1},{3,2},{4,3},{5,4},{6,5},{7,6},{8,15},{9,8},{10,9... | collective-permute-start | bytes 30728 | tf_op jit(solution)/shard_map/ppermute | solution.py:25
  13.3 18.9 %copy-start.18 = (pred[128]{0:T(512)(128)(4,1)}, pred[128]{0:T(512)(128)(4,1)S(1)}, u32[]{:S(2)}) copy-start(pred[128]{0:T(512)(128)(4,1)S(1)} %get-tuple-element.76) | copy-start | bytes 388
  13.3 18.9 %copy-start.20 = (pred[128]{0:T(512)(128)(4,1)}, pred[128]{0:T(512)(128)(4,1)S(1)}, u32[]{:S(2)}) copy-start(pred[128]{0:T(512)(128)(4,1)S(1)} %get-tuple-element.77) | copy-start | bytes 388
  15.0 5.0 %copy-start.13 = (f32[16,128]{1,0:T(8,128)S(1)}, f32[16,128]{1,0:T(8,128)}, u32[]{:S(2)}) copy-start(f32[16,128]{1,0:T(8,128)} %constant.165) | copy-start | bytes 24580
  15.0 5.0 %copy-start.14 = (f32[16,16,1]{1,0,2:T(8,128)S(1)}, f32[16,16,1]{1,0,2:T(8,128)}, u32[]{:S(2)}) copy-start(f32[16,16,1]{1,0,2:T(8,128)} %constant.170) | copy-start | bytes 3076
  16.0 3.9 %collective-permute-start.2 = (f32[160,128]{1,0:T(8,128)S(1)}, f32[160,128]{1,0:T(8,128)S(1)}, u32[]{:S(2)}, u32[]{:S(2)}) collective-permute-start(f32[160,128]{1,0:T(8,128)S(1)} %bitcast.153), channel_id=1, source_target_pairs={{0,8},{8,16},{16,24},{24,0},{1,9},{9,17},{17,25},{25,1},{2,10},{10... | collective-permute-start | bytes 245768 | tf_op jit(solution)/shard_map/ppermute | solution.py:23
  16.0 4.0 %collective-permute-start.3 = (f32[160,128]{1,0:T(8,128)S(1)}, f32[160,128]{1,0:T(8,128)S(1)}, u32[]{:S(2)}, u32[]{:S(2)}) collective-permute-start(f32[160,128]{1,0:T(8,128)S(1)} %bitcast.151), channel_id=1, source_target_pairs={{0,24},{8,0},{16,8},{24,16},{1,25},{9,1},{17,9},{25,17},{2,26},{10... | collective-permute-start | bytes 245768 | tf_op jit(solution)/shard_map/ppermute | solution.py:23
  17.8 19.6 %copy-start.22 = (pred[16]{0:T(512)(128)(4,1)}, pred[16]{0:T(512)(128)(4,1)S(1)}, u32[]{:S(2)}) copy-start(pred[16]{0:T(512)(128)(4,1)S(1)} %get-tuple-element.78) | copy-start | bytes 52
  17.8 19.6 %copy-start.24 = (pred[16]{0:T(512)(128)(4,1)}, pred[16]{0:T(512)(128)(4,1)S(1)}, u32[]{:S(2)}) copy-start(pred[16]{0:T(512)(128)(4,1)S(1)} %get-tuple-element.79) | copy-start | bytes 52
  25.5 6.5 %collective-permute-start.4 = (f32[20,128]{1,0:T(8,128)S(1)}, f32[20,128]{1,0:T(8,128)S(1)}, u32[]{:S(2)}, u32[]{:S(2)}) collective-permute-start(f32[20,128]{1,0:T(8,128)S(1)} %reshape_squeeze.41), channel_id=1, source_target_pairs={{0,1},{1,2},{2,3},{3,4},{4,5},{5,6},{6,7},{7,0},{8,9},{9,10},{10,1... | collective-permute-start | bytes 30728 | tf_op jit(solution)/shard_map/ppermute | solution.py:25
  27.0 5.1 %collective-permute-start.5 = (f32[20,128]{1,0:T(8,128)S(1)}, f32[20,128]{1,0:T(8,128)S(1)}, u32[]{:S(2)}, u32[]{:S(2)}) collective-permute-start(f32[20,128]{1,0:T(8,128)S(1)} %reshape_squeeze.42), channel_id=1, source_target_pairs={{0,7},{1,0},{2,1},{3,2},{4,3},{5,4},{6,5},{7,6},{8,15},{9,8},{10,9... | collective-permute-start | bytes 30728 | tf_op jit(solution)/shard_map/ppermute | solution.py:25
  32.2 2.8 %copy-start.26 = (s32[1,32]{1,0:T(1,128)S(1)}, s32[1,32]{1,0:T(1,128)}, u32[]{:S(2)}) copy-start(s32[1,32]{1,0:T(1,128)} %param.44) | copy-start | bytes 388
  32.2 3.5 %copy-start.15 = (s32[1,32,256]{2,1,0:T(8,128)S(1)}, s32[1,32,256]{2,1,0:T(8,128)}, u32[]{:S(2)}) copy-start(s32[1,32,256]{2,1,0:T(8,128)} %param.43) | copy-start | bytes 98308
  33.2 3.9 %collective-permute-start.6 = (f32[160,128]{1,0:T(8,128)S(1)}, f32[160,128]{1,0:T(8,128)S(1)}, u32[]{:S(2)}, u32[]{:S(2)}) collective-permute-start(f32[160,128]{1,0:T(8,128)S(1)} %bitcast.152), channel_id=1, source_target_pairs={{0,8},{8,16},{16,24},{24,0},{1,9},{9,17},{17,25},{25,1},{2,10},{10... | collective-permute-start | bytes 245768 | tf_op jit(solution)/shard_map/ppermute | solution.py:23
  34.1 3.3 %collective-permute-start.7 = (f32[160,128]{1,0:T(8,128)S(1)}, f32[160,128]{1,0:T(8,128)S(1)}, u32[]{:S(2)}, u32[]{:S(2)}) collective-permute-start(f32[160,128]{1,0:T(8,128)S(1)} %bitcast.150), channel_id=1, source_target_pairs={{0,24},{8,0},{16,8},{24,16},{1,25},{9,1},{17,9},{25,17},{2,26},{10... | collective-permute-start | bytes 245768 | tf_op jit(solution)/shard_map/ppermute | solution.py:23
  36.3 27.1 %copy-start = (f32[2,40,16,128]{3,2,1,0:T(8,128)S(1)}, f32[2,40,16,128]{3,2,1,0:T(8,128)}, u32[]{:S(2)}) copy-start(f32[2,40,16,128]{3,2,1,0:T(8,128)} %param.45) | copy-start | bytes 1966084
  38.3 26.5 %copy-start.3 = (f32[160,16,128]{2,1,0:T(8,128)}, f32[160,16,128]{2,1,0:T(8,128)S(1)}, u32[]{:S(2)}) copy-start(f32[160,16,128]{2,1,0:T(8,128)S(1)} %fusion.9) | copy-start | bytes 3932164
  39.0 25.8 %copy-start.12 = (f32[16,16,1,1]{1,0,3,2:T(8,128)S(1)}, f32[16,16,1,1]{1,0,3,2:T(8,128)}, u32[]{:S(2)}) copy-start(f32[16,16,1,1]{1,0,3,2:T(8,128)} %constant.173) | copy-start | bytes 3076
  63.5 1.7 %copy-start.9 = (f32[128,128,1,1]{1,0,3,2:T(8,128)S(1)}, f32[128,128,1,1]{1,0,3,2:T(8,128)}, u32[]{:S(2)}) copy-start(f32[128,128,1,1]{1,0,3,2:T(8,128)} %constant.172) | copy-start | bytes 196612
  64.8 0.9 copy-start.8
  65.2 4.3 %copy-start.2 = (f32[2,40,16,128]{3,2,1,0:T(8,128)S(1)}, f32[2,40,16,128]{3,2,1,0:T(8,128)}, u32[]{:S(2)}) copy-start(f32[2,40,16,128]{3,2,1,0:T(8,128)} %param.46) | copy-start | bytes 1966084
  66.7 3.9 %collective-permute-start.10 = (f32[10,128]{1,0:T(8,128)}, f32[10,128]{1,0:T(8,128)S(1)}, u32[]{:S(2)}, u32[]{:S(2)}) collective-permute-start(f32[10,128]{1,0:T(8,128)} %reshape_squeeze.46), channel_id=1, source_target_pairs={{0,7},{1,0},{2,1},{3,2},{4,3},{5,4},{6,5},{7,6},{8,15},{9,8},{10,9... | collective-permute-start | bytes 15368 | tf_op jit(solution)/shard_map/ppermute | solution.py:25
  68.9 6.5 %collective-permute-start.11 = (f32[10,128]{1,0:T(8,128)S(1)}, f32[10,128]{1,0:T(8,128)}, u32[]{:S(2)}, u32[]{:S(2)}) collective-permute-start(f32[10,128]{1,0:T(8,128)S(1)} %reshape_squeeze.47), channel_id=1, source_target_pairs={{0,1},{1,2},{2,3},{3,4},{4,5},{5,6},{6,7},{7,0},{8,9},{9,10},{10,1... | collective-permute-start | bytes 15368 | tf_op jit(solution)/shard_map/ppermute | solution.py:25
  68.9 7.2 %collective-permute-start.8 = (f32[80,128]{1,0:T(8,128)}, f32[80,128]{1,0:T(8,128)}, u32[]{:S(2)}, u32[]{:S(2)}) collective-permute-start(f32[80,128]{1,0:T(8,128)} %bitcast.155), channel_id=1, source_target_pairs={{0,24},{8,0},{16,8},{24,16},{1,25},{9,1},{17,9},{25,17},{2,26},{10... | collective-permute-start | bytes 122888 | tf_op jit(solution)/shard_map/ppermute | solution.py:23
  69.0 7.2 %collective-permute-start.9 = (f32[80,128]{1,0:T(8,128)S(1)}, f32[80,128]{1,0:T(8,128)}, u32[]{:S(2)}, u32[]{:S(2)}) collective-permute-start(f32[80,128]{1,0:T(8,128)S(1)} %bitcast.154), channel_id=1, source_target_pairs={{0,8},{8,16},{16,24},{24,0},{1,9},{9,17},{17,25},{25,1},{2,10},{10... | collective-permute-start | bytes 122888 | tf_op jit(solution)/shard_map/ppermute | solution.py:23
  69.5 6.7 %copy-start.19 = (pred[128]{0:T(512)(128)(4,1)S(1)}, pred[128]{0:T(512)(128)(4,1)}, u32[]{:S(2)}) copy-start(pred[128]{0:T(512)(128)(4,1)} %copy-done.18) | copy-start | bytes 388
  69.5 6.7 %copy-start.21 = (pred[128]{0:T(512)(128)(4,1)S(1)}, pred[128]{0:T(512)(128)(4,1)}, u32[]{:S(2)}) copy-start(pred[128]{0:T(512)(128)(4,1)} %copy-done.20) | copy-start | bytes 388
  69.5 6.7 %copy-start.23 = (pred[16]{0:T(512)(128)(4,1)S(1)}, pred[16]{0:T(512)(128)(4,1)}, u32[]{:S(2)}) copy-start(pred[16]{0:T(512)(128)(4,1)} %copy-done.22) | copy-start | bytes 52
  69.5 6.7 %copy-start.25 = (pred[16]{0:T(512)(128)(4,1)S(1)}, pred[16]{0:T(512)(128)(4,1)}, u32[]{:S(2)}) copy-start(pred[16]{0:T(512)(128)(4,1)} %copy-done.24) | copy-start | bytes 52
  78.9 8.5 %copy-start.4 = (f32[40,16,128]{2,1,0:T(8,128)S(1)}, f32[40,16,128]{2,1,0:T(8,128)}, u32[]{:S(2)}) copy-start(f32[40,16,128]{2,1,0:T(8,128)} %get-tuple-element.68) | copy-start | bytes 983044
  78.9 8.5 %copy-start.5 = (f32[40,16,128]{2,1,0:T(8,128)S(1)}, f32[40,16,128]{2,1,0:T(8,128)}, u32[]{:S(2)}) copy-start(f32[40,16,128]{2,1,0:T(8,128)} %get-tuple-element.69) | copy-start | bytes 983044
  79.6 3.7 %collective-permute-start.14 = (f32[10,128]{1,0:T(8,128)S(1)}, f32[10,128]{1,0:T(8,128)S(1)}, u32[]{:S(2)}, u32[]{:S(2)}) collective-permute-start(f32[10,128]{1,0:T(8,128)S(1)} %reshape_squeeze.50), channel_id=1, source_target_pairs={{0,7},{1,0},{2,1},{3,2},{4,3},{5,4},{6,5},{7,6},{8,15},{9,8},{10,9... | collective-permute-start | bytes 15368 | tf_op jit(solution)/shard_map/ppermute | solution.py:25
  80.9 6.4 %collective-permute-start.15 = (f32[10,128]{1,0:T(8,128)S(1)}, f32[10,128]{1,0:T(8,128)S(1)}, u32[]{:S(2)}, u32[]{:S(2)}) collective-permute-start(f32[10,128]{1,0:T(8,128)S(1)} %reshape_squeeze.51), channel_id=1, source_target_pairs={{0,1},{1,2},{2,3},{3,4},{4,5},{5,6},{6,7},{7,0},{8,9},{9,10},{10,1... | collective-permute-start | bytes 15368 | tf_op jit(solution)/shard_map/ppermute | solution.py:25
  81.8 5.6 %collective-permute-start.12 = (f32[80,128]{1,0:T(8,128)S(1)}, f32[80,128]{1,0:T(8,128)S(1)}, u32[]{:S(2)}, u32[]{:S(2)}) collective-permute-start(f32[80,128]{1,0:T(8,128)S(1)} %bitcast.157), channel_id=1, source_target_pairs={{0,24},{8,0},{16,8},{24,16},{1,25},{9,1},{17,9},{25,17},{2,26},{10... | collective-permute-start | bytes 122888 | tf_op jit(solution)/shard_map/ppermute | solution.py:23
  81.8 5.6 %collective-permute-start.13 = (f32[80,128]{1,0:T(8,128)S(1)}, f32[80,128]{1,0:T(8,128)S(1)}, u32[]{:S(2)}, u32[]{:S(2)}) collective-permute-start(f32[80,128]{1,0:T(8,128)S(1)} %bitcast.156), channel_id=1, source_target_pairs={{0,8},{8,16},{16,24},{24,0},{1,9},{9,17},{17,25},{25,1},{2,10},{10... | collective-permute-start | bytes 122888 | tf_op jit(solution)/shard_map/ppermute | solution.py:23

commit v16 on v15

--- a/solution.py
+++ b/solution.py
@@ -1,3 +1,4 @@
+import functools
 import math
 
 import jax
@@ -166,13 +167,17 @@
     )
 
 
-def gather_kernel(index_ref, scale_ref, table_ref, out_ref):
-    fields, rows, lanes = table_ref.shape
+def gather_kernel(index_ref, scale_ref, table_ref, out_ref, surface=False):
+    fields, rows, lanes = table_ref.shape[0], table_ref.shape[-2], table_ref.shape[-1]
     tile = out_ref.shape[1]
     index = index_ref[...]
     onehot = (lax.broadcasted_iota(jnp.int32, (lanes, tile), 0) == (index % lanes)).astype(jnp.bfloat16)
     select = lax.broadcasted_iota(jnp.int32, (rows, tile), 0) == (index // lanes)
-    rest = table_ref[...]
+    if surface:
+        bottom = table_ref[:, 0]
+        rest = bottom * jnp.sqrt(1.0 + bottom[0] * bottom[0] + bottom[1] * bottom[1])
+    else:
+        rest = table_ref[...]
     parts = []
     for part in range(3):
         piece = rest.astype(jnp.bfloat16)
@@ -195,8 +200,12 @@
         out_ref[...] = out_ref[...] + values
 
 
-def onehot_gather(table, index, scale, groups):
-    fields, rows, lanes = table.shape
+def onehot_gather(table, index, scale, groups, level=None):
+    fields, rows, lanes = table.shape[0], table.shape[-2], table.shape[-1]
+    if level is None:
+        table_spec = pl.BlockSpec((fields, rows, lanes), lambda step, group: (0, 0, 0))
+    else:
+        table_spec = pl.BlockSpec((fields, 1, rows, lanes), lambda step, group: (0, level, 0, 0))
     flat = index.reshape(1, -1)
     count = flat.shape[1]
     width = count // groups
@@ -205,12 +214,12 @@
         tile *= 2
     blocks = width // tile
     return pl.pallas_call(
-        gather_kernel,
+        functools.partial(gather_kernel, surface=level is not None),
         grid=(blocks, groups),
         in_specs=[
             pl.BlockSpec((1, tile), lambda step, group: (0, group * blocks + step)),
             pl.BlockSpec((1, tile), lambda step, group: (0, group * blocks + step)),
-            pl.BlockSpec((fields, rows, lanes), lambda step, group: (0, 0, 0)),
+            table_spec,
         ],
         out_specs=pl.BlockSpec((fields, tile), lambda step, group: (0, step)),
         out_shape=jax.ShapeDtypeStruct((fields, width), jnp.float32),
@@ -234,16 +243,11 @@
     for repeat in range(SUB):
         state_now = substep(state_now, metric, derivative_np, weights_np, inv_mass)
     atm_out = state_now.reshape(fields, levels, xlocal, ylocal)
-    bottom = atm_out[:, levels - 1]
-    speed = jnp.sqrt(1.0 + bottom[0] * bottom[0] + bottom[1] * bottom[1])
-    flux_flat = (bottom * speed).reshape(fields, xlocal * ylocal)
-    node_total = xlocal * ylocal
     rank_total = send_idx.shape[1]
     slot_cap = send_idx.shape[2]
     count_row = send_counts[0]
     live_slots = (jnp.arange(slot_cap)[None, :] < count_row[:, None]).astype(jnp.float32)
-    flux_table = flux_flat.reshape(fields, node_total // 128, 128)
-    payload = onehot_gather(flux_table, send_idx[0], live_slots, 1).reshape(fields, rank_total, slot_cap)
+    payload = onehot_gather(atm_out, send_idx[0], live_slots, 1, levels - 1).reshape(fields, rank_total, slot_cap)
     received = lax.all_to_all(payload, ("gx", "gy"), split_axis=1, concat_axis=1, tiled=True)
     source_count, ocean_x, ocean_y = remap_slots.shape
     ocean_flux = onehot_gather(received, remap_slots, remap_weights, source_count).reshape(fields, ocean_x, ocean_y)

time: 90.5 us -> 90.9 us (level)
  matrix products: 15.1 us -> 16.1 us
    dot_general x2, matrix products: 1.65 us -> 2.71 us  [substep(): jnp.einsum('ab,lby->lay', pair_x, merged, precision=precision)]
    unnamed x58 -> x56, local copies, waits for them, and re-layouts: 3.05 us -> 3.07 us
where the time goes in v16:
time: 90.9 us; the launch traced here: 90.1 us
  starting transfers between devices  19.8 us (22%)
  matrix products  16.1 us (18%)
  waiting for transfers between devices  15.7 us (17%)
  blocking collectives  14.6 us (16%)
  local copies, waits for them, and re-layouts  10.7 us (12%)
  Pallas kernels  8.33 us (9%)
  other arithmetic  3.71 us (4%)
  between operations  1.25 us (1%)
    ppermute x8, starting transfers between devices, neighbour(): lax.ppermute(values, 'gy', [(j, (j + step_y) % count_y) for j in range(co...  15.1 us
    all_to_all x1, blocking collectives, per_device(): lax.all_to_all(payload, ('gx', 'gy'), split_axis=1, concat_axis=1, tiled=...  14.6 us
    ppermute x8, waiting for transfers between devices, neighbour(): lax.ppermute(values, 'gy', [(j, (j + step_y) % count_y) for j in range(co...  12.4 us
    pallas_call x2, Pallas kernels, onehot_gather(): pl.pallas_call(functools.partial(gather_kernel, surface=level is not None...  8.33 us
    ppermute x8, starting transfers between devices, neighbour(): lax.ppermute(values, 'gx', [(i, (i + step_x) % count_x) for i in range(co...  4.67 us
    dot_general x2, matrix products, tracer_step(): jnp.einsum('ab,...by->...ay', sum_x, tracers, precision=precision)  4.15 us
    ppermute x8, waiting for transfers between devices, neighbour(): lax.ppermute(values, 'gx', [(i, (i + step_x) % count_x) for i in range(co...  3.28 us
    unnamed x56, local copies, waits for them, and re-layouts  3.07 us
  transfers between devices with their start and end apart: 16, of which 10 were waited for; matrix products, arithmetic and copies ran while one was open for 5% of the time, Pallas kernels for 0%

profile of v16, /device:TPU:0, one launch (start us, length us, event | category | flops | bytes accessed | tf_op | source)
XLA Modules:
  0.0 90.1 jit_solution(16614389841669370763)
XLA Ops:
  0.7 0.6 copy-done.16
  2.0 0.7 fusion.10
  2.7 0.7 convolution_bitcast_fusion.5
  3.5 0.7 fusion.45
  4.4 0.7 fusion.2
  5.2 0.7 fusion.1
  5.9 1.1 %slice_reduce_fusion.3 = (f32[160,16]{1,0:T(8,128)S(1)}, f32[160,16]{1,0:T(8,128)S(1)}) fusion(f32[160,16,128]{2,1,0:T(8,128)S(1)} %fusion.1), kind=kLoop, calls=%fused_computation.24 | loop fusion | bytes 40960 | tf_op jit(solution)/shard_map/slice | solution.py:88
  7.1 3.0 %collective-permute-start = (f32[20,128]{1,0:T(8,128)S(1)}, f32[20,128]{1,0:T(8,128)S(1)}, u32[]{:S(2)}, u32[]{:S(2)}) collective-permute-start(f32[20,128]{1,0:T(8,128)S(1)} %reshape_squeeze.39), channel_id=1, source_target_pairs={{0,1},{1,2},{2,3},{3,4},{4,5},{5,6},{6,7},{7,0},{8,9},{9,10},{10,1... | collective-permute-start | bytes 30728 | tf_op jit(solution)/shard_map/ppermute | solution.py:26
  10.1 3.1 %collective-permute-start.1 = (f32[20,128]{1,0:T(8,128)S(1)}, f32[20,128]{1,0:T(8,128)S(1)}, u32[]{:S(2)}, u32[]{:S(2)}) collective-permute-start(f32[20,128]{1,0:T(8,128)S(1)} %reshape_squeeze.40), channel_id=1, source_target_pairs={{0,7},{1,0},{2,1},{3,2},{4,3},{5,4},{6,5},{7,6},{8,15},{9,8},{10,9... | collective-permute-start | bytes 30728 | tf_op jit(solution)/shard_map/ppermute | solution.py:26
  13.3 1.5 %collective-permute-done = f32[20,128]{1,0:T(8,128)S(1)} collective-permute-done((f32[20,128]{1,0:T(8,128)S(1)}, f32[20,128]{1,0:T(8,128)S(1)}, u32[]{:S(2)}, u32[]{:S(2)}) %collective-permute-start) | collective-permute-done | bytes 10272 | tf_op jit(solution)/shard_map/ppermute | solution.py:26
  15.0 0.8 select_add_fusion.1
  16.0 1.7 %collective-permute-start.3 = (f32[160,128]{1,0:T(8,128)S(1)}, f32[160,128]{1,0:T(8,128)S(1)}, u32[]{:S(2)}, u32[]{:S(2)}) collective-permute-start(f32[160,128]{1,0:T(8,128)S(1)} %bitcast.142), channel_id=1, source_target_pairs={{0,24},{8,0},{16,8},{24,16},{1,25},{9,1},{17,9},{25,17},{2,26},{10... | collective-permute-start | bytes 245768 | tf_op jit(solution)/shard_map/ppermute | solution.py:24
  17.8 2.1 %collective-permute-done.2 = f32[160,128]{1,0:T(8,128)S(1)} collective-permute-done((f32[160,128]{1,0:T(8,128)S(1)}, f32[160,128]{1,0:T(8,128)S(1)}, u32[]{:S(2)}, u32[]{:S(2)}) %collective-permute-start.2) | collective-permute-done | bytes 81952 | tf_op jit(solution)/shard_map/ppermute | solution.py:24
  20.0 0.8 fusion.5
  20.8 0.7 fusion.6
  21.5 0.7 convolution_multiply_fusion.1
  22.2 0.7 convolution_bitcast_fusion.2
  22.9 0.7 fusion.46
  23.6 0.7 fusion
  24.3 1.1 %slice_reduce_fusion.1 = (f32[160,16]{1,0:T(8,128)S(1)}, f32[160,16]{1,0:T(8,128)S(1)}) fusion(f32[160,16,128]{2,1,0:T(8,128)S(1)} %fusion), kind=kLoop, calls=%fused_computation.22 | loop fusion | bytes 40960 | tf_op jit(solution)/shard_map/slice | solution.py:88
  25.5 1.4 %collective-permute-start.4 = (f32[20,128]{1,0:T(8,128)S(1)}, f32[20,128]{1,0:T(8,128)S(1)}, u32[]{:S(2)}, u32[]{:S(2)}) collective-permute-start(f32[20,128]{1,0:T(8,128)S(1)} %reshape_squeeze.41), channel_id=1, source_target_pairs={{0,1},{1,2},{2,3},{3,4},{4,5},{5,6},{6,7},{7,0},{8,9},{9,10},{10,1... | collective-permute-start | bytes 30728 | tf_op jit(solution)/shard_map/ppermute | solution.py:26
  27.0 3.4 %collective-permute-start.5 = (f32[20,128]{1,0:T(8,128)S(1)}, f32[20,128]{1,0:T(8,128)S(1)}, u32[]{:S(2)}, u32[]{:S(2)}) collective-permute-start(f32[20,128]{1,0:T(8,128)S(1)} %reshape_squeeze.42), channel_id=1, source_target_pairs={{0,7},{1,0},{2,1},{3,2},{4,3},{5,4},{6,5},{7,6},{8,15},{9,8},{10,9... | collective-permute-start | bytes 30728 | tf_op jit(solution)/shard_map/ppermute | solution.py:26
  30.4 1.5 %collective-permute-done.4 = f32[20,128]{1,0:T(8,128)S(1)} collective-permute-done((f32[20,128]{1,0:T(8,128)S(1)}, f32[20,128]{1,0:T(8,128)S(1)}, u32[]{:S(2)}, u32[]{:S(2)}) %collective-permute-start.4) | collective-permute-done | bytes 10272 | tf_op jit(solution)/shard_map/ppermute | solution.py:26
  32.2 0.8 select_add_fusion
  33.2 0.9 %collective-permute-start.6 = (f32[160,128]{1,0:T(8,128)S(1)}, f32[160,128]{1,0:T(8,128)S(1)}, u32[]{:S(2)}, u32[]{:S(2)}) collective-permute-start(f32[160,128]{1,0:T(8,128)S(1)} %bitcast.143), channel_id=1, source_target_pairs={{0,8},{8,16},{16,24},{24,0},{1,9},{9,17},{17,25},{25,1},{2,10},{10... | collective-permute-start | bytes 245768 | tf_op jit(solution)/shard_map/ppermute | solution.py:24
  34.1 0.9 collective-permute-start.7
  35.1 0.7 copy.48
  35.7 0.6 copy.47
  36.4 0.7 collective-permute-done.6
  37.4 1.9 %fusion.9 = f32[160,16,128]{2,1,0:T(8,128)} fusion(f32[160,16,128]{2,1,0:T(8,128)S(1)} %fusion.5, f32[160,16,128]{2,1,0:T(8,128)S(1)} %select_add_fusion, f32[16,16,1]{1,0,2:T(8,128)S(1)} %copy-done.13, f32[160,128]{1,0:T(8,128)S(1)} %collective-permute-done.7, f32[160,128]{1,0:T(8,128)S(1)} %collective-permute-done.6, f32[16,128]{1,0:T(8,128)S(1)} %copy-done.12, ...), kind=kOutput, calls=%fused_computation.18 | convolution fusion | flops 33095680 | bytes 4105248 | tf_op jit(solution)/shard_map/ab,lby->lay/dot_general | solution.py:95
  39.3 3.7 %shard_map.320 = f32[4,8192]{1,0:T(4,128)} custom-call(s32[1,8192]{1,0:T(1,128)} %bitcast.140, f32[1,8192]{1,0:T(1,128)} %bitcast.139, f32[4,40,16,128]{3,2,1,0:T(8,128)} %bitcast.136), custom_call_target="tpu_custom_call" | custom-call | tf_op jit(solution)/shard_map/pallas_call | solution.py:216
  43.0 14.6 %all_to_all.5 = f32[4,32,256]{2,0,1:T(4,128)S(1)} all-to-all(f32[4,32,256]{2,0,1:T(4,128)} %bitcast.138), channel_id=1, replica_groups=mesh['gx'=4,'gy'=8] {'gx','gy'}, dimensions={1} | all-to-all | bytes 262144 | tf_op jit(solution)/shard_map/all_to_all | solution.py:251
  57.5 0.7 copy.38.table_ref
  58.2 4.7 %shard_map.321 = f32[4,2048]{1,0:T(4,128)} custom-call(s32[1,8192]{1,0:T(1,128)} %bitcast.149, f32[1,8192]{1,0:T(1,128)} %bitcast.150, f32[4,32,256]{2,1,0:T(8,128)} %copy.38.table_ref), custom_call_target="tpu_custom_call" | custom-call | tf_op jit(solution)/shard_map/pallas_call | solution.py:216
  62.9 1.0 %fusion.37 = (f32[1,2048]{1,0:T(1,128)S(1)}, f32[1,2048]{1,0:T(1,128)S(1)}, f32[1,2048]{1,0:T(1,128)S(1)}, f32[1,2048]{1,0:T(1,128)S(1)}) fusion(f32[4,2048]{1,0:T(4,128)} %shard_map.321), kind=kLoop, calls=%fused_computation.74 | loop fusion | flops 8192 | bytes 65536 | tf_op jit(solution)/shard_map/mul | solution.py:255
  63.9 0.6 slice_reduce_fusion.7
  64.5 0.7 fusion.44
  66.5 0.7 reshape_squeeze.46
  67.2 2.0 %collective-permute-start.10 = (f32[10,128]{1,0:T(8,128)}, f32[10,128]{1,0:T(8,128)S(1)}, u32[]{:S(2)}, u32[]{:S(2)}) collective-permute-start(f32[10,128]{1,0:T(8,128)} %reshape_squeeze.46), channel_id=1, source_target_pairs={{0,7},{1,0},{2,1},{3,2},{4,3},{5,4},{6,5},{7,6},{8,15},{9,8},{10,9... | collective-permute-start | bytes 15368 | tf_op jit(solution)/shard_map/ppermute | solution.py:26
  69.9 0.9 fusion.36
  71.1 4.7 %collective-permute-done.11 = f32[10,128]{1,0:T(8,128)} collective-permute-done((f32[10,128]{1,0:T(8,128)S(1)}, f32[10,128]{1,0:T(8,128)}, u32[]{:S(2)}, u32[]{:S(2)}) %collective-permute-start.11) | collective-permute-done | bytes 5152 | tf_op jit(solution)/shard_map/ppermute | solution.py:26
  75.8 0.8 broadcast_in_dim.267
  76.6 1.9 %fusion.17 = f32[2,40,16,128]{3,2,1,0:T(8,128)S(1)} fusion(f32[2,40,16,128]{3,2,1,0:T(8,128)S(1)} %fusion.40, f32[2,40,16,128]{3,2,1,0:T(8,128)S(1)} %convolution_bitcast_fusion.8, f32[2,40,16,128]{3,2,1,0:T(8,128)S(1)} %fusion.47, f32[2,40,16,128]{3,2,1,0:T(8,128)S(1)} %fusion.48, f32[40,16,128]{2,1,0:T(8,128)} %get-tuple-element.67, ...), kind=kOutput, calls=%fused_computation.45 | convolution fusion | flops 19169280 | bytes 4025632 | tf_op jit(solution)/shard_map/ab,...by->...ay/dot_general | solution.py:121
  80.1 1.2 %collective-permute-start.14 = (f32[10,128]{1,0:T(8,128)S(1)}, f32[10,128]{1,0:T(8,128)S(1)}, u32[]{:S(2)}, u32[]{:S(2)}) collective-permute-start(f32[10,128]{1,0:T(8,128)S(1)} %reshape_squeeze.50), channel_id=1, source_target_pairs={{0,7},{1,0},{2,1},{3,2},{4,3},{5,4},{6,5},{7,6},{8,15},{9,8},{10,9... | collective-permute-start | bytes 15368 | tf_op jit(solution)/shard_map/ppermute | solution.py:26
  81.4 0.9 collective-permute-start.15
  83.1 0.6 collective-permute-done.14
  83.8 3.9 %collective-permute-done.15 = f32[10,128]{1,0:T(8,128)S(1)} collective-permute-done((f32[10,128]{1,0:T(8,128)S(1)}, f32[10,128]{1,0:T(8,128)S(1)}, u32[]{:S(2)}, u32[]{:S(2)}) %collective-permute-start.15) | collective-permute-done | bytes 5152 | tf_op jit(solution)/shard_map/ppermute | solution.py:26
  87.8 2.3 %fusion.29 = f32[2,40,16,128]{3,2,1,0:T(8,128)} fusion(f32[2,40,16,128]{3,2,1,0:T(8,128)S(1)} %fusion.17, f32[2,40,16,128]{3,2,1,0:T(8,128)S(1)} %convolution_bitcast_fusion.6, f32[2,40,16,128]{3,2,1,0:T(8,128)S(1)} %fusion.49, f32[2,40,16,128]{3,2,1,0:T(8,128)S(1)} %fusion.50, f32[2,40,16]{2,1,0:T(8,128)S(1)} %broadcast_in_dim.275, ...), kind=kOutput, calls=%fused_computation.57 | convolution fusion | flops 19169280 | bytes 4025632 | tf_op jit(solution)/shard_map/ab,...by->...ay/dot_general | solution.py:121
  (100 shorter events, 7.6 us)
Async XLA Ops:
  0.6 0.7 copy-start.16
  0.6 0.7 copy-start.26
  0.7 0.9 %copy-start.10 = (f32[16,16,1]{1,0,2:T(8,128)S(1)}, f32[16,16,1]{1,0,2:T(8,128)}, u32[]{:S(2)}) copy-start(f32[16,16,1]{1,0,2:T(8,128)} %constant.164) | copy-start | bytes 3076
  0.7 1.3 %copy-start.1 = (f32[4,40,16,128]{3,2,1,0:T(8,128)S(1)}, f32[4,40,16,128]{3,2,1,0:T(8,128)}, u32[]{:S(2)}) copy-start(f32[4,40,16,128]{3,2,1,0:T(8,128)} %param.41) | copy-start | bytes 3932164
  0.7 0.8 copy-start.15
  2.7 0.8 copy-start.9
  3.5 0.8 copy-start.6
  4.4 0.8 copy-start.5
  7.1 7.7 %collective-permute-start = (f32[20,128]{1,0:T(8,128)S(1)}, f32[20,128]{1,0:T(8,128)S(1)}, u32[]{:S(2)}, u32[]{:S(2)}) collective-permute-start(f32[20,128]{1,0:T(8,128)S(1)} %reshape_squeeze.39), channel_id=1, source_target_pairs={{0,1},{1,2},{2,3},{3,4},{4,5},{5,6},{6,7},{7,0},{8,9},{9,10},{10,1... | collective-permute-start | bytes 30728 | tf_op jit(solution)/shard_map/ppermute | solution.py:26
  10.1 4.7 %collective-permute-start.1 = (f32[20,128]{1,0:T(8,128)S(1)}, f32[20,128]{1,0:T(8,128)S(1)}, u32[]{:S(2)}, u32[]{:S(2)}) collective-permute-start(f32[20,128]{1,0:T(8,128)S(1)} %reshape_squeeze.40), channel_id=1, source_target_pairs={{0,7},{1,0},{2,1},{3,2},{4,3},{5,4},{6,5},{7,6},{8,15},{9,8},{10,9... | collective-permute-start | bytes 30728 | tf_op jit(solution)/shard_map/ppermute | solution.py:26
  13.3 18.9 %copy-start.17 = (pred[128]{0:T(512)(128)(4,1)}, pred[128]{0:T(512)(128)(4,1)S(1)}, u32[]{:S(2)}) copy-start(pred[128]{0:T(512)(128)(4,1)S(1)} %get-tuple-element.74) | copy-start | bytes 388
  13.3 18.9 %copy-start.19 = (pred[128]{0:T(512)(128)(4,1)}, pred[128]{0:T(512)(128)(4,1)S(1)}, u32[]{:S(2)}) copy-start(pred[128]{0:T(512)(128)(4,1)S(1)} %get-tuple-element.75) | copy-start | bytes 388
  15.0 5.0 %copy-start.12 = (f32[16,128]{1,0:T(8,128)S(1)}, f32[16,128]{1,0:T(8,128)}, u32[]{:S(2)}) copy-start(f32[16,128]{1,0:T(8,128)} %constant.163) | copy-start | bytes 24580
  15.0 5.0 %copy-start.13 = (f32[16,16,1]{1,0,2:T(8,128)S(1)}, f32[16,16,1]{1,0,2:T(8,128)}, u32[]{:S(2)}) copy-start(f32[16,16,1]{1,0,2:T(8,128)} %constant.168) | copy-start | bytes 3076
  16.0 3.9 %collective-permute-start.2 = (f32[160,128]{1,0:T(8,128)S(1)}, f32[160,128]{1,0:T(8,128)S(1)}, u32[]{:S(2)}, u32[]{:S(2)}) collective-permute-start(f32[160,128]{1,0:T(8,128)S(1)} %bitcast.144), channel_id=1, source_target_pairs={{0,8},{8,16},{16,24},{24,0},{1,9},{9,17},{17,25},{25,1},{2,10},{10... | collective-permute-start | bytes 245768 | tf_op jit(solution)/shard_map/ppermute | solution.py:24
  16.0 4.0 %collective-permute-start.3 = (f32[160,128]{1,0:T(8,128)S(1)}, f32[160,128]{1,0:T(8,128)S(1)}, u32[]{:S(2)}, u32[]{:S(2)}) collective-permute-start(f32[160,128]{1,0:T(8,128)S(1)} %bitcast.142), channel_id=1, source_target_pairs={{0,24},{8,0},{16,8},{24,16},{1,25},{9,1},{17,9},{25,17},{2,26},{10... | collective-permute-start | bytes 245768 | tf_op jit(solution)/shard_map/ppermute | solution.py:24
  17.8 19.6 %copy-start.21 = (pred[16]{0:T(512)(128)(4,1)}, pred[16]{0:T(512)(128)(4,1)S(1)}, u32[]{:S(2)}) copy-start(pred[16]{0:T(512)(128)(4,1)S(1)} %get-tuple-element.76) | copy-start | bytes 52
  17.8 19.6 %copy-start.23 = (pred[16]{0:T(512)(128)(4,1)}, pred[16]{0:T(512)(128)(4,1)S(1)}, u32[]{:S(2)}) copy-start(pred[16]{0:T(512)(128)(4,1)S(1)} %get-tuple-element.77) | copy-start | bytes 52
  25.5 6.5 %collective-permute-start.4 = (f32[20,128]{1,0:T(8,128)S(1)}, f32[20,128]{1,0:T(8,128)S(1)}, u32[]{:S(2)}, u32[]{:S(2)}) collective-permute-start(f32[20,128]{1,0:T(8,128)S(1)} %reshape_squeeze.41), channel_id=1, source_target_pairs={{0,1},{1,2},{2,3},{3,4},{4,5},{5,6},{6,7},{7,0},{8,9},{9,10},{10,1... | collective-permute-start | bytes 30728 | tf_op jit(solution)/shard_map/ppermute | solution.py:26
  27.0 5.1 %collective-permute-start.5 = (f32[20,128]{1,0:T(8,128)S(1)}, f32[20,128]{1,0:T(8,128)S(1)}, u32[]{:S(2)}, u32[]{:S(2)}) collective-permute-start(f32[20,128]{1,0:T(8,128)S(1)} %reshape_squeeze.42), channel_id=1, source_target_pairs={{0,7},{1,0},{2,1},{3,2},{4,3},{5,4},{6,5},{7,6},{8,15},{9,8},{10,9... | collective-permute-start | bytes 30728 | tf_op jit(solution)/shard_map/ppermute | solution.py:26
  32.2 2.8 %copy-start.25 = (s32[1,32]{1,0:T(1,128)S(1)}, s32[1,32]{1,0:T(1,128)}, u32[]{:S(2)}) copy-start(s32[1,32]{1,0:T(1,128)} %param.44) | copy-start | bytes 388
  32.2 3.5 %copy-start.14 = (s32[1,32,256]{2,1,0:T(8,128)S(1)}, s32[1,32,256]{2,1,0:T(8,128)}, u32[]{:S(2)}) copy-start(s32[1,32,256]{2,1,0:T(8,128)} %param.43) | copy-start | bytes 98308
  33.2 3.9 %collective-permute-start.6 = (f32[160,128]{1,0:T(8,128)S(1)}, f32[160,128]{1,0:T(8,128)S(1)}, u32[]{:S(2)}, u32[]{:S(2)}) collective-permute-start(f32[160,128]{1,0:T(8,128)S(1)} %bitcast.143), channel_id=1, source_target_pairs={{0,8},{8,16},{16,24},{24,0},{1,9},{9,17},{17,25},{25,1},{2,10},{10... | collective-permute-start | bytes 245768 | tf_op jit(solution)/shard_map/ppermute | solution.py:24
  34.1 3.3 %collective-permute-start.7 = (f32[160,128]{1,0:T(8,128)S(1)}, f32[160,128]{1,0:T(8,128)S(1)}, u32[]{:S(2)}, u32[]{:S(2)}) collective-permute-start(f32[160,128]{1,0:T(8,128)S(1)} %bitcast.141), channel_id=1, source_target_pairs={{0,24},{8,0},{16,8},{24,16},{1,25},{9,1},{17,9},{25,17},{2,26},{10... | collective-permute-start | bytes 245768 | tf_op jit(solution)/shard_map/ppermute | solution.py:24
  39.3 24.6 %copy-start = (f32[2,40,16,128]{3,2,1,0:T(8,128)S(1)}, f32[2,40,16,128]{3,2,1,0:T(8,128)}, u32[]{:S(2)}) copy-start(f32[2,40,16,128]{3,2,1,0:T(8,128)} %param.45) | copy-start | bytes 1966084
  43.0 22.2 %copy-start.11 = (f32[16,16,1,1]{1,0,3,2:T(8,128)S(1)}, f32[16,16,1,1]{1,0,3,2:T(8,128)}, u32[]{:S(2)}) copy-start(f32[16,16,1,1]{1,0,3,2:T(8,128)} %constant.171) | copy-start | bytes 3076
  63.9 1.7 %copy-start.8 = (f32[128,128,1,1]{1,0,3,2:T(8,128)S(1)}, f32[128,128,1,1]{1,0,3,2:T(8,128)}, u32[]{:S(2)}) copy-start(f32[128,128,1,1]{1,0,3,2:T(8,128)} %constant.170) | copy-start | bytes 196612
  65.2 0.9 copy-start.7
  65.6 4.3 %copy-start.2 = (f32[2,40,16,128]{3,2,1,0:T(8,128)S(1)}, f32[2,40,16,128]{3,2,1,0:T(8,128)}, u32[]{:S(2)}) copy-start(f32[2,40,16,128]{3,2,1,0:T(8,128)} %param.46) | copy-start | bytes 1966084
  67.2 3.9 %collective-permute-start.10 = (f32[10,128]{1,0:T(8,128)}, f32[10,128]{1,0:T(8,128)S(1)}, u32[]{:S(2)}, u32[]{:S(2)}) collective-permute-start(f32[10,128]{1,0:T(8,128)} %reshape_squeeze.46), channel_id=1, source_target_pairs={{0,7},{1,0},{2,1},{3,2},{4,3},{5,4},{6,5},{7,6},{8,15},{9,8},{10,9... | collective-permute-start | bytes 15368 | tf_op jit(solution)/shard_map/ppermute | solution.py:26
  69.3 6.5 %collective-permute-start.11 = (f32[10,128]{1,0:T(8,128)S(1)}, f32[10,128]{1,0:T(8,128)}, u32[]{:S(2)}, u32[]{:S(2)}) collective-permute-start(f32[10,128]{1,0:T(8,128)S(1)} %reshape_squeeze.47), channel_id=1, source_target_pairs={{0,1},{1,2},{2,3},{3,4},{4,5},{5,6},{6,7},{7,0},{8,9},{9,10},{10,1... | collective-permute-start | bytes 15368 | tf_op jit(solution)/shard_map/ppermute | solution.py:26
  69.3 7.2 %collective-permute-start.8 = (f32[80,128]{1,0:T(8,128)}, f32[80,128]{1,0:T(8,128)}, u32[]{:S(2)}, u32[]{:S(2)}) collective-permute-start(f32[80,128]{1,0:T(8,128)} %bitcast.146), channel_id=1, source_target_pairs={{0,24},{8,0},{16,8},{24,16},{1,25},{9,1},{17,9},{25,17},{2,26},{10... | collective-permute-start | bytes 122888 | tf_op jit(solution)/shard_map/ppermute | solution.py:24
  69.4 7.2 %collective-permute-start.9 = (f32[80,128]{1,0:T(8,128)S(1)}, f32[80,128]{1,0:T(8,128)}, u32[]{:S(2)}, u32[]{:S(2)}) collective-permute-start(f32[80,128]{1,0:T(8,128)S(1)} %bitcast.145), channel_id=1, source_target_pairs={{0,8},{8,16},{16,24},{24,0},{1,9},{9,17},{17,25},{25,1},{2,10},{10... | collective-permute-start | bytes 122888 | tf_op jit(solution)/shard_map/ppermute | solution.py:24
  69.9 6.7 %copy-start.18 = (pred[128]{0:T(512)(128)(4,1)S(1)}, pred[128]{0:T(512)(128)(4,1)}, u32[]{:S(2)}) copy-start(pred[128]{0:T(512)(128)(4,1)} %copy-done.17) | copy-start | bytes 388
  69.9 6.7 %copy-start.20 = (pred[128]{0:T(512)(128)(4,1)S(1)}, pred[128]{0:T(512)(128)(4,1)}, u32[]{:S(2)}) copy-start(pred[128]{0:T(512)(128)(4,1)} %copy-done.19) | copy-start | bytes 388
  69.9 6.7 %copy-start.22 = (pred[16]{0:T(512)(128)(4,1)S(1)}, pred[16]{0:T(512)(128)(4,1)}, u32[]{:S(2)}) copy-start(pred[16]{0:T(512)(128)(4,1)} %copy-done.21) | copy-start | bytes 52
  69.9 6.7 %copy-start.24 = (pred[16]{0:T(512)(128)(4,1)S(1)}, pred[16]{0:T(512)(128)(4,1)}, u32[]{:S(2)}) copy-start(pred[16]{0:T(512)(128)(4,1)} %copy-done.23) | copy-start | bytes 52
  79.3 8.5 %copy-start.3 = (f32[40,16,128]{2,1,0:T(8,128)S(1)}, f32[40,16,128]{2,1,0:T(8,128)}, u32[]{:S(2)}) copy-start(f32[40,16,128]{2,1,0:T(8,128)} %get-tuple-element.66) | copy-start | bytes 983044
  79.3 8.5 %copy-start.4 = (f32[40,16,128]{2,1,0:T(8,128)S(1)}, f32[40,16,128]{2,1,0:T(8,128)}, u32[]{:S(2)}) copy-start(f32[40,16,128]{2,1,0:T(8,128)} %get-tuple-element.67) | copy-start | bytes 983044
  80.1 3.7 %collective-permute-start.14 = (f32[10,128]{1,0:T(8,128)S(1)}, f32[10,128]{1,0:T(8,128)S(1)}, u32[]{:S(2)}, u32[]{:S(2)}) collective-permute-start(f32[10,128]{1,0:T(8,128)S(1)} %reshape_squeeze.50), channel_id=1, source_target_pairs={{0,7},{1,0},{2,1},{3,2},{4,3},{5,4},{6,5},{7,6},{8,15},{9,8},{10,9... | collective-permute-start | bytes 15368 | tf_op jit(solution)/shard_map/ppermute | solution.py:26
  81.4 6.4 %collective-permute-start.15 = (f32[10,128]{1,0:T(8,128)S(1)}, f32[10,128]{1,0:T(8,128)S(1)}, u32[]{:S(2)}, u32[]{:S(2)}) collective-permute-start(f32[10,128]{1,0:T(8,128)S(1)} %reshape_squeeze.51), channel_id=1, source_target_pairs={{0,1},{1,2},{2,3},{3,4},{4,5},{5,6},{6,7},{7,0},{8,9},{9,10},{10,1... | collective-permute-start | bytes 15368 | tf_op jit(solution)/shard_map/ppermute | solution.py:26
  82.2 5.6 %collective-permute-start.12 = (f32[80,128]{1,0:T(8,128)S(1)}, f32[80,128]{1,0:T(8,128)S(1)}, u32[]{:S(2)}, u32[]{:S(2)}) collective-permute-start(f32[80,128]{1,0:T(8,128)S(1)} %bitcast.148), channel_id=1, source_target_pairs={{0,24},{8,0},{16,8},{24,16},{1,25},{9,1},{17,9},{25,17},{2,26},{10... | collective-permute-start | bytes 122888 | tf_op jit(solution)/shard_map/ppermute | solution.py:24
  82.2 5.6 %collective-permute-start.13 = (f32[80,128]{1,0:T(8,128)S(1)}, f32[80,128]{1,0:T(8,128)S(1)}, u32[]{:S(2)}, u32[]{:S(2)}) collective-permute-start(f32[80,128]{1,0:T(8,128)S(1)} %bitcast.147), channel_id=1, source_target_pairs={{0,8},{8,16},{16,24},{24,0},{1,9},{9,17},{17,25},{25,1},{2,10},{10... | collective-permute-start | bytes 122888 | tf_op jit(solution)/shard_map/ppermute | solution.py:24

commit v17 on v15

--- a/solution.py
+++ b/solution.py
@@ -117,10 +117,12 @@
     west = jnp.where(row == 0, from_up, 0.0)
     north = jnp.where(column == last_y, from_right, 0.0)
     south = jnp.where(column == 0, from_left, 0.0)
-    across_x = jnp.einsum("ab,...by->...ay", sum_x, tracers, precision=precision) + (east + west)
-    slope_x = jnp.einsum("ab,...by->...ay", diff_x, tracers, precision=precision) + (east - west)
-    across_y = jnp.einsum("...xc,cd->...xd", tracers, sum_y, precision=precision) + (north + south)
-    slope_y = jnp.einsum("...xc,cd->...xd", tracers, diff_y, precision=precision) + (north - south)
+    both_x = jnp.einsum("ab,...by->...ay", jnp.concatenate([sum_x, diff_x], axis=0), tracers, precision=precision)
+    both_y = jnp.einsum("...xc,cd->...xd", tracers, jnp.concatenate([sum_y, diff_y], axis=1), precision=precision)
+    across_x = both_x[..., :xsize, :] + (east + west)
+    slope_x = both_x[..., xsize:, :] + (east - west)
+    across_y = both_y[..., :ysize] + (north + south)
+    slope_y = both_y[..., ysize:] + (north - south)
     return (
         tracers
         + diff_coef * (across_x + across_y - 4.0 * tracers)

time: 90.5 us -> 92.2 us (1.019)
  other arithmetic: 4.39 us -> 8.02 us
  matrix products: 15.1 us -> 13.4 us
    sub x0 -> x2, other arithmetic: none -> 4.53 us  [tracer_step(): tracers + diff_coef * (across_x + across_y - 4.0 * tracers)]
    dot_general x8 -> x4, matrix products: 6.61 us -> 4.93 us  [the longest x2 2.51 us: tracer_step(): jnp.einsum('ab,...by->...ay', jnp.concatenate([sum_x, diff_x], axis=0), t...]
    unnamed x58 -> x36, local copies, waits for them, and re-layouts: 3.05 us -> 4.05 us
  transfers between devices with their start and end apart: 16 -> 16, of which waited for: 10 -> 9; matrix products, arithmetic and copies ran while one was open for 5% -> 5% of each run, Pallas kernels for 0% -> 0%
where the time goes in v17:
time: 92.2 us; the launch traced here: 91.5 us
  starting transfers between devices  19.8 us (21%)
  waiting for transfers between devices  15.2 us (16%)
  blocking collectives  14.6 us (16%)
  matrix products  13.4 us (15%)
  local copies, waits for them, and re-layouts  11.1 us (12%)
  Pallas kernels  8.26 us (9%)
  other arithmetic  8.02 us (9%)
  between operations  1.13 us (1%)
    ppermute x8, starting transfers between devices, neighbour(): lax.ppermute(values, 'gy', [(j, (j + step_y) % count_y) for j in range(co...  15.1 us
    all_to_all x1, blocking collectives, per_device(): lax.all_to_all(payload, ('gx', 'gy'), split_axis=1, concat_axis=1, tiled=...  14.6 us
    ppermute x8, waiting for transfers between devices, neighbour(): lax.ppermute(values, 'gy', [(j, (j + step_y) % count_y) for j in range(co...  11.9 us
    pallas_call x2, Pallas kernels, onehot_gather(): pl.pallas_call(gather_kernel, grid=(blocks, groups), in_specs=[pl.BlockSp...  8.26 us
    ppermute x8, starting transfers between devices, neighbour(): lax.ppermute(values, 'gx', [(i, (i + step_x) % count_x) for i in range(co...  4.67 us
    sub x2, other arithmetic, tracer_step(): tracers + diff_coef * (across_x + across_y - 4.0 * tracers)  4.53 us
    unnamed x36, local copies, waits for them, and re-layouts  4.05 us
    ppermute x8, waiting for transfers between devices, neighbour(): lax.ppermute(values, 'gx', [(i, (i + step_x) % count_x) for i in range(co...  3.28 us
  transfers between devices with their start and end apart: 16, of which 9 were waited for; matrix products, arithmetic and copies ran while one was open for 5% of the time, Pallas kernels for 0%

profile of v17, /device:TPU:0, one launch (start us, length us, event | category | flops | bytes accessed | tf_op | source)
XLA Modules:
  0.0 91.5 jit_solution(3008444010651171030)
XLA Ops:
  2.0 0.7 fusion.10
  2.7 0.7 convolution_bitcast_fusion.5
  3.5 0.7 fusion.50
  4.4 0.7 fusion.2
  5.2 0.7 fusion.1
  5.9 1.1 %slice_reduce_fusion.3 = (f32[160,16]{1,0:T(8,128)S(1)}, f32[160,16]{1,0:T(8,128)S(1)}) fusion(f32[160,16,128]{2,1,0:T(8,128)S(1)} %fusion.1), kind=kLoop, calls=%fused_computation.26 | loop fusion | bytes 40960 | tf_op jit(solution)/shard_map/slice | solution.py:87
  7.1 3.0 %collective-permute-start = (f32[20,128]{1,0:T(8,128)S(1)}, f32[20,128]{1,0:T(8,128)S(1)}, u32[]{:S(2)}, u32[]{:S(2)}) collective-permute-start(f32[20,128]{1,0:T(8,128)S(1)} %reshape_squeeze.39), channel_id=1, source_target_pairs={{0,1},{1,2},{2,3},{3,4},{4,5},{5,6},{6,7},{7,0},{8,9},{9,10},{10,1... | collective-permute-start | bytes 30728 | tf_op jit(solution)/shard_map/ppermute | solution.py:25
  10.1 3.1 %collective-permute-start.1 = (f32[20,128]{1,0:T(8,128)S(1)}, f32[20,128]{1,0:T(8,128)S(1)}, u32[]{:S(2)}, u32[]{:S(2)}) collective-permute-start(f32[20,128]{1,0:T(8,128)S(1)} %reshape_squeeze.40), channel_id=1, source_target_pairs={{0,7},{1,0},{2,1},{3,2},{4,3},{5,4},{6,5},{7,6},{8,15},{9,8},{10,9... | collective-permute-start | bytes 30728 | tf_op jit(solution)/shard_map/ppermute | solution.py:25
  13.3 1.5 %collective-permute-done = f32[20,128]{1,0:T(8,128)S(1)} collective-permute-done((f32[20,128]{1,0:T(8,128)S(1)}, f32[20,128]{1,0:T(8,128)S(1)}, u32[]{:S(2)}, u32[]{:S(2)}) %collective-permute-start) | collective-permute-done | bytes 10272 | tf_op jit(solution)/shard_map/ppermute | solution.py:25
  15.0 0.8 select_add_fusion.1
  16.0 1.7 %collective-permute-start.3 = (f32[160,128]{1,0:T(8,128)S(1)}, f32[160,128]{1,0:T(8,128)S(1)}, u32[]{:S(2)}, u32[]{:S(2)}) collective-permute-start(f32[160,128]{1,0:T(8,128)S(1)} %bitcast.133), channel_id=1, source_target_pairs={{0,24},{8,0},{16,8},{24,16},{1,25},{9,1},{17,9},{25,17},{2,26},{10... | collective-permute-start | bytes 245768 | tf_op jit(solution)/shard_map/ppermute | solution.py:23
  17.8 2.1 %collective-permute-done.2 = f32[160,128]{1,0:T(8,128)S(1)} collective-permute-done((f32[160,128]{1,0:T(8,128)S(1)}, f32[160,128]{1,0:T(8,128)S(1)}, u32[]{:S(2)}, u32[]{:S(2)}) %collective-permute-start.2) | collective-permute-done | bytes 81952 | tf_op jit(solution)/shard_map/ppermute | solution.py:23
  20.0 0.8 fusion.5
  20.8 0.7 fusion.6
  21.5 0.7 convolution_multiply_fusion.1
  22.2 0.7 convolution_bitcast_fusion.2
  22.9 0.7 fusion.51
  23.6 0.7 fusion
  24.3 1.1 %slice_reduce_fusion.1 = (f32[160,16]{1,0:T(8,128)S(1)}, f32[160,16]{1,0:T(8,128)S(1)}) fusion(f32[160,16,128]{2,1,0:T(8,128)S(1)} %fusion), kind=kLoop, calls=%fused_computation.24 | loop fusion | bytes 40960 | tf_op jit(solution)/shard_map/slice | solution.py:87
  25.5 1.4 %collective-permute-start.4 = (f32[20,128]{1,0:T(8,128)S(1)}, f32[20,128]{1,0:T(8,128)S(1)}, u32[]{:S(2)}, u32[]{:S(2)}) collective-permute-start(f32[20,128]{1,0:T(8,128)S(1)} %reshape_squeeze.41), channel_id=1, source_target_pairs={{0,1},{1,2},{2,3},{3,4},{4,5},{5,6},{6,7},{7,0},{8,9},{9,10},{10,1... | collective-permute-start | bytes 30728 | tf_op jit(solution)/shard_map/ppermute | solution.py:25
  27.0 3.4 %collective-permute-start.5 = (f32[20,128]{1,0:T(8,128)S(1)}, f32[20,128]{1,0:T(8,128)S(1)}, u32[]{:S(2)}, u32[]{:S(2)}) collective-permute-start(f32[20,128]{1,0:T(8,128)S(1)} %reshape_squeeze.42), channel_id=1, source_target_pairs={{0,7},{1,0},{2,1},{3,2},{4,3},{5,4},{6,5},{7,6},{8,15},{9,8},{10,9... | collective-permute-start | bytes 30728 | tf_op jit(solution)/shard_map/ppermute | solution.py:25
  30.4 1.5 %collective-permute-done.4 = f32[20,128]{1,0:T(8,128)S(1)} collective-permute-done((f32[20,128]{1,0:T(8,128)S(1)}, f32[20,128]{1,0:T(8,128)S(1)}, u32[]{:S(2)}, u32[]{:S(2)}) %collective-permute-start.4) | collective-permute-done | bytes 10272 | tf_op jit(solution)/shard_map/ppermute | solution.py:25
  32.2 0.8 select_add_fusion
  33.2 0.9 %collective-permute-start.6 = (f32[160,128]{1,0:T(8,128)S(1)}, f32[160,128]{1,0:T(8,128)S(1)}, u32[]{:S(2)}, u32[]{:S(2)}) collective-permute-start(f32[160,128]{1,0:T(8,128)S(1)} %bitcast.134), channel_id=1, source_target_pairs={{0,8},{8,16},{16,24},{24,0},{1,9},{9,17},{17,25},{25,1},{2,10},{10... | collective-permute-start | bytes 245768 | tf_op jit(solution)/shard_map/ppermute | solution.py:23
  34.1 0.9 collective-permute-start.7
  35.0 0.7 copy.50
  36.3 0.7 collective-permute-done.6
  37.4 0.8 fusion.9
  38.3 1.0 %copy-done.3 = f32[160,16,128]{2,1,0:T(8,128)} copy-done((f32[160,16,128]{2,1,0:T(8,128)}, f32[160,16,128]{2,1,0:T(8,128)S(1)}, u32[]{:S(2)}) %copy-start.3) | copy-done | bytes 1310744
  39.9 3.6 %shard_map.320 = f32[4,8192]{1,0:T(4,128)} custom-call(s32[1,8192]{1,0:T(1,128)} %bitcast.131, f32[1,8192]{1,0:T(1,128)} %bitcast.130, f32[4,16,128]{2,1,0:T(8,128)} %fusion.37.table_ref), custom_call_target="tpu_custom_call" | custom-call | tf_op jit(solution)/shard_map/pallas_call | solution.py:209
  43.5 14.6 %all_to_all.5 = f32[4,32,256]{2,0,1:T(4,128)S(1)} all-to-all(f32[4,32,256]{2,0,1:T(4,128)} %bitcast.129), channel_id=1, replica_groups=mesh['gx'=4,'gy'=8] {'gx','gy'}, dimensions={1} | all-to-all | bytes 262144 | tf_op jit(solution)/shard_map/all_to_all | solution.py:249
  58.1 0.7 copy.41.table_ref
  58.8 4.7 %shard_map.321 = f32[4,2048]{1,0:T(4,128)} custom-call(s32[1,8192]{1,0:T(1,128)} %bitcast.141, f32[1,8192]{1,0:T(1,128)} %bitcast.142, f32[4,32,256]{2,1,0:T(8,128)} %copy.41.table_ref), custom_call_target="tpu_custom_call" | custom-call | tf_op jit(solution)/shard_map/pallas_call | solution.py:209
  63.4 1.0 %fusion.38 = (f32[1,2048]{1,0:T(1,128)S(1)}, f32[1,2048]{1,0:T(1,128)S(1)}, f32[1,2048]{1,0:T(1,128)S(1)}, f32[1,2048]{1,0:T(1,128)S(1)}) fusion(f32[4,2048]{1,0:T(4,128)} %shard_map.321), kind=kLoop, calls=%fused_computation.74 | loop fusion | flops 8192 | bytes 65536 | tf_op jit(solution)/shard_map/mul | solution.py:253
  65.0 0.7 fusion.49
  65.7 0.7 convolution_bitcast_fusion.7
  66.5 1.7 %fusion.52 = f32[2,40,16,256]{3,2,1,0:T(8,128)} fusion(f32[2,40,16,128]{3,2,1,0:T(8,128)S(1)} %fusion.41, f32[128,256,1,1]{1,0,3,2:T(8,128)S(1)} %copy-done.4), kind=kOutput, calls=%fused_computation.103 | convolution fusion | flops 251658240 | bytes 2097152 | tf_op jit(solution)/shard_map/...xc,cd->...xd/dot_general | solution.py:121
  68.3 2.1 %collective-permute-start.10 = (f32[10,128]{1,0:T(8,128)S(1)}, f32[10,128]{1,0:T(8,128)S(1)}, u32[]{:S(2)}, u32[]{:S(2)}) collective-permute-start(f32[10,128]{1,0:T(8,128)S(1)} %reshape_squeeze.46), channel_id=1, source_target_pairs={{0,7},{1,0},{2,1},{3,2},{4,3},{5,4},{6,5},{7,6},{8,15},{9,8},{10,9... | collective-permute-start | bytes 15368 | tf_op jit(solution)/shard_map/ppermute | solution.py:25
  71.1 0.9 collective-permute-done.10
  72.0 4.9 %collective-permute-done.11 = f32[10,128]{1,0:T(8,128)} collective-permute-done((f32[10,128]{1,0:T(8,128)S(1)}, f32[10,128]{1,0:T(8,128)}, u32[]{:S(2)}, u32[]{:S(2)}) %collective-permute-start.11) | collective-permute-done | bytes 5152 | tf_op jit(solution)/shard_map/ppermute | solution.py:25
  76.9 0.8 broadcast_in_dim.268
  77.7 1.8 %fusion.17 = f32[2,40,16,128]{3,2,1,0:T(8,128)S(1)} fusion(f32[2,40,16,128]{3,2,1,0:T(8,128)S(1)} %fusion.41, f32[2,40,16,256]{3,2,1,0:T(8,128)} %fusion.52, f32[2,40,32,128]{3,2,1,0:T(8,128)S(1)} %convolution_bitcast_fusion.7, f32[40,16,128]{2,1,0:T(8,128)S(1)} %get-tuple-element.69, f32[40,16,128]{2,1,0:T(8,128)S(1)} %get-tuple-element.68, ...), kind=kLoop, calls=%fused_computation.43 | loop fusion | flops 3440640 | bytes 4679968 | tf_op jit(solution)/shard_map/sub | solution.py:127
  79.5 0.7 fusion.53
  81.0 1.2 %collective-permute-start.14 = (f32[10,128]{1,0:T(8,128)S(1)}, f32[10,128]{1,0:T(8,128)S(1)}, u32[]{:S(2)}, u32[]{:S(2)}) collective-permute-start(f32[10,128]{1,0:T(8,128)S(1)} %reshape_squeeze.50), channel_id=1, source_target_pairs={{0,7},{1,0},{2,1},{3,2},{4,3},{5,4},{6,5},{7,6},{8,15},{9,8},{10,9... | collective-permute-start | bytes 15368 | tf_op jit(solution)/shard_map/ppermute | solution.py:25
  82.3 0.8 collective-permute-start.15
  83.6 1.8 %convolution_bitcast_fusion.6 = f32[2,40,32,128]{3,2,1,0:T(8,128)} fusion(f32[2,40,16,128]{3,2,1,0:T(8,128)S(1)} %fusion.17, f32[32,16,1,1]{0,1,3,2:T(8,128)S(1)} %copy-done.9), kind=kOutput, calls=%fused_computation.19 | convolution fusion | flops 31457280 | bytes 1968128 | tf_op jit(solution)/shard_map/ab,...by->...ay/dot_general | solution.py:120
  85.5 3.1 %collective-permute-done.15 = f32[10,128]{1,0:T(8,128)S(1)} collective-permute-done((f32[10,128]{1,0:T(8,128)S(1)}, f32[10,128]{1,0:T(8,128)S(1)}, u32[]{:S(2)}, u32[]{:S(2)}) %collective-permute-start.15) | collective-permute-done | bytes 5152 | tf_op jit(solution)/shard_map/ppermute | solution.py:25
  88.8 2.7 %fusion.29 = f32[2,40,16,128]{3,2,1,0:T(8,128)} fusion(f32[2,40,16,128]{3,2,1,0:T(8,128)S(1)} %fusion.17, f32[2,40,16,256]{3,2,1,0:T(8,128)S(1)} %fusion.53, f32[2,40,32,128]{3,2,1,0:T(8,128)} %convolution_bitcast_fusion.6, f32[2,40,16]{2,1,0:T(8,128)S(1)} %broadcast_in_dim.276, f32[2,40,16]{2,1,0:T(8,128)S(1)} %broadcast_in_dim.274, ...), kind=kLoop, calls=%fused_computation.55 | loop fusion | flops 3440640 | bytes 4679968 | tf_op jit(solution)/shard_map/sub | solution.py:127
  (80 shorter events, 7.5 us)
Async XLA Ops:
  0.6 0.7 copy-start.14
  0.6 0.7 copy-start.16
  0.7 0.9 %copy-start.8 = (f32[16,16,1]{1,0,2:T(8,128)S(1)}, f32[16,16,1]{1,0,2:T(8,128)}, u32[]{:S(2)}) copy-start(f32[16,16,1]{1,0,2:T(8,128)} %constant.168) | copy-start | bytes 3076
  0.7 1.3 %copy-start.1 = (f32[4,40,16,128]{3,2,1,0:T(8,128)S(1)}, f32[4,40,16,128]{3,2,1,0:T(8,128)}, u32[]{:S(2)}) copy-start(f32[4,40,16,128]{3,2,1,0:T(8,128)} %param.41) | copy-start | bytes 3932164
  0.7 0.8 copy-start.13
  2.7 0.8 copy-start.7
  3.5 0.8 copy-start.6
  4.4 0.8 copy-start.5
  7.1 7.7 %collective-permute-start = (f32[20,128]{1,0:T(8,128)S(1)}, f32[20,128]{1,0:T(8,128)S(1)}, u32[]{:S(2)}, u32[]{:S(2)}) collective-permute-start(f32[20,128]{1,0:T(8,128)S(1)} %reshape_squeeze.39), channel_id=1, source_target_pairs={{0,1},{1,2},{2,3},{3,4},{4,5},{5,6},{6,7},{7,0},{8,9},{9,10},{10,1... | collective-permute-start | bytes 30728 | tf_op jit(solution)/shard_map/ppermute | solution.py:25
  10.1 4.7 %collective-permute-start.1 = (f32[20,128]{1,0:T(8,128)S(1)}, f32[20,128]{1,0:T(8,128)S(1)}, u32[]{:S(2)}, u32[]{:S(2)}) collective-permute-start(f32[20,128]{1,0:T(8,128)S(1)} %reshape_squeeze.40), channel_id=1, source_target_pairs={{0,7},{1,0},{2,1},{3,2},{4,3},{5,4},{6,5},{7,6},{8,15},{9,8},{10,9... | collective-permute-start | bytes 30728 | tf_op jit(solution)/shard_map/ppermute | solution.py:25
  15.0 5.0 %copy-start.10 = (f32[16,128]{1,0:T(8,128)S(1)}, f32[16,128]{1,0:T(8,128)}, u32[]{:S(2)}) copy-start(f32[16,128]{1,0:T(8,128)} %constant.165) | copy-start | bytes 24580
  15.0 5.0 %copy-start.11 = (f32[16,16,1]{1,0,2:T(8,128)S(1)}, f32[16,16,1]{1,0,2:T(8,128)}, u32[]{:S(2)}) copy-start(f32[16,16,1]{1,0,2:T(8,128)} %constant.172) | copy-start | bytes 3076
  16.0 3.9 %collective-permute-start.2 = (f32[160,128]{1,0:T(8,128)S(1)}, f32[160,128]{1,0:T(8,128)S(1)}, u32[]{:S(2)}, u32[]{:S(2)}) collective-permute-start(f32[160,128]{1,0:T(8,128)S(1)} %bitcast.135), channel_id=1, source_target_pairs={{0,8},{8,16},{16,24},{24,0},{1,9},{9,17},{17,25},{25,1},{2,10},{10... | collective-permute-start | bytes 245768 | tf_op jit(solution)/shard_map/ppermute | solution.py:23
  16.0 4.0 %collective-permute-start.3 = (f32[160,128]{1,0:T(8,128)S(1)}, f32[160,128]{1,0:T(8,128)S(1)}, u32[]{:S(2)}, u32[]{:S(2)}) collective-permute-start(f32[160,128]{1,0:T(8,128)S(1)} %bitcast.133), channel_id=1, source_target_pairs={{0,24},{8,0},{16,8},{24,16},{1,25},{9,1},{17,9},{25,17},{2,26},{10... | collective-permute-start | bytes 245768 | tf_op jit(solution)/shard_map/ppermute | solution.py:23
  25.5 6.5 %collective-permute-start.4 = (f32[20,128]{1,0:T(8,128)S(1)}, f32[20,128]{1,0:T(8,128)S(1)}, u32[]{:S(2)}, u32[]{:S(2)}) collective-permute-start(f32[20,128]{1,0:T(8,128)S(1)} %reshape_squeeze.41), channel_id=1, source_target_pairs={{0,1},{1,2},{2,3},{3,4},{4,5},{5,6},{6,7},{7,0},{8,9},{9,10},{10,1... | collective-permute-start | bytes 30728 | tf_op jit(solution)/shard_map/ppermute | solution.py:25
  27.0 5.1 %collective-permute-start.5 = (f32[20,128]{1,0:T(8,128)S(1)}, f32[20,128]{1,0:T(8,128)S(1)}, u32[]{:S(2)}, u32[]{:S(2)}) collective-permute-start(f32[20,128]{1,0:T(8,128)S(1)} %reshape_squeeze.42), channel_id=1, source_target_pairs={{0,7},{1,0},{2,1},{3,2},{4,3},{5,4},{6,5},{7,6},{8,15},{9,8},{10,9... | collective-permute-start | bytes 30728 | tf_op jit(solution)/shard_map/ppermute | solution.py:25
  32.2 2.8 %copy-start.15 = (s32[1,32]{1,0:T(1,128)S(1)}, s32[1,32]{1,0:T(1,128)}, u32[]{:S(2)}) copy-start(s32[1,32]{1,0:T(1,128)} %param.44) | copy-start | bytes 388
  32.2 3.5 %copy-start.12 = (s32[1,32,256]{2,1,0:T(8,128)S(1)}, s32[1,32,256]{2,1,0:T(8,128)}, u32[]{:S(2)}) copy-start(s32[1,32,256]{2,1,0:T(8,128)} %param.43) | copy-start | bytes 98308
  33.2 3.9 %collective-permute-start.6 = (f32[160,128]{1,0:T(8,128)S(1)}, f32[160,128]{1,0:T(8,128)S(1)}, u32[]{:S(2)}, u32[]{:S(2)}) collective-permute-start(f32[160,128]{1,0:T(8,128)S(1)} %bitcast.134), channel_id=1, source_target_pairs={{0,8},{8,16},{16,24},{24,0},{1,9},{9,17},{17,25},{25,1},{2,10},{10... | collective-permute-start | bytes 245768 | tf_op jit(solution)/shard_map/ppermute | solution.py:23
  34.1 3.3 %collective-permute-start.7 = (f32[160,128]{1,0:T(8,128)S(1)}, f32[160,128]{1,0:T(8,128)S(1)}, u32[]{:S(2)}, u32[]{:S(2)}) collective-permute-start(f32[160,128]{1,0:T(8,128)S(1)} %bitcast.132), channel_id=1, source_target_pairs={{0,24},{8,0},{16,8},{24,16},{1,25},{9,1},{17,9},{25,17},{2,26},{10... | collective-permute-start | bytes 245768 | tf_op jit(solution)/shard_map/ppermute | solution.py:23
  36.3 28.0 %copy-start = (f32[2,40,16,128]{3,2,1,0:T(8,128)S(1)}, f32[2,40,16,128]{3,2,1,0:T(8,128)}, u32[]{:S(2)}) copy-start(f32[2,40,16,128]{3,2,1,0:T(8,128)} %param.45) | copy-start | bytes 1966084
  38.2 1.1 %copy-start.3 = (f32[160,16,128]{2,1,0:T(8,128)}, f32[160,16,128]{2,1,0:T(8,128)S(1)}, u32[]{:S(2)}) copy-start(f32[160,16,128]{2,1,0:T(8,128)S(1)} %fusion.9) | copy-start | bytes 3932164
  39.9 25.8 %copy-start.9 = (f32[32,16,1,1]{0,1,3,2:T(8,128)S(1)}, f32[32,16,1,1]{0,1,3,2:T(8,128)}, u32[]{:S(2)}) copy-start(f32[32,16,1,1]{0,1,3,2:T(8,128)} %constant.173) | copy-start | bytes 6148
  65.0 1.4 %copy-start.4 = (f32[128,256,1,1]{1,0,3,2:T(8,128)S(1)}, f32[128,256,1,1]{1,0,3,2:T(8,128)}, u32[]{:S(2)}) copy-start(f32[128,256,1,1]{1,0,3,2:T(8,128)} %constant.174) | copy-start | bytes 393220
  66.4 4.6 %copy-start.2 = (f32[2,40,16,128]{3,2,1,0:T(8,128)S(1)}, f32[2,40,16,128]{3,2,1,0:T(8,128)}, u32[]{:S(2)}) copy-start(f32[2,40,16,128]{3,2,1,0:T(8,128)} %param.46) | copy-start | bytes 1966084
  68.3 3.7 %collective-permute-start.10 = (f32[10,128]{1,0:T(8,128)S(1)}, f32[10,128]{1,0:T(8,128)S(1)}, u32[]{:S(2)}, u32[]{:S(2)}) collective-permute-start(f32[10,128]{1,0:T(8,128)S(1)} %reshape_squeeze.46), channel_id=1, source_target_pairs={{0,7},{1,0},{2,1},{3,2},{4,3},{5,4},{6,5},{7,6},{8,15},{9,8},{10,9... | collective-permute-start | bytes 15368 | tf_op jit(solution)/shard_map/ppermute | solution.py:25
  70.4 6.5 %collective-permute-start.11 = (f32[10,128]{1,0:T(8,128)S(1)}, f32[10,128]{1,0:T(8,128)}, u32[]{:S(2)}, u32[]{:S(2)}) collective-permute-start(f32[10,128]{1,0:T(8,128)S(1)} %reshape_squeeze.47), channel_id=1, source_target_pairs={{0,1},{1,2},{2,3},{3,4},{4,5},{5,6},{6,7},{7,0},{8,9},{9,10},{10,1... | collective-permute-start | bytes 15368 | tf_op jit(solution)/shard_map/ppermute | solution.py:25
  70.5 7.2 %collective-permute-start.8 = (f32[80,128]{1,0:T(8,128)}, f32[80,128]{1,0:T(8,128)S(1)}, u32[]{:S(2)}, u32[]{:S(2)}) collective-permute-start(f32[80,128]{1,0:T(8,128)} %bitcast.33), channel_id=1, source_target_pairs={{0,24},{8,0},{16,8},{24,16},{1,25},{9,1},{17,9},{25,17},{2,26},{10... | collective-permute-start | bytes 122888 | tf_op jit(solution)/shard_map/ppermute | solution.py:23
  70.5 7.2 %collective-permute-start.9 = (f32[80,128]{1,0:T(8,128)}, f32[80,128]{1,0:T(8,128)}, u32[]{:S(2)}, u32[]{:S(2)}) collective-permute-start(f32[80,128]{1,0:T(8,128)} %bitcast.35), channel_id=1, source_target_pairs={{0,8},{8,16},{16,24},{24,0},{1,9},{9,17},{17,25},{25,1},{2,10},{10... | collective-permute-start | bytes 122888 | tf_op jit(solution)/shard_map/ppermute | solution.py:23
  81.0 4.5 %collective-permute-start.14 = (f32[10,128]{1,0:T(8,128)S(1)}, f32[10,128]{1,0:T(8,128)S(1)}, u32[]{:S(2)}, u32[]{:S(2)}) collective-permute-start(f32[10,128]{1,0:T(8,128)S(1)} %reshape_squeeze.50), channel_id=1, source_target_pairs={{0,7},{1,0},{2,1},{3,2},{4,3},{5,4},{6,5},{7,6},{8,15},{9,8},{10,9... | collective-permute-start | bytes 15368 | tf_op jit(solution)/shard_map/ppermute | solution.py:25
  82.3 6.4 %collective-permute-start.15 = (f32[10,128]{1,0:T(8,128)S(1)}, f32[10,128]{1,0:T(8,128)S(1)}, u32[]{:S(2)}, u32[]{:S(2)}) collective-permute-start(f32[10,128]{1,0:T(8,128)S(1)} %reshape_squeeze.51), channel_id=1, source_target_pairs={{0,1},{1,2},{2,3},{3,4},{4,5},{5,6},{6,7},{7,0},{8,9},{9,10},{10,1... | collective-permute-start | bytes 15368 | tf_op jit(solution)/shard_map/ppermute | solution.py:25
  83.1 5.6 %collective-permute-start.12 = (f32[80,128]{1,0:T(8,128)S(1)}, f32[80,128]{1,0:T(8,128)S(1)}, u32[]{:S(2)}, u32[]{:S(2)}) collective-permute-start(f32[80,128]{1,0:T(8,128)S(1)} %bitcast.140), channel_id=1, source_target_pairs={{0,24},{8,0},{16,8},{24,16},{1,25},{9,1},{17,9},{25,17},{2,26},{10... | collective-permute-start | bytes 122888 | tf_op jit(solution)/shard_map/ppermute | solution.py:23
  83.1 5.6 %collective-permute-start.13 = (f32[80,128]{1,0:T(8,128)S(1)}, f32[80,128]{1,0:T(8,128)S(1)}, u32[]{:S(2)}, u32[]{:S(2)}) collective-permute-start(f32[80,128]{1,0:T(8,128)S(1)} %bitcast.139), channel_id=1, source_target_pairs={{0,8},{8,16},{16,24},{24,0},{1,9},{9,17},{17,25},{25,1},{2,10},{10... | collective-permute-start | bytes 122888 | tf_op jit(solution)/shard_map/ppermute | solution.py:23

commit v18 on v15

--- a/solution.py
+++ b/solution.py
@@ -247,8 +247,8 @@
     received = lax.all_to_all(payload, ("gx", "gy"), split_axis=1, concat_axis=1, tiled=True)
     source_count, ocean_x, ocean_y = remap_slots.shape
     ocean_flux = onehot_gather(received, remap_slots, remap_weights, source_count).reshape(fields, ocean_x, ocean_y)
-    velocity = ocean_velocity.at[0, 0].add(wind_coef * jnp.tanh(ocean_flux[0]))
-    velocity = velocity.at[1, 0].add(wind_coef * jnp.tanh(ocean_flux[1]))
+    surface_level = (jnp.arange(ocean_velocity.shape[1]) == 0)[:, None, None]
+    velocity = ocean_velocity + jnp.where(surface_level, wind_coef * jnp.tanh(ocean_flux[:2])[:, None], 0.0)
     tracers = ocean_tracers.at[0, 0].add(surf_coef * ocean_flux[2])
     tracers = tracers.at[1, 0].add(surf_coef * ocean_flux[3])
     for repeat in range(OSTEPS):

time: 90.5 us -> 93.7 us (1.035)
  blocking collectives: 14.6 us -> 0 us
  waiting for transfers between devices: 15.7 us -> 25.3 us
  starting transfers between devices: 19.8 us -> 24.9 us
  other arithmetic: 4.39 us -> 7.16 us
    all_to_all x1 -> x0, blocking collectives: 14.6 us -> none  [per_device(): lax.all_to_all(payload, ('gx', 'gy'), split_axis=1, concat_axis=1, tiled=...]
    all_to_all x0 -> x1, waiting for transfers between devices: none -> 7.16 us  [per_device(): lax.all_to_all(payload, ('gx', 'gy'), split_axis=1, concat_axis=1, tiled=...]
    ppermute x8, waiting for transfers between devices: 3.3 us -> 7.59 us  [neighbour(): lax.ppermute(values, 'gx', [(i, (i + step_x) % count_x) for i in range(co...]
    ppermute x8, starting transfers between devices: 15.1 us -> 17.7 us  [neighbour(): lax.ppermute(values, 'gy', [(j, (j + step_y) % count_y) for j in range(co...]
    all_to_all x0 -> x1, starting transfers between devices: none -> 2.58 us  [per_device(): lax.all_to_all(payload, ('gx', 'gy'), split_axis=1, concat_axis=1, tiled=...]
    ppermute x8, waiting for transfers between devices: 12.4 us -> 10.6 us  [neighbour(): lax.ppermute(values, 'gy', [(j, (j + step_y) % count_y) for j in range(co...]
    unnamed x58 -> x57, local copies, waits for them, and re-layouts: 3.05 us -> 2.46 us
  transfers between devices with their start and end apart: 16 -> 17, of which waited for: 10 -> 10; matrix products, arithmetic and copies ran while one was open for 5% -> 6% of each run, Pallas kernels for 0% -> 0%
where the time goes in v18:
time: 93.7 us; the launch traced here: 92.1 us
  waiting for transfers between devices  25.3 us (27%)
  starting transfers between devices  24.9 us (27%)
  matrix products  15.1 us (16%)
  local copies, waits for them, and re-layouts  10.1 us (11%)
  Pallas kernels  8.28 us (9%)
  other arithmetic  7.16 us (8%)
  between operations  1.32 us (1%)
    ppermute x8, starting transfers between devices, neighbour(): lax.ppermute(values, 'gy', [(j, (j + step_y) % count_y) for j in range(co...  17.7 us
    ppermute x8, waiting for transfers between devices, neighbour(): lax.ppermute(values, 'gy', [(j, (j + step_y) % count_y) for j in range(co...  10.6 us
    pallas_call x2, Pallas kernels, onehot_gather(): pl.pallas_call(gather_kernel, grid=(blocks, groups), in_specs=[pl.BlockSp...  8.28 us
    ppermute x8, waiting for transfers between devices, neighbour(): lax.ppermute(values, 'gx', [(i, (i + step_x) % count_x) for i in range(co...  7.59 us
    all_to_all x1, waiting for transfers between devices, per_device(): lax.all_to_all(payload, ('gx', 'gy'), split_axis=1, concat_axis=1, tiled=...  7.16 us
    ppermute x8, starting transfers between devices, neighbour(): lax.ppermute(values, 'gx', [(i, (i + step_x) % count_x) for i in range(co...  4.6 us
    dot_general x2, matrix products, tracer_step(): jnp.einsum('ab,...by->...ay', sum_x, tracers, precision=precision)  4.15 us
    all_to_all x1, starting transfers between devices, per_device(): lax.all_to_all(payload, ('gx', 'gy'), split_axis=1, concat_axis=1, tiled=...  2.58 us
  transfers between devices with their start and end apart: 17, of which 10 were waited for; matrix products, arithmetic and copies ran while one was open for 6% of the time, Pallas kernels for 0%

profile of v18, /device:TPU:0, one launch (start us, length us, event | category | flops | bytes accessed | tf_op | source)
XLA Modules:
  0.0 92.1 jit_solution(13609087902397727787)
XLA Ops:
  1.3 0.8 multiply_bitcast_fusion
  2.1 0.7 fusion.10
  2.8 0.7 convolution_bitcast_fusion.5
  3.6 0.7 fusion.49
  4.4 0.7 fusion.2
  5.3 0.7 fusion.1
  6.0 1.1 %slice_reduce_fusion.3 = (f32[160,16]{1,0:T(8,128)S(1)}, f32[160,16]{1,0:T(8,128)S(1)}) fusion(f32[160,16,128]{2,1,0:T(8,128)S(1)} %fusion.1), kind=kLoop, calls=%fused_computation.24 | loop fusion | bytes 40960 | tf_op jit(solution)/shard_map/slice | solution.py:87
  7.2 6.0 %collective-permute-start.1 = (f32[20,128]{1,0:T(8,128)S(1)}, f32[20,128]{1,0:T(8,128)S(1)}, u32[]{:S(2)}, u32[]{:S(2)}) collective-permute-start(f32[20,128]{1,0:T(8,128)S(1)} %reshape_squeeze.40), channel_id=1, source_target_pairs={{0,7},{1,0},{2,1},{3,2},{4,3},{5,4},{6,5},{7,6},{8,15},{9,8},{10,9... | collective-permute-start | bytes 30728 | tf_op jit(solution)/shard_map/ppermute | solution.py:25
  13.4 1.2 %collective-permute-done.1 = f32[20,128]{1,0:T(8,128)S(1)} collective-permute-done((f32[20,128]{1,0:T(8,128)S(1)}, f32[20,128]{1,0:T(8,128)S(1)}, u32[]{:S(2)}, u32[]{:S(2)}) %collective-permute-start.1) | collective-permute-done | bytes 10272 | tf_op jit(solution)/shard_map/ppermute | solution.py:25
  14.7 5.0 %collective-permute-done = f32[20,128]{1,0:T(8,128)S(1)} collective-permute-done((f32[20,128]{1,0:T(8,128)S(1)}, f32[20,128]{1,0:T(8,128)S(1)}, u32[]{:S(2)}, u32[]{:S(2)}) %collective-permute-start) | collective-permute-done | bytes 10272 | tf_op jit(solution)/shard_map/ppermute | solution.py:25
  19.8 0.8 select_add_fusion.1
  21.4 1.5 %collective-permute-done.3 = f32[160,128]{1,0:T(8,128)S(1)} collective-permute-done((f32[160,128]{1,0:T(8,128)S(1)}, f32[160,128]{1,0:T(8,128)S(1)}, u32[]{:S(2)}, u32[]{:S(2)}) %collective-permute-start.3) | collective-permute-done | bytes 81952 | tf_op jit(solution)/shard_map/ppermute | solution.py:23
  22.9 2.7 %collective-permute-done.2 = f32[160,128]{1,0:T(8,128)S(1)} collective-permute-done((f32[160,128]{1,0:T(8,128)S(1)}, f32[160,128]{1,0:T(8,128)S(1)}, u32[]{:S(2)}, u32[]{:S(2)}) %collective-permute-start.2) | collective-permute-done | bytes 81952 | tf_op jit(solution)/shard_map/ppermute | solution.py:23
  25.7 0.8 fusion.5
  26.5 0.7 fusion.6
  27.2 0.7 convolution_multiply_fusion.1
  27.9 0.7 convolution_bitcast_fusion.2
  28.6 0.7 fusion.50
  29.3 0.7 fusion
  30.0 1.1 %slice_reduce_fusion.1 = (f32[160,16]{1,0:T(8,128)S(1)}, f32[160,16]{1,0:T(8,128)S(1)}) fusion(f32[160,16,128]{2,1,0:T(8,128)S(1)} %fusion), kind=kLoop, calls=%fused_computation.22 | loop fusion | bytes 40960 | tf_op jit(solution)/shard_map/slice | solution.py:87
  31.3 2.1 %collective-permute-start.4 = (f32[20,128]{1,0:T(8,128)S(1)}, f32[20,128]{1,0:T(8,128)S(1)}, u32[]{:S(2)}, u32[]{:S(2)}) collective-permute-start(f32[20,128]{1,0:T(8,128)S(1)} %reshape_squeeze.41), channel_id=1, source_target_pairs={{0,1},{1,2},{2,3},{3,4},{4,5},{5,6},{6,7},{7,0},{8,9},{9,10},{10,1... | collective-permute-start | bytes 30728 | tf_op jit(solution)/shard_map/ppermute | solution.py:25
  33.4 1.5 %collective-permute-done.5 = f32[20,128]{1,0:T(8,128)S(1)} collective-permute-done((f32[20,128]{1,0:T(8,128)S(1)}, f32[20,128]{1,0:T(8,128)S(1)}, u32[]{:S(2)}, u32[]{:S(2)}) %collective-permute-start.5) | collective-permute-done | bytes 10272 | tf_op jit(solution)/shard_map/ppermute | solution.py:25
  35.0 2.8 %collective-permute-done.4 = f32[20,128]{1,0:T(8,128)S(1)} collective-permute-done((f32[20,128]{1,0:T(8,128)S(1)}, f32[20,128]{1,0:T(8,128)S(1)}, u32[]{:S(2)}, u32[]{:S(2)}) %collective-permute-start.4) | collective-permute-done | bytes 10272 | tf_op jit(solution)/shard_map/ppermute | solution.py:25
  37.9 0.8 select_add_fusion
  39.5 0.7 copy.51
  41.4 1.6 %collective-permute-done.6 = f32[160,128]{1,0:T(8,128)S(1)} collective-permute-done((f32[160,128]{1,0:T(8,128)S(1)}, f32[160,128]{1,0:T(8,128)S(1)}, u32[]{:S(2)}, u32[]{:S(2)}) %collective-permute-start.6) | collective-permute-done | bytes 81952 | tf_op jit(solution)/shard_map/ppermute | solution.py:23
  43.0 0.8 fusion.9
  43.9 0.7 fusion.37.table_ref
  44.6 3.6 %shard_map.320 = f32[4,8192]{1,0:T(4,128)} custom-call(s32[1,8192]{1,0:T(1,128)} %bitcast.151, f32[1,8192]{1,0:T(1,128)} %bitcast.152, f32[4,16,128]{2,1,0:T(8,128)} %fusion.37.table_ref), custom_call_target="tpu_custom_call" | custom-call | tf_op jit(solution)/shard_map/pallas_call | solution.py:207
  48.2 2.6 %all-to-all-start = ((f32[4,32,256]{2,0,1:T(4,128)}), f32[4,32,256]{2,0,1:T(4,128)S(1)}, u32[]{:S(2)}, u32[]{:S(2)}) async-start(f32[4,32,256]{2,0,1:T(4,128)} %bitcast.150), calls=%async_computation | async-start | bytes 262144 | tf_op jit(solution)/shard_map/all_to_all | solution.py:247
  51.4 7.2 %all-to-all-done = f32[4,32,256]{2,0,1:T(4,128)S(1)} async-done(((f32[4,32,256]{2,0,1:T(4,128)}), f32[4,32,256]{2,0,1:T(4,128)S(1)}, u32[]{:S(2)}, u32[]{:S(2)}) %all-to-all-start) | async-done | bytes 131104 | tf_op jit(solution)/shard_map/all_to_all | solution.py:247
  58.5 0.7 copy.41.table_ref
  59.2 4.7 %shard_map.321 = f32[4,2048]{1,0:T(4,128)} custom-call(s32[1,8192]{1,0:T(1,128)} %bitcast.162, f32[1,8192]{1,0:T(1,128)} %bitcast.163, f32[4,32,256]{2,1,0:T(8,128)} %copy.41.table_ref), custom_call_target="tpu_custom_call" | custom-call | tf_op jit(solution)/shard_map/pallas_call | solution.py:207
  63.9 0.9 slice_multiply_fusion.2
  64.7 0.8 fusion.39
  66.2 0.7 fusion.48
  68.2 0.7 reshape_squeeze.47
  68.8 1.2 %collective-permute-start.11 = (f32[10,128]{1,0:T(8,128)}, f32[10,128]{1,0:T(8,128)S(1)}, u32[]{:S(2)}, u32[]{:S(2)}) collective-permute-start(f32[10,128]{1,0:T(8,128)} %reshape_squeeze.47), channel_id=1, source_target_pairs={{0,1},{1,2},{2,3},{3,4},{4,5},{5,6},{6,7},{7,0},{8,9},{9,10},{10,1... | collective-permute-start | bytes 15368 | tf_op jit(solution)/shard_map/ppermute | solution.py:25
  70.2 3.5 %collective-permute-start.10 = (f32[10,128]{1,0:T(8,128)S(1)}, f32[10,128]{1,0:T(8,128)}, u32[]{:S(2)}, u32[]{:S(2)}) collective-permute-start(f32[10,128]{1,0:T(8,128)S(1)} %reshape_squeeze.46), channel_id=1, source_target_pairs={{0,7},{1,0},{2,1},{3,2},{4,3},{5,4},{6,5},{7,6},{8,15},{9,8},{10,9... | collective-permute-start | bytes 15368 | tf_op jit(solution)/shard_map/ppermute | solution.py:25
  73.7 1.7 %collective-permute-start.8 = (f32[80,128]{1,0:T(8,128)S(1)}, f32[80,128]{1,0:T(8,128)}, u32[]{:S(2)}, u32[]{:S(2)}) collective-permute-start(f32[80,128]{1,0:T(8,128)S(1)} %bitcast.158), channel_id=1, source_target_pairs={{0,24},{8,0},{16,8},{24,16},{1,25},{9,1},{17,9},{25,17},{2,26},{10... | collective-permute-start | bytes 122888 | tf_op jit(solution)/shard_map/ppermute | solution.py:23
  75.4 0.8 select_add_fusion.6
  76.2 0.9 fusion.36
  77.2 0.8 broadcast_in_dim.285
  78.1 1.9 %fusion.17 = f32[2,40,16,128]{3,2,1,0:T(8,128)S(1)} fusion(f32[2,40,16,128]{3,2,1,0:T(8,128)S(1)} %fusion.40, f32[2,40,16,128]{3,2,1,0:T(8,128)S(1)} %convolution_bitcast_fusion.8, f32[2,40,16,128]{3,2,1,0:T(8,128)S(1)} %fusion.51, f32[2,40,16,128]{3,2,1,0:T(8,128)S(1)} %fusion.52, f32[40,16,128]{2,1,0:T(8,128)} %get-tuple-element.45, ...), kind=kOutput, calls=%fused_computation.45 | convolution fusion | flops 19169280 | bytes 4025632 | tf_op jit(solution)/shard_map/ab,...by->...ay/dot_general | solution.py:120
  81.7 4.7 %collective-permute-start.14 = (f32[10,128]{1,0:T(8,128)S(1)}, f32[10,128]{1,0:T(8,128)S(1)}, u32[]{:S(2)}, u32[]{:S(2)}) collective-permute-start(f32[10,128]{1,0:T(8,128)S(1)} %reshape_squeeze.50), channel_id=1, source_target_pairs={{0,7},{1,0},{2,1},{3,2},{4,3},{5,4},{6,5},{7,6},{8,15},{9,8},{10,9... | collective-permute-start | bytes 15368 | tf_op jit(solution)/shard_map/ppermute | solution.py:25
  86.4 1.7 %collective-permute-start.12 = (f32[80,128]{1,0:T(8,128)S(1)}, f32[80,128]{1,0:T(8,128)S(1)}, u32[]{:S(2)}, u32[]{:S(2)}) collective-permute-start(f32[80,128]{1,0:T(8,128)S(1)} %bitcast.160), channel_id=1, source_target_pairs={{0,24},{8,0},{16,8},{24,16},{1,25},{9,1},{17,9},{25,17},{2,26},{10... | collective-permute-start | bytes 122888 | tf_op jit(solution)/shard_map/ppermute | solution.py:23
  88.7 1.1 %collective-permute-done.13 = f32[80,128]{1,0:T(8,128)S(1)} collective-permute-done((f32[80,128]{1,0:T(8,128)S(1)}, f32[80,128]{1,0:T(8,128)S(1)}, u32[]{:S(2)}, u32[]{:S(2)}) %collective-permute-start.13) | collective-permute-done | bytes 40992 | tf_op jit(solution)/shard_map/ppermute | solution.py:23
  89.8 2.3 %fusion.29 = f32[2,40,16,128]{3,2,1,0:T(8,128)} fusion(f32[2,40,16,128]{3,2,1,0:T(8,128)S(1)} %fusion.17, f32[2,40,16,128]{3,2,1,0:T(8,128)S(1)} %convolution_bitcast_fusion.6, f32[2,40,16,128]{3,2,1,0:T(8,128)S(1)} %fusion.53, f32[2,40,16,128]{3,2,1,0:T(8,128)S(1)} %fusion.54, f32[2,40,16]{2,1,0:T(8,128)S(1)} %broadcast_in_dim.298, ...), kind=kOutput, calls=%fused_computation.57 | convolution fusion | flops 19169280 | bytes 4025632 | tf_op jit(solution)/shard_map/ab,...by->...ay/dot_general | solution.py:120
  (105 shorter events, 9.5 us)
Async XLA Ops:
  0.6 0.7 copy-start.26
  0.6 0.7 copy-start.16
  0.7 1.4 %copy-start.11 = (f32[16,16,1]{1,0,2:T(8,128)S(1)}, f32[16,16,1]{1,0,2:T(8,128)}, u32[]{:S(2)}) copy-start(f32[16,16,1]{1,0,2:T(8,128)} %constant.125) | copy-start | bytes 3076
  0.7 1.4 %copy-start.1 = (f32[4,40,16,128]{3,2,1,0:T(8,128)S(1)}, f32[4,40,16,128]{3,2,1,0:T(8,128)}, u32[]{:S(2)}) copy-start(f32[4,40,16,128]{3,2,1,0:T(8,128)} %param.37) | copy-start | bytes 3932164
  2.8 0.8 copy-start.10
  3.6 0.8 copy-start.7
  4.4 0.8 copy-start.6
  7.2 7.4 %collective-permute-start.1 = (f32[20,128]{1,0:T(8,128)S(1)}, f32[20,128]{1,0:T(8,128)S(1)}, u32[]{:S(2)}, u32[]{:S(2)}) collective-permute-start(f32[20,128]{1,0:T(8,128)S(1)} %reshape_squeeze.40), channel_id=1, source_target_pairs={{0,7},{1,0},{2,1},{3,2},{4,3},{5,4},{6,5},{7,6},{8,15},{9,8},{10,9... | collective-permute-start | bytes 30728 | tf_op jit(solution)/shard_map/ppermute | solution.py:25
  13.3 6.4 %collective-permute-start = (f32[20,128]{1,0:T(8,128)S(1)}, f32[20,128]{1,0:T(8,128)S(1)}, u32[]{:S(2)}, u32[]{:S(2)}) collective-permute-start(f32[20,128]{1,0:T(8,128)S(1)} %reshape_squeeze.39), channel_id=1, source_target_pairs={{0,1},{1,2},{2,3},{3,4},{4,5},{5,6},{6,7},{7,0},{8,9},{9,10},{10,1... | collective-permute-start | bytes 30728 | tf_op jit(solution)/shard_map/ppermute | solution.py:25
  13.4 24.5 %copy-start.17 = (pred[128]{0:T(512)(128)(4,1)}, pred[128]{0:T(512)(128)(4,1)S(1)}, u32[]{:S(2)}) copy-start(pred[128]{0:T(512)(128)(4,1)S(1)} %get-tuple-element.50) | copy-start | bytes 388
  13.4 24.5 %copy-start.19 = (pred[128]{0:T(512)(128)(4,1)}, pred[128]{0:T(512)(128)(4,1)S(1)}, u32[]{:S(2)}) copy-start(pred[128]{0:T(512)(128)(4,1)S(1)} %get-tuple-element.51) | copy-start | bytes 388
  19.8 5.9 %copy-start.13 = (f32[16,16,1]{1,0,2:T(8,128)S(1)}, f32[16,16,1]{1,0,2:T(8,128)}, u32[]{:S(2)}) copy-start(f32[16,16,1]{1,0,2:T(8,128)} %constant.129) | copy-start | bytes 3076
  19.8 5.8 %copy-start.14 = (f32[16,128]{1,0:T(8,128)S(1)}, f32[16,128]{1,0:T(8,128)}, u32[]{:S(2)}) copy-start(f32[16,128]{1,0:T(8,128)} %constant.124) | copy-start | bytes 24580
  20.8 2.1 %collective-permute-start.3 = (f32[160,128]{1,0:T(8,128)S(1)}, f32[160,128]{1,0:T(8,128)S(1)}, u32[]{:S(2)}, u32[]{:S(2)}) collective-permute-start(f32[160,128]{1,0:T(8,128)S(1)} %bitcast.156), channel_id=1, source_target_pairs={{0,24},{8,0},{16,8},{24,16},{1,25},{9,1},{17,9},{25,17},{2,26},{10... | collective-permute-start | bytes 245768 | tf_op jit(solution)/shard_map/ppermute | solution.py:23
  20.9 4.8 %collective-permute-start.2 = (f32[160,128]{1,0:T(8,128)S(1)}, f32[160,128]{1,0:T(8,128)S(1)}, u32[]{:S(2)}, u32[]{:S(2)}) collective-permute-start(f32[160,128]{1,0:T(8,128)S(1)} %bitcast.154), channel_id=1, source_target_pairs={{0,8},{8,16},{16,24},{24,0},{1,9},{9,17},{17,25},{25,1},{2,10},{10... | collective-permute-start | bytes 245768 | tf_op jit(solution)/shard_map/ppermute | solution.py:23
  21.4 21.6 %copy-start.21 = (pred[16]{0:T(512)(128)(4,1)}, pred[16]{0:T(512)(128)(4,1)S(1)}, u32[]{:S(2)}) copy-start(pred[16]{0:T(512)(128)(4,1)S(1)} %get-tuple-element.52) | copy-start | bytes 52
  21.4 21.6 %copy-start.23 = (pred[16]{0:T(512)(128)(4,1)}, pred[16]{0:T(512)(128)(4,1)S(1)}, u32[]{:S(2)}) copy-start(pred[16]{0:T(512)(128)(4,1)S(1)} %get-tuple-element.53) | copy-start | bytes 52
  31.2 3.7 %collective-permute-start.5 = (f32[20,128]{1,0:T(8,128)S(1)}, f32[20,128]{1,0:T(8,128)S(1)}, u32[]{:S(2)}, u32[]{:S(2)}) collective-permute-start(f32[20,128]{1,0:T(8,128)S(1)} %reshape_squeeze.42), channel_id=1, source_target_pairs={{0,7},{1,0},{2,1},{3,2},{4,3},{5,4},{6,5},{7,6},{8,15},{9,8},{10,9... | collective-permute-start | bytes 30728 | tf_op jit(solution)/shard_map/ppermute | solution.py:25
  31.3 6.4 %collective-permute-start.4 = (f32[20,128]{1,0:T(8,128)S(1)}, f32[20,128]{1,0:T(8,128)S(1)}, u32[]{:S(2)}, u32[]{:S(2)}) collective-permute-start(f32[20,128]{1,0:T(8,128)S(1)} %reshape_squeeze.41), channel_id=1, source_target_pairs={{0,1},{1,2},{2,3},{3,4},{4,5},{5,6},{6,7},{7,0},{8,9},{9,10},{10,1... | collective-permute-start | bytes 30728 | tf_op jit(solution)/shard_map/ppermute | solution.py:25
  37.9 1.6 %copy-start.25 = (s32[1,32]{1,0:T(1,128)S(1)}, s32[1,32]{1,0:T(1,128)}, u32[]{:S(2)}) copy-start(s32[1,32]{1,0:T(1,128)} %param.40) | copy-start | bytes 388
  37.9 1.6 %copy-start.15 = (s32[1,32,256]{2,1,0:T(8,128)S(1)}, s32[1,32,256]{2,1,0:T(8,128)}, u32[]{:S(2)}) copy-start(s32[1,32,256]{2,1,0:T(8,128)} %param.39) | copy-start | bytes 98308
  38.9 2.6 %collective-permute-start.7 = (f32[160,128]{1,0:T(8,128)S(1)}, f32[160,128]{1,0:T(8,128)S(1)}, u32[]{:S(2)}, u32[]{:S(2)}) collective-permute-start(f32[160,128]{1,0:T(8,128)S(1)} %bitcast.155), channel_id=1, source_target_pairs={{0,24},{8,0},{16,8},{24,16},{1,25},{9,1},{17,9},{25,17},{2,26},{10... | collective-permute-start | bytes 245768 | tf_op jit(solution)/shard_map/ppermute | solution.py:23
  38.9 4.1 %collective-permute-start.6 = (f32[160,128]{1,0:T(8,128)S(1)}, f32[160,128]{1,0:T(8,128)S(1)}, u32[]{:S(2)}, u32[]{:S(2)}) collective-permute-start(f32[160,128]{1,0:T(8,128)S(1)} %bitcast.153), channel_id=1, source_target_pairs={{0,8},{8,16},{16,24},{24,0},{1,9},{9,17},{17,25},{25,1},{2,10},{10... | collective-permute-start | bytes 245768 | tf_op jit(solution)/shard_map/ppermute | solution.py:23
  40.8 24.7 %copy-start = (f32[2,40,16,128]{3,2,1,0:T(8,128)S(1)}, f32[2,40,16,128]{3,2,1,0:T(8,128)}, u32[]{:S(2)}) copy-start(f32[2,40,16,128]{3,2,1,0:T(8,128)} %param.41) | copy-start | bytes 1966084
  43.9 23.0 %copy-start.2 = (f32[160,16,128]{2,1,0:T(8,128)}, f32[160,16,128]{2,1,0:T(8,128)S(1)}, u32[]{:S(2)}) copy-start(f32[160,16,128]{2,1,0:T(8,128)S(1)} %fusion.9) | copy-start | bytes 3932164
  44.6 22.3 %copy-start.12 = (f32[16,16,1,1]{1,0,3,2:T(8,128)S(1)}, f32[16,16,1,1]{1,0,3,2:T(8,128)}, u32[]{:S(2)}) copy-start(f32[16,16,1,1]{1,0,3,2:T(8,128)} %constant.132) | copy-start | bytes 3076
  48.2 10.3 %all-to-all-start = ((f32[4,32,256]{2,0,1:T(4,128)}), f32[4,32,256]{2,0,1:T(4,128)S(1)}, u32[]{:S(2)}, u32[]{:S(2)}) async-start(f32[4,32,256]{2,0,1:T(4,128)} %bitcast.150), calls=%async_computation | async-start | bytes 262144 | tf_op jit(solution)/shard_map/all_to_all | solution.py:247
  65.6 1.7 %copy-start.9 = (f32[128,128,1,1]{1,0,3,2:T(8,128)S(1)}, f32[128,128,1,1]{1,0,3,2:T(8,128)}, u32[]{:S(2)}) copy-start(f32[128,128,1,1]{1,0,3,2:T(8,128)} %constant.131) | copy-start | bytes 196612
  66.9 0.9 copy-start.8
  67.3 8.1 %copy-start.3 = (f32[2,40,16,128]{3,2,1,0:T(8,128)S(1)}, f32[2,40,16,128]{3,2,1,0:T(8,128)}, u32[]{:S(2)}) copy-start(f32[2,40,16,128]{3,2,1,0:T(8,128)} %param.42) | copy-start | bytes 1966084
  68.8 8.3 %collective-permute-start.11 = (f32[10,128]{1,0:T(8,128)}, f32[10,128]{1,0:T(8,128)S(1)}, u32[]{:S(2)}, u32[]{:S(2)}) collective-permute-start(f32[10,128]{1,0:T(8,128)} %reshape_squeeze.47), channel_id=1, source_target_pairs={{0,1},{1,2},{2,3},{3,4},{4,5},{5,6},{6,7},{7,0},{8,9},{9,10},{10,1... | collective-permute-start | bytes 15368 | tf_op jit(solution)/shard_map/ppermute | solution.py:25
  70.2 7.1 %collective-permute-start.10 = (f32[10,128]{1,0:T(8,128)S(1)}, f32[10,128]{1,0:T(8,128)}, u32[]{:S(2)}, u32[]{:S(2)}) collective-permute-start(f32[10,128]{1,0:T(8,128)S(1)} %reshape_squeeze.46), channel_id=1, source_target_pairs={{0,7},{1,0},{2,1},{3,2},{4,3},{5,4},{6,5},{7,6},{8,15},{9,8},{10,9... | collective-permute-start | bytes 15368 | tf_op jit(solution)/shard_map/ppermute | solution.py:25
  73.7 4.3 %collective-permute-start.9 = (f32[80,128]{1,0:T(8,128)}, f32[80,128]{1,0:T(8,128)}, u32[]{:S(2)}, u32[]{:S(2)}) collective-permute-start(f32[80,128]{1,0:T(8,128)} %bitcast.159), channel_id=1, source_target_pairs={{0,8},{8,16},{16,24},{24,0},{1,9},{9,17},{17,25},{25,1},{2,10},{10... | collective-permute-start | bytes 122888 | tf_op jit(solution)/shard_map/ppermute | solution.py:23
  73.7 4.3 %collective-permute-start.8 = (f32[80,128]{1,0:T(8,128)S(1)}, f32[80,128]{1,0:T(8,128)}, u32[]{:S(2)}, u32[]{:S(2)}) collective-permute-start(f32[80,128]{1,0:T(8,128)S(1)} %bitcast.158), channel_id=1, source_target_pairs={{0,24},{8,0},{16,8},{24,16},{1,25},{9,1},{17,9},{25,17},{2,26},{10... | collective-permute-start | bytes 122888 | tf_op jit(solution)/shard_map/ppermute | solution.py:23
  76.2 1.8 %copy-start.18 = (pred[128]{0:T(512)(128)(4,1)S(1)}, pred[128]{0:T(512)(128)(4,1)}, u32[]{:S(2)}) copy-start(pred[128]{0:T(512)(128)(4,1)} %copy-done.17) | copy-start | bytes 388
  76.2 1.8 %copy-start.20 = (pred[128]{0:T(512)(128)(4,1)S(1)}, pred[128]{0:T(512)(128)(4,1)}, u32[]{:S(2)}) copy-start(pred[128]{0:T(512)(128)(4,1)} %copy-done.19) | copy-start | bytes 388
  76.2 1.8 %copy-start.22 = (pred[16]{0:T(512)(128)(4,1)S(1)}, pred[16]{0:T(512)(128)(4,1)}, u32[]{:S(2)}) copy-start(pred[16]{0:T(512)(128)(4,1)} %copy-done.21) | copy-start | bytes 52
  76.2 1.8 %copy-start.24 = (pred[16]{0:T(512)(128)(4,1)S(1)}, pred[16]{0:T(512)(128)(4,1)}, u32[]{:S(2)}) copy-start(pred[16]{0:T(512)(128)(4,1)} %copy-done.23) | copy-start | bytes 52
  80.8 9.0 %copy-start.4 = (f32[40,16,128]{2,1,0:T(8,128)S(1)}, f32[40,16,128]{2,1,0:T(8,128)}, u32[]{:S(2)}) copy-start(f32[40,16,128]{2,1,0:T(8,128)} %get-tuple-element.44) | copy-start | bytes 983044
  80.8 9.0 %copy-start.5 = (f32[40,16,128]{2,1,0:T(8,128)S(1)}, f32[40,16,128]{2,1,0:T(8,128)}, u32[]{:S(2)}) copy-start(f32[40,16,128]{2,1,0:T(8,128)} %get-tuple-element.45) | copy-start | bytes 983044
  81.6 7.0 %collective-permute-start.15 = (f32[10,128]{1,0:T(8,128)S(1)}, f32[10,128]{1,0:T(8,128)S(1)}, u32[]{:S(2)}, u32[]{:S(2)}) collective-permute-start(f32[10,128]{1,0:T(8,128)S(1)} %reshape_squeeze.51), channel_id=1, source_target_pairs={{0,1},{1,2},{2,3},{3,4},{4,5},{5,6},{6,7},{7,0},{8,9},{9,10},{10,1... | collective-permute-start | bytes 15368 | tf_op jit(solution)/shard_map/ppermute | solution.py:25
  81.7 7.0 %collective-permute-start.14 = (f32[10,128]{1,0:T(8,128)S(1)}, f32[10,128]{1,0:T(8,128)S(1)}, u32[]{:S(2)}, u32[]{:S(2)}) collective-permute-start(f32[10,128]{1,0:T(8,128)S(1)} %reshape_squeeze.50), channel_id=1, source_target_pairs={{0,7},{1,0},{2,1},{3,2},{4,3},{5,4},{6,5},{7,6},{8,15},{9,8},{10,9... | collective-permute-start | bytes 15368 | tf_op jit(solution)/shard_map/ppermute | solution.py:25
  86.4 3.4 %collective-permute-start.13 = (f32[80,128]{1,0:T(8,128)S(1)}, f32[80,128]{1,0:T(8,128)S(1)}, u32[]{:S(2)}, u32[]{:S(2)}) collective-permute-start(f32[80,128]{1,0:T(8,128)S(1)} %bitcast.161), channel_id=1, source_target_pairs={{0,8},{8,16},{16,24},{24,0},{1,9},{9,17},{17,25},{25,1},{2,10},{10... | collective-permute-start | bytes 122888 | tf_op jit(solution)/shard_map/ppermute | solution.py:23
  86.4 3.4 %collective-permute-start.12 = (f32[80,128]{1,0:T(8,128)S(1)}, f32[80,128]{1,0:T(8,128)S(1)}, u32[]{:S(2)}, u32[]{:S(2)}) collective-permute-start(f32[80,128]{1,0:T(8,128)S(1)} %bitcast.160), channel_id=1, source_target_pairs={{0,24},{8,0},{16,8},{24,16},{1,25},{9,1},{17,9},{25,17},{2,26},{10... | collective-permute-start | bytes 122888 | tf_op jit(solution)/shard_map/ppermute | solution.py:23

commit v19 on v15

--- a/solution.py
+++ b/solution.py
@@ -97,14 +97,16 @@
     return state_in - visc_coef * total * inv_mass
 
 
-def tracer_step(tracers, velocity):
+def tracer_step(tracers, velocity, edges=None):
     xsize, ysize = tracers.shape[-2], tracers.shape[-1]
     last_x, last_y = xsize - 1, ysize - 1
     precision = lax.Precision.HIGH
-    from_up = exchange(tracers[..., last_x, :], 1, 0)[..., None, :]
-    from_down = exchange(tracers[..., 0, :], -1, 0)[..., None, :]
-    from_left = exchange(tracers[..., last_y], 0, 1)[..., None]
-    from_right = exchange(tracers[..., 0], 0, -1)[..., None]
+    if edges is None:
+        edges = (tracers[..., last_x, :], tracers[..., 0, :], tracers[..., last_y], tracers[..., 0])
+    from_up = exchange(edges[0], 1, 0)[..., None, :]
+    from_down = exchange(edges[1], -1, 0)[..., None, :]
+    from_left = exchange(edges[2], 0, 1)[..., None]
+    from_right = exchange(edges[3], 0, -1)[..., None]
     above_x = np.eye(xsize, k=1)
     above_y = np.eye(ysize, k=1)
     sum_x = jnp.asarray(above_x + above_x.T, jnp.float32)
@@ -249,10 +251,18 @@
     ocean_flux = onehot_gather(received, remap_slots, remap_weights, source_count).reshape(fields, ocean_x, ocean_y)
     velocity = ocean_velocity.at[0, 0].add(wind_coef * jnp.tanh(ocean_flux[0]))
     velocity = velocity.at[1, 0].add(wind_coef * jnp.tanh(ocean_flux[1]))
-    tracers = ocean_tracers.at[0, 0].add(surf_coef * ocean_flux[2])
-    tracers = tracers.at[1, 0].add(surf_coef * ocean_flux[3])
+    surface = surf_coef * ocean_flux[2:]
+    tracers = ocean_tracers.at[:, 0].add(surface)
+    last_x, last_y = ocean_x - 1, ocean_y - 1
+    edges = (
+        ocean_tracers[..., last_x, :].at[:, 0].add(surface[:, last_x, :]),
+        ocean_tracers[..., 0, :].at[:, 0].add(surface[:, 0, :]),
+        ocean_tracers[..., last_y].at[:, 0].add(surface[:, :, last_y]),
+        ocean_tracers[..., 0].at[:, 0].add(surface[:, :, 0]),
+    )
     for repeat in range(OSTEPS):
-        tracers = tracer_step(tracers, velocity)
+        tracers = tracer_step(tracers, velocity, edges)
+        edges = None
     return (atm_out, tracers)
 
 

time: 90.5 us -> 91.7 us (1.013)
  blocking collectives: 14.6 us -> 0 us
  starting transfers between devices: 19.8 us -> 26.6 us
  waiting for transfers between devices: 15.7 us -> 19.3 us
  local copies, waits for them, and re-layouts: 10.7 us -> 13.3 us
  other arithmetic: 4.39 us -> 6.87 us
    all_to_all x1 -> x0, blocking collectives: 14.6 us -> none  [per_device(): lax.all_to_all(payload, ('gx', 'gy'), split_axis=1, concat_axis=1, tiled=...]
    all_to_all x0 -> x1, waiting for transfers between devices: none -> 6.85 us  [per_device(): lax.all_to_all(payload, ('gx', 'gy'), split_axis=1, concat_axis=1, tiled=...]
    all_to_all x0 -> x1, starting transfers between devices: none -> 6.74 us  [per_device(): lax.all_to_all(payload, ('gx', 'gy'), split_axis=1, concat_axis=1, tiled=...]
    ppermute x8, waiting for transfers between devices: 12.4 us -> 9.09 us  [neighbour(): lax.ppermute(values, 'gy', [(j, (j + step_y) % count_y) for j in range(co...]
    unnamed x58 -> x64, local copies, waits for them, and re-layouts: 3.05 us -> 6.23 us
    slice x4 -> x5, local copies, waits for them, and re-layouts: 1.93 us -> 2.05 us  [the longest x1 1.26 us: per_device(): ocean_tracers[..., 0].at[:, 0].add(surface[:, :, 0])]
  transfers between devices with their start and end apart: 16 -> 17, of which waited for: 10 -> 9; matrix products, arithmetic and copies ran while one was open for 5% -> 9% of each run, Pallas kernels for 0% -> 0%
where the time goes in v19:
time: 91.7 us; the launch traced here: 90.8 us
  starting transfers between devices  26.6 us (29%)
  waiting for transfers between devices  19.3 us (21%)
  matrix products  15.1 us (16%)
  local copies, waits for them, and re-layouts  13.3 us (15%)
  Pallas kernels  8.25 us (9%)
  other arithmetic  6.87 us (7%)
  between operations  1.33 us (1%)
    ppermute x8, starting transfers between devices, neighbour(): lax.ppermute(values, 'gy', [(j, (j + step_y) % count_y) for j in range(co...  15.1 us
    ppermute x8, waiting for transfers between devices, neighbour(): lax.ppermute(values, 'gy', [(j, (j + step_y) % count_y) for j in range(co...  9.09 us
    pallas_call x2, Pallas kernels, onehot_gather(): pl.pallas_call(gather_kernel, grid=(blocks, groups), in_specs=[pl.BlockSp...  8.25 us
    all_to_all x1, waiting for transfers between devices, per_device(): lax.all_to_all(payload, ('gx', 'gy'), split_axis=1, concat_axis=1, tiled=...  6.85 us
    all_to_all x1, starting transfers between devices, per_device(): lax.all_to_all(payload, ('gx', 'gy'), split_axis=1, concat_axis=1, tiled=...  6.74 us
    unnamed x64, local copies, waits for them, and re-layouts  6.23 us
    ppermute x8, starting transfers between devices, neighbour(): lax.ppermute(values, 'gx', [(i, (i + step_x) % count_x) for i in range(co...  4.77 us
    dot_general x2, matrix products, tracer_step(): jnp.einsum('ab,...by->...ay', sum_x, tracers, precision=precision)  4.18 us
  transfers between devices with their start and end apart: 17, of which 9 were waited for; matrix products, arithmetic and copies ran while one was open for 9% of the time, Pallas kernels for 0%

profile of v19, /device:TPU:0, one launch (start us, length us, event | category | flops | bytes accessed | tf_op | source)
XLA Modules:
  0.0 90.8 jit_solution(15861446608719995856)
XLA Ops:
  0.7 1.2 %copy.128 = f32[2,40,16,128]{3,2,1,0:T(8,128)S(1)} copy(f32[2,40,16,128]{3,2,1,0:T(8,128)} %param.51) | data formatting | bytes 1310720
  2.2 0.6 fusion.10
  2.9 0.7 convolution_bitcast_fusion.5
  3.7 0.7 fusion.56
  4.6 0.7 fusion.2
  5.4 0.7 fusion.1
  6.1 1.1 %slice_reduce_fusion.3 = (f32[160,16]{1,0:T(8,128)S(1)}, f32[160,16]{1,0:T(8,128)S(1)}) fusion(f32[160,16,128]{2,1,0:T(8,128)S(1)} %fusion.1), kind=kLoop, calls=%fused_computation.24 | loop fusion | bytes 40960 | tf_op jit(solution)/shard_map/slice | solution.py:87
  7.3 3.0 %collective-permute-start = (f32[20,128]{1,0:T(8,128)S(1)}, f32[20,128]{1,0:T(8,128)S(1)}, u32[]{:S(2)}, u32[]{:S(2)}) collective-permute-start(f32[20,128]{1,0:T(8,128)S(1)} %reshape_squeeze.27), channel_id=1, source_target_pairs={{0,1},{1,2},{2,3},{3,4},{4,5},{5,6},{6,7},{7,0},{8,9},{9,10},{10,1... | collective-permute-start | bytes 30728 | tf_op jit(solution)/shard_map/ppermute | solution.py:25
  10.4 3.1 %collective-permute-start.1 = (f32[20,128]{1,0:T(8,128)S(1)}, f32[20,128]{1,0:T(8,128)S(1)}, u32[]{:S(2)}, u32[]{:S(2)}) collective-permute-start(f32[20,128]{1,0:T(8,128)S(1)} %reshape_squeeze.28), channel_id=1, source_target_pairs={{0,7},{1,0},{2,1},{3,2},{4,3},{5,4},{6,5},{7,6},{8,15},{9,8},{10,9... | collective-permute-start | bytes 30728 | tf_op jit(solution)/shard_map/ppermute | solution.py:25
  13.5 1.3 %fusion.54 = (f32[2,40,16,1]{3,2,1,0:T(8,128)}, f32[2,40,16,1]{3,2,1,0:T(8,128)}) fusion(f32[2,40,16,128]{3,2,1,0:T(8,128)S(1)} %copy.128), kind=kLoop, calls=%fused_computation.110 | loop fusion | bytes 20480 | tf_op jit(solution)/shard_map/slice | solution.py:261
  15.5 1.5 %select_add_fusion.1 = f32[160,16,128]{2,1,0:T(8,128)S(1)} fusion(f32[160,16,128]{2,1,0:T(8,128)S(1)} %fusion.1, f32[160,16]{1,0:T(8,128)S(1)} %broadcast_in_dim.244, f32[160,16]{1,0:T(8,128)S(1)} %broadcast_in_dim.241, pred[128]{0:T(512)(128)(4,1)} %get-tuple-element.120, pred[128]{0:T(512)(128)(4,1)} %get-tuple-element.121), kind=kLoop, calls=%fused_computation.26 | loop fusion | flops 983040 | bytes 2642176 | tf_op jit(solution)/shard_map/add | solution.py:90
  17.2 1.7 %collective-permute-start.3 = (f32[160,128]{1,0:T(8,128)S(1)}, f32[160,128]{1,0:T(8,128)S(1)}, u32[]{:S(2)}, u32[]{:S(2)}) collective-permute-start(f32[160,128]{1,0:T(8,128)S(1)} %bitcast.189), channel_id=1, source_target_pairs={{0,24},{8,0},{16,8},{24,16},{1,25},{9,1},{17,9},{25,17},{2,26},{10... | collective-permute-start | bytes 245768 | tf_op jit(solution)/shard_map/ppermute | solution.py:23
  18.9 2.1 %collective-permute-done.2 = f32[160,128]{1,0:T(8,128)S(1)} collective-permute-done((f32[160,128]{1,0:T(8,128)S(1)}, f32[160,128]{1,0:T(8,128)S(1)}, u32[]{:S(2)}, u32[]{:S(2)}) %collective-permute-start.2) | collective-permute-done | bytes 81952 | tf_op jit(solution)/shard_map/ppermute | solution.py:23
  21.1 0.8 fusion.5
  22.0 0.7 fusion.6
  22.8 0.7 convolution_multiply_fusion.1
  23.5 0.7 convolution_bitcast_fusion.2
  24.4 0.7 fusion.57
  25.1 0.7 fusion
  25.8 1.1 %slice_reduce_fusion.1 = (f32[160,16]{1,0:T(8,128)S(1)}, f32[160,16]{1,0:T(8,128)S(1)}) fusion(f32[160,16,128]{2,1,0:T(8,128)S(1)} %fusion), kind=kLoop, calls=%fused_computation.22 | loop fusion | bytes 40960 | tf_op jit(solution)/shard_map/slice | solution.py:87
  26.9 1.2 %collective-permute-start.4 = (f32[20,128]{1,0:T(8,128)S(1)}, f32[20,128]{1,0:T(8,128)S(1)}, u32[]{:S(2)}, u32[]{:S(2)}) collective-permute-start(f32[20,128]{1,0:T(8,128)S(1)} %reshape_squeeze.29), channel_id=1, source_target_pairs={{0,1},{1,2},{2,3},{3,4},{4,5},{5,6},{6,7},{7,0},{8,9},{9,10},{10,1... | collective-permute-start | bytes 30728 | tf_op jit(solution)/shard_map/ppermute | solution.py:25
  28.2 3.7 %collective-permute-start.5 = (f32[20,128]{1,0:T(8,128)S(1)}, f32[20,128]{1,0:T(8,128)S(1)}, u32[]{:S(2)}, u32[]{:S(2)}) collective-permute-start(f32[20,128]{1,0:T(8,128)S(1)} %reshape_squeeze.30), channel_id=1, source_target_pairs={{0,7},{1,0},{2,1},{3,2},{4,3},{5,4},{6,5},{7,6},{8,15},{9,8},{10,9... | collective-permute-start | bytes 30728 | tf_op jit(solution)/shard_map/ppermute | solution.py:25
  31.9 0.7 convert_bitcast_fusion
  32.6 0.8 collective-permute-done.4
  33.6 0.8 select_add_fusion
  34.6 0.7 collective-permute-start.6
  35.3 1.1 %collective-permute-start.7 = (f32[160,128]{1,0:T(8,128)S(1)}, f32[160,128]{1,0:T(8,128)S(1)}, u32[]{:S(2)}, u32[]{:S(2)}) collective-permute-start(f32[160,128]{1,0:T(8,128)S(1)} %bitcast.188), channel_id=1, source_target_pairs={{0,24},{8,0},{16,8},{24,16},{1,25},{9,1},{17,9},{25,17},{2,26},{10... | collective-permute-start | bytes 245768 | tf_op jit(solution)/shard_map/ppermute | solution.py:23
  36.4 0.7 copy.113
  37.1 0.6 copy.112
  37.7 0.8 collective-permute-done.6
  38.8 0.8 fusion.9
  39.7 1.0 %copy-done.4 = f32[160,16,128]{2,1,0:T(8,128)} copy-done((f32[160,16,128]{2,1,0:T(8,128)}, f32[160,16,128]{2,1,0:T(8,128)S(1)}, u32[]{:S(2)}) %copy-start.4) | copy-done | bytes 1310744
  40.7 0.6 fusion.37.table_ref
  41.3 3.6 %shard_map.320 = f32[4,8192]{1,0:T(4,128)} custom-call(s32[1,8192]{1,0:T(1,128)} %bitcast.187, f32[1,8192]{1,0:T(1,128)} %bitcast.186, f32[4,16,128]{2,1,0:T(8,128)} %fusion.37.table_ref), custom_call_target="tpu_custom_call" | custom-call | tf_op jit(solution)/shard_map/pallas_call | solution.py:209
  44.9 6.7 %all-to-all-start = ((f32[4,32,256]{2,0,1:T(4,128)}), f32[4,32,256]{2,0,1:T(4,128)S(1)}, u32[]{:S(2)}, u32[]{:S(2)}) async-start(f32[4,32,256]{2,0,1:T(4,128)} %bitcast.184), calls=%async_computation | async-start | bytes 262144 | tf_op jit(solution)/shard_map/all_to_all | solution.py:249
  52.6 6.8 %all-to-all-done = f32[4,32,256]{2,0,1:T(4,128)S(1)} async-done(((f32[4,32,256]{2,0,1:T(4,128)}), f32[4,32,256]{2,0,1:T(4,128)S(1)}, u32[]{:S(2)}, u32[]{:S(2)}) %all-to-all-start) | async-done | bytes 131104 | tf_op jit(solution)/shard_map/all_to_all | solution.py:249
  59.4 0.7 copy.85.table_ref
  60.1 4.7 %shard_map.321 = f32[4,2048]{1,0:T(4,128)} custom-call(s32[1,8192]{1,0:T(1,128)} %bitcast.200, f32[1,8192]{1,0:T(1,128)} %bitcast.201, f32[4,32,256]{2,1,0:T(8,128)} %copy.85.table_ref), custom_call_target="tpu_custom_call" | custom-call | tf_op jit(solution)/shard_map/pallas_call | solution.py:209
  64.8 0.9 fusion.42
  65.6 0.8 fusion.40
  66.9 2.1 %collective-permute-start.10 = (f32[10,128]{1,0:T(8,128)S(1)}, f32[10,128]{1,0:T(8,128)S(1)}, u32[]{:S(2)}, u32[]{:S(2)}) collective-permute-start(f32[10,128]{1,0:T(8,128)S(1)} %reshape.457), channel_id=1, source_target_pairs={{0,7},{1,0},{2,1},{3,2},{4,3},{5,4},{6,5},{7,6},{8,15},{9,8},{10,9... | collective-permute-start | bytes 15368 | tf_op jit(solution)/shard_map/ppermute | solution.py:25
  71.6 0.9 fusion.36
  72.6 3.1 %collective-permute-done.11 = f32[10,128]{1,0:T(8,128)S(1)} collective-permute-done((f32[10,128]{1,0:T(8,128)S(1)}, f32[10,128]{1,0:T(8,128)S(1)}, u32[]{:S(2)}, u32[]{:S(2)}) %collective-permute-start.11) | collective-permute-done | bytes 5152 | tf_op jit(solution)/shard_map/ppermute | solution.py:25
  76.4 1.8 %fusion.17 = f32[2,40,16,128]{3,2,1,0:T(8,128)S(1)} fusion(f32[2,40,16,128]{3,2,1,0:T(8,128)S(1)} %fusion.39, f32[2,40,16,128]{3,2,1,0:T(8,128)S(1)} %convolution_bitcast_fusion.8, f32[2,40,16,128]{3,2,1,0:T(8,128)S(1)} %fusion.58, f32[2,40,16,128]{3,2,1,0:T(8,128)S(1)} %fusion.59, f32[40,16,128]{2,1,0:T(8,128)} %get-tuple-element.109, ...), kind=kOutput, calls=%fused_computation.45 | convolution fusion | flops 19169280 | bytes 4025632 | tf_op jit(solution)/shard_map/ab,...by->...ay/dot_general | solution.py:122
  79.1 0.6 slice_reduce_fusion.5
  79.9 1.9 %collective-permute-start.14 = (f32[10,128]{1,0:T(8,128)S(1)}, f32[10,128]{1,0:T(8,128)S(1)}, u32[]{:S(2)}, u32[]{:S(2)}) collective-permute-start(f32[10,128]{1,0:T(8,128)S(1)} %reshape_squeeze.34), channel_id=1, source_target_pairs={{0,7},{1,0},{2,1},{3,2},{4,3},{5,4},{6,5},{7,6},{8,15},{9,8},{10,9... | collective-permute-start | bytes 15368 | tf_op jit(solution)/shard_map/ppermute | solution.py:25
  83.6 4.6 %collective-permute-done.15 = f32[10,128]{1,0:T(8,128)S(1)} collective-permute-done((f32[10,128]{1,0:T(8,128)S(1)}, f32[10,128]{1,0:T(8,128)S(1)}, u32[]{:S(2)}, u32[]{:S(2)}) %collective-permute-start.15) | collective-permute-done | bytes 5152 | tf_op jit(solution)/shard_map/ppermute | solution.py:25
  88.4 2.4 %fusion.29 = f32[2,40,16,128]{3,2,1,0:T(8,128)} fusion(f32[2,40,16,128]{3,2,1,0:T(8,128)S(1)} %fusion.17, f32[2,40,16,128]{3,2,1,0:T(8,128)S(1)} %convolution_bitcast_fusion.6, f32[2,40,16,128]{3,2,1,0:T(8,128)S(1)} %fusion.60, f32[2,40,16,128]{3,2,1,0:T(8,128)S(1)} %fusion.61, f32[2,40,16]{2,1,0:T(8,128)S(1)} %broadcast_in_dim.276, ...), kind=kOutput, calls=%fused_computation.57 | convolution fusion | flops 19169280 | bytes 4025632 | tf_op jit(solution)/shard_map/ab,...by->...ay/dot_general | solution.py:122
  (125 shorter events, 10.5 us)
Async XLA Ops:
  0.6 1.3 %copy-start.20 = (f32[16]{0:T(128)S(1)}, f32[16]{0:T(128)}, u32[]{:S(2)}) copy-start(f32[16]{0:T(128)} %constant.236) | copy-start | bytes 196
  0.6 1.2 %copy-start.24 = (f32[128]{0:T(128)S(1)}, f32[128]{0:T(128)}, u32[]{:S(2)}) copy-start(f32[128]{0:T(128)} %constant.237) | copy-start | bytes 1540
  0.7 1.3 %copy-start.14 = (f32[16,16,1]{1,0,2:T(8,128)S(1)}, f32[16,16,1]{1,0,2:T(8,128)}, u32[]{:S(2)}) copy-start(f32[16,16,1]{1,0,2:T(8,128)} %constant.239) | copy-start | bytes 3076
  0.7 1.5 %copy-start = (f32[4,40,16,128]{3,2,1,0:T(8,128)S(1)}, f32[4,40,16,128]{3,2,1,0:T(8,128)}, u32[]{:S(2)}) copy-start(f32[4,40,16,128]{3,2,1,0:T(8,128)} %param.47) | copy-start | bytes 3932164
  0.7 1.2 %copy-start.19 = (f32[2,16,128]{2,1,0:T(8,128)S(1)}, f32[2,16,128]{2,1,0:T(8,128)}, u32[]{:S(2)}) copy-start(f32[2,16,128]{2,1,0:T(8,128)} %param.48) | copy-start | bytes 49156
  2.9 0.8 copy-start.12
  3.7 0.8 copy-start.8
  4.6 0.8 copy-start.7
  7.3 8.0 %collective-permute-start = (f32[20,128]{1,0:T(8,128)S(1)}, f32[20,128]{1,0:T(8,128)S(1)}, u32[]{:S(2)}, u32[]{:S(2)}) collective-permute-start(f32[20,128]{1,0:T(8,128)S(1)} %reshape_squeeze.27), channel_id=1, source_target_pairs={{0,1},{1,2},{2,3},{3,4},{4,5},{5,6},{6,7},{7,0},{8,9},{9,10},{10,1... | collective-permute-start | bytes 30728 | tf_op jit(solution)/shard_map/ppermute | solution.py:25
  10.4 5.0 %collective-permute-start.1 = (f32[20,128]{1,0:T(8,128)S(1)}, f32[20,128]{1,0:T(8,128)S(1)}, u32[]{:S(2)}, u32[]{:S(2)}) collective-permute-start(f32[20,128]{1,0:T(8,128)S(1)} %reshape_squeeze.28), channel_id=1, source_target_pairs={{0,7},{1,0},{2,1},{3,2},{4,3},{5,4},{6,5},{7,6},{8,15},{9,8},{10,9... | collective-permute-start | bytes 30728 | tf_op jit(solution)/shard_map/ppermute | solution.py:25
  15.4 5.7 %copy-start.16 = (f32[16,128]{1,0:T(8,128)S(1)}, f32[16,128]{1,0:T(8,128)}, u32[]{:S(2)}) copy-start(f32[16,128]{1,0:T(8,128)} %constant.238) | copy-start | bytes 24580
  15.5 5.7 %copy-start.17 = (f32[16,16,1]{1,0,2:T(8,128)S(1)}, f32[16,16,1]{1,0,2:T(8,128)}, u32[]{:S(2)}) copy-start(f32[16,16,1]{1,0,2:T(8,128)} %constant.243) | copy-start | bytes 3076
  17.1 3.9 %collective-permute-start.2 = (f32[160,128]{1,0:T(8,128)S(1)}, f32[160,128]{1,0:T(8,128)S(1)}, u32[]{:S(2)}, u32[]{:S(2)}) collective-permute-start(f32[160,128]{1,0:T(8,128)S(1)} %bitcast.191), channel_id=1, source_target_pairs={{0,8},{8,16},{16,24},{24,0},{1,9},{9,17},{17,25},{25,1},{2,10},{10... | collective-permute-start | bytes 245768 | tf_op jit(solution)/shard_map/ppermute | solution.py:23
  17.2 3.9 %collective-permute-start.3 = (f32[160,128]{1,0:T(8,128)S(1)}, f32[160,128]{1,0:T(8,128)S(1)}, u32[]{:S(2)}, u32[]{:S(2)}) collective-permute-start(f32[160,128]{1,0:T(8,128)S(1)} %bitcast.189), channel_id=1, source_target_pairs={{0,24},{8,0},{16,8},{24,16},{1,25},{9,1},{17,9},{25,17},{2,26},{10... | collective-permute-start | bytes 245768 | tf_op jit(solution)/shard_map/ppermute | solution.py:23
  22.0 0.8 copy-start.9
  23.5 0.8 copy-start.13
  24.4 0.7 copy-start.21
  25.7 7.9 %copy-start.22 = (pred[128]{0:T(512)(128)(4,1)S(1)}, pred[128]{0:T(512)(128)(4,1)}, u32[]{:S(2)}) copy-start(pred[128]{0:T(512)(128)(4,1)} %get-tuple-element.120) | copy-start | bytes 388
  25.7 7.9 %copy-start.23 = (pred[128]{0:T(512)(128)(4,1)S(1)}, pred[128]{0:T(512)(128)(4,1)}, u32[]{:S(2)}) copy-start(pred[128]{0:T(512)(128)(4,1)} %get-tuple-element.121) | copy-start | bytes 388
  26.9 6.4 %collective-permute-start.4 = (f32[20,128]{1,0:T(8,128)S(1)}, f32[20,128]{1,0:T(8,128)S(1)}, u32[]{:S(2)}, u32[]{:S(2)}) collective-permute-start(f32[20,128]{1,0:T(8,128)S(1)} %reshape_squeeze.29), channel_id=1, source_target_pairs={{0,1},{1,2},{2,3},{3,4},{4,5},{5,6},{6,7},{7,0},{8,9},{9,10},{10,1... | collective-permute-start | bytes 30728 | tf_op jit(solution)/shard_map/ppermute | solution.py:25
  28.2 5.3 %collective-permute-start.5 = (f32[20,128]{1,0:T(8,128)S(1)}, f32[20,128]{1,0:T(8,128)S(1)}, u32[]{:S(2)}, u32[]{:S(2)}) collective-permute-start(f32[20,128]{1,0:T(8,128)S(1)} %reshape_squeeze.30), channel_id=1, source_target_pairs={{0,7},{1,0},{2,1},{3,2},{4,3},{5,4},{6,5},{7,6},{8,15},{9,8},{10,9... | collective-permute-start | bytes 30728 | tf_op jit(solution)/shard_map/ppermute | solution.py:25
  33.6 3.4 %copy-start.18 = (s32[1,32,256]{2,1,0:T(8,128)S(1)}, s32[1,32,256]{2,1,0:T(8,128)}, u32[]{:S(2)}) copy-start(s32[1,32,256]{2,1,0:T(8,128)} %param.49) | copy-start | bytes 98308
  34.6 3.9 %collective-permute-start.6 = (f32[160,128]{1,0:T(8,128)S(1)}, f32[160,128]{1,0:T(8,128)S(1)}, u32[]{:S(2)}, u32[]{:S(2)}) collective-permute-start(f32[160,128]{1,0:T(8,128)S(1)} %bitcast.190), channel_id=1, source_target_pairs={{0,8},{8,16},{16,24},{24,0},{1,9},{9,17},{17,25},{25,1},{2,10},{10... | collective-permute-start | bytes 245768 | tf_op jit(solution)/shard_map/ppermute | solution.py:23
  35.3 3.6 %collective-permute-start.7 = (f32[160,128]{1,0:T(8,128)S(1)}, f32[160,128]{1,0:T(8,128)S(1)}, u32[]{:S(2)}, u32[]{:S(2)}) collective-permute-start(f32[160,128]{1,0:T(8,128)S(1)} %bitcast.188), channel_id=1, source_target_pairs={{0,24},{8,0},{16,8},{24,16},{1,25},{9,1},{17,9},{25,17},{2,26},{10... | collective-permute-start | bytes 245768 | tf_op jit(solution)/shard_map/ppermute | solution.py:23
  37.7 14.1 %copy-start.3 = (f32[2,40,16,1]{3,2,1,0:T(8,128)S(1)}, f32[2,40,16,1]{3,2,1,0:T(8,128)}, u32[]{:S(2)}) copy-start(f32[2,40,16,1]{3,2,1,0:T(8,128)} %get-tuple-element.106) | copy-start | bytes 15364
  39.7 1.1 %copy-start.4 = (f32[160,16,128]{2,1,0:T(8,128)}, f32[160,16,128]{2,1,0:T(8,128)S(1)}, u32[]{:S(2)}) copy-start(f32[160,16,128]{2,1,0:T(8,128)S(1)} %fusion.9) | copy-start | bytes 3932164
  39.7 12.5 %copy-start.2 = (f32[2,40,16,1]{3,2,1,0:T(8,128)S(1)}, f32[2,40,16,1]{3,2,1,0:T(8,128)}, u32[]{:S(2)}) copy-start(f32[2,40,16,1]{3,2,1,0:T(8,128)} %get-tuple-element.107) | copy-start | bytes 15364
  44.9 14.5 %all-to-all-start = ((f32[4,32,256]{2,0,1:T(4,128)}), f32[4,32,256]{2,0,1:T(4,128)S(1)}, u32[]{:S(2)}, u32[]{:S(2)}) async-start(f32[4,32,256]{2,0,1:T(4,128)} %bitcast.184), calls=%async_computation | async-start | bytes 262144 | tf_op jit(solution)/shard_map/all_to_all | solution.py:249
  51.8 18.3 %copy-start.15 = (f32[16,16,1,1]{1,0,3,2:T(8,128)S(1)}, f32[16,16,1,1]{1,0,3,2:T(8,128)}, u32[]{:S(2)}) copy-start(f32[16,16,1,1]{1,0,3,2:T(8,128)} %constant.246) | copy-start | bytes 3076
  52.5 18.0 %copy-start.11 = (f32[128,128,1,1]{1,0,3,2:T(8,128)S(1)}, f32[128,128,1,1]{1,0,3,2:T(8,128)}, u32[]{:S(2)}) copy-start(f32[128,128,1,1]{1,0,3,2:T(8,128)} %constant.245) | copy-start | bytes 196612
  66.9 5.6 %collective-permute-start.10 = (f32[10,128]{1,0:T(8,128)S(1)}, f32[10,128]{1,0:T(8,128)S(1)}, u32[]{:S(2)}, u32[]{:S(2)}) collective-permute-start(f32[10,128]{1,0:T(8,128)S(1)} %reshape.457), channel_id=1, source_target_pairs={{0,7},{1,0},{2,1},{3,2},{4,3},{5,4},{6,5},{7,6},{8,15},{9,8},{10,9... | collective-permute-start | bytes 15368 | tf_op jit(solution)/shard_map/ppermute | solution.py:25
  69.3 6.4 %collective-permute-start.11 = (f32[10,128]{1,0:T(8,128)S(1)}, f32[10,128]{1,0:T(8,128)S(1)}, u32[]{:S(2)}, u32[]{:S(2)}) collective-permute-start(f32[10,128]{1,0:T(8,128)S(1)} %reshape.460), channel_id=1, source_target_pairs={{0,1},{1,2},{2,3},{3,4},{4,5},{5,6},{6,7},{7,0},{8,9},{9,10},{10,1... | collective-permute-start | bytes 15368 | tf_op jit(solution)/shard_map/ppermute | solution.py:25
  69.4 6.4 %collective-permute-start.8 = (f32[80,128]{1,0:T(8,128)S(1)}, f32[80,128]{1,0:T(8,128)S(1)}, u32[]{:S(2)}, u32[]{:S(2)}) collective-permute-start(f32[80,128]{1,0:T(8,128)S(1)} %bitcast.197), channel_id=1, source_target_pairs={{0,24},{8,0},{16,8},{24,16},{1,25},{9,1},{17,9},{25,17},{2,26},{10... | collective-permute-start | bytes 122888 | tf_op jit(solution)/shard_map/ppermute | solution.py:23
  69.5 1.4 %copy-start.10 = (f32[128,128,1,1]{1,0,3,2:T(8,128)S(1)}, f32[128,128,1,1]{1,0,3,2:T(8,128)}, u32[]{:S(2)}) copy-start(f32[128,128,1,1]{1,0,3,2:T(8,128)} %constant.247) | copy-start | bytes 196612
  69.5 6.3 %collective-permute-start.9 = (f32[80,128]{1,0:T(8,128)S(1)}, f32[80,128]{1,0:T(8,128)S(1)}, u32[]{:S(2)}, u32[]{:S(2)}) collective-permute-start(f32[80,128]{1,0:T(8,128)S(1)} %bitcast.195), channel_id=1, source_target_pairs={{0,8},{8,16},{16,24},{24,0},{1,9},{9,17},{17,25},{25,1},{2,10},{10... | collective-permute-start | bytes 122888 | tf_op jit(solution)/shard_map/ppermute | solution.py:23
  70.5 1.1 %copy-start.1 = (f32[2,40,16,128]{3,2,1,0:T(8,128)S(1)}, f32[2,40,16,128]{3,2,1,0:T(8,128)}, u32[]{:S(2)}) copy-start(f32[2,40,16,128]{3,2,1,0:T(8,128)} %param.52) | copy-start | bytes 1966084
  70.9 5.5 %copy-start.27 = (f32[16,16,1,1]{1,0,3,2:T(8,128)S(1)}, f32[16,16,1,1]{1,0,3,2:T(8,128)}, u32[]{:S(2)}) copy-start(f32[16,16,1,1]{1,0,3,2:T(8,128)} %constant.244) | copy-start | bytes 3076
  75.8 0.6 copy-start.25
  75.8 0.6 copy-start.26
  79.1 9.3 %copy-start.5 = (f32[40,16,128]{2,1,0:T(8,128)S(1)}, f32[40,16,128]{2,1,0:T(8,128)}, u32[]{:S(2)}) copy-start(f32[40,16,128]{2,1,0:T(8,128)} %get-tuple-element.108) | copy-start | bytes 983044
  79.1 9.3 %copy-start.6 = (f32[40,16,128]{2,1,0:T(8,128)S(1)}, f32[40,16,128]{2,1,0:T(8,128)}, u32[]{:S(2)}) copy-start(f32[40,16,128]{2,1,0:T(8,128)} %get-tuple-element.109) | copy-start | bytes 983044
  79.9 3.7 %collective-permute-start.14 = (f32[10,128]{1,0:T(8,128)S(1)}, f32[10,128]{1,0:T(8,128)S(1)}, u32[]{:S(2)}, u32[]{:S(2)}) collective-permute-start(f32[10,128]{1,0:T(8,128)S(1)} %reshape_squeeze.34), channel_id=1, source_target_pairs={{0,7},{1,0},{2,1},{3,2},{4,3},{5,4},{6,5},{7,6},{8,15},{9,8},{10,9... | collective-permute-start | bytes 15368 | tf_op jit(solution)/shard_map/ppermute | solution.py:25
  81.9 6.4 %collective-permute-start.15 = (f32[10,128]{1,0:T(8,128)S(1)}, f32[10,128]{1,0:T(8,128)S(1)}, u32[]{:S(2)}, u32[]{:S(2)}) collective-permute-start(f32[10,128]{1,0:T(8,128)S(1)} %reshape_squeeze.35), channel_id=1, source_target_pairs={{0,1},{1,2},{2,3},{3,4},{4,5},{5,6},{6,7},{7,0},{8,9},{9,10},{10,1... | collective-permute-start | bytes 15368 | tf_op jit(solution)/shard_map/ppermute | solution.py:25
  82.0 6.3 %collective-permute-start.12 = (f32[80,128]{1,0:T(8,128)S(1)}, f32[80,128]{1,0:T(8,128)S(1)}, u32[]{:S(2)}, u32[]{:S(2)}) collective-permute-start(f32[80,128]{1,0:T(8,128)S(1)} %bitcast.199), channel_id=1, source_target_pairs={{0,24},{8,0},{16,8},{24,16},{1,25},{9,1},{17,9},{25,17},{2,26},{10... | collective-permute-start | bytes 122888 | tf_op jit(solution)/shard_map/ppermute | solution.py:23
  82.6 5.7 %collective-permute-start.13 = (f32[80,128]{1,0:T(8,128)S(1)}, f32[80,128]{1,0:T(8,128)}, u32[]{:S(2)}, u32[]{:S(2)}) collective-permute-start(f32[80,128]{1,0:T(8,128)S(1)} %bitcast.198), channel_id=1, source_target_pairs={{0,8},{8,16},{16,24},{24,0},{1,9},{9,17},{17,25},{25,1},{2,10},{10... | collective-permute-start | bytes 122888 | tf_op jit(solution)/shard_map/ppermute | solution.py:23

commit v20 on v15

--- a/solution.py
+++ b/solution.py
@@ -87,9 +87,10 @@
     from_left = exchange(merged[:, :, last_y], 0, 1)[:, :, None]
     from_right = exchange(merged[:, :, 0], 0, -1)[:, :, None]
     column = jnp.arange(ysize)
-    merged = merged + jnp.where(column == 0, from_left, jnp.where(column == last_y, from_right, 0.0))
-    from_up = exchange(merged[:, last_x, :], 1, 0)[:, None, :]
-    from_down = exchange(merged[:, 0, :], -1, 0)[:, None, :]
+    edge_add = jnp.where(column == 0, from_left, jnp.where(column == last_y, from_right, 0.0))
+    from_up = exchange(merged[:, last_x, :] + edge_add[:, last_x, :], 1, 0)[:, None, :]
+    from_down = exchange(merged[:, 0, :] + edge_add[:, 0, :], -1, 0)[:, None, :]
+    merged = merged + edge_add
     row = jnp.arange(xsize)[:, None]
     total = jnp.einsum("ab,lby->lay", pair_x, merged, precision=precision) + jnp.where(
         row == 0, from_up, jnp.where(row == last_x, from_down, 0.0)

time: 90.5 us -> 92.4 us (1.021)
  matrix products: 15.1 us -> 16.2 us
    select_n x0 -> x2, other arithmetic: none -> 1.48 us  [substep(): jnp.where(column == 0, from_left, jnp.where(column == last_y, from_right,...]
    add x2, other arithmetic: 1.69 us -> 0.35 us  [substep(): merged[:, last_x, :] + edge_add[:, last_x, :]]
    dot_general x2, matrix products: 1.65 us -> 2.81 us  [substep(): jnp.einsum('ab,lby->lay', pair_x, merged, precision=precision)]
    unnamed x58 -> x60, local copies, waits for them, and re-layouts: 3.05 us -> 3.8 us
where the time goes in v20:
time: 92.4 us; the launch traced here: 91.7 us
  starting transfers between devices  20 us (22%)
  matrix products  16.2 us (18%)
  waiting for transfers between devices  15.5 us (17%)
  blocking collectives  14.7 us (16%)
  local copies, waits for them, and re-layouts  11.2 us (12%)
  Pallas kernels  8.28 us (9%)
  other arithmetic  4.59 us (5%)
  between operations  1.27 us (1%)
    ppermute x8, starting transfers between devices, neighbour(): lax.ppermute(values, 'gy', [(j, (j + step_y) % count_y) for j in range(co...  15.3 us
    all_to_all x1, blocking collectives, per_device(): lax.all_to_all(payload, ('gx', 'gy'), split_axis=1, concat_axis=1, tiled=...  14.7 us
    ppermute x8, waiting for transfers between devices, neighbour(): lax.ppermute(values, 'gy', [(j, (j + step_y) % count_y) for j in range(co...  12.2 us
    pallas_call x2, Pallas kernels, onehot_gather(): pl.pallas_call(gather_kernel, grid=(blocks, groups), in_specs=[pl.BlockSp...  8.28 us
    ppermute x8, starting transfers between devices, neighbour(): lax.ppermute(values, 'gx', [(i, (i + step_x) % count_x) for i in range(co...  4.67 us
    dot_general x2, matrix products, tracer_step(): jnp.einsum('ab,...by->...ay', sum_x, tracers, precision=precision)  4.12 us
    unnamed x60, local copies, waits for them, and re-layouts  3.8 us
    ppermute x8, waiting for transfers between devices, neighbour(): lax.ppermute(values, 'gx', [(i, (i + step_x) % count_x) for i in range(co...  3.26 us
  transfers between devices with their start and end apart: 16, of which 10 were waited for; matrix products, arithmetic and copies ran while one was open for 5% of the time, Pallas kernels for 0%

profile of v20, /device:TPU:0, one launch (start us, length us, event | category | flops | bytes accessed | tf_op | source)
XLA Modules:
  0.0 91.7 jit_solution(18102500910220576455)
XLA Ops:
  0.7 0.6 copy-done.16
  2.0 0.7 fusion.10
  2.7 0.7 convolution_bitcast_fusion.5
  3.5 0.7 fusion.52
  4.4 0.7 fusion.2
  5.2 0.7 fusion.1
  5.9 1.1 %slice_reduce_fusion.3 = (f32[160,16]{1,0:T(8,128)S(1)}, f32[160,16]{1,0:T(8,128)S(1)}) fusion(f32[160,16,128]{2,1,0:T(8,128)S(1)} %fusion.1), kind=kLoop, calls=%fused_computation.24 | loop fusion | bytes 40960 | tf_op jit(solution)/shard_map/slice | solution.py:87
  7.1 3.0 %collective-permute-start = (f32[20,128]{1,0:T(8,128)S(1)}, f32[20,128]{1,0:T(8,128)S(1)}, u32[]{:S(2)}, u32[]{:S(2)}) collective-permute-start(f32[20,128]{1,0:T(8,128)S(1)} %reshape_squeeze.39), channel_id=1, source_target_pairs={{0,1},{1,2},{2,3},{3,4},{4,5},{5,6},{6,7},{7,0},{8,9},{9,10},{10,1... | collective-permute-start | bytes 30728 | tf_op jit(solution)/shard_map/ppermute | solution.py:25
  10.2 3.1 %collective-permute-start.1 = (f32[20,128]{1,0:T(8,128)S(1)}, f32[20,128]{1,0:T(8,128)S(1)}, u32[]{:S(2)}, u32[]{:S(2)}) collective-permute-start(f32[20,128]{1,0:T(8,128)S(1)} %reshape_squeeze.40), channel_id=1, source_target_pairs={{0,7},{1,0},{2,1},{3,2},{4,3},{5,4},{6,5},{7,6},{8,15},{9,8},{10,9... | collective-permute-start | bytes 30728 | tf_op jit(solution)/shard_map/ppermute | solution.py:25
  13.3 1.5 %collective-permute-done = f32[20,128]{1,0:T(8,128)S(1)} collective-permute-done((f32[20,128]{1,0:T(8,128)S(1)}, f32[20,128]{1,0:T(8,128)S(1)}, u32[]{:S(2)}, u32[]{:S(2)}) %collective-permute-start) | collective-permute-done | bytes 10272 | tf_op jit(solution)/shard_map/ppermute | solution.py:25
  15.0 0.7 select_select_fusion.1
  16.0 1.7 %collective-permute-start.3 = (f32[160,128]{1,0:T(8,128)S(1)}, f32[160,128]{1,0:T(8,128)S(1)}, u32[]{:S(2)}, u32[]{:S(2)}) collective-permute-start(f32[160,128]{1,0:T(8,128)S(1)} %bitcast.146), channel_id=1, source_target_pairs={{0,24},{8,0},{16,8},{24,16},{1,25},{9,1},{17,9},{25,17},{2,26},{10... | collective-permute-start | bytes 245768 | tf_op jit(solution)/shard_map/ppermute | solution.py:23
  17.7 2.1 %collective-permute-done.2 = f32[160,128]{1,0:T(8,128)S(1)} collective-permute-done((f32[160,128]{1,0:T(8,128)S(1)}, f32[160,128]{1,0:T(8,128)S(1)}, u32[]{:S(2)}, u32[]{:S(2)}) %collective-permute-start.2) | collective-permute-done | bytes 81952 | tf_op jit(solution)/shard_map/ppermute | solution.py:23
  20.0 1.4 %fusion.5 = f32[160,16,128]{2,1,0:T(8,128)S(1)} fusion(f32[160,16,128]{2,1,0:T(8,128)S(1)} %bitcast.141, f32[16,16,1]{1,0,2:T(8,128)S(1)} %copy-done.26, f32[160,16,128]{2,1,0:T(8,128)S(1)} %fusion.1, f32[16,128]{1,0:T(8,128)S(1)} %copy-done.25, f32[160,128]{1,0:T(8,128)S(1)} %collective-permute-done.3, f32[160,128]{1,0:T(8,128)S(1)} %collective-permute-done.2, ...), kind=kOutput, calls=%fused_computation.14 | convolution fusion | flops 34078720 | bytes 4125984 | tf_op jit(solution)/shard_map/ab,lby->lay/dot_general | solution.py:95
  21.4 0.7 fusion.6
  22.4 0.7 convolution_multiply_fusion.1
  23.1 0.7 convolution_bitcast_fusion.2
  23.9 0.7 fusion.53
  24.5 0.7 fusion
  25.2 1.1 %slice_reduce_fusion.1 = (f32[160,16]{1,0:T(8,128)S(1)}, f32[160,16]{1,0:T(8,128)S(1)}) fusion(f32[160,16,128]{2,1,0:T(8,128)S(1)} %fusion), kind=kLoop, calls=%fused_computation.22 | loop fusion | bytes 40960 | tf_op jit(solution)/shard_map/slice | solution.py:87
  26.4 1.4 %collective-permute-start.4 = (f32[20,128]{1,0:T(8,128)S(1)}, f32[20,128]{1,0:T(8,128)S(1)}, u32[]{:S(2)}, u32[]{:S(2)}) collective-permute-start(f32[20,128]{1,0:T(8,128)S(1)} %reshape_squeeze.41), channel_id=1, source_target_pairs={{0,1},{1,2},{2,3},{3,4},{4,5},{5,6},{6,7},{7,0},{8,9},{9,10},{10,1... | collective-permute-start | bytes 30728 | tf_op jit(solution)/shard_map/ppermute | solution.py:25
  28.0 3.6 %collective-permute-start.5 = (f32[20,128]{1,0:T(8,128)S(1)}, f32[20,128]{1,0:T(8,128)S(1)}, u32[]{:S(2)}, u32[]{:S(2)}) collective-permute-start(f32[20,128]{1,0:T(8,128)S(1)} %reshape_squeeze.42), channel_id=1, source_target_pairs={{0,7},{1,0},{2,1},{3,2},{4,3},{5,4},{6,5},{7,6},{8,15},{9,8},{10,9... | collective-permute-start | bytes 30728 | tf_op jit(solution)/shard_map/ppermute | solution.py:25
  31.6 1.3 %collective-permute-done.4 = f32[20,128]{1,0:T(8,128)S(1)} collective-permute-done((f32[20,128]{1,0:T(8,128)S(1)}, f32[20,128]{1,0:T(8,128)S(1)}, u32[]{:S(2)}, u32[]{:S(2)}) %collective-permute-start.4) | collective-permute-done | bytes 10272 | tf_op jit(solution)/shard_map/ppermute | solution.py:25
  33.1 0.7 select_select_fusion
  34.1 0.9 collective-permute-start.6
  35.0 0.9 collective-permute-start.7
  35.9 0.7 copy.52
  36.6 0.7 copy.51
  37.2 0.7 collective-permute-done.6
  38.3 1.4 %fusion.9 = f32[160,16,128]{2,1,0:T(8,128)S(1)} fusion(f32[160,16,128]{2,1,0:T(8,128)S(1)} %copy-done.3, f32[16,16,1]{1,0,2:T(8,128)S(1)} %copy-done.26, f32[160,16,128]{2,1,0:T(8,128)S(1)} %fusion, f32[160,128]{1,0:T(8,128)S(1)} %collective-permute-done.7, f32[160,128]{1,0:T(8,128)S(1)} %collective-permute-done.6, f32[16,128]{1,0:T(8,128)S(1)} %copy-done.25, ...), kind=kOutput, calls=%fused_computation.18 | convolution fusion | flops 34078720 | bytes 4125984 | tf_op jit(solution)/shard_map/ab,lby->lay/dot_general | solution.py:95
  39.8 0.7 fusion.39.table_ref
  40.8 3.6 %shard_map.320 = f32[4,8192]{1,0:T(4,128)} custom-call(s32[1,8192]{1,0:T(1,128)} %bitcast.144, f32[1,8192]{1,0:T(1,128)} %bitcast.143, f32[4,16,128]{2,1,0:T(8,128)} %fusion.39.table_ref), custom_call_target="tpu_custom_call" | custom-call | tf_op jit(solution)/shard_map/pallas_call | solution.py:208
  44.4 14.7 %all_to_all.5 = f32[4,32,256]{2,0,1:T(4,128)S(1)} all-to-all(f32[4,32,256]{2,0,1:T(4,128)} %bitcast.142), channel_id=1, replica_groups=mesh['gx'=4,'gy'=8] {'gx','gy'}, dimensions={1} | all-to-all | bytes 262144 | tf_op jit(solution)/shard_map/all_to_all | solution.py:248
  59.1 0.7 copy.41.table_ref
  59.8 4.7 %shard_map.321 = f32[4,2048]{1,0:T(4,128)} custom-call(s32[1,8192]{1,0:T(1,128)} %bitcast.153, f32[1,8192]{1,0:T(1,128)} %bitcast.154, f32[4,32,256]{2,1,0:T(8,128)} %copy.41.table_ref), custom_call_target="tpu_custom_call" | custom-call | tf_op jit(solution)/shard_map/pallas_call | solution.py:208
  64.5 1.0 %fusion.40 = (f32[1,2048]{1,0:T(1,128)S(1)}, f32[1,2048]{1,0:T(1,128)S(1)}, f32[1,2048]{1,0:T(1,128)S(1)}, f32[1,2048]{1,0:T(1,128)S(1)}) fusion(f32[4,2048]{1,0:T(4,128)} %shard_map.321), kind=kLoop, calls=%fused_computation.82 | loop fusion | flops 8192 | bytes 65536 | tf_op jit(solution)/shard_map/mul | solution.py:252
  66.1 0.7 fusion.51
  68.1 0.7 reshape_squeeze.46
  68.8 2.0 %collective-permute-start.10 = (f32[10,128]{1,0:T(8,128)}, f32[10,128]{1,0:T(8,128)S(1)}, u32[]{:S(2)}, u32[]{:S(2)}) collective-permute-start(f32[10,128]{1,0:T(8,128)} %reshape_squeeze.46), channel_id=1, source_target_pairs={{0,7},{1,0},{2,1},{3,2},{4,3},{5,4},{6,5},{7,6},{8,15},{9,8},{10,9... | collective-permute-start | bytes 15368 | tf_op jit(solution)/shard_map/ppermute | solution.py:25
  71.5 0.9 fusion.38
  72.7 4.7 %collective-permute-done.11 = f32[10,128]{1,0:T(8,128)} collective-permute-done((f32[10,128]{1,0:T(8,128)S(1)}, f32[10,128]{1,0:T(8,128)}, u32[]{:S(2)}, u32[]{:S(2)}) %collective-permute-start.11) | collective-permute-done | bytes 5152 | tf_op jit(solution)/shard_map/ppermute | solution.py:25
  77.4 0.8 broadcast_in_dim.268
  78.2 1.9 %fusion.19 = f32[2,40,16,128]{3,2,1,0:T(8,128)S(1)} fusion(f32[2,40,16,128]{3,2,1,0:T(8,128)S(1)} %fusion.43, f32[2,40,16,128]{3,2,1,0:T(8,128)S(1)} %convolution_bitcast_fusion.8, f32[2,40,16,128]{3,2,1,0:T(8,128)S(1)} %fusion.54, f32[2,40,16,128]{3,2,1,0:T(8,128)S(1)} %fusion.55, f32[40,16,128]{2,1,0:T(8,128)} %get-tuple-element.69, ...), kind=kOutput, calls=%fused_computation.47 | convolution fusion | flops 19169280 | bytes 4025632 | tf_op jit(solution)/shard_map/ab,...by->...ay/dot_general | solution.py:121
  81.7 1.2 %collective-permute-start.14 = (f32[10,128]{1,0:T(8,128)S(1)}, f32[10,128]{1,0:T(8,128)S(1)}, u32[]{:S(2)}, u32[]{:S(2)}) collective-permute-start(f32[10,128]{1,0:T(8,128)S(1)} %reshape_squeeze.50), channel_id=1, source_target_pairs={{0,7},{1,0},{2,1},{3,2},{4,3},{5,4},{6,5},{7,6},{8,15},{9,8},{10,9... | collective-permute-start | bytes 15368 | tf_op jit(solution)/shard_map/ppermute | solution.py:25
  83.0 0.9 collective-permute-start.15
  84.7 0.6 collective-permute-done.14
  85.4 3.9 %collective-permute-done.15 = f32[10,128]{1,0:T(8,128)S(1)} collective-permute-done((f32[10,128]{1,0:T(8,128)S(1)}, f32[10,128]{1,0:T(8,128)S(1)}, u32[]{:S(2)}, u32[]{:S(2)}) %collective-permute-start.15) | collective-permute-done | bytes 5152 | tf_op jit(solution)/shard_map/ppermute | solution.py:25
  89.4 2.3 %fusion.31 = f32[2,40,16,128]{3,2,1,0:T(8,128)} fusion(f32[2,40,16,128]{3,2,1,0:T(8,128)S(1)} %fusion.19, f32[2,40,16,128]{3,2,1,0:T(8,128)S(1)} %convolution_bitcast_fusion.6, f32[2,40,16,128]{3,2,1,0:T(8,128)S(1)} %fusion.56, f32[2,40,16,128]{3,2,1,0:T(8,128)S(1)} %fusion.57, f32[2,40,16]{2,1,0:T(8,128)S(1)} %broadcast_in_dim.276, ...), kind=kOutput, calls=%fused_computation.59 | convolution fusion | flops 19169280 | bytes 4025632 | tf_op jit(solution)/shard_map/ab,...by->...ay/dot_general | solution.py:121
  (106 shorter events, 9.1 us)
Async XLA Ops:
  0.6 0.7 copy-start.16
  0.6 0.7 copy-start.23
  0.7 0.9 %copy-start.12 = (f32[16,16,1]{1,0,2:T(8,128)S(1)}, f32[16,16,1]{1,0,2:T(8,128)}, u32[]{:S(2)}) copy-start(f32[16,16,1]{1,0,2:T(8,128)} %constant.166) | copy-start | bytes 3076
  0.7 1.3 %copy-start.1 = (f32[4,40,16,128]{3,2,1,0:T(8,128)S(1)}, f32[4,40,16,128]{3,2,1,0:T(8,128)}, u32[]{:S(2)}) copy-start(f32[4,40,16,128]{3,2,1,0:T(8,128)} %param.41) | copy-start | bytes 3932164
  0.7 0.8 copy-start.15
  2.7 0.8 copy-start.11
  3.5 0.8 copy-start.8
  4.4 0.8 copy-start.7
  7.0 13.0 %copy-start.25 = (f32[16,128]{1,0:T(8,128)S(1)}, f32[16,128]{1,0:T(8,128)}, u32[]{:S(2)}) copy-start(f32[16,128]{1,0:T(8,128)} %constant.165) | copy-start | bytes 24580
  7.0 13.0 %copy-start.26 = (f32[16,16,1]{1,0,2:T(8,128)S(1)}, f32[16,16,1]{1,0,2:T(8,128)}, u32[]{:S(2)}) copy-start(f32[16,16,1]{1,0,2:T(8,128)} %constant.170) | copy-start | bytes 3076
  7.1 7.7 %collective-permute-start = (f32[20,128]{1,0:T(8,128)S(1)}, f32[20,128]{1,0:T(8,128)S(1)}, u32[]{:S(2)}, u32[]{:S(2)}) collective-permute-start(f32[20,128]{1,0:T(8,128)S(1)} %reshape_squeeze.39), channel_id=1, source_target_pairs={{0,1},{1,2},{2,3},{3,4},{4,5},{5,6},{6,7},{7,0},{8,9},{9,10},{10,1... | collective-permute-start | bytes 30728 | tf_op jit(solution)/shard_map/ppermute | solution.py:25
  10.2 4.7 %collective-permute-start.1 = (f32[20,128]{1,0:T(8,128)S(1)}, f32[20,128]{1,0:T(8,128)S(1)}, u32[]{:S(2)}, u32[]{:S(2)}) collective-permute-start(f32[20,128]{1,0:T(8,128)S(1)} %reshape_squeeze.40), channel_id=1, source_target_pairs={{0,7},{1,0},{2,1},{3,2},{4,3},{5,4},{6,5},{7,6},{8,15},{9,8},{10,9... | collective-permute-start | bytes 30728 | tf_op jit(solution)/shard_map/ppermute | solution.py:25
  13.3 25.0 %copy-start.17 = (pred[128]{0:T(512)(128)(4,1)}, pred[128]{0:T(512)(128)(4,1)S(1)}, u32[]{:S(2)}) copy-start(pred[128]{0:T(512)(128)(4,1)S(1)} %get-tuple-element.76) | copy-start | bytes 388
  13.3 25.0 %copy-start.19 = (pred[128]{0:T(512)(128)(4,1)}, pred[128]{0:T(512)(128)(4,1)S(1)}, u32[]{:S(2)}) copy-start(pred[128]{0:T(512)(128)(4,1)S(1)} %get-tuple-element.77) | copy-start | bytes 388
  15.9 3.9 %collective-permute-start.2 = (f32[160,128]{1,0:T(8,128)S(1)}, f32[160,128]{1,0:T(8,128)S(1)}, u32[]{:S(2)}, u32[]{:S(2)}) collective-permute-start(f32[160,128]{1,0:T(8,128)S(1)} %bitcast.148), channel_id=1, source_target_pairs={{0,8},{8,16},{16,24},{24,0},{1,9},{9,17},{17,25},{25,1},{2,10},{10... | collective-permute-start | bytes 245768 | tf_op jit(solution)/shard_map/ppermute | solution.py:23
  16.0 4.0 %collective-permute-start.3 = (f32[160,128]{1,0:T(8,128)S(1)}, f32[160,128]{1,0:T(8,128)S(1)}, u32[]{:S(2)}, u32[]{:S(2)}) collective-permute-start(f32[160,128]{1,0:T(8,128)S(1)} %bitcast.146), channel_id=1, source_target_pairs={{0,24},{8,0},{16,8},{24,16},{1,25},{9,1},{17,9},{25,17},{2,26},{10... | collective-permute-start | bytes 245768 | tf_op jit(solution)/shard_map/ppermute | solution.py:23
  17.7 20.6 %copy-start.27 = (pred[16]{0:T(512)(128)(4,1)}, pred[16]{0:T(512)(128)(4,1)S(1)}, u32[]{:S(2)}) copy-start(pred[16]{0:T(512)(128)(4,1)S(1)} %get-tuple-element.78) | copy-start | bytes 52
  17.7 20.6 %copy-start.28 = (pred[16]{0:T(512)(128)(4,1)}, pred[16]{0:T(512)(128)(4,1)S(1)}, u32[]{:S(2)}) copy-start(pred[16]{0:T(512)(128)(4,1)S(1)} %get-tuple-element.79) | copy-start | bytes 52
  21.4 1.1 %copy-start.2 = (f32[160,16,128]{2,1,0:T(8,128)}, f32[160,16,128]{2,1,0:T(8,128)S(1)}, u32[]{:S(2)}) copy-start(f32[160,16,128]{2,1,0:T(8,128)S(1)} %fusion.5) | copy-start | bytes 3932164
  26.3 9.5 %copy-start.22 = (s32[1,32]{1,0:T(1,128)S(1)}, s32[1,32]{1,0:T(1,128)}, u32[]{:S(2)}) copy-start(s32[1,32]{1,0:T(1,128)} %param.44) | copy-start | bytes 388
  26.3 10.3 %copy-start.14 = (s32[1,32,256]{2,1,0:T(8,128)S(1)}, s32[1,32,256]{2,1,0:T(8,128)}, u32[]{:S(2)}) copy-start(s32[1,32,256]{2,1,0:T(8,128)} %param.43) | copy-start | bytes 98308
  26.3 12.0 %copy-start.3 = (f32[160,16,128]{2,1,0:T(8,128)S(1)}, f32[160,16,128]{2,1,0:T(8,128)}, u32[]{:S(2)}) copy-start(f32[160,16,128]{2,1,0:T(8,128)} %copy-done.2) | copy-start | bytes 3932164
  26.4 6.5 %collective-permute-start.4 = (f32[20,128]{1,0:T(8,128)S(1)}, f32[20,128]{1,0:T(8,128)S(1)}, u32[]{:S(2)}, u32[]{:S(2)}) collective-permute-start(f32[20,128]{1,0:T(8,128)S(1)} %reshape_squeeze.41), channel_id=1, source_target_pairs={{0,1},{1,2},{2,3},{3,4},{4,5},{5,6},{6,7},{7,0},{8,9},{9,10},{10,1... | collective-permute-start | bytes 30728 | tf_op jit(solution)/shard_map/ppermute | solution.py:25
  28.0 5.1 %collective-permute-start.5 = (f32[20,128]{1,0:T(8,128)S(1)}, f32[20,128]{1,0:T(8,128)S(1)}, u32[]{:S(2)}, u32[]{:S(2)}) collective-permute-start(f32[20,128]{1,0:T(8,128)S(1)} %reshape_squeeze.42), channel_id=1, source_target_pairs={{0,7},{1,0},{2,1},{3,2},{4,3},{5,4},{6,5},{7,6},{8,15},{9,8},{10,9... | collective-permute-start | bytes 30728 | tf_op jit(solution)/shard_map/ppermute | solution.py:25
  34.1 3.9 %collective-permute-start.6 = (f32[160,128]{1,0:T(8,128)S(1)}, f32[160,128]{1,0:T(8,128)S(1)}, u32[]{:S(2)}, u32[]{:S(2)}) collective-permute-start(f32[160,128]{1,0:T(8,128)S(1)} %bitcast.147), channel_id=1, source_target_pairs={{0,8},{8,16},{16,24},{24,0},{1,9},{9,17},{17,25},{25,1},{2,10},{10... | collective-permute-start | bytes 245768 | tf_op jit(solution)/shard_map/ppermute | solution.py:23
  35.0 3.3 %collective-permute-start.7 = (f32[160,128]{1,0:T(8,128)S(1)}, f32[160,128]{1,0:T(8,128)S(1)}, u32[]{:S(2)}, u32[]{:S(2)}) collective-permute-start(f32[160,128]{1,0:T(8,128)S(1)} %bitcast.145), channel_id=1, source_target_pairs={{0,24},{8,0},{16,8},{24,16},{1,25},{9,1},{17,9},{25,17},{2,26},{10... | collective-permute-start | bytes 245768 | tf_op jit(solution)/shard_map/ppermute | solution.py:23
  37.2 28.2 %copy-start = (f32[2,40,16,128]{3,2,1,0:T(8,128)S(1)}, f32[2,40,16,128]{3,2,1,0:T(8,128)}, u32[]{:S(2)}) copy-start(f32[2,40,16,128]{3,2,1,0:T(8,128)} %param.45) | copy-start | bytes 1966084
  39.7 1.1 %copy-start.21 = (f32[160,16,128]{2,1,0:T(8,128)}, f32[160,16,128]{2,1,0:T(8,128)S(1)}, u32[]{:S(2)}) copy-start(f32[160,16,128]{2,1,0:T(8,128)S(1)} %fusion.9) | copy-start | bytes 3932164
  40.8 26.0 %copy-start.13 = (f32[16,16,1,1]{1,0,3,2:T(8,128)S(1)}, f32[16,16,1,1]{1,0,3,2:T(8,128)}, u32[]{:S(2)}) copy-start(f32[16,16,1,1]{1,0,3,2:T(8,128)} %constant.173) | copy-start | bytes 3076
  65.5 1.7 %copy-start.10 = (f32[128,128,1,1]{1,0,3,2:T(8,128)S(1)}, f32[128,128,1,1]{1,0,3,2:T(8,128)}, u32[]{:S(2)}) copy-start(f32[128,128,1,1]{1,0,3,2:T(8,128)} %constant.172) | copy-start | bytes 196612
  66.8 0.9 copy-start.9
  67.2 4.3 %copy-start.4 = (f32[2,40,16,128]{3,2,1,0:T(8,128)S(1)}, f32[2,40,16,128]{3,2,1,0:T(8,128)}, u32[]{:S(2)}) copy-start(f32[2,40,16,128]{3,2,1,0:T(8,128)} %param.46) | copy-start | bytes 1966084
  68.8 3.9 %collective-permute-start.10 = (f32[10,128]{1,0:T(8,128)}, f32[10,128]{1,0:T(8,128)S(1)}, u32[]{:S(2)}, u32[]{:S(2)}) collective-permute-start(f32[10,128]{1,0:T(8,128)} %reshape_squeeze.46), channel_id=1, source_target_pairs={{0,7},{1,0},{2,1},{3,2},{4,3},{5,4},{6,5},{7,6},{8,15},{9,8},{10,9... | collective-permute-start | bytes 15368 | tf_op jit(solution)/shard_map/ppermute | solution.py:25
  70.9 6.5 %collective-permute-start.11 = (f32[10,128]{1,0:T(8,128)S(1)}, f32[10,128]{1,0:T(8,128)}, u32[]{:S(2)}, u32[]{:S(2)}) collective-permute-start(f32[10,128]{1,0:T(8,128)S(1)} %reshape_squeeze.47), channel_id=1, source_target_pairs={{0,1},{1,2},{2,3},{3,4},{4,5},{5,6},{6,7},{7,0},{8,9},{9,10},{10,1... | collective-permute-start | bytes 15368 | tf_op jit(solution)/shard_map/ppermute | solution.py:25
  70.9 7.2 %collective-permute-start.8 = (f32[80,128]{1,0:T(8,128)}, f32[80,128]{1,0:T(8,128)}, u32[]{:S(2)}, u32[]{:S(2)}) collective-permute-start(f32[80,128]{1,0:T(8,128)} %bitcast.150), channel_id=1, source_target_pairs={{0,24},{8,0},{16,8},{24,16},{1,25},{9,1},{17,9},{25,17},{2,26},{10... | collective-permute-start | bytes 122888 | tf_op jit(solution)/shard_map/ppermute | solution.py:23
  71.0 7.2 %collective-permute-start.9 = (f32[80,128]{1,0:T(8,128)S(1)}, f32[80,128]{1,0:T(8,128)}, u32[]{:S(2)}, u32[]{:S(2)}) collective-permute-start(f32[80,128]{1,0:T(8,128)S(1)} %bitcast.149), channel_id=1, source_target_pairs={{0,8},{8,16},{16,24},{24,0},{1,9},{9,17},{17,25},{25,1},{2,10},{10... | collective-permute-start | bytes 122888 | tf_op jit(solution)/shard_map/ppermute | solution.py:23
  71.5 6.7 %copy-start.18 = (pred[128]{0:T(512)(128)(4,1)S(1)}, pred[128]{0:T(512)(128)(4,1)}, u32[]{:S(2)}) copy-start(pred[128]{0:T(512)(128)(4,1)} %copy-done.17) | copy-start | bytes 388
  71.5 6.7 %copy-start.20 = (pred[128]{0:T(512)(128)(4,1)S(1)}, pred[128]{0:T(512)(128)(4,1)}, u32[]{:S(2)}) copy-start(pred[128]{0:T(512)(128)(4,1)} %copy-done.19) | copy-start | bytes 388
  71.5 6.7 %copy-start.24 = (f32[16,16,1,1]{1,0,3,2:T(8,128)S(1)}, f32[16,16,1,1]{1,0,3,2:T(8,128)}, u32[]{:S(2)}) copy-start(f32[16,16,1,1]{1,0,3,2:T(8,128)} %constant.171) | copy-start | bytes 3076
  80.9 8.5 %copy-start.5 = (f32[40,16,128]{2,1,0:T(8,128)S(1)}, f32[40,16,128]{2,1,0:T(8,128)}, u32[]{:S(2)}) copy-start(f32[40,16,128]{2,1,0:T(8,128)} %get-tuple-element.68) | copy-start | bytes 983044
  80.9 8.5 %copy-start.6 = (f32[40,16,128]{2,1,0:T(8,128)S(1)}, f32[40,16,128]{2,1,0:T(8,128)}, u32[]{:S(2)}) copy-start(f32[40,16,128]{2,1,0:T(8,128)} %get-tuple-element.69) | copy-start | bytes 983044
  81.7 3.7 %collective-permute-start.14 = (f32[10,128]{1,0:T(8,128)S(1)}, f32[10,128]{1,0:T(8,128)S(1)}, u32[]{:S(2)}, u32[]{:S(2)}) collective-permute-start(f32[10,128]{1,0:T(8,128)S(1)} %reshape_squeeze.50), channel_id=1, source_target_pairs={{0,7},{1,0},{2,1},{3,2},{4,3},{5,4},{6,5},{7,6},{8,15},{9,8},{10,9... | collective-permute-start | bytes 15368 | tf_op jit(solution)/shard_map/ppermute | solution.py:25
  83.0 6.4 %collective-permute-start.15 = (f32[10,128]{1,0:T(8,128)S(1)}, f32[10,128]{1,0:T(8,128)S(1)}, u32[]{:S(2)}, u32[]{:S(2)}) collective-permute-start(f32[10,128]{1,0:T(8,128)S(1)} %reshape_squeeze.51), channel_id=1, source_target_pairs={{0,1},{1,2},{2,3},{3,4},{4,5},{5,6},{6,7},{7,0},{8,9},{9,10},{10,1... | collective-permute-start | bytes 15368 | tf_op jit(solution)/shard_map/ppermute | solution.py:25
  83.8 5.6 %collective-permute-start.12 = (f32[80,128]{1,0:T(8,128)S(1)}, f32[80,128]{1,0:T(8,128)S(1)}, u32[]{:S(2)}, u32[]{:S(2)}) collective-permute-start(f32[80,128]{1,0:T(8,128)S(1)} %bitcast.152), channel_id=1, source_target_pairs={{0,24},{8,0},{16,8},{24,16},{1,25},{9,1},{17,9},{25,17},{2,26},{10... | collective-permute-start | bytes 122888 | tf_op jit(solution)/shard_map/ppermute | solution.py:23
  83.8 5.6 %collective-permute-start.13 = (f32[80,128]{1,0:T(8,128)S(1)}, f32[80,128]{1,0:T(8,128)S(1)}, u32[]{:S(2)}, u32[]{:S(2)}) collective-permute-start(f32[80,128]{1,0:T(8,128)S(1)} %bitcast.151), channel_id=1, source_target_pairs={{0,8},{8,16},{16,24},{24,0},{1,9},{9,17},{17,25},{25,1},{2,10},{10... | collective-permute-start | bytes 122888 | tf_op jit(solution)/shard_map/ppermute | solution.py:23

commit v21 on v15

--- a/solution.py
+++ b/solution.py
@@ -201,7 +201,7 @@
     count = flat.shape[1]
     width = count // groups
     tile = 128
-    while tile < 2048 and width % (2 * tile) == 0 and fields * rows * tile * 8 <= 4 * 2**20:
+    while tile < 8192 and width % (2 * tile) == 0 and fields * rows * tile * 8 <= 4 * 2**20:
         tile *= 2
     blocks = width // tile
     return pl.pallas_call(

time: 90.5 us -> 89.6 us (0.990)
  no operation moved by 1% of the time
where the time goes in v21:
time: 89.6 us; the launch traced here: 89 us
  starting transfers between devices  19.8 us (22%)
  waiting for transfers between devices  15.7 us (18%)
  matrix products  15.1 us (17%)
  blocking collectives  14.5 us (16%)
  local copies, waits for them, and re-layouts  10.7 us (12%)
  Pallas kernels  7.5 us (8%)
  other arithmetic  4.39 us (5%)
  between operations  1.27 us (1%)
    ppermute x8, starting transfers between devices, neighbour(): lax.ppermute(values, 'gy', [(j, (j + step_y) % count_y) for j in range(co...  15.1 us
    all_to_all x1, blocking collectives, per_device(): lax.all_to_all(payload, ('gx', 'gy'), split_axis=1, concat_axis=1, tiled=...  14.5 us
    ppermute x8, waiting for transfers between devices, neighbour(): lax.ppermute(values, 'gy', [(j, (j + step_y) % count_y) for j in range(co...  12.4 us
    pallas_call x2, Pallas kernels, onehot_gather(): pl.pallas_call(gather_kernel, grid=(blocks, groups), in_specs=[pl.BlockSp...  7.5 us
    ppermute x8, starting transfers between devices, neighbour(): lax.ppermute(values, 'gx', [(i, (i + step_x) % count_x) for i in range(co...  4.67 us
    dot_general x2, matrix products, tracer_step(): jnp.einsum('ab,...by->...ay', sum_x, tracers, precision=precision)  4.15 us
    ppermute x8, waiting for transfers between devices, neighbour(): lax.ppermute(values, 'gx', [(i, (i + step_x) % count_x) for i in range(co...  3.3 us
    unnamed x58, local copies, waits for them, and re-layouts  3.05 us
  transfers between devices with their start and end apart: 16, of which 10 were waited for; matrix products, arithmetic and copies ran while one was open for 5% of the time, Pallas kernels for 0%

profile of v21, /device:TPU:0, one launch (start us, length us, event | category | flops | bytes accessed | tf_op | source)
XLA Modules:
  0.0 89.0 jit_solution(7997155487935706859)
XLA Ops:
  0.7 0.6 copy-done.17
  2.0 0.7 fusion.10
  2.7 0.7 convolution_bitcast_fusion.5
  3.5 0.7 fusion.50
  4.4 0.7 fusion.2
  5.2 0.7 fusion.1
  5.9 1.1 %slice_reduce_fusion.3 = (f32[160,16]{1,0:T(8,128)S(1)}, f32[160,16]{1,0:T(8,128)S(1)}) fusion(f32[160,16,128]{2,1,0:T(8,128)S(1)} %fusion.1), kind=kLoop, calls=%fused_computation.24 | loop fusion | bytes 40960 | tf_op jit(solution)/shard_map/slice | solution.py:87
  7.1 3.0 %collective-permute-start = (f32[20,128]{1,0:T(8,128)S(1)}, f32[20,128]{1,0:T(8,128)S(1)}, u32[]{:S(2)}, u32[]{:S(2)}) collective-permute-start(f32[20,128]{1,0:T(8,128)S(1)} %reshape_squeeze.39), channel_id=1, source_target_pairs={{0,1},{1,2},{2,3},{3,4},{4,5},{5,6},{6,7},{7,0},{8,9},{9,10},{10,1... | collective-permute-start | bytes 30728 | tf_op jit(solution)/shard_map/ppermute | solution.py:25
  10.1 3.1 %collective-permute-start.1 = (f32[20,128]{1,0:T(8,128)S(1)}, f32[20,128]{1,0:T(8,128)S(1)}, u32[]{:S(2)}, u32[]{:S(2)}) collective-permute-start(f32[20,128]{1,0:T(8,128)S(1)} %reshape_squeeze.40), channel_id=1, source_target_pairs={{0,7},{1,0},{2,1},{3,2},{4,3},{5,4},{6,5},{7,6},{8,15},{9,8},{10,9... | collective-permute-start | bytes 30728 | tf_op jit(solution)/shard_map/ppermute | solution.py:25
  13.3 1.5 %collective-permute-done = f32[20,128]{1,0:T(8,128)S(1)} collective-permute-done((f32[20,128]{1,0:T(8,128)S(1)}, f32[20,128]{1,0:T(8,128)S(1)}, u32[]{:S(2)}, u32[]{:S(2)}) %collective-permute-start) | collective-permute-done | bytes 10272 | tf_op jit(solution)/shard_map/ppermute | solution.py:25
  15.0 0.8 select_add_fusion.1
  16.0 1.7 %collective-permute-start.3 = (f32[160,128]{1,0:T(8,128)S(1)}, f32[160,128]{1,0:T(8,128)S(1)}, u32[]{:S(2)}, u32[]{:S(2)}) collective-permute-start(f32[160,128]{1,0:T(8,128)S(1)} %bitcast.151), channel_id=1, source_target_pairs={{0,24},{8,0},{16,8},{24,16},{1,25},{9,1},{17,9},{25,17},{2,26},{10... | collective-permute-start | bytes 245768 | tf_op jit(solution)/shard_map/ppermute | solution.py:23
  17.8 2.1 %collective-permute-done.2 = f32[160,128]{1,0:T(8,128)S(1)} collective-permute-done((f32[160,128]{1,0:T(8,128)S(1)}, f32[160,128]{1,0:T(8,128)S(1)}, u32[]{:S(2)}, u32[]{:S(2)}) %collective-permute-start.2) | collective-permute-done | bytes 81952 | tf_op jit(solution)/shard_map/ppermute | solution.py:23
  20.0 0.8 fusion.5
  20.8 0.7 fusion.6
  21.5 0.7 convolution_multiply_fusion.1
  22.2 0.7 convolution_bitcast_fusion.2
  22.9 0.7 fusion.51
  23.6 0.7 fusion
  24.3 1.1 %slice_reduce_fusion.1 = (f32[160,16]{1,0:T(8,128)S(1)}, f32[160,16]{1,0:T(8,128)S(1)}) fusion(f32[160,16,128]{2,1,0:T(8,128)S(1)} %fusion), kind=kLoop, calls=%fused_computation.22 | loop fusion | bytes 40960 | tf_op jit(solution)/shard_map/slice | solution.py:87
  25.5 1.4 %collective-permute-start.4 = (f32[20,128]{1,0:T(8,128)S(1)}, f32[20,128]{1,0:T(8,128)S(1)}, u32[]{:S(2)}, u32[]{:S(2)}) collective-permute-start(f32[20,128]{1,0:T(8,128)S(1)} %reshape_squeeze.41), channel_id=1, source_target_pairs={{0,1},{1,2},{2,3},{3,4},{4,5},{5,6},{6,7},{7,0},{8,9},{9,10},{10,1... | collective-permute-start | bytes 30728 | tf_op jit(solution)/shard_map/ppermute | solution.py:25
  27.0 3.4 %collective-permute-start.5 = (f32[20,128]{1,0:T(8,128)S(1)}, f32[20,128]{1,0:T(8,128)S(1)}, u32[]{:S(2)}, u32[]{:S(2)}) collective-permute-start(f32[20,128]{1,0:T(8,128)S(1)} %reshape_squeeze.42), channel_id=1, source_target_pairs={{0,7},{1,0},{2,1},{3,2},{4,3},{5,4},{6,5},{7,6},{8,15},{9,8},{10,9... | collective-permute-start | bytes 30728 | tf_op jit(solution)/shard_map/ppermute | solution.py:25
  30.4 1.5 %collective-permute-done.4 = f32[20,128]{1,0:T(8,128)S(1)} collective-permute-done((f32[20,128]{1,0:T(8,128)S(1)}, f32[20,128]{1,0:T(8,128)S(1)}, u32[]{:S(2)}, u32[]{:S(2)}) %collective-permute-start.4) | collective-permute-done | bytes 10272 | tf_op jit(solution)/shard_map/ppermute | solution.py:25
  32.2 0.8 select_add_fusion
  33.2 0.9 %collective-permute-start.6 = (f32[160,128]{1,0:T(8,128)S(1)}, f32[160,128]{1,0:T(8,128)S(1)}, u32[]{:S(2)}, u32[]{:S(2)}) collective-permute-start(f32[160,128]{1,0:T(8,128)S(1)} %bitcast.152), channel_id=1, source_target_pairs={{0,8},{8,16},{16,24},{24,0},{1,9},{9,17},{17,25},{25,1},{2,10},{10... | collective-permute-start | bytes 245768 | tf_op jit(solution)/shard_map/ppermute | solution.py:23
  34.1 0.9 collective-permute-start.7
  35.1 0.6 copy.52
  35.7 0.6 copy.51
  36.3 0.8 collective-permute-done.6
  37.4 0.8 fusion.9
  38.3 0.7 fusion.37.table_ref
  39.0 2.8 %shard_map.320 = f32[4,8192]{1,0:T(4,128)} custom-call(s32[1,8192]{1,0:T(1,128)} %bitcast.149, f32[1,8192]{1,0:T(1,128)} %bitcast.148, f32[4,16,128]{2,1,0:T(8,128)} %fusion.37.table_ref), custom_call_target="tpu_custom_call" | custom-call | tf_op jit(solution)/shard_map/pallas_call | solution.py:207
  41.8 14.5 %all_to_all.5 = f32[4,32,256]{2,0,1:T(4,128)S(1)} all-to-all(f32[4,32,256]{2,0,1:T(4,128)} %bitcast.147), channel_id=1, replica_groups=mesh['gx'=4,'gy'=8] {'gx','gy'}, dimensions={1} | all-to-all | bytes 262144 | tf_op jit(solution)/shard_map/all_to_all | solution.py:247
  56.4 0.7 copy.41.table_ref
  57.1 4.7 %shard_map.321 = f32[4,2048]{1,0:T(4,128)} custom-call(s32[1,8192]{1,0:T(1,128)} %bitcast.158, f32[1,8192]{1,0:T(1,128)} %bitcast.159, f32[4,32,256]{2,1,0:T(8,128)} %copy.41.table_ref), custom_call_target="tpu_custom_call" | custom-call | tf_op jit(solution)/shard_map/pallas_call | solution.py:207
  61.7 1.0 %fusion.38 = (f32[1,2048]{1,0:T(1,128)S(1)}, f32[1,2048]{1,0:T(1,128)S(1)}, f32[1,2048]{1,0:T(1,128)S(1)}, f32[1,2048]{1,0:T(1,128)S(1)}) fusion(f32[4,2048]{1,0:T(4,128)} %shard_map.321), kind=kLoop, calls=%fused_computation.76 | loop fusion | flops 8192 | bytes 65536 | tf_op jit(solution)/shard_map/mul | solution.py:251
  63.3 0.7 fusion.49
  65.3 0.7 reshape_squeeze.46
  66.0 2.0 %collective-permute-start.10 = (f32[10,128]{1,0:T(8,128)}, f32[10,128]{1,0:T(8,128)S(1)}, u32[]{:S(2)}, u32[]{:S(2)}) collective-permute-start(f32[10,128]{1,0:T(8,128)} %reshape_squeeze.46), channel_id=1, source_target_pairs={{0,7},{1,0},{2,1},{3,2},{4,3},{5,4},{6,5},{7,6},{8,15},{9,8},{10,9... | collective-permute-start | bytes 15368 | tf_op jit(solution)/shard_map/ppermute | solution.py:25
  68.7 0.9 fusion.36
  69.9 4.7 %collective-permute-done.11 = f32[10,128]{1,0:T(8,128)} collective-permute-done((f32[10,128]{1,0:T(8,128)S(1)}, f32[10,128]{1,0:T(8,128)}, u32[]{:S(2)}, u32[]{:S(2)}) %collective-permute-start.11) | collective-permute-done | bytes 5152 | tf_op jit(solution)/shard_map/ppermute | solution.py:25
  74.6 0.8 broadcast_in_dim.268
  75.4 1.9 %fusion.17 = f32[2,40,16,128]{3,2,1,0:T(8,128)S(1)} fusion(f32[2,40,16,128]{3,2,1,0:T(8,128)S(1)} %fusion.41, f32[2,40,16,128]{3,2,1,0:T(8,128)S(1)} %convolution_bitcast_fusion.8, f32[2,40,16,128]{3,2,1,0:T(8,128)S(1)} %fusion.52, f32[2,40,16,128]{3,2,1,0:T(8,128)S(1)} %fusion.53, f32[40,16,128]{2,1,0:T(8,128)} %get-tuple-element.69, ...), kind=kOutput, calls=%fused_computation.45 | convolution fusion | flops 19169280 | bytes 4025632 | tf_op jit(solution)/shard_map/ab,...by->...ay/dot_general | solution.py:120
  78.9 1.2 %collective-permute-start.14 = (f32[10,128]{1,0:T(8,128)S(1)}, f32[10,128]{1,0:T(8,128)S(1)}, u32[]{:S(2)}, u32[]{:S(2)}) collective-permute-start(f32[10,128]{1,0:T(8,128)S(1)} %reshape_squeeze.50), channel_id=1, source_target_pairs={{0,7},{1,0},{2,1},{3,2},{4,3},{5,4},{6,5},{7,6},{8,15},{9,8},{10,9... | collective-permute-start | bytes 15368 | tf_op jit(solution)/shard_map/ppermute | solution.py:25
  80.2 0.9 collective-permute-start.15
  81.9 0.6 collective-permute-done.14
  82.6 3.9 %collective-permute-done.15 = f32[10,128]{1,0:T(8,128)S(1)} collective-permute-done((f32[10,128]{1,0:T(8,128)S(1)}, f32[10,128]{1,0:T(8,128)S(1)}, u32[]{:S(2)}, u32[]{:S(2)}) %collective-permute-start.15) | collective-permute-done | bytes 5152 | tf_op jit(solution)/shard_map/ppermute | solution.py:25
  86.7 2.3 %fusion.29 = f32[2,40,16,128]{3,2,1,0:T(8,128)} fusion(f32[2,40,16,128]{3,2,1,0:T(8,128)S(1)} %fusion.17, f32[2,40,16,128]{3,2,1,0:T(8,128)S(1)} %convolution_bitcast_fusion.6, f32[2,40,16,128]{3,2,1,0:T(8,128)S(1)} %fusion.54, f32[2,40,16,128]{3,2,1,0:T(8,128)S(1)} %fusion.55, f32[2,40,16]{2,1,0:T(8,128)S(1)} %broadcast_in_dim.276, ...), kind=kOutput, calls=%fused_computation.57 | convolution fusion | flops 19169280 | bytes 4025632 | tf_op jit(solution)/shard_map/ab,...by->...ay/dot_general | solution.py:120
  (104 shorter events, 8.2 us)
Async XLA Ops:
  0.6 0.7 copy-start.17
  0.6 0.7 copy-start.27
  0.7 0.9 %copy-start.11 = (f32[16,16,1]{1,0,2:T(8,128)S(1)}, f32[16,16,1]{1,0,2:T(8,128)}, u32[]{:S(2)}) copy-start(f32[16,16,1]{1,0,2:T(8,128)} %constant.166) | copy-start | bytes 3076
  0.7 1.3 %copy-start.1 = (f32[4,40,16,128]{3,2,1,0:T(8,128)S(1)}, f32[4,40,16,128]{3,2,1,0:T(8,128)}, u32[]{:S(2)}) copy-start(f32[4,40,16,128]{3,2,1,0:T(8,128)} %param.41) | copy-start | bytes 3932164
  0.7 0.8 copy-start.16
  2.7 0.8 copy-start.10
  3.5 0.8 copy-start.7
  4.4 0.8 copy-start.6
  7.1 7.7 %collective-permute-start = (f32[20,128]{1,0:T(8,128)S(1)}, f32[20,128]{1,0:T(8,128)S(1)}, u32[]{:S(2)}, u32[]{:S(2)}) collective-permute-start(f32[20,128]{1,0:T(8,128)S(1)} %reshape_squeeze.39), channel_id=1, source_target_pairs={{0,1},{1,2},{2,3},{3,4},{4,5},{5,6},{6,7},{7,0},{8,9},{9,10},{10,1... | collective-permute-start | bytes 30728 | tf_op jit(solution)/shard_map/ppermute | solution.py:25
  10.1 4.7 %collective-permute-start.1 = (f32[20,128]{1,0:T(8,128)S(1)}, f32[20,128]{1,0:T(8,128)S(1)}, u32[]{:S(2)}, u32[]{:S(2)}) collective-permute-start(f32[20,128]{1,0:T(8,128)S(1)} %reshape_squeeze.40), channel_id=1, source_target_pairs={{0,7},{1,0},{2,1},{3,2},{4,3},{5,4},{6,5},{7,6},{8,15},{9,8},{10,9... | collective-permute-start | bytes 30728 | tf_op jit(solution)/shard_map/ppermute | solution.py:25
  13.3 18.9 %copy-start.18 = (pred[128]{0:T(512)(128)(4,1)}, pred[128]{0:T(512)(128)(4,1)S(1)}, u32[]{:S(2)}) copy-start(pred[128]{0:T(512)(128)(4,1)S(1)} %get-tuple-element.76) | copy-start | bytes 388
  13.3 18.9 %copy-start.20 = (pred[128]{0:T(512)(128)(4,1)}, pred[128]{0:T(512)(128)(4,1)S(1)}, u32[]{:S(2)}) copy-start(pred[128]{0:T(512)(128)(4,1)S(1)} %get-tuple-element.77) | copy-start | bytes 388
  15.0 5.0 %copy-start.13 = (f32[16,128]{1,0:T(8,128)S(1)}, f32[16,128]{1,0:T(8,128)}, u32[]{:S(2)}) copy-start(f32[16,128]{1,0:T(8,128)} %constant.165) | copy-start | bytes 24580
  15.0 5.0 %copy-start.14 = (f32[16,16,1]{1,0,2:T(8,128)S(1)}, f32[16,16,1]{1,0,2:T(8,128)}, u32[]{:S(2)}) copy-start(f32[16,16,1]{1,0,2:T(8,128)} %constant.170) | copy-start | bytes 3076
  16.0 3.9 %collective-permute-start.2 = (f32[160,128]{1,0:T(8,128)S(1)}, f32[160,128]{1,0:T(8,128)S(1)}, u32[]{:S(2)}, u32[]{:S(2)}) collective-permute-start(f32[160,128]{1,0:T(8,128)S(1)} %bitcast.153), channel_id=1, source_target_pairs={{0,8},{8,16},{16,24},{24,0},{1,9},{9,17},{17,25},{25,1},{2,10},{10... | collective-permute-start | bytes 245768 | tf_op jit(solution)/shard_map/ppermute | solution.py:23
  16.0 4.0 %collective-permute-start.3 = (f32[160,128]{1,0:T(8,128)S(1)}, f32[160,128]{1,0:T(8,128)S(1)}, u32[]{:S(2)}, u32[]{:S(2)}) collective-permute-start(f32[160,128]{1,0:T(8,128)S(1)} %bitcast.151), channel_id=1, source_target_pairs={{0,24},{8,0},{16,8},{24,16},{1,25},{9,1},{17,9},{25,17},{2,26},{10... | collective-permute-start | bytes 245768 | tf_op jit(solution)/shard_map/ppermute | solution.py:23
  17.8 19.6 %copy-start.22 = (pred[16]{0:T(512)(128)(4,1)}, pred[16]{0:T(512)(128)(4,1)S(1)}, u32[]{:S(2)}) copy-start(pred[16]{0:T(512)(128)(4,1)S(1)} %get-tuple-element.78) | copy-start | bytes 52
  17.8 19.6 %copy-start.24 = (pred[16]{0:T(512)(128)(4,1)}, pred[16]{0:T(512)(128)(4,1)S(1)}, u32[]{:S(2)}) copy-start(pred[16]{0:T(512)(128)(4,1)S(1)} %get-tuple-element.79) | copy-start | bytes 52
  25.5 6.5 %collective-permute-start.4 = (f32[20,128]{1,0:T(8,128)S(1)}, f32[20,128]{1,0:T(8,128)S(1)}, u32[]{:S(2)}, u32[]{:S(2)}) collective-permute-start(f32[20,128]{1,0:T(8,128)S(1)} %reshape_squeeze.41), channel_id=1, source_target_pairs={{0,1},{1,2},{2,3},{3,4},{4,5},{5,6},{6,7},{7,0},{8,9},{9,10},{10,1... | collective-permute-start | bytes 30728 | tf_op jit(solution)/shard_map/ppermute | solution.py:25
  27.0 5.1 %collective-permute-start.5 = (f32[20,128]{1,0:T(8,128)S(1)}, f32[20,128]{1,0:T(8,128)S(1)}, u32[]{:S(2)}, u32[]{:S(2)}) collective-permute-start(f32[20,128]{1,0:T(8,128)S(1)} %reshape_squeeze.42), channel_id=1, source_target_pairs={{0,7},{1,0},{2,1},{3,2},{4,3},{5,4},{6,5},{7,6},{8,15},{9,8},{10,9... | collective-permute-start | bytes 30728 | tf_op jit(solution)/shard_map/ppermute | solution.py:25
  32.2 2.8 %copy-start.26 = (s32[1,32]{1,0:T(1,128)S(1)}, s32[1,32]{1,0:T(1,128)}, u32[]{:S(2)}) copy-start(s32[1,32]{1,0:T(1,128)} %param.44) | copy-start | bytes 388
  32.2 3.5 %copy-start.15 = (s32[1,32,256]{2,1,0:T(8,128)S(1)}, s32[1,32,256]{2,1,0:T(8,128)}, u32[]{:S(2)}) copy-start(s32[1,32,256]{2,1,0:T(8,128)} %param.43) | copy-start | bytes 98308
  33.2 3.9 %collective-permute-start.6 = (f32[160,128]{1,0:T(8,128)S(1)}, f32[160,128]{1,0:T(8,128)S(1)}, u32[]{:S(2)}, u32[]{:S(2)}) collective-permute-start(f32[160,128]{1,0:T(8,128)S(1)} %bitcast.152), channel_id=1, source_target_pairs={{0,8},{8,16},{16,24},{24,0},{1,9},{9,17},{17,25},{25,1},{2,10},{10... | collective-permute-start | bytes 245768 | tf_op jit(solution)/shard_map/ppermute | solution.py:23
  34.1 3.3 %collective-permute-start.7 = (f32[160,128]{1,0:T(8,128)S(1)}, f32[160,128]{1,0:T(8,128)S(1)}, u32[]{:S(2)}, u32[]{:S(2)}) collective-permute-start(f32[160,128]{1,0:T(8,128)S(1)} %bitcast.150), channel_id=1, source_target_pairs={{0,24},{8,0},{16,8},{24,16},{1,25},{9,1},{17,9},{25,17},{2,26},{10... | collective-permute-start | bytes 245768 | tf_op jit(solution)/shard_map/ppermute | solution.py:23
  36.3 26.3 %copy-start = (f32[2,40,16,128]{3,2,1,0:T(8,128)S(1)}, f32[2,40,16,128]{3,2,1,0:T(8,128)}, u32[]{:S(2)}) copy-start(f32[2,40,16,128]{3,2,1,0:T(8,128)} %param.45) | copy-start | bytes 1966084
  38.3 25.7 %copy-start.3 = (f32[160,16,128]{2,1,0:T(8,128)}, f32[160,16,128]{2,1,0:T(8,128)S(1)}, u32[]{:S(2)}) copy-start(f32[160,16,128]{2,1,0:T(8,128)S(1)} %fusion.9) | copy-start | bytes 3932164
  39.0 25.0 %copy-start.12 = (f32[16,16,1,1]{1,0,3,2:T(8,128)S(1)}, f32[16,16,1,1]{1,0,3,2:T(8,128)}, u32[]{:S(2)}) copy-start(f32[16,16,1,1]{1,0,3,2:T(8,128)} %constant.173) | copy-start | bytes 3076
  62.7 1.7 %copy-start.9 = (f32[128,128,1,1]{1,0,3,2:T(8,128)S(1)}, f32[128,128,1,1]{1,0,3,2:T(8,128)}, u32[]{:S(2)}) copy-start(f32[128,128,1,1]{1,0,3,2:T(8,128)} %constant.172) | copy-start | bytes 196612
  64.0 0.9 copy-start.8
  64.4 4.3 %copy-start.2 = (f32[2,40,16,128]{3,2,1,0:T(8,128)S(1)}, f32[2,40,16,128]{3,2,1,0:T(8,128)}, u32[]{:S(2)}) copy-start(f32[2,40,16,128]{3,2,1,0:T(8,128)} %param.46) | copy-start | bytes 1966084
  66.0 3.9 %collective-permute-start.10 = (f32[10,128]{1,0:T(8,128)}, f32[10,128]{1,0:T(8,128)S(1)}, u32[]{:S(2)}, u32[]{:S(2)}) collective-permute-start(f32[10,128]{1,0:T(8,128)} %reshape_squeeze.46), channel_id=1, source_target_pairs={{0,7},{1,0},{2,1},{3,2},{4,3},{5,4},{6,5},{7,6},{8,15},{9,8},{10,9... | collective-permute-start | bytes 15368 | tf_op jit(solution)/shard_map/ppermute | solution.py:25
  68.1 6.5 %collective-permute-start.11 = (f32[10,128]{1,0:T(8,128)S(1)}, f32[10,128]{1,0:T(8,128)}, u32[]{:S(2)}, u32[]{:S(2)}) collective-permute-start(f32[10,128]{1,0:T(8,128)S(1)} %reshape_squeeze.47), channel_id=1, source_target_pairs={{0,1},{1,2},{2,3},{3,4},{4,5},{5,6},{6,7},{7,0},{8,9},{9,10},{10,1... | collective-permute-start | bytes 15368 | tf_op jit(solution)/shard_map/ppermute | solution.py:25
  68.1 7.2 %collective-permute-start.8 = (f32[80,128]{1,0:T(8,128)}, f32[80,128]{1,0:T(8,128)}, u32[]{:S(2)}, u32[]{:S(2)}) collective-permute-start(f32[80,128]{1,0:T(8,128)} %bitcast.155), channel_id=1, source_target_pairs={{0,24},{8,0},{16,8},{24,16},{1,25},{9,1},{17,9},{25,17},{2,26},{10... | collective-permute-start | bytes 122888 | tf_op jit(solution)/shard_map/ppermute | solution.py:23
  68.2 7.2 %collective-permute-start.9 = (f32[80,128]{1,0:T(8,128)S(1)}, f32[80,128]{1,0:T(8,128)}, u32[]{:S(2)}, u32[]{:S(2)}) collective-permute-start(f32[80,128]{1,0:T(8,128)S(1)} %bitcast.154), channel_id=1, source_target_pairs={{0,8},{8,16},{16,24},{24,0},{1,9},{9,17},{17,25},{25,1},{2,10},{10... | collective-permute-start | bytes 122888 | tf_op jit(solution)/shard_map/ppermute | solution.py:23
  68.7 6.7 %copy-start.19 = (pred[128]{0:T(512)(128)(4,1)S(1)}, pred[128]{0:T(512)(128)(4,1)}, u32[]{:S(2)}) copy-start(pred[128]{0:T(512)(128)(4,1)} %copy-done.18) | copy-start | bytes 388
  68.7 6.7 %copy-start.21 = (pred[128]{0:T(512)(128)(4,1)S(1)}, pred[128]{0:T(512)(128)(4,1)}, u32[]{:S(2)}) copy-start(pred[128]{0:T(512)(128)(4,1)} %copy-done.20) | copy-start | bytes 388
  68.7 6.7 %copy-start.23 = (pred[16]{0:T(512)(128)(4,1)S(1)}, pred[16]{0:T(512)(128)(4,1)}, u32[]{:S(2)}) copy-start(pred[16]{0:T(512)(128)(4,1)} %copy-done.22) | copy-start | bytes 52
  68.7 6.7 %copy-start.25 = (pred[16]{0:T(512)(128)(4,1)S(1)}, pred[16]{0:T(512)(128)(4,1)}, u32[]{:S(2)}) copy-start(pred[16]{0:T(512)(128)(4,1)} %copy-done.24) | copy-start | bytes 52
  78.1 8.5 %copy-start.4 = (f32[40,16,128]{2,1,0:T(8,128)S(1)}, f32[40,16,128]{2,1,0:T(8,128)}, u32[]{:S(2)}) copy-start(f32[40,16,128]{2,1,0:T(8,128)} %get-tuple-element.68) | copy-start | bytes 983044
  78.1 8.5 %copy-start.5 = (f32[40,16,128]{2,1,0:T(8,128)S(1)}, f32[40,16,128]{2,1,0:T(8,128)}, u32[]{:S(2)}) copy-start(f32[40,16,128]{2,1,0:T(8,128)} %get-tuple-element.69) | copy-start | bytes 983044
  78.9 3.7 %collective-permute-start.14 = (f32[10,128]{1,0:T(8,128)S(1)}, f32[10,128]{1,0:T(8,128)S(1)}, u32[]{:S(2)}, u32[]{:S(2)}) collective-permute-start(f32[10,128]{1,0:T(8,128)S(1)} %reshape_squeeze.50), channel_id=1, source_target_pairs={{0,7},{1,0},{2,1},{3,2},{4,3},{5,4},{6,5},{7,6},{8,15},{9,8},{10,9... | collective-permute-start | bytes 15368 | tf_op jit(solution)/shard_map/ppermute | solution.py:25
  80.2 6.4 %collective-permute-start.15 = (f32[10,128]{1,0:T(8,128)S(1)}, f32[10,128]{1,0:T(8,128)S(1)}, u32[]{:S(2)}, u32[]{:S(2)}) collective-permute-start(f32[10,128]{1,0:T(8,128)S(1)} %reshape_squeeze.51), channel_id=1, source_target_pairs={{0,1},{1,2},{2,3},{3,4},{4,5},{5,6},{6,7},{7,0},{8,9},{9,10},{10,1... | collective-permute-start | bytes 15368 | tf_op jit(solution)/shard_map/ppermute | solution.py:25
  81.0 5.6 %collective-permute-start.12 = (f32[80,128]{1,0:T(8,128)S(1)}, f32[80,128]{1,0:T(8,128)S(1)}, u32[]{:S(2)}, u32[]{:S(2)}) collective-permute-start(f32[80,128]{1,0:T(8,128)S(1)} %bitcast.157), channel_id=1, source_target_pairs={{0,24},{8,0},{16,8},{24,16},{1,25},{9,1},{17,9},{25,17},{2,26},{10... | collective-permute-start | bytes 122888 | tf_op jit(solution)/shard_map/ppermute | solution.py:23
  81.0 5.6 %collective-permute-start.13 = (f32[80,128]{1,0:T(8,128)S(1)}, f32[80,128]{1,0:T(8,128)S(1)}, u32[]{:S(2)}, u32[]{:S(2)}) collective-permute-start(f32[80,128]{1,0:T(8,128)S(1)} %bitcast.156), channel_id=1, source_target_pairs={{0,8},{8,16},{16,24},{24,0},{1,9},{9,17},{17,25},{25,1},{2,10},{10... | collective-permute-start | bytes 122888 | tf_op jit(solution)/shard_map/ppermute | solution.py:23

commit v22 on v21

--- a/solution.py
+++ b/solution.py
@@ -1,3 +1,4 @@
+import functools
 import math
 
 import jax
@@ -166,9 +167,9 @@
     )
 
 
-def gather_kernel(index_ref, scale_ref, table_ref, out_ref):
+def gather_kernel(index_ref, scale_ref, table_ref, out_ref, per=1):
     fields, rows, lanes = table_ref.shape
-    tile = out_ref.shape[1]
+    tile = index_ref.shape[1]
     index = index_ref[...]
     onehot = (lax.broadcasted_iota(jnp.int32, (lanes, tile), 0) == (index % lanes)).astype(jnp.bfloat16)
     select = lax.broadcasted_iota(jnp.int32, (rows, tile), 0) == (index // lanes)
@@ -185,6 +186,11 @@
         [jnp.sum(jnp.where(select, picked[f * rows : (f + 1) * rows], 0.0), axis=0, keepdims=True) for f in range(fields)],
         axis=0,
     ) * scale
+    width = out_ref.shape[1]
+    total = values[:, :width]
+    for chunk in range(1, per):
+        total = total + values[:, chunk * width : (chunk + 1) * width]
+    values = total
 
     @pl.when(pl.program_id(1) == 0)
     def first():
@@ -204,12 +210,13 @@
     while tile < 8192 and width % (2 * tile) == 0 and fields * rows * tile * 8 <= 4 * 2**20:
         tile *= 2
     blocks = width // tile
+    per = groups if blocks == 1 and fields * rows * count * 8 <= 16 * 2**20 else 1
     return pl.pallas_call(
-        gather_kernel,
-        grid=(blocks, groups),
+        functools.partial(gather_kernel, per=per),
+        grid=(blocks, groups // per),
         in_specs=[
-            pl.BlockSpec((1, tile), lambda step, group: (0, group * blocks + step)),
-            pl.BlockSpec((1, tile), lambda step, group: (0, group * blocks + step)),
+            pl.BlockSpec((1, per * tile), lambda step, group: (0, group * blocks + step)),
+            pl.BlockSpec((1, per * tile), lambda step, group: (0, group * blocks + step)),
             pl.BlockSpec((fields, rows, lanes), lambda step, group: (0, 0, 0)),
         ],
         out_specs=pl.BlockSpec((fields, tile), lambda step, group: (0, step)),

time: 89.6 us -> 89.4 us (level)
  no operation moved by 1% of the time
where the time goes in v22:
time: 89.4 us; the launch traced here: 88.7 us
  starting transfers between devices  19.8 us (22%)
  waiting for transfers between devices  15.7 us (18%)
  matrix products  15.1 us (17%)
  blocking collectives  14.5 us (16%)
  local copies, waits for them, and re-layouts  10.7 us (12%)
  Pallas kernels  7.24 us (8%)
  other arithmetic  4.39 us (5%)
  between operations  1.27 us (1%)
    ppermute x8, starting transfers between devices, neighbour(): lax.ppermute(values, 'gy', [(j, (j + step_y) % count_y) for j in range(co...  15.1 us
    all_to_all x1, blocking collectives, per_device(): lax.all_to_all(payload, ('gx', 'gy'), split_axis=1, concat_axis=1, tiled=...  14.5 us
    ppermute x8, waiting for transfers between devices, neighbour(): lax.ppermute(values, 'gy', [(j, (j + step_y) % count_y) for j in range(co...  12.4 us
    pallas_call x2, Pallas kernels, onehot_gather(): pl.pallas_call(functools.partial(gather_kernel, per=per), grid=(blocks, g...  7.24 us
    ppermute x8, starting transfers between devices, neighbour(): lax.ppermute(values, 'gx', [(i, (i + step_x) % count_x) for i in range(co...  4.67 us
    dot_general x2, matrix products, tracer_step(): jnp.einsum('ab,...by->...ay', sum_x, tracers, precision=precision)  4.15 us
    ppermute x8, waiting for transfers between devices, neighbour(): lax.ppermute(values, 'gx', [(i, (i + step_x) % count_x) for i in range(co...  3.3 us
    unnamed x58, local copies, waits for them, and re-layouts  3.05 us
  transfers between devices with their start and end apart: 16, of which 10 were waited for; matrix products, arithmetic and copies ran while one was open for 5% of the time, Pallas kernels for 0%

profile of v22, /device:TPU:0, one launch (start us, length us, event | category | flops | bytes accessed | tf_op | source)
XLA Modules:
  0.0 88.7 jit_solution(6347182400957523687)
XLA Ops:
  0.7 0.6 copy-done.17
  2.0 0.7 fusion.10
  2.7 0.7 convolution_bitcast_fusion.5
  3.5 0.7 fusion.50
  4.4 0.7 fusion.2
  5.2 0.7 fusion.1
  5.9 1.1 %slice_reduce_fusion.3 = (f32[160,16]{1,0:T(8,128)S(1)}, f32[160,16]{1,0:T(8,128)S(1)}) fusion(f32[160,16,128]{2,1,0:T(8,128)S(1)} %fusion.1), kind=kLoop, calls=%fused_computation.24 | loop fusion | bytes 40960 | tf_op jit(solution)/shard_map/slice | solution.py:88
  7.1 3.0 %collective-permute-start = (f32[20,128]{1,0:T(8,128)S(1)}, f32[20,128]{1,0:T(8,128)S(1)}, u32[]{:S(2)}, u32[]{:S(2)}) collective-permute-start(f32[20,128]{1,0:T(8,128)S(1)} %reshape_squeeze.39), channel_id=1, source_target_pairs={{0,1},{1,2},{2,3},{3,4},{4,5},{5,6},{6,7},{7,0},{8,9},{9,10},{10,1... | collective-permute-start | bytes 30728 | tf_op jit(solution)/shard_map/ppermute | solution.py:26
  10.1 3.1 %collective-permute-start.1 = (f32[20,128]{1,0:T(8,128)S(1)}, f32[20,128]{1,0:T(8,128)S(1)}, u32[]{:S(2)}, u32[]{:S(2)}) collective-permute-start(f32[20,128]{1,0:T(8,128)S(1)} %reshape_squeeze.40), channel_id=1, source_target_pairs={{0,7},{1,0},{2,1},{3,2},{4,3},{5,4},{6,5},{7,6},{8,15},{9,8},{10,9... | collective-permute-start | bytes 30728 | tf_op jit(solution)/shard_map/ppermute | solution.py:26
  13.3 1.5 %collective-permute-done = f32[20,128]{1,0:T(8,128)S(1)} collective-permute-done((f32[20,128]{1,0:T(8,128)S(1)}, f32[20,128]{1,0:T(8,128)S(1)}, u32[]{:S(2)}, u32[]{:S(2)}) %collective-permute-start) | collective-permute-done | bytes 10272 | tf_op jit(solution)/shard_map/ppermute | solution.py:26
  15.0 0.8 select_add_fusion.1
  16.0 1.7 %collective-permute-start.3 = (f32[160,128]{1,0:T(8,128)S(1)}, f32[160,128]{1,0:T(8,128)S(1)}, u32[]{:S(2)}, u32[]{:S(2)}) collective-permute-start(f32[160,128]{1,0:T(8,128)S(1)} %bitcast.151), channel_id=1, source_target_pairs={{0,24},{8,0},{16,8},{24,16},{1,25},{9,1},{17,9},{25,17},{2,26},{10... | collective-permute-start | bytes 245768 | tf_op jit(solution)/shard_map/ppermute | solution.py:24
  17.8 2.1 %collective-permute-done.2 = f32[160,128]{1,0:T(8,128)S(1)} collective-permute-done((f32[160,128]{1,0:T(8,128)S(1)}, f32[160,128]{1,0:T(8,128)S(1)}, u32[]{:S(2)}, u32[]{:S(2)}) %collective-permute-start.2) | collective-permute-done | bytes 81952 | tf_op jit(solution)/shard_map/ppermute | solution.py:24
  20.0 0.8 fusion.5
  20.8 0.7 fusion.6
  21.5 0.7 convolution_multiply_fusion.1
  22.2 0.7 convolution_bitcast_fusion.2
  22.9 0.7 fusion.51
  23.6 0.7 fusion
  24.3 1.1 %slice_reduce_fusion.1 = (f32[160,16]{1,0:T(8,128)S(1)}, f32[160,16]{1,0:T(8,128)S(1)}) fusion(f32[160,16,128]{2,1,0:T(8,128)S(1)} %fusion), kind=kLoop, calls=%fused_computation.22 | loop fusion | bytes 40960 | tf_op jit(solution)/shard_map/slice | solution.py:88
  25.5 1.4 %collective-permute-start.4 = (f32[20,128]{1,0:T(8,128)S(1)}, f32[20,128]{1,0:T(8,128)S(1)}, u32[]{:S(2)}, u32[]{:S(2)}) collective-permute-start(f32[20,128]{1,0:T(8,128)S(1)} %reshape_squeeze.41), channel_id=1, source_target_pairs={{0,1},{1,2},{2,3},{3,4},{4,5},{5,6},{6,7},{7,0},{8,9},{9,10},{10,1... | collective-permute-start | bytes 30728 | tf_op jit(solution)/shard_map/ppermute | solution.py:26
  27.0 3.4 %collective-permute-start.5 = (f32[20,128]{1,0:T(8,128)S(1)}, f32[20,128]{1,0:T(8,128)S(1)}, u32[]{:S(2)}, u32[]{:S(2)}) collective-permute-start(f32[20,128]{1,0:T(8,128)S(1)} %reshape_squeeze.42), channel_id=1, source_target_pairs={{0,7},{1,0},{2,1},{3,2},{4,3},{5,4},{6,5},{7,6},{8,15},{9,8},{10,9... | collective-permute-start | bytes 30728 | tf_op jit(solution)/shard_map/ppermute | solution.py:26
  30.4 1.5 %collective-permute-done.4 = f32[20,128]{1,0:T(8,128)S(1)} collective-permute-done((f32[20,128]{1,0:T(8,128)S(1)}, f32[20,128]{1,0:T(8,128)S(1)}, u32[]{:S(2)}, u32[]{:S(2)}) %collective-permute-start.4) | collective-permute-done | bytes 10272 | tf_op jit(solution)/shard_map/ppermute | solution.py:26
  32.2 0.8 select_add_fusion
  33.2 0.9 %collective-permute-start.6 = (f32[160,128]{1,0:T(8,128)S(1)}, f32[160,128]{1,0:T(8,128)S(1)}, u32[]{:S(2)}, u32[]{:S(2)}) collective-permute-start(f32[160,128]{1,0:T(8,128)S(1)} %bitcast.152), channel_id=1, source_target_pairs={{0,8},{8,16},{16,24},{24,0},{1,9},{9,17},{17,25},{25,1},{2,10},{10... | collective-permute-start | bytes 245768 | tf_op jit(solution)/shard_map/ppermute | solution.py:24
  34.1 0.9 collective-permute-start.7
  35.1 0.6 copy.52
  35.7 0.6 copy.51
  36.3 0.8 collective-permute-done.6
  37.4 0.8 fusion.9
  38.3 0.7 fusion.37.table_ref
  39.0 2.8 %shard_map.320 = f32[4,8192]{1,0:T(4,128)} custom-call(s32[1,8192]{1,0:T(1,128)} %bitcast.149, f32[1,8192]{1,0:T(1,128)} %bitcast.148, f32[4,16,128]{2,1,0:T(8,128)} %fusion.37.table_ref), custom_call_target="tpu_custom_call" | custom-call | tf_op jit(solution)/shard_map/pallas_call | solution.py:214
  41.8 14.5 %all_to_all.5 = f32[4,32,256]{2,0,1:T(4,128)S(1)} all-to-all(f32[4,32,256]{2,0,1:T(4,128)} %bitcast.147), channel_id=1, replica_groups=mesh['gx'=4,'gy'=8] {'gx','gy'}, dimensions={1} | all-to-all | bytes 262144 | tf_op jit(solution)/shard_map/all_to_all | solution.py:254
  56.4 0.7 copy.41.table_ref
  57.1 4.4 %shard_map.321 = f32[4,2048]{1,0:T(4,128)} custom-call(s32[1,8192]{1,0:T(1,128)} %bitcast.158, f32[1,8192]{1,0:T(1,128)} %bitcast.159, f32[4,32,256]{2,1,0:T(8,128)} %copy.41.table_ref), custom_call_target="tpu_custom_call" | custom-call | tf_op jit(solution)/shard_map/pallas_call | solution.py:214
  61.5 1.0 %fusion.38 = (f32[1,2048]{1,0:T(1,128)S(1)}, f32[1,2048]{1,0:T(1,128)S(1)}, f32[1,2048]{1,0:T(1,128)S(1)}, f32[1,2048]{1,0:T(1,128)S(1)}) fusion(f32[4,2048]{1,0:T(4,128)} %shard_map.321), kind=kLoop, calls=%fused_computation.76 | loop fusion | flops 8192 | bytes 65536 | tf_op jit(solution)/shard_map/mul | solution.py:258
  63.1 0.7 fusion.49
  65.0 0.7 reshape_squeeze.46
  65.7 2.0 %collective-permute-start.10 = (f32[10,128]{1,0:T(8,128)}, f32[10,128]{1,0:T(8,128)S(1)}, u32[]{:S(2)}, u32[]{:S(2)}) collective-permute-start(f32[10,128]{1,0:T(8,128)} %reshape_squeeze.46), channel_id=1, source_target_pairs={{0,7},{1,0},{2,1},{3,2},{4,3},{5,4},{6,5},{7,6},{8,15},{9,8},{10,9... | collective-permute-start | bytes 15368 | tf_op jit(solution)/shard_map/ppermute | solution.py:26
  68.5 0.9 fusion.36
  69.6 4.7 %collective-permute-done.11 = f32[10,128]{1,0:T(8,128)} collective-permute-done((f32[10,128]{1,0:T(8,128)S(1)}, f32[10,128]{1,0:T(8,128)}, u32[]{:S(2)}, u32[]{:S(2)}) %collective-permute-start.11) | collective-permute-done | bytes 5152 | tf_op jit(solution)/shard_map/ppermute | solution.py:26
  74.3 0.8 broadcast_in_dim.268
  75.1 1.9 %fusion.17 = f32[2,40,16,128]{3,2,1,0:T(8,128)S(1)} fusion(f32[2,40,16,128]{3,2,1,0:T(8,128)S(1)} %fusion.41, f32[2,40,16,128]{3,2,1,0:T(8,128)S(1)} %convolution_bitcast_fusion.8, f32[2,40,16,128]{3,2,1,0:T(8,128)S(1)} %fusion.52, f32[2,40,16,128]{3,2,1,0:T(8,128)S(1)} %fusion.53, f32[40,16,128]{2,1,0:T(8,128)} %get-tuple-element.69, ...), kind=kOutput, calls=%fused_computation.45 | convolution fusion | flops 19169280 | bytes 4025632 | tf_op jit(solution)/shard_map/ab,...by->...ay/dot_general | solution.py:121
  78.6 1.2 %collective-permute-start.14 = (f32[10,128]{1,0:T(8,128)S(1)}, f32[10,128]{1,0:T(8,128)S(1)}, u32[]{:S(2)}, u32[]{:S(2)}) collective-permute-start(f32[10,128]{1,0:T(8,128)S(1)} %reshape_squeeze.50), channel_id=1, source_target_pairs={{0,7},{1,0},{2,1},{3,2},{4,3},{5,4},{6,5},{7,6},{8,15},{9,8},{10,9... | collective-permute-start | bytes 15368 | tf_op jit(solution)/shard_map/ppermute | solution.py:26
  79.9 0.9 collective-permute-start.15
  81.7 0.6 collective-permute-done.14
  82.4 3.9 %collective-permute-done.15 = f32[10,128]{1,0:T(8,128)S(1)} collective-permute-done((f32[10,128]{1,0:T(8,128)S(1)}, f32[10,128]{1,0:T(8,128)S(1)}, u32[]{:S(2)}, u32[]{:S(2)}) %collective-permute-start.15) | collective-permute-done | bytes 5152 | tf_op jit(solution)/shard_map/ppermute | solution.py:26
  86.4 2.3 %fusion.29 = f32[2,40,16,128]{3,2,1,0:T(8,128)} fusion(f32[2,40,16,128]{3,2,1,0:T(8,128)S(1)} %fusion.17, f32[2,40,16,128]{3,2,1,0:T(8,128)S(1)} %convolution_bitcast_fusion.6, f32[2,40,16,128]{3,2,1,0:T(8,128)S(1)} %fusion.54, f32[2,40,16,128]{3,2,1,0:T(8,128)S(1)} %fusion.55, f32[2,40,16]{2,1,0:T(8,128)S(1)} %broadcast_in_dim.276, ...), kind=kOutput, calls=%fused_computation.57 | convolution fusion | flops 19169280 | bytes 4025632 | tf_op jit(solution)/shard_map/ab,...by->...ay/dot_general | solution.py:121
  (104 shorter events, 8.2 us)
Async XLA Ops:
  0.6 0.7 copy-start.17
  0.6 0.7 copy-start.27
  0.7 0.9 %copy-start.11 = (f32[16,16,1]{1,0,2:T(8,128)S(1)}, f32[16,16,1]{1,0,2:T(8,128)}, u32[]{:S(2)}) copy-start(f32[16,16,1]{1,0,2:T(8,128)} %constant.166) | copy-start | bytes 3076
  0.7 1.3 %copy-start.1 = (f32[4,40,16,128]{3,2,1,0:T(8,128)S(1)}, f32[4,40,16,128]{3,2,1,0:T(8,128)}, u32[]{:S(2)}) copy-start(f32[4,40,16,128]{3,2,1,0:T(8,128)} %param.41) | copy-start | bytes 3932164
  0.7 0.8 copy-start.16
  2.7 0.8 copy-start.10
  3.5 0.8 copy-start.7
  4.4 0.8 copy-start.6
  7.1 7.7 %collective-permute-start = (f32[20,128]{1,0:T(8,128)S(1)}, f32[20,128]{1,0:T(8,128)S(1)}, u32[]{:S(2)}, u32[]{:S(2)}) collective-permute-start(f32[20,128]{1,0:T(8,128)S(1)} %reshape_squeeze.39), channel_id=1, source_target_pairs={{0,1},{1,2},{2,3},{3,4},{4,5},{5,6},{6,7},{7,0},{8,9},{9,10},{10,1... | collective-permute-start | bytes 30728 | tf_op jit(solution)/shard_map/ppermute | solution.py:26
  10.1 4.7 %collective-permute-start.1 = (f32[20,128]{1,0:T(8,128)S(1)}, f32[20,128]{1,0:T(8,128)S(1)}, u32[]{:S(2)}, u32[]{:S(2)}) collective-permute-start(f32[20,128]{1,0:T(8,128)S(1)} %reshape_squeeze.40), channel_id=1, source_target_pairs={{0,7},{1,0},{2,1},{3,2},{4,3},{5,4},{6,5},{7,6},{8,15},{9,8},{10,9... | collective-permute-start | bytes 30728 | tf_op jit(solution)/shard_map/ppermute | solution.py:26
  13.3 18.9 %copy-start.18 = (pred[128]{0:T(512)(128)(4,1)}, pred[128]{0:T(512)(128)(4,1)S(1)}, u32[]{:S(2)}) copy-start(pred[128]{0:T(512)(128)(4,1)S(1)} %get-tuple-element.76) | copy-start | bytes 388
  13.3 18.9 %copy-start.20 = (pred[128]{0:T(512)(128)(4,1)}, pred[128]{0:T(512)(128)(4,1)S(1)}, u32[]{:S(2)}) copy-start(pred[128]{0:T(512)(128)(4,1)S(1)} %get-tuple-element.77) | copy-start | bytes 388
  15.0 5.0 %copy-start.13 = (f32[16,128]{1,0:T(8,128)S(1)}, f32[16,128]{1,0:T(8,128)}, u32[]{:S(2)}) copy-start(f32[16,128]{1,0:T(8,128)} %constant.165) | copy-start | bytes 24580
  15.0 5.0 %copy-start.14 = (f32[16,16,1]{1,0,2:T(8,128)S(1)}, f32[16,16,1]{1,0,2:T(8,128)}, u32[]{:S(2)}) copy-start(f32[16,16,1]{1,0,2:T(8,128)} %constant.170) | copy-start | bytes 3076
  16.0 3.9 %collective-permute-start.2 = (f32[160,128]{1,0:T(8,128)S(1)}, f32[160,128]{1,0:T(8,128)S(1)}, u32[]{:S(2)}, u32[]{:S(2)}) collective-permute-start(f32[160,128]{1,0:T(8,128)S(1)} %bitcast.153), channel_id=1, source_target_pairs={{0,8},{8,16},{16,24},{24,0},{1,9},{9,17},{17,25},{25,1},{2,10},{10... | collective-permute-start | bytes 245768 | tf_op jit(solution)/shard_map/ppermute | solution.py:24
  16.0 4.0 %collective-permute-start.3 = (f32[160,128]{1,0:T(8,128)S(1)}, f32[160,128]{1,0:T(8,128)S(1)}, u32[]{:S(2)}, u32[]{:S(2)}) collective-permute-start(f32[160,128]{1,0:T(8,128)S(1)} %bitcast.151), channel_id=1, source_target_pairs={{0,24},{8,0},{16,8},{24,16},{1,25},{9,1},{17,9},{25,17},{2,26},{10... | collective-permute-start | bytes 245768 | tf_op jit(solution)/shard_map/ppermute | solution.py:24
  17.8 19.6 %copy-start.22 = (pred[16]{0:T(512)(128)(4,1)}, pred[16]{0:T(512)(128)(4,1)S(1)}, u32[]{:S(2)}) copy-start(pred[16]{0:T(512)(128)(4,1)S(1)} %get-tuple-element.78) | copy-start | bytes 52
  17.8 19.6 %copy-start.24 = (pred[16]{0:T(512)(128)(4,1)}, pred[16]{0:T(512)(128)(4,1)S(1)}, u32[]{:S(2)}) copy-start(pred[16]{0:T(512)(128)(4,1)S(1)} %get-tuple-element.79) | copy-start | bytes 52
  25.5 6.5 %collective-permute-start.4 = (f32[20,128]{1,0:T(8,128)S(1)}, f32[20,128]{1,0:T(8,128)S(1)}, u32[]{:S(2)}, u32[]{:S(2)}) collective-permute-start(f32[20,128]{1,0:T(8,128)S(1)} %reshape_squeeze.41), channel_id=1, source_target_pairs={{0,1},{1,2},{2,3},{3,4},{4,5},{5,6},{6,7},{7,0},{8,9},{9,10},{10,1... | collective-permute-start | bytes 30728 | tf_op jit(solution)/shard_map/ppermute | solution.py:26
  27.0 5.1 %collective-permute-start.5 = (f32[20,128]{1,0:T(8,128)S(1)}, f32[20,128]{1,0:T(8,128)S(1)}, u32[]{:S(2)}, u32[]{:S(2)}) collective-permute-start(f32[20,128]{1,0:T(8,128)S(1)} %reshape_squeeze.42), channel_id=1, source_target_pairs={{0,7},{1,0},{2,1},{3,2},{4,3},{5,4},{6,5},{7,6},{8,15},{9,8},{10,9... | collective-permute-start | bytes 30728 | tf_op jit(solution)/shard_map/ppermute | solution.py:26
  32.2 2.8 %copy-start.26 = (s32[1,32]{1,0:T(1,128)S(1)}, s32[1,32]{1,0:T(1,128)}, u32[]{:S(2)}) copy-start(s32[1,32]{1,0:T(1,128)} %param.44) | copy-start | bytes 388
  32.2 3.5 %copy-start.15 = (s32[1,32,256]{2,1,0:T(8,128)S(1)}, s32[1,32,256]{2,1,0:T(8,128)}, u32[]{:S(2)}) copy-start(s32[1,32,256]{2,1,0:T(8,128)} %param.43) | copy-start | bytes 98308
  33.2 3.9 %collective-permute-start.6 = (f32[160,128]{1,0:T(8,128)S(1)}, f32[160,128]{1,0:T(8,128)S(1)}, u32[]{:S(2)}, u32[]{:S(2)}) collective-permute-start(f32[160,128]{1,0:T(8,128)S(1)} %bitcast.152), channel_id=1, source_target_pairs={{0,8},{8,16},{16,24},{24,0},{1,9},{9,17},{17,25},{25,1},{2,10},{10... | collective-permute-start | bytes 245768 | tf_op jit(solution)/shard_map/ppermute | solution.py:24
  34.1 3.3 %collective-permute-start.7 = (f32[160,128]{1,0:T(8,128)S(1)}, f32[160,128]{1,0:T(8,128)S(1)}, u32[]{:S(2)}, u32[]{:S(2)}) collective-permute-start(f32[160,128]{1,0:T(8,128)S(1)} %bitcast.150), channel_id=1, source_target_pairs={{0,24},{8,0},{16,8},{24,16},{1,25},{9,1},{17,9},{25,17},{2,26},{10... | collective-permute-start | bytes 245768 | tf_op jit(solution)/shard_map/ppermute | solution.py:24
  36.3 26.1 %copy-start = (f32[2,40,16,128]{3,2,1,0:T(8,128)S(1)}, f32[2,40,16,128]{3,2,1,0:T(8,128)}, u32[]{:S(2)}) copy-start(f32[2,40,16,128]{3,2,1,0:T(8,128)} %param.45) | copy-start | bytes 1966084
  38.3 25.5 %copy-start.3 = (f32[160,16,128]{2,1,0:T(8,128)}, f32[160,16,128]{2,1,0:T(8,128)S(1)}, u32[]{:S(2)}) copy-start(f32[160,16,128]{2,1,0:T(8,128)S(1)} %fusion.9) | copy-start | bytes 3932164
  39.0 24.8 %copy-start.12 = (f32[16,16,1,1]{1,0,3,2:T(8,128)S(1)}, f32[16,16,1,1]{1,0,3,2:T(8,128)}, u32[]{:S(2)}) copy-start(f32[16,16,1,1]{1,0,3,2:T(8,128)} %constant.173) | copy-start | bytes 3076
  62.4 1.7 %copy-start.9 = (f32[128,128,1,1]{1,0,3,2:T(8,128)S(1)}, f32[128,128,1,1]{1,0,3,2:T(8,128)}, u32[]{:S(2)}) copy-start(f32[128,128,1,1]{1,0,3,2:T(8,128)} %constant.172) | copy-start | bytes 196612
  63.7 0.9 copy-start.8
  64.2 4.3 %copy-start.2 = (f32[2,40,16,128]{3,2,1,0:T(8,128)S(1)}, f32[2,40,16,128]{3,2,1,0:T(8,128)}, u32[]{:S(2)}) copy-start(f32[2,40,16,128]{3,2,1,0:T(8,128)} %param.46) | copy-start | bytes 1966084
  65.7 3.9 %collective-permute-start.10 = (f32[10,128]{1,0:T(8,128)}, f32[10,128]{1,0:T(8,128)S(1)}, u32[]{:S(2)}, u32[]{:S(2)}) collective-permute-start(f32[10,128]{1,0:T(8,128)} %reshape_squeeze.46), channel_id=1, source_target_pairs={{0,7},{1,0},{2,1},{3,2},{4,3},{5,4},{6,5},{7,6},{8,15},{9,8},{10,9... | collective-permute-start | bytes 15368 | tf_op jit(solution)/shard_map/ppermute | solution.py:26
  67.8 6.5 %collective-permute-start.11 = (f32[10,128]{1,0:T(8,128)S(1)}, f32[10,128]{1,0:T(8,128)}, u32[]{:S(2)}, u32[]{:S(2)}) collective-permute-start(f32[10,128]{1,0:T(8,128)S(1)} %reshape_squeeze.47), channel_id=1, source_target_pairs={{0,1},{1,2},{2,3},{3,4},{4,5},{5,6},{6,7},{7,0},{8,9},{9,10},{10,1... | collective-permute-start | bytes 15368 | tf_op jit(solution)/shard_map/ppermute | solution.py:26
  67.9 7.2 %collective-permute-start.8 = (f32[80,128]{1,0:T(8,128)}, f32[80,128]{1,0:T(8,128)}, u32[]{:S(2)}, u32[]{:S(2)}) collective-permute-start(f32[80,128]{1,0:T(8,128)} %bitcast.155), channel_id=1, source_target_pairs={{0,24},{8,0},{16,8},{24,16},{1,25},{9,1},{17,9},{25,17},{2,26},{10... | collective-permute-start | bytes 122888 | tf_op jit(solution)/shard_map/ppermute | solution.py:24
  67.9 7.2 %collective-permute-start.9 = (f32[80,128]{1,0:T(8,128)S(1)}, f32[80,128]{1,0:T(8,128)}, u32[]{:S(2)}, u32[]{:S(2)}) collective-permute-start(f32[80,128]{1,0:T(8,128)S(1)} %bitcast.154), channel_id=1, source_target_pairs={{0,8},{8,16},{16,24},{24,0},{1,9},{9,17},{17,25},{25,1},{2,10},{10... | collective-permute-start | bytes 122888 | tf_op jit(solution)/shard_map/ppermute | solution.py:24
  68.4 6.7 %copy-start.19 = (pred[128]{0:T(512)(128)(4,1)S(1)}, pred[128]{0:T(512)(128)(4,1)}, u32[]{:S(2)}) copy-start(pred[128]{0:T(512)(128)(4,1)} %copy-done.18) | copy-start | bytes 388
  68.4 6.7 %copy-start.21 = (pred[128]{0:T(512)(128)(4,1)S(1)}, pred[128]{0:T(512)(128)(4,1)}, u32[]{:S(2)}) copy-start(pred[128]{0:T(512)(128)(4,1)} %copy-done.20) | copy-start | bytes 388
  68.4 6.7 %copy-start.23 = (pred[16]{0:T(512)(128)(4,1)S(1)}, pred[16]{0:T(512)(128)(4,1)}, u32[]{:S(2)}) copy-start(pred[16]{0:T(512)(128)(4,1)} %copy-done.22) | copy-start | bytes 52
  68.5 6.7 %copy-start.25 = (pred[16]{0:T(512)(128)(4,1)S(1)}, pred[16]{0:T(512)(128)(4,1)}, u32[]{:S(2)}) copy-start(pred[16]{0:T(512)(128)(4,1)} %copy-done.24) | copy-start | bytes 52
  77.8 8.5 %copy-start.4 = (f32[40,16,128]{2,1,0:T(8,128)S(1)}, f32[40,16,128]{2,1,0:T(8,128)}, u32[]{:S(2)}) copy-start(f32[40,16,128]{2,1,0:T(8,128)} %get-tuple-element.68) | copy-start | bytes 983044
  77.9 8.5 %copy-start.5 = (f32[40,16,128]{2,1,0:T(8,128)S(1)}, f32[40,16,128]{2,1,0:T(8,128)}, u32[]{:S(2)}) copy-start(f32[40,16,128]{2,1,0:T(8,128)} %get-tuple-element.69) | copy-start | bytes 983044
  78.6 3.7 %collective-permute-start.14 = (f32[10,128]{1,0:T(8,128)S(1)}, f32[10,128]{1,0:T(8,128)S(1)}, u32[]{:S(2)}, u32[]{:S(2)}) collective-permute-start(f32[10,128]{1,0:T(8,128)S(1)} %reshape_squeeze.50), channel_id=1, source_target_pairs={{0,7},{1,0},{2,1},{3,2},{4,3},{5,4},{6,5},{7,6},{8,15},{9,8},{10,9... | collective-permute-start | bytes 15368 | tf_op jit(solution)/shard_map/ppermute | solution.py:26
  79.9 6.4 %collective-permute-start.15 = (f32[10,128]{1,0:T(8,128)S(1)}, f32[10,128]{1,0:T(8,128)S(1)}, u32[]{:S(2)}, u32[]{:S(2)}) collective-permute-start(f32[10,128]{1,0:T(8,128)S(1)} %reshape_squeeze.51), channel_id=1, source_target_pairs={{0,1},{1,2},{2,3},{3,4},{4,5},{5,6},{6,7},{7,0},{8,9},{9,10},{10,1... | collective-permute-start | bytes 15368 | tf_op jit(solution)/shard_map/ppermute | solution.py:26
  80.8 5.6 %collective-permute-start.12 = (f32[80,128]{1,0:T(8,128)S(1)}, f32[80,128]{1,0:T(8,128)S(1)}, u32[]{:S(2)}, u32[]{:S(2)}) collective-permute-start(f32[80,128]{1,0:T(8,128)S(1)} %bitcast.157), channel_id=1, source_target_pairs={{0,24},{8,0},{16,8},{24,16},{1,25},{9,1},{17,9},{25,17},{2,26},{10... | collective-permute-start | bytes 122888 | tf_op jit(solution)/shard_map/ppermute | solution.py:24
  80.8 5.6 %collective-permute-start.13 = (f32[80,128]{1,0:T(8,128)S(1)}, f32[80,128]{1,0:T(8,128)S(1)}, u32[]{:S(2)}, u32[]{:S(2)}) collective-permute-start(f32[80,128]{1,0:T(8,128)S(1)} %bitcast.156), channel_id=1, source_target_pairs={{0,8},{8,16},{16,24},{24,0},{1,9},{9,17},{17,25},{25,1},{2,10},{10... | collective-permute-start | bytes 122888 | tf_op jit(solution)/shard_map/ppermute | solution.py:24

commit v23 on v22

--- a/solution.py
+++ b/solution.py
@@ -169,8 +169,8 @@
 
 def gather_kernel(index_ref, scale_ref, table_ref, out_ref, per=1):
     fields, rows, lanes = table_ref.shape
-    tile = index_ref.shape[1]
-    index = index_ref[...]
+    tile = index_ref.shape[0] * index_ref.shape[1]
+    index = jnp.concatenate([index_ref[pl.ds(r, 1), :] for r in range(index_ref.shape[0])], axis=1)
     onehot = (lax.broadcasted_iota(jnp.int32, (lanes, tile), 0) == (index % lanes)).astype(jnp.bfloat16)
     select = lax.broadcasted_iota(jnp.int32, (rows, tile), 0) == (index // lanes)
     rest = table_ref[...]
@@ -181,7 +181,7 @@
         parts.append(piece)
     stacked = jnp.concatenate(parts, axis=2).reshape(fields * rows, 3 * lanes)
     picked = jnp.dot(stacked, jnp.concatenate([onehot] * 3, axis=0), preferred_element_type=jnp.float32)
-    scale = scale_ref[...]
+    scale = jnp.concatenate([scale_ref[pl.ds(r, 1), :] for r in range(scale_ref.shape[0])], axis=1)
     values = jnp.concatenate(
         [jnp.sum(jnp.where(select, picked[f * rows : (f + 1) * rows], 0.0), axis=0, keepdims=True) for f in range(fields)],
         axis=0,
@@ -203,8 +203,9 @@
 
 def onehot_gather(table, index, scale, groups):
     fields, rows, lanes = table.shape
-    flat = index.reshape(1, -1)
-    count = flat.shape[1]
+    flat = index.reshape(-1, index.shape[-1])
+    columns = flat.shape[1]
+    count = flat.size
     width = count // groups
     tile = 128
     while tile < 8192 and width % (2 * tile) == 0 and fields * rows * tile * 8 <= 4 * 2**20:
@@ -215,13 +216,13 @@
         functools.partial(gather_kernel, per=per),
         grid=(blocks, groups // per),
         in_specs=[
-            pl.BlockSpec((1, per * tile), lambda step, group: (0, group * blocks + step)),
-            pl.BlockSpec((1, per * tile), lambda step, group: (0, group * blocks + step)),
+            pl.BlockSpec((per * tile // columns, columns), lambda step, group: (group * blocks + step, 0)),
+            pl.BlockSpec((per * tile // columns, columns), lambda step, group: (group * blocks + step, 0)),
             pl.BlockSpec((fields, rows, lanes), lambda step, group: (0, 0, 0)),
         ],
         out_specs=pl.BlockSpec((fields, tile), lambda step, group: (0, step)),
         out_shape=jax.ShapeDtypeStruct((fields, width), jnp.float32),
-    )(flat, scale.reshape(1, -1), table)
+    )(flat, scale.reshape(flat.shape), table)
 
 
 def per_device(

time: 89.4 us -> 89.5 us (level)
  local copies, waits for them, and re-layouts: 10.7 us -> 9.38 us
    unnamed x58 -> x54, local copies, waits for them, and re-layouts: 3.05 us -> 1.77 us
  transfers between devices with their start and end apart: 16 -> 16, of which waited for: 10 -> 10; matrix products, arithmetic and copies ran while one was open for 5% -> 4% of each run, Pallas kernels for 0% -> 0%
where the time goes in v23:
time: 89.5 us; the launch traced here: 88.8 us
  starting transfers between devices  19.8 us (22%)
  waiting for transfers between devices  16.4 us (18%)
  matrix products  15.1 us (17%)
  blocking collectives  14.5 us (16%)
  local copies, waits for them, and re-layouts  9.38 us (10%)
  Pallas kernels  7.33 us (8%)
  other arithmetic  5.04 us (6%)
  between operations  1.26 us (1%)
    ppermute x8, starting transfers between devices, neighbour(): lax.ppermute(values, 'gy', [(j, (j + step_y) % count_y) for j in range(co...  15.1 us
    all_to_all x1, blocking collectives, per_device(): lax.all_to_all(payload, ('gx', 'gy'), split_axis=1, concat_axis=1, tiled=...  14.5 us
    ppermute x8, waiting for transfers between devices, neighbour(): lax.ppermute(values, 'gy', [(j, (j + step_y) % count_y) for j in range(co...  12.4 us
    pallas_call x2, Pallas kernels, onehot_gather(): pl.pallas_call(functools.partial(gather_kernel, per=per), grid=(blocks, g...  7.33 us
    ppermute x8, starting transfers between devices, neighbour(): lax.ppermute(values, 'gx', [(i, (i + step_x) % count_x) for i in range(co...  4.67 us
    dot_general x2, matrix products, tracer_step(): jnp.einsum('ab,...by->...ay', sum_x, tracers, precision=precision)  4.15 us
    ppermute x8, waiting for transfers between devices, neighbour(): lax.ppermute(values, 'gx', [(i, (i + step_x) % count_x) for i in range(co...  3.97 us
    slice x2, local copies, waits for them, and re-layouts, substep(): from_left = exchange(merged[:, :, last_y], 0, 1)[:, :, None]  2.2 us
  transfers between devices with their start and end apart: 16, of which 10 were waited for; matrix products, arithmetic and copies ran while one was open for 4% of the time, Pallas kernels for 0%

profile of v23, /device:TPU:0, one launch (start us, length us, event | category | flops | bytes accessed | tf_op | source)
XLA Modules:
  0.0 88.8 jit_solution(9481655152124998527)
XLA Ops:
  0.7 0.6 copy-done.16
  2.0 0.7 fusion.10
  2.7 0.7 convolution_bitcast_fusion.5
  3.5 0.7 fusion.51
  4.4 0.7 fusion.2
  5.2 0.7 fusion.1
  5.9 1.1 %slice_reduce_fusion.3 = (f32[160,16]{1,0:T(8,128)S(1)}, f32[160,16]{1,0:T(8,128)S(1)}) fusion(f32[160,16,128]{2,1,0:T(8,128)S(1)} %fusion.1), kind=kLoop, calls=%fused_computation.24 | loop fusion | bytes 40960 | tf_op jit(solution)/shard_map/slice | solution.py:88
  7.1 3.0 %collective-permute-start = (f32[20,128]{1,0:T(8,128)S(1)}, f32[20,128]{1,0:T(8,128)S(1)}, u32[]{:S(2)}, u32[]{:S(2)}) collective-permute-start(f32[20,128]{1,0:T(8,128)S(1)} %reshape_squeeze.36), channel_id=1, source_target_pairs={{0,1},{1,2},{2,3},{3,4},{4,5},{5,6},{6,7},{7,0},{8,9},{9,10},{10,1... | collective-permute-start | bytes 30728 | tf_op jit(solution)/shard_map/ppermute | solution.py:26
  10.1 3.1 %collective-permute-start.1 = (f32[20,128]{1,0:T(8,128)S(1)}, f32[20,128]{1,0:T(8,128)S(1)}, u32[]{:S(2)}, u32[]{:S(2)}) collective-permute-start(f32[20,128]{1,0:T(8,128)S(1)} %reshape_squeeze.37), channel_id=1, source_target_pairs={{0,7},{1,0},{2,1},{3,2},{4,3},{5,4},{6,5},{7,6},{8,15},{9,8},{10,9... | collective-permute-start | bytes 30728 | tf_op jit(solution)/shard_map/ppermute | solution.py:26
  13.3 1.5 %collective-permute-done = f32[20,128]{1,0:T(8,128)S(1)} collective-permute-done((f32[20,128]{1,0:T(8,128)S(1)}, f32[20,128]{1,0:T(8,128)S(1)}, u32[]{:S(2)}, u32[]{:S(2)}) %collective-permute-start) | collective-permute-done | bytes 10272 | tf_op jit(solution)/shard_map/ppermute | solution.py:26
  15.0 0.8 select_add_fusion.1
  16.0 1.7 %collective-permute-start.3 = (f32[160,128]{1,0:T(8,128)S(1)}, f32[160,128]{1,0:T(8,128)S(1)}, u32[]{:S(2)}, u32[]{:S(2)}) collective-permute-start(f32[160,128]{1,0:T(8,128)S(1)} %bitcast.143), channel_id=1, source_target_pairs={{0,24},{8,0},{16,8},{24,16},{1,25},{9,1},{17,9},{25,17},{2,26},{10... | collective-permute-start | bytes 245768 | tf_op jit(solution)/shard_map/ppermute | solution.py:24
  17.8 2.1 %collective-permute-done.2 = f32[160,128]{1,0:T(8,128)S(1)} collective-permute-done((f32[160,128]{1,0:T(8,128)S(1)}, f32[160,128]{1,0:T(8,128)S(1)}, u32[]{:S(2)}, u32[]{:S(2)}) %collective-permute-start.2) | collective-permute-done | bytes 81952 | tf_op jit(solution)/shard_map/ppermute | solution.py:24
  20.0 0.8 fusion.5
  20.8 0.7 fusion.6
  21.5 0.7 convolution_multiply_fusion.1
  22.2 0.7 convolution_bitcast_fusion.2
  22.9 0.7 fusion.52
  23.6 0.7 fusion
  24.3 1.1 %slice_reduce_fusion.1 = (f32[160,16]{1,0:T(8,128)S(1)}, f32[160,16]{1,0:T(8,128)S(1)}) fusion(f32[160,16,128]{2,1,0:T(8,128)S(1)} %fusion), kind=kLoop, calls=%fused_computation.22 | loop fusion | bytes 40960 | tf_op jit(solution)/shard_map/slice | solution.py:88
  25.5 1.4 %collective-permute-start.4 = (f32[20,128]{1,0:T(8,128)S(1)}, f32[20,128]{1,0:T(8,128)S(1)}, u32[]{:S(2)}, u32[]{:S(2)}) collective-permute-start(f32[20,128]{1,0:T(8,128)S(1)} %reshape_squeeze.38), channel_id=1, source_target_pairs={{0,1},{1,2},{2,3},{3,4},{4,5},{5,6},{6,7},{7,0},{8,9},{9,10},{10,1... | collective-permute-start | bytes 30728 | tf_op jit(solution)/shard_map/ppermute | solution.py:26
  27.0 3.4 %collective-permute-start.5 = (f32[20,128]{1,0:T(8,128)S(1)}, f32[20,128]{1,0:T(8,128)S(1)}, u32[]{:S(2)}, u32[]{:S(2)}) collective-permute-start(f32[20,128]{1,0:T(8,128)S(1)} %reshape_squeeze.39), channel_id=1, source_target_pairs={{0,7},{1,0},{2,1},{3,2},{4,3},{5,4},{6,5},{7,6},{8,15},{9,8},{10,9... | collective-permute-start | bytes 30728 | tf_op jit(solution)/shard_map/ppermute | solution.py:26
  30.4 1.5 %collective-permute-done.4 = f32[20,128]{1,0:T(8,128)S(1)} collective-permute-done((f32[20,128]{1,0:T(8,128)S(1)}, f32[20,128]{1,0:T(8,128)S(1)}, u32[]{:S(2)}, u32[]{:S(2)}) %collective-permute-start.4) | collective-permute-done | bytes 10272 | tf_op jit(solution)/shard_map/ppermute | solution.py:26
  32.2 0.8 select_add_fusion
  33.2 0.9 %collective-permute-start.6 = (f32[160,128]{1,0:T(8,128)S(1)}, f32[160,128]{1,0:T(8,128)S(1)}, u32[]{:S(2)}, u32[]{:S(2)}) collective-permute-start(f32[160,128]{1,0:T(8,128)S(1)} %bitcast.146), channel_id=1, source_target_pairs={{0,8},{8,16},{16,24},{24,0},{1,9},{9,17},{17,25},{25,1},{2,10},{10... | collective-permute-start | bytes 245768 | tf_op jit(solution)/shard_map/ppermute | solution.py:24
  34.1 0.9 collective-permute-start.7
  35.0 0.7 fusion.38.scale_ref
  35.7 1.4 %collective-permute-done.6 = f32[160,128]{1,0:T(8,128)S(1)} collective-permute-done((f32[160,128]{1,0:T(8,128)S(1)}, f32[160,128]{1,0:T(8,128)S(1)}, u32[]{:S(2)}, u32[]{:S(2)}) %collective-permute-start.6) | collective-permute-done | bytes 81952 | tf_op jit(solution)/shard_map/ppermute | solution.py:24
  37.4 0.8 fusion.9
  38.3 0.7 fusion.37.table_ref
  39.0 2.9 %shard_map.320 = f32[4,8192]{1,0:T(4,128)} custom-call(s32[32,256]{1,0:T(8,128)} %bitcast.151, f32[32,256]{1,0:T(8,128)} %fusion.38.scale_ref, f32[4,16,128]{2,1,0:T(8,128)} %fusion.37.table_ref), custom_call_target="tpu_custom_call" | custom-call | tf_op jit(solution)/shard_map/pallas_call | solution.py:215
  41.9 14.5 %all_to_all.5 = f32[4,32,256]{2,0,1:T(4,128)S(1)} all-to-all(f32[4,32,256]{2,0,1:T(4,128)} %bitcast.142), channel_id=1, replica_groups=mesh['gx'=4,'gy'=8] {'gx','gy'}, dimensions={1} | all-to-all | bytes 262144 | tf_op jit(solution)/shard_map/all_to_all | solution.py:255
  56.5 0.7 copy.41.table_ref
  57.1 4.4 %shard_map.321 = f32[4,2048]{1,0:T(4,128)} custom-call(s32[64,128]{1,0:T(8,128)} %bitcast.152, f32[64,128]{1,0:T(8,128)} %bitcast.153, f32[4,32,256]{2,1,0:T(8,128)} %copy.41.table_ref), custom_call_target="tpu_custom_call" | custom-call | tf_op jit(solution)/shard_map/pallas_call | solution.py:215
  61.6 1.0 %fusion.39 = (f32[1,2048]{1,0:T(1,128)S(1)}, f32[1,2048]{1,0:T(1,128)S(1)}, f32[1,2048]{1,0:T(1,128)S(1)}, f32[1,2048]{1,0:T(1,128)S(1)}) fusion(f32[4,2048]{1,0:T(4,128)} %shard_map.321), kind=kLoop, calls=%fused_computation.76 | loop fusion | flops 8192 | bytes 65536 | tf_op jit(solution)/shard_map/mul | solution.py:259
  62.6 0.6 slice_reduce_fusion.7
  63.2 0.7 fusion.50
  65.1 0.7 reshape_squeeze.42
  65.8 2.0 %collective-permute-start.10 = (f32[10,128]{1,0:T(8,128)}, f32[10,128]{1,0:T(8,128)S(1)}, u32[]{:S(2)}, u32[]{:S(2)}) collective-permute-start(f32[10,128]{1,0:T(8,128)} %reshape_squeeze.42), channel_id=1, source_target_pairs={{0,7},{1,0},{2,1},{3,2},{4,3},{5,4},{6,5},{7,6},{8,15},{9,8},{10,9... | collective-permute-start | bytes 15368 | tf_op jit(solution)/shard_map/ppermute | solution.py:26
  68.6 0.9 fusion.36
  69.8 4.7 %collective-permute-done.11 = f32[10,128]{1,0:T(8,128)} collective-permute-done((f32[10,128]{1,0:T(8,128)S(1)}, f32[10,128]{1,0:T(8,128)}, u32[]{:S(2)}, u32[]{:S(2)}) %collective-permute-start.11) | collective-permute-done | bytes 5152 | tf_op jit(solution)/shard_map/ppermute | solution.py:26
  74.4 0.8 broadcast_in_dim.268
  75.3 1.9 %fusion.17 = f32[2,40,16,128]{3,2,1,0:T(8,128)S(1)} fusion(f32[2,40,16,128]{3,2,1,0:T(8,128)S(1)} %fusion.42, f32[2,40,16,128]{3,2,1,0:T(8,128)S(1)} %convolution_bitcast_fusion.8, f32[2,40,16,128]{3,2,1,0:T(8,128)S(1)} %fusion.53, f32[2,40,16,128]{3,2,1,0:T(8,128)S(1)} %fusion.54, f32[40,16,128]{2,1,0:T(8,128)} %get-tuple-element.69, ...), kind=kOutput, calls=%fused_computation.45 | convolution fusion | flops 19169280 | bytes 4025632 | tf_op jit(solution)/shard_map/ab,...by->...ay/dot_general | solution.py:121
  78.7 1.2 %collective-permute-start.14 = (f32[10,128]{1,0:T(8,128)S(1)}, f32[10,128]{1,0:T(8,128)S(1)}, u32[]{:S(2)}, u32[]{:S(2)}) collective-permute-start(f32[10,128]{1,0:T(8,128)S(1)} %reshape_squeeze.46), channel_id=1, source_target_pairs={{0,7},{1,0},{2,1},{3,2},{4,3},{5,4},{6,5},{7,6},{8,15},{9,8},{10,9... | collective-permute-start | bytes 15368 | tf_op jit(solution)/shard_map/ppermute | solution.py:26
  80.0 0.9 collective-permute-start.15
  81.8 0.6 collective-permute-done.14
  82.5 3.9 %collective-permute-done.15 = f32[10,128]{1,0:T(8,128)S(1)} collective-permute-done((f32[10,128]{1,0:T(8,128)S(1)}, f32[10,128]{1,0:T(8,128)S(1)}, u32[]{:S(2)}, u32[]{:S(2)}) %collective-permute-start.15) | collective-permute-done | bytes 5152 | tf_op jit(solution)/shard_map/ppermute | solution.py:26
  86.5 2.3 %fusion.29 = f32[2,40,16,128]{3,2,1,0:T(8,128)} fusion(f32[2,40,16,128]{3,2,1,0:T(8,128)S(1)} %fusion.17, f32[2,40,16,128]{3,2,1,0:T(8,128)S(1)} %convolution_bitcast_fusion.6, f32[2,40,16,128]{3,2,1,0:T(8,128)S(1)} %fusion.55, f32[2,40,16,128]{3,2,1,0:T(8,128)S(1)} %fusion.56, f32[2,40,16]{2,1,0:T(8,128)S(1)} %broadcast_in_dim.276, ...), kind=kOutput, calls=%fused_computation.57 | convolution fusion | flops 19169280 | bytes 4025632 | tf_op jit(solution)/shard_map/ab,...by->...ay/dot_general | solution.py:121
  (100 shorter events, 7.6 us)
Async XLA Ops:
  0.6 0.7 copy-start.16
  0.6 0.7 copy-start.26
  0.7 0.9 %copy-start.11 = (f32[16,16,1]{1,0,2:T(8,128)S(1)}, f32[16,16,1]{1,0,2:T(8,128)}, u32[]{:S(2)}) copy-start(f32[16,16,1]{1,0,2:T(8,128)} %constant.166) | copy-start | bytes 3076
  0.7 1.3 %copy-start.1 = (f32[4,40,16,128]{3,2,1,0:T(8,128)S(1)}, f32[4,40,16,128]{3,2,1,0:T(8,128)}, u32[]{:S(2)}) copy-start(f32[4,40,16,128]{3,2,1,0:T(8,128)} %param.41) | copy-start | bytes 3932164
  0.7 0.8 copy-start.15
  2.7 0.8 copy-start.10
  3.5 0.8 copy-start.7
  4.4 0.8 copy-start.6
  7.1 7.7 %collective-permute-start = (f32[20,128]{1,0:T(8,128)S(1)}, f32[20,128]{1,0:T(8,128)S(1)}, u32[]{:S(2)}, u32[]{:S(2)}) collective-permute-start(f32[20,128]{1,0:T(8,128)S(1)} %reshape_squeeze.36), channel_id=1, source_target_pairs={{0,1},{1,2},{2,3},{3,4},{4,5},{5,6},{6,7},{7,0},{8,9},{9,10},{10,1... | collective-permute-start | bytes 30728 | tf_op jit(solution)/shard_map/ppermute | solution.py:26
  10.1 4.7 %collective-permute-start.1 = (f32[20,128]{1,0:T(8,128)S(1)}, f32[20,128]{1,0:T(8,128)S(1)}, u32[]{:S(2)}, u32[]{:S(2)}) collective-permute-start(f32[20,128]{1,0:T(8,128)S(1)} %reshape_squeeze.37), channel_id=1, source_target_pairs={{0,7},{1,0},{2,1},{3,2},{4,3},{5,4},{6,5},{7,6},{8,15},{9,8},{10,9... | collective-permute-start | bytes 30728 | tf_op jit(solution)/shard_map/ppermute | solution.py:26
  13.3 18.9 %copy-start.17 = (pred[128]{0:T(512)(128)(4,1)}, pred[128]{0:T(512)(128)(4,1)S(1)}, u32[]{:S(2)}) copy-start(pred[128]{0:T(512)(128)(4,1)S(1)} %get-tuple-element.76) | copy-start | bytes 388
  13.3 18.9 %copy-start.19 = (pred[128]{0:T(512)(128)(4,1)}, pred[128]{0:T(512)(128)(4,1)S(1)}, u32[]{:S(2)}) copy-start(pred[128]{0:T(512)(128)(4,1)S(1)} %get-tuple-element.77) | copy-start | bytes 388
  15.0 5.0 %copy-start.13 = (f32[16,128]{1,0:T(8,128)S(1)}, f32[16,128]{1,0:T(8,128)}, u32[]{:S(2)}) copy-start(f32[16,128]{1,0:T(8,128)} %constant.165) | copy-start | bytes 24580
  15.0 5.0 %copy-start.14 = (f32[16,16,1]{1,0,2:T(8,128)S(1)}, f32[16,16,1]{1,0,2:T(8,128)}, u32[]{:S(2)}) copy-start(f32[16,16,1]{1,0,2:T(8,128)} %constant.170) | copy-start | bytes 3076
  16.0 3.9 %collective-permute-start.2 = (f32[160,128]{1,0:T(8,128)S(1)}, f32[160,128]{1,0:T(8,128)S(1)}, u32[]{:S(2)}, u32[]{:S(2)}) collective-permute-start(f32[160,128]{1,0:T(8,128)S(1)} %bitcast.145), channel_id=1, source_target_pairs={{0,8},{8,16},{16,24},{24,0},{1,9},{9,17},{17,25},{25,1},{2,10},{10... | collective-permute-start | bytes 245768 | tf_op jit(solution)/shard_map/ppermute | solution.py:24
  16.0 4.0 %collective-permute-start.3 = (f32[160,128]{1,0:T(8,128)S(1)}, f32[160,128]{1,0:T(8,128)S(1)}, u32[]{:S(2)}, u32[]{:S(2)}) collective-permute-start(f32[160,128]{1,0:T(8,128)S(1)} %bitcast.143), channel_id=1, source_target_pairs={{0,24},{8,0},{16,8},{24,16},{1,25},{9,1},{17,9},{25,17},{2,26},{10... | collective-permute-start | bytes 245768 | tf_op jit(solution)/shard_map/ppermute | solution.py:24
  17.8 19.6 %copy-start.21 = (pred[16]{0:T(512)(128)(4,1)}, pred[16]{0:T(512)(128)(4,1)S(1)}, u32[]{:S(2)}) copy-start(pred[16]{0:T(512)(128)(4,1)S(1)} %get-tuple-element.78) | copy-start | bytes 52
  17.8 19.6 %copy-start.23 = (pred[16]{0:T(512)(128)(4,1)}, pred[16]{0:T(512)(128)(4,1)S(1)}, u32[]{:S(2)}) copy-start(pred[16]{0:T(512)(128)(4,1)S(1)} %get-tuple-element.79) | copy-start | bytes 52
  25.5 6.5 %collective-permute-start.4 = (f32[20,128]{1,0:T(8,128)S(1)}, f32[20,128]{1,0:T(8,128)S(1)}, u32[]{:S(2)}, u32[]{:S(2)}) collective-permute-start(f32[20,128]{1,0:T(8,128)S(1)} %reshape_squeeze.38), channel_id=1, source_target_pairs={{0,1},{1,2},{2,3},{3,4},{4,5},{5,6},{6,7},{7,0},{8,9},{9,10},{10,1... | collective-permute-start | bytes 30728 | tf_op jit(solution)/shard_map/ppermute | solution.py:26
  27.0 5.1 %collective-permute-start.5 = (f32[20,128]{1,0:T(8,128)S(1)}, f32[20,128]{1,0:T(8,128)S(1)}, u32[]{:S(2)}, u32[]{:S(2)}) collective-permute-start(f32[20,128]{1,0:T(8,128)S(1)} %reshape_squeeze.39), channel_id=1, source_target_pairs={{0,7},{1,0},{2,1},{3,2},{4,3},{5,4},{6,5},{7,6},{8,15},{9,8},{10,9... | collective-permute-start | bytes 30728 | tf_op jit(solution)/shard_map/ppermute | solution.py:26
  32.2 2.8 %copy-start.25 = (s32[1,32]{1,0:T(1,128)S(1)}, s32[1,32]{1,0:T(1,128)}, u32[]{:S(2)}) copy-start(s32[1,32]{1,0:T(1,128)} %param.44) | copy-start | bytes 388
  33.2 3.9 %collective-permute-start.6 = (f32[160,128]{1,0:T(8,128)S(1)}, f32[160,128]{1,0:T(8,128)S(1)}, u32[]{:S(2)}, u32[]{:S(2)}) collective-permute-start(f32[160,128]{1,0:T(8,128)S(1)} %bitcast.146), channel_id=1, source_target_pairs={{0,8},{8,16},{16,24},{24,0},{1,9},{9,17},{17,25},{25,1},{2,10},{10... | collective-permute-start | bytes 245768 | tf_op jit(solution)/shard_map/ppermute | solution.py:24
  34.1 3.3 %collective-permute-start.7 = (f32[160,128]{1,0:T(8,128)S(1)}, f32[160,128]{1,0:T(8,128)S(1)}, u32[]{:S(2)}, u32[]{:S(2)}) collective-permute-start(f32[160,128]{1,0:T(8,128)S(1)} %bitcast.144), channel_id=1, source_target_pairs={{0,24},{8,0},{16,8},{24,16},{1,25},{9,1},{17,9},{25,17},{2,26},{10... | collective-permute-start | bytes 245768 | tf_op jit(solution)/shard_map/ppermute | solution.py:24
  35.7 26.9 %copy-start = (f32[2,40,16,128]{3,2,1,0:T(8,128)S(1)}, f32[2,40,16,128]{3,2,1,0:T(8,128)}, u32[]{:S(2)}) copy-start(f32[2,40,16,128]{3,2,1,0:T(8,128)} %param.45) | copy-start | bytes 1966084
  38.3 25.6 %copy-start.3 = (f32[160,16,128]{2,1,0:T(8,128)}, f32[160,16,128]{2,1,0:T(8,128)S(1)}, u32[]{:S(2)}) copy-start(f32[160,16,128]{2,1,0:T(8,128)S(1)} %fusion.9) | copy-start | bytes 3932164
  39.0 24.9 %copy-start.12 = (f32[16,16,1,1]{1,0,3,2:T(8,128)S(1)}, f32[16,16,1,1]{1,0,3,2:T(8,128)}, u32[]{:S(2)}) copy-start(f32[16,16,1,1]{1,0,3,2:T(8,128)} %constant.173) | copy-start | bytes 3076
  62.6 1.7 %copy-start.9 = (f32[128,128,1,1]{1,0,3,2:T(8,128)S(1)}, f32[128,128,1,1]{1,0,3,2:T(8,128)}, u32[]{:S(2)}) copy-start(f32[128,128,1,1]{1,0,3,2:T(8,128)} %constant.172) | copy-start | bytes 196612
  63.9 0.9 copy-start.8
  64.3 4.3 %copy-start.2 = (f32[2,40,16,128]{3,2,1,0:T(8,128)S(1)}, f32[2,40,16,128]{3,2,1,0:T(8,128)}, u32[]{:S(2)}) copy-start(f32[2,40,16,128]{3,2,1,0:T(8,128)} %param.46) | copy-start | bytes 1966084
  65.8 3.9 %collective-permute-start.10 = (f32[10,128]{1,0:T(8,128)}, f32[10,128]{1,0:T(8,128)S(1)}, u32[]{:S(2)}, u32[]{:S(2)}) collective-permute-start(f32[10,128]{1,0:T(8,128)} %reshape_squeeze.42), channel_id=1, source_target_pairs={{0,7},{1,0},{2,1},{3,2},{4,3},{5,4},{6,5},{7,6},{8,15},{9,8},{10,9... | collective-permute-start | bytes 15368 | tf_op jit(solution)/shard_map/ppermute | solution.py:26
  68.0 6.5 %collective-permute-start.11 = (f32[10,128]{1,0:T(8,128)S(1)}, f32[10,128]{1,0:T(8,128)}, u32[]{:S(2)}, u32[]{:S(2)}) collective-permute-start(f32[10,128]{1,0:T(8,128)S(1)} %reshape_squeeze.43), channel_id=1, source_target_pairs={{0,1},{1,2},{2,3},{3,4},{4,5},{5,6},{6,7},{7,0},{8,9},{9,10},{10,1... | collective-permute-start | bytes 15368 | tf_op jit(solution)/shard_map/ppermute | solution.py:26
  68.0 7.2 %collective-permute-start.8 = (f32[80,128]{1,0:T(8,128)}, f32[80,128]{1,0:T(8,128)}, u32[]{:S(2)}, u32[]{:S(2)}) collective-permute-start(f32[80,128]{1,0:T(8,128)} %bitcast.148), channel_id=1, source_target_pairs={{0,24},{8,0},{16,8},{24,16},{1,25},{9,1},{17,9},{25,17},{2,26},{10... | collective-permute-start | bytes 122888 | tf_op jit(solution)/shard_map/ppermute | solution.py:24
  68.1 7.2 %collective-permute-start.9 = (f32[80,128]{1,0:T(8,128)S(1)}, f32[80,128]{1,0:T(8,128)}, u32[]{:S(2)}, u32[]{:S(2)}) collective-permute-start(f32[80,128]{1,0:T(8,128)S(1)} %bitcast.147), channel_id=1, source_target_pairs={{0,8},{8,16},{16,24},{24,0},{1,9},{9,17},{17,25},{25,1},{2,10},{10... | collective-permute-start | bytes 122888 | tf_op jit(solution)/shard_map/ppermute | solution.py:24
  68.6 6.7 %copy-start.18 = (pred[128]{0:T(512)(128)(4,1)S(1)}, pred[128]{0:T(512)(128)(4,1)}, u32[]{:S(2)}) copy-start(pred[128]{0:T(512)(128)(4,1)} %copy-done.17) | copy-start | bytes 388
  68.6 6.7 %copy-start.20 = (pred[128]{0:T(512)(128)(4,1)S(1)}, pred[128]{0:T(512)(128)(4,1)}, u32[]{:S(2)}) copy-start(pred[128]{0:T(512)(128)(4,1)} %copy-done.19) | copy-start | bytes 388
  68.6 6.7 %copy-start.22 = (pred[16]{0:T(512)(128)(4,1)S(1)}, pred[16]{0:T(512)(128)(4,1)}, u32[]{:S(2)}) copy-start(pred[16]{0:T(512)(128)(4,1)} %copy-done.21) | copy-start | bytes 52
  68.6 6.7 %copy-start.24 = (pred[16]{0:T(512)(128)(4,1)S(1)}, pred[16]{0:T(512)(128)(4,1)}, u32[]{:S(2)}) copy-start(pred[16]{0:T(512)(128)(4,1)} %copy-done.23) | copy-start | bytes 52
  78.0 8.5 %copy-start.4 = (f32[40,16,128]{2,1,0:T(8,128)S(1)}, f32[40,16,128]{2,1,0:T(8,128)}, u32[]{:S(2)}) copy-start(f32[40,16,128]{2,1,0:T(8,128)} %get-tuple-element.68) | copy-start | bytes 983044
  78.0 8.5 %copy-start.5 = (f32[40,16,128]{2,1,0:T(8,128)S(1)}, f32[40,16,128]{2,1,0:T(8,128)}, u32[]{:S(2)}) copy-start(f32[40,16,128]{2,1,0:T(8,128)} %get-tuple-element.69) | copy-start | bytes 983044
  78.7 3.7 %collective-permute-start.14 = (f32[10,128]{1,0:T(8,128)S(1)}, f32[10,128]{1,0:T(8,128)S(1)}, u32[]{:S(2)}, u32[]{:S(2)}) collective-permute-start(f32[10,128]{1,0:T(8,128)S(1)} %reshape_squeeze.46), channel_id=1, source_target_pairs={{0,7},{1,0},{2,1},{3,2},{4,3},{5,4},{6,5},{7,6},{8,15},{9,8},{10,9... | collective-permute-start | bytes 15368 | tf_op jit(solution)/shard_map/ppermute | solution.py:26
  80.0 6.4 %collective-permute-start.15 = (f32[10,128]{1,0:T(8,128)S(1)}, f32[10,128]{1,0:T(8,128)S(1)}, u32[]{:S(2)}, u32[]{:S(2)}) collective-permute-start(f32[10,128]{1,0:T(8,128)S(1)} %reshape_squeeze.47), channel_id=1, source_target_pairs={{0,1},{1,2},{2,3},{3,4},{4,5},{5,6},{6,7},{7,0},{8,9},{9,10},{10,1... | collective-permute-start | bytes 15368 | tf_op jit(solution)/shard_map/ppermute | solution.py:26
  80.9 5.6 %collective-permute-start.12 = (f32[80,128]{1,0:T(8,128)S(1)}, f32[80,128]{1,0:T(8,128)S(1)}, u32[]{:S(2)}, u32[]{:S(2)}) collective-permute-start(f32[80,128]{1,0:T(8,128)S(1)} %bitcast.150), channel_id=1, source_target_pairs={{0,24},{8,0},{16,8},{24,16},{1,25},{9,1},{17,9},{25,17},{2,26},{10... | collective-permute-start | bytes 122888 | tf_op jit(solution)/shard_map/ppermute | solution.py:24
  80.9 5.6 %collective-permute-start.13 = (f32[80,128]{1,0:T(8,128)S(1)}, f32[80,128]{1,0:T(8,128)S(1)}, u32[]{:S(2)}, u32[]{:S(2)}) collective-permute-start(f32[80,128]{1,0:T(8,128)S(1)} %bitcast.149), channel_id=1, source_target_pairs={{0,8},{8,16},{16,24},{24,0},{1,9},{9,17},{17,25},{25,1},{2,10},{10... | collective-permute-start | bytes 122888 | tf_op jit(solution)/shard_map/ppermute | solution.py:24

commit v24 on v22

--- a/solution.py
+++ b/solution.py
@@ -179,8 +179,9 @@
         piece = rest.astype(jnp.bfloat16)
         rest = rest - piece.astype(jnp.float32)
         parts.append(piece)
-    stacked = jnp.concatenate(parts, axis=2).reshape(fields * rows, 3 * lanes)
-    picked = jnp.dot(stacked, jnp.concatenate([onehot] * 3, axis=0), preferred_element_type=jnp.float32)
+    picked = jnp.dot(parts[0].reshape(fields * rows, lanes), onehot, preferred_element_type=jnp.float32)
+    for piece in parts[1:]:
+        picked = picked + jnp.dot(piece.reshape(fields * rows, lanes), onehot, preferred_element_type=jnp.float32)
     scale = scale_ref[...]
     values = jnp.concatenate(
         [jnp.sum(jnp.where(select, picked[f * rows : (f + 1) * rows], 0.0), axis=0, keepdims=True) for f in range(fields)],

time: 89.4 us -> 89.1 us (level)
  no operation moved by 1% of the time
where the time goes in v24:
time: 89.1 us; the launch traced here: 88.4 us
  starting transfers between devices  19.8 us (22%)
  waiting for transfers between devices  15.7 us (18%)
  matrix products  15.1 us (17%)
  blocking collectives  14.5 us (16%)
  local copies, waits for them, and re-layouts  10.7 us (12%)
  Pallas kernels  6.98 us (8%)
  other arithmetic  4.39 us (5%)
  between operations  1.27 us (1%)
    ppermute x8, starting transfers between devices, neighbour(): lax.ppermute(values, 'gy', [(j, (j + step_y) % count_y) for j in range(co...  15.1 us
    all_to_all x1, blocking collectives, per_device(): lax.all_to_all(payload, ('gx', 'gy'), split_axis=1, concat_axis=1, tiled=...  14.5 us
    ppermute x8, waiting for transfers between devices, neighbour(): lax.ppermute(values, 'gy', [(j, (j + step_y) % count_y) for j in range(co...  12.4 us
    pallas_call x2, Pallas kernels, onehot_gather(): pl.pallas_call(functools.partial(gather_kernel, per=per), grid=(blocks, g...  6.98 us
    ppermute x8, starting transfers between devices, neighbour(): lax.ppermute(values, 'gx', [(i, (i + step_x) % count_x) for i in range(co...  4.67 us
    dot_general x2, matrix products, tracer_step(): jnp.einsum('ab,...by->...ay', sum_x, tracers, precision=precision)  4.15 us
    ppermute x8, waiting for transfers between devices, neighbour(): lax.ppermute(values, 'gx', [(i, (i + step_x) % count_x) for i in range(co...  3.3 us
    unnamed x58, local copies, waits for them, and re-layouts  3.05 us
  transfers between devices with their start and end apart: 16, of which 10 were waited for; matrix products, arithmetic and copies ran while one was open for 5% of the time, Pallas kernels for 0%

profile of v24, /device:TPU:0, one launch (start us, length us, event | category | flops | bytes accessed | tf_op | source)
XLA Modules:
  0.0 88.4 jit_solution(12405062063557064980)
XLA Ops:
  0.7 0.6 copy-done.17
  2.0 0.7 fusion.10
  2.7 0.7 convolution_bitcast_fusion.5
  3.5 0.7 fusion.50
  4.4 0.7 fusion.2
  5.2 0.7 fusion.1
  5.9 1.1 %slice_reduce_fusion.3 = (f32[160,16]{1,0:T(8,128)S(1)}, f32[160,16]{1,0:T(8,128)S(1)}) fusion(f32[160,16,128]{2,1,0:T(8,128)S(1)} %fusion.1), kind=kLoop, calls=%fused_computation.24 | loop fusion | bytes 40960 | tf_op jit(solution)/shard_map/slice | solution.py:88
  7.1 3.0 %collective-permute-start = (f32[20,128]{1,0:T(8,128)S(1)}, f32[20,128]{1,0:T(8,128)S(1)}, u32[]{:S(2)}, u32[]{:S(2)}) collective-permute-start(f32[20,128]{1,0:T(8,128)S(1)} %reshape_squeeze.39), channel_id=1, source_target_pairs={{0,1},{1,2},{2,3},{3,4},{4,5},{5,6},{6,7},{7,0},{8,9},{9,10},{10,1... | collective-permute-start | bytes 30728 | tf_op jit(solution)/shard_map/ppermute | solution.py:26
  10.1 3.1 %collective-permute-start.1 = (f32[20,128]{1,0:T(8,128)S(1)}, f32[20,128]{1,0:T(8,128)S(1)}, u32[]{:S(2)}, u32[]{:S(2)}) collective-permute-start(f32[20,128]{1,0:T(8,128)S(1)} %reshape_squeeze.40), channel_id=1, source_target_pairs={{0,7},{1,0},{2,1},{3,2},{4,3},{5,4},{6,5},{7,6},{8,15},{9,8},{10,9... | collective-permute-start | bytes 30728 | tf_op jit(solution)/shard_map/ppermute | solution.py:26
  13.3 1.5 %collective-permute-done = f32[20,128]{1,0:T(8,128)S(1)} collective-permute-done((f32[20,128]{1,0:T(8,128)S(1)}, f32[20,128]{1,0:T(8,128)S(1)}, u32[]{:S(2)}, u32[]{:S(2)}) %collective-permute-start) | collective-permute-done | bytes 10272 | tf_op jit(solution)/shard_map/ppermute | solution.py:26
  15.0 0.8 select_add_fusion.1
  16.0 1.7 %collective-permute-start.3 = (f32[160,128]{1,0:T(8,128)S(1)}, f32[160,128]{1,0:T(8,128)S(1)}, u32[]{:S(2)}, u32[]{:S(2)}) collective-permute-start(f32[160,128]{1,0:T(8,128)S(1)} %bitcast.151), channel_id=1, source_target_pairs={{0,24},{8,0},{16,8},{24,16},{1,25},{9,1},{17,9},{25,17},{2,26},{10... | collective-permute-start | bytes 245768 | tf_op jit(solution)/shard_map/ppermute | solution.py:24
  17.8 2.1 %collective-permute-done.2 = f32[160,128]{1,0:T(8,128)S(1)} collective-permute-done((f32[160,128]{1,0:T(8,128)S(1)}, f32[160,128]{1,0:T(8,128)S(1)}, u32[]{:S(2)}, u32[]{:S(2)}) %collective-permute-start.2) | collective-permute-done | bytes 81952 | tf_op jit(solution)/shard_map/ppermute | solution.py:24
  20.0 0.8 fusion.5
  20.8 0.7 fusion.6
  21.5 0.7 convolution_multiply_fusion.1
  22.2 0.7 convolution_bitcast_fusion.2
  22.9 0.7 fusion.51
  23.6 0.7 fusion
  24.3 1.1 %slice_reduce_fusion.1 = (f32[160,16]{1,0:T(8,128)S(1)}, f32[160,16]{1,0:T(8,128)S(1)}) fusion(f32[160,16,128]{2,1,0:T(8,128)S(1)} %fusion), kind=kLoop, calls=%fused_computation.22 | loop fusion | bytes 40960 | tf_op jit(solution)/shard_map/slice | solution.py:88
  25.5 1.4 %collective-permute-start.4 = (f32[20,128]{1,0:T(8,128)S(1)}, f32[20,128]{1,0:T(8,128)S(1)}, u32[]{:S(2)}, u32[]{:S(2)}) collective-permute-start(f32[20,128]{1,0:T(8,128)S(1)} %reshape_squeeze.41), channel_id=1, source_target_pairs={{0,1},{1,2},{2,3},{3,4},{4,5},{5,6},{6,7},{7,0},{8,9},{9,10},{10,1... | collective-permute-start | bytes 30728 | tf_op jit(solution)/shard_map/ppermute | solution.py:26
  27.0 3.4 %collective-permute-start.5 = (f32[20,128]{1,0:T(8,128)S(1)}, f32[20,128]{1,0:T(8,128)S(1)}, u32[]{:S(2)}, u32[]{:S(2)}) collective-permute-start(f32[20,128]{1,0:T(8,128)S(1)} %reshape_squeeze.42), channel_id=1, source_target_pairs={{0,7},{1,0},{2,1},{3,2},{4,3},{5,4},{6,5},{7,6},{8,15},{9,8},{10,9... | collective-permute-start | bytes 30728 | tf_op jit(solution)/shard_map/ppermute | solution.py:26
  30.4 1.5 %collective-permute-done.4 = f32[20,128]{1,0:T(8,128)S(1)} collective-permute-done((f32[20,128]{1,0:T(8,128)S(1)}, f32[20,128]{1,0:T(8,128)S(1)}, u32[]{:S(2)}, u32[]{:S(2)}) %collective-permute-start.4) | collective-permute-done | bytes 10272 | tf_op jit(solution)/shard_map/ppermute | solution.py:26
  32.2 0.8 select_add_fusion
  33.2 0.9 %collective-permute-start.6 = (f32[160,128]{1,0:T(8,128)S(1)}, f32[160,128]{1,0:T(8,128)S(1)}, u32[]{:S(2)}, u32[]{:S(2)}) collective-permute-start(f32[160,128]{1,0:T(8,128)S(1)} %bitcast.152), channel_id=1, source_target_pairs={{0,8},{8,16},{16,24},{24,0},{1,9},{9,17},{17,25},{25,1},{2,10},{10... | collective-permute-start | bytes 245768 | tf_op jit(solution)/shard_map/ppermute | solution.py:24
  34.1 0.9 collective-permute-start.7
  35.1 0.6 copy.52
  35.7 0.6 copy.51
  36.3 0.8 collective-permute-done.6
  37.4 0.8 fusion.9
  38.3 0.7 fusion.37.table_ref
  39.0 2.9 %shard_map.320 = f32[4,8192]{1,0:T(4,128)} custom-call(s32[1,8192]{1,0:T(1,128)} %bitcast.149, f32[1,8192]{1,0:T(1,128)} %bitcast.148, f32[4,16,128]{2,1,0:T(8,128)} %fusion.37.table_ref), custom_call_target="tpu_custom_call" | custom-call | tf_op jit(solution)/shard_map/pallas_call | solution.py:215
  41.9 14.5 %all_to_all.5 = f32[4,32,256]{2,0,1:T(4,128)S(1)} all-to-all(f32[4,32,256]{2,0,1:T(4,128)} %bitcast.147), channel_id=1, replica_groups=mesh['gx'=4,'gy'=8] {'gx','gy'}, dimensions={1} | all-to-all | bytes 262144 | tf_op jit(solution)/shard_map/all_to_all | solution.py:255
  56.4 0.7 copy.41.table_ref
  57.1 4.1 %shard_map.321 = f32[4,2048]{1,0:T(4,128)} custom-call(s32[1,8192]{1,0:T(1,128)} %bitcast.158, f32[1,8192]{1,0:T(1,128)} %bitcast.159, f32[4,32,256]{2,1,0:T(8,128)} %copy.41.table_ref), custom_call_target="tpu_custom_call" | custom-call | tf_op jit(solution)/shard_map/pallas_call | solution.py:215
  61.2 1.0 %fusion.38 = (f32[1,2048]{1,0:T(1,128)S(1)}, f32[1,2048]{1,0:T(1,128)S(1)}, f32[1,2048]{1,0:T(1,128)S(1)}, f32[1,2048]{1,0:T(1,128)S(1)}) fusion(f32[4,2048]{1,0:T(4,128)} %shard_map.321), kind=kLoop, calls=%fused_computation.76 | loop fusion | flops 8192 | bytes 65536 | tf_op jit(solution)/shard_map/mul | solution.py:259
  62.8 0.7 fusion.49
  64.8 0.7 reshape_squeeze.46
  65.4 2.0 %collective-permute-start.10 = (f32[10,128]{1,0:T(8,128)}, f32[10,128]{1,0:T(8,128)S(1)}, u32[]{:S(2)}, u32[]{:S(2)}) collective-permute-start(f32[10,128]{1,0:T(8,128)} %reshape_squeeze.46), channel_id=1, source_target_pairs={{0,7},{1,0},{2,1},{3,2},{4,3},{5,4},{6,5},{7,6},{8,15},{9,8},{10,9... | collective-permute-start | bytes 15368 | tf_op jit(solution)/shard_map/ppermute | solution.py:26
  68.2 0.9 fusion.36
  69.4 4.7 %collective-permute-done.11 = f32[10,128]{1,0:T(8,128)} collective-permute-done((f32[10,128]{1,0:T(8,128)S(1)}, f32[10,128]{1,0:T(8,128)}, u32[]{:S(2)}, u32[]{:S(2)}) %collective-permute-start.11) | collective-permute-done | bytes 5152 | tf_op jit(solution)/shard_map/ppermute | solution.py:26
  74.0 0.8 broadcast_in_dim.268
  74.9 1.9 %fusion.17 = f32[2,40,16,128]{3,2,1,0:T(8,128)S(1)} fusion(f32[2,40,16,128]{3,2,1,0:T(8,128)S(1)} %fusion.41, f32[2,40,16,128]{3,2,1,0:T(8,128)S(1)} %convolution_bitcast_fusion.8, f32[2,40,16,128]{3,2,1,0:T(8,128)S(1)} %fusion.52, f32[2,40,16,128]{3,2,1,0:T(8,128)S(1)} %fusion.53, f32[40,16,128]{2,1,0:T(8,128)} %get-tuple-element.69, ...), kind=kOutput, calls=%fused_computation.45 | convolution fusion | flops 19169280 | bytes 4025632 | tf_op jit(solution)/shard_map/ab,...by->...ay/dot_general | solution.py:121
  78.4 1.2 %collective-permute-start.14 = (f32[10,128]{1,0:T(8,128)S(1)}, f32[10,128]{1,0:T(8,128)S(1)}, u32[]{:S(2)}, u32[]{:S(2)}) collective-permute-start(f32[10,128]{1,0:T(8,128)S(1)} %reshape_squeeze.50), channel_id=1, source_target_pairs={{0,7},{1,0},{2,1},{3,2},{4,3},{5,4},{6,5},{7,6},{8,15},{9,8},{10,9... | collective-permute-start | bytes 15368 | tf_op jit(solution)/shard_map/ppermute | solution.py:26
  79.7 0.9 collective-permute-start.15
  81.4 0.6 collective-permute-done.14
  82.1 3.9 %collective-permute-done.15 = f32[10,128]{1,0:T(8,128)S(1)} collective-permute-done((f32[10,128]{1,0:T(8,128)S(1)}, f32[10,128]{1,0:T(8,128)S(1)}, u32[]{:S(2)}, u32[]{:S(2)}) %collective-permute-start.15) | collective-permute-done | bytes 5152 | tf_op jit(solution)/shard_map/ppermute | solution.py:26
  86.1 2.3 %fusion.29 = f32[2,40,16,128]{3,2,1,0:T(8,128)} fusion(f32[2,40,16,128]{3,2,1,0:T(8,128)S(1)} %fusion.17, f32[2,40,16,128]{3,2,1,0:T(8,128)S(1)} %convolution_bitcast_fusion.6, f32[2,40,16,128]{3,2,1,0:T(8,128)S(1)} %fusion.54, f32[2,40,16,128]{3,2,1,0:T(8,128)S(1)} %fusion.55, f32[2,40,16]{2,1,0:T(8,128)S(1)} %broadcast_in_dim.276, ...), kind=kOutput, calls=%fused_computation.57 | convolution fusion | flops 19169280 | bytes 4025632 | tf_op jit(solution)/shard_map/ab,...by->...ay/dot_general | solution.py:121
  (104 shorter events, 8.2 us)
Async XLA Ops:
  0.6 0.7 copy-start.17
  0.6 0.7 copy-start.27
  0.7 0.9 %copy-start.11 = (f32[16,16,1]{1,0,2:T(8,128)S(1)}, f32[16,16,1]{1,0,2:T(8,128)}, u32[]{:S(2)}) copy-start(f32[16,16,1]{1,0,2:T(8,128)} %constant.166) | copy-start | bytes 3076
  0.7 1.3 %copy-start.1 = (f32[4,40,16,128]{3,2,1,0:T(8,128)S(1)}, f32[4,40,16,128]{3,2,1,0:T(8,128)}, u32[]{:S(2)}) copy-start(f32[4,40,16,128]{3,2,1,0:T(8,128)} %param.41) | copy-start | bytes 3932164
  0.7 0.8 copy-start.16
  2.7 0.8 copy-start.10
  3.5 0.8 copy-start.7
  4.4 0.8 copy-start.6
  7.1 7.7 %collective-permute-start = (f32[20,128]{1,0:T(8,128)S(1)}, f32[20,128]{1,0:T(8,128)S(1)}, u32[]{:S(2)}, u32[]{:S(2)}) collective-permute-start(f32[20,128]{1,0:T(8,128)S(1)} %reshape_squeeze.39), channel_id=1, source_target_pairs={{0,1},{1,2},{2,3},{3,4},{4,5},{5,6},{6,7},{7,0},{8,9},{9,10},{10,1... | collective-permute-start | bytes 30728 | tf_op jit(solution)/shard_map/ppermute | solution.py:26
  10.1 4.7 %collective-permute-start.1 = (f32[20,128]{1,0:T(8,128)S(1)}, f32[20,128]{1,0:T(8,128)S(1)}, u32[]{:S(2)}, u32[]{:S(2)}) collective-permute-start(f32[20,128]{1,0:T(8,128)S(1)} %reshape_squeeze.40), channel_id=1, source_target_pairs={{0,7},{1,0},{2,1},{3,2},{4,3},{5,4},{6,5},{7,6},{8,15},{9,8},{10,9... | collective-permute-start | bytes 30728 | tf_op jit(solution)/shard_map/ppermute | solution.py:26
  13.3 18.9 %copy-start.18 = (pred[128]{0:T(512)(128)(4,1)}, pred[128]{0:T(512)(128)(4,1)S(1)}, u32[]{:S(2)}) copy-start(pred[128]{0:T(512)(128)(4,1)S(1)} %get-tuple-element.76) | copy-start | bytes 388
  13.3 18.9 %copy-start.20 = (pred[128]{0:T(512)(128)(4,1)}, pred[128]{0:T(512)(128)(4,1)S(1)}, u32[]{:S(2)}) copy-start(pred[128]{0:T(512)(128)(4,1)S(1)} %get-tuple-element.77) | copy-start | bytes 388
  15.0 5.0 %copy-start.13 = (f32[16,128]{1,0:T(8,128)S(1)}, f32[16,128]{1,0:T(8,128)}, u32[]{:S(2)}) copy-start(f32[16,128]{1,0:T(8,128)} %constant.165) | copy-start | bytes 24580
  15.0 5.0 %copy-start.14 = (f32[16,16,1]{1,0,2:T(8,128)S(1)}, f32[16,16,1]{1,0,2:T(8,128)}, u32[]{:S(2)}) copy-start(f32[16,16,1]{1,0,2:T(8,128)} %constant.170) | copy-start | bytes 3076
  16.0 3.9 %collective-permute-start.2 = (f32[160,128]{1,0:T(8,128)S(1)}, f32[160,128]{1,0:T(8,128)S(1)}, u32[]{:S(2)}, u32[]{:S(2)}) collective-permute-start(f32[160,128]{1,0:T(8,128)S(1)} %bitcast.153), channel_id=1, source_target_pairs={{0,8},{8,16},{16,24},{24,0},{1,9},{9,17},{17,25},{25,1},{2,10},{10... | collective-permute-start | bytes 245768 | tf_op jit(solution)/shard_map/ppermute | solution.py:24
  16.0 4.0 %collective-permute-start.3 = (f32[160,128]{1,0:T(8,128)S(1)}, f32[160,128]{1,0:T(8,128)S(1)}, u32[]{:S(2)}, u32[]{:S(2)}) collective-permute-start(f32[160,128]{1,0:T(8,128)S(1)} %bitcast.151), channel_id=1, source_target_pairs={{0,24},{8,0},{16,8},{24,16},{1,25},{9,1},{17,9},{25,17},{2,26},{10... | collective-permute-start | bytes 245768 | tf_op jit(solution)/shard_map/ppermute | solution.py:24
  17.8 19.6 %copy-start.22 = (pred[16]{0:T(512)(128)(4,1)}, pred[16]{0:T(512)(128)(4,1)S(1)}, u32[]{:S(2)}) copy-start(pred[16]{0:T(512)(128)(4,1)S(1)} %get-tuple-element.78) | copy-start | bytes 52
  17.8 19.6 %copy-start.24 = (pred[16]{0:T(512)(128)(4,1)}, pred[16]{0:T(512)(128)(4,1)S(1)}, u32[]{:S(2)}) copy-start(pred[16]{0:T(512)(128)(4,1)S(1)} %get-tuple-element.79) | copy-start | bytes 52
  25.5 6.5 %collective-permute-start.4 = (f32[20,128]{1,0:T(8,128)S(1)}, f32[20,128]{1,0:T(8,128)S(1)}, u32[]{:S(2)}, u32[]{:S(2)}) collective-permute-start(f32[20,128]{1,0:T(8,128)S(1)} %reshape_squeeze.41), channel_id=1, source_target_pairs={{0,1},{1,2},{2,3},{3,4},{4,5},{5,6},{6,7},{7,0},{8,9},{9,10},{10,1... | collective-permute-start | bytes 30728 | tf_op jit(solution)/shard_map/ppermute | solution.py:26
  27.0 5.1 %collective-permute-start.5 = (f32[20,128]{1,0:T(8,128)S(1)}, f32[20,128]{1,0:T(8,128)S(1)}, u32[]{:S(2)}, u32[]{:S(2)}) collective-permute-start(f32[20,128]{1,0:T(8,128)S(1)} %reshape_squeeze.42), channel_id=1, source_target_pairs={{0,7},{1,0},{2,1},{3,2},{4,3},{5,4},{6,5},{7,6},{8,15},{9,8},{10,9... | collective-permute-start | bytes 30728 | tf_op jit(solution)/shard_map/ppermute | solution.py:26
  32.2 2.8 %copy-start.26 = (s32[1,32]{1,0:T(1,128)S(1)}, s32[1,32]{1,0:T(1,128)}, u32[]{:S(2)}) copy-start(s32[1,32]{1,0:T(1,128)} %param.44) | copy-start | bytes 388
  32.2 3.5 %copy-start.15 = (s32[1,32,256]{2,1,0:T(8,128)S(1)}, s32[1,32,256]{2,1,0:T(8,128)}, u32[]{:S(2)}) copy-start(s32[1,32,256]{2,1,0:T(8,128)} %param.43) | copy-start | bytes 98308
  33.2 3.9 %collective-permute-start.6 = (f32[160,128]{1,0:T(8,128)S(1)}, f32[160,128]{1,0:T(8,128)S(1)}, u32[]{:S(2)}, u32[]{:S(2)}) collective-permute-start(f32[160,128]{1,0:T(8,128)S(1)} %bitcast.152), channel_id=1, source_target_pairs={{0,8},{8,16},{16,24},{24,0},{1,9},{9,17},{17,25},{25,1},{2,10},{10... | collective-permute-start | bytes 245768 | tf_op jit(solution)/shard_map/ppermute | solution.py:24
  34.1 3.3 %collective-permute-start.7 = (f32[160,128]{1,0:T(8,128)S(1)}, f32[160,128]{1,0:T(8,128)S(1)}, u32[]{:S(2)}, u32[]{:S(2)}) collective-permute-start(f32[160,128]{1,0:T(8,128)S(1)} %bitcast.150), channel_id=1, source_target_pairs={{0,24},{8,0},{16,8},{24,16},{1,25},{9,1},{17,9},{25,17},{2,26},{10... | collective-permute-start | bytes 245768 | tf_op jit(solution)/shard_map/ppermute | solution.py:24
  36.3 25.8 %copy-start = (f32[2,40,16,128]{3,2,1,0:T(8,128)S(1)}, f32[2,40,16,128]{3,2,1,0:T(8,128)}, u32[]{:S(2)}) copy-start(f32[2,40,16,128]{3,2,1,0:T(8,128)} %param.45) | copy-start | bytes 1966084
  38.3 25.2 %copy-start.3 = (f32[160,16,128]{2,1,0:T(8,128)}, f32[160,16,128]{2,1,0:T(8,128)S(1)}, u32[]{:S(2)}) copy-start(f32[160,16,128]{2,1,0:T(8,128)S(1)} %fusion.9) | copy-start | bytes 3932164
  39.0 24.5 %copy-start.12 = (f32[16,16,1,1]{1,0,3,2:T(8,128)S(1)}, f32[16,16,1,1]{1,0,3,2:T(8,128)}, u32[]{:S(2)}) copy-start(f32[16,16,1,1]{1,0,3,2:T(8,128)} %constant.173) | copy-start | bytes 3076
  62.2 1.7 %copy-start.9 = (f32[128,128,1,1]{1,0,3,2:T(8,128)S(1)}, f32[128,128,1,1]{1,0,3,2:T(8,128)}, u32[]{:S(2)}) copy-start(f32[128,128,1,1]{1,0,3,2:T(8,128)} %constant.172) | copy-start | bytes 196612
  63.5 0.9 copy-start.8
  63.9 4.3 %copy-start.2 = (f32[2,40,16,128]{3,2,1,0:T(8,128)S(1)}, f32[2,40,16,128]{3,2,1,0:T(8,128)}, u32[]{:S(2)}) copy-start(f32[2,40,16,128]{3,2,1,0:T(8,128)} %param.46) | copy-start | bytes 1966084
  65.4 3.9 %collective-permute-start.10 = (f32[10,128]{1,0:T(8,128)}, f32[10,128]{1,0:T(8,128)S(1)}, u32[]{:S(2)}, u32[]{:S(2)}) collective-permute-start(f32[10,128]{1,0:T(8,128)} %reshape_squeeze.46), channel_id=1, source_target_pairs={{0,7},{1,0},{2,1},{3,2},{4,3},{5,4},{6,5},{7,6},{8,15},{9,8},{10,9... | collective-permute-start | bytes 15368 | tf_op jit(solution)/shard_map/ppermute | solution.py:26
  67.6 6.5 %collective-permute-start.11 = (f32[10,128]{1,0:T(8,128)S(1)}, f32[10,128]{1,0:T(8,128)}, u32[]{:S(2)}, u32[]{:S(2)}) collective-permute-start(f32[10,128]{1,0:T(8,128)S(1)} %reshape_squeeze.47), channel_id=1, source_target_pairs={{0,1},{1,2},{2,3},{3,4},{4,5},{5,6},{6,7},{7,0},{8,9},{9,10},{10,1... | collective-permute-start | bytes 15368 | tf_op jit(solution)/shard_map/ppermute | solution.py:26
  67.6 7.2 %collective-permute-start.8 = (f32[80,128]{1,0:T(8,128)}, f32[80,128]{1,0:T(8,128)}, u32[]{:S(2)}, u32[]{:S(2)}) collective-permute-start(f32[80,128]{1,0:T(8,128)} %bitcast.155), channel_id=1, source_target_pairs={{0,24},{8,0},{16,8},{24,16},{1,25},{9,1},{17,9},{25,17},{2,26},{10... | collective-permute-start | bytes 122888 | tf_op jit(solution)/shard_map/ppermute | solution.py:24
  67.7 7.2 %collective-permute-start.9 = (f32[80,128]{1,0:T(8,128)S(1)}, f32[80,128]{1,0:T(8,128)}, u32[]{:S(2)}, u32[]{:S(2)}) collective-permute-start(f32[80,128]{1,0:T(8,128)S(1)} %bitcast.154), channel_id=1, source_target_pairs={{0,8},{8,16},{16,24},{24,0},{1,9},{9,17},{17,25},{25,1},{2,10},{10... | collective-permute-start | bytes 122888 | tf_op jit(solution)/shard_map/ppermute | solution.py:24
  68.2 6.7 %copy-start.19 = (pred[128]{0:T(512)(128)(4,1)S(1)}, pred[128]{0:T(512)(128)(4,1)}, u32[]{:S(2)}) copy-start(pred[128]{0:T(512)(128)(4,1)} %copy-done.18) | copy-start | bytes 388
  68.2 6.7 %copy-start.21 = (pred[128]{0:T(512)(128)(4,1)S(1)}, pred[128]{0:T(512)(128)(4,1)}, u32[]{:S(2)}) copy-start(pred[128]{0:T(512)(128)(4,1)} %copy-done.20) | copy-start | bytes 388
  68.2 6.7 %copy-start.23 = (pred[16]{0:T(512)(128)(4,1)S(1)}, pred[16]{0:T(512)(128)(4,1)}, u32[]{:S(2)}) copy-start(pred[16]{0:T(512)(128)(4,1)} %copy-done.22) | copy-start | bytes 52
  68.2 6.7 %copy-start.25 = (pred[16]{0:T(512)(128)(4,1)S(1)}, pred[16]{0:T(512)(128)(4,1)}, u32[]{:S(2)}) copy-start(pred[16]{0:T(512)(128)(4,1)} %copy-done.24) | copy-start | bytes 52
  77.6 8.5 %copy-start.4 = (f32[40,16,128]{2,1,0:T(8,128)S(1)}, f32[40,16,128]{2,1,0:T(8,128)}, u32[]{:S(2)}) copy-start(f32[40,16,128]{2,1,0:T(8,128)} %get-tuple-element.68) | copy-start | bytes 983044
  77.6 8.5 %copy-start.5 = (f32[40,16,128]{2,1,0:T(8,128)S(1)}, f32[40,16,128]{2,1,0:T(8,128)}, u32[]{:S(2)}) copy-start(f32[40,16,128]{2,1,0:T(8,128)} %get-tuple-element.69) | copy-start | bytes 983044
  78.4 3.7 %collective-permute-start.14 = (f32[10,128]{1,0:T(8,128)S(1)}, f32[10,128]{1,0:T(8,128)S(1)}, u32[]{:S(2)}, u32[]{:S(2)}) collective-permute-start(f32[10,128]{1,0:T(8,128)S(1)} %reshape_squeeze.50), channel_id=1, source_target_pairs={{0,7},{1,0},{2,1},{3,2},{4,3},{5,4},{6,5},{7,6},{8,15},{9,8},{10,9... | collective-permute-start | bytes 15368 | tf_op jit(solution)/shard_map/ppermute | solution.py:26
  79.7 6.4 %collective-permute-start.15 = (f32[10,128]{1,0:T(8,128)S(1)}, f32[10,128]{1,0:T(8,128)S(1)}, u32[]{:S(2)}, u32[]{:S(2)}) collective-permute-start(f32[10,128]{1,0:T(8,128)S(1)} %reshape_squeeze.51), channel_id=1, source_target_pairs={{0,1},{1,2},{2,3},{3,4},{4,5},{5,6},{6,7},{7,0},{8,9},{9,10},{10,1... | collective-permute-start | bytes 15368 | tf_op jit(solution)/shard_map/ppermute | solution.py:26
  80.5 5.6 %collective-permute-start.12 = (f32[80,128]{1,0:T(8,128)S(1)}, f32[80,128]{1,0:T(8,128)S(1)}, u32[]{:S(2)}, u32[]{:S(2)}) collective-permute-start(f32[80,128]{1,0:T(8,128)S(1)} %bitcast.157), channel_id=1, source_target_pairs={{0,24},{8,0},{16,8},{24,16},{1,25},{9,1},{17,9},{25,17},{2,26},{10... | collective-permute-start | bytes 122888 | tf_op jit(solution)/shard_map/ppermute | solution.py:24
  80.5 5.6 %collective-permute-start.13 = (f32[80,128]{1,0:T(8,128)S(1)}, f32[80,128]{1,0:T(8,128)S(1)}, u32[]{:S(2)}, u32[]{:S(2)}) collective-permute-start(f32[80,128]{1,0:T(8,128)S(1)} %bitcast.156), channel_id=1, source_target_pairs={{0,8},{8,16},{16,24},{24,0},{1,9},{9,17},{17,25},{25,1},{2,10},{10... | collective-permute-start | bytes 122888 | tf_op jit(solution)/shard_map/ppermute | solution.py:24

commit v25 on v22

--- a/solution.py
+++ b/solution.py
@@ -186,7 +186,7 @@
         [jnp.sum(jnp.where(select, picked[f * rows : (f + 1) * rows], 0.0), axis=0, keepdims=True) for f in range(fields)],
         axis=0,
     ) * scale
-    width = out_ref.shape[1]
+    width = out_ref.shape[1] * out_ref.shape[2]
     total = values[:, :width]
     for chunk in range(1, per):
         total = total + values[:, chunk * width : (chunk + 1) * width]
@@ -194,11 +194,11 @@
 
     @pl.when(pl.program_id(1) == 0)
     def first():
-        out_ref[...] = values
+        out_ref[...] = values.reshape(out_ref.shape)
 
     @pl.when(pl.program_id(1) > 0)
     def rest_steps():
-        out_ref[...] = out_ref[...] + values
+        out_ref[...] = out_ref[...] + values.reshape(out_ref.shape)
 
 
 def onehot_gather(table, index, scale, groups):
@@ -219,8 +219,8 @@
             pl.BlockSpec((1, per * tile), lambda step, group: (0, group * blocks + step)),
             pl.BlockSpec((fields, rows, lanes), lambda step, group: (0, 0, 0)),
         ],
-        out_specs=pl.BlockSpec((fields, tile), lambda step, group: (0, step)),
-        out_shape=jax.ShapeDtypeStruct((fields, width), jnp.float32),
+        out_specs=pl.BlockSpec((fields, tile // 128, 128), lambda step, group: (0, step, 0)),
+        out_shape=jax.ShapeDtypeStruct((fields, width // 128, 128), jnp.float32),
     )(flat, scale.reshape(1, -1), table)
 
 

time: 89.4 us -> 90.4 us (1.011)
    reshape x0 -> x2, local copies, waits for them, and re-layouts: none -> 1.03 us  [per_device(): onehot_gather(flux_table, send_idx[0], live_slots, 1)]
    mul x1 -> x0, other arithmetic: 0.95 us -> none  [per_device(): velocity = velocity.at[1, 0].add(wind_coef * jnp.tanh(ocean_flux[1]))]
    unnamed x58 -> x60, local copies, waits for them, and re-layouts: 3.05 us -> 3.06 us
  transfers between devices with their start and end apart: 16 -> 16, of which waited for: 10 -> 9; matrix products, arithmetic and copies ran while one was open for 5% -> 4% of each run, Pallas kernels for 0% -> 0%
where the time goes in v25:
time: 90.4 us; the launch traced here: 89.8 us
  starting transfers between devices  19.8 us (22%)
  waiting for transfers between devices  16.4 us (18%)
  matrix products  15.2 us (17%)
  blocking collectives  14.3 us (16%)
  local copies, waits for them, and re-layouts  10.4 us (12%)
  Pallas kernels  7.48 us (8%)
  other arithmetic  4.78 us (5%)
  between operations  1.3 us (1%)
    ppermute x8, starting transfers between devices, neighbour(): lax.ppermute(values, 'gy', [(j, (j + step_y) % count_y) for j in range(co...  15.1 us
    all_to_all x1, blocking collectives, per_device(): lax.all_to_all(payload, ('gx', 'gy'), split_axis=1, concat_axis=1, tiled=...  14.3 us
    ppermute x8, waiting for transfers between devices, neighbour(): lax.ppermute(values, 'gy', [(j, (j + step_y) % count_y) for j in range(co...  13.1 us
    pallas_call x2, Pallas kernels, onehot_gather(): pl.pallas_call(functools.partial(gather_kernel, per=per), grid=(blocks, g...  7.48 us
    ppermute x8, starting transfers between devices, neighbour(): lax.ppermute(values, 'gx', [(i, (i + step_x) % count_x) for i in range(co...  4.71 us
    dot_general x2, matrix products, tracer_step(): jnp.einsum('ab,...by->...ay', sum_x, tracers, precision=precision)  4.25 us
    ppermute x8, waiting for transfers between devices, neighbour(): lax.ppermute(values, 'gx', [(i, (i + step_x) % count_x) for i in range(co...  3.3 us
    unnamed x60, local copies, waits for them, and re-layouts  3.06 us
  transfers between devices with their start and end apart: 16, of which 9 were waited for; matrix products, arithmetic and copies ran while one was open for 4% of the time, Pallas kernels for 0%

profile of v25, /device:TPU:0, one launch (start us, length us, event | category | flops | bytes accessed | tf_op | source)
XLA Modules:
  0.0 89.8 jit_solution(12904618033511356871)
XLA Ops:
  0.7 0.6 copy-done.17
  2.0 0.7 fusion.10
  2.7 0.7 convolution_bitcast_fusion.5
  3.5 0.7 fusion.60
  4.4 0.7 fusion.2
  5.2 0.7 fusion.1
  5.9 1.1 %slice_reduce_fusion.3 = (f32[160,16]{1,0:T(8,128)S(1)}, f32[160,16]{1,0:T(8,128)S(1)}) fusion(f32[160,16,128]{2,1,0:T(8,128)S(1)} %fusion.1), kind=kLoop, calls=%fused_computation.24 | loop fusion | bytes 40960 | tf_op jit(solution)/shard_map/slice | solution.py:88
  7.1 3.0 %collective-permute-start = (f32[20,128]{1,0:T(8,128)S(1)}, f32[20,128]{1,0:T(8,128)S(1)}, u32[]{:S(2)}, u32[]{:S(2)}) collective-permute-start(f32[20,128]{1,0:T(8,128)S(1)} %reshape_squeeze.39), channel_id=1, source_target_pairs={{0,1},{1,2},{2,3},{3,4},{4,5},{5,6},{6,7},{7,0},{8,9},{9,10},{10,1... | collective-permute-start | bytes 30728 | tf_op jit(solution)/shard_map/ppermute | solution.py:26
  10.1 3.1 %collective-permute-start.1 = (f32[20,128]{1,0:T(8,128)S(1)}, f32[20,128]{1,0:T(8,128)S(1)}, u32[]{:S(2)}, u32[]{:S(2)}) collective-permute-start(f32[20,128]{1,0:T(8,128)S(1)} %reshape_squeeze.40), channel_id=1, source_target_pairs={{0,7},{1,0},{2,1},{3,2},{4,3},{5,4},{6,5},{7,6},{8,15},{9,8},{10,9... | collective-permute-start | bytes 30728 | tf_op jit(solution)/shard_map/ppermute | solution.py:26
  13.3 1.5 %collective-permute-done = f32[20,128]{1,0:T(8,128)S(1)} collective-permute-done((f32[20,128]{1,0:T(8,128)S(1)}, f32[20,128]{1,0:T(8,128)S(1)}, u32[]{:S(2)}, u32[]{:S(2)}) %collective-permute-start) | collective-permute-done | bytes 10272 | tf_op jit(solution)/shard_map/ppermute | solution.py:26
  15.0 0.8 select_add_fusion.1
  16.0 1.7 %collective-permute-start.3 = (f32[160,128]{1,0:T(8,128)S(1)}, f32[160,128]{1,0:T(8,128)S(1)}, u32[]{:S(2)}, u32[]{:S(2)}) collective-permute-start(f32[160,128]{1,0:T(8,128)S(1)} %bitcast.169), channel_id=1, source_target_pairs={{0,24},{8,0},{16,8},{24,16},{1,25},{9,1},{17,9},{25,17},{2,26},{10... | collective-permute-start | bytes 245768 | tf_op jit(solution)/shard_map/ppermute | solution.py:24
  17.8 2.1 %collective-permute-done.2 = f32[160,128]{1,0:T(8,128)S(1)} collective-permute-done((f32[160,128]{1,0:T(8,128)S(1)}, f32[160,128]{1,0:T(8,128)S(1)}, u32[]{:S(2)}, u32[]{:S(2)}) %collective-permute-start.2) | collective-permute-done | bytes 81952 | tf_op jit(solution)/shard_map/ppermute | solution.py:24
  20.0 0.8 fusion.5
  20.8 0.7 fusion.6
  21.5 0.7 convolution_multiply_fusion.1
  22.2 0.7 convolution_bitcast_fusion.2
  22.9 0.7 fusion.61
  23.6 0.7 fusion
  24.3 1.1 %slice_reduce_fusion.1 = (f32[160,16]{1,0:T(8,128)S(1)}, f32[160,16]{1,0:T(8,128)S(1)}) fusion(f32[160,16,128]{2,1,0:T(8,128)S(1)} %fusion), kind=kLoop, calls=%fused_computation.22 | loop fusion | bytes 40960 | tf_op jit(solution)/shard_map/slice | solution.py:88
  25.5 1.4 %collective-permute-start.4 = (f32[20,128]{1,0:T(8,128)S(1)}, f32[20,128]{1,0:T(8,128)S(1)}, u32[]{:S(2)}, u32[]{:S(2)}) collective-permute-start(f32[20,128]{1,0:T(8,128)S(1)} %reshape_squeeze.41), channel_id=1, source_target_pairs={{0,1},{1,2},{2,3},{3,4},{4,5},{5,6},{6,7},{7,0},{8,9},{9,10},{10,1... | collective-permute-start | bytes 30728 | tf_op jit(solution)/shard_map/ppermute | solution.py:26
  27.0 3.4 %collective-permute-start.5 = (f32[20,128]{1,0:T(8,128)S(1)}, f32[20,128]{1,0:T(8,128)S(1)}, u32[]{:S(2)}, u32[]{:S(2)}) collective-permute-start(f32[20,128]{1,0:T(8,128)S(1)} %reshape_squeeze.42), channel_id=1, source_target_pairs={{0,7},{1,0},{2,1},{3,2},{4,3},{5,4},{6,5},{7,6},{8,15},{9,8},{10,9... | collective-permute-start | bytes 30728 | tf_op jit(solution)/shard_map/ppermute | solution.py:26
  30.4 1.5 %collective-permute-done.4 = f32[20,128]{1,0:T(8,128)S(1)} collective-permute-done((f32[20,128]{1,0:T(8,128)S(1)}, f32[20,128]{1,0:T(8,128)S(1)}, u32[]{:S(2)}, u32[]{:S(2)}) %collective-permute-start.4) | collective-permute-done | bytes 10272 | tf_op jit(solution)/shard_map/ppermute | solution.py:26
  32.2 0.8 select_add_fusion
  33.2 0.9 %collective-permute-start.6 = (f32[160,128]{1,0:T(8,128)S(1)}, f32[160,128]{1,0:T(8,128)S(1)}, u32[]{:S(2)}, u32[]{:S(2)}) collective-permute-start(f32[160,128]{1,0:T(8,128)S(1)} %bitcast.170), channel_id=1, source_target_pairs={{0,8},{8,16},{16,24},{24,0},{1,9},{9,17},{17,25},{25,1},{2,10},{10... | collective-permute-start | bytes 245768 | tf_op jit(solution)/shard_map/ppermute | solution.py:24
  34.1 0.9 collective-permute-start.7
  35.1 0.6 copy.52
  35.7 0.6 copy.51
  36.3 0.8 collective-permute-done.6
  37.4 0.8 fusion.9
  38.3 0.6 fusion.37.table_ref
  38.9 3.1 %shard_map.320 = f32[4,64,128]{2,1,0:T(8,128)} custom-call(s32[1,8192]{1,0:T(1,128)} %bitcast.167, f32[1,8192]{1,0:T(1,128)} %bitcast.166, f32[4,16,128]{2,1,0:T(8,128)} %fusion.37.table_ref), custom_call_target="tpu_custom_call" | custom-call | tf_op jit(solution)/shard_map/pallas_call | solution.py:214
  42.0 0.9 %reshape.315 = f32[4,32,256]{2,1,0:T(8,128)S(1)} reshape(f32[4,64,128]{2,1,0:T(8,128)} %shard_map.320) | data formatting | bytes 262144 | tf_op jit(solution)/shard_map/reshape | solution.py:253
  43.1 14.3 %all_to_all.5 = f32[4,32,256]{2,0,1:T(4,128)S(1)} all-to-all(f32[4,32,256]{2,0,1:T(4,128)S(1)} %copy.40), channel_id=1, replica_groups=mesh['gx'=4,'gy'=8] {'gx','gy'}, dimensions={1} | all-to-all | bytes 262144 | tf_op jit(solution)/shard_map/all_to_all | solution.py:254
  57.4 0.7 copy.41.table_ref
  58.1 4.4 %shard_map.321 = f32[4,16,128]{2,1,0:T(8,128)} custom-call(s32[1,8192]{1,0:T(1,128)} %bitcast.176, f32[1,8192]{1,0:T(1,128)} %bitcast.177, f32[4,32,256]{2,1,0:T(8,128)} %copy.41.table_ref), custom_call_target="tpu_custom_call" | custom-call | tf_op jit(solution)/shard_map/pallas_call | solution.py:214
  62.5 0.7 fusion.45
  63.2 0.7 fusion.41
  63.9 0.6 slice_reduce_fusion.7
  64.6 0.7 fusion.59
  66.6 2.1 %collective-permute-start.10 = (f32[10,128]{1,0:T(8,128)S(1)}, f32[10,128]{1,0:T(8,128)S(1)}, u32[]{:S(2)}, u32[]{:S(2)}) collective-permute-start(f32[10,128]{1,0:T(8,128)S(1)} %reshape_squeeze.46), channel_id=1, source_target_pairs={{0,7},{1,0},{2,1},{3,2},{4,3},{5,4},{6,5},{7,6},{8,15},{9,8},{10,9... | collective-permute-start | bytes 15368 | tf_op jit(solution)/shard_map/ppermute | solution.py:26
  69.3 0.9 fusion.36
  70.3 4.8 %collective-permute-done.11 = f32[10,128]{1,0:T(8,128)S(1)} collective-permute-done((f32[10,128]{1,0:T(8,128)S(1)}, f32[10,128]{1,0:T(8,128)S(1)}, u32[]{:S(2)}, u32[]{:S(2)}) %collective-permute-start.11) | collective-permute-done | bytes 5152 | tf_op jit(solution)/shard_map/ppermute | solution.py:26
  75.2 1.9 %fusion.17 = f32[2,40,16,128]{3,2,1,0:T(8,128)S(1)} fusion(f32[2,40,16,128]{3,2,1,0:T(8,128)S(1)} %get-tuple-element.71, f32[2,40,16,128]{3,2,1,0:T(8,128)S(1)} %convolution_bitcast_fusion.8, f32[2,40,16,128]{3,2,1,0:T(8,128)S(1)} %fusion.62, f32[2,40,16,128]{3,2,1,0:T(8,128)S(1)} %fusion.63, f32[40,16,128]{2,1,0:T(8,128)} %get-tuple-element.69, ...), kind=kOutput, calls=%fused_computation.45 | convolution fusion | flops 19169280 | bytes 4025632 | tf_op jit(solution)/shard_map/ab,...by->...ay/dot_general | solution.py:121
  78.0 0.6 slice_reduce_fusion.5
  78.8 2.0 %collective-permute-start.14 = (f32[10,128]{1,0:T(8,128)S(1)}, f32[10,128]{1,0:T(8,128)S(1)}, u32[]{:S(2)}, u32[]{:S(2)}) collective-permute-start(f32[10,128]{1,0:T(8,128)S(1)} %reshape_squeeze.50), channel_id=1, source_target_pairs={{0,7},{1,0},{2,1},{3,2},{4,3},{5,4},{6,5},{7,6},{8,15},{9,8},{10,9... | collective-permute-start | bytes 15368 | tf_op jit(solution)/shard_map/ppermute | solution.py:26
  82.5 4.7 %collective-permute-done.15 = f32[10,128]{1,0:T(8,128)S(1)} collective-permute-done((f32[10,128]{1,0:T(8,128)S(1)}, f32[10,128]{1,0:T(8,128)S(1)}, u32[]{:S(2)}, u32[]{:S(2)}) %collective-permute-start.15) | collective-permute-done | bytes 5152 | tf_op jit(solution)/shard_map/ppermute | solution.py:26
  87.4 2.4 %fusion.29 = f32[2,40,16,128]{3,2,1,0:T(8,128)} fusion(f32[2,40,16,128]{3,2,1,0:T(8,128)S(1)} %fusion.17, f32[2,40,16,128]{3,2,1,0:T(8,128)S(1)} %convolution_bitcast_fusion.6, f32[2,40,16,128]{3,2,1,0:T(8,128)S(1)} %fusion.64, f32[2,40,16,128]{3,2,1,0:T(8,128)S(1)} %fusion.65, f32[2,40,16]{2,1,0:T(8,128)S(1)} %broadcast_in_dim.276, ...), kind=kOutput, calls=%fused_computation.57 | convolution fusion | flops 19169280 | bytes 4025632 | tf_op jit(solution)/shard_map/ab,...by->...ay/dot_general | solution.py:121
  (105 shorter events, 7.8 us)
Async XLA Ops:
  0.6 0.7 copy-start.17
  0.6 0.7 copy-start.27
  0.7 0.9 %copy-start.11 = (f32[16,16,1]{1,0,2:T(8,128)S(1)}, f32[16,16,1]{1,0,2:T(8,128)}, u32[]{:S(2)}) copy-start(f32[16,16,1]{1,0,2:T(8,128)} %constant.166) | copy-start | bytes 3076
  0.7 1.3 %copy-start.1 = (f32[4,40,16,128]{3,2,1,0:T(8,128)S(1)}, f32[4,40,16,128]{3,2,1,0:T(8,128)}, u32[]{:S(2)}) copy-start(f32[4,40,16,128]{3,2,1,0:T(8,128)} %param.41) | copy-start | bytes 3932164
  0.7 0.8 copy-start.16
  2.7 0.8 copy-start.10
  3.5 0.8 copy-start.7
  4.4 0.8 copy-start.6
  7.1 7.7 %collective-permute-start = (f32[20,128]{1,0:T(8,128)S(1)}, f32[20,128]{1,0:T(8,128)S(1)}, u32[]{:S(2)}, u32[]{:S(2)}) collective-permute-start(f32[20,128]{1,0:T(8,128)S(1)} %reshape_squeeze.39), channel_id=1, source_target_pairs={{0,1},{1,2},{2,3},{3,4},{4,5},{5,6},{6,7},{7,0},{8,9},{9,10},{10,1... | collective-permute-start | bytes 30728 | tf_op jit(solution)/shard_map/ppermute | solution.py:26
  10.1 4.7 %collective-permute-start.1 = (f32[20,128]{1,0:T(8,128)S(1)}, f32[20,128]{1,0:T(8,128)S(1)}, u32[]{:S(2)}, u32[]{:S(2)}) collective-permute-start(f32[20,128]{1,0:T(8,128)S(1)} %reshape_squeeze.40), channel_id=1, source_target_pairs={{0,7},{1,0},{2,1},{3,2},{4,3},{5,4},{6,5},{7,6},{8,15},{9,8},{10,9... | collective-permute-start | bytes 30728 | tf_op jit(solution)/shard_map/ppermute | solution.py:26
  13.3 18.9 %copy-start.18 = (pred[128]{0:T(512)(128)(4,1)}, pred[128]{0:T(512)(128)(4,1)S(1)}, u32[]{:S(2)}) copy-start(pred[128]{0:T(512)(128)(4,1)S(1)} %get-tuple-element.76) | copy-start | bytes 388
  13.3 18.9 %copy-start.20 = (pred[128]{0:T(512)(128)(4,1)}, pred[128]{0:T(512)(128)(4,1)S(1)}, u32[]{:S(2)}) copy-start(pred[128]{0:T(512)(128)(4,1)S(1)} %get-tuple-element.77) | copy-start | bytes 388
  15.0 5.0 %copy-start.13 = (f32[16,128]{1,0:T(8,128)S(1)}, f32[16,128]{1,0:T(8,128)}, u32[]{:S(2)}) copy-start(f32[16,128]{1,0:T(8,128)} %constant.165) | copy-start | bytes 24580
  15.0 5.0 %copy-start.14 = (f32[16,16,1]{1,0,2:T(8,128)S(1)}, f32[16,16,1]{1,0,2:T(8,128)}, u32[]{:S(2)}) copy-start(f32[16,16,1]{1,0,2:T(8,128)} %constant.170) | copy-start | bytes 3076
  16.0 3.9 %collective-permute-start.2 = (f32[160,128]{1,0:T(8,128)S(1)}, f32[160,128]{1,0:T(8,128)S(1)}, u32[]{:S(2)}, u32[]{:S(2)}) collective-permute-start(f32[160,128]{1,0:T(8,128)S(1)} %bitcast.171), channel_id=1, source_target_pairs={{0,8},{8,16},{16,24},{24,0},{1,9},{9,17},{17,25},{25,1},{2,10},{10... | collective-permute-start | bytes 245768 | tf_op jit(solution)/shard_map/ppermute | solution.py:24
  16.0 4.0 %collective-permute-start.3 = (f32[160,128]{1,0:T(8,128)S(1)}, f32[160,128]{1,0:T(8,128)S(1)}, u32[]{:S(2)}, u32[]{:S(2)}) collective-permute-start(f32[160,128]{1,0:T(8,128)S(1)} %bitcast.169), channel_id=1, source_target_pairs={{0,24},{8,0},{16,8},{24,16},{1,25},{9,1},{17,9},{25,17},{2,26},{10... | collective-permute-start | bytes 245768 | tf_op jit(solution)/shard_map/ppermute | solution.py:24
  17.8 19.6 %copy-start.22 = (pred[16]{0:T(512)(128)(4,1)}, pred[16]{0:T(512)(128)(4,1)S(1)}, u32[]{:S(2)}) copy-start(pred[16]{0:T(512)(128)(4,1)S(1)} %get-tuple-element.78) | copy-start | bytes 52
  17.8 19.6 %copy-start.24 = (pred[16]{0:T(512)(128)(4,1)}, pred[16]{0:T(512)(128)(4,1)S(1)}, u32[]{:S(2)}) copy-start(pred[16]{0:T(512)(128)(4,1)S(1)} %get-tuple-element.79) | copy-start | bytes 52
  25.5 6.5 %collective-permute-start.4 = (f32[20,128]{1,0:T(8,128)S(1)}, f32[20,128]{1,0:T(8,128)S(1)}, u32[]{:S(2)}, u32[]{:S(2)}) collective-permute-start(f32[20,128]{1,0:T(8,128)S(1)} %reshape_squeeze.41), channel_id=1, source_target_pairs={{0,1},{1,2},{2,3},{3,4},{4,5},{5,6},{6,7},{7,0},{8,9},{9,10},{10,1... | collective-permute-start | bytes 30728 | tf_op jit(solution)/shard_map/ppermute | solution.py:26
  27.0 5.1 %collective-permute-start.5 = (f32[20,128]{1,0:T(8,128)S(1)}, f32[20,128]{1,0:T(8,128)S(1)}, u32[]{:S(2)}, u32[]{:S(2)}) collective-permute-start(f32[20,128]{1,0:T(8,128)S(1)} %reshape_squeeze.42), channel_id=1, source_target_pairs={{0,7},{1,0},{2,1},{3,2},{4,3},{5,4},{6,5},{7,6},{8,15},{9,8},{10,9... | collective-permute-start | bytes 30728 | tf_op jit(solution)/shard_map/ppermute | solution.py:26
  32.2 2.8 %copy-start.26 = (s32[1,32]{1,0:T(1,128)S(1)}, s32[1,32]{1,0:T(1,128)}, u32[]{:S(2)}) copy-start(s32[1,32]{1,0:T(1,128)} %param.44) | copy-start | bytes 388
  32.2 3.5 %copy-start.15 = (s32[1,32,256]{2,1,0:T(8,128)S(1)}, s32[1,32,256]{2,1,0:T(8,128)}, u32[]{:S(2)}) copy-start(s32[1,32,256]{2,1,0:T(8,128)} %param.43) | copy-start | bytes 98308
  33.2 3.9 %collective-permute-start.6 = (f32[160,128]{1,0:T(8,128)S(1)}, f32[160,128]{1,0:T(8,128)S(1)}, u32[]{:S(2)}, u32[]{:S(2)}) collective-permute-start(f32[160,128]{1,0:T(8,128)S(1)} %bitcast.170), channel_id=1, source_target_pairs={{0,8},{8,16},{16,24},{24,0},{1,9},{9,17},{17,25},{25,1},{2,10},{10... | collective-permute-start | bytes 245768 | tf_op jit(solution)/shard_map/ppermute | solution.py:24
  34.1 3.3 %collective-permute-start.7 = (f32[160,128]{1,0:T(8,128)S(1)}, f32[160,128]{1,0:T(8,128)S(1)}, u32[]{:S(2)}, u32[]{:S(2)}) collective-permute-start(f32[160,128]{1,0:T(8,128)S(1)} %bitcast.168), channel_id=1, source_target_pairs={{0,24},{8,0},{16,8},{24,16},{1,25},{9,1},{17,9},{25,17},{2,26},{10... | collective-permute-start | bytes 245768 | tf_op jit(solution)/shard_map/ppermute | solution.py:24
  38.3 26.3 %copy-start.3 = (f32[160,16,128]{2,1,0:T(8,128)}, f32[160,16,128]{2,1,0:T(8,128)S(1)}, u32[]{:S(2)}) copy-start(f32[160,16,128]{2,1,0:T(8,128)S(1)} %fusion.9) | copy-start | bytes 3932164
  38.3 24.2 %copy-start = (f32[2,40,16,128]{3,2,1,0:T(8,128)S(1)}, f32[2,40,16,128]{3,2,1,0:T(8,128)}, u32[]{:S(2)}) copy-start(f32[2,40,16,128]{3,2,1,0:T(8,128)} %param.45) | copy-start | bytes 1966084
  38.3 24.2 %copy-start.2 = (f32[2,40,16,128]{3,2,1,0:T(8,128)S(1)}, f32[2,40,16,128]{3,2,1,0:T(8,128)}, u32[]{:S(2)}) copy-start(f32[2,40,16,128]{3,2,1,0:T(8,128)} %param.46) | copy-start | bytes 1966084
  42.9 22.3 %copy-start.12 = (f32[16,16,1,1]{1,0,3,2:T(8,128)S(1)}, f32[16,16,1,1]{1,0,3,2:T(8,128)}, u32[]{:S(2)}) copy-start(f32[16,16,1,1]{1,0,3,2:T(8,128)} %constant.173) | copy-start | bytes 3076
  63.9 1.7 %copy-start.9 = (f32[128,128,1,1]{1,0,3,2:T(8,128)S(1)}, f32[128,128,1,1]{1,0,3,2:T(8,128)}, u32[]{:S(2)}) copy-start(f32[128,128,1,1]{1,0,3,2:T(8,128)} %constant.172) | copy-start | bytes 196612
  65.2 0.8 copy-start.8
  66.6 3.7 %collective-permute-start.10 = (f32[10,128]{1,0:T(8,128)S(1)}, f32[10,128]{1,0:T(8,128)S(1)}, u32[]{:S(2)}, u32[]{:S(2)}) collective-permute-start(f32[10,128]{1,0:T(8,128)S(1)} %reshape_squeeze.46), channel_id=1, source_target_pairs={{0,7},{1,0},{2,1},{3,2},{4,3},{5,4},{6,5},{7,6},{8,15},{9,8},{10,9... | collective-permute-start | bytes 15368 | tf_op jit(solution)/shard_map/ppermute | solution.py:26
  68.7 6.4 %collective-permute-start.11 = (f32[10,128]{1,0:T(8,128)S(1)}, f32[10,128]{1,0:T(8,128)S(1)}, u32[]{:S(2)}, u32[]{:S(2)}) collective-permute-start(f32[10,128]{1,0:T(8,128)S(1)} %reshape_squeeze.47), channel_id=1, source_target_pairs={{0,1},{1,2},{2,3},{3,4},{4,5},{5,6},{6,7},{7,0},{8,9},{9,10},{10,1... | collective-permute-start | bytes 15368 | tf_op jit(solution)/shard_map/ppermute | solution.py:26
  68.8 6.4 %collective-permute-start.8 = (f32[80,128]{1,0:T(8,128)}, f32[80,128]{1,0:T(8,128)}, u32[]{:S(2)}, u32[]{:S(2)}) collective-permute-start(f32[80,128]{1,0:T(8,128)} %bitcast.173), channel_id=1, source_target_pairs={{0,24},{8,0},{16,8},{24,16},{1,25},{9,1},{17,9},{25,17},{2,26},{10... | collective-permute-start | bytes 122888 | tf_op jit(solution)/shard_map/ppermute | solution.py:24
  68.8 6.4 %collective-permute-start.9 = (f32[80,128]{1,0:T(8,128)S(1)}, f32[80,128]{1,0:T(8,128)}, u32[]{:S(2)}, u32[]{:S(2)}) collective-permute-start(f32[80,128]{1,0:T(8,128)S(1)} %bitcast.172), channel_id=1, source_target_pairs={{0,8},{8,16},{16,24},{24,0},{1,9},{9,17},{17,25},{25,1},{2,10},{10... | collective-permute-start | bytes 122888 | tf_op jit(solution)/shard_map/ppermute | solution.py:24
  77.9 9.4 %copy-start.4 = (f32[40,16,128]{2,1,0:T(8,128)S(1)}, f32[40,16,128]{2,1,0:T(8,128)}, u32[]{:S(2)}) copy-start(f32[40,16,128]{2,1,0:T(8,128)} %get-tuple-element.68) | copy-start | bytes 983044
  77.9 9.4 %copy-start.5 = (f32[40,16,128]{2,1,0:T(8,128)S(1)}, f32[40,16,128]{2,1,0:T(8,128)}, u32[]{:S(2)}) copy-start(f32[40,16,128]{2,1,0:T(8,128)} %get-tuple-element.69) | copy-start | bytes 983044
  78.0 9.4 %copy-start.19 = (pred[128]{0:T(512)(128)(4,1)S(1)}, pred[128]{0:T(512)(128)(4,1)}, u32[]{:S(2)}) copy-start(pred[128]{0:T(512)(128)(4,1)} %copy-done.18) | copy-start | bytes 388
  78.0 9.4 %copy-start.21 = (pred[128]{0:T(512)(128)(4,1)S(1)}, pred[128]{0:T(512)(128)(4,1)}, u32[]{:S(2)}) copy-start(pred[128]{0:T(512)(128)(4,1)} %copy-done.20) | copy-start | bytes 388
  78.0 9.4 %copy-start.23 = (pred[16]{0:T(512)(128)(4,1)S(1)}, pred[16]{0:T(512)(128)(4,1)}, u32[]{:S(2)}) copy-start(pred[16]{0:T(512)(128)(4,1)} %copy-done.22) | copy-start | bytes 52
  78.0 9.4 %copy-start.25 = (pred[16]{0:T(512)(128)(4,1)S(1)}, pred[16]{0:T(512)(128)(4,1)}, u32[]{:S(2)}) copy-start(pred[16]{0:T(512)(128)(4,1)} %copy-done.24) | copy-start | bytes 52
  78.0 9.4 %copy-start.28 = (f32[16,16,1,1]{1,0,3,2:T(8,128)S(1)}, f32[16,16,1,1]{1,0,3,2:T(8,128)}, u32[]{:S(2)}) copy-start(f32[16,16,1,1]{1,0,3,2:T(8,128)} %constant.171) | copy-start | bytes 3076
  78.8 3.7 %collective-permute-start.14 = (f32[10,128]{1,0:T(8,128)S(1)}, f32[10,128]{1,0:T(8,128)S(1)}, u32[]{:S(2)}, u32[]{:S(2)}) collective-permute-start(f32[10,128]{1,0:T(8,128)S(1)} %reshape_squeeze.50), channel_id=1, source_target_pairs={{0,7},{1,0},{2,1},{3,2},{4,3},{5,4},{6,5},{7,6},{8,15},{9,8},{10,9... | collective-permute-start | bytes 15368 | tf_op jit(solution)/shard_map/ppermute | solution.py:26
  80.9 6.4 %collective-permute-start.15 = (f32[10,128]{1,0:T(8,128)S(1)}, f32[10,128]{1,0:T(8,128)S(1)}, u32[]{:S(2)}, u32[]{:S(2)}) collective-permute-start(f32[10,128]{1,0:T(8,128)S(1)} %reshape_squeeze.51), channel_id=1, source_target_pairs={{0,1},{1,2},{2,3},{3,4},{4,5},{5,6},{6,7},{7,0},{8,9},{9,10},{10,1... | collective-permute-start | bytes 15368 | tf_op jit(solution)/shard_map/ppermute | solution.py:26
  80.9 6.4 %collective-permute-start.12 = (f32[80,128]{1,0:T(8,128)S(1)}, f32[80,128]{1,0:T(8,128)S(1)}, u32[]{:S(2)}, u32[]{:S(2)}) collective-permute-start(f32[80,128]{1,0:T(8,128)S(1)} %bitcast.175), channel_id=1, source_target_pairs={{0,24},{8,0},{16,8},{24,16},{1,25},{9,1},{17,9},{25,17},{2,26},{10... | collective-permute-start | bytes 122888 | tf_op jit(solution)/shard_map/ppermute | solution.py:24
  81.2 6.1 %collective-permute-start.13 = (f32[80,128]{1,0:T(8,128)S(1)}, f32[80,128]{1,0:T(8,128)}, u32[]{:S(2)}, u32[]{:S(2)}) collective-permute-start(f32[80,128]{1,0:T(8,128)S(1)} %bitcast.174), channel_id=1, source_target_pairs={{0,8},{8,16},{16,24},{24,0},{1,9},{9,17},{17,25},{25,1},{2,10},{10... | collective-permute-start | bytes 122888 | tf_op jit(solution)/shard_map/ppermute | solution.py:24
